TPU v7x, 32 devices: a whole 2x2x4 slice. The times are simulated.
32 devices in a mesh: groups: 2 (over y), dict: 8 (over z, x), section: 2 (over core).
Axes of the slice: x: 2, y: 2, z: 4, core: 2. Of those that a mesh axis runs over, the one named last changes fastest.
Arguments:
- cotangent: bfloat16 [256, 4608], P(('groups', 'dict')), parts along dimension 0, may hold values from -6 to 6
- routes: int32 [2, 256, 8], P('section', ('groups', 'dict')), parts along dimension 1, may hold values from 0 to 15, as said below
- acts: bfloat16 [2, 256, 1024], P('section', ('groups', 'dict')), parts along dimension 1, as said below
- decoder: bfloat16 [2, 2048, 4608], P('section', 'dict'), may hold values from -0.09375 to 0.09375
- encoder: bfloat16 [2, 2048, 4608], P('section', 'dict'), may hold values from -0.1875 to 0.1875
- gain: float32 [2, 4608], P('section'), may hold values from 0.3 to 3
- inv_rms: float32 [2, 256], P('section', ('groups', 'dict')), parts along dimension 1, may hold values from 0.3 to 3
Outputs:
- attributions: float32 [2, 256, 1024], P('section', ('groups', 'dict')), parts along dimension 1
- grads: bfloat16 [2, 256, 4608], P('section', ('groups', 'dict')), parts along dimension 1
There are 2 independent parts, one for each index of `groups`. A program takes and returns all parts, laid end to end along the dimension named above; an argument that names none is the same for every part. Nothing has to cross between parts.
Inputs may be any that keep to these rules, and one draw needn't show every extreme that they name: `routes`: each row lists 8 blocks whose ranges b // 2 all differ; in each layer, among the 16 rows of one index of dict, every range is listed either 16 times or one time fewer, and some range exactly 16 times. `acts`: nonnegative, roughly half of the entries zero.
All inputs are finite; a program needn't handle non-finite values.
Results may differ from a plain program's by a relative error of at most 0.012.
Values may be sent and summed in bfloat16 or wider, within the bound.
No kernel may reach another device: no remote copies, remote signals or barrier semaphores. Data moves between devices by JAX's collectives and lax.ppermute only.
A program may use at most 64 MiB of HBM per device.

v0:
```python
import jax
import jax.numpy as jnp
from jax import lax
from jax.sharding import PartitionSpec as P


def passed_along(block, axis, distance):
    devices = range(lax.axis_size(axis))
    route = [(i - distance, i) for i in devices if i - distance in devices]
    return lax.ppermute(block, axis, route)


def owner_work(recv_g, recv_act, dec_local, enc_local):
    width = recv_g.shape[-1]
    columns = dec_local.shape[0]
    flat_g = recv_g.reshape(-1, width)
    flat_act = recv_act.reshape(-1, columns)
    coef = lax.dot_general(
        flat_g, dec_local, (((1,), (1,)), ((), ())), preferred_element_type=jnp.float32
    ).astype(jnp.bfloat16)
    masked = jnp.where(flat_act > 0, coef, jnp.zeros_like(coef))
    contrib = jnp.dot(masked, enc_local, preferred_element_type=jnp.float32).astype(jnp.bfloat16)
    lead = recv_g.shape[:-1]
    return (coef.reshape(lead + (columns,)), contrib.reshape(lead + (width,)))


def layer_pass(g_rows, routes_l, acts_l, dec_local, enc_local, gain_l, scale_l, peers):
    tok_count, listed = routes_l.shape
    block = acts_l.shape[1] // listed
    width = dec_local.shape[1]
    held = dec_local.shape[0] // block
    slots_per = (tok_count * listed + peers - 1) // peers
    total_slots = peers * slots_per
    owner = routes_l // held
    within = routes_l - owner * held
    owners = jnp.arange(peers, dtype=jnp.int32)
    hits = (owner[:, :, None] == owners[None, None, :]).astype(jnp.int32)
    per_row = jnp.sum(hits, axis=1)
    earlier = jnp.cumsum(per_row, axis=0) - per_row
    place = jnp.sum(hits * earlier[:, None, :], axis=2)
    slot_of = (owner * slots_per + place).reshape(-1)
    slot_ids = jnp.arange(total_slots, dtype=jnp.int32)
    pick = (slot_ids[:, None] == slot_of[None, :]).astype(jnp.bfloat16)
    row_pick = jnp.sum(
        pick.reshape(total_slots, tok_count, listed).astype(jnp.float32), axis=2
    ).astype(jnp.bfloat16)
    send_g = jnp.dot(row_pick, g_rows, preferred_element_type=jnp.float32).astype(jnp.bfloat16)
    block_act = jnp.dot(
        pick, acts_l.reshape(tok_count * listed, block), preferred_element_type=jnp.float32
    ).astype(jnp.bfloat16)
    within_hot = (within.reshape(-1)[:, None] == jnp.arange(held, dtype=jnp.int32)[None, :]).astype(
        jnp.bfloat16
    )
    slot_within = jnp.dot(pick, within_hot, preferred_element_type=jnp.float32).astype(jnp.bfloat16)
    send_act = (slot_within[:, :, None] * block_act[:, None, :]).reshape(total_slots, held * block)
    send_g = send_g.reshape(peers, slots_per, width)
    send_act = send_act.reshape(peers, slots_per, held * block)
    recv_g, recv_act = (
        lax.all_to_all(send_g, "dict", split_axis=0, concat_axis=0, tiled=True),
        lax.all_to_all(send_act, "dict", split_axis=0, concat_axis=0, tiled=True),
    )
    coef_here, contrib_here = owner_work(recv_g, recv_act, dec_local, enc_local)
    coef_back, contrib_back = (
        lax.all_to_all(coef_here, "dict", split_axis=0, concat_axis=0, tiled=True),
        lax.all_to_all(contrib_here, "dict", split_axis=0, concat_axis=0, tiled=True),
    )
    coef_back = coef_back.reshape(total_slots, held, block)
    contrib_back = contrib_back.reshape(total_slots, width)
    coef_chosen = jnp.sum(
        slot_within.astype(jnp.float32)[:, :, None] * coef_back.astype(jnp.float32), axis=1
    ).astype(jnp.bfloat16)
    coef_rows = lax.dot_general(
        pick, coef_chosen, (((0,), (0,)), ((), ())), preferred_element_type=jnp.float32
    )
    attr = (acts_l.reshape(tok_count * listed, block).astype(jnp.float32) * coef_rows).reshape(
        tok_count, listed * block
    )
    summed = lax.dot_general(
        row_pick, contrib_back, (((0,), (0,)), ((), ())), preferred_element_type=jnp.float32
    )
    new_g = (g_rows.astype(jnp.float32) + scale_l[:, None] * gain_l[None, :] * summed).astype(
        jnp.bfloat16
    )
    return (attr, new_g)


def per_device(cotangent, routes, acts, decoder, encoder, gain, inv_rms):
    peers = lax.axis_size("dict")
    depth = lax.axis_size("section")
    here = lax.axis_index("section")
    routes_l = routes[0]
    acts_l = acts[0]
    dec_local = decoder[0]
    enc_local = encoder[0]
    gain_l = gain[0]
    scale_l = inv_rms[0]
    tok_count, listed = routes_l.shape
    attr_keep = jnp.zeros((tok_count, acts_l.shape[1]), jnp.float32)
    grad_keep = jnp.zeros(cotangent.shape, jnp.bfloat16)
    g_new = cotangent
    for turn in range(depth):
        if turn > 0:
            g_now = passed_along(g_new, "section", -1)
        else:
            g_now = cotangent
        active = here == depth - 1 - turn
        attr, g_new = layer_pass(
            g_now, routes_l, acts_l, dec_local, enc_local, gain_l, scale_l, peers
        )
        attr_keep = jnp.where(active, attr, attr_keep)
        grad_keep = jnp.where(active, g_new, grad_keep)
    return (attr_keep[None], grad_keep[None])


def solution(mesh):
    placed = (
        P(("groups", "dict"), None),
        P("section", ("groups", "dict"), None),
        P("section", ("groups", "dict"), None),
        P("section", "dict", None),
        P("section", "dict", None),
        P("section", None),
        P("section", ("groups", "dict")),
    )
    return jax.shard_map(
        per_device,
        mesh=mesh,
        in_specs=placed,
        out_specs=(P("section", ("groups", "dict"), None), P("section", ("groups", "dict"), None)),
        check_vma=False,
    )
```

profile of v0, /device:TPU:0, one launch (start us, length us, event | category | flops | bytes accessed | tf_op | source)
XLA Modules:
  0.0 178.2 jit_solution(12961441000112676020)
XLA Ops:
  0.6 0.8 add_select_fusion
  3.1 0.8 reshape_squeeze.2
  5.0 7.3 %all-to-all-start = ((bf16[8,16,256]{2,1,0:T(8,128)(2,1)}), bf16[8,16,256]{2,1,0:T(8,128)(2,1)S(1)}, u32[]{:S(2)}, u32[]{:S(2)}) async-start(bf16[8,16,256]{2,1,0:T(8,128)(2,1)} %mul.119), calls=%async_computation | async-start | bytes 131072 | tf_op jit(solution)/shard_map/all_to_all | solution.py:60
  13.1 2.4 %convolution_convert_fusion.3 = bf16[128,4608]{1,0:T(8,128)(2,1)} fusion(bf16[128,16]{0,1:T(8,128)(2,1)S(1)} %fusion.19, bf16[16,4608]{1,0:T(8,128)(2,1)} %param.7), kind=kOutput, calls=%fused_computation.3 | convolution fusion | flops 19464192 | bytes 1331200 | tf_op jit(solution)/shard_map/dot_general | solution.py:47
  15.5 3.6 %all-to-all-done = bf16[8,16,256]{2,1,0:T(8,128)(2,1)S(1)} async-done(((bf16[8,16,256]{2,1,0:T(8,128)(2,1)}), bf16[8,16,256]{2,1,0:T(8,128)(2,1)S(1)}, u32[]{:S(2)}, u32[]{:S(2)}) %all-to-all-start) | async-done | bytes 65568 | tf_op jit(solution)/shard_map/all_to_all | solution.py:60
  19.8 3.6 %all-to-all-start.1 = ((bf16[8,16,4608]{2,1,0:T(8,128)(2,1)}), bf16[8,16,4608]{2,1,0:T(8,128)(2,1)S(1)}, u32[]{:S(2)}, u32[]{:S(2)}) async-start(bf16[8,16,4608]{2,1,0:T(8,128)(2,1)} %bitcast.70), calls=%async_computation.1 | async-start | bytes 2359296 | tf_op jit(solution)/shard_map/all_to_all | solution.py:59
  23.3 1.5 broadcast_compare_fusion
  24.8 26.1 %all-to-all-done.1 = bf16[8,16,4608]{2,1,0:T(8,128)(2,1)S(1)} async-done(((bf16[8,16,4608]{2,1,0:T(8,128)(2,1)}), bf16[8,16,4608]{2,1,0:T(8,128)(2,1)S(1)}, u32[]{:S(2)}, u32[]{:S(2)}) %all-to-all-start.1) | async-done | bytes 1179680 | tf_op jit(solution)/shard_map/all_to_all | solution.py:59
  50.9 3.2 %bitcast_select_fusion.1 = (bf16[128,256]{1,0:T(8,128)(2,1)S(1)}, bf16[128,256]{1,0:T(8,128)(2,1)}) fusion(pred[8,16,256]{2,1,0:T(8,128)(4,1)} %broadcast_compare_fusion, bf16[128,4608]{1,0:T(8,128)(2,1)S(1)} %bitcast.67, bf16[1,256,4608]{2,1,0:T(8,128)(2,1)} %param.10), kind=kOutput, calls=%fused_computation.28 | convolution fusion | flops 302055424 | bytes 3702784 | tf_op jit(solution)/shard_map/dot_general | solution.py:18
  54.0 1.5 convolution_convert_fusion.2
  55.5 3.7 %all-to-all-start.2 = ((bf16[8,16,4608]{2,1,0:T(8,128)(2,1)}), bf16[8,16,4608]{2,1,0:T(8,128)(2,1)S(1)}, u32[]{:S(2)}, u32[]{:S(2)}) async-start(bf16[8,16,4608]{2,1,0:T(8,128)(2,1)} %bitcast.7), calls=%async_computation.2 | async-start | bytes 2359296 | tf_op jit(solution)/shard_map/all_to_all | solution.py:65
  59.2 1.4 reduce.1
  60.6 27.2 %all-to-all-done.2 = bf16[8,16,4608]{2,1,0:T(8,128)(2,1)S(1)} async-done(((bf16[8,16,4608]{2,1,0:T(8,128)(2,1)}), bf16[8,16,4608]{2,1,0:T(8,128)(2,1)S(1)}, u32[]{:S(2)}, u32[]{:S(2)}) %all-to-all-start.2) | async-done | bytes 1179680 | tf_op jit(solution)/shard_map/all_to_all | solution.py:65
  87.9 1.2 fusion.1
  89.1 1.3 collective-permute-start
  90.4 2.0 %collective-permute-done = bf16[16,4608]{1,0:T(8,128)(2,1)S(1)} collective-permute-done((bf16[16,4608]{1,0:T(8,128)(2,1)S(1)}, bf16[16,4608]{1,0:T(8,128)(2,1)S(1)}, u32[]{:S(2)}, u32[]{:S(2)}) %collective-permute-start) | collective-permute-done | bytes 147488 | tf_op jit(solution)/shard_map/ppermute | solution.py:10
  92.8 32.7 %all_to_all.36 = bf16[8,16,4608]{2,1,0:T(8,128)(2,1)S(1)} all-to-all(bf16[8,16,4608]{2,1,0:T(8,128)(2,1)S(1)} %bitcast.72), channel_id=1, replica_groups=mesh['groups'=2,'dict'=8,'section'=2] {'dict'}, dimensions={0} | all-to-all | bytes 2359296 | tf_op jit(solution)/shard_map/all_to_all | solution.py:59
  125.5 4.0 %all-to-all-start.5 = ((bf16[8,16,256]{2,1,0:T(8,128)(2,1)}), bf16[8,16,256]{2,1,0:T(8,128)(2,1)}, u32[]{:S(2)}, u32[]{:S(2)}) async-start(bf16[8,16,256]{2,1,0:T(8,128)(2,1)} %bitcast.73), calls=%async_computation.5 | async-start | bytes 131072 | tf_op jit(solution)/shard_map/all_to_all | solution.py:64
  129.4 3.2 %bitcast_select_fusion = (bf16[128,256]{1,0:T(8,128)(2,1)}, bf16[128,256]{1,0:T(8,128)(2,1)}) fusion(pred[8,16,256]{2,1,0:T(8,128)(4,1)} %broadcast_compare_fusion, bf16[128,4608]{1,0:T(8,128)(2,1)S(1)} %bitcast.68, bf16[1,256,4608]{2,1,0:T(8,128)(2,1)} %param.10), kind=kOutput, calls=%fused_computation.27 | convolution fusion | flops 302055424 | bytes 3702784 | tf_op jit(solution)/shard_map/dot_general | solution.py:18
  132.6 3.7 %all-to-all-done.5 = bf16[8,16,256]{2,1,0:T(8,128)(2,1)} async-done(((bf16[8,16,256]{2,1,0:T(8,128)(2,1)}), bf16[8,16,256]{2,1,0:T(8,128)(2,1)}, u32[]{:S(2)}, u32[]{:S(2)}) %all-to-all-start.5) | async-done | bytes 65568 | tf_op jit(solution)/shard_map/all_to_all | solution.py:64
  136.4 3.3 %all-to-all-start.4 = ((bf16[8,16,256]{2,1,0:T(8,128)(2,1)}), bf16[8,16,256]{2,1,0:T(8,128)(2,1)S(1)}, u32[]{:S(2)}, u32[]{:S(2)}) async-start(bf16[8,16,256]{2,1,0:T(8,128)(2,1)} %bitcast.74), calls=%async_computation.4 | async-start | bytes 131072 | tf_op jit(solution)/shard_map/all_to_all | solution.py:64
  139.7 2.3 %convolution_convert_fusion = bf16[128,4608]{1,0:T(8,128)(2,1)} fusion(bf16[128,256]{1,0:T(8,128)(2,1)} %get-tuple-element.8, bf16[1,256,4608]{2,1,0:T(8,128)(2,1)S(1)} %copy-done), kind=kOutput, calls=%fused_computation | convolution fusion | flops 302579712 | bytes 3604480 | tf_op jit(solution)/shard_map/dot_general | solution.py:22
  142.1 4.5 %all-to-all-done.4 = bf16[8,16,256]{2,1,0:T(8,128)(2,1)S(1)} async-done(((bf16[8,16,256]{2,1,0:T(8,128)(2,1)}), bf16[8,16,256]{2,1,0:T(8,128)(2,1)S(1)}, u32[]{:S(2)}, u32[]{:S(2)}) %all-to-all-start.4) | async-done | bytes 65568 | tf_op jit(solution)/shard_map/all_to_all | solution.py:64
  147.2 3.6 %all-to-all-start.6 = ((bf16[8,16,4608]{2,1,0:T(8,128)(2,1)}), bf16[8,16,4608]{2,1,0:T(8,128)(2,1)S(1)}, u32[]{:S(2)}, u32[]{:S(2)}) async-start(bf16[8,16,4608]{2,1,0:T(8,128)(2,1)} %bitcast.13), calls=%async_computation.6 | async-start | bytes 2359296 | tf_op jit(solution)/shard_map/all_to_all | solution.py:65
  151.5 1.6 reshape.207
  153.1 1.5 reshape.206
  154.6 1.4 multiply_reduce_fusion
  156.0 1.0 convolution_multiply_fusion.3
  157.0 1.6 fusion.15
  158.6 1.5 select_n.81
  160.1 16.3 %all-to-all-done.6 = bf16[8,16,4608]{2,1,0:T(8,128)(2,1)S(1)} async-done(((bf16[8,16,4608]{2,1,0:T(8,128)(2,1)}), bf16[8,16,4608]{2,1,0:T(8,128)(2,1)S(1)}, u32[]{:S(2)}, u32[]{:S(2)}) %all-to-all-start.6) | async-done | bytes 1179680 | tf_op jit(solution)/shard_map/all_to_all | solution.py:65
  176.3 1.8 %fusion.17 = bf16[1,16,4608]{2,1,0:T(8,128)(2,1)} fusion(bf16[16,4608]{1,0:T(8,128)(2,1)} %copy-done.2, bf16[16,4608]{1,0:T(8,128)(2,1)} %copy-done.1, bf16[128,16]{0,1:T(8,128)(2,1)S(1)} %fusion.19, bf16[128,4608]{1,0:T(8,128)(2,1)S(1)} %bitcast.69, f32[4608]{0:T(1024)} %reduce.1, f32[16]{0:T(128)S(1)} %bitcast.76, pred[]{:T(512)S(6)} %eq.42, pred[]{:T(512)S(6)} %eq.29), kind=kOutput, calls=%fused_computation.24 | convolution fusion | flops 19390464 | bytes 1644610 | tf_op jit(solution)/shard_map/dot_general | solution.py:78
  (36 shorter events, 6.0 us)
Async XLA Ops:
  0.6 53.4 %copy-start = (bf16[1,256,4608]{2,1,0:T(8,128)(2,1)S(1)}, bf16[1,256,4608]{2,1,0:T(8,128)(2,1)}, u32[]{:S(2)}) copy-start(bf16[1,256,4608]{2,1,0:T(8,128)(2,1)} %param.11) | copy-start | bytes 7077892
  3.9 15.2 %copy-start.3 = (bf16[128,128]{1,0:T(8,128)(2,1)}, bf16[128,128]{1,0:T(8,128)(2,1)S(1)}, u32[]{:S(2)}) copy-start(bf16[128,128]{1,0:T(8,128)(2,1)S(1)} %reshape_squeeze.2) | copy-start | bytes 98308
  5.0 14.2 %all-to-all-start = ((bf16[8,16,256]{2,1,0:T(8,128)(2,1)}), bf16[8,16,256]{2,1,0:T(8,128)(2,1)S(1)}, u32[]{:S(2)}, u32[]{:S(2)}) async-start(bf16[8,16,256]{2,1,0:T(8,128)(2,1)} %mul.119), calls=%async_computation | async-start | bytes 131072 | tf_op jit(solution)/shard_map/all_to_all | solution.py:60
  19.1 0.6 copy-start.5
  19.8 31.1 %all-to-all-start.1 = ((bf16[8,16,4608]{2,1,0:T(8,128)(2,1)}), bf16[8,16,4608]{2,1,0:T(8,128)(2,1)S(1)}, u32[]{:S(2)}, u32[]{:S(2)}) async-start(bf16[8,16,4608]{2,1,0:T(8,128)(2,1)} %bitcast.70), calls=%async_computation.1 | async-start | bytes 2359296 | tf_op jit(solution)/shard_map/all_to_all | solution.py:59
  55.5 32.3 %copy-start.6 = (f32[1,16]{1,0:T(1,128)S(1)}, f32[1,16]{1,0:T(1,128)}, u32[]{:S(2)}) copy-start(f32[1,16]{1,0:T(1,128)} %param.13) | copy-start | bytes 196
  55.5 32.3 %all-to-all-start.2 = ((bf16[8,16,4608]{2,1,0:T(8,128)(2,1)}), bf16[8,16,4608]{2,1,0:T(8,128)(2,1)S(1)}, u32[]{:S(2)}, u32[]{:S(2)}) async-start(bf16[8,16,4608]{2,1,0:T(8,128)(2,1)} %bitcast.7), calls=%async_computation.2 | async-start | bytes 2359296 | tf_op jit(solution)/shard_map/all_to_all | solution.py:65
  89.0 1.3 copy-start.1
  89.1 3.3 %collective-permute-start = (bf16[16,4608]{1,0:T(8,128)(2,1)S(1)}, bf16[16,4608]{1,0:T(8,128)(2,1)S(1)}, u32[]{:S(2)}, u32[]{:S(2)}) collective-permute-start(bf16[16,4608]{1,0:T(8,128)(2,1)S(1)} %fusion.1), channel_id=1, source_target_pairs={{1,0},{3,2},{5,4},{7,6},{9,8},{11,10},{13,12},{15,14},{17,16},{19,... | collective-permute-start | bytes 442376 | tf_op jit(solution)/shard_map/ppermute | solution.py:10
  92.3 33.1 %copy-start.2 = (bf16[16,4608]{1,0:T(8,128)(2,1)}, bf16[16,4608]{1,0:T(8,128)(2,1)S(1)}, u32[]{:S(2)}) copy-start(bf16[16,4608]{1,0:T(8,128)(2,1)S(1)} %collective-permute-done) | copy-start | bytes 442372
  125.5 10.9 %all-to-all-start.5 = ((bf16[8,16,256]{2,1,0:T(8,128)(2,1)}), bf16[8,16,256]{2,1,0:T(8,128)(2,1)}, u32[]{:S(2)}, u32[]{:S(2)}) async-start(bf16[8,16,256]{2,1,0:T(8,128)(2,1)} %bitcast.73), calls=%async_computation.5 | async-start | bytes 131072 | tf_op jit(solution)/shard_map/all_to_all | solution.py:64
  136.4 10.2 %all-to-all-start.4 = ((bf16[8,16,256]{2,1,0:T(8,128)(2,1)}), bf16[8,16,256]{2,1,0:T(8,128)(2,1)S(1)}, u32[]{:S(2)}, u32[]{:S(2)}) async-start(bf16[8,16,256]{2,1,0:T(8,128)(2,1)} %bitcast.74), calls=%async_computation.4 | async-start | bytes 131072 | tf_op jit(solution)/shard_map/all_to_all | solution.py:64
  146.6 0.6 copy-start.4
  147.2 29.2 %all-to-all-start.6 = ((bf16[8,16,4608]{2,1,0:T(8,128)(2,1)}), bf16[8,16,4608]{2,1,0:T(8,128)(2,1)S(1)}, u32[]{:S(2)}, u32[]{:S(2)}) async-start(bf16[8,16,4608]{2,1,0:T(8,128)(2,1)} %bitcast.13), calls=%async_computation.6 | async-start | bytes 2359296 | tf_op jit(solution)/shard_map/all_to_all | solution.py:65
where the time goes:
time: 179 us; the launch traced here: 178 us
  waiting for transfers between devices  83.3 us (47%)
  blocking collectives  32.7 us (18%)
  starting transfers between devices  26.7 us (15%)
  matrix products  19.1 us (11%)
  local copies, waits for them, and re-layouts  9.44 us (5%)
  other arithmetic  6.2 us (3%)
    all_to_all x2, waiting for transfers between devices, layer_pass(): lax.all_to_all(contrib_here, 'dict', split_axis=0, concat_axis=0, tiled=T...  43.5 us
    all_to_all x1, blocking collectives, layer_pass(): lax.all_to_all(send_g, 'dict', split_axis=0, concat_axis=0, tiled=True)  32.7 us
    all_to_all x1, waiting for transfers between devices, layer_pass(): lax.all_to_all(send_g, 'dict', split_axis=0, concat_axis=0, tiled=True)  26.1 us
    all_to_all x2, waiting for transfers between devices, layer_pass(): lax.all_to_all(coef_here, 'dict', split_axis=0, concat_axis=0, tiled=True)  8.21 us
    all_to_all x2, starting transfers between devices, layer_pass(): lax.all_to_all(coef_here, 'dict', split_axis=0, concat_axis=0, tiled=True)  7.32 us
    all_to_all x2, starting transfers between devices, layer_pass(): lax.all_to_all(contrib_here, 'dict', split_axis=0, concat_axis=0, tiled=T...  7.26 us
    all_to_all x1, starting transfers between devices, layer_pass(): lax.all_to_all(send_act, 'dict', split_axis=0, concat_axis=0, tiled=True)  7.25 us
    dot_general x2, matrix products, owner_work(): lax.dot_general(flat_g, dec_local, (((1,), (1,)), ((), ())), preferred_el...  6.37 us
  transfers between devices with their start and end apart: 7, of which 7 were waited for; matrix products, arithmetic and copies ran while one was open for 12% of the time, Pallas kernels for 0%

commit v1 on v0

--- a/solution.py
+++ b/solution.py
@@ -84,7 +84,7 @@
     return (attr, new_g)
 
 
-def per_device(cotangent, routes, acts, decoder, encoder, gain, inv_rms):
+def slot_device(cotangent, routes, acts, decoder, encoder, gain, inv_rms):
     peers = lax.axis_size("dict")
     depth = lax.axis_size("section")
     here = lax.axis_index("section")
@@ -112,6 +112,112 @@
     return (attr_keep[None], grad_keep[None])
 
 
+def swap_cores(block):
+    return lax.ppermute(block, "section", [(0, 1), (1, 0)])
+
+
+def exchange(parts, sign):
+    peers = parts.shape[0]
+    moved = [parts[0]]
+    for shift in range(1, peers):
+        route = [(d, (d + sign * shift) % peers) for d in range(peers)]
+        moved.append(lax.ppermute(parts[shift], "dict", route))
+    return jnp.stack(moved, axis=0)
+
+
+def split_layer(g_half, routes_l, acts_l, dec_half, enc_half, gain_half, scale_l):
+    peers = lax.axis_size("dict")
+    me = lax.axis_index("dict")
+    rows, listed = routes_l.shape
+    block = acts_l.shape[1] // listed
+    held = dec_half.shape[0] // block
+    half = g_half.shape[1]
+    owner = routes_l // held
+    within = routes_l - owner * held
+    rel = (owner - me) % peers
+    shifts = jnp.arange(peers, dtype=jnp.int32)
+    spots = jnp.arange(held, dtype=jnp.int32)
+    at_rel = (rel[:, :, None] == shifts[None, None, :]).astype(jnp.bfloat16)
+    at_spot = (within[:, :, None] == spots[None, None, :]).astype(jnp.bfloat16)
+    act_grid = acts_l.reshape(rows, listed, block)
+    placed = jnp.einsum(
+        "rks,rkw,rkj->srwj", at_rel, at_spot, act_grid, preferred_element_type=jnp.float32
+    ).astype(jnp.bfloat16).reshape(peers, rows, held * block)
+    sent = jnp.concatenate(
+        [jnp.broadcast_to(g_half[None], (peers, rows, half)), placed], axis=-1
+    )
+    got = exchange(sent, 1).reshape(peers * rows, half + held * block)
+    g_all = got[:, :half]
+    act_all = got[:, half:]
+    part = lax.dot_general(
+        g_all, dec_half, (((1,), (1,)), ((), ())), preferred_element_type=jnp.float32
+    )
+    coef = (part + swap_cores(part)).astype(jnp.bfloat16)
+    dz = jnp.where(act_all > 0, coef, jnp.zeros_like(coef))
+    contrib = jnp.dot(dz, enc_half, preferred_element_type=jnp.float32).astype(jnp.bfloat16)
+    dz_pick = dz[:, :block]
+    for spot in range(1, held):
+        dz_pick = dz_pick + dz[:, spot * block:(spot + 1) * block]
+    back = jnp.concatenate([contrib, dz_pick], axis=-1).reshape(peers, rows, half + block)
+    returned = exchange(back, -1)
+    total = jnp.sum(returned[:, :, :half].astype(jnp.float32), axis=0)
+    dz_back = returned[:, :, half:]
+    dz_slot = jnp.einsum("rks,srj->rkj", at_rel, dz_back, preferred_element_type=jnp.float32)
+    attr = (act_grid.astype(jnp.float32) * dz_slot).reshape(rows, listed * block)
+    new_half = (g_half.astype(jnp.float32) + scale_l[:, None] * gain_half[None, :] * total).astype(
+        jnp.bfloat16
+    )
+    return attr, new_half
+
+
+def split_device(cotangent, routes, acts, decoder, encoder, gain, inv_rms):
+    depth = lax.axis_size("section")
+    here = lax.axis_index("section")
+    rows, width = cotangent.shape
+    half = width // depth
+    mine = here * half
+    theirs = (1 - here) * half
+    weights = jnp.stack([decoder[0], encoder[0]], axis=0)
+    own_w = lax.dynamic_slice_in_dim(weights, mine, half, axis=2)
+    other_w = swap_cores(lax.dynamic_slice_in_dim(weights, theirs, half, axis=2))
+    small = jnp.concatenate(
+        [gain[0], inv_rms[0], routes[0].reshape(-1).astype(jnp.float32)], axis=0
+    )
+    other_small = swap_cores(small)
+    other_acts = swap_cores(acts[0])
+    attr_keep = jnp.zeros((rows, acts.shape[2]), jnp.float32)
+    grad_keep = jnp.zeros(cotangent.shape, jnp.bfloat16)
+    g_half = lax.dynamic_slice_in_dim(cotangent, mine, half, axis=1)
+    for layer in reversed(range(depth)):
+        is_own = here == layer
+        w = jnp.where(is_own, own_w, other_w)
+        s = jnp.where(is_own, small, other_small)
+        acts_l = jnp.where(is_own, acts[0], other_acts)
+        gain_half = lax.dynamic_slice_in_dim(s[:width], mine, half, axis=0)
+        scale_l = s[width:width + rows]
+        routes_l = s[width + rows:].astype(jnp.int32).reshape(routes.shape[1:])
+        attr, g_half = split_layer(g_half, routes_l, acts_l, w[0], w[1], gain_half, scale_l)
+        partner = swap_cores(g_half)
+        full = jnp.where(
+            here == 0,
+            jnp.concatenate([g_half, partner], axis=1),
+            jnp.concatenate([partner, g_half], axis=1),
+        )
+        attr_keep = jnp.where(is_own, attr, attr_keep)
+        grad_keep = jnp.where(is_own, full, grad_keep)
+    return (attr_keep[None], grad_keep[None])
+
+
+def per_device(cotangent, routes, acts, decoder, encoder, gain, inv_rms):
+    peers = lax.axis_size("dict")
+    depth = lax.axis_size("section")
+    listed = routes.shape[-1]
+    width = cotangent.shape[1]
+    if listed == peers and depth == 2 and width % (depth * 128) == 0:
+        return split_device(cotangent, routes, acts, decoder, encoder, gain, inv_rms)
+    return slot_device(cotangent, routes, acts, decoder, encoder, gain, inv_rms)
+
+
 def solution(mesh):
     placed = (
         P(("groups", "dict"), None),

time: 179 us -> 112 us (0.63)
  waiting for transfers between devices: 83.3 us -> 26.8 us
  blocking collectives: 32.7 us -> 0 us
  starting transfers between devices: 26.7 us -> 59 us
  matrix products: 19.1 us -> 3.71 us
  local copies, waits for them, and re-layouts: 9.44 us -> 14.7 us
    all_to_all x6 -> x0, waiting for transfers between devices: 81.4 us -> none  [the longest x2 43.5 us: layer_pass(): lax.all_to_all(contrib_here, 'dict', split_axis=0, concat_axis=0, tiled=T...]
    ppermute x1 -> x35, starting transfers between devices: 1.29 us -> 59 us  [the longest x28 57.1 us: exchange(): moved.append(lax.ppermute(parts[shift], 'dict', route))]
    all_to_all x1 -> x0, blocking collectives: 32.7 us -> none  [layer_pass(): lax.all_to_all(send_g, 'dict', split_axis=0, concat_axis=0, tiled=True)]
    all_to_all x6 -> x0, starting transfers between devices: 25.4 us -> none  [the longest x2 7.32 us: layer_pass(): lax.all_to_all(coef_here, 'dict', split_axis=0, concat_axis=0, tiled=True)]
    ppermute x1 -> x35, waiting for transfers between devices: 1.96 us -> 26.8 us  [the longest x28 20.9 us: exchange(): moved.append(lax.ppermute(parts[shift], 'dict', route))]
    dot_general x12 -> x8, matrix products: 19.1 us -> 3.71 us  [the longest x2 1.94 us: split_layer(): jnp.dot(dz, enc_half, preferred_element_type=jnp.float32)]
    unnamed x15 -> x43, local copies, waits for them, and re-layouts: 2.02 us -> 8.86 us
    select_n x1 -> x5, other arithmetic: 0.85 us -> 4.93 us  [the longest x1 3.28 us: split_device(): w = jnp.where(is_own, own_w, other_w)]
  transfers between devices with their start and end apart: 7 -> 35, of which waited for: 7 -> 14; matrix products, arithmetic and copies ran while one was open for 12% -> 14% of each run, Pallas kernels for 0% -> 0%
where the time goes in v1:
time: 112 us
  starting transfers between devices  59 us (53%)
  waiting for transfers between devices  26.8 us (24%)
  local copies, waits for them, and re-layouts  14.7 us (13%)
  other arithmetic  6.55 us (6%)
  matrix products  3.71 us (3%)
    ppermute x28, starting transfers between devices, exchange(): moved.append(lax.ppermute(parts[shift], 'dict', route))  57.1 us
    ppermute x28, waiting for transfers between devices, exchange(): moved.append(lax.ppermute(parts[shift], 'dict', route))  20.9 us
    unnamed x43, local copies, waits for them, and re-layouts  8.86 us
    ppermute x7, waiting for transfers between devices, swap_cores(): return lax.ppermute(block, 'section', [(0, 1), (1, 0)])  5.86 us
    select_n x1, other arithmetic, split_device(): w = jnp.where(is_own, own_w, other_w)  3.28 us
  transfers between devices with their start and end apart: 35, of which 14 were waited for; matrix products, arithmetic and copies ran while one was open for 14% of the time, Pallas kernels for 0%

profile of v1, /device:TPU:0, one launch (start us, length us, event | category | flops | bytes accessed | tf_op | source)
XLA Modules:
  0.0 111.8 jit_solution(7205811518248280423)
XLA Ops:
  1.1 3.4 %constant_dynamic-update-slice_fusion.1 = bf16[2,256,4608]{2,1,0:T(8,128)(2,1)} fusion(bf16[1,256,4608]{2,1,0:T(8,128)(2,1)} %param.10), kind=kLoop, calls=%fused_computation.165 | loop fusion | bytes 4718592
  4.5 1.6 %constant_dynamic-update-slice_fusion = bf16[2,256,4608]{2,1,0:T(8,128)(2,1)} fusion(bf16[2,256,4608]{2,1,0:T(8,128)(2,1)} %constant_dynamic-update-slice_fusion.1, bf16[1,256,4608]{2,1,0:T(8,128)(2,1)S(1)} %copy-done.1), kind=kLoop, calls=%fused_computation.164 | loop fusion | bytes 4718592 | tf_op jit(solution)/shard_map/stack | solution.py:180
  6.1 1.9 %constant_dynamic-slice_fusion = bf16[2,256,2304]{2,1,0:T(8,128)(2,1)S(1)} fusion(bf16[2,256,4608]{2,1,0:T(8,128)(2,1)} %constant_dynamic-update-slice_fusion, s32[]{:T(128)S(6)} %select_n.174), kind=kLoop, calls=%fused_computation.215 | loop fusion | bytes 4718596 | tf_op jit(solution)/shard_map/dynamic_slice | solution.py:182
  9.0 3.7 %collective-permute-done.1 = f32[4752]{0:T(1024)S(1)} collective-permute-done((f32[4752]{0:T(1024)S(1)}, f32[4752]{0:T(1024)S(1)}, u32[]{:S(2)}, u32[]{:S(2)}) %collective-permute-start.1) | collective-permute-done | bytes 19040 | tf_op jit(solution)/shard_map/ppermute | solution.py:116
  14.4 2.6 %collective-permute-start.2 = (bf16[16,2560]{1,0:T(8,128)(2,1)S(1)}, bf16[16,2560]{1,0:T(8,128)(2,1)S(1)}, u32[]{:S(2)}, u32[]{:S(2)}) collective-permute-start(bf16[16,2560]{1,0:T(8,128)(2,1)S(1)} %get-tuple-element.14), channel_id=1, source_target_pairs={{0,2},{2,4},{4,6},{6,8},{8,10},{10,12},{12,14},{14,0},{1,3},{3,5},... | collective-permute-start | bytes 245768 | tf_op jit(solution)/shard_map/ppermute | solution.py:124
  17.2 1.6 %collective-permute-start.3 = (bf16[16,2560]{1,0:T(8,128)(2,1)S(1)}, bf16[16,2560]{1,0:T(8,128)(2,1)S(1)}, u32[]{:S(2)}, u32[]{:S(2)}) collective-permute-start(bf16[16,2560]{1,0:T(8,128)(2,1)S(1)} %get-tuple-element.15), channel_id=1, source_target_pairs={{0,4},{2,6},{4,8},{6,10},{8,12},{10,14},{12,0},{14,2},{1,5},{3,7},... | collective-permute-start | bytes 245768 | tf_op jit(solution)/shard_map/ppermute | solution.py:124
  18.8 2.6 %collective-permute-start.4 = (bf16[16,2560]{1,0:T(8,128)(2,1)S(1)}, bf16[16,2560]{1,0:T(8,128)(2,1)S(1)}, u32[]{:S(2)}, u32[]{:S(2)}) collective-permute-start(bf16[16,2560]{1,0:T(8,128)(2,1)S(1)} %get-tuple-element.16), channel_id=1, source_target_pairs={{0,6},{2,8},{4,10},{6,12},{8,14},{10,0},{12,2},{14,4},{1,7},{3,9},... | collective-permute-start | bytes 245768 | tf_op jit(solution)/shard_map/ppermute | solution.py:124
  21.4 1.2 %collective-permute-start.5 = (bf16[16,2560]{1,0:T(8,128)(2,1)S(1)}, bf16[16,2560]{1,0:T(8,128)(2,1)S(1)}, u32[]{:S(2)}, u32[]{:S(2)}) collective-permute-start(bf16[16,2560]{1,0:T(8,128)(2,1)S(1)} %get-tuple-element.17), channel_id=1, source_target_pairs={{0,8},{2,10},{4,12},{6,14},{8,0},{10,2},{12,4},{14,6},{1,9},{3,11}... | collective-permute-start | bytes 245768 | tf_op jit(solution)/shard_map/ppermute | solution.py:124
  23.3 1.9 %collective-permute-start.6 = (bf16[16,2560]{1,0:T(8,128)(2,1)S(1)}, bf16[16,2560]{1,0:T(8,128)(2,1)S(1)}, u32[]{:S(2)}, u32[]{:S(2)}) collective-permute-start(bf16[16,2560]{1,0:T(8,128)(2,1)S(1)} %get-tuple-element.18), channel_id=1, source_target_pairs={{0,10},{2,12},{4,14},{6,0},{8,2},{10,4},{12,6},{14,8},{1,11},{3,13... | collective-permute-start | bytes 245768 | tf_op jit(solution)/shard_map/ppermute | solution.py:124
  25.9 1.3 %collective-permute-start.7 = (bf16[16,2560]{1,0:T(8,128)(2,1)S(1)}, bf16[16,2560]{1,0:T(8,128)(2,1)S(1)}, u32[]{:S(2)}, u32[]{:S(2)}) collective-permute-start(bf16[16,2560]{1,0:T(8,128)(2,1)S(1)} %get-tuple-element.19), channel_id=1, source_target_pairs={{0,12},{2,14},{4,0},{6,2},{8,4},{10,6},{12,8},{14,10},{1,13},{3,15... | collective-permute-start | bytes 245768 | tf_op jit(solution)/shard_map/ppermute | solution.py:124
  27.8 2.4 %collective-permute-done.4 = bf16[16,2560]{1,0:T(8,128)(2,1)S(1)} collective-permute-done((bf16[16,2560]{1,0:T(8,128)(2,1)S(1)}, bf16[16,2560]{1,0:T(8,128)(2,1)S(1)}, u32[]{:S(2)}, u32[]{:S(2)}) %collective-permute-start.4) | collective-permute-done | bytes 81952 | tf_op jit(solution)/shard_map/ppermute | solution.py:124
  30.2 5.0 %collective-permute-start.8 = (bf16[16,2560]{1,0:T(8,128)(2,1)S(1)}, bf16[16,2560]{1,0:T(8,128)(2,1)S(1)}, u32[]{:S(2)}, u32[]{:S(2)}) collective-permute-start(bf16[16,2560]{1,0:T(8,128)(2,1)S(1)} %get-tuple-element.12), channel_id=1, source_target_pairs={{0,14},{2,0},{4,2},{6,4},{8,6},{10,8},{12,10},{14,12},{1,15},{3,1}... | collective-permute-start | bytes 245768 | tf_op jit(solution)/shard_map/ppermute | solution.py:124
  38.5 3.3 %broadcast_select_fusion.1 = (bf16[2,256,2304]{2,1,0:T(8,128)(2,1)S(1)}, bf16[2,256,2304]{2,1,0:T(8,128)(2,1)S(1)}) fusion(bf16[2,256,2304]{2,1,0:T(8,128)(2,1)} %collective-permute-done.9, pred[]{:T(512)S(6)} %eq.67, bf16[2,256,4608]{2,1,0:T(8,128)(2,1)} %constant_dynamic-update-slice_fusion, s32[]{:T(128)S(6)} %select_n.166, pred[]{:T(512)S(6)} %eq.31), kind=kLoop, calls=%fused_computation.3 | loop fusion | flops 2359296 | bytes 9437190 | tf_op jit(solution)/shard_map/jit(_where)/select_n | solution.py:193
  41.8 1.4 %copy-done = bf16[2,256,2304]{2,1,0:T(8,128)(2,1)} copy-done((bf16[2,256,2304]{2,1,0:T(8,128)(2,1)}, bf16[2,256,2304]{2,1,0:T(8,128)(2,1)S(1)}, u32[]{:S(2)}) %copy-start) | copy-done | bytes 2359320
  46.0 1.6 %convolution_convert_fusion.1 = bf16[128,2304]{1,0:T(8,128)(2,1)S(1)} fusion(bf16[128,256]{1,0:T(8,128)(2,1)S(1)} %compare_select_fusion.1, bf16[2,256,2304]{2,1,0:T(8,128)(2,1)} %copy-done), kind=kOutput, calls=%fused_computation.1 | convolution fusion | flops 151289856 | bytes 1835008 | tf_op jit(solution)/shard_map/dot_general | solution.py:157
  47.7 4.6 %collective-permute-start.11 = (bf16[16,2432]{1,0:T(8,128)(2,1)S(1)}, bf16[16,2432]{1,0:T(8,128)(2,1)S(1)}, u32[]{:S(2)}, u32[]{:S(2)}) collective-permute-start(bf16[16,2432]{1,0:T(8,128)(2,1)S(1)} %get-tuple-element.28), channel_id=1, source_target_pairs={{0,14},{2,0},{4,2},{6,4},{8,6},{10,8},{12,10},{14,12},{1,15},{3,1}... | collective-permute-start | bytes 233480 | tf_op jit(solution)/shard_map/ppermute | solution.py:124
  52.4 2.9 %collective-permute-start.14 = (bf16[16,2432]{1,0:T(8,128)(2,1)S(1)}, bf16[16,2432]{1,0:T(8,128)(2,1)S(1)}, u32[]{:S(2)}, u32[]{:S(2)}) collective-permute-start(bf16[16,2432]{1,0:T(8,128)(2,1)S(1)} %get-tuple-element.31), channel_id=1, source_target_pairs={{0,8},{2,10},{4,12},{6,14},{8,0},{10,2},{12,4},{14,6},{1,9},{3,11}... | collective-permute-start | bytes 233480 | tf_op jit(solution)/shard_map/ppermute | solution.py:124
  55.3 2.0 %collective-permute-start.16 = (bf16[16,2432]{1,0:T(8,128)(2,1)S(1)}, bf16[16,2432]{1,0:T(8,128)(2,1)S(1)}, u32[]{:S(2)}, u32[]{:S(2)}) collective-permute-start(bf16[16,2432]{1,0:T(8,128)(2,1)S(1)} %get-tuple-element.33), channel_id=1, source_target_pairs={{0,4},{2,6},{4,8},{6,10},{8,12},{10,14},{12,0},{14,2},{1,5},{3,7},... | collective-permute-start | bytes 233480 | tf_op jit(solution)/shard_map/ppermute | solution.py:124
  57.3 1.5 %collective-permute-start.17 = (bf16[16,2432]{1,0:T(8,128)(2,1)S(1)}, bf16[16,2432]{1,0:T(8,128)(2,1)S(1)}, u32[]{:S(2)}, u32[]{:S(2)}) collective-permute-start(bf16[16,2432]{1,0:T(8,128)(2,1)S(1)} %get-tuple-element.27), channel_id=1, source_target_pairs={{0,2},{2,4},{4,6},{6,8},{8,10},{10,12},{12,14},{14,0},{1,3},{3,5},... | collective-permute-start | bytes 233480 | tf_op jit(solution)/shard_map/ppermute | solution.py:124
  58.8 6.2 %collective-permute-done.14 = bf16[16,2432]{1,0:T(8,128)(2,1)S(1)} collective-permute-done((bf16[16,2432]{1,0:T(8,128)(2,1)S(1)}, bf16[16,2432]{1,0:T(8,128)(2,1)S(1)}, u32[]{:S(2)}, u32[]{:S(2)}) %collective-permute-start.14) | collective-permute-done | bytes 77856 | tf_op jit(solution)/shard_map/ppermute | solution.py:124
  65.0 3.5 %collective-permute-done.15 = bf16[16,2432]{1,0:T(8,128)(2,1)S(1)} collective-permute-done((bf16[16,2432]{1,0:T(8,128)(2,1)S(1)}, bf16[16,2432]{1,0:T(8,128)(2,1)S(1)}, u32[]{:S(2)}, u32[]{:S(2)}) %collective-permute-start.15) | collective-permute-done | bytes 77856 | tf_op jit(solution)/shard_map/ppermute | solution.py:124
  69.0 2.2 %collective-permute-start.20 = (bf16[16,2560]{1,0:T(8,128)(2,1)S(1)}, bf16[16,2560]{1,0:T(8,128)(2,1)S(1)}, u32[]{:S(2)}, u32[]{:S(2)}) collective-permute-start(bf16[16,2560]{1,0:T(8,128)(2,1)S(1)} %get-tuple-element.8), channel_id=1, source_target_pairs={{0,6},{2,8},{4,10},{6,12},{8,14},{10,0},{12,2},{14,4},{1,7},{3,9},... | collective-permute-start | bytes 245768 | tf_op jit(solution)/shard_map/ppermute | solution.py:124
  71.1 3.0 %collective-permute-start.21 = (bf16[16,2560]{1,0:T(8,128)(2,1)S(1)}, bf16[16,2560]{1,0:T(8,128)(2,1)S(1)}, u32[]{:S(2)}, u32[]{:S(2)}) collective-permute-start(bf16[16,2560]{1,0:T(8,128)(2,1)S(1)} %get-tuple-element.9), channel_id=1, source_target_pairs={{0,8},{2,10},{4,12},{6,14},{8,0},{10,2},{12,4},{14,6},{1,9},{3,11}... | collective-permute-start | bytes 245768 | tf_op jit(solution)/shard_map/ppermute | solution.py:124
  74.2 2.8 %collective-permute-done.18 = bf16[16,2560]{1,0:T(8,128)(2,1)S(1)} collective-permute-done((bf16[16,2560]{1,0:T(8,128)(2,1)S(1)}, bf16[16,2560]{1,0:T(8,128)(2,1)S(1)}, u32[]{:S(2)}, u32[]{:S(2)}) %collective-permute-start.18) | collective-permute-done | bytes 81952 | tf_op jit(solution)/shard_map/ppermute | solution.py:124
  77.1 2.3 %collective-permute-start.24 = (bf16[16,2560]{1,0:T(8,128)(2,1)S(1)}, bf16[16,2560]{1,0:T(8,128)(2,1)S(1)}, u32[]{:S(2)}, u32[]{:S(2)}) collective-permute-start(bf16[16,2560]{1,0:T(8,128)(2,1)S(1)} %get-tuple-element.4), channel_id=1, source_target_pairs={{0,14},{2,0},{4,2},{6,4},{8,6},{10,8},{12,10},{14,12},{1,15},{3,1}... | collective-permute-start | bytes 245768 | tf_op jit(solution)/shard_map/ppermute | solution.py:124
  79.4 2.4 %collective-permute-done.20 = bf16[16,2560]{1,0:T(8,128)(2,1)S(1)} collective-permute-done((bf16[16,2560]{1,0:T(8,128)(2,1)S(1)}, bf16[16,2560]{1,0:T(8,128)(2,1)S(1)}, u32[]{:S(2)}, u32[]{:S(2)}) %collective-permute-start.20) | collective-permute-done | bytes 81952 | tf_op jit(solution)/shard_map/ppermute | solution.py:124
  84.8 7.1 %collective-permute-start.26 = (bf16[16,2432]{1,0:T(8,128)(2,1)S(1)}, bf16[16,2432]{1,0:T(8,128)(2,1)S(1)}, u32[]{:S(2)}, u32[]{:S(2)}) collective-permute-start(bf16[16,2432]{1,0:T(8,128)(2,1)S(1)} %get-tuple-element.21), channel_id=1, source_target_pairs={{0,14},{2,0},{4,2},{6,4},{8,6},{10,8},{12,10},{14,12},{1,15},{3,1}... | collective-permute-start | bytes 233480 | tf_op jit(solution)/shard_map/ppermute | solution.py:124
  92.0 1.9 %collective-permute-start.27 = (bf16[16,2432]{1,0:T(8,128)(2,1)S(1)}, bf16[16,2432]{1,0:T(8,128)(2,1)S(1)}, u32[]{:S(2)}, u32[]{:S(2)}) collective-permute-start(bf16[16,2432]{1,0:T(8,128)(2,1)S(1)} %get-tuple-element.22), channel_id=1, source_target_pairs={{0,12},{2,14},{4,0},{6,2},{8,4},{10,6},{12,8},{14,10},{1,13},{3,15... | collective-permute-start | bytes 233480 | tf_op jit(solution)/shard_map/ppermute | solution.py:124
  95.0 2.3 %collective-permute-start.30 = (bf16[16,2432]{1,0:T(8,128)(2,1)S(1)}, bf16[16,2432]{1,0:T(8,128)(2,1)S(1)}, u32[]{:S(2)}, u32[]{:S(2)}) collective-permute-start(bf16[16,2432]{1,0:T(8,128)(2,1)S(1)} %get-tuple-element.25), channel_id=1, source_target_pairs={{0,6},{2,8},{4,10},{6,12},{8,14},{10,0},{12,2},{14,4},{1,7},{3,9},... | collective-permute-start | bytes 233480 | tf_op jit(solution)/shard_map/ppermute | solution.py:124
  97.3 1.9 %collective-permute-start.31 = (bf16[16,2432]{1,0:T(8,128)(2,1)S(1)}, bf16[16,2432]{1,0:T(8,128)(2,1)S(1)}, u32[]{:S(2)}, u32[]{:S(2)}) collective-permute-start(bf16[16,2432]{1,0:T(8,128)(2,1)S(1)} %get-tuple-element.26), channel_id=1, source_target_pairs={{0,4},{2,6},{4,8},{6,10},{8,12},{10,14},{12,0},{14,2},{1,5},{3,7},... | collective-permute-start | bytes 233480 | tf_op jit(solution)/shard_map/ppermute | solution.py:124
  99.6 7.7 %collective-permute-start.32 = (bf16[16,2432]{1,0:T(8,128)(2,1)S(1)}, bf16[16,2432]{1,0:T(8,128)(2,1)S(1)}, u32[]{:S(2)}, u32[]{:S(2)}) collective-permute-start(bf16[16,2432]{1,0:T(8,128)(2,1)S(1)} %get-tuple-element.20), channel_id=1, source_target_pairs={{0,2},{2,4},{4,6},{6,8},{8,10},{10,12},{12,14},{14,0},{1,3},{3,5},... | collective-permute-start | bytes 233480 | tf_op jit(solution)/shard_map/ppermute | solution.py:124
  107.3 1.4 %collective-permute-done.30 = bf16[16,2432]{1,0:T(8,128)(2,1)S(1)} collective-permute-done((bf16[16,2432]{1,0:T(8,128)(2,1)S(1)}, bf16[16,2432]{1,0:T(8,128)(2,1)S(1)}, u32[]{:S(2)}, u32[]{:S(2)}) %collective-permute-start.30) | collective-permute-done | bytes 77856 | tf_op jit(solution)/shard_map/ppermute | solution.py:124
  (143 shorter events, 19.4 us)
Async XLA Ops:
  0.6 12.7 %collective-permute-start = (bf16[16,1024]{1,0:T(8,128)(2,1)}, bf16[16,1024]{1,0:T(8,128)(2,1)S(1)}, u32[]{:S(2)}, u32[]{:S(2)}) collective-permute-start(bf16[16,1024]{1,0:T(8,128)(2,1)} %bitcast.152), channel_id=1, source_target_pairs={{0,1},{1,0},{2,3},{3,2},{4,5},{5,4},{6,7},{7,6},{8,9},{9,8},{10,11... | collective-permute-start | bytes 98312 | tf_op jit(solution)/shard_map/ppermute | solution.py:116
  8.1 30.4 %collective-permute-start.9 = (bf16[2,256,2304]{2,1,0:T(8,128)(2,1)S(1)}, bf16[2,256,2304]{2,1,0:T(8,128)(2,1)}, u32[]{:S(2)}, u32[]{:S(2)}) collective-permute-start(bf16[2,256,2304]{2,1,0:T(8,128)(2,1)S(1)} %constant_dynamic-slice_fusion), channel_id=1, source_target_pairs={{0,1},{1,0},{2,3},{3,2},{4,5},{5,4},{6,7},{7,6},{8,9},{9,8},{10,11... | collective-permute-start | bytes 7077896 | tf_op jit(solution)/shard_map/ppermute | solution.py:116
  8.5 4.2 %collective-permute-start.1 = (f32[4752]{0:T(1024)S(1)}, f32[4752]{0:T(1024)S(1)}, u32[]{:S(2)}, u32[]{:S(2)}) collective-permute-start(f32[4752]{0:T(1024)S(1)} %concatenate.63), channel_id=1, source_target_pairs={{0,1},{1,0},{2,3},{3,2},{4,5},{5,4},{6,7},{7,6},{8,9},{9,8},{10,11... | collective-permute-start | bytes 57032 | tf_op jit(solution)/shard_map/ppermute | solution.py:116
  14.4 8.9 %collective-permute-start.2 = (bf16[16,2560]{1,0:T(8,128)(2,1)S(1)}, bf16[16,2560]{1,0:T(8,128)(2,1)S(1)}, u32[]{:S(2)}, u32[]{:S(2)}) collective-permute-start(bf16[16,2560]{1,0:T(8,128)(2,1)S(1)} %get-tuple-element.14), channel_id=1, source_target_pairs={{0,2},{2,4},{4,6},{6,8},{8,10},{10,12},{12,14},{14,0},{1,3},{3,5},... | collective-permute-start | bytes 245768 | tf_op jit(solution)/shard_map/ppermute | solution.py:124
  17.2 8.7 %collective-permute-start.3 = (bf16[16,2560]{1,0:T(8,128)(2,1)S(1)}, bf16[16,2560]{1,0:T(8,128)(2,1)S(1)}, u32[]{:S(2)}, u32[]{:S(2)}) collective-permute-start(bf16[16,2560]{1,0:T(8,128)(2,1)S(1)} %get-tuple-element.15), channel_id=1, source_target_pairs={{0,4},{2,6},{4,8},{6,10},{8,12},{10,14},{12,0},{14,2},{1,5},{3,7},... | collective-permute-start | bytes 245768 | tf_op jit(solution)/shard_map/ppermute | solution.py:124
  18.8 11.4 %collective-permute-start.4 = (bf16[16,2560]{1,0:T(8,128)(2,1)S(1)}, bf16[16,2560]{1,0:T(8,128)(2,1)S(1)}, u32[]{:S(2)}, u32[]{:S(2)}) collective-permute-start(bf16[16,2560]{1,0:T(8,128)(2,1)S(1)} %get-tuple-element.16), channel_id=1, source_target_pairs={{0,6},{2,8},{4,10},{6,12},{8,14},{10,0},{12,2},{14,4},{1,7},{3,9},... | collective-permute-start | bytes 245768 | tf_op jit(solution)/shard_map/ppermute | solution.py:124
  21.4 14.5 %collective-permute-start.5 = (bf16[16,2560]{1,0:T(8,128)(2,1)S(1)}, bf16[16,2560]{1,0:T(8,128)(2,1)S(1)}, u32[]{:S(2)}, u32[]{:S(2)}) collective-permute-start(bf16[16,2560]{1,0:T(8,128)(2,1)S(1)} %get-tuple-element.17), channel_id=1, source_target_pairs={{0,8},{2,10},{4,12},{6,14},{8,0},{10,2},{12,4},{14,6},{1,9},{3,11}... | collective-permute-start | bytes 245768 | tf_op jit(solution)/shard_map/ppermute | solution.py:124
  23.3 13.2 %collective-permute-start.6 = (bf16[16,2560]{1,0:T(8,128)(2,1)S(1)}, bf16[16,2560]{1,0:T(8,128)(2,1)S(1)}, u32[]{:S(2)}, u32[]{:S(2)}) collective-permute-start(bf16[16,2560]{1,0:T(8,128)(2,1)S(1)} %get-tuple-element.18), channel_id=1, source_target_pairs={{0,10},{2,12},{4,14},{6,0},{8,2},{10,4},{12,6},{14,8},{1,11},{3,13... | collective-permute-start | bytes 245768 | tf_op jit(solution)/shard_map/ppermute | solution.py:124
  25.9 11.3 %collective-permute-start.7 = (bf16[16,2560]{1,0:T(8,128)(2,1)S(1)}, bf16[16,2560]{1,0:T(8,128)(2,1)S(1)}, u32[]{:S(2)}, u32[]{:S(2)}) collective-permute-start(bf16[16,2560]{1,0:T(8,128)(2,1)S(1)} %get-tuple-element.19), channel_id=1, source_target_pairs={{0,12},{2,14},{4,0},{6,2},{8,4},{10,6},{12,8},{14,10},{1,13},{3,15... | collective-permute-start | bytes 245768 | tf_op jit(solution)/shard_map/ppermute | solution.py:124
  30.2 7.6 %collective-permute-start.8 = (bf16[16,2560]{1,0:T(8,128)(2,1)S(1)}, bf16[16,2560]{1,0:T(8,128)(2,1)S(1)}, u32[]{:S(2)}, u32[]{:S(2)}) collective-permute-start(bf16[16,2560]{1,0:T(8,128)(2,1)S(1)} %get-tuple-element.12), channel_id=1, source_target_pairs={{0,14},{2,0},{4,2},{6,4},{8,6},{10,8},{12,10},{14,12},{1,15},{3,1}... | collective-permute-start | bytes 245768 | tf_op jit(solution)/shard_map/ppermute | solution.py:124
  47.7 7.6 %collective-permute-start.11 = (bf16[16,2432]{1,0:T(8,128)(2,1)S(1)}, bf16[16,2432]{1,0:T(8,128)(2,1)S(1)}, u32[]{:S(2)}, u32[]{:S(2)}) collective-permute-start(bf16[16,2432]{1,0:T(8,128)(2,1)S(1)} %get-tuple-element.28), channel_id=1, source_target_pairs={{0,14},{2,0},{4,2},{6,4},{8,6},{10,8},{12,10},{14,12},{1,15},{3,1}... | collective-permute-start | bytes 233480 | tf_op jit(solution)/shard_map/ppermute | solution.py:124
  52.3 5.0 %collective-permute-start.12 = (bf16[16,2432]{1,0:T(8,128)(2,1)S(1)}, bf16[16,2432]{1,0:T(8,128)(2,1)S(1)}, u32[]{:S(2)}, u32[]{:S(2)}) collective-permute-start(bf16[16,2432]{1,0:T(8,128)(2,1)S(1)} %get-tuple-element.29), channel_id=1, source_target_pairs={{0,12},{2,14},{4,0},{6,2},{8,4},{10,6},{12,8},{14,10},{1,13},{3,15... | collective-permute-start | bytes 233480 | tf_op jit(solution)/shard_map/ppermute | solution.py:124
  52.3 6.5 %collective-permute-start.13 = (bf16[16,2432]{1,0:T(8,128)(2,1)S(1)}, bf16[16,2432]{1,0:T(8,128)(2,1)S(1)}, u32[]{:S(2)}, u32[]{:S(2)}) collective-permute-start(bf16[16,2432]{1,0:T(8,128)(2,1)S(1)} %get-tuple-element.30), channel_id=1, source_target_pairs={{0,10},{2,12},{4,14},{6,0},{8,2},{10,4},{12,6},{14,8},{1,11},{3,13... | collective-permute-start | bytes 233480 | tf_op jit(solution)/shard_map/ppermute | solution.py:124
  52.4 12.7 %collective-permute-start.14 = (bf16[16,2432]{1,0:T(8,128)(2,1)S(1)}, bf16[16,2432]{1,0:T(8,128)(2,1)S(1)}, u32[]{:S(2)}, u32[]{:S(2)}) collective-permute-start(bf16[16,2432]{1,0:T(8,128)(2,1)S(1)} %get-tuple-element.31), channel_id=1, source_target_pairs={{0,8},{2,10},{4,12},{6,14},{8,0},{10,2},{12,4},{14,6},{1,9},{3,11}... | collective-permute-start | bytes 233480 | tf_op jit(solution)/shard_map/ppermute | solution.py:124
  55.3 13.2 %collective-permute-start.15 = (bf16[16,2432]{1,0:T(8,128)(2,1)S(1)}, bf16[16,2432]{1,0:T(8,128)(2,1)S(1)}, u32[]{:S(2)}, u32[]{:S(2)}) collective-permute-start(bf16[16,2432]{1,0:T(8,128)(2,1)S(1)} %get-tuple-element.32), channel_id=1, source_target_pairs={{0,6},{2,8},{4,10},{6,12},{8,14},{10,0},{12,2},{14,4},{1,7},{3,9},... | collective-permute-start | bytes 233480 | tf_op jit(solution)/shard_map/ppermute | solution.py:124
  55.3 13.2 %collective-permute-start.16 = (bf16[16,2432]{1,0:T(8,128)(2,1)S(1)}, bf16[16,2432]{1,0:T(8,128)(2,1)S(1)}, u32[]{:S(2)}, u32[]{:S(2)}) collective-permute-start(bf16[16,2432]{1,0:T(8,128)(2,1)S(1)} %get-tuple-element.33), channel_id=1, source_target_pairs={{0,4},{2,6},{4,8},{6,10},{8,12},{10,14},{12,0},{14,2},{1,5},{3,7},... | collective-permute-start | bytes 233480 | tf_op jit(solution)/shard_map/ppermute | solution.py:124
  57.3 11.3 %collective-permute-start.17 = (bf16[16,2432]{1,0:T(8,128)(2,1)S(1)}, bf16[16,2432]{1,0:T(8,128)(2,1)S(1)}, u32[]{:S(2)}, u32[]{:S(2)}) collective-permute-start(bf16[16,2432]{1,0:T(8,128)(2,1)S(1)} %get-tuple-element.27), channel_id=1, source_target_pairs={{0,2},{2,4},{4,6},{6,8},{8,10},{10,12},{12,14},{14,0},{1,3},{3,5},... | collective-permute-start | bytes 233480 | tf_op jit(solution)/shard_map/ppermute | solution.py:124
  68.8 8.2 %collective-permute-start.18 = (bf16[16,2560]{1,0:T(8,128)(2,1)S(1)}, bf16[16,2560]{1,0:T(8,128)(2,1)S(1)}, u32[]{:S(2)}, u32[]{:S(2)}) collective-permute-start(bf16[16,2560]{1,0:T(8,128)(2,1)S(1)} %get-tuple-element.6), channel_id=1, source_target_pairs={{0,2},{2,4},{4,6},{6,8},{8,10},{10,12},{12,14},{14,0},{1,3},{3,5},... | collective-permute-start | bytes 245768 | tf_op jit(solution)/shard_map/ppermute | solution.py:124
  68.9 8.2 %collective-permute-start.19 = (bf16[16,2560]{1,0:T(8,128)(2,1)S(1)}, bf16[16,2560]{1,0:T(8,128)(2,1)S(1)}, u32[]{:S(2)}, u32[]{:S(2)}) collective-permute-start(bf16[16,2560]{1,0:T(8,128)(2,1)S(1)} %get-tuple-element.7), channel_id=1, source_target_pairs={{0,4},{2,6},{4,8},{6,10},{8,12},{10,14},{12,0},{14,2},{1,5},{3,7},... | collective-permute-start | bytes 245768 | tf_op jit(solution)/shard_map/ppermute | solution.py:124
  69.0 12.9 %collective-permute-start.20 = (bf16[16,2560]{1,0:T(8,128)(2,1)S(1)}, bf16[16,2560]{1,0:T(8,128)(2,1)S(1)}, u32[]{:S(2)}, u32[]{:S(2)}) collective-permute-start(bf16[16,2560]{1,0:T(8,128)(2,1)S(1)} %get-tuple-element.8), channel_id=1, source_target_pairs={{0,6},{2,8},{4,10},{6,12},{8,14},{10,0},{12,2},{14,4},{1,7},{3,9},... | collective-permute-start | bytes 245768 | tf_op jit(solution)/shard_map/ppermute | solution.py:124
  71.1 11.2 %collective-permute-start.21 = (bf16[16,2560]{1,0:T(8,128)(2,1)S(1)}, bf16[16,2560]{1,0:T(8,128)(2,1)S(1)}, u32[]{:S(2)}, u32[]{:S(2)}) collective-permute-start(bf16[16,2560]{1,0:T(8,128)(2,1)S(1)} %get-tuple-element.9), channel_id=1, source_target_pairs={{0,8},{2,10},{4,12},{6,14},{8,0},{10,2},{12,4},{14,6},{1,9},{3,11}... | collective-permute-start | bytes 245768 | tf_op jit(solution)/shard_map/ppermute | solution.py:124
  74.2 8.2 %collective-permute-start.22 = (bf16[16,2560]{1,0:T(8,128)(2,1)S(1)}, bf16[16,2560]{1,0:T(8,128)(2,1)S(1)}, u32[]{:S(2)}, u32[]{:S(2)}) collective-permute-start(bf16[16,2560]{1,0:T(8,128)(2,1)S(1)} %get-tuple-element.10), channel_id=1, source_target_pairs={{0,10},{2,12},{4,14},{6,0},{8,2},{10,4},{12,6},{14,8},{1,11},{3,13... | collective-permute-start | bytes 245768 | tf_op jit(solution)/shard_map/ppermute | solution.py:124
  77.0 5.4 %collective-permute-start.23 = (bf16[16,2560]{1,0:T(8,128)(2,1)S(1)}, bf16[16,2560]{1,0:T(8,128)(2,1)S(1)}, u32[]{:S(2)}, u32[]{:S(2)}) collective-permute-start(bf16[16,2560]{1,0:T(8,128)(2,1)S(1)} %get-tuple-element.11), channel_id=1, source_target_pairs={{0,12},{2,14},{4,0},{6,2},{8,4},{10,6},{12,8},{14,10},{1,13},{3,15... | collective-permute-start | bytes 245768 | tf_op jit(solution)/shard_map/ppermute | solution.py:124
  77.1 5.3 %collective-permute-start.24 = (bf16[16,2560]{1,0:T(8,128)(2,1)S(1)}, bf16[16,2560]{1,0:T(8,128)(2,1)S(1)}, u32[]{:S(2)}, u32[]{:S(2)}) collective-permute-start(bf16[16,2560]{1,0:T(8,128)(2,1)S(1)} %get-tuple-element.4), channel_id=1, source_target_pairs={{0,14},{2,0},{4,2},{6,4},{8,6},{10,8},{12,10},{14,12},{1,15},{3,1}... | collective-permute-start | bytes 245768 | tf_op jit(solution)/shard_map/ppermute | solution.py:124
  83.2 27.5 %collective-permute-start.34 = (bf16[16,2304]{1,0:T(8,128)(2,1)S(1)}, bf16[16,2304]{1,0:T(8,128)(2,1)S(1)}, u32[]{:S(2)}, u32[]{:S(2)}) collective-permute-start(bf16[16,2304]{1,0:T(8,128)(2,1)S(1)} %add_convert_fusion.1), channel_id=1, source_target_pairs={{0,1},{1,0},{2,3},{3,2},{4,5},{5,4},{6,7},{7,6},{8,9},{9,8},{10,11... | collective-permute-start | bytes 221192 | tf_op jit(solution)/shard_map/ppermute | solution.py:116
  84.8 10.2 %collective-permute-start.26 = (bf16[16,2432]{1,0:T(8,128)(2,1)S(1)}, bf16[16,2432]{1,0:T(8,128)(2,1)S(1)}, u32[]{:S(2)}, u32[]{:S(2)}) collective-permute-start(bf16[16,2432]{1,0:T(8,128)(2,1)S(1)} %get-tuple-element.21), channel_id=1, source_target_pairs={{0,14},{2,0},{4,2},{6,4},{8,6},{10,8},{12,10},{14,12},{1,15},{3,1}... | collective-permute-start | bytes 233480 | tf_op jit(solution)/shard_map/ppermute | solution.py:124
  92.0 5.3 %collective-permute-start.27 = (bf16[16,2432]{1,0:T(8,128)(2,1)S(1)}, bf16[16,2432]{1,0:T(8,128)(2,1)S(1)}, u32[]{:S(2)}, u32[]{:S(2)}) collective-permute-start(bf16[16,2432]{1,0:T(8,128)(2,1)S(1)} %get-tuple-element.22), channel_id=1, source_target_pairs={{0,12},{2,14},{4,0},{6,2},{8,4},{10,6},{12,8},{14,10},{1,13},{3,15... | collective-permute-start | bytes 233480 | tf_op jit(solution)/shard_map/ppermute | solution.py:124
  93.9 5.7 %collective-permute-start.28 = (bf16[16,2432]{1,0:T(8,128)(2,1)S(1)}, bf16[16,2432]{1,0:T(8,128)(2,1)S(1)}, u32[]{:S(2)}, u32[]{:S(2)}) collective-permute-start(bf16[16,2432]{1,0:T(8,128)(2,1)S(1)} %get-tuple-element.23), channel_id=1, source_target_pairs={{0,10},{2,12},{4,14},{6,0},{8,2},{10,4},{12,6},{14,8},{1,11},{3,13... | collective-permute-start | bytes 233480 | tf_op jit(solution)/shard_map/ppermute | solution.py:124
  93.9 13.4 %collective-permute-start.29 = (bf16[16,2432]{1,0:T(8,128)(2,1)S(1)}, bf16[16,2432]{1,0:T(8,128)(2,1)S(1)}, u32[]{:S(2)}, u32[]{:S(2)}) collective-permute-start(bf16[16,2432]{1,0:T(8,128)(2,1)S(1)} %get-tuple-element.24), channel_id=1, source_target_pairs={{0,8},{2,10},{4,12},{6,14},{8,0},{10,2},{12,4},{14,6},{1,9},{3,11}... | collective-permute-start | bytes 233480 | tf_op jit(solution)/shard_map/ppermute | solution.py:124
  95.0 13.7 %collective-permute-start.30 = (bf16[16,2432]{1,0:T(8,128)(2,1)S(1)}, bf16[16,2432]{1,0:T(8,128)(2,1)S(1)}, u32[]{:S(2)}, u32[]{:S(2)}) collective-permute-start(bf16[16,2432]{1,0:T(8,128)(2,1)S(1)} %get-tuple-element.25), channel_id=1, source_target_pairs={{0,6},{2,8},{4,10},{6,12},{8,14},{10,0},{12,2},{14,4},{1,7},{3,9},... | collective-permute-start | bytes 233480 | tf_op jit(solution)/shard_map/ppermute | solution.py:124
  97.3 11.5 %collective-permute-start.31 = (bf16[16,2432]{1,0:T(8,128)(2,1)S(1)}, bf16[16,2432]{1,0:T(8,128)(2,1)S(1)}, u32[]{:S(2)}, u32[]{:S(2)}) collective-permute-start(bf16[16,2432]{1,0:T(8,128)(2,1)S(1)} %get-tuple-element.26), channel_id=1, source_target_pairs={{0,4},{2,6},{4,8},{6,10},{8,12},{10,14},{12,0},{14,2},{1,5},{3,7},... | collective-permute-start | bytes 233480 | tf_op jit(solution)/shard_map/ppermute | solution.py:124
  99.6 9.7 %collective-permute-start.32 = (bf16[16,2432]{1,0:T(8,128)(2,1)S(1)}, bf16[16,2432]{1,0:T(8,128)(2,1)S(1)}, u32[]{:S(2)}, u32[]{:S(2)}) collective-permute-start(bf16[16,2432]{1,0:T(8,128)(2,1)S(1)} %get-tuple-element.20), channel_id=1, source_target_pairs={{0,2},{2,4},{4,6},{6,8},{8,10},{10,12},{12,14},{14,0},{1,3},{3,5},... | collective-permute-start | bytes 233480 | tf_op jit(solution)/shard_map/ppermute | solution.py:124
  (11 other events, 30.3 us)

commit v2 on v1

--- a/solution.py
+++ b/solution.py
@@ -125,12 +125,12 @@
     return jnp.stack(moved, axis=0)
 
 
-def split_layer(g_half, routes_l, acts_l, dec_half, enc_half, gain_half, scale_l):
+def split_layer(g_half, routes_l, acts_l, own, other, is_own, gain_half, scale_l):
     peers = lax.axis_size("dict")
     me = lax.axis_index("dict")
     rows, listed = routes_l.shape
     block = acts_l.shape[1] // listed
-    held = dec_half.shape[0] // block
+    held = own[0].shape[0] // block
     half = g_half.shape[1]
     owner = routes_l // held
     within = routes_l - owner * held
@@ -149,12 +149,22 @@
     got = exchange(sent, 1).reshape(peers * rows, half + held * block)
     g_all = got[:, :half]
     act_all = got[:, half:]
-    part = lax.dot_general(
-        g_all, dec_half, (((1,), (1,)), ((), ())), preferred_element_type=jnp.float32
-    )
-    coef = (part + swap_cores(part)).astype(jnp.bfloat16)
-    dz = jnp.where(act_all > 0, coef, jnp.zeros_like(coef))
-    contrib = jnp.dot(dz, enc_half, preferred_element_type=jnp.float32).astype(jnp.bfloat16)
+
+    def with_dec(dec):
+        return lax.dot_general(
+            g_all, dec, (((1,), (1,)), ((), ())), preferred_element_type=jnp.float32
+        )
+
+    part = jnp.where(is_own, with_dec(own[0]), with_dec(other[0]))
+    paired = swap_cores(jnp.concatenate([part, act_all.astype(jnp.float32)], axis=1))
+    coef = (part + paired[:, :held * block]).astype(jnp.bfloat16)
+    act_used = jnp.where(is_own, act_all.astype(jnp.float32), paired[:, held * block:])
+    dz = jnp.where(act_used > 0, coef, jnp.zeros_like(coef))
+
+    def with_enc(enc):
+        return jnp.dot(dz, enc, preferred_element_type=jnp.float32)
+
+    contrib = jnp.where(is_own, with_enc(own[1]), with_enc(other[1])).astype(jnp.bfloat16)
     dz_pick = dz[:, :block]
     for spot in range(1, held):
         dz_pick = dz_pick + dz[:, spot * block:(spot + 1) * block]
@@ -174,29 +184,34 @@
     depth = lax.axis_size("section")
     here = lax.axis_index("section")
     rows, width = cotangent.shape
+    blocks = decoder.shape[1]
     half = width // depth
     mine = here * half
     theirs = (1 - here) * half
-    weights = jnp.stack([decoder[0], encoder[0]], axis=0)
-    own_w = lax.dynamic_slice_in_dim(weights, mine, half, axis=2)
-    other_w = swap_cores(lax.dynamic_slice_in_dim(weights, theirs, half, axis=2))
-    small = jnp.concatenate(
-        [gain[0], inv_rms[0], routes[0].reshape(-1).astype(jnp.float32)], axis=0
-    )
+    small = jnp.concatenate([gain[0], inv_rms[0]], axis=0)
     other_small = swap_cores(small)
-    other_acts = swap_cores(acts[0])
+    sent_w = jnp.concatenate(
+        [
+            lax.dynamic_slice_in_dim(decoder[0], theirs, half, axis=1),
+            lax.dynamic_slice_in_dim(encoder[0], theirs, half, axis=1),
+        ],
+        axis=0,
+    )
+    other_w = swap_cores(sent_w)
+    other = (other_w[:blocks], other_w[blocks:])
+    own = (
+        lax.dynamic_slice_in_dim(decoder[0], mine, half, axis=1),
+        lax.dynamic_slice_in_dim(encoder[0], mine, half, axis=1),
+    )
     attr_keep = jnp.zeros((rows, acts.shape[2]), jnp.float32)
     grad_keep = jnp.zeros(cotangent.shape, jnp.bfloat16)
     g_half = lax.dynamic_slice_in_dim(cotangent, mine, half, axis=1)
     for layer in reversed(range(depth)):
         is_own = here == layer
-        w = jnp.where(is_own, own_w, other_w)
         s = jnp.where(is_own, small, other_small)
-        acts_l = jnp.where(is_own, acts[0], other_acts)
         gain_half = lax.dynamic_slice_in_dim(s[:width], mine, half, axis=0)
         scale_l = s[width:width + rows]
-        routes_l = s[width + rows:].astype(jnp.int32).reshape(routes.shape[1:])
-        attr, g_half = split_layer(g_half, routes_l, acts_l, w[0], w[1], gain_half, scale_l)
+        attr, g_half = split_layer(g_half, routes[0], acts[0], own, other, is_own, gain_half, scale_l)
         partner = swap_cores(g_half)
         full = jnp.where(
             here == 0,

time: 112 us -> 98.1 us (0.88)
  waiting for transfers between devices: 26.8 us -> 20.6 us
  local copies, waits for them, and re-layouts: 14.7 us -> 9.1 us
  starting transfers between devices: 59 us -> 55.3 us
  matrix products: 3.71 us -> 5.34 us
    ppermute x28, waiting for transfers between devices: 20.9 us -> 16.5 us  [exchange(): moved.append(lax.ppermute(parts[shift], 'dict', route))]
    select_n x3 -> x2, other arithmetic: 4.16 us -> 0.07 us  [split_layer(): dz = jnp.where(act_used > 0, coef, jnp.zeros_like(coef))]
    unnamed x43 -> x39, local copies, waits for them, and re-layouts: 8.86 us -> 5.47 us
    ppermute x28, starting transfers between devices: 57.1 us -> 54 us  [exchange(): moved.append(lax.ppermute(parts[shift], 'dict', route))]
    concatenate x0 -> x4, other arithmetic: none -> 2.35 us  [the longest x1 1.57 us: split_device(): jnp.concatenate([lax.dynamic_slice_in_dim(decoder[0], theirs, half, axis=...]
    dot_general x4 -> x8, matrix products: 3.01 us -> 4.77 us  [the longest x4 2.6 us: with_enc(): return jnp.dot(dz, enc, preferred_element_type=jnp.float32)]
    ppermute x7 -> x6, waiting for transfers between devices: 5.86 us -> 4.18 us  [swap_cores(): return lax.ppermute(block, 'section', [(0, 1), (1, 0)])]
    another operation x3 -> x1, local copies, waits for them, and re-layouts: 1.74 us -> 0.08 us  [the longest x1 1.59 us: split_device(): weights = jnp.stack([decoder[0], encoder[0]], axis=0)]
  transfers between devices with their start and end apart: 35 -> 34, of which waited for: 14 -> 12; matrix products, arithmetic and copies ran while one was open for 14% -> 11% of each run, Pallas kernels for 0% -> 0%
where the time goes in v2:
time: 98.1 us; the launch traced here: 97.6 us
  starting transfers between devices  55.3 us (56%)
  waiting for transfers between devices  20.6 us (21%)
  local copies, waits for them, and re-layouts  9.1 us (9%)
  other arithmetic  6.15 us (6%)
  matrix products  5.34 us (5%)
  between operations  1.09 us (1%)
    ppermute x28, starting transfers between devices, exchange(): moved.append(lax.ppermute(parts[shift], 'dict', route))  54 us
    ppermute x28, waiting for transfers between devices, exchange(): moved.append(lax.ppermute(parts[shift], 'dict', route))  16.5 us
    unnamed x39, local copies, waits for them, and re-layouts  5.47 us
    ppermute x6, waiting for transfers between devices, swap_cores(): return lax.ppermute(block, 'section', [(0, 1), (1, 0)])  4.18 us
    dot_general x4, matrix products, with_enc(): return jnp.dot(dz, enc, preferred_element_type=jnp.float32)  2.6 us
    dot_general x4, matrix products, with_dec(): lax.dot_general(g_all, dec, (((1,), (1,)), ((), ())), preferred_element_t...  2.17 us
  transfers between devices with their start and end apart: 34, of which 12 were waited for; matrix products, arithmetic and copies ran while one was open for 11% of the time, Pallas kernels for 0%

profile of v2, /device:TPU:0, one launch (start us, length us, event | category | flops | bytes accessed | tf_op | source)
XLA Modules:
  0.0 97.6 jit_solution(17481943359600991153)
XLA Ops:
  4.5 2.9 %collective-permute-start.1 = (bf16[16,2560]{1,0:T(8,128)(2,1)}, bf16[16,2560]{1,0:T(8,128)(2,1)}, u32[]{:S(2)}, u32[]{:S(2)}) collective-permute-start(bf16[16,2560]{1,0:T(8,128)(2,1)} %get-tuple-element.12), channel_id=1, source_target_pairs={{0,2},{2,4},{4,6},{6,8},{8,10},{10,12},{12,14},{14,0},{1,3},{3,5},... | collective-permute-start | bytes 245768 | tf_op jit(solution)/shard_map/ppermute | solution.py:124
  7.5 1.6 %collective-permute-start.2 = (bf16[16,2560]{1,0:T(8,128)(2,1)}, bf16[16,2560]{1,0:T(8,128)(2,1)}, u32[]{:S(2)}, u32[]{:S(2)}) collective-permute-start(bf16[16,2560]{1,0:T(8,128)(2,1)} %get-tuple-element.13), channel_id=1, source_target_pairs={{0,4},{2,6},{4,8},{6,10},{8,12},{10,14},{12,0},{14,2},{1,5},{3,7},... | collective-permute-start | bytes 245768 | tf_op jit(solution)/shard_map/ppermute | solution.py:124
  9.0 2.6 %collective-permute-start.3 = (bf16[16,2560]{1,0:T(8,128)(2,1)}, bf16[16,2560]{1,0:T(8,128)(2,1)}, u32[]{:S(2)}, u32[]{:S(2)}) collective-permute-start(bf16[16,2560]{1,0:T(8,128)(2,1)} %get-tuple-element.14), channel_id=1, source_target_pairs={{0,6},{2,8},{4,10},{6,12},{8,14},{10,0},{12,2},{14,4},{1,7},{3,9},... | collective-permute-start | bytes 245768 | tf_op jit(solution)/shard_map/ppermute | solution.py:124
  11.6 1.2 %collective-permute-start.4 = (bf16[16,2560]{1,0:T(8,128)(2,1)S(1)}, bf16[16,2560]{1,0:T(8,128)(2,1)}, u32[]{:S(2)}, u32[]{:S(2)}) collective-permute-start(bf16[16,2560]{1,0:T(8,128)(2,1)S(1)} %get-tuple-element.15), channel_id=1, source_target_pairs={{0,8},{2,10},{4,12},{6,14},{8,0},{10,2},{12,4},{14,6},{1,9},{3,11}... | collective-permute-start | bytes 245768 | tf_op jit(solution)/shard_map/ppermute | solution.py:124
  12.8 2.6 %collective-permute-start.5 = (bf16[16,2560]{1,0:T(8,128)(2,1)S(1)}, bf16[16,2560]{1,0:T(8,128)(2,1)}, u32[]{:S(2)}, u32[]{:S(2)}) collective-permute-start(bf16[16,2560]{1,0:T(8,128)(2,1)S(1)} %get-tuple-element.16), channel_id=1, source_target_pairs={{0,10},{2,12},{4,14},{6,0},{8,2},{10,4},{12,6},{14,8},{1,11},{3,13... | collective-permute-start | bytes 245768 | tf_op jit(solution)/shard_map/ppermute | solution.py:124
  15.4 1.5 %dynamic-slice_bitcast_fusion = (bf16[256,2304]{1,0:T(8,128)(2,1)S(1)}, bf16[256,2304]{1,0:T(8,128)(2,1)S(1)}) fusion(bf16[1,256,4608]{2,1,0:T(8,128)(2,1)} %param.11, s32[]{:T(128)S(6)} %select_n.186, bf16[1,256,4608]{2,1,0:T(8,128)(2,1)S(1)} %copy-done), kind=kLoop, calls=%fused_computation.48 | loop fusion | bytes 4718596 | tf_op jit(solution)/shard_map/dynamic_slice | solution.py:196
  16.9 1.6 %pad_maximum_fusion = bf16[512,2304]{1,0:T(8,128)(2,1)} fusion(bf16[256,2304]{1,0:T(8,128)(2,1)S(1)} %get-tuple-element.36, bf16[256,2304]{1,0:T(8,128)(2,1)S(1)} %get-tuple-element.37), kind=kLoop, calls=%fused_computation.4 | loop fusion | flops 4718592 | bytes 4718592 | tf_op jit(solution)/shard_map/concatenate | solution.py:193
  18.6 1.4 %collective-permute-start.6 = (bf16[16,2560]{1,0:T(8,128)(2,1)S(1)}, bf16[16,2560]{1,0:T(8,128)(2,1)S(1)}, u32[]{:S(2)}, u32[]{:S(2)}) collective-permute-start(bf16[16,2560]{1,0:T(8,128)(2,1)S(1)} %get-tuple-element.17), channel_id=1, source_target_pairs={{0,12},{2,14},{4,0},{6,2},{8,4},{10,6},{12,8},{14,10},{1,13},{3,15... | collective-permute-start | bytes 245768 | tf_op jit(solution)/shard_map/ppermute | solution.py:124
  20.9 1.5 %collective-permute-start.7 = (bf16[16,2560]{1,0:T(8,128)(2,1)S(1)}, bf16[16,2560]{1,0:T(8,128)(2,1)S(1)}, u32[]{:S(2)}, u32[]{:S(2)}) collective-permute-start(bf16[16,2560]{1,0:T(8,128)(2,1)S(1)} %get-tuple-element.10), channel_id=1, source_target_pairs={{0,14},{2,0},{4,2},{6,4},{8,6},{10,8},{12,10},{14,12},{1,15},{3,1}... | collective-permute-start | bytes 245768 | tf_op jit(solution)/shard_map/ppermute | solution.py:124
  26.1 2.0 %collective-permute-done.8 = bf16[512,2304]{1,0:T(8,128)(2,1)S(1)} collective-permute-done((bf16[512,2304]{1,0:T(8,128)(2,1)}, bf16[512,2304]{1,0:T(8,128)(2,1)S(1)}, u32[]{:S(2)}, u32[]{:S(2)}) %collective-permute-start.8) | collective-permute-done | bytes 2359328 | tf_op jit(solution)/shard_map/ppermute | solution.py:116
  30.5 1.1 %collective-permute-done = f32[4624]{0:T(1024)} collective-permute-done((f32[4624]{0:T(1024)S(1)}, f32[4624]{0:T(1024)}, u32[]{:S(2)}, u32[]{:S(2)}) %collective-permute-start) | collective-permute-done | bytes 18528 | tf_op jit(solution)/shard_map/ppermute | solution.py:116
  32.5 1.6 %fusion.19 = bf16[128,2304]{1,0:T(8,128)(2,1)S(1)} fusion(bf16[128,256]{1,0:T(8,128)(2,1)S(1)} %fusion.40, bf16[512,2304]{1,0:T(8,128)(2,1)} %copy-done.2), kind=kOutput, calls=%fused_computation.60 | convolution fusion | flops 150994944 | bytes 1835008 | tf_op jit(solution)/shard_map/dot_general | solution.py:165
  34.5 1.5 %collective-permute-start.10 = (bf16[16,2432]{1,0:T(8,128)(2,1)S(1)}, bf16[16,2432]{1,0:T(8,128)(2,1)S(1)}, u32[]{:S(2)}, u32[]{:S(2)}) collective-permute-start(bf16[16,2432]{1,0:T(8,128)(2,1)S(1)} %get-tuple-element.26), channel_id=1, source_target_pairs={{0,14},{2,0},{4,2},{6,4},{8,6},{10,8},{12,10},{14,12},{1,15},{3,1}... | collective-permute-start | bytes 233480 | tf_op jit(solution)/shard_map/ppermute | solution.py:124
  36.8 1.4 %collective-permute-start.12 = (bf16[16,2432]{1,0:T(8,128)(2,1)S(1)}, bf16[16,2432]{1,0:T(8,128)(2,1)S(1)}, u32[]{:S(2)}, u32[]{:S(2)}) collective-permute-start(bf16[16,2432]{1,0:T(8,128)(2,1)S(1)} %get-tuple-element.28), channel_id=1, source_target_pairs={{0,10},{2,12},{4,14},{6,0},{8,2},{10,4},{12,6},{14,8},{1,11},{3,13... | collective-permute-start | bytes 233480 | tf_op jit(solution)/shard_map/ppermute | solution.py:124
  38.1 3.0 %collective-permute-start.13 = (bf16[16,2432]{1,0:T(8,128)(2,1)S(1)}, bf16[16,2432]{1,0:T(8,128)(2,1)S(1)}, u32[]{:S(2)}, u32[]{:S(2)}) collective-permute-start(bf16[16,2432]{1,0:T(8,128)(2,1)S(1)} %get-tuple-element.29), channel_id=1, source_target_pairs={{0,8},{2,10},{4,12},{6,14},{8,0},{10,2},{12,4},{14,6},{1,9},{3,11}... | collective-permute-start | bytes 233480 | tf_op jit(solution)/shard_map/ppermute | solution.py:124
  41.1 1.5 %collective-permute-start.15 = (bf16[16,2432]{1,0:T(8,128)(2,1)S(1)}, bf16[16,2432]{1,0:T(8,128)(2,1)S(1)}, u32[]{:S(2)}, u32[]{:S(2)}) collective-permute-start(bf16[16,2432]{1,0:T(8,128)(2,1)S(1)} %get-tuple-element.31), channel_id=1, source_target_pairs={{0,4},{2,6},{4,8},{6,10},{8,12},{10,14},{12,0},{14,2},{1,5},{3,7},... | collective-permute-start | bytes 233480 | tf_op jit(solution)/shard_map/ppermute | solution.py:124
  43.3 7.7 %collective-permute-done.13 = bf16[16,2432]{1,0:T(8,128)(2,1)S(1)} collective-permute-done((bf16[16,2432]{1,0:T(8,128)(2,1)S(1)}, bf16[16,2432]{1,0:T(8,128)(2,1)S(1)}, u32[]{:S(2)}, u32[]{:S(2)}) %collective-permute-start.13) | collective-permute-done | bytes 77856 | tf_op jit(solution)/shard_map/ppermute | solution.py:124
  51.0 1.7 %collective-permute-done.14 = bf16[16,2432]{1,0:T(8,128)(2,1)S(1)} collective-permute-done((bf16[16,2432]{1,0:T(8,128)(2,1)S(1)}, bf16[16,2432]{1,0:T(8,128)(2,1)S(1)}, u32[]{:S(2)}, u32[]{:S(2)}) %collective-permute-start.14) | collective-permute-done | bytes 77856 | tf_op jit(solution)/shard_map/ppermute | solution.py:124
  54.0 2.8 %collective-permute-start.19 = (bf16[16,2560]{1,0:T(8,128)(2,1)S(1)}, bf16[16,2560]{1,0:T(8,128)(2,1)S(1)}, u32[]{:S(2)}, u32[]{:S(2)}) collective-permute-start(bf16[16,2560]{1,0:T(8,128)(2,1)S(1)} %get-tuple-element.6), channel_id=1, source_target_pairs={{0,6},{2,8},{4,10},{6,12},{8,14},{10,0},{12,2},{14,4},{1,7},{3,9},... | collective-permute-start | bytes 245768 | tf_op jit(solution)/shard_map/ppermute | solution.py:124
  56.8 1.7 %collective-permute-start.20 = (bf16[16,2560]{1,0:T(8,128)(2,1)S(1)}, bf16[16,2560]{1,0:T(8,128)(2,1)S(1)}, u32[]{:S(2)}, u32[]{:S(2)}) collective-permute-start(bf16[16,2560]{1,0:T(8,128)(2,1)S(1)} %get-tuple-element.7), channel_id=1, source_target_pairs={{0,8},{2,10},{4,12},{6,14},{8,0},{10,2},{12,4},{14,6},{1,9},{3,11}... | collective-permute-start | bytes 245768 | tf_op jit(solution)/shard_map/ppermute | solution.py:124
  58.5 1.2 %collective-permute-start.21 = (bf16[16,2560]{1,0:T(8,128)(2,1)S(1)}, bf16[16,2560]{1,0:T(8,128)(2,1)S(1)}, u32[]{:S(2)}, u32[]{:S(2)}) collective-permute-start(bf16[16,2560]{1,0:T(8,128)(2,1)S(1)} %get-tuple-element.8), channel_id=1, source_target_pairs={{0,10},{2,12},{4,14},{6,0},{8,2},{10,4},{12,6},{14,8},{1,11},{3,13... | collective-permute-start | bytes 245768 | tf_op jit(solution)/shard_map/ppermute | solution.py:124
  59.7 1.4 %collective-permute-done.17 = bf16[16,2560]{1,0:T(8,128)(2,1)S(1)} collective-permute-done((bf16[16,2560]{1,0:T(8,128)(2,1)S(1)}, bf16[16,2560]{1,0:T(8,128)(2,1)S(1)}, u32[]{:S(2)}, u32[]{:S(2)}) %collective-permute-start.17) | collective-permute-done | bytes 81952 | tf_op jit(solution)/shard_map/ppermute | solution.py:124
  62.2 2.9 %collective-permute-start.23 = (bf16[16,2560]{1,0:T(8,128)(2,1)S(1)}, bf16[16,2560]{1,0:T(8,128)(2,1)S(1)}, u32[]{:S(2)}, u32[]{:S(2)}) collective-permute-start(bf16[16,2560]{1,0:T(8,128)(2,1)S(1)} %get-tuple-element.2), channel_id=1, source_target_pairs={{0,14},{2,0},{4,2},{6,4},{8,6},{10,8},{12,10},{14,12},{1,15},{3,1}... | collective-permute-start | bytes 245768 | tf_op jit(solution)/shard_map/ppermute | solution.py:124
  65.1 1.5 %collective-permute-done.19 = bf16[16,2560]{1,0:T(8,128)(2,1)S(1)} collective-permute-done((bf16[16,2560]{1,0:T(8,128)(2,1)S(1)}, bf16[16,2560]{1,0:T(8,128)(2,1)S(1)}, u32[]{:S(2)}, u32[]{:S(2)}) %collective-permute-start.19) | collective-permute-done | bytes 81952 | tf_op jit(solution)/shard_map/ppermute | solution.py:124
  66.6 1.3 %collective-permute-done.20 = bf16[16,2560]{1,0:T(8,128)(2,1)S(1)} collective-permute-done((bf16[16,2560]{1,0:T(8,128)(2,1)S(1)}, bf16[16,2560]{1,0:T(8,128)(2,1)S(1)}, u32[]{:S(2)}, u32[]{:S(2)}) %collective-permute-start.20) | collective-permute-done | bytes 81952 | tf_op jit(solution)/shard_map/ppermute | solution.py:124
  71.5 6.7 %collective-permute-start.25 = (bf16[16,2432]{1,0:T(8,128)(2,1)S(1)}, bf16[16,2432]{1,0:T(8,128)(2,1)S(1)}, u32[]{:S(2)}, u32[]{:S(2)}) collective-permute-start(bf16[16,2432]{1,0:T(8,128)(2,1)S(1)} %get-tuple-element.19), channel_id=1, source_target_pairs={{0,14},{2,0},{4,2},{6,4},{8,6},{10,8},{12,10},{14,12},{1,15},{3,1}... | collective-permute-start | bytes 233480 | tf_op jit(solution)/shard_map/ppermute | solution.py:124
  78.1 2.6 %collective-permute-start.26 = (bf16[16,2432]{1,0:T(8,128)(2,1)S(1)}, bf16[16,2432]{1,0:T(8,128)(2,1)S(1)}, u32[]{:S(2)}, u32[]{:S(2)}) collective-permute-start(bf16[16,2432]{1,0:T(8,128)(2,1)S(1)} %get-tuple-element.20), channel_id=1, source_target_pairs={{0,12},{2,14},{4,0},{6,2},{8,4},{10,6},{12,8},{14,10},{1,13},{3,15... | collective-permute-start | bytes 233480 | tf_op jit(solution)/shard_map/ppermute | solution.py:124
  80.7 1.1 %collective-permute-start.28 = (bf16[16,2432]{1,0:T(8,128)(2,1)S(1)}, bf16[16,2432]{1,0:T(8,128)(2,1)S(1)}, u32[]{:S(2)}, u32[]{:S(2)}) collective-permute-start(bf16[16,2432]{1,0:T(8,128)(2,1)S(1)} %get-tuple-element.22), channel_id=1, source_target_pairs={{0,8},{2,10},{4,12},{6,14},{8,0},{10,2},{12,4},{14,6},{1,9},{3,11}... | collective-permute-start | bytes 233480 | tf_op jit(solution)/shard_map/ppermute | solution.py:124
  81.8 1.8 %collective-permute-start.29 = (bf16[16,2432]{1,0:T(8,128)(2,1)S(1)}, bf16[16,2432]{1,0:T(8,128)(2,1)S(1)}, u32[]{:S(2)}, u32[]{:S(2)}) collective-permute-start(bf16[16,2432]{1,0:T(8,128)(2,1)S(1)} %get-tuple-element.23), channel_id=1, source_target_pairs={{0,6},{2,8},{4,10},{6,12},{8,14},{10,0},{12,2},{14,4},{1,7},{3,9},... | collective-permute-start | bytes 233480 | tf_op jit(solution)/shard_map/ppermute | solution.py:124
  83.7 2.3 %collective-permute-start.30 = (bf16[16,2432]{1,0:T(8,128)(2,1)S(1)}, bf16[16,2432]{1,0:T(8,128)(2,1)S(1)}, u32[]{:S(2)}, u32[]{:S(2)}) collective-permute-start(bf16[16,2432]{1,0:T(8,128)(2,1)S(1)} %get-tuple-element.24), channel_id=1, source_target_pairs={{0,4},{2,6},{4,8},{6,10},{8,12},{10,14},{12,0},{14,2},{1,5},{3,7},... | collective-permute-start | bytes 233480 | tf_op jit(solution)/shard_map/ppermute | solution.py:124
  86.8 6.5 %collective-permute-start.31 = (bf16[16,2432]{1,0:T(8,128)(2,1)S(1)}, bf16[16,2432]{1,0:T(8,128)(2,1)S(1)}, u32[]{:S(2)}, u32[]{:S(2)}) collective-permute-start(bf16[16,2432]{1,0:T(8,128)(2,1)S(1)} %get-tuple-element.18), channel_id=1, source_target_pairs={{0,2},{2,4},{4,6},{6,8},{8,10},{10,12},{12,14},{14,0},{1,3},{3,5},... | collective-permute-start | bytes 233480 | tf_op jit(solution)/shard_map/ppermute | solution.py:124
  94.1 1.2 %collective-permute-done.31 = bf16[16,2432]{1,0:T(8,128)(2,1)S(1)} collective-permute-done((bf16[16,2432]{1,0:T(8,128)(2,1)S(1)}, bf16[16,2432]{1,0:T(8,128)(2,1)S(1)}, u32[]{:S(2)}, u32[]{:S(2)}) %collective-permute-start.31) | collective-permute-done | bytes 77856 | tf_op jit(solution)/shard_map/ppermute | solution.py:124
  (132 shorter events, 23.3 us)
Async XLA Ops:
  4.5 14.0 %collective-permute-start.1 = (bf16[16,2560]{1,0:T(8,128)(2,1)}, bf16[16,2560]{1,0:T(8,128)(2,1)}, u32[]{:S(2)}, u32[]{:S(2)}) collective-permute-start(bf16[16,2560]{1,0:T(8,128)(2,1)} %get-tuple-element.12), channel_id=1, source_target_pairs={{0,2},{2,4},{4,6},{6,8},{8,10},{10,12},{12,14},{14,0},{1,3},{3,5},... | collective-permute-start | bytes 245768 | tf_op jit(solution)/shard_map/ppermute | solution.py:124
  7.5 13.4 %collective-permute-start.2 = (bf16[16,2560]{1,0:T(8,128)(2,1)}, bf16[16,2560]{1,0:T(8,128)(2,1)}, u32[]{:S(2)}, u32[]{:S(2)}) collective-permute-start(bf16[16,2560]{1,0:T(8,128)(2,1)} %get-tuple-element.13), channel_id=1, source_target_pairs={{0,4},{2,6},{4,8},{6,10},{8,12},{10,14},{12,0},{14,2},{1,5},{3,7},... | collective-permute-start | bytes 245768 | tf_op jit(solution)/shard_map/ppermute | solution.py:124
  9.0 14.2 %collective-permute-start.3 = (bf16[16,2560]{1,0:T(8,128)(2,1)}, bf16[16,2560]{1,0:T(8,128)(2,1)}, u32[]{:S(2)}, u32[]{:S(2)}) collective-permute-start(bf16[16,2560]{1,0:T(8,128)(2,1)} %get-tuple-element.14), channel_id=1, source_target_pairs={{0,6},{2,8},{4,10},{6,12},{8,14},{10,0},{12,2},{14,4},{1,7},{3,9},... | collective-permute-start | bytes 245768 | tf_op jit(solution)/shard_map/ppermute | solution.py:124
  11.6 12.6 %collective-permute-start.4 = (bf16[16,2560]{1,0:T(8,128)(2,1)S(1)}, bf16[16,2560]{1,0:T(8,128)(2,1)}, u32[]{:S(2)}, u32[]{:S(2)}) collective-permute-start(bf16[16,2560]{1,0:T(8,128)(2,1)S(1)} %get-tuple-element.15), channel_id=1, source_target_pairs={{0,8},{2,10},{4,12},{6,14},{8,0},{10,2},{12,4},{14,6},{1,9},{3,11}... | collective-permute-start | bytes 245768 | tf_op jit(solution)/shard_map/ppermute | solution.py:124
  12.8 12.3 %collective-permute-start.5 = (bf16[16,2560]{1,0:T(8,128)(2,1)S(1)}, bf16[16,2560]{1,0:T(8,128)(2,1)}, u32[]{:S(2)}, u32[]{:S(2)}) collective-permute-start(bf16[16,2560]{1,0:T(8,128)(2,1)S(1)} %get-tuple-element.16), channel_id=1, source_target_pairs={{0,10},{2,12},{4,14},{6,0},{8,2},{10,4},{12,6},{14,8},{1,11},{3,13... | collective-permute-start | bytes 245768 | tf_op jit(solution)/shard_map/ppermute | solution.py:124
  18.6 7.5 %collective-permute-start.6 = (bf16[16,2560]{1,0:T(8,128)(2,1)S(1)}, bf16[16,2560]{1,0:T(8,128)(2,1)S(1)}, u32[]{:S(2)}, u32[]{:S(2)}) collective-permute-start(bf16[16,2560]{1,0:T(8,128)(2,1)S(1)} %get-tuple-element.17), channel_id=1, source_target_pairs={{0,12},{2,14},{4,0},{6,2},{8,4},{10,6},{12,8},{14,10},{1,13},{3,15... | collective-permute-start | bytes 245768 | tf_op jit(solution)/shard_map/ppermute | solution.py:124
  20.9 5.2 %collective-permute-start.7 = (bf16[16,2560]{1,0:T(8,128)(2,1)S(1)}, bf16[16,2560]{1,0:T(8,128)(2,1)S(1)}, u32[]{:S(2)}, u32[]{:S(2)}) collective-permute-start(bf16[16,2560]{1,0:T(8,128)(2,1)S(1)} %get-tuple-element.10), channel_id=1, source_target_pairs={{0,14},{2,0},{4,2},{6,4},{8,6},{10,8},{12,10},{14,12},{1,15},{3,1}... | collective-permute-start | bytes 245768 | tf_op jit(solution)/shard_map/ppermute | solution.py:124
  23.2 4.8 %collective-permute-start.8 = (bf16[512,2304]{1,0:T(8,128)(2,1)}, bf16[512,2304]{1,0:T(8,128)(2,1)S(1)}, u32[]{:S(2)}, u32[]{:S(2)}) collective-permute-start(bf16[512,2304]{1,0:T(8,128)(2,1)} %pad_maximum_fusion), channel_id=1, source_target_pairs={{0,1},{1,0},{2,3},{3,2},{4,5},{5,4},{6,7},{7,6},{8,9},{9,8},{10,11... | collective-permute-start | bytes 7077896 | tf_op jit(solution)/shard_map/ppermute | solution.py:116
  29.9 2.5 %collective-permute-start.9 = (f32[128,512]{1,0:T(8,128)}, f32[128,512]{1,0:T(8,128)S(1)}, u32[]{:S(2)}, u32[]{:S(2)}) collective-permute-start(f32[128,512]{1,0:T(8,128)} %pad_maximum_fusion.1), channel_id=1, source_target_pairs={{0,1},{1,0},{2,3},{3,2},{4,5},{5,4},{6,7},{7,6},{8,9},{9,8},{10,11... | collective-permute-start | bytes 786440 | tf_op jit(solution)/shard_map/ppermute | solution.py:116
  34.5 6.6 %collective-permute-start.10 = (bf16[16,2432]{1,0:T(8,128)(2,1)S(1)}, bf16[16,2432]{1,0:T(8,128)(2,1)S(1)}, u32[]{:S(2)}, u32[]{:S(2)}) collective-permute-start(bf16[16,2432]{1,0:T(8,128)(2,1)S(1)} %get-tuple-element.26), channel_id=1, source_target_pairs={{0,14},{2,0},{4,2},{6,4},{8,6},{10,8},{12,10},{14,12},{1,15},{3,1}... | collective-permute-start | bytes 233480 | tf_op jit(solution)/shard_map/ppermute | solution.py:124
  36.0 6.6 %collective-permute-start.11 = (bf16[16,2432]{1,0:T(8,128)(2,1)S(1)}, bf16[16,2432]{1,0:T(8,128)(2,1)S(1)}, u32[]{:S(2)}, u32[]{:S(2)}) collective-permute-start(bf16[16,2432]{1,0:T(8,128)(2,1)S(1)} %get-tuple-element.27), channel_id=1, source_target_pairs={{0,12},{2,14},{4,0},{6,2},{8,4},{10,6},{12,8},{14,10},{1,13},{3,15... | collective-permute-start | bytes 233480 | tf_op jit(solution)/shard_map/ppermute | solution.py:124
  36.8 6.5 %collective-permute-start.12 = (bf16[16,2432]{1,0:T(8,128)(2,1)S(1)}, bf16[16,2432]{1,0:T(8,128)(2,1)S(1)}, u32[]{:S(2)}, u32[]{:S(2)}) collective-permute-start(bf16[16,2432]{1,0:T(8,128)(2,1)S(1)} %get-tuple-element.28), channel_id=1, source_target_pairs={{0,10},{2,12},{4,14},{6,0},{8,2},{10,4},{12,6},{14,8},{1,11},{3,13... | collective-permute-start | bytes 233480 | tf_op jit(solution)/shard_map/ppermute | solution.py:124
  38.1 12.9 %collective-permute-start.13 = (bf16[16,2432]{1,0:T(8,128)(2,1)S(1)}, bf16[16,2432]{1,0:T(8,128)(2,1)S(1)}, u32[]{:S(2)}, u32[]{:S(2)}) collective-permute-start(bf16[16,2432]{1,0:T(8,128)(2,1)S(1)} %get-tuple-element.29), channel_id=1, source_target_pairs={{0,8},{2,10},{4,12},{6,14},{8,0},{10,2},{12,4},{14,6},{1,9},{3,11}... | collective-permute-start | bytes 233480 | tf_op jit(solution)/shard_map/ppermute | solution.py:124
  41.1 11.7 %collective-permute-start.14 = (bf16[16,2432]{1,0:T(8,128)(2,1)S(1)}, bf16[16,2432]{1,0:T(8,128)(2,1)S(1)}, u32[]{:S(2)}, u32[]{:S(2)}) collective-permute-start(bf16[16,2432]{1,0:T(8,128)(2,1)S(1)} %get-tuple-element.30), channel_id=1, source_target_pairs={{0,6},{2,8},{4,10},{6,12},{8,14},{10,0},{12,2},{14,4},{1,7},{3,9},... | collective-permute-start | bytes 233480 | tf_op jit(solution)/shard_map/ppermute | solution.py:124
  41.1 11.7 %collective-permute-start.15 = (bf16[16,2432]{1,0:T(8,128)(2,1)S(1)}, bf16[16,2432]{1,0:T(8,128)(2,1)S(1)}, u32[]{:S(2)}, u32[]{:S(2)}) collective-permute-start(bf16[16,2432]{1,0:T(8,128)(2,1)S(1)} %get-tuple-element.31), channel_id=1, source_target_pairs={{0,4},{2,6},{4,8},{6,10},{8,12},{10,14},{12,0},{14,2},{1,5},{3,7},... | collective-permute-start | bytes 233480 | tf_op jit(solution)/shard_map/ppermute | solution.py:124
  42.6 10.3 %collective-permute-start.16 = (bf16[16,2432]{1,0:T(8,128)(2,1)S(1)}, bf16[16,2432]{1,0:T(8,128)(2,1)S(1)}, u32[]{:S(2)}, u32[]{:S(2)}) collective-permute-start(bf16[16,2432]{1,0:T(8,128)(2,1)S(1)} %get-tuple-element.25), channel_id=1, source_target_pairs={{0,2},{2,4},{4,6},{6,8},{8,10},{10,12},{12,14},{14,0},{1,3},{3,5},... | collective-permute-start | bytes 233480 | tf_op jit(solution)/shard_map/ppermute | solution.py:124
  53.2 8.0 %collective-permute-start.17 = (bf16[16,2560]{1,0:T(8,128)(2,1)S(1)}, bf16[16,2560]{1,0:T(8,128)(2,1)S(1)}, u32[]{:S(2)}, u32[]{:S(2)}) collective-permute-start(bf16[16,2560]{1,0:T(8,128)(2,1)S(1)} %get-tuple-element.4), channel_id=1, source_target_pairs={{0,2},{2,4},{4,6},{6,8},{8,10},{10,12},{12,14},{14,0},{1,3},{3,5},... | collective-permute-start | bytes 245768 | tf_op jit(solution)/shard_map/ppermute | solution.py:124
  53.2 9.0 %collective-permute-start.18 = (bf16[16,2560]{1,0:T(8,128)(2,1)S(1)}, bf16[16,2560]{1,0:T(8,128)(2,1)S(1)}, u32[]{:S(2)}, u32[]{:S(2)}) collective-permute-start(bf16[16,2560]{1,0:T(8,128)(2,1)S(1)} %get-tuple-element.5), channel_id=1, source_target_pairs={{0,4},{2,6},{4,8},{6,10},{8,12},{10,14},{12,0},{14,2},{1,5},{3,7},... | collective-permute-start | bytes 245768 | tf_op jit(solution)/shard_map/ppermute | solution.py:124
  54.0 12.6 %collective-permute-start.19 = (bf16[16,2560]{1,0:T(8,128)(2,1)S(1)}, bf16[16,2560]{1,0:T(8,128)(2,1)S(1)}, u32[]{:S(2)}, u32[]{:S(2)}) collective-permute-start(bf16[16,2560]{1,0:T(8,128)(2,1)S(1)} %get-tuple-element.6), channel_id=1, source_target_pairs={{0,6},{2,8},{4,10},{6,12},{8,14},{10,0},{12,2},{14,4},{1,7},{3,9},... | collective-permute-start | bytes 245768 | tf_op jit(solution)/shard_map/ppermute | solution.py:124
  56.8 11.0 %collective-permute-start.20 = (bf16[16,2560]{1,0:T(8,128)(2,1)S(1)}, bf16[16,2560]{1,0:T(8,128)(2,1)S(1)}, u32[]{:S(2)}, u32[]{:S(2)}) collective-permute-start(bf16[16,2560]{1,0:T(8,128)(2,1)S(1)} %get-tuple-element.7), channel_id=1, source_target_pairs={{0,8},{2,10},{4,12},{6,14},{8,0},{10,2},{12,4},{14,6},{1,9},{3,11}... | collective-permute-start | bytes 245768 | tf_op jit(solution)/shard_map/ppermute | solution.py:124
  58.5 9.4 %collective-permute-start.21 = (bf16[16,2560]{1,0:T(8,128)(2,1)S(1)}, bf16[16,2560]{1,0:T(8,128)(2,1)S(1)}, u32[]{:S(2)}, u32[]{:S(2)}) collective-permute-start(bf16[16,2560]{1,0:T(8,128)(2,1)S(1)} %get-tuple-element.8), channel_id=1, source_target_pairs={{0,10},{2,12},{4,14},{6,0},{8,2},{10,4},{12,6},{14,8},{1,11},{3,13... | collective-permute-start | bytes 245768 | tf_op jit(solution)/shard_map/ppermute | solution.py:124
  61.1 6.7 %collective-permute-start.22 = (bf16[16,2560]{1,0:T(8,128)(2,1)S(1)}, bf16[16,2560]{1,0:T(8,128)(2,1)S(1)}, u32[]{:S(2)}, u32[]{:S(2)}) collective-permute-start(bf16[16,2560]{1,0:T(8,128)(2,1)S(1)} %get-tuple-element.9), channel_id=1, source_target_pairs={{0,12},{2,14},{4,0},{6,2},{8,4},{10,6},{12,8},{14,10},{1,13},{3,15... | collective-permute-start | bytes 245768 | tf_op jit(solution)/shard_map/ppermute | solution.py:124
  62.2 5.7 %collective-permute-start.23 = (bf16[16,2560]{1,0:T(8,128)(2,1)S(1)}, bf16[16,2560]{1,0:T(8,128)(2,1)S(1)}, u32[]{:S(2)}, u32[]{:S(2)}) collective-permute-start(bf16[16,2560]{1,0:T(8,128)(2,1)S(1)} %get-tuple-element.2), channel_id=1, source_target_pairs={{0,14},{2,0},{4,2},{6,4},{8,6},{10,8},{12,10},{14,12},{1,15},{3,1}... | collective-permute-start | bytes 245768 | tf_op jit(solution)/shard_map/ppermute | solution.py:124
  69.1 1.6 %collective-permute-start.24 = (f32[128,512]{1,0:T(8,128)S(1)}, f32[128,512]{1,0:T(8,128)S(1)}, u32[]{:S(2)}, u32[]{:S(2)}) collective-permute-start(f32[128,512]{1,0:T(8,128)S(1)} %pad_maximum_fusion.2), channel_id=1, source_target_pairs={{0,1},{1,0},{2,3},{3,2},{4,5},{5,4},{6,7},{7,6},{8,9},{9,8},{10,11... | collective-permute-start | bytes 786440 | tf_op jit(solution)/shard_map/ppermute | solution.py:116
  69.3 27.4 %collective-permute-start.33 = (bf16[16,2304]{1,0:T(8,128)(2,1)S(1)}, bf16[16,2304]{1,0:T(8,128)(2,1)S(1)}, u32[]{:S(2)}, u32[]{:S(2)}) collective-permute-start(bf16[16,2304]{1,0:T(8,128)(2,1)S(1)} %add_convert_fusion.1), channel_id=1, source_target_pairs={{0,1},{1,0},{2,3},{3,2},{4,5},{5,4},{6,7},{7,6},{8,9},{9,8},{10,11... | collective-permute-start | bytes 221192 | tf_op jit(solution)/shard_map/ppermute | solution.py:116
  71.5 10.4 %collective-permute-start.25 = (bf16[16,2432]{1,0:T(8,128)(2,1)S(1)}, bf16[16,2432]{1,0:T(8,128)(2,1)S(1)}, u32[]{:S(2)}, u32[]{:S(2)}) collective-permute-start(bf16[16,2432]{1,0:T(8,128)(2,1)S(1)} %get-tuple-element.19), channel_id=1, source_target_pairs={{0,14},{2,0},{4,2},{6,4},{8,6},{10,8},{12,10},{14,12},{1,15},{3,1}... | collective-permute-start | bytes 233480 | tf_op jit(solution)/shard_map/ppermute | solution.py:124
  78.1 5.5 %collective-permute-start.26 = (bf16[16,2432]{1,0:T(8,128)(2,1)S(1)}, bf16[16,2432]{1,0:T(8,128)(2,1)S(1)}, u32[]{:S(2)}, u32[]{:S(2)}) collective-permute-start(bf16[16,2432]{1,0:T(8,128)(2,1)S(1)} %get-tuple-element.20), channel_id=1, source_target_pairs={{0,12},{2,14},{4,0},{6,2},{8,4},{10,6},{12,8},{14,10},{1,13},{3,15... | collective-permute-start | bytes 233480 | tf_op jit(solution)/shard_map/ppermute | solution.py:124
  80.7 6.1 %collective-permute-start.27 = (bf16[16,2432]{1,0:T(8,128)(2,1)S(1)}, bf16[16,2432]{1,0:T(8,128)(2,1)S(1)}, u32[]{:S(2)}, u32[]{:S(2)}) collective-permute-start(bf16[16,2432]{1,0:T(8,128)(2,1)S(1)} %get-tuple-element.21), channel_id=1, source_target_pairs={{0,10},{2,12},{4,14},{6,0},{8,2},{10,4},{12,6},{14,8},{1,11},{3,13... | collective-permute-start | bytes 233480 | tf_op jit(solution)/shard_map/ppermute | solution.py:124
  80.7 12.6 %collective-permute-start.28 = (bf16[16,2432]{1,0:T(8,128)(2,1)S(1)}, bf16[16,2432]{1,0:T(8,128)(2,1)S(1)}, u32[]{:S(2)}, u32[]{:S(2)}) collective-permute-start(bf16[16,2432]{1,0:T(8,128)(2,1)S(1)} %get-tuple-element.22), channel_id=1, source_target_pairs={{0,8},{2,10},{4,12},{6,14},{8,0},{10,2},{12,4},{14,6},{1,9},{3,11}... | collective-permute-start | bytes 233480 | tf_op jit(solution)/shard_map/ppermute | solution.py:124
  81.8 12.2 %collective-permute-start.29 = (bf16[16,2432]{1,0:T(8,128)(2,1)S(1)}, bf16[16,2432]{1,0:T(8,128)(2,1)S(1)}, u32[]{:S(2)}, u32[]{:S(2)}) collective-permute-start(bf16[16,2432]{1,0:T(8,128)(2,1)S(1)} %get-tuple-element.23), channel_id=1, source_target_pairs={{0,6},{2,8},{4,10},{6,12},{8,14},{10,0},{12,2},{14,4},{1,7},{3,9},... | collective-permute-start | bytes 233480 | tf_op jit(solution)/shard_map/ppermute | solution.py:124
  83.7 10.4 %collective-permute-start.30 = (bf16[16,2432]{1,0:T(8,128)(2,1)S(1)}, bf16[16,2432]{1,0:T(8,128)(2,1)S(1)}, u32[]{:S(2)}, u32[]{:S(2)}) collective-permute-start(bf16[16,2432]{1,0:T(8,128)(2,1)S(1)} %get-tuple-element.24), channel_id=1, source_target_pairs={{0,4},{2,6},{4,8},{6,10},{8,12},{10,14},{12,0},{14,2},{1,5},{3,7},... | collective-permute-start | bytes 233480 | tf_op jit(solution)/shard_map/ppermute | solution.py:124
  86.8 8.5 %collective-permute-start.31 = (bf16[16,2432]{1,0:T(8,128)(2,1)S(1)}, bf16[16,2432]{1,0:T(8,128)(2,1)S(1)}, u32[]{:S(2)}, u32[]{:S(2)}) collective-permute-start(bf16[16,2432]{1,0:T(8,128)(2,1)S(1)} %get-tuple-element.18), channel_id=1, source_target_pairs={{0,2},{2,4},{4,6},{6,8},{8,10},{10,12},{12,14},{14,0},{1,3},{3,5},... | collective-permute-start | bytes 233480 | tf_op jit(solution)/shard_map/ppermute | solution.py:124
  (9 other events, 62.3 us)

commit v3 on v2

--- a/solution.py
+++ b/solution.py
@@ -155,7 +155,8 @@
             g_all, dec, (((1,), (1,)), ((), ())), preferred_element_type=jnp.float32
         )
 
-    part = jnp.where(is_own, with_dec(own[0]), with_dec(other[0]))
+    on_first = lax.axis_index("section") == 0
+    part = jnp.where(on_first, with_dec(own[0]), with_dec(other[0]))
     paired = swap_cores(jnp.concatenate([part, act_all.astype(jnp.float32)], axis=1))
     coef = (part + paired[:, :held * block]).astype(jnp.bfloat16)
     act_used = jnp.where(is_own, act_all.astype(jnp.float32), paired[:, held * block:])
@@ -164,7 +165,7 @@
     def with_enc(enc):
         return jnp.dot(dz, enc, preferred_element_type=jnp.float32)
 
-    contrib = jnp.where(is_own, with_enc(own[1]), with_enc(other[1])).astype(jnp.bfloat16)
+    contrib = jnp.where(on_first, with_enc(own[1]), with_enc(other[1])).astype(jnp.bfloat16)
     dz_pick = dz[:, :block]
     for spot in range(1, held):
         dz_pick = dz_pick + dz[:, spot * block:(spot + 1) * block]
@@ -190,19 +191,8 @@
     theirs = (1 - here) * half
     small = jnp.concatenate([gain[0], inv_rms[0]], axis=0)
     other_small = swap_cores(small)
-    sent_w = jnp.concatenate(
-        [
-            lax.dynamic_slice_in_dim(decoder[0], theirs, half, axis=1),
-            lax.dynamic_slice_in_dim(encoder[0], theirs, half, axis=1),
-        ],
-        axis=0,
-    )
-    other_w = swap_cores(sent_w)
-    other = (other_w[:blocks], other_w[blocks:])
-    own = (
-        lax.dynamic_slice_in_dim(decoder[0], mine, half, axis=1),
-        lax.dynamic_slice_in_dim(encoder[0], mine, half, axis=1),
-    )
+    dec_here, enc_here = decoder[0], encoder[0]
+    dec_there, enc_there = swap_cores(dec_here), swap_cores(enc_here)
     attr_keep = jnp.zeros((rows, acts.shape[2]), jnp.float32)
     grad_keep = jnp.zeros(cotangent.shape, jnp.bfloat16)
     g_half = lax.dynamic_slice_in_dim(cotangent, mine, half, axis=1)
@@ -211,7 +201,15 @@
         s = jnp.where(is_own, small, other_small)
         gain_half = lax.dynamic_slice_in_dim(s[:width], mine, half, axis=0)
         scale_l = s[width:width + rows]
-        attr, g_half = split_layer(g_half, routes[0], acts[0], own, other, is_own, gain_half, scale_l)
+        if layer == 0:
+            first, second = (dec_here, enc_here), (dec_there, enc_there)
+        else:
+            first, second = (dec_there, enc_there), (dec_here, enc_here)
+        first = (first[0][:, :half], first[1][:, :half])
+        second = (second[0][:, half:], second[1][:, half:])
+        attr, g_half = split_layer(
+            g_half, routes[0], acts[0], first, second, is_own, gain_half, scale_l
+        )
         partner = swap_cores(g_half)
         full = jnp.where(
             here == 0,

time: 98.1 us -> 106 us (1.081)
  the two profiles are of different devices: /device:TPU:0 before, /device:TPU:7 now
where the time goes in v3:
time: 106 us; the launch traced here: 105 us
  starting transfers between devices  55.4 us (52%)
  waiting for transfers between devices  28.4 us (27%)
  matrix products  8.04 us (8%)
  local copies, waits for them, and re-layouts  7.63 us (7%)
  other arithmetic  4.83 us (5%)
  between operations  1.11 us (1%)
    ppermute x28, starting transfers between devices, exchange(): moved.append(lax.ppermute(parts[shift], 'dict', route))  40.3 us
    ppermute x28, waiting for transfers between devices, exchange(): moved.append(lax.ppermute(parts[shift], 'dict', route))  26.5 us
    ppermute x7, starting transfers between devices, swap_cores(): return lax.ppermute(block, 'section', [(0, 1), (1, 0)])  15.1 us
    unnamed x41, local copies, waits for them, and re-layouts  4.83 us
    dot_general x4, matrix products, with_enc(): return jnp.dot(dz, enc, preferred_element_type=jnp.float32)  3.87 us
    dot_general x4, matrix products, with_dec(): lax.dot_general(g_all, dec, (((1,), (1,)), ((), ())), preferred_element_t...  3.6 us
  transfers between devices with their start and end apart: 35, of which 12 were waited for; matrix products, arithmetic and copies ran while one was open for 12% of the time, Pallas kernels for 0%

profile of v3, /device:TPU:7, one launch (start us, length us, event | category | flops | bytes accessed | tf_op | source)
XLA Modules:
  0.0 105.4 jit_solution(17640292136778143260)
XLA Ops:
  4.5 1.3 %collective-permute-start.1 = (bf16[16,2560]{1,0:T(8,128)(2,1)S(1)}, bf16[16,2560]{1,0:T(8,128)(2,1)S(1)}, u32[]{:S(2)}, u32[]{:S(2)}) collective-permute-start(bf16[16,2560]{1,0:T(8,128)(2,1)S(1)} %get-tuple-element.12), channel_id=1, source_target_pairs={{0,2},{2,4},{4,6},{6,8},{8,10},{10,12},{12,14},{14,0},{1,3},{3,5},... | collective-permute-start | bytes 245768 | tf_op jit(solution)/shard_map/ppermute | solution.py:124
  6.0 1.3 %collective-permute-start.2 = (bf16[16,2560]{1,0:T(8,128)(2,1)S(1)}, bf16[16,2560]{1,0:T(8,128)(2,1)S(1)}, u32[]{:S(2)}, u32[]{:S(2)}) collective-permute-start(bf16[16,2560]{1,0:T(8,128)(2,1)S(1)} %get-tuple-element.13), channel_id=1, source_target_pairs={{0,4},{2,6},{4,8},{6,10},{8,12},{10,14},{12,0},{14,2},{1,5},{3,7},... | collective-permute-start | bytes 245768 | tf_op jit(solution)/shard_map/ppermute | solution.py:124
  7.2 3.2 %collective-permute-start.3 = (bf16[16,2560]{1,0:T(8,128)(2,1)S(1)}, bf16[16,2560]{1,0:T(8,128)(2,1)S(1)}, u32[]{:S(2)}, u32[]{:S(2)}) collective-permute-start(bf16[16,2560]{1,0:T(8,128)(2,1)S(1)} %get-tuple-element.14), channel_id=1, source_target_pairs={{0,6},{2,8},{4,10},{6,12},{8,14},{10,0},{12,2},{14,4},{1,7},{3,9},... | collective-permute-start | bytes 245768 | tf_op jit(solution)/shard_map/ppermute | solution.py:124
  11.1 1.8 %collective-permute-start.5 = (bf16[16,2560]{1,0:T(8,128)(2,1)S(1)}, bf16[16,2560]{1,0:T(8,128)(2,1)S(1)}, u32[]{:S(2)}, u32[]{:S(2)}) collective-permute-start(bf16[16,2560]{1,0:T(8,128)(2,1)S(1)} %get-tuple-element.16), channel_id=1, source_target_pairs={{0,10},{2,12},{4,14},{6,0},{8,2},{10,4},{12,6},{14,8},{1,11},{3,13... | collective-permute-start | bytes 245768 | tf_op jit(solution)/shard_map/ppermute | solution.py:124
  13.6 1.5 %collective-permute-start.6 = (bf16[16,2560]{1,0:T(8,128)(2,1)S(1)}, bf16[16,2560]{1,0:T(8,128)(2,1)S(1)}, u32[]{:S(2)}, u32[]{:S(2)}) collective-permute-start(bf16[16,2560]{1,0:T(8,128)(2,1)S(1)} %get-tuple-element.17), channel_id=1, source_target_pairs={{0,12},{2,14},{4,0},{6,2},{8,4},{10,6},{12,8},{14,10},{1,13},{3,15... | collective-permute-start | bytes 245768 | tf_op jit(solution)/shard_map/ppermute | solution.py:124
  15.8 3.0 %collective-permute-start.8 = (bf16[256,4608]{1,0:T(8,128)(2,1)}, bf16[256,4608]{1,0:T(8,128)(2,1)S(1)}, u32[]{:S(2)}, u32[]{:S(2)}) collective-permute-start(bf16[256,4608]{1,0:T(8,128)(2,1)} %bitcast.160), channel_id=1, source_target_pairs={{0,1},{1,0},{2,3},{3,2},{4,5},{5,4},{6,7},{7,6},{8,9},{9,8},{10,11... | collective-permute-start | bytes 7077896 | tf_op jit(solution)/shard_map/ppermute | solution.py:116
  21.2 1.7 %collective-permute-done.5 = bf16[16,2560]{1,0:T(8,128)(2,1)S(1)} collective-permute-done((bf16[16,2560]{1,0:T(8,128)(2,1)S(1)}, bf16[16,2560]{1,0:T(8,128)(2,1)S(1)}, u32[]{:S(2)}, u32[]{:S(2)}) %collective-permute-start.5) | collective-permute-done | bytes 81952 | tf_op jit(solution)/shard_map/ppermute | solution.py:124
  25.7 2.0 %fusion.12 = f32[128,256]{1,0:T(8,128)S(1)} fusion(bf16[256,4608]{1,0:T(8,128)(2,1)} %bitcast.161, bf16[128,2560]{1,0:T(8,128)(2,1)} %bitcast.148), kind=kOutput, calls=%fused_computation.49 | convolution fusion | flops 150994944 | bytes 1900544 | tf_op jit(solution)/shard_map/dot_general | solution.py:154
  28.3 1.9 %collective-permute-start.9 = (f32[128,512]{1,0:T(8,128)S(1)}, f32[128,512]{1,0:T(8,128)S(1)}, u32[]{:S(2)}, u32[]{:S(2)}) collective-permute-start(f32[128,512]{1,0:T(8,128)S(1)} %pad_maximum_fusion), channel_id=1, source_target_pairs={{0,1},{1,0},{2,3},{3,2},{4,5},{5,4},{6,7},{7,6},{8,9},{9,8},{10,11... | collective-permute-start | bytes 786440 | tf_op jit(solution)/shard_map/ppermute | solution.py:116
  33.2 1.6 %fusion = bf16[128,2304]{1,0:T(8,128)(2,1)S(1)} fusion(bf16[128,2304]{1,0:T(8,128)(2,1)S(1)} %fusion.9, bf16[128,256]{1,0:T(8,128)(2,1)S(1)} %fusion.36, bf16[256,4608]{1,0:T(8,128)(2,1)} %collective-permute-done.10, pred[]{:T(512)S(6)} %eq.19), kind=kOutput, calls=%fused_computation.2 | convolution fusion | flops 151289856 | bytes 2424833 | tf_op jit(solution)/shard_map/dot_general | solution.py:166
  35.0 2.3 %collective-permute-start.17 = (bf16[16,2432]{1,0:T(8,128)(2,1)S(1)}, bf16[16,2432]{1,0:T(8,128)(2,1)S(1)}, u32[]{:S(2)}, u32[]{:S(2)}) collective-permute-start(bf16[16,2432]{1,0:T(8,128)(2,1)S(1)} %get-tuple-element.25), channel_id=1, source_target_pairs={{0,2},{2,4},{4,6},{6,8},{8,10},{10,12},{12,14},{14,0},{1,3},{3,5},... | collective-permute-start | bytes 233480 | tf_op jit(solution)/shard_map/ppermute | solution.py:124
  37.3 4.3 %collective-permute-start.12 = (bf16[16,2432]{1,0:T(8,128)(2,1)S(1)}, bf16[16,2432]{1,0:T(8,128)(2,1)S(1)}, u32[]{:S(2)}, u32[]{:S(2)}) collective-permute-start(bf16[16,2432]{1,0:T(8,128)(2,1)S(1)} %get-tuple-element.27), channel_id=1, source_target_pairs={{0,12},{2,14},{4,0},{6,2},{8,4},{10,6},{12,8},{14,10},{1,13},{3,15... | collective-permute-start | bytes 233480 | tf_op jit(solution)/shard_map/ppermute | solution.py:124
  41.6 3.3 %collective-permute-start.15 = (bf16[16,2432]{1,0:T(8,128)(2,1)S(1)}, bf16[16,2432]{1,0:T(8,128)(2,1)S(1)}, u32[]{:S(2)}, u32[]{:S(2)}) collective-permute-start(bf16[16,2432]{1,0:T(8,128)(2,1)S(1)} %get-tuple-element.30), channel_id=1, source_target_pairs={{0,6},{2,8},{4,10},{6,12},{8,14},{10,0},{12,2},{14,4},{1,7},{3,9},... | collective-permute-start | bytes 233480 | tf_op jit(solution)/shard_map/ppermute | solution.py:124
  45.3 7.4 %collective-permute-done.13 = bf16[16,2432]{1,0:T(8,128)(2,1)S(1)} collective-permute-done((bf16[16,2432]{1,0:T(8,128)(2,1)S(1)}, bf16[16,2432]{1,0:T(8,128)(2,1)S(1)}, u32[]{:S(2)}, u32[]{:S(2)}) %collective-permute-start.13) | collective-permute-done | bytes 77856 | tf_op jit(solution)/shard_map/ppermute | solution.py:124
  53.8 1.9 %collective-permute-start.24 = (bf16[16,2560]{1,0:T(8,128)(2,1)S(1)}, bf16[16,2560]{1,0:T(8,128)(2,1)S(1)}, u32[]{:S(2)}, u32[]{:S(2)}) collective-permute-start(bf16[16,2560]{1,0:T(8,128)(2,1)S(1)} %get-tuple-element.2), channel_id=1, source_target_pairs={{0,14},{2,0},{4,2},{6,4},{8,6},{10,8},{12,10},{14,12},{1,15},{3,1}... | collective-permute-start | bytes 245768 | tf_op jit(solution)/shard_map/ppermute | solution.py:124
  56.0 2.6 %collective-permute-start.20 = (bf16[16,2560]{1,0:T(8,128)(2,1)S(1)}, bf16[16,2560]{1,0:T(8,128)(2,1)S(1)}, u32[]{:S(2)}, u32[]{:S(2)}) collective-permute-start(bf16[16,2560]{1,0:T(8,128)(2,1)S(1)} %get-tuple-element.6), channel_id=1, source_target_pairs={{0,6},{2,8},{4,10},{6,12},{8,14},{10,0},{12,2},{14,4},{1,7},{3,9},... | collective-permute-start | bytes 245768 | tf_op jit(solution)/shard_map/ppermute | solution.py:124
  58.6 3.3 %collective-permute-start.21 = (bf16[16,2560]{1,0:T(8,128)(2,1)S(1)}, bf16[16,2560]{1,0:T(8,128)(2,1)S(1)}, u32[]{:S(2)}, u32[]{:S(2)}) collective-permute-start(bf16[16,2560]{1,0:T(8,128)(2,1)S(1)} %get-tuple-element.7), channel_id=1, source_target_pairs={{0,8},{2,10},{4,12},{6,14},{8,0},{10,2},{12,4},{14,6},{1,9},{3,11}... | collective-permute-start | bytes 245768 | tf_op jit(solution)/shard_map/ppermute | solution.py:124
  61.9 1.0 collective-permute-start.22
  62.9 2.4 %collective-permute-start.23 = (bf16[16,2560]{1,0:T(8,128)(2,1)S(1)}, bf16[16,2560]{1,0:T(8,128)(2,1)S(1)}, u32[]{:S(2)}, u32[]{:S(2)}) collective-permute-start(bf16[16,2560]{1,0:T(8,128)(2,1)S(1)} %get-tuple-element.9), channel_id=1, source_target_pairs={{0,12},{2,14},{4,0},{6,2},{8,4},{10,6},{12,8},{14,10},{1,13},{3,15... | collective-permute-start | bytes 245768 | tf_op jit(solution)/shard_map/ppermute | solution.py:124
  65.6 4.7 %collective-permute-done.21 = bf16[16,2560]{1,0:T(8,128)(2,1)S(1)} collective-permute-done((bf16[16,2560]{1,0:T(8,128)(2,1)S(1)}, bf16[16,2560]{1,0:T(8,128)(2,1)S(1)}, u32[]{:S(2)}, u32[]{:S(2)}) %collective-permute-start.21) | collective-permute-done | bytes 81952 | tf_op jit(solution)/shard_map/ppermute | solution.py:124
  70.4 2.5 %collective-permute-done.22 = bf16[16,2560]{1,0:T(8,128)(2,1)S(1)} collective-permute-done((bf16[16,2560]{1,0:T(8,128)(2,1)S(1)}, bf16[16,2560]{1,0:T(8,128)(2,1)S(1)}, u32[]{:S(2)}, u32[]{:S(2)}) %collective-permute-start.22) | collective-permute-done | bytes 81952 | tf_op jit(solution)/shard_map/ppermute | solution.py:124
  74.1 2.0 %collective-permute-start.25 = (f32[128,512]{1,0:T(8,128)S(1)}, f32[128,512]{1,0:T(8,128)S(1)}, u32[]{:S(2)}, u32[]{:S(2)}) collective-permute-start(f32[128,512]{1,0:T(8,128)S(1)} %pad_maximum_fusion.1), channel_id=1, source_target_pairs={{0,1},{1,0},{2,3},{3,2},{4,5},{5,4},{6,7},{7,6},{8,9},{9,8},{10,11... | collective-permute-start | bytes 786440 | tf_op jit(solution)/shard_map/ppermute | solution.py:116
  76.3 1.0 collective-permute-done.25
  77.4 1.6 %fusion.2 = bf16[128,2304]{1,0:T(8,128)(2,1)S(1)} fusion(bf16[128,256]{1,0:T(8,128)(2,1)S(1)} %fusion.37, bf16[256,4608]{1,0:T(8,128)(2,1)} %collective-permute-done.10), kind=kOutput, calls=%fused_computation.39 | convolution fusion | flops 150994944 | bytes 1835008 | tf_op jit(solution)/shard_map/dot_general | solution.py:166
  79.4 2.3 %collective-permute-start.32 = (bf16[16,2432]{1,0:T(8,128)(2,1)S(1)}, bf16[16,2432]{1,0:T(8,128)(2,1)S(1)}, u32[]{:S(2)}, u32[]{:S(2)}) collective-permute-start(bf16[16,2432]{1,0:T(8,128)(2,1)S(1)} %get-tuple-element.18), channel_id=1, source_target_pairs={{0,2},{2,4},{4,6},{6,8},{8,10},{10,12},{12,14},{14,0},{1,3},{3,5},... | collective-permute-start | bytes 233480 | tf_op jit(solution)/shard_map/ppermute | solution.py:124
  81.8 3.7 %collective-permute-start.27 = (bf16[16,2432]{1,0:T(8,128)(2,1)S(1)}, bf16[16,2432]{1,0:T(8,128)(2,1)S(1)}, u32[]{:S(2)}, u32[]{:S(2)}) collective-permute-start(bf16[16,2432]{1,0:T(8,128)(2,1)S(1)} %get-tuple-element.20), channel_id=1, source_target_pairs={{0,12},{2,14},{4,0},{6,2},{8,4},{10,6},{12,8},{14,10},{1,13},{3,15... | collective-permute-start | bytes 233480 | tf_op jit(solution)/shard_map/ppermute | solution.py:124
  85.5 1.4 %collective-permute-done.27 = bf16[16,2432]{1,0:T(8,128)(2,1)S(1)} collective-permute-done((bf16[16,2432]{1,0:T(8,128)(2,1)S(1)}, bf16[16,2432]{1,0:T(8,128)(2,1)S(1)}, u32[]{:S(2)}, u32[]{:S(2)}) %collective-permute-start.27) | collective-permute-done | bytes 77856 | tf_op jit(solution)/shard_map/ppermute | solution.py:124
  86.9 1.9 %collective-permute-start.30 = (bf16[16,2432]{1,0:T(8,128)(2,1)S(1)}, bf16[16,2432]{1,0:T(8,128)(2,1)S(1)}, u32[]{:S(2)}, u32[]{:S(2)}) collective-permute-start(bf16[16,2432]{1,0:T(8,128)(2,1)S(1)} %get-tuple-element.23), channel_id=1, source_target_pairs={{0,6},{2,8},{4,10},{6,12},{8,14},{10,0},{12,2},{14,4},{1,7},{3,9},... | collective-permute-start | bytes 233480 | tf_op jit(solution)/shard_map/ppermute | solution.py:124
  88.8 2.5 %collective-permute-done.28 = bf16[16,2432]{1,0:T(8,128)(2,1)S(1)} collective-permute-done((bf16[16,2432]{1,0:T(8,128)(2,1)S(1)}, bf16[16,2432]{1,0:T(8,128)(2,1)S(1)}, u32[]{:S(2)}, u32[]{:S(2)}) %collective-permute-start.28) | collective-permute-done | bytes 77856 | tf_op jit(solution)/shard_map/ppermute | solution.py:124
  91.4 1.7 %collective-permute-done.30 = bf16[16,2432]{1,0:T(8,128)(2,1)S(1)} collective-permute-done((bf16[16,2432]{1,0:T(8,128)(2,1)S(1)}, bf16[16,2432]{1,0:T(8,128)(2,1)S(1)}, u32[]{:S(2)}, u32[]{:S(2)}) %collective-permute-start.30) | collective-permute-done | bytes 77856 | tf_op jit(solution)/shard_map/ppermute | solution.py:124
  93.2 3.5 %collective-permute-done.31 = bf16[16,2432]{1,0:T(8,128)(2,1)S(1)} collective-permute-done((bf16[16,2432]{1,0:T(8,128)(2,1)S(1)}, bf16[16,2432]{1,0:T(8,128)(2,1)S(1)}, u32[]{:S(2)}, u32[]{:S(2)}) %collective-permute-start.31) | collective-permute-done | bytes 77856 | tf_op jit(solution)/shard_map/ppermute | solution.py:124
  96.9 6.7 %collective-permute-start.33 = (bf16[16,2304]{1,0:T(8,128)(2,1)S(1)}, bf16[16,2304]{1,0:T(8,128)(2,1)S(1)}, u32[]{:S(2)}, u32[]{:S(2)}) collective-permute-start(bf16[16,2304]{1,0:T(8,128)(2,1)S(1)} %add_convert_fusion), channel_id=1, source_target_pairs={{0,1},{1,0},{2,3},{3,2},{4,5},{5,4},{6,7},{7,6},{8,9},{9,8},{10,11... | collective-permute-start | bytes 221192 | tf_op jit(solution)/shard_map/ppermute | solution.py:116
  (134 shorter events, 20.9 us)
Async XLA Ops:
  4.5 6.6 %collective-permute-start.1 = (bf16[16,2560]{1,0:T(8,128)(2,1)S(1)}, bf16[16,2560]{1,0:T(8,128)(2,1)S(1)}, u32[]{:S(2)}, u32[]{:S(2)}) collective-permute-start(bf16[16,2560]{1,0:T(8,128)(2,1)S(1)} %get-tuple-element.12), channel_id=1, source_target_pairs={{0,2},{2,4},{4,6},{6,8},{8,10},{10,12},{12,14},{14,0},{1,3},{3,5},... | collective-permute-start | bytes 245768 | tf_op jit(solution)/shard_map/ppermute | solution.py:124
  5.8 18.4 %collective-permute-start.7 = (bf16[16,2560]{1,0:T(8,128)(2,1)S(1)}, bf16[16,2560]{1,0:T(8,128)(2,1)S(1)}, u32[]{:S(2)}, u32[]{:S(2)}) collective-permute-start(bf16[16,2560]{1,0:T(8,128)(2,1)S(1)} %get-tuple-element.10), channel_id=1, source_target_pairs={{0,14},{2,0},{4,2},{6,4},{8,6},{10,8},{12,10},{14,12},{1,15},{3,1}... | collective-permute-start | bytes 245768 | tf_op jit(solution)/shard_map/ppermute | solution.py:124
  6.0 7.6 %collective-permute-start.2 = (bf16[16,2560]{1,0:T(8,128)(2,1)S(1)}, bf16[16,2560]{1,0:T(8,128)(2,1)S(1)}, u32[]{:S(2)}, u32[]{:S(2)}) collective-permute-start(bf16[16,2560]{1,0:T(8,128)(2,1)S(1)} %get-tuple-element.13), channel_id=1, source_target_pairs={{0,4},{2,6},{4,8},{6,10},{8,12},{10,14},{12,0},{14,2},{1,5},{3,7},... | collective-permute-start | bytes 245768 | tf_op jit(solution)/shard_map/ppermute | solution.py:124
  7.2 8.5 %collective-permute-start.3 = (bf16[16,2560]{1,0:T(8,128)(2,1)S(1)}, bf16[16,2560]{1,0:T(8,128)(2,1)S(1)}, u32[]{:S(2)}, u32[]{:S(2)}) collective-permute-start(bf16[16,2560]{1,0:T(8,128)(2,1)S(1)} %get-tuple-element.14), channel_id=1, source_target_pairs={{0,6},{2,8},{4,10},{6,12},{8,14},{10,0},{12,2},{14,4},{1,7},{3,9},... | collective-permute-start | bytes 245768 | tf_op jit(solution)/shard_map/ppermute | solution.py:124
  10.4 9.6 %collective-permute-start.4 = (bf16[16,2560]{1,0:T(8,128)(2,1)S(1)}, bf16[16,2560]{1,0:T(8,128)(2,1)S(1)}, u32[]{:S(2)}, u32[]{:S(2)}) collective-permute-start(bf16[16,2560]{1,0:T(8,128)(2,1)S(1)} %get-tuple-element.15), channel_id=1, source_target_pairs={{0,8},{2,10},{4,12},{6,14},{8,0},{10,2},{12,4},{14,6},{1,9},{3,11}... | collective-permute-start | bytes 245768 | tf_op jit(solution)/shard_map/ppermute | solution.py:124
  11.1 11.7 %collective-permute-start.5 = (bf16[16,2560]{1,0:T(8,128)(2,1)S(1)}, bf16[16,2560]{1,0:T(8,128)(2,1)S(1)}, u32[]{:S(2)}, u32[]{:S(2)}) collective-permute-start(bf16[16,2560]{1,0:T(8,128)(2,1)S(1)} %get-tuple-element.16), channel_id=1, source_target_pairs={{0,10},{2,12},{4,14},{6,0},{8,2},{10,4},{12,6},{14,8},{1,11},{3,13... | collective-permute-start | bytes 245768 | tf_op jit(solution)/shard_map/ppermute | solution.py:124
  13.6 10.0 %collective-permute-start.6 = (bf16[16,2560]{1,0:T(8,128)(2,1)S(1)}, bf16[16,2560]{1,0:T(8,128)(2,1)S(1)}, u32[]{:S(2)}, u32[]{:S(2)}) collective-permute-start(bf16[16,2560]{1,0:T(8,128)(2,1)S(1)} %get-tuple-element.17), channel_id=1, source_target_pairs={{0,12},{2,14},{4,0},{6,2},{8,4},{10,6},{12,8},{14,10},{1,13},{3,15... | collective-permute-start | bytes 245768 | tf_op jit(solution)/shard_map/ppermute | solution.py:124
  15.8 12.0 %collective-permute-start.8 = (bf16[256,4608]{1,0:T(8,128)(2,1)}, bf16[256,4608]{1,0:T(8,128)(2,1)S(1)}, u32[]{:S(2)}, u32[]{:S(2)}) collective-permute-start(bf16[256,4608]{1,0:T(8,128)(2,1)} %bitcast.160), channel_id=1, source_target_pairs={{0,1},{1,0},{2,3},{3,2},{4,5},{5,4},{6,7},{7,6},{8,9},{9,8},{10,11... | collective-permute-start | bytes 7077896 | tf_op jit(solution)/shard_map/ppermute | solution.py:116
  20.0 13.2 %collective-permute-start.10 = (bf16[256,4608]{1,0:T(8,128)(2,1)S(1)}, bf16[256,4608]{1,0:T(8,128)(2,1)}, u32[]{:S(2)}, u32[]{:S(2)}) collective-permute-start(bf16[256,4608]{1,0:T(8,128)(2,1)S(1)} %bitcast.137), channel_id=1, source_target_pairs={{0,1},{1,0},{2,3},{3,2},{4,5},{5,4},{6,7},{7,6},{8,9},{9,8},{10,11... | collective-permute-start | bytes 7077896 | tf_op jit(solution)/shard_map/ppermute | solution.py:116
  34.9 6.7 %collective-permute-start.11 = (bf16[16,2432]{1,0:T(8,128)(2,1)S(1)}, bf16[16,2432]{1,0:T(8,128)(2,1)S(1)}, u32[]{:S(2)}, u32[]{:S(2)}) collective-permute-start(bf16[16,2432]{1,0:T(8,128)(2,1)S(1)} %get-tuple-element.26), channel_id=1, source_target_pairs={{0,14},{2,0},{4,2},{6,4},{8,6},{10,8},{12,10},{14,12},{1,15},{3,1}... | collective-permute-start | bytes 233480 | tf_op jit(solution)/shard_map/ppermute | solution.py:124
  35.0 17.8 %collective-permute-start.17 = (bf16[16,2432]{1,0:T(8,128)(2,1)S(1)}, bf16[16,2432]{1,0:T(8,128)(2,1)S(1)}, u32[]{:S(2)}, u32[]{:S(2)}) collective-permute-start(bf16[16,2432]{1,0:T(8,128)(2,1)S(1)} %get-tuple-element.25), channel_id=1, source_target_pairs={{0,2},{2,4},{4,6},{6,8},{8,10},{10,12},{12,14},{14,0},{1,3},{3,5},... | collective-permute-start | bytes 233480 | tf_op jit(solution)/shard_map/ppermute | solution.py:124
  37.3 7.6 %collective-permute-start.12 = (bf16[16,2432]{1,0:T(8,128)(2,1)S(1)}, bf16[16,2432]{1,0:T(8,128)(2,1)S(1)}, u32[]{:S(2)}, u32[]{:S(2)}) collective-permute-start(bf16[16,2432]{1,0:T(8,128)(2,1)S(1)} %get-tuple-element.27), channel_id=1, source_target_pairs={{0,12},{2,14},{4,0},{6,2},{8,4},{10,6},{12,8},{14,10},{1,13},{3,15... | collective-permute-start | bytes 233480 | tf_op jit(solution)/shard_map/ppermute | solution.py:124
  41.6 11.0 %collective-permute-start.13 = (bf16[16,2432]{1,0:T(8,128)(2,1)S(1)}, bf16[16,2432]{1,0:T(8,128)(2,1)S(1)}, u32[]{:S(2)}, u32[]{:S(2)}) collective-permute-start(bf16[16,2432]{1,0:T(8,128)(2,1)S(1)} %get-tuple-element.28), channel_id=1, source_target_pairs={{0,10},{2,12},{4,14},{6,0},{8,2},{10,4},{12,6},{14,8},{1,11},{3,13... | collective-permute-start | bytes 233480 | tf_op jit(solution)/shard_map/ppermute | solution.py:124
  41.6 11.1 %collective-permute-start.14 = (bf16[16,2432]{1,0:T(8,128)(2,1)S(1)}, bf16[16,2432]{1,0:T(8,128)(2,1)S(1)}, u32[]{:S(2)}, u32[]{:S(2)}) collective-permute-start(bf16[16,2432]{1,0:T(8,128)(2,1)S(1)} %get-tuple-element.29), channel_id=1, source_target_pairs={{0,8},{2,10},{4,12},{6,14},{8,0},{10,2},{12,4},{14,6},{1,9},{3,11}... | collective-permute-start | bytes 233480 | tf_op jit(solution)/shard_map/ppermute | solution.py:124
  41.6 11.1 %collective-permute-start.15 = (bf16[16,2432]{1,0:T(8,128)(2,1)S(1)}, bf16[16,2432]{1,0:T(8,128)(2,1)S(1)}, u32[]{:S(2)}, u32[]{:S(2)}) collective-permute-start(bf16[16,2432]{1,0:T(8,128)(2,1)S(1)} %get-tuple-element.30), channel_id=1, source_target_pairs={{0,6},{2,8},{4,10},{6,12},{8,14},{10,0},{12,2},{14,4},{1,7},{3,9},... | collective-permute-start | bytes 233480 | tf_op jit(solution)/shard_map/ppermute | solution.py:124
  44.9 7.8 %collective-permute-start.16 = (bf16[16,2432]{1,0:T(8,128)(2,1)S(1)}, bf16[16,2432]{1,0:T(8,128)(2,1)S(1)}, u32[]{:S(2)}, u32[]{:S(2)}) collective-permute-start(bf16[16,2432]{1,0:T(8,128)(2,1)S(1)} %get-tuple-element.31), channel_id=1, source_target_pairs={{0,4},{2,6},{4,8},{6,10},{8,12},{10,14},{12,0},{14,2},{1,5},{3,7},... | collective-permute-start | bytes 233480 | tf_op jit(solution)/shard_map/ppermute | solution.py:124
  53.1 8.8 %collective-permute-start.18 = (bf16[16,2560]{1,0:T(8,128)(2,1)S(1)}, bf16[16,2560]{1,0:T(8,128)(2,1)S(1)}, u32[]{:S(2)}, u32[]{:S(2)}) collective-permute-start(bf16[16,2560]{1,0:T(8,128)(2,1)S(1)} %get-tuple-element.4), channel_id=1, source_target_pairs={{0,2},{2,4},{4,6},{6,8},{8,10},{10,12},{12,14},{14,0},{1,3},{3,5},... | collective-permute-start | bytes 245768 | tf_op jit(solution)/shard_map/ppermute | solution.py:124
  53.8 19.2 %collective-permute-start.24 = (bf16[16,2560]{1,0:T(8,128)(2,1)S(1)}, bf16[16,2560]{1,0:T(8,128)(2,1)S(1)}, u32[]{:S(2)}, u32[]{:S(2)}) collective-permute-start(bf16[16,2560]{1,0:T(8,128)(2,1)S(1)} %get-tuple-element.2), channel_id=1, source_target_pairs={{0,14},{2,0},{4,2},{6,4},{8,6},{10,8},{12,10},{14,12},{1,15},{3,1}... | collective-permute-start | bytes 245768 | tf_op jit(solution)/shard_map/ppermute | solution.py:124
  55.7 7.2 %collective-permute-start.19 = (bf16[16,2560]{1,0:T(8,128)(2,1)S(1)}, bf16[16,2560]{1,0:T(8,128)(2,1)S(1)}, u32[]{:S(2)}, u32[]{:S(2)}) collective-permute-start(bf16[16,2560]{1,0:T(8,128)(2,1)S(1)} %get-tuple-element.5), channel_id=1, source_target_pairs={{0,4},{2,6},{4,8},{6,10},{8,12},{10,14},{12,0},{14,2},{1,5},{3,7},... | collective-permute-start | bytes 245768 | tf_op jit(solution)/shard_map/ppermute | solution.py:124
  56.0 9.6 %collective-permute-start.20 = (bf16[16,2560]{1,0:T(8,128)(2,1)S(1)}, bf16[16,2560]{1,0:T(8,128)(2,1)S(1)}, u32[]{:S(2)}, u32[]{:S(2)}) collective-permute-start(bf16[16,2560]{1,0:T(8,128)(2,1)S(1)} %get-tuple-element.6), channel_id=1, source_target_pairs={{0,6},{2,8},{4,10},{6,12},{8,14},{10,0},{12,2},{14,4},{1,7},{3,9},... | collective-permute-start | bytes 245768 | tf_op jit(solution)/shard_map/ppermute | solution.py:124
  58.6 11.8 %collective-permute-start.21 = (bf16[16,2560]{1,0:T(8,128)(2,1)S(1)}, bf16[16,2560]{1,0:T(8,128)(2,1)S(1)}, u32[]{:S(2)}, u32[]{:S(2)}) collective-permute-start(bf16[16,2560]{1,0:T(8,128)(2,1)S(1)} %get-tuple-element.7), channel_id=1, source_target_pairs={{0,8},{2,10},{4,12},{6,14},{8,0},{10,2},{12,4},{14,6},{1,9},{3,11}... | collective-permute-start | bytes 245768 | tf_op jit(solution)/shard_map/ppermute | solution.py:124
  61.9 11.0 %collective-permute-start.22 = (bf16[16,2560]{1,0:T(8,128)(2,1)S(1)}, bf16[16,2560]{1,0:T(8,128)(2,1)S(1)}, u32[]{:S(2)}, u32[]{:S(2)}) collective-permute-start(bf16[16,2560]{1,0:T(8,128)(2,1)S(1)} %get-tuple-element.8), channel_id=1, source_target_pairs={{0,10},{2,12},{4,14},{6,0},{8,2},{10,4},{12,6},{14,8},{1,11},{3,13... | collective-permute-start | bytes 245768 | tf_op jit(solution)/shard_map/ppermute | solution.py:124
  62.9 10.0 %collective-permute-start.23 = (bf16[16,2560]{1,0:T(8,128)(2,1)S(1)}, bf16[16,2560]{1,0:T(8,128)(2,1)S(1)}, u32[]{:S(2)}, u32[]{:S(2)}) collective-permute-start(bf16[16,2560]{1,0:T(8,128)(2,1)S(1)} %get-tuple-element.9), channel_id=1, source_target_pairs={{0,12},{2,14},{4,0},{6,2},{8,4},{10,6},{12,8},{14,10},{1,13},{3,15... | collective-permute-start | bytes 245768 | tf_op jit(solution)/shard_map/ppermute | solution.py:124
  76.2 28.4 %collective-permute-start.34 = (bf16[16,2304]{1,0:T(8,128)(2,1)S(1)}, bf16[16,2304]{1,0:T(8,128)(2,1)S(1)}, u32[]{:S(2)}, u32[]{:S(2)}) collective-permute-start(bf16[16,2304]{1,0:T(8,128)(2,1)S(1)} %add_convert_fusion.1), channel_id=1, source_target_pairs={{0,1},{1,0},{2,3},{3,2},{4,5},{5,4},{6,7},{7,6},{8,9},{9,8},{10,11... | collective-permute-start | bytes 221192 | tf_op jit(solution)/shard_map/ppermute | solution.py:116
  79.4 6.1 %collective-permute-start.26 = (bf16[16,2432]{1,0:T(8,128)(2,1)S(1)}, bf16[16,2432]{1,0:T(8,128)(2,1)S(1)}, u32[]{:S(2)}, u32[]{:S(2)}) collective-permute-start(bf16[16,2432]{1,0:T(8,128)(2,1)S(1)} %get-tuple-element.19), channel_id=1, source_target_pairs={{0,14},{2,0},{4,2},{6,4},{8,6},{10,8},{12,10},{14,12},{1,15},{3,1}... | collective-permute-start | bytes 233480 | tf_op jit(solution)/shard_map/ppermute | solution.py:124
  79.4 17.2 %collective-permute-start.32 = (bf16[16,2432]{1,0:T(8,128)(2,1)S(1)}, bf16[16,2432]{1,0:T(8,128)(2,1)S(1)}, u32[]{:S(2)}, u32[]{:S(2)}) collective-permute-start(bf16[16,2432]{1,0:T(8,128)(2,1)S(1)} %get-tuple-element.18), channel_id=1, source_target_pairs={{0,2},{2,4},{4,6},{6,8},{8,10},{10,12},{12,14},{14,0},{1,3},{3,5},... | collective-permute-start | bytes 233480 | tf_op jit(solution)/shard_map/ppermute | solution.py:124
  81.8 5.1 %collective-permute-start.27 = (bf16[16,2432]{1,0:T(8,128)(2,1)S(1)}, bf16[16,2432]{1,0:T(8,128)(2,1)S(1)}, u32[]{:S(2)}, u32[]{:S(2)}) collective-permute-start(bf16[16,2432]{1,0:T(8,128)(2,1)S(1)} %get-tuple-element.20), channel_id=1, source_target_pairs={{0,12},{2,14},{4,0},{6,2},{8,4},{10,6},{12,8},{14,10},{1,13},{3,15... | collective-permute-start | bytes 233480 | tf_op jit(solution)/shard_map/ppermute | solution.py:124
  85.5 5.9 %collective-permute-start.28 = (bf16[16,2432]{1,0:T(8,128)(2,1)S(1)}, bf16[16,2432]{1,0:T(8,128)(2,1)S(1)}, u32[]{:S(2)}, u32[]{:S(2)}) collective-permute-start(bf16[16,2432]{1,0:T(8,128)(2,1)S(1)} %get-tuple-element.21), channel_id=1, source_target_pairs={{0,10},{2,12},{4,14},{6,0},{8,2},{10,4},{12,6},{14,8},{1,11},{3,13... | collective-permute-start | bytes 233480 | tf_op jit(solution)/shard_map/ppermute | solution.py:124
  85.5 5.9 %collective-permute-start.29 = (bf16[16,2432]{1,0:T(8,128)(2,1)S(1)}, bf16[16,2432]{1,0:T(8,128)(2,1)S(1)}, u32[]{:S(2)}, u32[]{:S(2)}) collective-permute-start(bf16[16,2432]{1,0:T(8,128)(2,1)S(1)} %get-tuple-element.22), channel_id=1, source_target_pairs={{0,8},{2,10},{4,12},{6,14},{8,0},{10,2},{12,4},{14,6},{1,9},{3,11}... | collective-permute-start | bytes 233480 | tf_op jit(solution)/shard_map/ppermute | solution.py:124
  86.9 6.2 %collective-permute-start.30 = (bf16[16,2432]{1,0:T(8,128)(2,1)S(1)}, bf16[16,2432]{1,0:T(8,128)(2,1)S(1)}, u32[]{:S(2)}, u32[]{:S(2)}) collective-permute-start(bf16[16,2432]{1,0:T(8,128)(2,1)S(1)} %get-tuple-element.23), channel_id=1, source_target_pairs={{0,6},{2,8},{4,10},{6,12},{8,14},{10,0},{12,2},{14,4},{1,7},{3,9},... | collective-permute-start | bytes 233480 | tf_op jit(solution)/shard_map/ppermute | solution.py:124
  91.4 5.3 %collective-permute-start.31 = (bf16[16,2432]{1,0:T(8,128)(2,1)S(1)}, bf16[16,2432]{1,0:T(8,128)(2,1)S(1)}, u32[]{:S(2)}, u32[]{:S(2)}) collective-permute-start(bf16[16,2432]{1,0:T(8,128)(2,1)S(1)} %get-tuple-element.24), channel_id=1, source_target_pairs={{0,4},{2,6},{4,8},{6,10},{8,12},{10,14},{12,0},{14,2},{1,5},{3,7},... | collective-permute-start | bytes 233480 | tf_op jit(solution)/shard_map/ppermute | solution.py:124
  96.9 7.7 %collective-permute-start.33 = (bf16[16,2304]{1,0:T(8,128)(2,1)S(1)}, bf16[16,2304]{1,0:T(8,128)(2,1)S(1)}, u32[]{:S(2)}, u32[]{:S(2)}) collective-permute-start(bf16[16,2304]{1,0:T(8,128)(2,1)S(1)} %add_convert_fusion), channel_id=1, source_target_pairs={{0,1},{1,0},{2,3},{3,2},{4,5},{5,4},{6,7},{7,6},{8,9},{9,8},{10,11... | collective-permute-start | bytes 221192 | tf_op jit(solution)/shard_map/ppermute | solution.py:116
  (11 other events, 107.0 us)

commit v4 on v2

--- a/solution.py
+++ b/solution.py
@@ -197,8 +197,6 @@
         ],
         axis=0,
     )
-    other_w = swap_cores(sent_w)
-    other = (other_w[:blocks], other_w[blocks:])
     own = (
         lax.dynamic_slice_in_dim(decoder[0], mine, half, axis=1),
         lax.dynamic_slice_in_dim(encoder[0], mine, half, axis=1),
@@ -206,6 +204,9 @@
     attr_keep = jnp.zeros((rows, acts.shape[2]), jnp.float32)
     grad_keep = jnp.zeros(cotangent.shape, jnp.bfloat16)
     g_half = lax.dynamic_slice_in_dim(cotangent, mine, half, axis=1)
+    g_half, own, sent_w = lax.optimization_barrier((g_half, own, sent_w))
+    other_w = swap_cores(sent_w)
+    other = (other_w[:blocks], other_w[blocks:])
     for layer in reversed(range(depth)):
         is_own = here == layer
         s = jnp.where(is_own, small, other_small)

time: 98.1 us -> 103 us (1.050)
  starting transfers between devices: 55.3 us -> 60.9 us
  waiting for transfers between devices: 20.6 us -> 19.1 us
    ppermute x28, starting transfers between devices: 54 us -> 59.6 us  [exchange(): moved.append(lax.ppermute(parts[shift], 'dict', route))]
    ppermute x28, waiting for transfers between devices: 16.5 us -> 15.2 us  [exchange(): moved.append(lax.ppermute(parts[shift], 'dict', route))]
    dynamic_slice x1, local copies, waits for them, and re-layouts: 1.46 us -> 2.64 us  [split_device(): lax.dynamic_slice_in_dim(encoder[0], theirs, half, axis=1)]
  transfers between devices with their start and end apart: 34 -> 34, of which waited for: 12 -> 15; matrix products, arithmetic and copies ran while one was open for 11% -> 7% of each run, Pallas kernels for 0% -> 0%
where the time goes in v4:
time: 103 us
  starting transfers between devices  60.9 us (59%)
  waiting for transfers between devices  19.1 us (19%)
  local copies, waits for them, and re-layouts  9.84 us (10%)
  other arithmetic  6.56 us (6%)
  matrix products  5.32 us (5%)
  between operations  1.09 us (1%)
    ppermute x28, starting transfers between devices, exchange(): moved.append(lax.ppermute(parts[shift], 'dict', route))  59.6 us
    ppermute x28, waiting for transfers between devices, exchange(): moved.append(lax.ppermute(parts[shift], 'dict', route))  15.2 us
    unnamed x39, local copies, waits for them, and re-layouts  5.91 us
    ppermute x6, waiting for transfers between devices, swap_cores(): return lax.ppermute(block, 'section', [(0, 1), (1, 0)])  3.89 us
    dynamic_slice x1, local copies, waits for them, and re-layouts, split_device(): lax.dynamic_slice_in_dim(encoder[0], theirs, half, axis=1)  2.64 us
    dot_general x4, matrix products, with_enc(): return jnp.dot(dz, enc, preferred_element_type=jnp.float32)  2.6 us
    dot_general x4, matrix products, with_dec(): lax.dot_general(g_all, dec, (((1,), (1,)), ((), ())), preferred_element_t...  2.16 us
  transfers between devices with their start and end apart: 34, of which 15 were waited for; matrix products, arithmetic and copies ran while one was open for 7% of the time, Pallas kernels for 0%

profile of v4, /device:TPU:0, one launch (start us, length us, event | category | flops | bytes accessed | tf_op | source)
XLA Modules:
  0.0 102.7 jit_solution(151021761467504766)
XLA Ops:
  1.6 2.6 %dynamic-slice_bitcast_fusion = (bf16[256,2304]{1,0:T(8,128)(2,1)S(1)}, bf16[256,2304]{1,0:T(8,128)(2,1)S(1)}, bf16[256,2304]{1,0:T(8,128)(2,1)S(1)}, bf16[256,2304]{1,0:T(8,128)(2,1)S(1)}) fusion(bf16[1,256,4608]{2,1,0:T(8,128)(2,1)} %param.11, s32[]{:T(128)S(6)} %select_n.182, s32[]{:T(128)S(6)} %select_n.181, bf16[1,256,4608]{2,1,0:T(8,128)(2,1)} %param.10), kind=kLoop, calls=%fused_computation.42 | loop fusion | bytes 9437192 | tf_op jit(solution)/shard_map/dynamic_slice | solution.py:196
  4.2 1.6 %pad_maximum_fusion = bf16[512,2304]{1,0:T(8,128)(2,1)} fusion(bf16[256,2304]{1,0:T(8,128)(2,1)S(1)} %get-tuple-element.12, bf16[256,2304]{1,0:T(8,128)(2,1)S(1)} %get-tuple-element.49), kind=kLoop, calls=%fused_computation.4 | loop fusion | flops 4718592 | bytes 4718592 | tf_op jit(solution)/shard_map/concatenate | solution.py:193
  7.3 2.9 %collective-permute-start.1 = (bf16[16,2560]{1,0:T(8,128)(2,1)}, bf16[16,2560]{1,0:T(8,128)(2,1)}, u32[]{:S(2)}, u32[]{:S(2)}) collective-permute-start(bf16[16,2560]{1,0:T(8,128)(2,1)} %get-tuple-element.24), channel_id=1, source_target_pairs={{0,2},{2,4},{4,6},{6,8},{8,10},{10,12},{12,14},{14,0},{1,3},{3,5},... | collective-permute-start | bytes 245768 | tf_op jit(solution)/shard_map/ppermute | solution.py:124
  10.2 1.6 %collective-permute-start.2 = (bf16[16,2560]{1,0:T(8,128)(2,1)}, bf16[16,2560]{1,0:T(8,128)(2,1)}, u32[]{:S(2)}, u32[]{:S(2)}) collective-permute-start(bf16[16,2560]{1,0:T(8,128)(2,1)} %get-tuple-element.25), channel_id=1, source_target_pairs={{0,4},{2,6},{4,8},{6,10},{8,12},{10,14},{12,0},{14,2},{1,5},{3,7},... | collective-permute-start | bytes 245768 | tf_op jit(solution)/shard_map/ppermute | solution.py:124
  11.8 2.6 %collective-permute-start.3 = (bf16[16,2560]{1,0:T(8,128)(2,1)}, bf16[16,2560]{1,0:T(8,128)(2,1)}, u32[]{:S(2)}, u32[]{:S(2)}) collective-permute-start(bf16[16,2560]{1,0:T(8,128)(2,1)} %get-tuple-element.26), channel_id=1, source_target_pairs={{0,6},{2,8},{4,10},{6,12},{8,14},{10,0},{12,2},{14,4},{1,7},{3,9},... | collective-permute-start | bytes 245768 | tf_op jit(solution)/shard_map/ppermute | solution.py:124
  14.3 1.2 %collective-permute-start.4 = (bf16[16,2560]{1,0:T(8,128)(2,1)}, bf16[16,2560]{1,0:T(8,128)(2,1)}, u32[]{:S(2)}, u32[]{:S(2)}) collective-permute-start(bf16[16,2560]{1,0:T(8,128)(2,1)} %get-tuple-element.27), channel_id=1, source_target_pairs={{0,8},{2,10},{4,12},{6,14},{8,0},{10,2},{12,4},{14,6},{1,9},{3,11}... | collective-permute-start | bytes 245768 | tf_op jit(solution)/shard_map/ppermute | solution.py:124
  15.6 2.6 %collective-permute-start.5 = (bf16[16,2560]{1,0:T(8,128)(2,1)}, bf16[16,2560]{1,0:T(8,128)(2,1)}, u32[]{:S(2)}, u32[]{:S(2)}) collective-permute-start(bf16[16,2560]{1,0:T(8,128)(2,1)} %get-tuple-element.28), channel_id=1, source_target_pairs={{0,10},{2,12},{4,14},{6,0},{8,2},{10,4},{12,6},{14,8},{1,11},{3,13... | collective-permute-start | bytes 245768 | tf_op jit(solution)/shard_map/ppermute | solution.py:124
  18.3 1.4 %collective-permute-start.6 = (bf16[16,2560]{1,0:T(8,128)(2,1)}, bf16[16,2560]{1,0:T(8,128)(2,1)S(1)}, u32[]{:S(2)}, u32[]{:S(2)}) collective-permute-start(bf16[16,2560]{1,0:T(8,128)(2,1)} %get-tuple-element.29), channel_id=1, source_target_pairs={{0,12},{2,14},{4,0},{6,2},{8,4},{10,6},{12,8},{14,10},{1,13},{3,15... | collective-permute-start | bytes 245768 | tf_op jit(solution)/shard_map/ppermute | solution.py:124
  20.6 1.5 %collective-permute-start.7 = (bf16[16,2560]{1,0:T(8,128)(2,1)S(1)}, bf16[16,2560]{1,0:T(8,128)(2,1)S(1)}, u32[]{:S(2)}, u32[]{:S(2)}) collective-permute-start(bf16[16,2560]{1,0:T(8,128)(2,1)S(1)} %get-tuple-element.22), channel_id=1, source_target_pairs={{0,14},{2,0},{4,2},{6,4},{8,6},{10,8},{12,10},{14,12},{1,15},{3,1}... | collective-permute-start | bytes 245768 | tf_op jit(solution)/shard_map/ppermute | solution.py:124
  26.4 1.6 %collective-permute-done.8 = bf16[512,2304]{1,0:T(8,128)(2,1)S(1)} collective-permute-done((bf16[512,2304]{1,0:T(8,128)(2,1)}, bf16[512,2304]{1,0:T(8,128)(2,1)S(1)}, u32[]{:S(2)}, u32[]{:S(2)}) %collective-permute-start.8) | collective-permute-done | bytes 2359328 | tf_op jit(solution)/shard_map/ppermute | solution.py:116
  32.0 1.0 fusion.24
  33.0 1.6 %fusion.7 = bf16[128,2304]{1,0:T(8,128)(2,1)S(1)} fusion(bf16[128,256]{1,0:T(8,128)(2,1)S(1)} %fusion.24, bf16[512,2304]{1,0:T(8,128)(2,1)} %copy-done.1), kind=kOutput, calls=%fused_computation.56 | convolution fusion | flops 150994944 | bytes 1835008 | tf_op jit(solution)/shard_map/dot_general | solution.py:165
  35.0 4.3 %collective-permute-start.10 = (bf16[16,2432]{1,0:T(8,128)(2,1)S(1)}, bf16[16,2432]{1,0:T(8,128)(2,1)S(1)}, u32[]{:S(2)}, u32[]{:S(2)}) collective-permute-start(bf16[16,2432]{1,0:T(8,128)(2,1)S(1)} %get-tuple-element.38), channel_id=1, source_target_pairs={{0,14},{2,0},{4,2},{6,4},{8,6},{10,8},{12,10},{14,12},{1,15},{3,1}... | collective-permute-start | bytes 233480 | tf_op jit(solution)/shard_map/ppermute | solution.py:124
  39.3 1.7 %collective-permute-start.11 = (bf16[16,2432]{1,0:T(8,128)(2,1)S(1)}, bf16[16,2432]{1,0:T(8,128)(2,1)S(1)}, u32[]{:S(2)}, u32[]{:S(2)}) collective-permute-start(bf16[16,2432]{1,0:T(8,128)(2,1)S(1)} %get-tuple-element.39), channel_id=1, source_target_pairs={{0,12},{2,14},{4,0},{6,2},{8,4},{10,6},{12,8},{14,10},{1,13},{3,15... | collective-permute-start | bytes 233480 | tf_op jit(solution)/shard_map/ppermute | solution.py:124
  41.0 4.3 %collective-permute-start.13 = (bf16[16,2432]{1,0:T(8,128)(2,1)S(1)}, bf16[16,2432]{1,0:T(8,128)(2,1)S(1)}, u32[]{:S(2)}, u32[]{:S(2)}) collective-permute-start(bf16[16,2432]{1,0:T(8,128)(2,1)S(1)} %get-tuple-element.41), channel_id=1, source_target_pairs={{0,8},{2,10},{4,12},{6,14},{8,0},{10,2},{12,4},{14,6},{1,9},{3,11}... | collective-permute-start | bytes 233480 | tf_op jit(solution)/shard_map/ppermute | solution.py:124
  45.9 1.6 %collective-permute-start.16 = (bf16[16,2432]{1,0:T(8,128)(2,1)S(1)}, bf16[16,2432]{1,0:T(8,128)(2,1)S(1)}, u32[]{:S(2)}, u32[]{:S(2)}) collective-permute-start(bf16[16,2432]{1,0:T(8,128)(2,1)S(1)} %get-tuple-element.37), channel_id=1, source_target_pairs={{0,2},{2,4},{4,6},{6,8},{8,10},{10,12},{12,14},{14,0},{1,3},{3,5},... | collective-permute-start | bytes 233480 | tf_op jit(solution)/shard_map/ppermute | solution.py:124
  47.5 7.6 %collective-permute-done.13 = bf16[16,2432]{1,0:T(8,128)(2,1)S(1)} collective-permute-done((bf16[16,2432]{1,0:T(8,128)(2,1)S(1)}, bf16[16,2432]{1,0:T(8,128)(2,1)S(1)}, u32[]{:S(2)}, u32[]{:S(2)}) %collective-permute-start.13) | collective-permute-done | bytes 77856 | tf_op jit(solution)/shard_map/ppermute | solution.py:124
  56.5 1.6 %collective-permute-start.18 = (bf16[16,2560]{1,0:T(8,128)(2,1)S(1)}, bf16[16,2560]{1,0:T(8,128)(2,1)S(1)}, u32[]{:S(2)}, u32[]{:S(2)}) collective-permute-start(bf16[16,2560]{1,0:T(8,128)(2,1)S(1)} %get-tuple-element.17), channel_id=1, source_target_pairs={{0,4},{2,6},{4,8},{6,10},{8,12},{10,14},{12,0},{14,2},{1,5},{3,7},... | collective-permute-start | bytes 245768 | tf_op jit(solution)/shard_map/ppermute | solution.py:124
  58.2 2.8 %collective-permute-start.19 = (bf16[16,2560]{1,0:T(8,128)(2,1)S(1)}, bf16[16,2560]{1,0:T(8,128)(2,1)S(1)}, u32[]{:S(2)}, u32[]{:S(2)}) collective-permute-start(bf16[16,2560]{1,0:T(8,128)(2,1)S(1)} %get-tuple-element.18), channel_id=1, source_target_pairs={{0,6},{2,8},{4,10},{6,12},{8,14},{10,0},{12,2},{14,4},{1,7},{3,9},... | collective-permute-start | bytes 245768 | tf_op jit(solution)/shard_map/ppermute | solution.py:124
  61.8 2.1 %collective-permute-start.21 = (bf16[16,2560]{1,0:T(8,128)(2,1)S(1)}, bf16[16,2560]{1,0:T(8,128)(2,1)S(1)}, u32[]{:S(2)}, u32[]{:S(2)}) collective-permute-start(bf16[16,2560]{1,0:T(8,128)(2,1)S(1)} %get-tuple-element.20), channel_id=1, source_target_pairs={{0,10},{2,12},{4,14},{6,0},{8,2},{10,4},{12,6},{14,8},{1,11},{3,13... | collective-permute-start | bytes 245768 | tf_op jit(solution)/shard_map/ppermute | solution.py:124
  64.3 2.0 %collective-permute-start.22 = (bf16[16,2560]{1,0:T(8,128)(2,1)S(1)}, bf16[16,2560]{1,0:T(8,128)(2,1)S(1)}, u32[]{:S(2)}, u32[]{:S(2)}) collective-permute-start(bf16[16,2560]{1,0:T(8,128)(2,1)S(1)} %get-tuple-element.21), channel_id=1, source_target_pairs={{0,12},{2,14},{4,0},{6,2},{8,4},{10,6},{12,8},{14,10},{1,13},{3,15... | collective-permute-start | bytes 245768 | tf_op jit(solution)/shard_map/ppermute | solution.py:124
  66.4 2.9 %collective-permute-start.23 = (bf16[16,2560]{1,0:T(8,128)(2,1)S(1)}, bf16[16,2560]{1,0:T(8,128)(2,1)S(1)}, u32[]{:S(2)}, u32[]{:S(2)}) collective-permute-start(bf16[16,2560]{1,0:T(8,128)(2,1)S(1)} %get-tuple-element.14), channel_id=1, source_target_pairs={{0,14},{2,0},{4,2},{6,4},{8,6},{10,8},{12,10},{14,12},{1,15},{3,1}... | collective-permute-start | bytes 245768 | tf_op jit(solution)/shard_map/ppermute | solution.py:124
  69.3 1.0 collective-permute-done.19
  70.3 1.7 %collective-permute-done.20 = bf16[16,2560]{1,0:T(8,128)(2,1)S(1)} collective-permute-done((bf16[16,2560]{1,0:T(8,128)(2,1)S(1)}, bf16[16,2560]{1,0:T(8,128)(2,1)S(1)}, u32[]{:S(2)}, u32[]{:S(2)}) %collective-permute-start.20) | collective-permute-done | bytes 81952 | tf_op jit(solution)/shard_map/ppermute | solution.py:124
  75.6 6.3 %collective-permute-start.25 = (bf16[16,2432]{1,0:T(8,128)(2,1)S(1)}, bf16[16,2432]{1,0:T(8,128)(2,1)S(1)}, u32[]{:S(2)}, u32[]{:S(2)}) collective-permute-start(bf16[16,2432]{1,0:T(8,128)(2,1)S(1)} %get-tuple-element.31), channel_id=1, source_target_pairs={{0,14},{2,0},{4,2},{6,4},{8,6},{10,8},{12,10},{14,12},{1,15},{3,1}... | collective-permute-start | bytes 233480 | tf_op jit(solution)/shard_map/ppermute | solution.py:124
  81.9 2.9 %collective-permute-start.26 = (bf16[16,2432]{1,0:T(8,128)(2,1)S(1)}, bf16[16,2432]{1,0:T(8,128)(2,1)S(1)}, u32[]{:S(2)}, u32[]{:S(2)}) collective-permute-start(bf16[16,2432]{1,0:T(8,128)(2,1)S(1)} %get-tuple-element.32), channel_id=1, source_target_pairs={{0,12},{2,14},{4,0},{6,2},{8,4},{10,6},{12,8},{14,10},{1,13},{3,15... | collective-permute-start | bytes 233480 | tf_op jit(solution)/shard_map/ppermute | solution.py:124
  84.9 1.1 %collective-permute-start.28 = (bf16[16,2432]{1,0:T(8,128)(2,1)S(1)}, bf16[16,2432]{1,0:T(8,128)(2,1)S(1)}, u32[]{:S(2)}, u32[]{:S(2)}) collective-permute-start(bf16[16,2432]{1,0:T(8,128)(2,1)S(1)} %get-tuple-element.34), channel_id=1, source_target_pairs={{0,8},{2,10},{4,12},{6,14},{8,0},{10,2},{12,4},{14,6},{1,9},{3,11}... | collective-permute-start | bytes 233480 | tf_op jit(solution)/shard_map/ppermute | solution.py:124
  86.0 1.8 %collective-permute-start.29 = (bf16[16,2432]{1,0:T(8,128)(2,1)S(1)}, bf16[16,2432]{1,0:T(8,128)(2,1)S(1)}, u32[]{:S(2)}, u32[]{:S(2)}) collective-permute-start(bf16[16,2432]{1,0:T(8,128)(2,1)S(1)} %get-tuple-element.35), channel_id=1, source_target_pairs={{0,6},{2,8},{4,10},{6,12},{8,14},{10,0},{12,2},{14,4},{1,7},{3,9},... | collective-permute-start | bytes 233480 | tf_op jit(solution)/shard_map/ppermute | solution.py:124
  87.8 2.3 %collective-permute-start.30 = (bf16[16,2432]{1,0:T(8,128)(2,1)S(1)}, bf16[16,2432]{1,0:T(8,128)(2,1)S(1)}, u32[]{:S(2)}, u32[]{:S(2)}) collective-permute-start(bf16[16,2432]{1,0:T(8,128)(2,1)S(1)} %get-tuple-element.36), channel_id=1, source_target_pairs={{0,4},{2,6},{4,8},{6,10},{8,12},{10,14},{12,0},{14,2},{1,5},{3,7},... | collective-permute-start | bytes 233480 | tf_op jit(solution)/shard_map/ppermute | solution.py:124
  91.0 6.5 %collective-permute-start.31 = (bf16[16,2432]{1,0:T(8,128)(2,1)S(1)}, bf16[16,2432]{1,0:T(8,128)(2,1)S(1)}, u32[]{:S(2)}, u32[]{:S(2)}) collective-permute-start(bf16[16,2432]{1,0:T(8,128)(2,1)S(1)} %get-tuple-element.30), channel_id=1, source_target_pairs={{0,2},{2,4},{4,6},{6,8},{8,10},{10,12},{12,14},{14,0},{1,3},{3,5},... | collective-permute-start | bytes 233480 | tf_op jit(solution)/shard_map/ppermute | solution.py:124
  98.1 1.4 %collective-permute-done.31 = bf16[16,2432]{1,0:T(8,128)(2,1)S(1)} collective-permute-done((bf16[16,2432]{1,0:T(8,128)(2,1)S(1)}, bf16[16,2432]{1,0:T(8,128)(2,1)S(1)}, u32[]{:S(2)}, u32[]{:S(2)}) %collective-permute-start.31) | collective-permute-done | bytes 77856 | tf_op jit(solution)/shard_map/ppermute | solution.py:124
  101.0 1.7 %fusion.17 = bf16[1,16,4608]{2,1,0:T(8,128)(2,1)} fusion(bf16[1,16,2304]{2,1,0:T(8,128)(2,1)S(1)} %bitcast.160, bf16[1,16,2304]{2,1,0:T(8,128)(2,1)S(1)} %bitcast.159, bf16[1,16,2304]{2,1,0:T(8,128)(2,1)} %bitcast.57, bf16[1,16,2304]{2,1,0:T(8,128)(2,1)S(1)} %bitcast.147, pred[]{:T(512)S(6)} %eq.23, pred[]{:T(512)S(6)} %eq.19), kind=kLoop, calls=%fused_computation.83 | loop fusion | flops 1474560 | bytes 442370 | tf_op jit(solution)/shard_map/jit(_where)/select_n | solution.py:223
  (132 shorter events, 21.6 us)
Async XLA Ops:
  7.3 11.0 %collective-permute-start.1 = (bf16[16,2560]{1,0:T(8,128)(2,1)}, bf16[16,2560]{1,0:T(8,128)(2,1)}, u32[]{:S(2)}, u32[]{:S(2)}) collective-permute-start(bf16[16,2560]{1,0:T(8,128)(2,1)} %get-tuple-element.24), channel_id=1, source_target_pairs={{0,2},{2,4},{4,6},{6,8},{8,10},{10,12},{12,14},{14,0},{1,3},{3,5},... | collective-permute-start | bytes 245768 | tf_op jit(solution)/shard_map/ppermute | solution.py:124
  10.2 10.4 %collective-permute-start.2 = (bf16[16,2560]{1,0:T(8,128)(2,1)}, bf16[16,2560]{1,0:T(8,128)(2,1)}, u32[]{:S(2)}, u32[]{:S(2)}) collective-permute-start(bf16[16,2560]{1,0:T(8,128)(2,1)} %get-tuple-element.25), channel_id=1, source_target_pairs={{0,4},{2,6},{4,8},{6,10},{8,12},{10,14},{12,0},{14,2},{1,5},{3,7},... | collective-permute-start | bytes 245768 | tf_op jit(solution)/shard_map/ppermute | solution.py:124
  11.8 11.4 %collective-permute-start.3 = (bf16[16,2560]{1,0:T(8,128)(2,1)}, bf16[16,2560]{1,0:T(8,128)(2,1)}, u32[]{:S(2)}, u32[]{:S(2)}) collective-permute-start(bf16[16,2560]{1,0:T(8,128)(2,1)} %get-tuple-element.26), channel_id=1, source_target_pairs={{0,6},{2,8},{4,10},{6,12},{8,14},{10,0},{12,2},{14,4},{1,7},{3,9},... | collective-permute-start | bytes 245768 | tf_op jit(solution)/shard_map/ppermute | solution.py:124
  14.3 9.8 %collective-permute-start.4 = (bf16[16,2560]{1,0:T(8,128)(2,1)}, bf16[16,2560]{1,0:T(8,128)(2,1)}, u32[]{:S(2)}, u32[]{:S(2)}) collective-permute-start(bf16[16,2560]{1,0:T(8,128)(2,1)} %get-tuple-element.27), channel_id=1, source_target_pairs={{0,8},{2,10},{4,12},{6,14},{8,0},{10,2},{12,4},{14,6},{1,9},{3,11}... | collective-permute-start | bytes 245768 | tf_op jit(solution)/shard_map/ppermute | solution.py:124
  15.6 9.4 %collective-permute-start.5 = (bf16[16,2560]{1,0:T(8,128)(2,1)}, bf16[16,2560]{1,0:T(8,128)(2,1)}, u32[]{:S(2)}, u32[]{:S(2)}) collective-permute-start(bf16[16,2560]{1,0:T(8,128)(2,1)} %get-tuple-element.28), channel_id=1, source_target_pairs={{0,10},{2,12},{4,14},{6,0},{8,2},{10,4},{12,6},{14,8},{1,11},{3,13... | collective-permute-start | bytes 245768 | tf_op jit(solution)/shard_map/ppermute | solution.py:124
  18.3 8.1 %collective-permute-start.6 = (bf16[16,2560]{1,0:T(8,128)(2,1)}, bf16[16,2560]{1,0:T(8,128)(2,1)S(1)}, u32[]{:S(2)}, u32[]{:S(2)}) collective-permute-start(bf16[16,2560]{1,0:T(8,128)(2,1)} %get-tuple-element.29), channel_id=1, source_target_pairs={{0,12},{2,14},{4,0},{6,2},{8,4},{10,6},{12,8},{14,10},{1,13},{3,15... | collective-permute-start | bytes 245768 | tf_op jit(solution)/shard_map/ppermute | solution.py:124
  20.6 5.8 %collective-permute-start.7 = (bf16[16,2560]{1,0:T(8,128)(2,1)S(1)}, bf16[16,2560]{1,0:T(8,128)(2,1)S(1)}, u32[]{:S(2)}, u32[]{:S(2)}) collective-permute-start(bf16[16,2560]{1,0:T(8,128)(2,1)S(1)} %get-tuple-element.22), channel_id=1, source_target_pairs={{0,14},{2,0},{4,2},{6,4},{8,6},{10,8},{12,10},{14,12},{1,15},{3,1}... | collective-permute-start | bytes 245768 | tf_op jit(solution)/shard_map/ppermute | solution.py:124
  23.2 4.7 %collective-permute-start.8 = (bf16[512,2304]{1,0:T(8,128)(2,1)}, bf16[512,2304]{1,0:T(8,128)(2,1)S(1)}, u32[]{:S(2)}, u32[]{:S(2)}) collective-permute-start(bf16[512,2304]{1,0:T(8,128)(2,1)} %pad_maximum_fusion), channel_id=1, source_target_pairs={{0,1},{1,0},{2,3},{3,2},{4,5},{5,4},{6,7},{7,6},{8,9},{9,8},{10,11... | collective-permute-start | bytes 7077896 | tf_op jit(solution)/shard_map/ppermute | solution.py:116
  30.1 1.9 %collective-permute-start.9 = (f32[128,512]{1,0:T(8,128)}, f32[128,512]{1,0:T(8,128)}, u32[]{:S(2)}, u32[]{:S(2)}) collective-permute-start(f32[128,512]{1,0:T(8,128)} %pad_maximum_fusion.1), channel_id=1, source_target_pairs={{0,1},{1,0},{2,3},{3,2},{4,5},{5,4},{6,7},{7,6},{8,9},{9,8},{10,11... | collective-permute-start | bytes 786440 | tf_op jit(solution)/shard_map/ppermute | solution.py:116
  35.0 10.3 %collective-permute-start.10 = (bf16[16,2432]{1,0:T(8,128)(2,1)S(1)}, bf16[16,2432]{1,0:T(8,128)(2,1)S(1)}, u32[]{:S(2)}, u32[]{:S(2)}) collective-permute-start(bf16[16,2432]{1,0:T(8,128)(2,1)S(1)} %get-tuple-element.38), channel_id=1, source_target_pairs={{0,14},{2,0},{4,2},{6,4},{8,6},{10,8},{12,10},{14,12},{1,15},{3,1}... | collective-permute-start | bytes 233480 | tf_op jit(solution)/shard_map/ppermute | solution.py:124
  39.3 6.6 %collective-permute-start.11 = (bf16[16,2432]{1,0:T(8,128)(2,1)S(1)}, bf16[16,2432]{1,0:T(8,128)(2,1)S(1)}, u32[]{:S(2)}, u32[]{:S(2)}) collective-permute-start(bf16[16,2432]{1,0:T(8,128)(2,1)S(1)} %get-tuple-element.39), channel_id=1, source_target_pairs={{0,12},{2,14},{4,0},{6,2},{8,4},{10,6},{12,8},{14,10},{1,13},{3,15... | collective-permute-start | bytes 233480 | tf_op jit(solution)/shard_map/ppermute | solution.py:124
  41.0 6.5 %collective-permute-start.12 = (bf16[16,2432]{1,0:T(8,128)(2,1)S(1)}, bf16[16,2432]{1,0:T(8,128)(2,1)S(1)}, u32[]{:S(2)}, u32[]{:S(2)}) collective-permute-start(bf16[16,2432]{1,0:T(8,128)(2,1)S(1)} %get-tuple-element.40), channel_id=1, source_target_pairs={{0,10},{2,12},{4,14},{6,0},{8,2},{10,4},{12,6},{14,8},{1,11},{3,13... | collective-permute-start | bytes 233480 | tf_op jit(solution)/shard_map/ppermute | solution.py:124
  41.0 14.1 %collective-permute-start.13 = (bf16[16,2432]{1,0:T(8,128)(2,1)S(1)}, bf16[16,2432]{1,0:T(8,128)(2,1)S(1)}, u32[]{:S(2)}, u32[]{:S(2)}) collective-permute-start(bf16[16,2432]{1,0:T(8,128)(2,1)S(1)} %get-tuple-element.41), channel_id=1, source_target_pairs={{0,8},{2,10},{4,12},{6,14},{8,0},{10,2},{12,4},{14,6},{1,9},{3,11}... | collective-permute-start | bytes 233480 | tf_op jit(solution)/shard_map/ppermute | solution.py:124
  45.4 10.7 %collective-permute-start.14 = (bf16[16,2432]{1,0:T(8,128)(2,1)S(1)}, bf16[16,2432]{1,0:T(8,128)(2,1)S(1)}, u32[]{:S(2)}, u32[]{:S(2)}) collective-permute-start(bf16[16,2432]{1,0:T(8,128)(2,1)S(1)} %get-tuple-element.42), channel_id=1, source_target_pairs={{0,6},{2,8},{4,10},{6,12},{8,14},{10,0},{12,2},{14,4},{1,7},{3,9},... | collective-permute-start | bytes 233480 | tf_op jit(solution)/shard_map/ppermute | solution.py:124
  45.4 10.7 %collective-permute-start.15 = (bf16[16,2432]{1,0:T(8,128)(2,1)S(1)}, bf16[16,2432]{1,0:T(8,128)(2,1)S(1)}, u32[]{:S(2)}, u32[]{:S(2)}) collective-permute-start(bf16[16,2432]{1,0:T(8,128)(2,1)S(1)} %get-tuple-element.43), channel_id=1, source_target_pairs={{0,4},{2,6},{4,8},{6,10},{8,12},{10,14},{12,0},{14,2},{1,5},{3,7},... | collective-permute-start | bytes 233480 | tf_op jit(solution)/shard_map/ppermute | solution.py:124
  45.9 10.2 %collective-permute-start.16 = (bf16[16,2432]{1,0:T(8,128)(2,1)S(1)}, bf16[16,2432]{1,0:T(8,128)(2,1)S(1)}, u32[]{:S(2)}, u32[]{:S(2)}) collective-permute-start(bf16[16,2432]{1,0:T(8,128)(2,1)S(1)} %get-tuple-element.37), channel_id=1, source_target_pairs={{0,2},{2,4},{4,6},{6,8},{8,10},{10,12},{12,14},{14,0},{1,3},{3,5},... | collective-permute-start | bytes 233480 | tf_op jit(solution)/shard_map/ppermute | solution.py:124
  56.4 7.9 %collective-permute-start.17 = (bf16[16,2560]{1,0:T(8,128)(2,1)S(1)}, bf16[16,2560]{1,0:T(8,128)(2,1)S(1)}, u32[]{:S(2)}, u32[]{:S(2)}) collective-permute-start(bf16[16,2560]{1,0:T(8,128)(2,1)S(1)} %get-tuple-element.16), channel_id=1, source_target_pairs={{0,2},{2,4},{4,6},{6,8},{8,10},{10,12},{12,14},{14,0},{1,3},{3,5},... | collective-permute-start | bytes 245768 | tf_op jit(solution)/shard_map/ppermute | solution.py:124
  56.5 9.8 %collective-permute-start.18 = (bf16[16,2560]{1,0:T(8,128)(2,1)S(1)}, bf16[16,2560]{1,0:T(8,128)(2,1)S(1)}, u32[]{:S(2)}, u32[]{:S(2)}) collective-permute-start(bf16[16,2560]{1,0:T(8,128)(2,1)S(1)} %get-tuple-element.17), channel_id=1, source_target_pairs={{0,4},{2,6},{4,8},{6,10},{8,12},{10,14},{12,0},{14,2},{1,5},{3,7},... | collective-permute-start | bytes 245768 | tf_op jit(solution)/shard_map/ppermute | solution.py:124
  58.2 12.1 %collective-permute-start.19 = (bf16[16,2560]{1,0:T(8,128)(2,1)S(1)}, bf16[16,2560]{1,0:T(8,128)(2,1)S(1)}, u32[]{:S(2)}, u32[]{:S(2)}) collective-permute-start(bf16[16,2560]{1,0:T(8,128)(2,1)S(1)} %get-tuple-element.18), channel_id=1, source_target_pairs={{0,6},{2,8},{4,10},{6,12},{8,14},{10,0},{12,2},{14,4},{1,7},{3,9},... | collective-permute-start | bytes 245768 | tf_op jit(solution)/shard_map/ppermute | solution.py:124
  61.0 11.0 %collective-permute-start.20 = (bf16[16,2560]{1,0:T(8,128)(2,1)S(1)}, bf16[16,2560]{1,0:T(8,128)(2,1)S(1)}, u32[]{:S(2)}, u32[]{:S(2)}) collective-permute-start(bf16[16,2560]{1,0:T(8,128)(2,1)S(1)} %get-tuple-element.19), channel_id=1, source_target_pairs={{0,8},{2,10},{4,12},{6,14},{8,0},{10,2},{12,4},{14,6},{1,9},{3,11}... | collective-permute-start | bytes 245768 | tf_op jit(solution)/shard_map/ppermute | solution.py:124
  61.8 10.2 %collective-permute-start.21 = (bf16[16,2560]{1,0:T(8,128)(2,1)S(1)}, bf16[16,2560]{1,0:T(8,128)(2,1)S(1)}, u32[]{:S(2)}, u32[]{:S(2)}) collective-permute-start(bf16[16,2560]{1,0:T(8,128)(2,1)S(1)} %get-tuple-element.20), channel_id=1, source_target_pairs={{0,10},{2,12},{4,14},{6,0},{8,2},{10,4},{12,6},{14,8},{1,11},{3,13... | collective-permute-start | bytes 245768 | tf_op jit(solution)/shard_map/ppermute | solution.py:124
  64.3 7.7 %collective-permute-start.22 = (bf16[16,2560]{1,0:T(8,128)(2,1)S(1)}, bf16[16,2560]{1,0:T(8,128)(2,1)S(1)}, u32[]{:S(2)}, u32[]{:S(2)}) collective-permute-start(bf16[16,2560]{1,0:T(8,128)(2,1)S(1)} %get-tuple-element.21), channel_id=1, source_target_pairs={{0,12},{2,14},{4,0},{6,2},{8,4},{10,6},{12,8},{14,10},{1,13},{3,15... | collective-permute-start | bytes 245768 | tf_op jit(solution)/shard_map/ppermute | solution.py:124
  66.4 5.7 %collective-permute-start.23 = (bf16[16,2560]{1,0:T(8,128)(2,1)S(1)}, bf16[16,2560]{1,0:T(8,128)(2,1)S(1)}, u32[]{:S(2)}, u32[]{:S(2)}) collective-permute-start(bf16[16,2560]{1,0:T(8,128)(2,1)S(1)} %get-tuple-element.14), channel_id=1, source_target_pairs={{0,14},{2,0},{4,2},{6,4},{8,6},{10,8},{12,10},{14,12},{1,15},{3,1}... | collective-permute-start | bytes 245768 | tf_op jit(solution)/shard_map/ppermute | solution.py:124
  73.2 1.6 %collective-permute-start.24 = (f32[128,512]{1,0:T(8,128)S(1)}, f32[128,512]{1,0:T(8,128)S(1)}, u32[]{:S(2)}, u32[]{:S(2)}) collective-permute-start(f32[128,512]{1,0:T(8,128)S(1)} %pad_maximum_fusion.2), channel_id=1, source_target_pairs={{0,1},{1,0},{2,3},{3,2},{4,5},{5,4},{6,7},{7,6},{8,9},{9,8},{10,11... | collective-permute-start | bytes 786440 | tf_op jit(solution)/shard_map/ppermute | solution.py:116
  73.4 27.4 %collective-permute-start.33 = (bf16[16,2304]{1,0:T(8,128)(2,1)S(1)}, bf16[16,2304]{1,0:T(8,128)(2,1)}, u32[]{:S(2)}, u32[]{:S(2)}) collective-permute-start(bf16[16,2304]{1,0:T(8,128)(2,1)S(1)} %add_convert_fusion.1), channel_id=1, source_target_pairs={{0,1},{1,0},{2,3},{3,2},{4,5},{5,4},{6,7},{7,6},{8,9},{9,8},{10,11... | collective-permute-start | bytes 221192 | tf_op jit(solution)/shard_map/ppermute | solution.py:116
  75.6 10.4 %collective-permute-start.25 = (bf16[16,2432]{1,0:T(8,128)(2,1)S(1)}, bf16[16,2432]{1,0:T(8,128)(2,1)S(1)}, u32[]{:S(2)}, u32[]{:S(2)}) collective-permute-start(bf16[16,2432]{1,0:T(8,128)(2,1)S(1)} %get-tuple-element.31), channel_id=1, source_target_pairs={{0,14},{2,0},{4,2},{6,4},{8,6},{10,8},{12,10},{14,12},{1,15},{3,1}... | collective-permute-start | bytes 233480 | tf_op jit(solution)/shard_map/ppermute | solution.py:124
  81.9 5.9 %collective-permute-start.26 = (bf16[16,2432]{1,0:T(8,128)(2,1)S(1)}, bf16[16,2432]{1,0:T(8,128)(2,1)S(1)}, u32[]{:S(2)}, u32[]{:S(2)}) collective-permute-start(bf16[16,2432]{1,0:T(8,128)(2,1)S(1)} %get-tuple-element.32), channel_id=1, source_target_pairs={{0,12},{2,14},{4,0},{6,2},{8,4},{10,6},{12,8},{14,10},{1,13},{3,15... | collective-permute-start | bytes 233480 | tf_op jit(solution)/shard_map/ppermute | solution.py:124
  84.9 6.1 %collective-permute-start.27 = (bf16[16,2432]{1,0:T(8,128)(2,1)S(1)}, bf16[16,2432]{1,0:T(8,128)(2,1)S(1)}, u32[]{:S(2)}, u32[]{:S(2)}) collective-permute-start(bf16[16,2432]{1,0:T(8,128)(2,1)S(1)} %get-tuple-element.33), channel_id=1, source_target_pairs={{0,10},{2,12},{4,14},{6,0},{8,2},{10,4},{12,6},{14,8},{1,11},{3,13... | collective-permute-start | bytes 233480 | tf_op jit(solution)/shard_map/ppermute | solution.py:124
  84.9 12.6 %collective-permute-start.28 = (bf16[16,2432]{1,0:T(8,128)(2,1)S(1)}, bf16[16,2432]{1,0:T(8,128)(2,1)S(1)}, u32[]{:S(2)}, u32[]{:S(2)}) collective-permute-start(bf16[16,2432]{1,0:T(8,128)(2,1)S(1)} %get-tuple-element.34), channel_id=1, source_target_pairs={{0,8},{2,10},{4,12},{6,14},{8,0},{10,2},{12,4},{14,6},{1,9},{3,11}... | collective-permute-start | bytes 233480 | tf_op jit(solution)/shard_map/ppermute | solution.py:124
  86.0 12.1 %collective-permute-start.29 = (bf16[16,2432]{1,0:T(8,128)(2,1)S(1)}, bf16[16,2432]{1,0:T(8,128)(2,1)S(1)}, u32[]{:S(2)}, u32[]{:S(2)}) collective-permute-start(bf16[16,2432]{1,0:T(8,128)(2,1)S(1)} %get-tuple-element.35), channel_id=1, source_target_pairs={{0,6},{2,8},{4,10},{6,12},{8,14},{10,0},{12,2},{14,4},{1,7},{3,9},... | collective-permute-start | bytes 233480 | tf_op jit(solution)/shard_map/ppermute | solution.py:124
  87.8 10.3 %collective-permute-start.30 = (bf16[16,2432]{1,0:T(8,128)(2,1)S(1)}, bf16[16,2432]{1,0:T(8,128)(2,1)S(1)}, u32[]{:S(2)}, u32[]{:S(2)}) collective-permute-start(bf16[16,2432]{1,0:T(8,128)(2,1)S(1)} %get-tuple-element.36), channel_id=1, source_target_pairs={{0,4},{2,6},{4,8},{6,10},{8,12},{10,14},{12,0},{14,2},{1,5},{3,7},... | collective-permute-start | bytes 233480 | tf_op jit(solution)/shard_map/ppermute | solution.py:124
  91.0 8.5 %collective-permute-start.31 = (bf16[16,2432]{1,0:T(8,128)(2,1)S(1)}, bf16[16,2432]{1,0:T(8,128)(2,1)S(1)}, u32[]{:S(2)}, u32[]{:S(2)}) collective-permute-start(bf16[16,2432]{1,0:T(8,128)(2,1)S(1)} %get-tuple-element.30), channel_id=1, source_target_pairs={{0,2},{2,4},{4,6},{6,8},{8,10},{10,12},{12,14},{14,0},{1,3},{3,5},... | collective-permute-start | bytes 233480 | tf_op jit(solution)/shard_map/ppermute | solution.py:124
  (9 other events, 38.1 us)

commit v5 on v2

--- a/solution.py
+++ b/solution.py
@@ -136,19 +136,18 @@
     within = routes_l - owner * held
     rel = (owner - me) % peers
     shifts = jnp.arange(peers, dtype=jnp.int32)
-    spots = jnp.arange(held, dtype=jnp.int32)
     at_rel = (rel[:, :, None] == shifts[None, None, :]).astype(jnp.bfloat16)
-    at_spot = (within[:, :, None] == spots[None, None, :]).astype(jnp.bfloat16)
     act_grid = acts_l.reshape(rows, listed, block)
+    live = (act_grid > 0).astype(jnp.bfloat16) * (1 + within).astype(jnp.bfloat16)[:, :, None]
     placed = jnp.einsum(
-        "rks,rkw,rkj->srwj", at_rel, at_spot, act_grid, preferred_element_type=jnp.float32
-    ).astype(jnp.bfloat16).reshape(peers, rows, held * block)
+        "rks,rkj->srj", at_rel, live, preferred_element_type=jnp.float32
+    ).astype(jnp.bfloat16)
     sent = jnp.concatenate(
         [jnp.broadcast_to(g_half[None], (peers, rows, half)), placed], axis=-1
     )
-    got = exchange(sent, 1).reshape(peers * rows, half + held * block)
+    got = exchange(sent, 1).reshape(peers * rows, half + block)
     g_all = got[:, :half]
-    act_all = got[:, half:]
+    code_all = got[:, half:]
 
     def with_dec(dec):
         return lax.dot_general(
@@ -156,10 +155,11 @@
         )
 
     part = jnp.where(is_own, with_dec(own[0]), with_dec(other[0]))
-    paired = swap_cores(jnp.concatenate([part, act_all.astype(jnp.float32)], axis=1))
+    paired = swap_cores(jnp.concatenate([part, code_all.astype(jnp.float32)], axis=1))
     coef = (part + paired[:, :held * block]).astype(jnp.bfloat16)
-    act_used = jnp.where(is_own, act_all.astype(jnp.float32), paired[:, held * block:])
-    dz = jnp.where(act_used > 0, coef, jnp.zeros_like(coef))
+    code = jnp.where(is_own, code_all.astype(jnp.float32), paired[:, held * block:])
+    marks = jnp.concatenate([code == spot + 1 for spot in range(held)], axis=1)
+    dz = jnp.where(marks, coef, jnp.zeros_like(coef))
 
     def with_enc(enc):
         return jnp.dot(dz, enc, preferred_element_type=jnp.float32)

time: 98.1 us -> 94.1 us (0.959)
  matrix products: 5.34 us -> 4.18 us
    dot_general x4, matrix products: 2.6 us -> 1.33 us  [with_enc(): return jnp.dot(dz, enc, preferred_element_type=jnp.float32)]
    unnamed x39 -> x38, local copies, waits for them, and re-layouts: 5.47 us -> 4.79 us
  transfers between devices with their start and end apart: 34 -> 34, of which waited for: 12 -> 12; matrix products, arithmetic and copies ran while one was open for 11% -> 12% of each run, Pallas kernels for 0% -> 0%
where the time goes in v5:
time: 94.1 us; the launch traced here: 93.6 us
  starting transfers between devices  54.6 us (58%)
  waiting for transfers between devices  20 us (21%)
  local copies, waits for them, and re-layouts  8.28 us (9%)
  other arithmetic  5.44 us (6%)
  matrix products  4.18 us (4%)
  between operations  1.12 us (1%)
    ppermute x28, starting transfers between devices, exchange(): moved.append(lax.ppermute(parts[shift], 'dict', route))  53.2 us
    ppermute x28, waiting for transfers between devices, exchange(): moved.append(lax.ppermute(parts[shift], 'dict', route))  16.4 us
    unnamed x38, local copies, waits for them, and re-layouts  4.79 us
    ppermute x6, waiting for transfers between devices, swap_cores(): return lax.ppermute(block, 'section', [(0, 1), (1, 0)])  3.57 us
    dot_general x4, matrix products, with_dec(): lax.dot_general(g_all, dec, (((1,), (1,)), ((), ())), preferred_element_t...  2.16 us
  transfers between devices with their start and end apart: 34, of which 12 were waited for; matrix products, arithmetic and copies ran while one was open for 12% of the time, Pallas kernels for 0%

profile of v5, /device:TPU:0, one launch (start us, length us, event | category | flops | bytes accessed | tf_op | source)
XLA Modules:
  0.0 93.6 jit_solution(9020368106931536137)
XLA Ops:
  4.5 2.9 %collective-permute-start.1 = (bf16[16,2432]{1,0:T(8,128)(2,1)}, bf16[16,2432]{1,0:T(8,128)(2,1)}, u32[]{:S(2)}, u32[]{:S(2)}) collective-permute-start(bf16[16,2432]{1,0:T(8,128)(2,1)} %get-tuple-element.31), channel_id=1, source_target_pairs={{0,2},{2,4},{4,6},{6,8},{8,10},{10,12},{12,14},{14,0},{1,3},{3,5},... | collective-permute-start | bytes 233480 | tf_op jit(solution)/shard_map/ppermute | solution.py:124
  7.4 1.6 %collective-permute-start.2 = (bf16[16,2432]{1,0:T(8,128)(2,1)S(1)}, bf16[16,2432]{1,0:T(8,128)(2,1)}, u32[]{:S(2)}, u32[]{:S(2)}) collective-permute-start(bf16[16,2432]{1,0:T(8,128)(2,1)S(1)} %get-tuple-element.32), channel_id=1, source_target_pairs={{0,4},{2,6},{4,8},{6,10},{8,12},{10,14},{12,0},{14,2},{1,5},{3,7},... | collective-permute-start | bytes 233480 | tf_op jit(solution)/shard_map/ppermute | solution.py:124
  9.0 2.6 %collective-permute-start.3 = (bf16[16,2432]{1,0:T(8,128)(2,1)S(1)}, bf16[16,2432]{1,0:T(8,128)(2,1)}, u32[]{:S(2)}, u32[]{:S(2)}) collective-permute-start(bf16[16,2432]{1,0:T(8,128)(2,1)S(1)} %get-tuple-element.33), channel_id=1, source_target_pairs={{0,6},{2,8},{4,10},{6,12},{8,14},{10,0},{12,2},{14,4},{1,7},{3,9},... | collective-permute-start | bytes 233480 | tf_op jit(solution)/shard_map/ppermute | solution.py:124
  11.5 1.2 %collective-permute-start.4 = (bf16[16,2432]{1,0:T(8,128)(2,1)S(1)}, bf16[16,2432]{1,0:T(8,128)(2,1)}, u32[]{:S(2)}, u32[]{:S(2)}) collective-permute-start(bf16[16,2432]{1,0:T(8,128)(2,1)S(1)} %get-tuple-element.34), channel_id=1, source_target_pairs={{0,8},{2,10},{4,12},{6,14},{8,0},{10,2},{12,4},{14,6},{1,9},{3,11}... | collective-permute-start | bytes 233480 | tf_op jit(solution)/shard_map/ppermute | solution.py:124
  12.8 2.6 %collective-permute-start.5 = (bf16[16,2432]{1,0:T(8,128)(2,1)S(1)}, bf16[16,2432]{1,0:T(8,128)(2,1)}, u32[]{:S(2)}, u32[]{:S(2)}) collective-permute-start(bf16[16,2432]{1,0:T(8,128)(2,1)S(1)} %get-tuple-element.29), channel_id=1, source_target_pairs={{0,10},{2,12},{4,14},{6,0},{8,2},{10,4},{12,6},{14,8},{1,11},{3,13... | collective-permute-start | bytes 233480 | tf_op jit(solution)/shard_map/ppermute | solution.py:124
  15.4 1.5 %dynamic-slice_bitcast_fusion = (bf16[256,2304]{1,0:T(8,128)(2,1)S(1)}, bf16[256,2304]{1,0:T(8,128)(2,1)S(1)}) fusion(bf16[1,256,4608]{2,1,0:T(8,128)(2,1)} %param.11, s32[]{:T(128)S(6)} %select_n.193, bf16[1,256,4608]{2,1,0:T(8,128)(2,1)S(1)} %copy-done), kind=kLoop, calls=%fused_computation.48 | loop fusion | bytes 4718596 | tf_op jit(solution)/shard_map/dynamic_slice | solution.py:196
  16.9 1.6 %pad_maximum_fusion = bf16[512,2304]{1,0:T(8,128)(2,1)} fusion(bf16[256,2304]{1,0:T(8,128)(2,1)S(1)} %get-tuple-element.40, bf16[256,2304]{1,0:T(8,128)(2,1)S(1)} %get-tuple-element.41), kind=kLoop, calls=%fused_computation.4 | loop fusion | flops 4718592 | bytes 4718592 | tf_op jit(solution)/shard_map/concatenate | solution.py:193
  18.5 1.4 %collective-permute-start.6 = (bf16[16,2432]{1,0:T(8,128)(2,1)S(1)}, bf16[16,2432]{1,0:T(8,128)(2,1)S(1)}, u32[]{:S(2)}, u32[]{:S(2)}) collective-permute-start(bf16[16,2432]{1,0:T(8,128)(2,1)S(1)} %get-tuple-element.35), channel_id=1, source_target_pairs={{0,12},{2,14},{4,0},{6,2},{8,4},{10,6},{12,8},{14,10},{1,13},{3,15... | collective-permute-start | bytes 233480 | tf_op jit(solution)/shard_map/ppermute | solution.py:124
  20.8 1.5 %collective-permute-start.7 = (bf16[16,2432]{1,0:T(8,128)(2,1)S(1)}, bf16[16,2432]{1,0:T(8,128)(2,1)S(1)}, u32[]{:S(2)}, u32[]{:S(2)}) collective-permute-start(bf16[16,2432]{1,0:T(8,128)(2,1)S(1)} %get-tuple-element.28), channel_id=1, source_target_pairs={{0,14},{2,0},{4,2},{6,4},{8,6},{10,8},{12,10},{14,12},{1,15},{3,1}... | collective-permute-start | bytes 233480 | tf_op jit(solution)/shard_map/ppermute | solution.py:124
  23.3 0.9 bitcast_dynamic-update-slice_fusion.27
  26.6 1.4 %collective-permute-done.8 = bf16[512,2304]{1,0:T(8,128)(2,1)S(1)} collective-permute-done((bf16[512,2304]{1,0:T(8,128)(2,1)}, bf16[512,2304]{1,0:T(8,128)(2,1)S(1)}, u32[]{:S(2)}, u32[]{:S(2)}) %collective-permute-start.8) | collective-permute-done | bytes 2359328 | tf_op jit(solution)/shard_map/ppermute | solution.py:116
  29.5 1.2 %collective-permute-done.9 = f32[128,384]{1,0:T(8,128)S(1)} collective-permute-done((f32[128,384]{1,0:T(8,128)S(1)}, f32[128,384]{1,0:T(8,128)S(1)}, u32[]{:S(2)}, u32[]{:S(2)}) %collective-permute-start.9) | collective-permute-done | bytes 196640 | tf_op jit(solution)/shard_map/ppermute | solution.py:116
  31.5 1.5 %collective-permute-start.10 = (bf16[16,2432]{1,0:T(8,128)(2,1)S(1)}, bf16[16,2432]{1,0:T(8,128)(2,1)S(1)}, u32[]{:S(2)}, u32[]{:S(2)}) collective-permute-start(bf16[16,2432]{1,0:T(8,128)(2,1)S(1)} %get-tuple-element.22), channel_id=1, source_target_pairs={{0,14},{2,0},{4,2},{6,4},{8,6},{10,8},{12,10},{14,12},{1,15},{3,1}... | collective-permute-start | bytes 233480 | tf_op jit(solution)/shard_map/ppermute | solution.py:124
  33.4 1.8 %collective-permute-start.12 = (bf16[16,2432]{1,0:T(8,128)(2,1)S(1)}, bf16[16,2432]{1,0:T(8,128)(2,1)S(1)}, u32[]{:S(2)}, u32[]{:S(2)}) collective-permute-start(bf16[16,2432]{1,0:T(8,128)(2,1)S(1)} %get-tuple-element.24), channel_id=1, source_target_pairs={{0,10},{2,12},{4,14},{6,0},{8,2},{10,4},{12,6},{14,8},{1,11},{3,13... | collective-permute-start | bytes 233480 | tf_op jit(solution)/shard_map/ppermute | solution.py:124
  35.1 2.4 %collective-permute-start.13 = (bf16[16,2432]{1,0:T(8,128)(2,1)S(1)}, bf16[16,2432]{1,0:T(8,128)(2,1)S(1)}, u32[]{:S(2)}, u32[]{:S(2)}) collective-permute-start(bf16[16,2432]{1,0:T(8,128)(2,1)S(1)} %get-tuple-element.25), channel_id=1, source_target_pairs={{0,8},{2,10},{4,12},{6,14},{8,0},{10,2},{12,4},{14,6},{1,9},{3,11}... | collective-permute-start | bytes 233480 | tf_op jit(solution)/shard_map/ppermute | solution.py:124
  38.0 1.6 %collective-permute-start.15 = (bf16[16,2432]{1,0:T(8,128)(2,1)S(1)}, bf16[16,2432]{1,0:T(8,128)(2,1)S(1)}, u32[]{:S(2)}, u32[]{:S(2)}) collective-permute-start(bf16[16,2432]{1,0:T(8,128)(2,1)S(1)} %get-tuple-element.27), channel_id=1, source_target_pairs={{0,4},{2,6},{4,8},{6,10},{8,12},{10,14},{12,0},{14,2},{1,5},{3,7},... | collective-permute-start | bytes 233480 | tf_op jit(solution)/shard_map/ppermute | solution.py:124
  39.8 8.0 %collective-permute-done.13 = bf16[16,2432]{1,0:T(8,128)(2,1)S(1)} collective-permute-done((bf16[16,2432]{1,0:T(8,128)(2,1)S(1)}, bf16[16,2432]{1,0:T(8,128)(2,1)S(1)}, u32[]{:S(2)}, u32[]{:S(2)}) %collective-permute-start.13) | collective-permute-done | bytes 77856 | tf_op jit(solution)/shard_map/ppermute | solution.py:124
  47.8 1.8 %collective-permute-done.14 = bf16[16,2432]{1,0:T(8,128)(2,1)S(1)} collective-permute-done((bf16[16,2432]{1,0:T(8,128)(2,1)S(1)}, bf16[16,2432]{1,0:T(8,128)(2,1)S(1)}, u32[]{:S(2)}, u32[]{:S(2)}) %collective-permute-start.14) | collective-permute-done | bytes 77856 | tf_op jit(solution)/shard_map/ppermute | solution.py:124
  50.8 2.7 %collective-permute-start.19 = (bf16[16,2432]{1,0:T(8,128)(2,1)S(1)}, bf16[16,2432]{1,0:T(8,128)(2,1)S(1)}, u32[]{:S(2)}, u32[]{:S(2)}) collective-permute-start(bf16[16,2432]{1,0:T(8,128)(2,1)S(1)} %get-tuple-element.15), channel_id=1, source_target_pairs={{0,6},{2,8},{4,10},{6,12},{8,14},{10,0},{12,2},{14,4},{1,7},{3,9},... | collective-permute-start | bytes 233480 | tf_op jit(solution)/shard_map/ppermute | solution.py:124
  53.5 2.5 %collective-permute-start.20 = (bf16[16,2432]{1,0:T(8,128)(2,1)S(1)}, bf16[16,2432]{1,0:T(8,128)(2,1)S(1)}, u32[]{:S(2)}, u32[]{:S(2)}) collective-permute-start(bf16[16,2432]{1,0:T(8,128)(2,1)S(1)} %get-tuple-element.14), channel_id=1, source_target_pairs={{0,8},{2,10},{4,12},{6,14},{8,0},{10,2},{12,4},{14,6},{1,9},{3,11}... | collective-permute-start | bytes 233480 | tf_op jit(solution)/shard_map/ppermute | solution.py:124
  56.4 1.5 %collective-permute-done.17 = bf16[16,2432]{1,0:T(8,128)(2,1)S(1)} collective-permute-done((bf16[16,2432]{1,0:T(8,128)(2,1)S(1)}, bf16[16,2432]{1,0:T(8,128)(2,1)S(1)}, u32[]{:S(2)}, u32[]{:S(2)}) %collective-permute-start.17) | collective-permute-done | bytes 77856 | tf_op jit(solution)/shard_map/ppermute | solution.py:124
  57.9 1.0 %collective-permute-start.22 = (bf16[16,2432]{1,0:T(8,128)(2,1)S(1)}, bf16[16,2432]{1,0:T(8,128)(2,1)S(1)}, u32[]{:S(2)}, u32[]{:S(2)}) collective-permute-start(bf16[16,2432]{1,0:T(8,128)(2,1)S(1)} %get-tuple-element.19), channel_id=1, source_target_pairs={{0,12},{2,14},{4,0},{6,2},{8,4},{10,6},{12,8},{14,10},{1,13},{3,15... | collective-permute-start | bytes 233480 | tf_op jit(solution)/shard_map/ppermute | solution.py:124
  58.9 2.9 %collective-permute-start.23 = (bf16[16,2432]{1,0:T(8,128)(2,1)S(1)}, bf16[16,2432]{1,0:T(8,128)(2,1)S(1)}, u32[]{:S(2)}, u32[]{:S(2)}) collective-permute-start(bf16[16,2432]{1,0:T(8,128)(2,1)S(1)} %get-tuple-element.13), channel_id=1, source_target_pairs={{0,14},{2,0},{4,2},{6,4},{8,6},{10,8},{12,10},{14,12},{1,15},{3,1}... | collective-permute-start | bytes 233480 | tf_op jit(solution)/shard_map/ppermute | solution.py:124
  61.8 1.1 %collective-permute-done.19 = bf16[16,2432]{1,0:T(8,128)(2,1)S(1)} collective-permute-done((bf16[16,2432]{1,0:T(8,128)(2,1)S(1)}, bf16[16,2432]{1,0:T(8,128)(2,1)S(1)}, u32[]{:S(2)}, u32[]{:S(2)}) %collective-permute-start.19) | collective-permute-done | bytes 77856 | tf_op jit(solution)/shard_map/ppermute | solution.py:124
  62.9 1.3 %collective-permute-done.20 = bf16[16,2432]{1,0:T(8,128)(2,1)S(1)} collective-permute-done((bf16[16,2432]{1,0:T(8,128)(2,1)S(1)}, bf16[16,2432]{1,0:T(8,128)(2,1)S(1)}, u32[]{:S(2)}, u32[]{:S(2)}) %collective-permute-start.20) | collective-permute-done | bytes 77856 | tf_op jit(solution)/shard_map/ppermute | solution.py:124
  67.7 6.5 %collective-permute-start.25 = (bf16[16,2432]{1,0:T(8,128)(2,1)S(1)}, bf16[16,2432]{1,0:T(8,128)(2,1)S(1)}, u32[]{:S(2)}, u32[]{:S(2)}) collective-permute-start(bf16[16,2432]{1,0:T(8,128)(2,1)S(1)} %get-tuple-element.7), channel_id=1, source_target_pairs={{0,14},{2,0},{4,2},{6,4},{8,6},{10,8},{12,10},{14,12},{1,15},{3,1}... | collective-permute-start | bytes 233480 | tf_op jit(solution)/shard_map/ppermute | solution.py:124
  74.2 2.6 %collective-permute-start.26 = (bf16[16,2432]{1,0:T(8,128)(2,1)S(1)}, bf16[16,2432]{1,0:T(8,128)(2,1)S(1)}, u32[]{:S(2)}, u32[]{:S(2)}) collective-permute-start(bf16[16,2432]{1,0:T(8,128)(2,1)S(1)} %get-tuple-element.8), channel_id=1, source_target_pairs={{0,12},{2,14},{4,0},{6,2},{8,4},{10,6},{12,8},{14,10},{1,13},{3,15... | collective-permute-start | bytes 233480 | tf_op jit(solution)/shard_map/ppermute | solution.py:124
  76.8 1.1 %collective-permute-start.28 = (bf16[16,2432]{1,0:T(8,128)(2,1)S(1)}, bf16[16,2432]{1,0:T(8,128)(2,1)S(1)}, u32[]{:S(2)}, u32[]{:S(2)}) collective-permute-start(bf16[16,2432]{1,0:T(8,128)(2,1)S(1)} %get-tuple-element.10), channel_id=1, source_target_pairs={{0,8},{2,10},{4,12},{6,14},{8,0},{10,2},{12,4},{14,6},{1,9},{3,11}... | collective-permute-start | bytes 233480 | tf_op jit(solution)/shard_map/ppermute | solution.py:124
  77.9 1.8 %collective-permute-start.29 = (bf16[16,2432]{1,0:T(8,128)(2,1)S(1)}, bf16[16,2432]{1,0:T(8,128)(2,1)S(1)}, u32[]{:S(2)}, u32[]{:S(2)}) collective-permute-start(bf16[16,2432]{1,0:T(8,128)(2,1)S(1)} %get-tuple-element.11), channel_id=1, source_target_pairs={{0,6},{2,8},{4,10},{6,12},{8,14},{10,0},{12,2},{14,4},{1,7},{3,9},... | collective-permute-start | bytes 233480 | tf_op jit(solution)/shard_map/ppermute | solution.py:124
  79.7 2.3 %collective-permute-start.30 = (bf16[16,2432]{1,0:T(8,128)(2,1)S(1)}, bf16[16,2432]{1,0:T(8,128)(2,1)S(1)}, u32[]{:S(2)}, u32[]{:S(2)}) collective-permute-start(bf16[16,2432]{1,0:T(8,128)(2,1)S(1)} %get-tuple-element.12), channel_id=1, source_target_pairs={{0,4},{2,6},{4,8},{6,10},{8,12},{10,14},{12,0},{14,2},{1,5},{3,7},... | collective-permute-start | bytes 233480 | tf_op jit(solution)/shard_map/ppermute | solution.py:124
  82.9 6.5 %collective-permute-start.31 = (bf16[16,2432]{1,0:T(8,128)(2,1)S(1)}, bf16[16,2432]{1,0:T(8,128)(2,1)S(1)}, u32[]{:S(2)}, u32[]{:S(2)}) collective-permute-start(bf16[16,2432]{1,0:T(8,128)(2,1)S(1)} %get-tuple-element.6), channel_id=1, source_target_pairs={{0,2},{2,4},{4,6},{6,8},{8,10},{10,12},{12,14},{14,0},{1,3},{3,5},... | collective-permute-start | bytes 233480 | tf_op jit(solution)/shard_map/ppermute | solution.py:124
  90.2 1.2 %collective-permute-done.31 = bf16[16,2432]{1,0:T(8,128)(2,1)S(1)} collective-permute-done((bf16[16,2432]{1,0:T(8,128)(2,1)S(1)}, bf16[16,2432]{1,0:T(8,128)(2,1)S(1)}, u32[]{:S(2)}, u32[]{:S(2)}) %collective-permute-start.31) | collective-permute-done | bytes 77856 | tf_op jit(solution)/shard_map/ppermute | solution.py:124
  (132 shorter events, 20.3 us)
Async XLA Ops:
  4.5 14.1 %collective-permute-start.1 = (bf16[16,2432]{1,0:T(8,128)(2,1)}, bf16[16,2432]{1,0:T(8,128)(2,1)}, u32[]{:S(2)}, u32[]{:S(2)}) collective-permute-start(bf16[16,2432]{1,0:T(8,128)(2,1)} %get-tuple-element.31), channel_id=1, source_target_pairs={{0,2},{2,4},{4,6},{6,8},{8,10},{10,12},{12,14},{14,0},{1,3},{3,5},... | collective-permute-start | bytes 233480 | tf_op jit(solution)/shard_map/ppermute | solution.py:124
  7.4 13.5 %collective-permute-start.2 = (bf16[16,2432]{1,0:T(8,128)(2,1)S(1)}, bf16[16,2432]{1,0:T(8,128)(2,1)}, u32[]{:S(2)}, u32[]{:S(2)}) collective-permute-start(bf16[16,2432]{1,0:T(8,128)(2,1)S(1)} %get-tuple-element.32), channel_id=1, source_target_pairs={{0,4},{2,6},{4,8},{6,10},{8,12},{10,14},{12,0},{14,2},{1,5},{3,7},... | collective-permute-start | bytes 233480 | tf_op jit(solution)/shard_map/ppermute | solution.py:124
  9.0 14.3 %collective-permute-start.3 = (bf16[16,2432]{1,0:T(8,128)(2,1)S(1)}, bf16[16,2432]{1,0:T(8,128)(2,1)}, u32[]{:S(2)}, u32[]{:S(2)}) collective-permute-start(bf16[16,2432]{1,0:T(8,128)(2,1)S(1)} %get-tuple-element.33), channel_id=1, source_target_pairs={{0,6},{2,8},{4,10},{6,12},{8,14},{10,0},{12,2},{14,4},{1,7},{3,9},... | collective-permute-start | bytes 233480 | tf_op jit(solution)/shard_map/ppermute | solution.py:124
  11.5 12.7 %collective-permute-start.4 = (bf16[16,2432]{1,0:T(8,128)(2,1)S(1)}, bf16[16,2432]{1,0:T(8,128)(2,1)}, u32[]{:S(2)}, u32[]{:S(2)}) collective-permute-start(bf16[16,2432]{1,0:T(8,128)(2,1)S(1)} %get-tuple-element.34), channel_id=1, source_target_pairs={{0,8},{2,10},{4,12},{6,14},{8,0},{10,2},{12,4},{14,6},{1,9},{3,11}... | collective-permute-start | bytes 233480 | tf_op jit(solution)/shard_map/ppermute | solution.py:124
  12.8 12.9 %collective-permute-start.5 = (bf16[16,2432]{1,0:T(8,128)(2,1)S(1)}, bf16[16,2432]{1,0:T(8,128)(2,1)}, u32[]{:S(2)}, u32[]{:S(2)}) collective-permute-start(bf16[16,2432]{1,0:T(8,128)(2,1)S(1)} %get-tuple-element.29), channel_id=1, source_target_pairs={{0,10},{2,12},{4,14},{6,0},{8,2},{10,4},{12,6},{14,8},{1,11},{3,13... | collective-permute-start | bytes 233480 | tf_op jit(solution)/shard_map/ppermute | solution.py:124
  18.5 8.0 %collective-permute-start.6 = (bf16[16,2432]{1,0:T(8,128)(2,1)S(1)}, bf16[16,2432]{1,0:T(8,128)(2,1)S(1)}, u32[]{:S(2)}, u32[]{:S(2)}) collective-permute-start(bf16[16,2432]{1,0:T(8,128)(2,1)S(1)} %get-tuple-element.35), channel_id=1, source_target_pairs={{0,12},{2,14},{4,0},{6,2},{8,4},{10,6},{12,8},{14,10},{1,13},{3,15... | collective-permute-start | bytes 233480 | tf_op jit(solution)/shard_map/ppermute | solution.py:124
  20.8 5.7 %collective-permute-start.7 = (bf16[16,2432]{1,0:T(8,128)(2,1)S(1)}, bf16[16,2432]{1,0:T(8,128)(2,1)S(1)}, u32[]{:S(2)}, u32[]{:S(2)}) collective-permute-start(bf16[16,2432]{1,0:T(8,128)(2,1)S(1)} %get-tuple-element.28), channel_id=1, source_target_pairs={{0,14},{2,0},{4,2},{6,4},{8,6},{10,8},{12,10},{14,12},{1,15},{3,1}... | collective-permute-start | bytes 233480 | tf_op jit(solution)/shard_map/ppermute | solution.py:124
  23.2 4.8 %collective-permute-start.8 = (bf16[512,2304]{1,0:T(8,128)(2,1)}, bf16[512,2304]{1,0:T(8,128)(2,1)S(1)}, u32[]{:S(2)}, u32[]{:S(2)}) collective-permute-start(bf16[512,2304]{1,0:T(8,128)(2,1)} %pad_maximum_fusion), channel_id=1, source_target_pairs={{0,1},{1,0},{2,3},{3,2},{4,5},{5,4},{6,7},{7,6},{8,9},{9,8},{10,11... | collective-permute-start | bytes 7077896 | tf_op jit(solution)/shard_map/ppermute | solution.py:116
  24.2 5.2 %collective-permute-start = (f32[4624]{0:T(1024)S(1)}, f32[4624]{0:T(1024)S(1)}, u32[]{:S(2)}, u32[]{:S(2)}) collective-permute-start(f32[4624]{0:T(1024)S(1)} %pad_maximum_fusion.7), channel_id=1, source_target_pairs={{0,1},{1,0},{2,3},{3,2},{4,5},{5,4},{6,7},{7,6},{8,9},{9,8},{10,11... | collective-permute-start | bytes 55496 | tf_op jit(solution)/shard_map/ppermute | solution.py:116
  29.2 1.5 %collective-permute-start.9 = (f32[128,384]{1,0:T(8,128)S(1)}, f32[128,384]{1,0:T(8,128)S(1)}, u32[]{:S(2)}, u32[]{:S(2)}) collective-permute-start(f32[128,384]{1,0:T(8,128)S(1)} %pad_maximum_fusion.1), channel_id=1, source_target_pairs={{0,1},{1,0},{2,3},{3,2},{4,5},{5,4},{6,7},{7,6},{8,9},{9,8},{10,11... | collective-permute-start | bytes 589832 | tf_op jit(solution)/shard_map/ppermute | solution.py:116
  31.5 6.5 %collective-permute-start.10 = (bf16[16,2432]{1,0:T(8,128)(2,1)S(1)}, bf16[16,2432]{1,0:T(8,128)(2,1)S(1)}, u32[]{:S(2)}, u32[]{:S(2)}) collective-permute-start(bf16[16,2432]{1,0:T(8,128)(2,1)S(1)} %get-tuple-element.22), channel_id=1, source_target_pairs={{0,14},{2,0},{4,2},{6,4},{8,6},{10,8},{12,10},{14,12},{1,15},{3,1}... | collective-permute-start | bytes 233480 | tf_op jit(solution)/shard_map/ppermute | solution.py:124
  33.0 6.6 %collective-permute-start.11 = (bf16[16,2432]{1,0:T(8,128)(2,1)S(1)}, bf16[16,2432]{1,0:T(8,128)(2,1)S(1)}, u32[]{:S(2)}, u32[]{:S(2)}) collective-permute-start(bf16[16,2432]{1,0:T(8,128)(2,1)S(1)} %get-tuple-element.23), channel_id=1, source_target_pairs={{0,12},{2,14},{4,0},{6,2},{8,4},{10,6},{12,8},{14,10},{1,13},{3,15... | collective-permute-start | bytes 233480 | tf_op jit(solution)/shard_map/ppermute | solution.py:124
  33.4 6.4 %collective-permute-start.12 = (bf16[16,2432]{1,0:T(8,128)(2,1)S(1)}, bf16[16,2432]{1,0:T(8,128)(2,1)S(1)}, u32[]{:S(2)}, u32[]{:S(2)}) collective-permute-start(bf16[16,2432]{1,0:T(8,128)(2,1)S(1)} %get-tuple-element.24), channel_id=1, source_target_pairs={{0,10},{2,12},{4,14},{6,0},{8,2},{10,4},{12,6},{14,8},{1,11},{3,13... | collective-permute-start | bytes 233480 | tf_op jit(solution)/shard_map/ppermute | solution.py:124
  35.1 12.6 %collective-permute-start.13 = (bf16[16,2432]{1,0:T(8,128)(2,1)S(1)}, bf16[16,2432]{1,0:T(8,128)(2,1)S(1)}, u32[]{:S(2)}, u32[]{:S(2)}) collective-permute-start(bf16[16,2432]{1,0:T(8,128)(2,1)S(1)} %get-tuple-element.25), channel_id=1, source_target_pairs={{0,8},{2,10},{4,12},{6,14},{8,0},{10,2},{12,4},{14,6},{1,9},{3,11}... | collective-permute-start | bytes 233480 | tf_op jit(solution)/shard_map/ppermute | solution.py:124
  37.6 12.0 %collective-permute-start.14 = (bf16[16,2432]{1,0:T(8,128)(2,1)S(1)}, bf16[16,2432]{1,0:T(8,128)(2,1)S(1)}, u32[]{:S(2)}, u32[]{:S(2)}) collective-permute-start(bf16[16,2432]{1,0:T(8,128)(2,1)S(1)} %get-tuple-element.26), channel_id=1, source_target_pairs={{0,6},{2,8},{4,10},{6,12},{8,14},{10,0},{12,2},{14,4},{1,7},{3,9},... | collective-permute-start | bytes 233480 | tf_op jit(solution)/shard_map/ppermute | solution.py:124
  38.0 11.6 %collective-permute-start.15 = (bf16[16,2432]{1,0:T(8,128)(2,1)S(1)}, bf16[16,2432]{1,0:T(8,128)(2,1)S(1)}, u32[]{:S(2)}, u32[]{:S(2)}) collective-permute-start(bf16[16,2432]{1,0:T(8,128)(2,1)S(1)} %get-tuple-element.27), channel_id=1, source_target_pairs={{0,4},{2,6},{4,8},{6,10},{8,12},{10,14},{12,0},{14,2},{1,5},{3,7},... | collective-permute-start | bytes 233480 | tf_op jit(solution)/shard_map/ppermute | solution.py:124
  39.6 10.0 %collective-permute-start.16 = (bf16[16,2432]{1,0:T(8,128)(2,1)S(1)}, bf16[16,2432]{1,0:T(8,128)(2,1)S(1)}, u32[]{:S(2)}, u32[]{:S(2)}) collective-permute-start(bf16[16,2432]{1,0:T(8,128)(2,1)S(1)} %get-tuple-element.21), channel_id=1, source_target_pairs={{0,2},{2,4},{4,6},{6,8},{8,10},{10,12},{12,14},{14,0},{1,3},{3,5},... | collective-permute-start | bytes 233480 | tf_op jit(solution)/shard_map/ppermute | solution.py:124
  49.9 8.0 %collective-permute-start.17 = (bf16[16,2432]{1,0:T(8,128)(2,1)S(1)}, bf16[16,2432]{1,0:T(8,128)(2,1)S(1)}, u32[]{:S(2)}, u32[]{:S(2)}) collective-permute-start(bf16[16,2432]{1,0:T(8,128)(2,1)S(1)} %get-tuple-element.17), channel_id=1, source_target_pairs={{0,2},{2,4},{4,6},{6,8},{8,10},{10,12},{12,14},{14,0},{1,3},{3,5},... | collective-permute-start | bytes 233480 | tf_op jit(solution)/shard_map/ppermute | solution.py:124
  50.0 8.9 %collective-permute-start.18 = (bf16[16,2432]{1,0:T(8,128)(2,1)S(1)}, bf16[16,2432]{1,0:T(8,128)(2,1)S(1)}, u32[]{:S(2)}, u32[]{:S(2)}) collective-permute-start(bf16[16,2432]{1,0:T(8,128)(2,1)S(1)} %get-tuple-element.16), channel_id=1, source_target_pairs={{0,4},{2,6},{4,8},{6,10},{8,12},{10,14},{12,0},{14,2},{1,5},{3,7},... | collective-permute-start | bytes 233480 | tf_op jit(solution)/shard_map/ppermute | solution.py:124
  50.8 12.1 %collective-permute-start.19 = (bf16[16,2432]{1,0:T(8,128)(2,1)S(1)}, bf16[16,2432]{1,0:T(8,128)(2,1)S(1)}, u32[]{:S(2)}, u32[]{:S(2)}) collective-permute-start(bf16[16,2432]{1,0:T(8,128)(2,1)S(1)} %get-tuple-element.15), channel_id=1, source_target_pairs={{0,6},{2,8},{4,10},{6,12},{8,14},{10,0},{12,2},{14,4},{1,7},{3,9},... | collective-permute-start | bytes 233480 | tf_op jit(solution)/shard_map/ppermute | solution.py:124
  53.5 10.7 %collective-permute-start.20 = (bf16[16,2432]{1,0:T(8,128)(2,1)S(1)}, bf16[16,2432]{1,0:T(8,128)(2,1)S(1)}, u32[]{:S(2)}, u32[]{:S(2)}) collective-permute-start(bf16[16,2432]{1,0:T(8,128)(2,1)S(1)} %get-tuple-element.14), channel_id=1, source_target_pairs={{0,8},{2,10},{4,12},{6,14},{8,0},{10,2},{12,4},{14,6},{1,9},{3,11}... | collective-permute-start | bytes 233480 | tf_op jit(solution)/shard_map/ppermute | solution.py:124
  56.0 8.2 %collective-permute-start.21 = (bf16[16,2432]{1,0:T(8,128)(2,1)S(1)}, bf16[16,2432]{1,0:T(8,128)(2,1)S(1)}, u32[]{:S(2)}, u32[]{:S(2)}) collective-permute-start(bf16[16,2432]{1,0:T(8,128)(2,1)S(1)} %get-tuple-element.18), channel_id=1, source_target_pairs={{0,10},{2,12},{4,14},{6,0},{8,2},{10,4},{12,6},{14,8},{1,11},{3,13... | collective-permute-start | bytes 233480 | tf_op jit(solution)/shard_map/ppermute | solution.py:124
  57.9 6.3 %collective-permute-start.22 = (bf16[16,2432]{1,0:T(8,128)(2,1)S(1)}, bf16[16,2432]{1,0:T(8,128)(2,1)S(1)}, u32[]{:S(2)}, u32[]{:S(2)}) collective-permute-start(bf16[16,2432]{1,0:T(8,128)(2,1)S(1)} %get-tuple-element.19), channel_id=1, source_target_pairs={{0,12},{2,14},{4,0},{6,2},{8,4},{10,6},{12,8},{14,10},{1,13},{3,15... | collective-permute-start | bytes 233480 | tf_op jit(solution)/shard_map/ppermute | solution.py:124
  58.9 5.4 %collective-permute-start.23 = (bf16[16,2432]{1,0:T(8,128)(2,1)S(1)}, bf16[16,2432]{1,0:T(8,128)(2,1)S(1)}, u32[]{:S(2)}, u32[]{:S(2)}) collective-permute-start(bf16[16,2432]{1,0:T(8,128)(2,1)S(1)} %get-tuple-element.13), channel_id=1, source_target_pairs={{0,14},{2,0},{4,2},{6,4},{8,6},{10,8},{12,10},{14,12},{1,15},{3,1}... | collective-permute-start | bytes 233480 | tf_op jit(solution)/shard_map/ppermute | solution.py:124
  65.6 27.1 %collective-permute-start.33 = (bf16[16,2304]{1,0:T(8,128)(2,1)S(1)}, bf16[16,2304]{1,0:T(8,128)(2,1)S(1)}, u32[]{:S(2)}, u32[]{:S(2)}) collective-permute-start(bf16[16,2304]{1,0:T(8,128)(2,1)S(1)} %add_convert_fusion.1), channel_id=1, source_target_pairs={{0,1},{1,0},{2,3},{3,2},{4,5},{5,4},{6,7},{7,6},{8,9},{9,8},{10,11... | collective-permute-start | bytes 221192 | tf_op jit(solution)/shard_map/ppermute | solution.py:116
  67.7 10.2 %collective-permute-start.25 = (bf16[16,2432]{1,0:T(8,128)(2,1)S(1)}, bf16[16,2432]{1,0:T(8,128)(2,1)S(1)}, u32[]{:S(2)}, u32[]{:S(2)}) collective-permute-start(bf16[16,2432]{1,0:T(8,128)(2,1)S(1)} %get-tuple-element.7), channel_id=1, source_target_pairs={{0,14},{2,0},{4,2},{6,4},{8,6},{10,8},{12,10},{14,12},{1,15},{3,1}... | collective-permute-start | bytes 233480 | tf_op jit(solution)/shard_map/ppermute | solution.py:124
  74.2 5.5 %collective-permute-start.26 = (bf16[16,2432]{1,0:T(8,128)(2,1)S(1)}, bf16[16,2432]{1,0:T(8,128)(2,1)S(1)}, u32[]{:S(2)}, u32[]{:S(2)}) collective-permute-start(bf16[16,2432]{1,0:T(8,128)(2,1)S(1)} %get-tuple-element.8), channel_id=1, source_target_pairs={{0,12},{2,14},{4,0},{6,2},{8,4},{10,6},{12,8},{14,10},{1,13},{3,15... | collective-permute-start | bytes 233480 | tf_op jit(solution)/shard_map/ppermute | solution.py:124
  76.8 6.1 %collective-permute-start.27 = (bf16[16,2432]{1,0:T(8,128)(2,1)S(1)}, bf16[16,2432]{1,0:T(8,128)(2,1)S(1)}, u32[]{:S(2)}, u32[]{:S(2)}) collective-permute-start(bf16[16,2432]{1,0:T(8,128)(2,1)S(1)} %get-tuple-element.9), channel_id=1, source_target_pairs={{0,10},{2,12},{4,14},{6,0},{8,2},{10,4},{12,6},{14,8},{1,11},{3,13... | collective-permute-start | bytes 233480 | tf_op jit(solution)/shard_map/ppermute | solution.py:124
  76.8 12.6 %collective-permute-start.28 = (bf16[16,2432]{1,0:T(8,128)(2,1)S(1)}, bf16[16,2432]{1,0:T(8,128)(2,1)S(1)}, u32[]{:S(2)}, u32[]{:S(2)}) collective-permute-start(bf16[16,2432]{1,0:T(8,128)(2,1)S(1)} %get-tuple-element.10), channel_id=1, source_target_pairs={{0,8},{2,10},{4,12},{6,14},{8,0},{10,2},{12,4},{14,6},{1,9},{3,11}... | collective-permute-start | bytes 233480 | tf_op jit(solution)/shard_map/ppermute | solution.py:124
  77.9 12.3 %collective-permute-start.29 = (bf16[16,2432]{1,0:T(8,128)(2,1)S(1)}, bf16[16,2432]{1,0:T(8,128)(2,1)S(1)}, u32[]{:S(2)}, u32[]{:S(2)}) collective-permute-start(bf16[16,2432]{1,0:T(8,128)(2,1)S(1)} %get-tuple-element.11), channel_id=1, source_target_pairs={{0,6},{2,8},{4,10},{6,12},{8,14},{10,0},{12,2},{14,4},{1,7},{3,9},... | collective-permute-start | bytes 233480 | tf_op jit(solution)/shard_map/ppermute | solution.py:124
  79.7 10.4 %collective-permute-start.30 = (bf16[16,2432]{1,0:T(8,128)(2,1)S(1)}, bf16[16,2432]{1,0:T(8,128)(2,1)S(1)}, u32[]{:S(2)}, u32[]{:S(2)}) collective-permute-start(bf16[16,2432]{1,0:T(8,128)(2,1)S(1)} %get-tuple-element.12), channel_id=1, source_target_pairs={{0,4},{2,6},{4,8},{6,10},{8,12},{10,14},{12,0},{14,2},{1,5},{3,7},... | collective-permute-start | bytes 233480 | tf_op jit(solution)/shard_map/ppermute | solution.py:124
  82.9 8.5 %collective-permute-start.31 = (bf16[16,2432]{1,0:T(8,128)(2,1)S(1)}, bf16[16,2432]{1,0:T(8,128)(2,1)S(1)}, u32[]{:S(2)}, u32[]{:S(2)}) collective-permute-start(bf16[16,2432]{1,0:T(8,128)(2,1)S(1)} %get-tuple-element.6), channel_id=1, source_target_pairs={{0,2},{2,4},{4,6},{6,8},{8,10},{10,12},{12,14},{14,0},{1,3},{3,5},... | collective-permute-start | bytes 233480 | tf_op jit(solution)/shard_map/ppermute | solution.py:124
  (8 other events, 42.9 us)

commit v6 on v5

--- a/solution.py
+++ b/solution.py
@@ -116,13 +116,16 @@
     return lax.ppermute(block, "section", [(0, 1), (1, 0)])
 
 
-def exchange(parts, sign):
+def exchange(parts, sign, gate=None):
     peers = parts.shape[0]
     moved = [parts[0]]
     for shift in range(1, peers):
+        piece = parts[shift]
+        if gate is not None and shift >= peers // 2 + 1:
+            piece, gate = lax.optimization_barrier((piece, gate))
         route = [(d, (d + sign * shift) % peers) for d in range(peers)]
-        moved.append(lax.ppermute(parts[shift], "dict", route))
-    return jnp.stack(moved, axis=0)
+        moved.append(lax.ppermute(piece, "dict", route))
+    return jnp.stack(moved, axis=0), gate
 
 
 def split_layer(g_half, routes_l, acts_l, own, other, is_own, gain_half, scale_l):
@@ -145,7 +148,8 @@
     sent = jnp.concatenate(
         [jnp.broadcast_to(g_half[None], (peers, rows, half)), placed], axis=-1
     )
-    got = exchange(sent, 1).reshape(peers * rows, half + block)
+    got, other = exchange(sent, 1, other)
+    got = got.reshape(peers * rows, half + block)
     g_all = got[:, :half]
     code_all = got[:, half:]
 
@@ -169,7 +173,7 @@
     for spot in range(1, held):
         dz_pick = dz_pick + dz[:, spot * block:(spot + 1) * block]
     back = jnp.concatenate([contrib, dz_pick], axis=-1).reshape(peers, rows, half + block)
-    returned = exchange(back, -1)
+    returned, _ = exchange(back, -1)
     total = jnp.sum(returned[:, :, :half].astype(jnp.float32), axis=0)
     dz_back = returned[:, :, half:]
     dz_slot = jnp.einsum("rks,srj->rkj", at_rel, dz_back, preferred_element_type=jnp.float32)

time: 94.1 us -> 101 us (1.073)
  waiting for transfers between devices: 20 us -> 32.2 us
  starting transfers between devices: 54.6 us -> 50 us
    ppermute x28, waiting for transfers between devices: 16.4 us -> 30 us  [exchange(): moved.append(lax.ppermute(piece, 'dict', route))]
    ppermute x28, starting transfers between devices: 53.2 us -> 48.8 us  [exchange(): moved.append(lax.ppermute(piece, 'dict', route))]
    ppermute x6, waiting for transfers between devices: 3.57 us -> 2.27 us  [swap_cores(): return lax.ppermute(block, 'section', [(0, 1), (1, 0)])]
    unnamed x38 -> x40, local copies, waits for them, and re-layouts: 4.79 us -> 5.15 us
  transfers between devices with their start and end apart: 34 -> 34, of which waited for: 12 -> 15; matrix products, arithmetic and copies ran while one was open for 12% -> 9% of each run, Pallas kernels for 0% -> 0%
where the time goes in v6:
time: 101 us; the launch traced here: 100 us
  starting transfers between devices  50 us (50%)
  waiting for transfers between devices  32.2 us (32%)
  local copies, waits for them, and re-layouts  8.25 us (8%)
  other arithmetic  4.52 us (4%)
  matrix products  4.17 us (4%)
  between operations  1.14 us (1%)
    ppermute x28, starting transfers between devices, exchange(): moved.append(lax.ppermute(piece, 'dict', route))  48.8 us
    ppermute x28, waiting for transfers between devices, exchange(): moved.append(lax.ppermute(piece, 'dict', route))  30 us
    unnamed x40, local copies, waits for them, and re-layouts  5.15 us
    ppermute x6, waiting for transfers between devices, swap_cores(): return lax.ppermute(block, 'section', [(0, 1), (1, 0)])  2.27 us
    dot_general x4, matrix products, with_dec(): lax.dot_general(g_all, dec, (((1,), (1,)), ((), ())), preferred_element_t...  2.15 us
  transfers between devices with their start and end apart: 34, of which 15 were waited for; matrix products, arithmetic and copies ran while one was open for 9% of the time, Pallas kernels for 0%

profile of v6, /device:TPU:0, one launch (start us, length us, event | category | flops | bytes accessed | tf_op | source)
XLA Modules:
  0.0 100.3 jit_solution(14031424802433944574)
XLA Ops:
  0.6 1.8 %dynamic-slice_bitcast_fusion = (bf16[256,2304]{1,0:T(8,128)(2,1)S(1)}, bf16[256,2304]{1,0:T(8,128)(2,1)S(1)}) fusion(bf16[1,256,4608]{2,1,0:T(8,128)(2,1)} %param.11, s32[]{:T(128)S(6)} %select_n.192, bf16[1,256,4608]{2,1,0:T(8,128)(2,1)} %param.10), kind=kLoop, calls=%fused_computation.48 | loop fusion | bytes 4718596 | tf_op jit(solution)/shard_map/dynamic_slice | solution.py:200
  2.5 1.6 %pad_maximum_fusion = bf16[512,2304]{1,0:T(8,128)(2,1)} fusion(bf16[256,2304]{1,0:T(8,128)(2,1)S(1)} %get-tuple-element.78, bf16[256,2304]{1,0:T(8,128)(2,1)S(1)} %get-tuple-element.79), kind=kLoop, calls=%fused_computation.4 | loop fusion | flops 4718592 | bytes 4718592 | tf_op jit(solution)/shard_map/concatenate | solution.py:197
  5.9 2.5 %collective-permute-start.1 = (bf16[16,2432]{1,0:T(8,128)(2,1)}, bf16[16,2432]{1,0:T(8,128)(2,1)}, u32[]{:S(2)}, u32[]{:S(2)}) collective-permute-start(bf16[16,2432]{1,0:T(8,128)(2,1)} %get-tuple-element.69), channel_id=1, source_target_pairs={{0,2},{2,4},{4,6},{6,8},{8,10},{10,12},{12,14},{14,0},{1,3},{3,5},... | collective-permute-start | bytes 233480 | tf_op jit(solution)/shard_map/ppermute | solution.py:127
  8.4 1.6 %collective-permute-start.2 = (bf16[16,2432]{1,0:T(8,128)(2,1)}, bf16[16,2432]{1,0:T(8,128)(2,1)}, u32[]{:S(2)}, u32[]{:S(2)}) collective-permute-start(bf16[16,2432]{1,0:T(8,128)(2,1)} %get-tuple-element.70), channel_id=1, source_target_pairs={{0,4},{2,6},{4,8},{6,10},{8,12},{10,14},{12,0},{14,2},{1,5},{3,7},... | collective-permute-start | bytes 233480 | tf_op jit(solution)/shard_map/ppermute | solution.py:127
  9.9 2.6 %collective-permute-start.3 = (bf16[16,2432]{1,0:T(8,128)(2,1)}, bf16[16,2432]{1,0:T(8,128)(2,1)}, u32[]{:S(2)}, u32[]{:S(2)}) collective-permute-start(bf16[16,2432]{1,0:T(8,128)(2,1)} %get-tuple-element.71), channel_id=1, source_target_pairs={{0,6},{2,8},{4,10},{6,12},{8,14},{10,0},{12,2},{14,4},{1,7},{3,9},... | collective-permute-start | bytes 233480 | tf_op jit(solution)/shard_map/ppermute | solution.py:127
  12.5 1.2 %collective-permute-start.4 = (bf16[16,2432]{1,0:T(8,128)(2,1)S(1)}, bf16[16,2432]{1,0:T(8,128)(2,1)}, u32[]{:S(2)}, u32[]{:S(2)}) collective-permute-start(bf16[16,2432]{1,0:T(8,128)(2,1)S(1)} %get-tuple-element.72), channel_id=1, source_target_pairs={{0,8},{2,10},{4,12},{6,14},{8,0},{10,2},{12,4},{14,6},{1,9},{3,11}... | collective-permute-start | bytes 233480 | tf_op jit(solution)/shard_map/ppermute | solution.py:127
  15.0 0.9 bitcast_dynamic-update-slice_fusion.29
  15.9 0.9 bitcast_dynamic-update-slice_fusion.28
  16.8 4.7 %collective-permute-done.3 = bf16[16,2432]{1,0:T(8,128)(2,1)} collective-permute-done((bf16[16,2432]{1,0:T(8,128)(2,1)}, bf16[16,2432]{1,0:T(8,128)(2,1)}, u32[]{:S(2)}, u32[]{:S(2)}) %collective-permute-start.3) | collective-permute-done | bytes 77856 | tf_op jit(solution)/shard_map/ppermute | solution.py:127
  23.8 1.8 %collective-permute-start.8 = (bf16[16,2432]{1,0:T(8,128)(2,1)S(1)}, bf16[16,2432]{1,0:T(8,128)(2,1)S(1)}, u32[]{:S(2)}, u32[]{:S(2)}) collective-permute-start(bf16[16,2432]{1,0:T(8,128)(2,1)S(1)} %get-tuple-element.26), channel_id=1, source_target_pairs={{0,14},{2,0},{4,2},{6,4},{8,6},{10,8},{12,10},{14,12},{1,15},{3,1}... | collective-permute-start | bytes 233480 | tf_op jit(solution)/shard_map/ppermute | solution.py:127
  25.6 2.4 %collective-permute-done.6 = bf16[16,2432]{1,0:T(8,128)(2,1)S(1)} collective-permute-done((bf16[16,2432]{1,0:T(8,128)(2,1)S(1)}, bf16[16,2432]{1,0:T(8,128)(2,1)S(1)}, u32[]{:S(2)}, u32[]{:S(2)}) %collective-permute-start.6) | collective-permute-done | bytes 77856 | tf_op jit(solution)/shard_map/ppermute | solution.py:127
  28.0 3.6 %collective-permute-done.7 = bf16[16,2432]{1,0:T(8,128)(2,1)S(1)} collective-permute-done((bf16[16,2432]{1,0:T(8,128)(2,1)S(1)}, bf16[16,2432]{1,0:T(8,128)(2,1)S(1)}, u32[]{:S(2)}, u32[]{:S(2)}) %collective-permute-start.7) | collective-permute-done | bytes 77856 | tf_op jit(solution)/shard_map/ppermute | solution.py:127
  33.0 1.3 %collective-permute-done.9 = f32[128,384]{1,0:T(8,128)S(1)} collective-permute-done((f32[128,384]{1,0:T(8,128)S(1)}, f32[128,384]{1,0:T(8,128)S(1)}, u32[]{:S(2)}, u32[]{:S(2)}) %collective-permute-start.9) | collective-permute-done | bytes 196640 | tf_op jit(solution)/shard_map/ppermute | solution.py:116
  34.7 1.2 %copy-done.1 = bf16[1,256,4608]{2,1,0:T(8,128)(2,1)S(1)} copy-done((bf16[1,256,4608]{2,1,0:T(8,128)(2,1)S(1)}, bf16[1,256,4608]{2,1,0:T(8,128)(2,1)}, u32[]{:S(2)}) %copy-start.1) | copy-done | bytes 2359320
  36.3 1.6 %collective-permute-start.10 = (bf16[16,2432]{1,0:T(8,128)(2,1)S(1)}, bf16[16,2432]{1,0:T(8,128)(2,1)S(1)}, u32[]{:S(2)}, u32[]{:S(2)}) collective-permute-start(bf16[16,2432]{1,0:T(8,128)(2,1)S(1)} %get-tuple-element.60), channel_id=1, source_target_pairs={{0,14},{2,0},{4,2},{6,4},{8,6},{10,8},{12,10},{14,12},{1,15},{3,1}... | collective-permute-start | bytes 233480 | tf_op jit(solution)/shard_map/ppermute | solution.py:127
  37.9 2.5 %collective-permute-start.12 = (bf16[16,2432]{1,0:T(8,128)(2,1)S(1)}, bf16[16,2432]{1,0:T(8,128)(2,1)S(1)}, u32[]{:S(2)}, u32[]{:S(2)}) collective-permute-start(bf16[16,2432]{1,0:T(8,128)(2,1)S(1)} %get-tuple-element.62), channel_id=1, source_target_pairs={{0,10},{2,12},{4,14},{6,0},{8,2},{10,4},{12,6},{14,8},{1,11},{3,13... | collective-permute-start | bytes 233480 | tf_op jit(solution)/shard_map/ppermute | solution.py:127
  40.5 1.8 %collective-permute-start.13 = (bf16[16,2432]{1,0:T(8,128)(2,1)S(1)}, bf16[16,2432]{1,0:T(8,128)(2,1)S(1)}, u32[]{:S(2)}, u32[]{:S(2)}) collective-permute-start(bf16[16,2432]{1,0:T(8,128)(2,1)S(1)} %get-tuple-element.63), channel_id=1, source_target_pairs={{0,8},{2,10},{4,12},{6,14},{8,0},{10,2},{12,4},{14,6},{1,9},{3,11}... | collective-permute-start | bytes 233480 | tf_op jit(solution)/shard_map/ppermute | solution.py:127
  42.8 1.5 %collective-permute-start.15 = (bf16[16,2432]{1,0:T(8,128)(2,1)S(1)}, bf16[16,2432]{1,0:T(8,128)(2,1)S(1)}, u32[]{:S(2)}, u32[]{:S(2)}) collective-permute-start(bf16[16,2432]{1,0:T(8,128)(2,1)S(1)} %get-tuple-element.65), channel_id=1, source_target_pairs={{0,4},{2,6},{4,8},{6,10},{8,12},{10,14},{12,0},{14,2},{1,5},{3,7},... | collective-permute-start | bytes 233480 | tf_op jit(solution)/shard_map/ppermute | solution.py:127
  45.1 7.5 %collective-permute-done.13 = bf16[16,2432]{1,0:T(8,128)(2,1)S(1)} collective-permute-done((bf16[16,2432]{1,0:T(8,128)(2,1)S(1)}, bf16[16,2432]{1,0:T(8,128)(2,1)S(1)}, u32[]{:S(2)}, u32[]{:S(2)}) %collective-permute-start.13) | collective-permute-done | bytes 77856 | tf_op jit(solution)/shard_map/ppermute | solution.py:127
  52.6 2.0 %collective-permute-done.14 = bf16[16,2432]{1,0:T(8,128)(2,1)S(1)} collective-permute-done((bf16[16,2432]{1,0:T(8,128)(2,1)S(1)}, bf16[16,2432]{1,0:T(8,128)(2,1)S(1)}, u32[]{:S(2)}, u32[]{:S(2)}) %collective-permute-start.14) | collective-permute-done | bytes 77856 | tf_op jit(solution)/shard_map/ppermute | solution.py:127
  54.9 4.7 %collective-permute-start.23 = (bf16[16,2432]{1,0:T(8,128)(2,1)S(1)}, bf16[16,2432]{1,0:T(8,128)(2,1)S(1)}, u32[]{:S(2)}, u32[]{:S(2)}) collective-permute-start(bf16[16,2432]{1,0:T(8,128)(2,1)S(1)} %get-tuple-element.35), channel_id=1, source_target_pairs={{0,14},{2,0},{4,2},{6,4},{8,6},{10,8},{12,10},{14,12},{1,15},{3,1}... | collective-permute-start | bytes 233480 | tf_op jit(solution)/shard_map/ppermute | solution.py:127
  59.7 2.0 %collective-permute-start.18 = (bf16[16,2432]{1,0:T(8,128)(2,1)S(1)}, bf16[16,2432]{1,0:T(8,128)(2,1)S(1)}, u32[]{:S(2)}, u32[]{:S(2)}) collective-permute-start(bf16[16,2432]{1,0:T(8,128)(2,1)S(1)} %get-tuple-element.54), channel_id=1, source_target_pairs={{0,4},{2,6},{4,8},{6,10},{8,12},{10,14},{12,0},{14,2},{1,5},{3,7},... | collective-permute-start | bytes 233480 | tf_op jit(solution)/shard_map/ppermute | solution.py:127
  62.3 2.3 %collective-permute-start.19 = (bf16[16,2432]{1,0:T(8,128)(2,1)S(1)}, bf16[16,2432]{1,0:T(8,128)(2,1)S(1)}, u32[]{:S(2)}, u32[]{:S(2)}) collective-permute-start(bf16[16,2432]{1,0:T(8,128)(2,1)S(1)} %get-tuple-element.53), channel_id=1, source_target_pairs={{0,6},{2,8},{4,10},{6,12},{8,14},{10,0},{12,2},{14,4},{1,7},{3,9},... | collective-permute-start | bytes 233480 | tf_op jit(solution)/shard_map/ppermute | solution.py:127
  64.6 2.2 %collective-permute-done.18 = bf16[16,2432]{1,0:T(8,128)(2,1)S(1)} collective-permute-done((bf16[16,2432]{1,0:T(8,128)(2,1)S(1)}, bf16[16,2432]{1,0:T(8,128)(2,1)S(1)}, u32[]{:S(2)}, u32[]{:S(2)}) %collective-permute-start.18) | collective-permute-done | bytes 77856 | tf_op jit(solution)/shard_map/ppermute | solution.py:127
  66.9 3.8 %collective-permute-start.20 = (bf16[16,2432]{1,0:T(8,128)(2,1)S(1)}, bf16[16,2432]{1,0:T(8,128)(2,1)S(1)}, u32[]{:S(2)}, u32[]{:S(2)}) collective-permute-start(bf16[16,2432]{1,0:T(8,128)(2,1)S(1)} %get-tuple-element.52), channel_id=1, source_target_pairs={{0,8},{2,10},{4,12},{6,14},{8,0},{10,2},{12,4},{14,6},{1,9},{3,11}... | collective-permute-start | bytes 233480 | tf_op jit(solution)/shard_map/ppermute | solution.py:127
  70.7 1.6 %collective-permute-done.19 = bf16[16,2432]{1,0:T(8,128)(2,1)S(1)} collective-permute-done((bf16[16,2432]{1,0:T(8,128)(2,1)S(1)}, bf16[16,2432]{1,0:T(8,128)(2,1)S(1)}, u32[]{:S(2)}, u32[]{:S(2)}) %collective-permute-start.19) | collective-permute-done | bytes 77856 | tf_op jit(solution)/shard_map/ppermute | solution.py:127
  72.3 2.5 %collective-permute-done.20 = bf16[16,2432]{1,0:T(8,128)(2,1)S(1)} collective-permute-done((bf16[16,2432]{1,0:T(8,128)(2,1)S(1)}, bf16[16,2432]{1,0:T(8,128)(2,1)S(1)}, u32[]{:S(2)}, u32[]{:S(2)}) %collective-permute-start.20) | collective-permute-done | bytes 77856 | tf_op jit(solution)/shard_map/ppermute | solution.py:127
  78.6 3.5 %collective-permute-start.26 = (bf16[16,2432]{1,0:T(8,128)(2,1)S(1)}, bf16[16,2432]{1,0:T(8,128)(2,1)S(1)}, u32[]{:S(2)}, u32[]{:S(2)}) collective-permute-start(bf16[16,2432]{1,0:T(8,128)(2,1)S(1)} %get-tuple-element.46), channel_id=1, source_target_pairs={{0,12},{2,14},{4,0},{6,2},{8,4},{10,6},{12,8},{14,10},{1,13},{3,15... | collective-permute-start | bytes 233480 | tf_op jit(solution)/shard_map/ppermute | solution.py:127
  82.1 3.2 %collective-permute-start.28 = (bf16[16,2432]{1,0:T(8,128)(2,1)S(1)}, bf16[16,2432]{1,0:T(8,128)(2,1)S(1)}, u32[]{:S(2)}, u32[]{:S(2)}) collective-permute-start(bf16[16,2432]{1,0:T(8,128)(2,1)S(1)} %get-tuple-element.48), channel_id=1, source_target_pairs={{0,8},{2,10},{4,12},{6,14},{8,0},{10,2},{12,4},{14,6},{1,9},{3,11}... | collective-permute-start | bytes 233480 | tf_op jit(solution)/shard_map/ppermute | solution.py:127
  85.3 2.1 %collective-permute-start.30 = (bf16[16,2432]{1,0:T(8,128)(2,1)S(1)}, bf16[16,2432]{1,0:T(8,128)(2,1)S(1)}, u32[]{:S(2)}, u32[]{:S(2)}) collective-permute-start(bf16[16,2432]{1,0:T(8,128)(2,1)S(1)} %get-tuple-element.50), channel_id=1, source_target_pairs={{0,4},{2,6},{4,8},{6,10},{8,12},{10,14},{12,0},{14,2},{1,5},{3,7},... | collective-permute-start | bytes 233480 | tf_op jit(solution)/shard_map/ppermute | solution.py:127
  87.9 8.1 %collective-permute-start.31 = (bf16[16,2432]{1,0:T(8,128)(2,1)S(1)}, bf16[16,2432]{1,0:T(8,128)(2,1)S(1)}, u32[]{:S(2)}, u32[]{:S(2)}) collective-permute-start(bf16[16,2432]{1,0:T(8,128)(2,1)S(1)} %get-tuple-element.44), channel_id=1, source_target_pairs={{0,2},{2,4},{4,6},{6,8},{8,10},{10,12},{12,14},{14,0},{1,3},{3,5},... | collective-permute-start | bytes 233480 | tf_op jit(solution)/shard_map/ppermute | solution.py:127
  96.0 1.9 %collective-permute-done.31 = bf16[16,2432]{1,0:T(8,128)(2,1)S(1)} collective-permute-done((bf16[16,2432]{1,0:T(8,128)(2,1)S(1)}, bf16[16,2432]{1,0:T(8,128)(2,1)S(1)}, u32[]{:S(2)}, u32[]{:S(2)}) %collective-permute-start.31) | collective-permute-done | bytes 77856 | tf_op jit(solution)/shard_map/ppermute | solution.py:127
  (135 shorter events, 16.2 us)
Async XLA Ops:
  4.0 18.4 %collective-permute-start.5 = (bf16[512,2304]{1,0:T(8,128)(2,1)}, bf16[512,2304]{1,0:T(8,128)(2,1)S(1)}, u32[]{:S(2)}, u32[]{:S(2)}) collective-permute-start(bf16[512,2304]{1,0:T(8,128)(2,1)} %pad_maximum_fusion), channel_id=1, source_target_pairs={{0,1},{1,0},{2,3},{3,2},{4,5},{5,4},{6,7},{7,6},{8,9},{9,8},{10,11... | collective-permute-start | bytes 7077896 | tf_op jit(solution)/shard_map/ppermute | solution.py:116
  5.9 9.1 %collective-permute-start.1 = (bf16[16,2432]{1,0:T(8,128)(2,1)}, bf16[16,2432]{1,0:T(8,128)(2,1)}, u32[]{:S(2)}, u32[]{:S(2)}) collective-permute-start(bf16[16,2432]{1,0:T(8,128)(2,1)} %get-tuple-element.69), channel_id=1, source_target_pairs={{0,2},{2,4},{4,6},{6,8},{8,10},{10,12},{12,14},{14,0},{1,3},{3,5},... | collective-permute-start | bytes 233480 | tf_op jit(solution)/shard_map/ppermute | solution.py:127
  8.4 7.5 %collective-permute-start.2 = (bf16[16,2432]{1,0:T(8,128)(2,1)}, bf16[16,2432]{1,0:T(8,128)(2,1)}, u32[]{:S(2)}, u32[]{:S(2)}) collective-permute-start(bf16[16,2432]{1,0:T(8,128)(2,1)} %get-tuple-element.70), channel_id=1, source_target_pairs={{0,4},{2,6},{4,8},{6,10},{8,12},{10,14},{12,0},{14,2},{1,5},{3,7},... | collective-permute-start | bytes 233480 | tf_op jit(solution)/shard_map/ppermute | solution.py:127
  9.9 11.6 %collective-permute-start.3 = (bf16[16,2432]{1,0:T(8,128)(2,1)}, bf16[16,2432]{1,0:T(8,128)(2,1)}, u32[]{:S(2)}, u32[]{:S(2)}) collective-permute-start(bf16[16,2432]{1,0:T(8,128)(2,1)} %get-tuple-element.71), channel_id=1, source_target_pairs={{0,6},{2,8},{4,10},{6,12},{8,14},{10,0},{12,2},{14,4},{1,7},{3,9},... | collective-permute-start | bytes 233480 | tf_op jit(solution)/shard_map/ppermute | solution.py:127
  12.5 10.4 %collective-permute-start.4 = (bf16[16,2432]{1,0:T(8,128)(2,1)S(1)}, bf16[16,2432]{1,0:T(8,128)(2,1)}, u32[]{:S(2)}, u32[]{:S(2)}) collective-permute-start(bf16[16,2432]{1,0:T(8,128)(2,1)S(1)} %get-tuple-element.72), channel_id=1, source_target_pairs={{0,8},{2,10},{4,12},{6,14},{8,0},{10,2},{12,4},{14,6},{1,9},{3,11}... | collective-permute-start | bytes 233480 | tf_op jit(solution)/shard_map/ppermute | solution.py:127
  15.0 17.9 %collective-permute-start = (f32[4624]{0:T(1024)S(1)}, f32[4624]{0:T(1024)S(1)}, u32[]{:S(2)}, u32[]{:S(2)}) collective-permute-start(f32[4624]{0:T(1024)S(1)} %pad_maximum_fusion.7), channel_id=1, source_target_pairs={{0,1},{1,0},{2,3},{3,2},{4,5},{5,4},{6,7},{7,6},{8,9},{9,8},{10,11... | collective-permute-start | bytes 55496 | tf_op jit(solution)/shard_map/ppermute | solution.py:116
  22.6 5.4 %collective-permute-start.6 = (bf16[16,2432]{1,0:T(8,128)(2,1)S(1)}, bf16[16,2432]{1,0:T(8,128)(2,1)S(1)}, u32[]{:S(2)}, u32[]{:S(2)}) collective-permute-start(bf16[16,2432]{1,0:T(8,128)(2,1)S(1)} %get-tuple-element.20), channel_id=1, source_target_pairs={{0,10},{2,12},{4,14},{6,0},{8,2},{10,4},{12,6},{14,8},{1,11},{3,13... | collective-permute-start | bytes 233480 | tf_op jit(solution)/shard_map/ppermute | solution.py:127
  23.8 7.8 %collective-permute-start.8 = (bf16[16,2432]{1,0:T(8,128)(2,1)S(1)}, bf16[16,2432]{1,0:T(8,128)(2,1)S(1)}, u32[]{:S(2)}, u32[]{:S(2)}) collective-permute-start(bf16[16,2432]{1,0:T(8,128)(2,1)S(1)} %get-tuple-element.26), channel_id=1, source_target_pairs={{0,14},{2,0},{4,2},{6,4},{8,6},{10,8},{12,10},{14,12},{1,15},{3,1}... | collective-permute-start | bytes 233480 | tf_op jit(solution)/shard_map/ppermute | solution.py:127
  25.6 6.0 %collective-permute-start.7 = (bf16[16,2432]{1,0:T(8,128)(2,1)S(1)}, bf16[16,2432]{1,0:T(8,128)(2,1)S(1)}, u32[]{:S(2)}, u32[]{:S(2)}) collective-permute-start(bf16[16,2432]{1,0:T(8,128)(2,1)S(1)} %get-tuple-element.23), channel_id=1, source_target_pairs={{0,12},{2,14},{4,0},{6,2},{8,4},{10,6},{12,8},{14,10},{1,13},{3,15... | collective-permute-start | bytes 233480 | tf_op jit(solution)/shard_map/ppermute | solution.py:127
  32.7 1.5 %collective-permute-start.9 = (f32[128,384]{1,0:T(8,128)S(1)}, f32[128,384]{1,0:T(8,128)S(1)}, u32[]{:S(2)}, u32[]{:S(2)}) collective-permute-start(f32[128,384]{1,0:T(8,128)S(1)} %pad_maximum_fusion.1), channel_id=1, source_target_pairs={{0,1},{1,0},{2,3},{3,2},{4,5},{5,4},{6,7},{7,6},{8,9},{9,8},{10,11... | collective-permute-start | bytes 589832 | tf_op jit(solution)/shard_map/ppermute | solution.py:116
  36.3 6.5 %collective-permute-start.10 = (bf16[16,2432]{1,0:T(8,128)(2,1)S(1)}, bf16[16,2432]{1,0:T(8,128)(2,1)S(1)}, u32[]{:S(2)}, u32[]{:S(2)}) collective-permute-start(bf16[16,2432]{1,0:T(8,128)(2,1)S(1)} %get-tuple-element.60), channel_id=1, source_target_pairs={{0,14},{2,0},{4,2},{6,4},{8,6},{10,8},{12,10},{14,12},{1,15},{3,1}... | collective-permute-start | bytes 233480 | tf_op jit(solution)/shard_map/ppermute | solution.py:127
  37.9 6.5 %collective-permute-start.11 = (bf16[16,2432]{1,0:T(8,128)(2,1)S(1)}, bf16[16,2432]{1,0:T(8,128)(2,1)S(1)}, u32[]{:S(2)}, u32[]{:S(2)}) collective-permute-start(bf16[16,2432]{1,0:T(8,128)(2,1)S(1)} %get-tuple-element.61), channel_id=1, source_target_pairs={{0,12},{2,14},{4,0},{6,2},{8,4},{10,6},{12,8},{14,10},{1,13},{3,15... | collective-permute-start | bytes 233480 | tf_op jit(solution)/shard_map/ppermute | solution.py:127
  37.9 7.2 %collective-permute-start.12 = (bf16[16,2432]{1,0:T(8,128)(2,1)S(1)}, bf16[16,2432]{1,0:T(8,128)(2,1)S(1)}, u32[]{:S(2)}, u32[]{:S(2)}) collective-permute-start(bf16[16,2432]{1,0:T(8,128)(2,1)S(1)} %get-tuple-element.62), channel_id=1, source_target_pairs={{0,10},{2,12},{4,14},{6,0},{8,2},{10,4},{12,6},{14,8},{1,11},{3,13... | collective-permute-start | bytes 233480 | tf_op jit(solution)/shard_map/ppermute | solution.py:127
  40.5 12.1 %collective-permute-start.13 = (bf16[16,2432]{1,0:T(8,128)(2,1)S(1)}, bf16[16,2432]{1,0:T(8,128)(2,1)S(1)}, u32[]{:S(2)}, u32[]{:S(2)}) collective-permute-start(bf16[16,2432]{1,0:T(8,128)(2,1)S(1)} %get-tuple-element.63), channel_id=1, source_target_pairs={{0,8},{2,10},{4,12},{6,14},{8,0},{10,2},{12,4},{14,6},{1,9},{3,11}... | collective-permute-start | bytes 233480 | tf_op jit(solution)/shard_map/ppermute | solution.py:127
  42.3 12.3 %collective-permute-start.14 = (bf16[16,2432]{1,0:T(8,128)(2,1)S(1)}, bf16[16,2432]{1,0:T(8,128)(2,1)S(1)}, u32[]{:S(2)}, u32[]{:S(2)}) collective-permute-start(bf16[16,2432]{1,0:T(8,128)(2,1)S(1)} %get-tuple-element.64), channel_id=1, source_target_pairs={{0,6},{2,8},{4,10},{6,12},{8,14},{10,0},{12,2},{14,4},{1,7},{3,9},... | collective-permute-start | bytes 233480 | tf_op jit(solution)/shard_map/ppermute | solution.py:127
  42.8 11.7 %collective-permute-start.15 = (bf16[16,2432]{1,0:T(8,128)(2,1)S(1)}, bf16[16,2432]{1,0:T(8,128)(2,1)S(1)}, u32[]{:S(2)}, u32[]{:S(2)}) collective-permute-start(bf16[16,2432]{1,0:T(8,128)(2,1)S(1)} %get-tuple-element.65), channel_id=1, source_target_pairs={{0,4},{2,6},{4,8},{6,10},{8,12},{10,14},{12,0},{14,2},{1,5},{3,7},... | collective-permute-start | bytes 233480 | tf_op jit(solution)/shard_map/ppermute | solution.py:127
  44.4 10.2 %collective-permute-start.16 = (bf16[16,2432]{1,0:T(8,128)(2,1)S(1)}, bf16[16,2432]{1,0:T(8,128)(2,1)S(1)}, u32[]{:S(2)}, u32[]{:S(2)}) collective-permute-start(bf16[16,2432]{1,0:T(8,128)(2,1)S(1)} %get-tuple-element.59), channel_id=1, source_target_pairs={{0,2},{2,4},{4,6},{6,8},{8,10},{10,12},{12,14},{14,0},{1,3},{3,5},... | collective-permute-start | bytes 233480 | tf_op jit(solution)/shard_map/ppermute | solution.py:127
  54.9 7.4 %collective-permute-start.17 = (bf16[16,2432]{1,0:T(8,128)(2,1)S(1)}, bf16[16,2432]{1,0:T(8,128)(2,1)S(1)}, u32[]{:S(2)}, u32[]{:S(2)}) collective-permute-start(bf16[16,2432]{1,0:T(8,128)(2,1)S(1)} %get-tuple-element.55), channel_id=1, source_target_pairs={{0,2},{2,4},{4,6},{6,8},{8,10},{10,12},{12,14},{14,0},{1,3},{3,5},... | collective-permute-start | bytes 233480 | tf_op jit(solution)/shard_map/ppermute | solution.py:127
  54.9 19.9 %collective-permute-start.23 = (bf16[16,2432]{1,0:T(8,128)(2,1)S(1)}, bf16[16,2432]{1,0:T(8,128)(2,1)S(1)}, u32[]{:S(2)}, u32[]{:S(2)}) collective-permute-start(bf16[16,2432]{1,0:T(8,128)(2,1)S(1)} %get-tuple-element.35), channel_id=1, source_target_pairs={{0,14},{2,0},{4,2},{6,4},{8,6},{10,8},{12,10},{14,12},{1,15},{3,1}... | collective-permute-start | bytes 233480 | tf_op jit(solution)/shard_map/ppermute | solution.py:127
  59.7 15.2 %collective-permute-start.22 = (bf16[16,2432]{1,0:T(8,128)(2,1)S(1)}, bf16[16,2432]{1,0:T(8,128)(2,1)S(1)}, u32[]{:S(2)}, u32[]{:S(2)}) collective-permute-start(bf16[16,2432]{1,0:T(8,128)(2,1)S(1)} %get-tuple-element.32), channel_id=1, source_target_pairs={{0,12},{2,14},{4,0},{6,2},{8,4},{10,6},{12,8},{14,10},{1,13},{3,15... | collective-permute-start | bytes 233480 | tf_op jit(solution)/shard_map/ppermute | solution.py:127
  59.7 15.2 %collective-permute-start.21 = (bf16[16,2432]{1,0:T(8,128)(2,1)S(1)}, bf16[16,2432]{1,0:T(8,128)(2,1)S(1)}, u32[]{:S(2)}, u32[]{:S(2)}) collective-permute-start(bf16[16,2432]{1,0:T(8,128)(2,1)S(1)} %get-tuple-element.29), channel_id=1, source_target_pairs={{0,10},{2,12},{4,14},{6,0},{8,2},{10,4},{12,6},{14,8},{1,11},{3,13... | collective-permute-start | bytes 233480 | tf_op jit(solution)/shard_map/ppermute | solution.py:127
  59.7 7.2 %collective-permute-start.18 = (bf16[16,2432]{1,0:T(8,128)(2,1)S(1)}, bf16[16,2432]{1,0:T(8,128)(2,1)S(1)}, u32[]{:S(2)}, u32[]{:S(2)}) collective-permute-start(bf16[16,2432]{1,0:T(8,128)(2,1)S(1)} %get-tuple-element.54), channel_id=1, source_target_pairs={{0,4},{2,6},{4,8},{6,10},{8,12},{10,14},{12,0},{14,2},{1,5},{3,7},... | collective-permute-start | bytes 233480 | tf_op jit(solution)/shard_map/ppermute | solution.py:127
  62.3 10.0 %collective-permute-start.19 = (bf16[16,2432]{1,0:T(8,128)(2,1)S(1)}, bf16[16,2432]{1,0:T(8,128)(2,1)S(1)}, u32[]{:S(2)}, u32[]{:S(2)}) collective-permute-start(bf16[16,2432]{1,0:T(8,128)(2,1)S(1)} %get-tuple-element.53), channel_id=1, source_target_pairs={{0,6},{2,8},{4,10},{6,12},{8,14},{10,0},{12,2},{14,4},{1,7},{3,9},... | collective-permute-start | bytes 233480 | tf_op jit(solution)/shard_map/ppermute | solution.py:127
  66.9 7.9 %collective-permute-start.20 = (bf16[16,2432]{1,0:T(8,128)(2,1)S(1)}, bf16[16,2432]{1,0:T(8,128)(2,1)S(1)}, u32[]{:S(2)}, u32[]{:S(2)}) collective-permute-start(bf16[16,2432]{1,0:T(8,128)(2,1)S(1)} %get-tuple-element.52), channel_id=1, source_target_pairs={{0,8},{2,10},{4,12},{6,14},{8,0},{10,2},{12,4},{14,6},{1,9},{3,11}... | collective-permute-start | bytes 233480 | tf_op jit(solution)/shard_map/ppermute | solution.py:127
  76.2 23.1 %collective-permute-start.33 = (bf16[16,2304]{1,0:T(8,128)(2,1)S(1)}, bf16[16,2304]{1,0:T(8,128)(2,1)S(1)}, u32[]{:S(2)}, u32[]{:S(2)}) collective-permute-start(bf16[16,2304]{1,0:T(8,128)(2,1)S(1)} %add_convert_fusion.1), channel_id=1, source_target_pairs={{0,1},{1,0},{2,3},{3,2},{4,5},{5,4},{6,7},{7,6},{8,9},{9,8},{10,11... | collective-permute-start | bytes 221192 | tf_op jit(solution)/shard_map/ppermute | solution.py:116
  78.3 7.0 %collective-permute-start.25 = (bf16[16,2432]{1,0:T(8,128)(2,1)S(1)}, bf16[16,2432]{1,0:T(8,128)(2,1)S(1)}, u32[]{:S(2)}, u32[]{:S(2)}) collective-permute-start(bf16[16,2432]{1,0:T(8,128)(2,1)S(1)} %get-tuple-element.45), channel_id=1, source_target_pairs={{0,14},{2,0},{4,2},{6,4},{8,6},{10,8},{12,10},{14,12},{1,15},{3,1}... | collective-permute-start | bytes 233480 | tf_op jit(solution)/shard_map/ppermute | solution.py:127
  78.6 6.7 %collective-permute-start.26 = (bf16[16,2432]{1,0:T(8,128)(2,1)S(1)}, bf16[16,2432]{1,0:T(8,128)(2,1)S(1)}, u32[]{:S(2)}, u32[]{:S(2)}) collective-permute-start(bf16[16,2432]{1,0:T(8,128)(2,1)S(1)} %get-tuple-element.46), channel_id=1, source_target_pairs={{0,12},{2,14},{4,0},{6,2},{8,4},{10,6},{12,8},{14,10},{1,13},{3,15... | collective-permute-start | bytes 233480 | tf_op jit(solution)/shard_map/ppermute | solution.py:127
  82.1 5.7 %collective-permute-start.27 = (bf16[16,2432]{1,0:T(8,128)(2,1)S(1)}, bf16[16,2432]{1,0:T(8,128)(2,1)S(1)}, u32[]{:S(2)}, u32[]{:S(2)}) collective-permute-start(bf16[16,2432]{1,0:T(8,128)(2,1)S(1)} %get-tuple-element.47), channel_id=1, source_target_pairs={{0,10},{2,12},{4,14},{6,0},{8,2},{10,4},{12,6},{14,8},{1,11},{3,13... | collective-permute-start | bytes 233480 | tf_op jit(solution)/shard_map/ppermute | solution.py:127
  82.1 13.8 %collective-permute-start.28 = (bf16[16,2432]{1,0:T(8,128)(2,1)S(1)}, bf16[16,2432]{1,0:T(8,128)(2,1)S(1)}, u32[]{:S(2)}, u32[]{:S(2)}) collective-permute-start(bf16[16,2432]{1,0:T(8,128)(2,1)S(1)} %get-tuple-element.48), channel_id=1, source_target_pairs={{0,8},{2,10},{4,12},{6,14},{8,0},{10,2},{12,4},{14,6},{1,9},{3,11}... | collective-permute-start | bytes 233480 | tf_op jit(solution)/shard_map/ppermute | solution.py:127
  85.3 10.7 %collective-permute-start.29 = (bf16[16,2432]{1,0:T(8,128)(2,1)S(1)}, bf16[16,2432]{1,0:T(8,128)(2,1)S(1)}, u32[]{:S(2)}, u32[]{:S(2)}) collective-permute-start(bf16[16,2432]{1,0:T(8,128)(2,1)S(1)} %get-tuple-element.49), channel_id=1, source_target_pairs={{0,6},{2,8},{4,10},{6,12},{8,14},{10,0},{12,2},{14,4},{1,7},{3,9},... | collective-permute-start | bytes 233480 | tf_op jit(solution)/shard_map/ppermute | solution.py:127
  85.3 10.7 %collective-permute-start.30 = (bf16[16,2432]{1,0:T(8,128)(2,1)S(1)}, bf16[16,2432]{1,0:T(8,128)(2,1)S(1)}, u32[]{:S(2)}, u32[]{:S(2)}) collective-permute-start(bf16[16,2432]{1,0:T(8,128)(2,1)S(1)} %get-tuple-element.50), channel_id=1, source_target_pairs={{0,4},{2,6},{4,8},{6,10},{8,12},{10,14},{12,0},{14,2},{1,5},{3,7},... | collective-permute-start | bytes 233480 | tf_op jit(solution)/shard_map/ppermute | solution.py:127
  87.9 10.1 %collective-permute-start.31 = (bf16[16,2432]{1,0:T(8,128)(2,1)S(1)}, bf16[16,2432]{1,0:T(8,128)(2,1)S(1)}, u32[]{:S(2)}, u32[]{:S(2)}) collective-permute-start(bf16[16,2432]{1,0:T(8,128)(2,1)S(1)} %get-tuple-element.44), channel_id=1, source_target_pairs={{0,2},{2,4},{4,6},{6,8},{8,10},{10,12},{12,14},{14,0},{1,3},{3,5},... | collective-permute-start | bytes 233480 | tf_op jit(solution)/shard_map/ppermute | solution.py:127
  (9 other events, 25.3 us)

commit v7 on v5

--- a/solution.py
+++ b/solution.py
@@ -190,22 +190,17 @@
     theirs = (1 - here) * half
     small = jnp.concatenate([gain[0], inv_rms[0]], axis=0)
     other_small = swap_cores(small)
-    sent_w = jnp.concatenate(
-        [
-            lax.dynamic_slice_in_dim(decoder[0], theirs, half, axis=1),
-            lax.dynamic_slice_in_dim(encoder[0], theirs, half, axis=1),
-        ],
-        axis=0,
-    )
-    other_w = swap_cores(sent_w)
-    other = (other_w[:blocks], other_w[blocks:])
+    other = (
+        swap_cores(lax.dynamic_slice_in_dim(decoder[0], theirs, half, axis=1)),
+        swap_cores(lax.dynamic_slice_in_dim(encoder[0], theirs, half, axis=1)),
+    )
     own = (
         lax.dynamic_slice_in_dim(decoder[0], mine, half, axis=1),
         lax.dynamic_slice_in_dim(encoder[0], mine, half, axis=1),
     )
     attr_keep = jnp.zeros((rows, acts.shape[2]), jnp.float32)
     grad_keep = jnp.zeros(cotangent.shape, jnp.bfloat16)
-    g_half = lax.dynamic_slice_in_dim(cotangent, mine, half, axis=1)
+    g_half = jnp.where(here == 0, cotangent[:, :half], cotangent[:, half:])
     for layer in reversed(range(depth)):
         is_own = here == layer
         s = jnp.where(is_own, small, other_small)

time: 94.1 us -> 104 us (1.11); the launches traced: 93.6 us -> 102 us
  waiting for transfers between devices: 20 us -> 34 us
  starting transfers between devices: 54.6 us -> 47.7 us
    ppermute x28, waiting for transfers between devices: 16.4 us -> 31.7 us  [exchange(): moved.append(lax.ppermute(parts[shift], 'dict', route))]
    ppermute x28, starting transfers between devices: 53.2 us -> 45.9 us  [exchange(): moved.append(lax.ppermute(parts[shift], 'dict', route))]
    concatenate x1 -> x0, other arithmetic: 1.58 us -> none  [split_device(): jnp.concatenate([lax.dynamic_slice_in_dim(decoder[0], theirs, half, axis=...]
    unnamed x38 -> x36, local copies, waits for them, and re-layouts: 4.79 us -> 3.26 us
    dynamic_slice x1, local copies, waits for them, and re-layouts: 0.9 us -> 2.39 us  [split_device(): lax.dynamic_slice_in_dim(decoder[0], theirs, half, axis=1)]
    ppermute x6 -> x7, waiting for transfers between devices: 3.57 us -> 2.35 us  [swap_cores(): return lax.ppermute(block, 'section', [(0, 1), (1, 0)])]
  transfers between devices with their start and end apart: 34 -> 35, of which waited for: 12 -> 17; matrix products, arithmetic and copies ran while one was open for 12% -> 14% of each run, Pallas kernels for 0% -> 0%
where the time goes in v7:
time: 104 us; the launch traced here: 102 us
  starting transfers between devices  47.7 us (46%)
  waiting for transfers between devices  34 us (33%)
  local copies, waits for them, and re-layouts  8.76 us (8%)
  other arithmetic  6.17 us (6%)
  matrix products  4.2 us (4%)
  between operations  1.08 us (1%)
    ppermute x28, starting transfers between devices, exchange(): moved.append(lax.ppermute(parts[shift], 'dict', route))  45.9 us
    ppermute x28, waiting for transfers between devices, exchange(): moved.append(lax.ppermute(parts[shift], 'dict', route))  31.7 us
    unnamed x36, local copies, waits for them, and re-layouts  3.26 us
    dynamic_slice x1, local copies, waits for them, and re-layouts, split_device(): lax.dynamic_slice_in_dim(decoder[0], theirs, half, axis=1)  2.39 us
    ppermute x7, waiting for transfers between devices, swap_cores(): return lax.ppermute(block, 'section', [(0, 1), (1, 0)])  2.35 us
    dot_general x4, matrix products, with_dec(): lax.dot_general(g_all, dec, (((1,), (1,)), ((), ())), preferred_element_t...  2.17 us
  transfers between devices with their start and end apart: 35, of which 17 were waited for; matrix products, arithmetic and copies ran while one was open for 14% of the time, Pallas kernels for 0%

profile of v7, /device:TPU:0, one launch (start us, length us, event | category | flops | bytes accessed | tf_op | source)
XLA Modules:
  0.0 102.0 jit_solution(8418140679885581606)
XLA Ops:
  0.6 0.9 reduce
  4.7 0.9 slice_select_fusion
  6.4 5.5 %collective-permute-start.7 = (bf16[16,2432]{1,0:T(8,128)(2,1)S(1)}, bf16[16,2432]{1,0:T(8,128)(2,1)}, u32[]{:S(2)}, u32[]{:S(2)}) collective-permute-start(bf16[16,2432]{1,0:T(8,128)(2,1)S(1)} %get-tuple-element.28), channel_id=1, source_target_pairs={{0,14},{2,0},{4,2},{6,4},{8,6},{10,8},{12,10},{14,12},{1,15},{3,1}... | collective-permute-start | bytes 233480 | tf_op jit(solution)/shard_map/ppermute | solution.py:124
  11.9 1.9 %collective-permute-start.1 = (bf16[16,2432]{1,0:T(8,128)(2,1)}, bf16[16,2432]{1,0:T(8,128)(2,1)}, u32[]{:S(2)}, u32[]{:S(2)}) collective-permute-start(bf16[16,2432]{1,0:T(8,128)(2,1)} %get-tuple-element.31), channel_id=1, source_target_pairs={{0,2},{2,4},{4,6},{6,8},{8,10},{10,12},{12,14},{14,0},{1,3},{3,5},... | collective-permute-start | bytes 233480 | tf_op jit(solution)/shard_map/ppermute | solution.py:124
  13.8 1.6 %collective-permute-start.2 = (bf16[16,2432]{1,0:T(8,128)(2,1)S(1)}, bf16[16,2432]{1,0:T(8,128)(2,1)}, u32[]{:S(2)}, u32[]{:S(2)}) collective-permute-start(bf16[16,2432]{1,0:T(8,128)(2,1)S(1)} %get-tuple-element.32), channel_id=1, source_target_pairs={{0,4},{2,6},{4,8},{6,10},{8,12},{10,14},{12,0},{14,2},{1,5},{3,7},... | collective-permute-start | bytes 233480 | tf_op jit(solution)/shard_map/ppermute | solution.py:124
  15.4 2.4 %dynamic-slice_bitcast_fusion.1 = bf16[256,2304]{1,0:T(8,128)(2,1)} fusion(bf16[1,256,4608]{2,1,0:T(8,128)(2,1)} %param.10, s32[]{:T(128)S(6)} %select_n.202), kind=kLoop, calls=%fused_computation.48 | loop fusion | bytes 2359300 | tf_op jit(solution)/shard_map/dynamic_slice | solution.py:194
  17.8 1.1 %dynamic-slice_bitcast_fusion = bf16[256,2304]{1,0:T(8,128)(2,1)} fusion(bf16[1,256,4608]{2,1,0:T(8,128)(2,1)S(1)} %copy-done, s32[]{:T(128)S(6)} %select_n.202), kind=kLoop, calls=%fused_computation.47 | loop fusion | bytes 2359300 | tf_op jit(solution)/shard_map/dynamic_slice | solution.py:195
  18.9 1.2 %collective-permute-done.1 = bf16[16,2432]{1,0:T(8,128)(2,1)} collective-permute-done((bf16[16,2432]{1,0:T(8,128)(2,1)}, bf16[16,2432]{1,0:T(8,128)(2,1)}, u32[]{:S(2)}, u32[]{:S(2)}) %collective-permute-start.1) | collective-permute-done | bytes 77856 | tf_op jit(solution)/shard_map/ppermute | solution.py:124
  21.0 1.7 %collective-permute-start.4 = (bf16[16,2432]{1,0:T(8,128)(2,1)S(1)}, bf16[16,2432]{1,0:T(8,128)(2,1)S(1)}, u32[]{:S(2)}, u32[]{:S(2)}) collective-permute-start(bf16[16,2432]{1,0:T(8,128)(2,1)S(1)} %get-tuple-element.34), channel_id=1, source_target_pairs={{0,8},{2,10},{4,12},{6,14},{8,0},{10,2},{12,4},{14,6},{1,9},{3,11}... | collective-permute-start | bytes 233480 | tf_op jit(solution)/shard_map/ppermute | solution.py:124
  23.6 5.5 %collective-permute-done.3 = bf16[16,2432]{1,0:T(8,128)(2,1)S(1)} collective-permute-done((bf16[16,2432]{1,0:T(8,128)(2,1)S(1)}, bf16[16,2432]{1,0:T(8,128)(2,1)S(1)}, u32[]{:S(2)}, u32[]{:S(2)}) %collective-permute-start.3) | collective-permute-done | bytes 77856 | tf_op jit(solution)/shard_map/ppermute | solution.py:124
  30.6 1.0 %bitcast_dynamic-update-slice_fusion.25 = bf16[8,16,2432]{2,1,0:T(8,128)(2,1)S(1)} fusion(bf16[8,16,2432]{2,1,0:T(8,128)(2,1)S(1)} %bitcast_dynamic-update-slice_fusion.26, bf16[16,2432]{1,0:T(8,128)(2,1)} %collective-permute-done.5), kind=kLoop, calls=%fused_computation.168 | loop fusion | bytes 155648
  31.6 1.9 %collective-permute-done.6 = bf16[16,2432]{1,0:T(8,128)(2,1)S(1)} collective-permute-done((bf16[16,2432]{1,0:T(8,128)(2,1)S(1)}, bf16[16,2432]{1,0:T(8,128)(2,1)S(1)}, u32[]{:S(2)}, u32[]{:S(2)}) %collective-permute-start.6) | collective-permute-done | bytes 77856 | tf_op jit(solution)/shard_map/ppermute | solution.py:124
  33.6 0.9 bitcast_dynamic-update-slice_fusion.23
  36.2 1.2 %collective-permute-done.9 = f32[128,384]{1,0:T(8,128)S(1)} collective-permute-done((f32[128,384]{1,0:T(8,128)S(1)}, f32[128,384]{1,0:T(8,128)S(1)}, u32[]{:S(2)}, u32[]{:S(2)}) %collective-permute-start.9) | collective-permute-done | bytes 196640 | tf_op jit(solution)/shard_map/ppermute | solution.py:116
  38.2 3.3 %collective-permute-start.11 = (bf16[16,2432]{1,0:T(8,128)(2,1)S(1)}, bf16[16,2432]{1,0:T(8,128)(2,1)S(1)}, u32[]{:S(2)}, u32[]{:S(2)}) collective-permute-start(bf16[16,2432]{1,0:T(8,128)(2,1)S(1)} %get-tuple-element.22), channel_id=1, source_target_pairs={{0,14},{2,0},{4,2},{6,4},{8,6},{10,8},{12,10},{14,12},{1,15},{3,1}... | collective-permute-start | bytes 233480 | tf_op jit(solution)/shard_map/ppermute | solution.py:124
  41.6 1.1 %collective-permute-start.12 = (bf16[16,2432]{1,0:T(8,128)(2,1)S(1)}, bf16[16,2432]{1,0:T(8,128)(2,1)S(1)}, u32[]{:S(2)}, u32[]{:S(2)}) collective-permute-start(bf16[16,2432]{1,0:T(8,128)(2,1)S(1)} %get-tuple-element.23), channel_id=1, source_target_pairs={{0,12},{2,14},{4,0},{6,2},{8,4},{10,6},{12,8},{14,10},{1,13},{3,15... | collective-permute-start | bytes 233480 | tf_op jit(solution)/shard_map/ppermute | solution.py:124
  43.1 6.1 %collective-permute-start.14 = (bf16[16,2432]{1,0:T(8,128)(2,1)S(1)}, bf16[16,2432]{1,0:T(8,128)(2,1)S(1)}, u32[]{:S(2)}, u32[]{:S(2)}) collective-permute-start(bf16[16,2432]{1,0:T(8,128)(2,1)S(1)} %get-tuple-element.25), channel_id=1, source_target_pairs={{0,8},{2,10},{4,12},{6,14},{8,0},{10,2},{12,4},{14,6},{1,9},{3,11}... | collective-permute-start | bytes 233480 | tf_op jit(solution)/shard_map/ppermute | solution.py:124
  50.4 7.0 %collective-permute-done.14 = bf16[16,2432]{1,0:T(8,128)(2,1)S(1)} collective-permute-done((bf16[16,2432]{1,0:T(8,128)(2,1)S(1)}, bf16[16,2432]{1,0:T(8,128)(2,1)S(1)}, u32[]{:S(2)}, u32[]{:S(2)}) %collective-permute-start.14) | collective-permute-done | bytes 77856 | tf_op jit(solution)/shard_map/ppermute | solution.py:124
  58.6 4.7 %collective-permute-start.24 = (bf16[16,2432]{1,0:T(8,128)(2,1)S(1)}, bf16[16,2432]{1,0:T(8,128)(2,1)S(1)}, u32[]{:S(2)}, u32[]{:S(2)}) collective-permute-start(bf16[16,2432]{1,0:T(8,128)(2,1)S(1)} %get-tuple-element.13), channel_id=1, source_target_pairs={{0,14},{2,0},{4,2},{6,4},{8,6},{10,8},{12,10},{14,12},{1,15},{3,1}... | collective-permute-start | bytes 233480 | tf_op jit(solution)/shard_map/ppermute | solution.py:124
  64.1 2.5 %collective-permute-done.18 = bf16[16,2432]{1,0:T(8,128)(2,1)S(1)} collective-permute-done((bf16[16,2432]{1,0:T(8,128)(2,1)S(1)}, bf16[16,2432]{1,0:T(8,128)(2,1)S(1)}, u32[]{:S(2)}, u32[]{:S(2)}) %collective-permute-start.18) | collective-permute-done | bytes 77856 | tf_op jit(solution)/shard_map/ppermute | solution.py:124
  66.6 1.3 %collective-permute-start.22 = (bf16[16,2432]{1,0:T(8,128)(2,1)S(1)}, bf16[16,2432]{1,0:T(8,128)(2,1)S(1)}, u32[]{:S(2)}, u32[]{:S(2)}) collective-permute-start(bf16[16,2432]{1,0:T(8,128)(2,1)S(1)} %get-tuple-element.18), channel_id=1, source_target_pairs={{0,10},{2,12},{4,14},{6,0},{8,2},{10,4},{12,6},{14,8},{1,11},{3,13... | collective-permute-start | bytes 233480 | tf_op jit(solution)/shard_map/ppermute | solution.py:124
  67.9 3.0 %collective-permute-done.19 = bf16[16,2432]{1,0:T(8,128)(2,1)S(1)} collective-permute-done((bf16[16,2432]{1,0:T(8,128)(2,1)S(1)}, bf16[16,2432]{1,0:T(8,128)(2,1)S(1)}, u32[]{:S(2)}, u32[]{:S(2)}) %collective-permute-start.19) | collective-permute-done | bytes 77856 | tf_op jit(solution)/shard_map/ppermute | solution.py:124
  70.9 2.2 %collective-permute-start.23 = (bf16[16,2432]{1,0:T(8,128)(2,1)S(1)}, bf16[16,2432]{1,0:T(8,128)(2,1)S(1)}, u32[]{:S(2)}, u32[]{:S(2)}) collective-permute-start(bf16[16,2432]{1,0:T(8,128)(2,1)S(1)} %get-tuple-element.19), channel_id=1, source_target_pairs={{0,12},{2,14},{4,0},{6,2},{8,4},{10,6},{12,8},{14,10},{1,13},{3,15... | collective-permute-start | bytes 233480 | tf_op jit(solution)/shard_map/ppermute | solution.py:124
  74.2 1.8 %collective-permute-done.23 = bf16[16,2432]{1,0:T(8,128)(2,1)S(1)} collective-permute-done((bf16[16,2432]{1,0:T(8,128)(2,1)S(1)}, bf16[16,2432]{1,0:T(8,128)(2,1)S(1)}, u32[]{:S(2)}, u32[]{:S(2)}) %collective-permute-start.23) | collective-permute-done | bytes 77856 | tf_op jit(solution)/shard_map/ppermute | solution.py:124
  79.4 3.9 %collective-permute-start.26 = (bf16[16,2432]{1,0:T(8,128)(2,1)S(1)}, bf16[16,2432]{1,0:T(8,128)(2,1)S(1)}, u32[]{:S(2)}, u32[]{:S(2)}) collective-permute-start(bf16[16,2432]{1,0:T(8,128)(2,1)S(1)} %get-tuple-element.7), channel_id=1, source_target_pairs={{0,14},{2,0},{4,2},{6,4},{8,6},{10,8},{12,10},{14,12},{1,15},{3,1}... | collective-permute-start | bytes 233480 | tf_op jit(solution)/shard_map/ppermute | solution.py:124
  83.4 1.8 %collective-permute-start.27 = (bf16[16,2432]{1,0:T(8,128)(2,1)S(1)}, bf16[16,2432]{1,0:T(8,128)(2,1)S(1)}, u32[]{:S(2)}, u32[]{:S(2)}) collective-permute-start(bf16[16,2432]{1,0:T(8,128)(2,1)S(1)} %get-tuple-element.8), channel_id=1, source_target_pairs={{0,12},{2,14},{4,0},{6,2},{8,4},{10,6},{12,8},{14,10},{1,13},{3,15... | collective-permute-start | bytes 233480 | tf_op jit(solution)/shard_map/ppermute | solution.py:124
  85.2 1.4 %collective-permute-start.28 = (bf16[16,2432]{1,0:T(8,128)(2,1)S(1)}, bf16[16,2432]{1,0:T(8,128)(2,1)S(1)}, u32[]{:S(2)}, u32[]{:S(2)}) collective-permute-start(bf16[16,2432]{1,0:T(8,128)(2,1)S(1)} %get-tuple-element.9), channel_id=1, source_target_pairs={{0,10},{2,12},{4,14},{6,0},{8,2},{10,4},{12,6},{14,8},{1,11},{3,13... | collective-permute-start | bytes 233480 | tf_op jit(solution)/shard_map/ppermute | solution.py:124
  86.6 4.4 %collective-permute-start.29 = (bf16[16,2432]{1,0:T(8,128)(2,1)S(1)}, bf16[16,2432]{1,0:T(8,128)(2,1)S(1)}, u32[]{:S(2)}, u32[]{:S(2)}) collective-permute-start(bf16[16,2432]{1,0:T(8,128)(2,1)S(1)} %get-tuple-element.10), channel_id=1, source_target_pairs={{0,8},{2,10},{4,12},{6,14},{8,0},{10,2},{12,4},{14,6},{1,9},{3,11}... | collective-permute-start | bytes 233480 | tf_op jit(solution)/shard_map/ppermute | solution.py:124
  91.1 1.0 collective-permute-start.30
  92.1 0.9 collective-permute-done.28
  93.0 1.2 %collective-permute-start.31 = (bf16[16,2432]{1,0:T(8,128)(2,1)S(1)}, bf16[16,2432]{1,0:T(8,128)(2,1)S(1)}, u32[]{:S(2)}, u32[]{:S(2)}) collective-permute-start(bf16[16,2432]{1,0:T(8,128)(2,1)S(1)} %get-tuple-element.12), channel_id=1, source_target_pairs={{0,4},{2,6},{4,8},{6,10},{8,12},{10,14},{12,0},{14,2},{1,5},{3,7},... | collective-permute-start | bytes 233480 | tf_op jit(solution)/shard_map/ppermute | solution.py:124
  94.2 5.4 %collective-permute-done.29 = bf16[16,2432]{1,0:T(8,128)(2,1)S(1)} collective-permute-done((bf16[16,2432]{1,0:T(8,128)(2,1)S(1)}, bf16[16,2432]{1,0:T(8,128)(2,1)S(1)}, u32[]{:S(2)}, u32[]{:S(2)}) %collective-permute-start.29) | collective-permute-done | bytes 77856 | tf_op jit(solution)/shard_map/ppermute | solution.py:124
  (132 shorter events, 20.0 us)
Async XLA Ops:
  2.2 33.9 %collective-permute-start = (f32[4624]{0:T(1024)S(1)}, f32[4624]{0:T(1024)S(1)}, u32[]{:S(2)}, u32[]{:S(2)}) collective-permute-start(f32[4624]{0:T(1024)S(1)} %pad_maximum_fusion.6), channel_id=1, source_target_pairs={{0,1},{1,0},{2,3},{3,2},{4,5},{5,4},{6,7},{7,6},{8,9},{9,8},{10,11... | collective-permute-start | bytes 55496 | tf_op jit(solution)/shard_map/ppermute | solution.py:116
  6.4 27.2 %collective-permute-start.7 = (bf16[16,2432]{1,0:T(8,128)(2,1)S(1)}, bf16[16,2432]{1,0:T(8,128)(2,1)}, u32[]{:S(2)}, u32[]{:S(2)}) collective-permute-start(bf16[16,2432]{1,0:T(8,128)(2,1)S(1)} %get-tuple-element.28), channel_id=1, source_target_pairs={{0,14},{2,0},{4,2},{6,4},{8,6},{10,8},{12,10},{14,12},{1,15},{3,1}... | collective-permute-start | bytes 233480 | tf_op jit(solution)/shard_map/ppermute | solution.py:124
  11.9 18.1 %collective-permute-start.5 = (bf16[16,2432]{1,0:T(8,128)(2,1)S(1)}, bf16[16,2432]{1,0:T(8,128)(2,1)}, u32[]{:S(2)}, u32[]{:S(2)}) collective-permute-start(bf16[16,2432]{1,0:T(8,128)(2,1)S(1)} %get-tuple-element.29), channel_id=1, source_target_pairs={{0,10},{2,12},{4,14},{6,0},{8,2},{10,4},{12,6},{14,8},{1,11},{3,13... | collective-permute-start | bytes 233480 | tf_op jit(solution)/shard_map/ppermute | solution.py:124
  11.9 8.2 %collective-permute-start.1 = (bf16[16,2432]{1,0:T(8,128)(2,1)}, bf16[16,2432]{1,0:T(8,128)(2,1)}, u32[]{:S(2)}, u32[]{:S(2)}) collective-permute-start(bf16[16,2432]{1,0:T(8,128)(2,1)} %get-tuple-element.31), channel_id=1, source_target_pairs={{0,2},{2,4},{4,6},{6,8},{8,10},{10,12},{12,14},{14,0},{1,3},{3,5},... | collective-permute-start | bytes 233480 | tf_op jit(solution)/shard_map/ppermute | solution.py:124
  13.8 7.2 %collective-permute-start.2 = (bf16[16,2432]{1,0:T(8,128)(2,1)S(1)}, bf16[16,2432]{1,0:T(8,128)(2,1)}, u32[]{:S(2)}, u32[]{:S(2)}) collective-permute-start(bf16[16,2432]{1,0:T(8,128)(2,1)S(1)} %get-tuple-element.32), channel_id=1, source_target_pairs={{0,4},{2,6},{4,8},{6,10},{8,12},{10,14},{12,0},{14,2},{1,5},{3,7},... | collective-permute-start | bytes 233480 | tf_op jit(solution)/shard_map/ppermute | solution.py:124
  20.1 9.1 %collective-permute-start.3 = (bf16[16,2432]{1,0:T(8,128)(2,1)S(1)}, bf16[16,2432]{1,0:T(8,128)(2,1)S(1)}, u32[]{:S(2)}, u32[]{:S(2)}) collective-permute-start(bf16[16,2432]{1,0:T(8,128)(2,1)S(1)} %get-tuple-element.33), channel_id=1, source_target_pairs={{0,6},{2,8},{4,10},{6,12},{8,14},{10,0},{12,2},{14,4},{1,7},{3,9},... | collective-permute-start | bytes 233480 | tf_op jit(solution)/shard_map/ppermute | solution.py:124
  21.0 8.9 %collective-permute-start.4 = (bf16[16,2432]{1,0:T(8,128)(2,1)S(1)}, bf16[16,2432]{1,0:T(8,128)(2,1)S(1)}, u32[]{:S(2)}, u32[]{:S(2)}) collective-permute-start(bf16[16,2432]{1,0:T(8,128)(2,1)S(1)} %get-tuple-element.34), channel_id=1, source_target_pairs={{0,8},{2,10},{4,12},{6,14},{8,0},{10,2},{12,4},{14,6},{1,9},{3,11}... | collective-permute-start | bytes 233480 | tf_op jit(solution)/shard_map/ppermute | solution.py:124
  29.2 4.4 %collective-permute-start.6 = (bf16[16,2432]{1,0:T(8,128)(2,1)S(1)}, bf16[16,2432]{1,0:T(8,128)(2,1)S(1)}, u32[]{:S(2)}, u32[]{:S(2)}) collective-permute-start(bf16[16,2432]{1,0:T(8,128)(2,1)S(1)} %get-tuple-element.35), channel_id=1, source_target_pairs={{0,12},{2,14},{4,0},{6,2},{8,4},{10,6},{12,8},{14,10},{1,13},{3,15... | collective-permute-start | bytes 233480 | tf_op jit(solution)/shard_map/ppermute | solution.py:124
  29.9 7.5 %collective-permute-start.10 = (bf16[256,2304]{1,0:T(8,128)(2,1)}, bf16[256,2304]{1,0:T(8,128)(2,1)S(1)}, u32[]{:S(2)}, u32[]{:S(2)}) collective-permute-start(bf16[256,2304]{1,0:T(8,128)(2,1)} %dynamic-slice_bitcast_fusion), channel_id=1, source_target_pairs={{0,1},{1,0},{2,3},{3,2},{4,5},{5,4},{6,7},{7,6},{8,9},{9,8},{10,11... | collective-permute-start | bytes 3538952 | tf_op jit(solution)/shard_map/ppermute | solution.py:116
  30.0 4.7 %collective-permute-start.8 = (bf16[256,2304]{1,0:T(8,128)(2,1)}, bf16[256,2304]{1,0:T(8,128)(2,1)S(1)}, u32[]{:S(2)}, u32[]{:S(2)}) collective-permute-start(bf16[256,2304]{1,0:T(8,128)(2,1)} %dynamic-slice_bitcast_fusion.1), channel_id=1, source_target_pairs={{0,1},{1,0},{2,3},{3,2},{4,5},{5,4},{6,7},{7,6},{8,9},{9,8},{10,11... | collective-permute-start | bytes 3538952 | tf_op jit(solution)/shard_map/ppermute | solution.py:116
  38.2 11.0 %collective-permute-start.11 = (bf16[16,2432]{1,0:T(8,128)(2,1)S(1)}, bf16[16,2432]{1,0:T(8,128)(2,1)S(1)}, u32[]{:S(2)}, u32[]{:S(2)}) collective-permute-start(bf16[16,2432]{1,0:T(8,128)(2,1)S(1)} %get-tuple-element.22), channel_id=1, source_target_pairs={{0,14},{2,0},{4,2},{6,4},{8,6},{10,8},{12,10},{14,12},{1,15},{3,1}... | collective-permute-start | bytes 233480 | tf_op jit(solution)/shard_map/ppermute | solution.py:124
  41.6 16.6 %collective-permute-start.17 = (bf16[16,2432]{1,0:T(8,128)(2,1)S(1)}, bf16[16,2432]{1,0:T(8,128)(2,1)S(1)}, u32[]{:S(2)}, u32[]{:S(2)}) collective-permute-start(bf16[16,2432]{1,0:T(8,128)(2,1)S(1)} %get-tuple-element.21), channel_id=1, source_target_pairs={{0,2},{2,4},{4,6},{6,8},{8,10},{10,12},{12,14},{14,0},{1,3},{3,5},... | collective-permute-start | bytes 233480 | tf_op jit(solution)/shard_map/ppermute | solution.py:124
  41.6 7.7 %collective-permute-start.12 = (bf16[16,2432]{1,0:T(8,128)(2,1)S(1)}, bf16[16,2432]{1,0:T(8,128)(2,1)S(1)}, u32[]{:S(2)}, u32[]{:S(2)}) collective-permute-start(bf16[16,2432]{1,0:T(8,128)(2,1)S(1)} %get-tuple-element.23), channel_id=1, source_target_pairs={{0,12},{2,14},{4,0},{6,2},{8,4},{10,6},{12,8},{14,10},{1,13},{3,15... | collective-permute-start | bytes 233480 | tf_op jit(solution)/shard_map/ppermute | solution.py:124
  42.6 7.8 %collective-permute-start.13 = (bf16[16,2432]{1,0:T(8,128)(2,1)S(1)}, bf16[16,2432]{1,0:T(8,128)(2,1)S(1)}, u32[]{:S(2)}, u32[]{:S(2)}) collective-permute-start(bf16[16,2432]{1,0:T(8,128)(2,1)S(1)} %get-tuple-element.24), channel_id=1, source_target_pairs={{0,10},{2,12},{4,14},{6,0},{8,2},{10,4},{12,6},{14,8},{1,11},{3,13... | collective-permute-start | bytes 233480 | tf_op jit(solution)/shard_map/ppermute | solution.py:124
  43.1 14.3 %collective-permute-start.14 = (bf16[16,2432]{1,0:T(8,128)(2,1)S(1)}, bf16[16,2432]{1,0:T(8,128)(2,1)S(1)}, u32[]{:S(2)}, u32[]{:S(2)}) collective-permute-start(bf16[16,2432]{1,0:T(8,128)(2,1)S(1)} %get-tuple-element.25), channel_id=1, source_target_pairs={{0,8},{2,10},{4,12},{6,14},{8,0},{10,2},{12,4},{14,6},{1,9},{3,11}... | collective-permute-start | bytes 233480 | tf_op jit(solution)/shard_map/ppermute | solution.py:124
  49.2 9.0 %collective-permute-start.15 = (bf16[16,2432]{1,0:T(8,128)(2,1)S(1)}, bf16[16,2432]{1,0:T(8,128)(2,1)S(1)}, u32[]{:S(2)}, u32[]{:S(2)}) collective-permute-start(bf16[16,2432]{1,0:T(8,128)(2,1)S(1)} %get-tuple-element.26), channel_id=1, source_target_pairs={{0,6},{2,8},{4,10},{6,12},{8,14},{10,0},{12,2},{14,4},{1,7},{3,9},... | collective-permute-start | bytes 233480 | tf_op jit(solution)/shard_map/ppermute | solution.py:124
  49.2 8.9 %collective-permute-start.16 = (bf16[16,2432]{1,0:T(8,128)(2,1)S(1)}, bf16[16,2432]{1,0:T(8,128)(2,1)S(1)}, u32[]{:S(2)}, u32[]{:S(2)}) collective-permute-start(bf16[16,2432]{1,0:T(8,128)(2,1)S(1)} %get-tuple-element.27), channel_id=1, source_target_pairs={{0,4},{2,6},{4,8},{6,10},{8,12},{10,14},{12,0},{14,2},{1,5},{3,7},... | collective-permute-start | bytes 233480 | tf_op jit(solution)/shard_map/ppermute | solution.py:124
  58.5 8.1 %collective-permute-start.18 = (bf16[16,2432]{1,0:T(8,128)(2,1)S(1)}, bf16[16,2432]{1,0:T(8,128)(2,1)S(1)}, u32[]{:S(2)}, u32[]{:S(2)}) collective-permute-start(bf16[16,2432]{1,0:T(8,128)(2,1)S(1)} %get-tuple-element.17), channel_id=1, source_target_pairs={{0,2},{2,4},{4,6},{6,8},{8,10},{10,12},{12,14},{14,0},{1,3},{3,5},... | collective-permute-start | bytes 233480 | tf_op jit(solution)/shard_map/ppermute | solution.py:124
  58.6 17.4 %collective-permute-start.24 = (bf16[16,2432]{1,0:T(8,128)(2,1)S(1)}, bf16[16,2432]{1,0:T(8,128)(2,1)S(1)}, u32[]{:S(2)}, u32[]{:S(2)}) collective-permute-start(bf16[16,2432]{1,0:T(8,128)(2,1)S(1)} %get-tuple-element.13), channel_id=1, source_target_pairs={{0,14},{2,0},{4,2},{6,4},{8,6},{10,8},{12,10},{14,12},{1,15},{3,1}... | collective-permute-start | bytes 233480 | tf_op jit(solution)/shard_map/ppermute | solution.py:124
  63.3 10.6 %collective-permute-start.21 = (bf16[16,2432]{1,0:T(8,128)(2,1)S(1)}, bf16[16,2432]{1,0:T(8,128)(2,1)S(1)}, u32[]{:S(2)}, u32[]{:S(2)}) collective-permute-start(bf16[16,2432]{1,0:T(8,128)(2,1)S(1)} %get-tuple-element.14), channel_id=1, source_target_pairs={{0,8},{2,10},{4,12},{6,14},{8,0},{10,2},{12,4},{14,6},{1,9},{3,11}... | collective-permute-start | bytes 233480 | tf_op jit(solution)/shard_map/ppermute | solution.py:124
  63.3 10.5 %collective-permute-start.20 = (bf16[16,2432]{1,0:T(8,128)(2,1)S(1)}, bf16[16,2432]{1,0:T(8,128)(2,1)S(1)}, u32[]{:S(2)}, u32[]{:S(2)}) collective-permute-start(bf16[16,2432]{1,0:T(8,128)(2,1)S(1)} %get-tuple-element.15), channel_id=1, source_target_pairs={{0,6},{2,8},{4,10},{6,12},{8,14},{10,0},{12,2},{14,4},{1,7},{3,9},... | collective-permute-start | bytes 233480 | tf_op jit(solution)/shard_map/ppermute | solution.py:124
  63.9 7.0 %collective-permute-start.19 = (bf16[16,2432]{1,0:T(8,128)(2,1)S(1)}, bf16[16,2432]{1,0:T(8,128)(2,1)S(1)}, u32[]{:S(2)}, u32[]{:S(2)}) collective-permute-start(bf16[16,2432]{1,0:T(8,128)(2,1)S(1)} %get-tuple-element.16), channel_id=1, source_target_pairs={{0,4},{2,6},{4,8},{6,10},{8,12},{10,14},{12,0},{14,2},{1,5},{3,7},... | collective-permute-start | bytes 233480 | tf_op jit(solution)/shard_map/ppermute | solution.py:124
  66.6 7.6 %collective-permute-start.22 = (bf16[16,2432]{1,0:T(8,128)(2,1)S(1)}, bf16[16,2432]{1,0:T(8,128)(2,1)S(1)}, u32[]{:S(2)}, u32[]{:S(2)}) collective-permute-start(bf16[16,2432]{1,0:T(8,128)(2,1)S(1)} %get-tuple-element.18), channel_id=1, source_target_pairs={{0,10},{2,12},{4,14},{6,0},{8,2},{10,4},{12,6},{14,8},{1,11},{3,13... | collective-permute-start | bytes 233480 | tf_op jit(solution)/shard_map/ppermute | solution.py:124
  70.9 5.1 %collective-permute-start.23 = (bf16[16,2432]{1,0:T(8,128)(2,1)S(1)}, bf16[16,2432]{1,0:T(8,128)(2,1)S(1)}, u32[]{:S(2)}, u32[]{:S(2)}) collective-permute-start(bf16[16,2432]{1,0:T(8,128)(2,1)S(1)} %get-tuple-element.19), channel_id=1, source_target_pairs={{0,12},{2,14},{4,0},{6,2},{8,4},{10,6},{12,8},{14,10},{1,13},{3,15... | collective-permute-start | bytes 233480 | tf_op jit(solution)/shard_map/ppermute | solution.py:124
  77.4 23.6 %collective-permute-start.34 = (bf16[16,2304]{1,0:T(8,128)(2,1)S(1)}, bf16[16,2304]{1,0:T(8,128)(2,1)S(1)}, u32[]{:S(2)}, u32[]{:S(2)}) collective-permute-start(bf16[16,2304]{1,0:T(8,128)(2,1)S(1)} %add_convert_fusion.1), channel_id=1, source_target_pairs={{0,1},{1,0},{2,3},{3,2},{4,5},{5,4},{6,7},{7,6},{8,9},{9,8},{10,11... | collective-permute-start | bytes 221192 | tf_op jit(solution)/shard_map/ppermute | solution.py:116
  79.4 7.2 %collective-permute-start.26 = (bf16[16,2432]{1,0:T(8,128)(2,1)S(1)}, bf16[16,2432]{1,0:T(8,128)(2,1)S(1)}, u32[]{:S(2)}, u32[]{:S(2)}) collective-permute-start(bf16[16,2432]{1,0:T(8,128)(2,1)S(1)} %get-tuple-element.7), channel_id=1, source_target_pairs={{0,14},{2,0},{4,2},{6,4},{8,6},{10,8},{12,10},{14,12},{1,15},{3,1}... | collective-permute-start | bytes 233480 | tf_op jit(solution)/shard_map/ppermute | solution.py:124
  83.4 16.3 %collective-permute-start.32 = (bf16[16,2432]{1,0:T(8,128)(2,1)S(1)}, bf16[16,2432]{1,0:T(8,128)(2,1)S(1)}, u32[]{:S(2)}, u32[]{:S(2)}) collective-permute-start(bf16[16,2432]{1,0:T(8,128)(2,1)S(1)} %get-tuple-element.6), channel_id=1, source_target_pairs={{0,2},{2,4},{4,6},{6,8},{8,10},{10,12},{12,14},{14,0},{1,3},{3,5},... | collective-permute-start | bytes 233480 | tf_op jit(solution)/shard_map/ppermute | solution.py:124
  83.4 7.7 %collective-permute-start.27 = (bf16[16,2432]{1,0:T(8,128)(2,1)S(1)}, bf16[16,2432]{1,0:T(8,128)(2,1)S(1)}, u32[]{:S(2)}, u32[]{:S(2)}) collective-permute-start(bf16[16,2432]{1,0:T(8,128)(2,1)S(1)} %get-tuple-element.8), channel_id=1, source_target_pairs={{0,12},{2,14},{4,0},{6,2},{8,4},{10,6},{12,8},{14,10},{1,13},{3,15... | collective-permute-start | bytes 233480 | tf_op jit(solution)/shard_map/ppermute | solution.py:124
  85.2 7.8 %collective-permute-start.28 = (bf16[16,2432]{1,0:T(8,128)(2,1)S(1)}, bf16[16,2432]{1,0:T(8,128)(2,1)S(1)}, u32[]{:S(2)}, u32[]{:S(2)}) collective-permute-start(bf16[16,2432]{1,0:T(8,128)(2,1)S(1)} %get-tuple-element.9), channel_id=1, source_target_pairs={{0,10},{2,12},{4,14},{6,0},{8,2},{10,4},{12,6},{14,8},{1,11},{3,13... | collective-permute-start | bytes 233480 | tf_op jit(solution)/shard_map/ppermute | solution.py:124
  86.6 13.0 %collective-permute-start.29 = (bf16[16,2432]{1,0:T(8,128)(2,1)S(1)}, bf16[16,2432]{1,0:T(8,128)(2,1)S(1)}, u32[]{:S(2)}, u32[]{:S(2)}) collective-permute-start(bf16[16,2432]{1,0:T(8,128)(2,1)S(1)} %get-tuple-element.10), channel_id=1, source_target_pairs={{0,8},{2,10},{4,12},{6,14},{8,0},{10,2},{12,4},{14,6},{1,9},{3,11}... | collective-permute-start | bytes 233480 | tf_op jit(solution)/shard_map/ppermute | solution.py:124
  91.1 8.5 %collective-permute-start.30 = (bf16[16,2432]{1,0:T(8,128)(2,1)S(1)}, bf16[16,2432]{1,0:T(8,128)(2,1)S(1)}, u32[]{:S(2)}, u32[]{:S(2)}) collective-permute-start(bf16[16,2432]{1,0:T(8,128)(2,1)S(1)} %get-tuple-element.11), channel_id=1, source_target_pairs={{0,6},{2,8},{4,10},{6,12},{8,14},{10,0},{12,2},{14,4},{1,7},{3,9},... | collective-permute-start | bytes 233480 | tf_op jit(solution)/shard_map/ppermute | solution.py:124
  93.0 6.6 %collective-permute-start.31 = (bf16[16,2432]{1,0:T(8,128)(2,1)S(1)}, bf16[16,2432]{1,0:T(8,128)(2,1)S(1)}, u32[]{:S(2)}, u32[]{:S(2)}) collective-permute-start(bf16[16,2432]{1,0:T(8,128)(2,1)S(1)} %get-tuple-element.12), channel_id=1, source_target_pairs={{0,4},{2,6},{4,8},{6,10},{8,12},{10,14},{12,0},{14,2},{1,5},{3,7},... | collective-permute-start | bytes 233480 | tf_op jit(solution)/shard_map/ppermute | solution.py:124
  (8 other events, 47.9 us)

commit v8 on v5

--- a/solution.py
+++ b/solution.py
@@ -125,7 +125,11 @@
     return jnp.stack(moved, axis=0)
 
 
-def split_layer(g_half, routes_l, acts_l, own, other, is_own, gain_half, scale_l):
+def after(value, gate):
+    return lax.optimization_barrier((value, gate))
+
+
+def split_layer(g_half, routes_l, acts_l, own, other, is_own, gain_half, scale_l, gate):
     peers = lax.axis_size("dict")
     me = lax.axis_index("dict")
     rows, listed = routes_l.shape
@@ -145,6 +149,8 @@
     sent = jnp.concatenate(
         [jnp.broadcast_to(g_half[None], (peers, rows, half)), placed], axis=-1
     )
+    if gate is not None:
+        sent, other = after(sent, other)
     got = exchange(sent, 1).reshape(peers * rows, half + block)
     g_all = got[:, :half]
     code_all = got[:, half:]
@@ -211,7 +217,10 @@
         s = jnp.where(is_own, small, other_small)
         gain_half = lax.dynamic_slice_in_dim(s[:width], mine, half, axis=0)
         scale_l = s[width:width + rows]
-        attr, g_half = split_layer(g_half, routes[0], acts[0], own, other, is_own, gain_half, scale_l)
+        gate = True if layer == depth - 1 else None
+        attr, g_half = split_layer(
+            g_half, routes[0], acts[0], own, other, is_own, gain_half, scale_l, gate
+        )
         partner = swap_cores(g_half)
         full = jnp.where(
             here == 0,

time: 94.1 us -> 107 us (1.14)
  waiting for transfers between devices: 20 us -> 23.9 us
  local copies, waits for them, and re-layouts: 8.28 us -> 11 us
  matrix products: 4.18 us -> 6.7 us
  starting transfers between devices: 54.6 us -> 56.5 us
  other arithmetic: 5.44 us -> 6.8 us
    ppermute x28, waiting for transfers between devices: 16.4 us -> 19.3 us  [exchange(): moved.append(lax.ppermute(parts[shift], 'dict', route))]
    dot_general x4, matrix products: 2.16 us -> 4.69 us  [with_dec(): lax.dot_general(g_all, dec, (((1,), (1,)), ((), ())), preferred_element_t...]
    ppermute x28, starting transfers between devices: 53.2 us -> 55.4 us  [exchange(): moved.append(lax.ppermute(parts[shift], 'dict', route))]
    slice x0 -> x1, local copies, waits for them, and re-layouts: none -> 1.19 us  [split_device(): other = (other_w[:blocks], other_w[blocks:])]
    unnamed x38 -> x52, local copies, waits for them, and re-layouts: 4.79 us -> 5.47 us
  transfers between devices with their start and end apart: 34 -> 34, of which waited for: 12 -> 16; matrix products, arithmetic and copies ran while one was open for 12% -> 14% of each run, Pallas kernels for 0% -> 0%
where the time goes in v8:
time: 107 us; the launch traced here: 106 us
  starting transfers between devices  56.5 us (53%)
  waiting for transfers between devices  23.9 us (22%)
  local copies, waits for them, and re-layouts  11 us (10%)
  other arithmetic  6.8 us (6%)
  matrix products  6.7 us (6%)
  between operations  1.12 us (1%)
    ppermute x28, starting transfers between devices, exchange(): moved.append(lax.ppermute(parts[shift], 'dict', route))  55.4 us
    ppermute x28, waiting for transfers between devices, exchange(): moved.append(lax.ppermute(parts[shift], 'dict', route))  19.3 us
    unnamed x52, local copies, waits for them, and re-layouts  5.47 us
    dot_general x4, matrix products, with_dec(): lax.dot_general(g_all, dec, (((1,), (1,)), ((), ())), preferred_element_t...  4.69 us
    ppermute x6, waiting for transfers between devices, swap_cores(): return lax.ppermute(block, 'section', [(0, 1), (1, 0)])  4.53 us
  transfers between devices with their start and end apart: 34, of which 16 were waited for; matrix products, arithmetic and copies ran while one was open for 14% of the time, Pallas kernels for 0%

profile of v8, /device:TPU:0, one launch (start us, length us, event | category | flops | bytes accessed | tf_op | source)
XLA Modules:
  0.0 106.1 jit_solution(6908615667418221777)
XLA Ops:
  0.6 1.8 %dynamic-slice_bitcast_fusion = (bf16[256,2304]{1,0:T(8,128)(2,1)S(1)}, bf16[256,2304]{1,0:T(8,128)(2,1)S(1)}) fusion(bf16[1,256,4608]{2,1,0:T(8,128)(2,1)} %param.11, s32[]{:T(128)S(6)} %select_n.192, bf16[1,256,4608]{2,1,0:T(8,128)(2,1)} %param.10), kind=kLoop, calls=%fused_computation.42 | loop fusion | bytes 4718596 | tf_op jit(solution)/shard_map/dynamic_slice | solution.py:202
  2.5 1.6 %pad_maximum_fusion = bf16[512,2304]{1,0:T(8,128)(2,1)} fusion(bf16[256,2304]{1,0:T(8,128)(2,1)S(1)} %get-tuple-element.48, bf16[256,2304]{1,0:T(8,128)(2,1)S(1)} %get-tuple-element.49), kind=kLoop, calls=%fused_computation.4 | loop fusion | flops 4718592 | bytes 4718592 | tf_op jit(solution)/shard_map/concatenate | solution.py:199
  5.9 3.0 %collective-permute-done.1 = bf16[512,2304]{1,0:T(8,128)(2,1)S(1)} collective-permute-done((bf16[512,2304]{1,0:T(8,128)(2,1)}, bf16[512,2304]{1,0:T(8,128)(2,1)S(1)}, u32[]{:S(2)}, u32[]{:S(2)}) %collective-permute-start.1) | collective-permute-done | bytes 2359328 | tf_op jit(solution)/shard_map/ppermute | solution.py:116
  8.9 1.2 %fusion.78 = (bf16[256,2304]{1,0:T(8,128)(2,1)S(1)}, bf16[256,2304]{1,0:T(8,128)(2,1)}) fusion(bf16[512,2304]{1,0:T(8,128)(2,1)S(1)} %collective-permute-done.1), kind=kLoop, calls=%fused_computation.206 | loop fusion | bytes 4718592 | tf_op jit(solution)/shard_map/slice | solution.py:207
  10.9 2.9 %collective-permute-start.2 = (bf16[16,2432]{1,0:T(8,128)(2,1)}, bf16[16,2432]{1,0:T(8,128)(2,1)}, u32[]{:S(2)}, u32[]{:S(2)}) collective-permute-start(bf16[16,2432]{1,0:T(8,128)(2,1)} %get-tuple-element.42), channel_id=1, source_target_pairs={{0,2},{2,4},{4,6},{6,8},{8,10},{10,12},{12,14},{14,0},{1,3},{3,5},... | collective-permute-start | bytes 233480 | tf_op jit(solution)/shard_map/ppermute | solution.py:124
  14.4 1.6 %collective-permute-start.3 = (bf16[16,2432]{1,0:T(8,128)(2,1)}, bf16[16,2432]{1,0:T(8,128)(2,1)S(1)}, u32[]{:S(2)}, u32[]{:S(2)}) collective-permute-start(bf16[16,2432]{1,0:T(8,128)(2,1)} %get-tuple-element.41), channel_id=1, source_target_pairs={{0,4},{2,6},{4,8},{6,10},{8,12},{10,14},{12,0},{14,2},{1,5},{3,7},... | collective-permute-start | bytes 233480 | tf_op jit(solution)/shard_map/ppermute | solution.py:124
  15.9 2.6 %collective-permute-start.4 = (bf16[16,2432]{1,0:T(8,128)(2,1)}, bf16[16,2432]{1,0:T(8,128)(2,1)S(1)}, u32[]{:S(2)}, u32[]{:S(2)}) collective-permute-start(bf16[16,2432]{1,0:T(8,128)(2,1)} %get-tuple-element.40), channel_id=1, source_target_pairs={{0,6},{2,8},{4,10},{6,12},{8,14},{10,0},{12,2},{14,4},{1,7},{3,9},... | collective-permute-start | bytes 233480 | tf_op jit(solution)/shard_map/ppermute | solution.py:124
  18.5 1.2 %collective-permute-start.5 = (bf16[16,2432]{1,0:T(8,128)(2,1)}, bf16[16,2432]{1,0:T(8,128)(2,1)S(1)}, u32[]{:S(2)}, u32[]{:S(2)}) collective-permute-start(bf16[16,2432]{1,0:T(8,128)(2,1)} %get-tuple-element.39), channel_id=1, source_target_pairs={{0,8},{2,10},{4,12},{6,14},{8,0},{10,2},{12,4},{14,6},{1,9},{3,11}... | collective-permute-start | bytes 233480 | tf_op jit(solution)/shard_map/ppermute | solution.py:124
  19.8 2.6 %collective-permute-start.6 = (bf16[16,2432]{1,0:T(8,128)(2,1)}, bf16[16,2432]{1,0:T(8,128)(2,1)S(1)}, u32[]{:S(2)}, u32[]{:S(2)}) collective-permute-start(bf16[16,2432]{1,0:T(8,128)(2,1)} %get-tuple-element.38), channel_id=1, source_target_pairs={{0,10},{2,12},{4,14},{6,0},{8,2},{10,4},{12,6},{14,8},{1,11},{3,13... | collective-permute-start | bytes 233480 | tf_op jit(solution)/shard_map/ppermute | solution.py:124
  22.3 1.5 %bitcast_dynamic-update-slice_fusion.29 = bf16[8,16,2432]{2,1,0:T(8,128)(2,1)} fusion(bf16[8,16,2432]{2,1,0:T(8,128)(2,1)} %get-tuple-element.43, bf16[16,2432]{1,0:T(8,128)(2,1)} %collective-permute-done.2), kind=kLoop, calls=%fused_computation.151 | loop fusion | bytes 155648
  23.9 1.3 %collective-permute-start.7 = (bf16[16,2432]{1,0:T(8,128)(2,1)}, bf16[16,2432]{1,0:T(8,128)(2,1)S(1)}, u32[]{:S(2)}, u32[]{:S(2)}) collective-permute-start(bf16[16,2432]{1,0:T(8,128)(2,1)} %get-tuple-element.37), channel_id=1, source_target_pairs={{0,12},{2,14},{4,0},{6,2},{8,4},{10,6},{12,8},{14,10},{1,13},{3,15... | collective-permute-start | bytes 233480 | tf_op jit(solution)/shard_map/ppermute | solution.py:124
  25.9 1.4 %collective-permute-done.4 = bf16[16,2432]{1,0:T(8,128)(2,1)S(1)} collective-permute-done((bf16[16,2432]{1,0:T(8,128)(2,1)}, bf16[16,2432]{1,0:T(8,128)(2,1)S(1)}, u32[]{:S(2)}, u32[]{:S(2)}) %collective-permute-start.4) | collective-permute-done | bytes 77856 | tf_op jit(solution)/shard_map/ppermute | solution.py:124
  29.9 1.9 %collective-permute-done.7 = bf16[16,2432]{1,0:T(8,128)(2,1)S(1)} collective-permute-done((bf16[16,2432]{1,0:T(8,128)(2,1)}, bf16[16,2432]{1,0:T(8,128)(2,1)S(1)}, u32[]{:S(2)}, u32[]{:S(2)}) %collective-permute-start.7) | collective-permute-done | bytes 77856 | tf_op jit(solution)/shard_map/ppermute | solution.py:124
  33.8 2.0 %fusion.24 = f32[128,256]{1,0:T(8,128)S(1)} fusion(bf16[256,2304]{1,0:T(8,128)(2,1)} %get-tuple-element.6, bf16[128,2432]{1,0:T(8,128)(2,1)} %bitcast.159), kind=kOutput, calls=%fused_computation.59 | convolution fusion | flops 150994944 | bytes 1900544 | tf_op jit(solution)/shard_map/dot_general | solution.py:159
  35.8 1.6 %fusion.8 = f32[128,256]{1,0:T(8,128)S(1)} fusion(f32[128,256]{1,0:T(8,128)S(1)} %fusion.24, bf16[1,256,4608]{2,1,0:T(8,128)(2,1)S(1)} %copy-done, s32[]{:T(128)S(6)} %select_n.187, bf16[128,2432]{1,0:T(8,128)(2,1)} %bitcast.160, pred[]{:T(512)S(6)} %eq.47), kind=kOutput, calls=%fused_computation.44 | convolution fusion | flops 151027712 | bytes 2031621 | tf_op jit(solution)/shard_map/dot_general | solution.py:159
  41.1 4.3 %collective-permute-start.10 = (bf16[16,2432]{1,0:T(8,128)(2,1)S(1)}, bf16[16,2432]{1,0:T(8,128)(2,1)S(1)}, u32[]{:S(2)}, u32[]{:S(2)}) collective-permute-start(bf16[16,2432]{1,0:T(8,128)(2,1)S(1)} %get-tuple-element.30), channel_id=1, source_target_pairs={{0,14},{2,0},{4,2},{6,4},{8,6},{10,8},{12,10},{14,12},{1,15},{3,1}... | collective-permute-start | bytes 233480 | tf_op jit(solution)/shard_map/ppermute | solution.py:124
  45.4 1.4 %collective-permute-start.11 = (bf16[16,2432]{1,0:T(8,128)(2,1)S(1)}, bf16[16,2432]{1,0:T(8,128)(2,1)S(1)}, u32[]{:S(2)}, u32[]{:S(2)}) collective-permute-start(bf16[16,2432]{1,0:T(8,128)(2,1)S(1)} %get-tuple-element.31), channel_id=1, source_target_pairs={{0,12},{2,14},{4,0},{6,2},{8,4},{10,6},{12,8},{14,10},{1,13},{3,15... | collective-permute-start | bytes 233480 | tf_op jit(solution)/shard_map/ppermute | solution.py:124
  46.7 3.5 %collective-permute-start.13 = (bf16[16,2432]{1,0:T(8,128)(2,1)S(1)}, bf16[16,2432]{1,0:T(8,128)(2,1)S(1)}, u32[]{:S(2)}, u32[]{:S(2)}) collective-permute-start(bf16[16,2432]{1,0:T(8,128)(2,1)S(1)} %get-tuple-element.33), channel_id=1, source_target_pairs={{0,8},{2,10},{4,12},{6,14},{8,0},{10,2},{12,4},{14,6},{1,9},{3,11}... | collective-permute-start | bytes 233480 | tf_op jit(solution)/shard_map/ppermute | solution.py:124
  52.5 7.7 %collective-permute-done.13 = bf16[16,2432]{1,0:T(8,128)(2,1)S(1)} collective-permute-done((bf16[16,2432]{1,0:T(8,128)(2,1)S(1)}, bf16[16,2432]{1,0:T(8,128)(2,1)S(1)}, u32[]{:S(2)}, u32[]{:S(2)}) %collective-permute-start.13) | collective-permute-done | bytes 77856 | tf_op jit(solution)/shard_map/ppermute | solution.py:124
  60.2 1.4 %collective-permute-done.14 = bf16[16,2432]{1,0:T(8,128)(2,1)S(1)} collective-permute-done((bf16[16,2432]{1,0:T(8,128)(2,1)S(1)}, bf16[16,2432]{1,0:T(8,128)(2,1)S(1)}, u32[]{:S(2)}, u32[]{:S(2)}) %collective-permute-start.14) | collective-permute-done | bytes 77856 | tf_op jit(solution)/shard_map/ppermute | solution.py:124
  63.1 2.8 %collective-permute-start.19 = (bf16[16,2432]{1,0:T(8,128)(2,1)S(1)}, bf16[16,2432]{1,0:T(8,128)(2,1)S(1)}, u32[]{:S(2)}, u32[]{:S(2)}) collective-permute-start(bf16[16,2432]{1,0:T(8,128)(2,1)S(1)} %get-tuple-element.26), channel_id=1, source_target_pairs={{0,6},{2,8},{4,10},{6,12},{8,14},{10,0},{12,2},{14,4},{1,7},{3,9},... | collective-permute-start | bytes 233480 | tf_op jit(solution)/shard_map/ppermute | solution.py:124
  65.9 1.5 %collective-permute-start.20 = (bf16[16,2432]{1,0:T(8,128)(2,1)S(1)}, bf16[16,2432]{1,0:T(8,128)(2,1)S(1)}, u32[]{:S(2)}, u32[]{:S(2)}) collective-permute-start(bf16[16,2432]{1,0:T(8,128)(2,1)S(1)} %get-tuple-element.27), channel_id=1, source_target_pairs={{0,8},{2,10},{4,12},{6,14},{8,0},{10,2},{12,4},{14,6},{1,9},{3,11}... | collective-permute-start | bytes 233480 | tf_op jit(solution)/shard_map/ppermute | solution.py:124
  67.3 1.5 %collective-permute-start.21 = (bf16[16,2432]{1,0:T(8,128)(2,1)S(1)}, bf16[16,2432]{1,0:T(8,128)(2,1)S(1)}, u32[]{:S(2)}, u32[]{:S(2)}) collective-permute-start(bf16[16,2432]{1,0:T(8,128)(2,1)S(1)} %get-tuple-element.28), channel_id=1, source_target_pairs={{0,10},{2,12},{4,14},{6,0},{8,2},{10,4},{12,6},{14,8},{1,11},{3,13... | collective-permute-start | bytes 233480 | tf_op jit(solution)/shard_map/ppermute | solution.py:124
  69.8 1.5 %collective-permute-start.22 = (bf16[16,2432]{1,0:T(8,128)(2,1)S(1)}, bf16[16,2432]{1,0:T(8,128)(2,1)S(1)}, u32[]{:S(2)}, u32[]{:S(2)}) collective-permute-start(bf16[16,2432]{1,0:T(8,128)(2,1)S(1)} %get-tuple-element.22), channel_id=1, source_target_pairs={{0,12},{2,14},{4,0},{6,2},{8,4},{10,6},{12,8},{14,10},{1,13},{3,15... | collective-permute-start | bytes 233480 | tf_op jit(solution)/shard_map/ppermute | solution.py:124
  71.3 2.9 %collective-permute-start.23 = (bf16[16,2432]{1,0:T(8,128)(2,1)S(1)}, bf16[16,2432]{1,0:T(8,128)(2,1)S(1)}, u32[]{:S(2)}, u32[]{:S(2)}) collective-permute-start(bf16[16,2432]{1,0:T(8,128)(2,1)S(1)} %get-tuple-element.21), channel_id=1, source_target_pairs={{0,14},{2,0},{4,2},{6,4},{8,6},{10,8},{12,10},{14,12},{1,15},{3,1}... | collective-permute-start | bytes 233480 | tf_op jit(solution)/shard_map/ppermute | solution.py:124
  75.2 1.3 %collective-permute-done.20 = bf16[16,2432]{1,0:T(8,128)(2,1)S(1)} collective-permute-done((bf16[16,2432]{1,0:T(8,128)(2,1)S(1)}, bf16[16,2432]{1,0:T(8,128)(2,1)S(1)}, u32[]{:S(2)}, u32[]{:S(2)}) %collective-permute-start.20) | collective-permute-done | bytes 77856 | tf_op jit(solution)/shard_map/ppermute | solution.py:124
  80.1 6.3 %collective-permute-start.25 = (bf16[16,2432]{1,0:T(8,128)(2,1)S(1)}, bf16[16,2432]{1,0:T(8,128)(2,1)S(1)}, u32[]{:S(2)}, u32[]{:S(2)}) collective-permute-start(bf16[16,2432]{1,0:T(8,128)(2,1)S(1)} %get-tuple-element.15), channel_id=1, source_target_pairs={{0,14},{2,0},{4,2},{6,4},{8,6},{10,8},{12,10},{14,12},{1,15},{3,1}... | collective-permute-start | bytes 233480 | tf_op jit(solution)/shard_map/ppermute | solution.py:124
  86.4 2.7 %collective-permute-start.26 = (bf16[16,2432]{1,0:T(8,128)(2,1)S(1)}, bf16[16,2432]{1,0:T(8,128)(2,1)S(1)}, u32[]{:S(2)}, u32[]{:S(2)}) collective-permute-start(bf16[16,2432]{1,0:T(8,128)(2,1)S(1)} %get-tuple-element.16), channel_id=1, source_target_pairs={{0,12},{2,14},{4,0},{6,2},{8,4},{10,6},{12,8},{14,10},{1,13},{3,15... | collective-permute-start | bytes 233480 | tf_op jit(solution)/shard_map/ppermute | solution.py:124
  90.3 1.8 %collective-permute-start.29 = (bf16[16,2432]{1,0:T(8,128)(2,1)S(1)}, bf16[16,2432]{1,0:T(8,128)(2,1)S(1)}, u32[]{:S(2)}, u32[]{:S(2)}) collective-permute-start(bf16[16,2432]{1,0:T(8,128)(2,1)S(1)} %get-tuple-element.19), channel_id=1, source_target_pairs={{0,6},{2,8},{4,10},{6,12},{8,14},{10,0},{12,2},{14,4},{1,7},{3,9},... | collective-permute-start | bytes 233480 | tf_op jit(solution)/shard_map/ppermute | solution.py:124
  92.1 2.3 %collective-permute-start.30 = (bf16[16,2432]{1,0:T(8,128)(2,1)S(1)}, bf16[16,2432]{1,0:T(8,128)(2,1)S(1)}, u32[]{:S(2)}, u32[]{:S(2)}) collective-permute-start(bf16[16,2432]{1,0:T(8,128)(2,1)S(1)} %get-tuple-element.20), channel_id=1, source_target_pairs={{0,4},{2,6},{4,8},{6,10},{8,12},{10,14},{12,0},{14,2},{1,5},{3,7},... | collective-permute-start | bytes 233480 | tf_op jit(solution)/shard_map/ppermute | solution.py:124
  95.3 6.5 %collective-permute-start.31 = (bf16[16,2432]{1,0:T(8,128)(2,1)S(1)}, bf16[16,2432]{1,0:T(8,128)(2,1)S(1)}, u32[]{:S(2)}, u32[]{:S(2)}) collective-permute-start(bf16[16,2432]{1,0:T(8,128)(2,1)S(1)} %get-tuple-element.14), channel_id=1, source_target_pairs={{0,2},{2,4},{4,6},{6,8},{8,10},{10,12},{12,14},{14,0},{1,3},{3,5},... | collective-permute-start | bytes 233480 | tf_op jit(solution)/shard_map/ppermute | solution.py:124
  102.4 1.4 %collective-permute-done.31 = bf16[16,2432]{1,0:T(8,128)(2,1)S(1)} collective-permute-done((bf16[16,2432]{1,0:T(8,128)(2,1)S(1)}, bf16[16,2432]{1,0:T(8,128)(2,1)S(1)}, u32[]{:S(2)}, u32[]{:S(2)}) %collective-permute-start.31) | collective-permute-done | bytes 77856 | tf_op jit(solution)/shard_map/ppermute | solution.py:124
  (148 shorter events, 26.0 us)
Async XLA Ops:
  4.1 4.8 %collective-permute-start.1 = (bf16[512,2304]{1,0:T(8,128)(2,1)}, bf16[512,2304]{1,0:T(8,128)(2,1)S(1)}, u32[]{:S(2)}, u32[]{:S(2)}) collective-permute-start(bf16[512,2304]{1,0:T(8,128)(2,1)} %pad_maximum_fusion), channel_id=1, source_target_pairs={{0,1},{1,0},{2,3},{3,2},{4,5},{5,4},{6,7},{7,6},{8,9},{9,8},{10,11... | collective-permute-start | bytes 7077896 | tf_op jit(solution)/shard_map/ppermute | solution.py:116
  10.9 8.9 %collective-permute-start.2 = (bf16[16,2432]{1,0:T(8,128)(2,1)}, bf16[16,2432]{1,0:T(8,128)(2,1)}, u32[]{:S(2)}, u32[]{:S(2)}) collective-permute-start(bf16[16,2432]{1,0:T(8,128)(2,1)} %get-tuple-element.42), channel_id=1, source_target_pairs={{0,2},{2,4},{4,6},{6,8},{8,10},{10,12},{12,14},{14,0},{1,3},{3,5},... | collective-permute-start | bytes 233480 | tf_op jit(solution)/shard_map/ppermute | solution.py:124
  14.3 23.2 %collective-permute-start = (f32[4624]{0:T(1024)}, f32[4624]{0:T(1024)}, u32[]{:S(2)}, u32[]{:S(2)}) collective-permute-start(f32[4624]{0:T(1024)} %pad_maximum_fusion.7), channel_id=1, source_target_pairs={{0,1},{1,0},{2,3},{3,2},{4,5},{5,4},{6,7},{7,6},{8,9},{9,8},{10,11... | collective-permute-start | bytes 55496 | tf_op jit(solution)/shard_map/ppermute | solution.py:116
  14.4 9.5 %collective-permute-start.3 = (bf16[16,2432]{1,0:T(8,128)(2,1)}, bf16[16,2432]{1,0:T(8,128)(2,1)S(1)}, u32[]{:S(2)}, u32[]{:S(2)}) collective-permute-start(bf16[16,2432]{1,0:T(8,128)(2,1)} %get-tuple-element.41), channel_id=1, source_target_pairs={{0,4},{2,6},{4,8},{6,10},{8,12},{10,14},{12,0},{14,2},{1,5},{3,7},... | collective-permute-start | bytes 233480 | tf_op jit(solution)/shard_map/ppermute | solution.py:124
  15.9 11.4 %collective-permute-start.4 = (bf16[16,2432]{1,0:T(8,128)(2,1)}, bf16[16,2432]{1,0:T(8,128)(2,1)S(1)}, u32[]{:S(2)}, u32[]{:S(2)}) collective-permute-start(bf16[16,2432]{1,0:T(8,128)(2,1)} %get-tuple-element.40), channel_id=1, source_target_pairs={{0,6},{2,8},{4,10},{6,12},{8,14},{10,0},{12,2},{14,4},{1,7},{3,9},... | collective-permute-start | bytes 233480 | tf_op jit(solution)/shard_map/ppermute | solution.py:124
  18.5 10.1 %collective-permute-start.5 = (bf16[16,2432]{1,0:T(8,128)(2,1)}, bf16[16,2432]{1,0:T(8,128)(2,1)S(1)}, u32[]{:S(2)}, u32[]{:S(2)}) collective-permute-start(bf16[16,2432]{1,0:T(8,128)(2,1)} %get-tuple-element.39), channel_id=1, source_target_pairs={{0,8},{2,10},{4,12},{6,14},{8,0},{10,2},{12,4},{14,6},{1,9},{3,11}... | collective-permute-start | bytes 233480 | tf_op jit(solution)/shard_map/ppermute | solution.py:124
  19.8 9.5 %collective-permute-start.6 = (bf16[16,2432]{1,0:T(8,128)(2,1)}, bf16[16,2432]{1,0:T(8,128)(2,1)S(1)}, u32[]{:S(2)}, u32[]{:S(2)}) collective-permute-start(bf16[16,2432]{1,0:T(8,128)(2,1)} %get-tuple-element.38), channel_id=1, source_target_pairs={{0,10},{2,12},{4,14},{6,0},{8,2},{10,4},{12,6},{14,8},{1,11},{3,13... | collective-permute-start | bytes 233480 | tf_op jit(solution)/shard_map/ppermute | solution.py:124
  23.9 7.9 %collective-permute-start.7 = (bf16[16,2432]{1,0:T(8,128)(2,1)}, bf16[16,2432]{1,0:T(8,128)(2,1)S(1)}, u32[]{:S(2)}, u32[]{:S(2)}) collective-permute-start(bf16[16,2432]{1,0:T(8,128)(2,1)} %get-tuple-element.37), channel_id=1, source_target_pairs={{0,12},{2,14},{4,0},{6,2},{8,4},{10,6},{12,8},{14,10},{1,13},{3,15... | collective-permute-start | bytes 233480 | tf_op jit(solution)/shard_map/ppermute | solution.py:124
  27.3 5.1 %collective-permute-start.8 = (bf16[16,2432]{1,0:T(8,128)(2,1)}, bf16[16,2432]{1,0:T(8,128)(2,1)S(1)}, u32[]{:S(2)}, u32[]{:S(2)}) collective-permute-start(bf16[16,2432]{1,0:T(8,128)(2,1)} %get-tuple-element.36), channel_id=1, source_target_pairs={{0,14},{2,0},{4,2},{6,4},{8,6},{10,8},{12,10},{14,12},{1,15},{3,1}... | collective-permute-start | bytes 233480 | tf_op jit(solution)/shard_map/ppermute | solution.py:124
  37.5 1.5 %collective-permute-start.9 = (f32[128,384]{1,0:T(8,128)S(1)}, f32[128,384]{1,0:T(8,128)S(1)}, u32[]{:S(2)}, u32[]{:S(2)}) collective-permute-start(f32[128,384]{1,0:T(8,128)S(1)} %pad_maximum_fusion.2), channel_id=1, source_target_pairs={{0,1},{1,0},{2,3},{3,2},{4,5},{5,4},{6,7},{7,6},{8,9},{9,8},{10,11... | collective-permute-start | bytes 589832 | tf_op jit(solution)/shard_map/ppermute | solution.py:116
  41.1 9.2 %collective-permute-start.10 = (bf16[16,2432]{1,0:T(8,128)(2,1)S(1)}, bf16[16,2432]{1,0:T(8,128)(2,1)S(1)}, u32[]{:S(2)}, u32[]{:S(2)}) collective-permute-start(bf16[16,2432]{1,0:T(8,128)(2,1)S(1)} %get-tuple-element.30), channel_id=1, source_target_pairs={{0,14},{2,0},{4,2},{6,4},{8,6},{10,8},{12,10},{14,12},{1,15},{3,1}... | collective-permute-start | bytes 233480 | tf_op jit(solution)/shard_map/ppermute | solution.py:124
  45.4 5.8 %collective-permute-start.11 = (bf16[16,2432]{1,0:T(8,128)(2,1)S(1)}, bf16[16,2432]{1,0:T(8,128)(2,1)S(1)}, u32[]{:S(2)}, u32[]{:S(2)}) collective-permute-start(bf16[16,2432]{1,0:T(8,128)(2,1)S(1)} %get-tuple-element.31), channel_id=1, source_target_pairs={{0,12},{2,14},{4,0},{6,2},{8,4},{10,6},{12,8},{14,10},{1,13},{3,15... | collective-permute-start | bytes 233480 | tf_op jit(solution)/shard_map/ppermute | solution.py:124
  46.7 5.7 %collective-permute-start.12 = (bf16[16,2432]{1,0:T(8,128)(2,1)S(1)}, bf16[16,2432]{1,0:T(8,128)(2,1)S(1)}, u32[]{:S(2)}, u32[]{:S(2)}) collective-permute-start(bf16[16,2432]{1,0:T(8,128)(2,1)S(1)} %get-tuple-element.32), channel_id=1, source_target_pairs={{0,10},{2,12},{4,14},{6,0},{8,2},{10,4},{12,6},{14,8},{1,11},{3,13... | collective-permute-start | bytes 233480 | tf_op jit(solution)/shard_map/ppermute | solution.py:124
  46.7 13.5 %collective-permute-start.13 = (bf16[16,2432]{1,0:T(8,128)(2,1)S(1)}, bf16[16,2432]{1,0:T(8,128)(2,1)S(1)}, u32[]{:S(2)}, u32[]{:S(2)}) collective-permute-start(bf16[16,2432]{1,0:T(8,128)(2,1)S(1)} %get-tuple-element.33), channel_id=1, source_target_pairs={{0,8},{2,10},{4,12},{6,14},{8,0},{10,2},{12,4},{14,6},{1,9},{3,11}... | collective-permute-start | bytes 233480 | tf_op jit(solution)/shard_map/ppermute | solution.py:124
  50.2 11.4 %collective-permute-start.14 = (bf16[16,2432]{1,0:T(8,128)(2,1)S(1)}, bf16[16,2432]{1,0:T(8,128)(2,1)S(1)}, u32[]{:S(2)}, u32[]{:S(2)}) collective-permute-start(bf16[16,2432]{1,0:T(8,128)(2,1)S(1)} %get-tuple-element.34), channel_id=1, source_target_pairs={{0,6},{2,8},{4,10},{6,12},{8,14},{10,0},{12,2},{14,4},{1,7},{3,9},... | collective-permute-start | bytes 233480 | tf_op jit(solution)/shard_map/ppermute | solution.py:124
  50.2 11.4 %collective-permute-start.15 = (bf16[16,2432]{1,0:T(8,128)(2,1)S(1)}, bf16[16,2432]{1,0:T(8,128)(2,1)S(1)}, u32[]{:S(2)}, u32[]{:S(2)}) collective-permute-start(bf16[16,2432]{1,0:T(8,128)(2,1)S(1)} %get-tuple-element.35), channel_id=1, source_target_pairs={{0,4},{2,6},{4,8},{6,10},{8,12},{10,14},{12,0},{14,2},{1,5},{3,7},... | collective-permute-start | bytes 233480 | tf_op jit(solution)/shard_map/ppermute | solution.py:124
  51.2 10.5 %collective-permute-start.16 = (bf16[16,2432]{1,0:T(8,128)(2,1)S(1)}, bf16[16,2432]{1,0:T(8,128)(2,1)S(1)}, u32[]{:S(2)}, u32[]{:S(2)}) collective-permute-start(bf16[16,2432]{1,0:T(8,128)(2,1)S(1)} %get-tuple-element.29), channel_id=1, source_target_pairs={{0,2},{2,4},{4,6},{6,8},{8,10},{10,12},{12,14},{14,0},{1,3},{3,5},... | collective-permute-start | bytes 233480 | tf_op jit(solution)/shard_map/ppermute | solution.py:124
  62.0 7.8 %collective-permute-start.17 = (bf16[16,2432]{1,0:T(8,128)(2,1)S(1)}, bf16[16,2432]{1,0:T(8,128)(2,1)S(1)}, u32[]{:S(2)}, u32[]{:S(2)}) collective-permute-start(bf16[16,2432]{1,0:T(8,128)(2,1)S(1)} %get-tuple-element.24), channel_id=1, source_target_pairs={{0,2},{2,4},{4,6},{6,8},{8,10},{10,12},{12,14},{14,0},{1,3},{3,5},... | collective-permute-start | bytes 233480 | tf_op jit(solution)/shard_map/ppermute | solution.py:124
  62.1 9.2 %collective-permute-start.18 = (bf16[16,2432]{1,0:T(8,128)(2,1)S(1)}, bf16[16,2432]{1,0:T(8,128)(2,1)S(1)}, u32[]{:S(2)}, u32[]{:S(2)}) collective-permute-start(bf16[16,2432]{1,0:T(8,128)(2,1)S(1)} %get-tuple-element.25), channel_id=1, source_target_pairs={{0,4},{2,6},{4,8},{6,10},{8,12},{10,14},{12,0},{14,2},{1,5},{3,7},... | collective-permute-start | bytes 233480 | tf_op jit(solution)/shard_map/ppermute | solution.py:124
  63.1 12.1 %collective-permute-start.19 = (bf16[16,2432]{1,0:T(8,128)(2,1)S(1)}, bf16[16,2432]{1,0:T(8,128)(2,1)S(1)}, u32[]{:S(2)}, u32[]{:S(2)}) collective-permute-start(bf16[16,2432]{1,0:T(8,128)(2,1)S(1)} %get-tuple-element.26), channel_id=1, source_target_pairs={{0,6},{2,8},{4,10},{6,12},{8,14},{10,0},{12,2},{14,4},{1,7},{3,9},... | collective-permute-start | bytes 233480 | tf_op jit(solution)/shard_map/ppermute | solution.py:124
  65.9 10.7 %collective-permute-start.20 = (bf16[16,2432]{1,0:T(8,128)(2,1)S(1)}, bf16[16,2432]{1,0:T(8,128)(2,1)S(1)}, u32[]{:S(2)}, u32[]{:S(2)}) collective-permute-start(bf16[16,2432]{1,0:T(8,128)(2,1)S(1)} %get-tuple-element.27), channel_id=1, source_target_pairs={{0,8},{2,10},{4,12},{6,14},{8,0},{10,2},{12,4},{14,6},{1,9},{3,11}... | collective-permute-start | bytes 233480 | tf_op jit(solution)/shard_map/ppermute | solution.py:124
  67.3 9.2 %collective-permute-start.21 = (bf16[16,2432]{1,0:T(8,128)(2,1)S(1)}, bf16[16,2432]{1,0:T(8,128)(2,1)S(1)}, u32[]{:S(2)}, u32[]{:S(2)}) collective-permute-start(bf16[16,2432]{1,0:T(8,128)(2,1)S(1)} %get-tuple-element.28), channel_id=1, source_target_pairs={{0,10},{2,12},{4,14},{6,0},{8,2},{10,4},{12,6},{14,8},{1,11},{3,13... | collective-permute-start | bytes 233480 | tf_op jit(solution)/shard_map/ppermute | solution.py:124
  69.8 6.8 %collective-permute-start.22 = (bf16[16,2432]{1,0:T(8,128)(2,1)S(1)}, bf16[16,2432]{1,0:T(8,128)(2,1)S(1)}, u32[]{:S(2)}, u32[]{:S(2)}) collective-permute-start(bf16[16,2432]{1,0:T(8,128)(2,1)S(1)} %get-tuple-element.22), channel_id=1, source_target_pairs={{0,12},{2,14},{4,0},{6,2},{8,4},{10,6},{12,8},{14,10},{1,13},{3,15... | collective-permute-start | bytes 233480 | tf_op jit(solution)/shard_map/ppermute | solution.py:124
  71.3 5.4 %collective-permute-start.23 = (bf16[16,2432]{1,0:T(8,128)(2,1)S(1)}, bf16[16,2432]{1,0:T(8,128)(2,1)S(1)}, u32[]{:S(2)}, u32[]{:S(2)}) collective-permute-start(bf16[16,2432]{1,0:T(8,128)(2,1)S(1)} %get-tuple-element.21), channel_id=1, source_target_pairs={{0,14},{2,0},{4,2},{6,4},{8,6},{10,8},{12,10},{14,12},{1,15},{3,1}... | collective-permute-start | bytes 233480 | tf_op jit(solution)/shard_map/ppermute | solution.py:124
  78.1 27.0 %collective-permute-start.33 = (bf16[16,2304]{1,0:T(8,128)(2,1)S(1)}, bf16[16,2304]{1,0:T(8,128)(2,1)S(1)}, u32[]{:S(2)}, u32[]{:S(2)}) collective-permute-start(bf16[16,2304]{1,0:T(8,128)(2,1)S(1)} %add_convert_fusion.1), channel_id=1, source_target_pairs={{0,1},{1,0},{2,3},{3,2},{4,5},{5,4},{6,7},{7,6},{8,9},{9,8},{10,11... | collective-permute-start | bytes 221192 | tf_op jit(solution)/shard_map/ppermute | solution.py:116
  80.1 10.1 %collective-permute-start.25 = (bf16[16,2432]{1,0:T(8,128)(2,1)S(1)}, bf16[16,2432]{1,0:T(8,128)(2,1)S(1)}, u32[]{:S(2)}, u32[]{:S(2)}) collective-permute-start(bf16[16,2432]{1,0:T(8,128)(2,1)S(1)} %get-tuple-element.15), channel_id=1, source_target_pairs={{0,14},{2,0},{4,2},{6,4},{8,6},{10,8},{12,10},{14,12},{1,15},{3,1}... | collective-permute-start | bytes 233480 | tf_op jit(solution)/shard_map/ppermute | solution.py:124
  86.4 5.7 %collective-permute-start.26 = (bf16[16,2432]{1,0:T(8,128)(2,1)S(1)}, bf16[16,2432]{1,0:T(8,128)(2,1)S(1)}, u32[]{:S(2)}, u32[]{:S(2)}) collective-permute-start(bf16[16,2432]{1,0:T(8,128)(2,1)S(1)} %get-tuple-element.16), channel_id=1, source_target_pairs={{0,12},{2,14},{4,0},{6,2},{8,4},{10,6},{12,8},{14,10},{1,13},{3,15... | collective-permute-start | bytes 233480 | tf_op jit(solution)/shard_map/ppermute | solution.py:124
  89.2 6.1 %collective-permute-start.27 = (bf16[16,2432]{1,0:T(8,128)(2,1)S(1)}, bf16[16,2432]{1,0:T(8,128)(2,1)S(1)}, u32[]{:S(2)}, u32[]{:S(2)}) collective-permute-start(bf16[16,2432]{1,0:T(8,128)(2,1)S(1)} %get-tuple-element.17), channel_id=1, source_target_pairs={{0,10},{2,12},{4,14},{6,0},{8,2},{10,4},{12,6},{14,8},{1,11},{3,13... | collective-permute-start | bytes 233480 | tf_op jit(solution)/shard_map/ppermute | solution.py:124
  89.2 12.6 %collective-permute-start.28 = (bf16[16,2432]{1,0:T(8,128)(2,1)S(1)}, bf16[16,2432]{1,0:T(8,128)(2,1)S(1)}, u32[]{:S(2)}, u32[]{:S(2)}) collective-permute-start(bf16[16,2432]{1,0:T(8,128)(2,1)S(1)} %get-tuple-element.18), channel_id=1, source_target_pairs={{0,8},{2,10},{4,12},{6,14},{8,0},{10,2},{12,4},{14,6},{1,9},{3,11}... | collective-permute-start | bytes 233480 | tf_op jit(solution)/shard_map/ppermute | solution.py:124
  90.3 12.1 %collective-permute-start.29 = (bf16[16,2432]{1,0:T(8,128)(2,1)S(1)}, bf16[16,2432]{1,0:T(8,128)(2,1)S(1)}, u32[]{:S(2)}, u32[]{:S(2)}) collective-permute-start(bf16[16,2432]{1,0:T(8,128)(2,1)S(1)} %get-tuple-element.19), channel_id=1, source_target_pairs={{0,6},{2,8},{4,10},{6,12},{8,14},{10,0},{12,2},{14,4},{1,7},{3,9},... | collective-permute-start | bytes 233480 | tf_op jit(solution)/shard_map/ppermute | solution.py:124
  92.1 10.3 %collective-permute-start.30 = (bf16[16,2432]{1,0:T(8,128)(2,1)S(1)}, bf16[16,2432]{1,0:T(8,128)(2,1)S(1)}, u32[]{:S(2)}, u32[]{:S(2)}) collective-permute-start(bf16[16,2432]{1,0:T(8,128)(2,1)S(1)} %get-tuple-element.20), channel_id=1, source_target_pairs={{0,4},{2,6},{4,8},{6,10},{8,12},{10,14},{12,0},{14,2},{1,5},{3,7},... | collective-permute-start | bytes 233480 | tf_op jit(solution)/shard_map/ppermute | solution.py:124
  95.3 8.5 %collective-permute-start.31 = (bf16[16,2432]{1,0:T(8,128)(2,1)S(1)}, bf16[16,2432]{1,0:T(8,128)(2,1)S(1)}, u32[]{:S(2)}, u32[]{:S(2)}) collective-permute-start(bf16[16,2432]{1,0:T(8,128)(2,1)S(1)} %get-tuple-element.14), channel_id=1, source_target_pairs={{0,2},{2,4},{4,6},{6,8},{8,10},{10,12},{12,14},{14,0},{1,3},{3,5},... | collective-permute-start | bytes 233480 | tf_op jit(solution)/shard_map/ppermute | solution.py:124
  (15 other events, 62.2 us)

commit v9 on v5

--- a/solution.py
+++ b/solution.py
@@ -125,6 +125,17 @@
     return jnp.stack(moved, axis=0)
 
 
+def send_pieces(pieces, shifts, sign, peers):
+    moved = []
+    for piece, shift in zip(pieces, shifts):
+        if shift == 0:
+            moved.append(piece)
+        else:
+            route = [(d, (d + sign * shift) % peers) for d in range(peers)]
+            moved.append(lax.ppermute(piece, "dict", route))
+    return moved
+
+
 def split_layer(g_half, routes_l, acts_l, own, other, is_own, gain_half, scale_l):
     peers = lax.axis_size("dict")
     me = lax.axis_index("dict")
@@ -145,31 +156,39 @@
     sent = jnp.concatenate(
         [jnp.broadcast_to(g_half[None], (peers, rows, half)), placed], axis=-1
     )
-    got = exchange(sent, 1).reshape(peers * rows, half + block)
-    g_all = got[:, :half]
-    code_all = got[:, half:]
-
-    def with_dec(dec):
-        return lax.dot_general(
-            g_all, dec, (((1,), (1,)), ((), ())), preferred_element_type=jnp.float32
-        )
-
-    part = jnp.where(is_own, with_dec(own[0]), with_dec(other[0]))
-    paired = swap_cores(jnp.concatenate([part, code_all.astype(jnp.float32)], axis=1))
-    coef = (part + paired[:, :held * block]).astype(jnp.bfloat16)
-    code = jnp.where(is_own, code_all.astype(jnp.float32), paired[:, held * block:])
-    marks = jnp.concatenate([code == spot + 1 for spot in range(held)], axis=1)
-    dz = jnp.where(marks, coef, jnp.zeros_like(coef))
-
-    def with_enc(enc):
-        return jnp.dot(dz, enc, preferred_element_type=jnp.float32)
-
-    contrib = jnp.where(is_own, with_enc(own[1]), with_enc(other[1])).astype(jnp.bfloat16)
-    dz_pick = dz[:, :block]
-    for spot in range(1, held):
-        dz_pick = dz_pick + dz[:, spot * block:(spot + 1) * block]
-    back = jnp.concatenate([contrib, dz_pick], axis=-1).reshape(peers, rows, half + block)
-    returned = exchange(back, -1)
+    order = list(range(peers))
+    got = send_pieces([sent[s] for s in order], order, 1, peers)
+    cut = peers // 2 + 1
+    returned = [None] * peers
+    for group in (order[:cut], order[cut:]):
+        taken = jnp.concatenate([got[s] for s in group], axis=0)
+        g_all = taken[:, :half]
+        code_all = taken[:, half:]
+
+        def with_dec(dec):
+            return lax.dot_general(
+                g_all, dec, (((1,), (1,)), ((), ())), preferred_element_type=jnp.float32
+            )
+
+        part = jnp.where(is_own, with_dec(own[0]), with_dec(other[0]))
+        paired = swap_cores(jnp.concatenate([part, code_all.astype(jnp.float32)], axis=1))
+        coef = (part + paired[:, :held * block]).astype(jnp.bfloat16)
+        code = jnp.where(is_own, code_all.astype(jnp.float32), paired[:, held * block:])
+        marks = jnp.concatenate([code == spot + 1 for spot in range(held)], axis=1)
+        dz = jnp.where(marks, coef, jnp.zeros_like(coef))
+
+        def with_enc(enc):
+            return jnp.dot(dz, enc, preferred_element_type=jnp.float32)
+
+        contrib = jnp.where(is_own, with_enc(own[1]), with_enc(other[1])).astype(jnp.bfloat16)
+        dz_pick = dz[:, :block]
+        for spot in range(1, held):
+            dz_pick = dz_pick + dz[:, spot * block:(spot + 1) * block]
+        back = jnp.concatenate([contrib, dz_pick], axis=-1)
+        pieces = [back[i * rows:(i + 1) * rows] for i in range(len(group))]
+        for shift, piece in zip(group, send_pieces(pieces, group, -1, peers)):
+            returned[shift] = piece
+    returned = jnp.stack(returned, axis=0)
     total = jnp.sum(returned[:, :, :half].astype(jnp.float32), axis=0)
     dz_back = returned[:, :, half:]
     dz_slot = jnp.einsum("rks,srj->rkj", at_rel, dz_back, preferred_element_type=jnp.float32)

time: 94.1 us -> 113 us (1.20); the launches traced: 93.6 us -> 111 us
  waiting for transfers between devices: 20 us -> 36.5 us
  matrix products: 4.18 us -> 7.33 us
  starting transfers between devices: 54.6 us -> 51.6 us
  other arithmetic: 5.44 us -> 6.98 us
    ppermute x28, waiting for transfers between devices: 16.4 us -> 35 us  [send_pieces(): moved.append(lax.ppermute(piece, 'dict', route))]
    ppermute x28, starting transfers between devices: 53.2 us -> 50.2 us  [send_pieces(): moved.append(lax.ppermute(piece, 'dict', route))]
    ppermute x6 -> x8, waiting for transfers between devices: 3.57 us -> 1.54 us  [swap_cores(): return lax.ppermute(block, 'section', [(0, 1), (1, 0)])]
    unnamed x38 -> x42, local copies, waits for them, and re-layouts: 4.79 us -> 2.99 us
    dot_general x4 -> x8, matrix products: 2.16 us -> 3.93 us  [with_dec(): lax.dot_general(g_all, dec, (((1,), (1,)), ((), ())), preferred_element_t...]
    dot_general x4 -> x8, matrix products: 1.33 us -> 2.7 us  [with_enc(): return jnp.dot(dz, enc, preferred_element_type=jnp.float32)]
  transfers between devices with their start and end apart: 34 -> 36, of which waited for: 12 -> 17; matrix products, arithmetic and copies ran while one was open for 12% -> 13% of each run, Pallas kernels for 0% -> 0%
where the time goes in v9:
time: 113 us; the launch traced here: 111 us
  starting transfers between devices  51.6 us (46%)
  waiting for transfers between devices  36.5 us (32%)
  local copies, waits for them, and re-layouts  7.4 us (7%)
  matrix products  7.33 us (6%)
  other arithmetic  6.98 us (6%)
  between operations  1.26 us (1%)
    ppermute x28, starting transfers between devices, send_pieces(): moved.append(lax.ppermute(piece, 'dict', route))  50.2 us
    ppermute x28, waiting for transfers between devices, send_pieces(): moved.append(lax.ppermute(piece, 'dict', route))  35 us
    dot_general x8, matrix products, with_dec(): lax.dot_general(g_all, dec, (((1,), (1,)), ((), ())), preferred_element_t...  3.93 us
    unnamed x42, local copies, waits for them, and re-layouts  2.99 us
    dot_general x8, matrix products, with_enc(): return jnp.dot(dz, enc, preferred_element_type=jnp.float32)  2.7 us
  transfers between devices with their start and end apart: 36, of which 17 were waited for; matrix products, arithmetic and copies ran while one was open for 13% of the time, Pallas kernels for 0%

profile of v9, /device:TPU:0, one launch (start us, length us, event | category | flops | bytes accessed | tf_op | source)
XLA Modules:
  0.0 111.1 jit_solution(14023437525984524352)
XLA Ops:
  4.5 2.9 %collective-permute-start.1 = (bf16[16,2432]{1,0:T(8,128)(2,1)}, bf16[16,2432]{1,0:T(8,128)(2,1)}, u32[]{:S(2)}, u32[]{:S(2)}) collective-permute-start(bf16[16,2432]{1,0:T(8,128)(2,1)} %get-tuple-element.11), channel_id=1, source_target_pairs={{0,2},{2,4},{4,6},{6,8},{8,10},{10,12},{12,14},{14,0},{1,3},{3,5},... | collective-permute-start | bytes 233480 | tf_op jit(solution)/shard_map/ppermute | solution.py:135
  7.5 1.6 %collective-permute-start.2 = (bf16[16,2432]{1,0:T(8,128)(2,1)}, bf16[16,2432]{1,0:T(8,128)(2,1)}, u32[]{:S(2)}, u32[]{:S(2)}) collective-permute-start(bf16[16,2432]{1,0:T(8,128)(2,1)} %get-tuple-element.12), channel_id=1, source_target_pairs={{0,4},{2,6},{4,8},{6,10},{8,12},{10,14},{12,0},{14,2},{1,5},{3,7},... | collective-permute-start | bytes 233480 | tf_op jit(solution)/shard_map/ppermute | solution.py:135
  9.1 2.6 %collective-permute-start.3 = (bf16[16,2432]{1,0:T(8,128)(2,1)}, bf16[16,2432]{1,0:T(8,128)(2,1)}, u32[]{:S(2)}, u32[]{:S(2)}) collective-permute-start(bf16[16,2432]{1,0:T(8,128)(2,1)} %get-tuple-element.13), channel_id=1, source_target_pairs={{0,6},{2,8},{4,10},{6,12},{8,14},{10,0},{12,2},{14,4},{1,7},{3,9},... | collective-permute-start | bytes 233480 | tf_op jit(solution)/shard_map/ppermute | solution.py:135
  13.6 1.5 %dynamic-slice_bitcast_fusion = (bf16[256,2304]{1,0:T(8,128)(2,1)S(1)}, bf16[256,2304]{1,0:T(8,128)(2,1)S(1)}) fusion(bf16[1,256,4608]{2,1,0:T(8,128)(2,1)} %param.11, s32[]{:T(128)S(6)} %select_n.242, bf16[1,256,4608]{2,1,0:T(8,128)(2,1)S(1)} %copy-done), kind=kLoop, calls=%fused_computation.44 | loop fusion | bytes 4718596 | tf_op jit(solution)/shard_map/dynamic_slice | solution.py:215
  15.1 1.6 %pad_maximum_fusion = bf16[512,2304]{1,0:T(8,128)(2,1)} fusion(bf16[256,2304]{1,0:T(8,128)(2,1)S(1)} %get-tuple-element.42, bf16[256,2304]{1,0:T(8,128)(2,1)S(1)} %get-tuple-element.43), kind=kLoop, calls=%fused_computation.8 | loop fusion | flops 4718592 | bytes 4718592 | tf_op jit(solution)/shard_map/concatenate | solution.py:212
  16.7 2.7 %collective-permute-start.11 = (bf16[16,2432]{1,0:T(8,128)(2,1)S(1)}, bf16[16,2432]{1,0:T(8,128)(2,1)S(1)}, u32[]{:S(2)}, u32[]{:S(2)}) collective-permute-start(bf16[16,2432]{1,0:T(8,128)(2,1)S(1)} %copy-done.5), channel_id=1, source_target_pairs={{0,10},{2,12},{4,14},{6,0},{8,2},{10,4},{12,6},{14,8},{1,11},{3,13... | collective-permute-start | bytes 233480 | tf_op jit(solution)/shard_map/ppermute | solution.py:135
  20.3 2.8 %collective-permute-done.11 = bf16[16,2432]{1,0:T(8,128)(2,1)S(1)} collective-permute-done((bf16[16,2432]{1,0:T(8,128)(2,1)S(1)}, bf16[16,2432]{1,0:T(8,128)(2,1)S(1)}, u32[]{:S(2)}, u32[]{:S(2)}) %collective-permute-start.11) | collective-permute-done | bytes 77856 | tf_op jit(solution)/shard_map/ppermute | solution.py:135
  23.2 2.2 %collective-permute-start.12 = (bf16[16,2432]{1,0:T(8,128)(2,1)S(1)}, bf16[16,2432]{1,0:T(8,128)(2,1)S(1)}, u32[]{:S(2)}, u32[]{:S(2)}) collective-permute-start(bf16[16,2432]{1,0:T(8,128)(2,1)S(1)} %copy-done.4), channel_id=1, source_target_pairs={{0,12},{2,14},{4,0},{6,2},{8,4},{10,6},{12,8},{14,10},{1,13},{3,15... | collective-permute-start | bytes 233480 | tf_op jit(solution)/shard_map/ppermute | solution.py:135
  26.3 2.2 %collective-permute-start.13 = (bf16[16,2432]{1,0:T(8,128)(2,1)S(1)}, bf16[16,2432]{1,0:T(8,128)(2,1)S(1)}, u32[]{:S(2)}, u32[]{:S(2)}) collective-permute-start(bf16[16,2432]{1,0:T(8,128)(2,1)S(1)} %get-tuple-element.9), channel_id=1, source_target_pairs={{0,14},{2,0},{4,2},{6,4},{8,6},{10,8},{12,10},{14,12},{1,15},{3,1}... | collective-permute-start | bytes 233480 | tf_op jit(solution)/shard_map/ppermute | solution.py:135
  36.6 1.9 %collective-permute-start.15 = (bf16[16,2432]{1,0:T(8,128)(2,1)S(1)}, bf16[16,2432]{1,0:T(8,128)(2,1)S(1)}, u32[]{:S(2)}, u32[]{:S(2)}) collective-permute-start(bf16[16,2432]{1,0:T(8,128)(2,1)S(1)} %get-tuple-element.36), channel_id=1, source_target_pairs={{0,6},{2,8},{4,10},{6,12},{8,14},{10,0},{12,2},{14,4},{1,7},{3,9},... | collective-permute-start | bytes 233480 | tf_op jit(solution)/shard_map/ppermute | solution.py:135
  40.3 3.9 %collective-permute-start.7 = (bf16[16,2432]{1,0:T(8,128)(2,1)S(1)}, bf16[16,2432]{1,0:T(8,128)(2,1)S(1)}, u32[]{:S(2)}, u32[]{:S(2)}) collective-permute-start(bf16[16,2432]{1,0:T(8,128)(2,1)S(1)} %get-tuple-element.25), channel_id=1, source_target_pairs={{0,14},{2,0},{4,2},{6,4},{8,6},{10,8},{12,10},{14,12},{1,15},{3,1}... | collective-permute-start | bytes 233480 | tf_op jit(solution)/shard_map/ppermute | solution.py:135
  44.1 2.2 %collective-permute-start.8 = (bf16[16,2432]{1,0:T(8,128)(2,1)S(1)}, bf16[16,2432]{1,0:T(8,128)(2,1)S(1)}, u32[]{:S(2)}, u32[]{:S(2)}) collective-permute-start(bf16[16,2432]{1,0:T(8,128)(2,1)S(1)} %get-tuple-element.26), channel_id=1, source_target_pairs={{0,12},{2,14},{4,0},{6,2},{8,4},{10,6},{12,8},{14,10},{1,13},{3,15... | collective-permute-start | bytes 233480 | tf_op jit(solution)/shard_map/ppermute | solution.py:135
  46.4 2.4 %collective-permute-done.7 = bf16[16,2432]{1,0:T(8,128)(2,1)S(1)} collective-permute-done((bf16[16,2432]{1,0:T(8,128)(2,1)S(1)}, bf16[16,2432]{1,0:T(8,128)(2,1)S(1)}, u32[]{:S(2)}, u32[]{:S(2)}) %collective-permute-start.7) | collective-permute-done | bytes 77856 | tf_op jit(solution)/shard_map/ppermute | solution.py:135
  48.8 2.2 %collective-permute-start.9 = (bf16[16,2432]{1,0:T(8,128)(2,1)S(1)}, bf16[16,2432]{1,0:T(8,128)(2,1)S(1)}, u32[]{:S(2)}, u32[]{:S(2)}) collective-permute-start(bf16[16,2432]{1,0:T(8,128)(2,1)S(1)} %get-tuple-element.27), channel_id=1, source_target_pairs={{0,10},{2,12},{4,14},{6,0},{8,2},{10,4},{12,6},{14,8},{1,11},{3,13... | collective-permute-start | bytes 233480 | tf_op jit(solution)/shard_map/ppermute | solution.py:135
  51.0 2.0 %collective-permute-start.10 = (bf16[16,2432]{1,0:T(8,128)(2,1)S(1)}, bf16[16,2432]{1,0:T(8,128)(2,1)S(1)}, u32[]{:S(2)}, u32[]{:S(2)}) collective-permute-start(bf16[16,2432]{1,0:T(8,128)(2,1)S(1)} %get-tuple-element.24), channel_id=1, source_target_pairs={{0,8},{2,10},{4,12},{6,14},{8,0},{10,2},{12,4},{14,6},{1,9},{3,11}... | collective-permute-start | bytes 233480 | tf_op jit(solution)/shard_map/ppermute | solution.py:135
  54.4 4.2 %collective-permute-done.10 = bf16[16,2432]{1,0:T(8,128)(2,1)S(1)} collective-permute-done((bf16[16,2432]{1,0:T(8,128)(2,1)S(1)}, bf16[16,2432]{1,0:T(8,128)(2,1)S(1)}, u32[]{:S(2)}, u32[]{:S(2)}) %collective-permute-start.10) | collective-permute-done | bytes 77856 | tf_op jit(solution)/shard_map/ppermute | solution.py:135
  59.8 2.7 %collective-permute-start.20 = (bf16[16,2432]{1,0:T(8,128)(2,1)S(1)}, bf16[16,2432]{1,0:T(8,128)(2,1)S(1)}, u32[]{:S(2)}, u32[]{:S(2)}) collective-permute-start(bf16[16,2432]{1,0:T(8,128)(2,1)S(1)} %get-tuple-element.4), channel_id=1, source_target_pairs={{0,6},{2,8},{4,10},{6,12},{8,14},{10,0},{12,2},{14,4},{1,7},{3,9},... | collective-permute-start | bytes 233480 | tf_op jit(solution)/shard_map/ppermute | solution.py:135
  62.5 2.0 %collective-permute-start.21 = (bf16[16,2432]{1,0:T(8,128)(2,1)S(1)}, bf16[16,2432]{1,0:T(8,128)(2,1)S(1)}, u32[]{:S(2)}, u32[]{:S(2)}) collective-permute-start(bf16[16,2432]{1,0:T(8,128)(2,1)S(1)} %get-tuple-element.3), channel_id=1, source_target_pairs={{0,8},{2,10},{4,12},{6,14},{8,0},{10,2},{12,4},{14,6},{1,9},{3,11}... | collective-permute-start | bytes 233480 | tf_op jit(solution)/shard_map/ppermute | solution.py:135
  64.5 2.5 %collective-permute-done.18 = bf16[16,2432]{1,0:T(8,128)(2,1)S(1)} collective-permute-done((bf16[16,2432]{1,0:T(8,128)(2,1)S(1)}, bf16[16,2432]{1,0:T(8,128)(2,1)S(1)}, u32[]{:S(2)}, u32[]{:S(2)}) %collective-permute-start.18) | collective-permute-done | bytes 77856 | tf_op jit(solution)/shard_map/ppermute | solution.py:135
  67.5 5.3 %collective-permute-done.20 = bf16[16,2432]{1,0:T(8,128)(2,1)S(1)} collective-permute-done((bf16[16,2432]{1,0:T(8,128)(2,1)S(1)}, bf16[16,2432]{1,0:T(8,128)(2,1)S(1)}, u32[]{:S(2)}, u32[]{:S(2)}) %collective-permute-start.20) | collective-permute-done | bytes 77856 | tf_op jit(solution)/shard_map/ppermute | solution.py:135
  73.7 1.4 %collective-permute-done.27 = bf16[16,2432]{1,0:T(8,128)(2,1)S(1)} collective-permute-done((bf16[16,2432]{1,0:T(8,128)(2,1)S(1)}, bf16[16,2432]{1,0:T(8,128)(2,1)S(1)}, u32[]{:S(2)}, u32[]{:S(2)}) %collective-permute-start.27) | collective-permute-done | bytes 77856 | tf_op jit(solution)/shard_map/ppermute | solution.py:135
  75.7 1.5 %collective-permute-done.29 = bf16[16,2432]{1,0:T(8,128)(2,1)S(1)} collective-permute-done((bf16[16,2432]{1,0:T(8,128)(2,1)S(1)}, bf16[16,2432]{1,0:T(8,128)(2,1)S(1)}, u32[]{:S(2)}, u32[]{:S(2)}) %collective-permute-start.29) | collective-permute-done | bytes 77856 | tf_op jit(solution)/shard_map/ppermute | solution.py:135
  80.3 2.3 %collective-permute-start.31 = (bf16[16,2432]{1,0:T(8,128)(2,1)S(1)}, bf16[16,2432]{1,0:T(8,128)(2,1)S(1)}, u32[]{:S(2)}, u32[]{:S(2)}) collective-permute-start(bf16[16,2432]{1,0:T(8,128)(2,1)S(1)} %get-tuple-element.33), channel_id=1, source_target_pairs={{0,6},{2,8},{4,10},{6,12},{8,14},{10,0},{12,2},{14,4},{1,7},{3,9},... | collective-permute-start | bytes 233480 | tf_op jit(solution)/shard_map/ppermute | solution.py:135
  82.6 1.9 %collective-permute-start.32 = (bf16[16,2432]{1,0:T(8,128)(2,1)S(1)}, bf16[16,2432]{1,0:T(8,128)(2,1)S(1)}, u32[]{:S(2)}, u32[]{:S(2)}) collective-permute-start(bf16[16,2432]{1,0:T(8,128)(2,1)S(1)} %get-tuple-element.34), channel_id=1, source_target_pairs={{0,4},{2,6},{4,8},{6,10},{8,12},{10,14},{12,0},{14,2},{1,5},{3,7},... | collective-permute-start | bytes 233480 | tf_op jit(solution)/shard_map/ppermute | solution.py:135
  84.5 1.4 %collective-permute-start.33 = (bf16[16,2432]{1,0:T(8,128)(2,1)S(1)}, bf16[16,2432]{1,0:T(8,128)(2,1)S(1)}, u32[]{:S(2)}, u32[]{:S(2)}) collective-permute-start(bf16[16,2432]{1,0:T(8,128)(2,1)S(1)} %get-tuple-element.32), channel_id=1, source_target_pairs={{0,2},{2,4},{4,6},{6,8},{8,10},{10,12},{12,14},{14,0},{1,3},{3,5},... | collective-permute-start | bytes 233480 | tf_op jit(solution)/shard_map/ppermute | solution.py:135
  86.7 3.4 %collective-permute-start.23 = (bf16[16,2432]{1,0:T(8,128)(2,1)S(1)}, bf16[16,2432]{1,0:T(8,128)(2,1)S(1)}, u32[]{:S(2)}, u32[]{:S(2)}) collective-permute-start(bf16[16,2432]{1,0:T(8,128)(2,1)S(1)} %get-tuple-element.21), channel_id=1, source_target_pairs={{0,14},{2,0},{4,2},{6,4},{8,6},{10,8},{12,10},{14,12},{1,15},{3,1}... | collective-permute-start | bytes 233480 | tf_op jit(solution)/shard_map/ppermute | solution.py:135
  90.1 3.1 %collective-permute-done.23 = bf16[16,2432]{1,0:T(8,128)(2,1)S(1)} collective-permute-done((bf16[16,2432]{1,0:T(8,128)(2,1)S(1)}, bf16[16,2432]{1,0:T(8,128)(2,1)S(1)}, u32[]{:S(2)}, u32[]{:S(2)}) %collective-permute-start.23) | collective-permute-done | bytes 77856 | tf_op jit(solution)/shard_map/ppermute | solution.py:135
  93.9 3.7 %collective-permute-done.24 = bf16[16,2432]{1,0:T(8,128)(2,1)S(1)} collective-permute-done((bf16[16,2432]{1,0:T(8,128)(2,1)S(1)}, bf16[16,2432]{1,0:T(8,128)(2,1)S(1)}, u32[]{:S(2)}, u32[]{:S(2)}) %collective-permute-start.24) | collective-permute-done | bytes 77856 | tf_op jit(solution)/shard_map/ppermute | solution.py:135
  97.6 2.6 %collective-permute-start.25 = (bf16[16,2432]{1,0:T(8,128)(2,1)S(1)}, bf16[16,2432]{1,0:T(8,128)(2,1)S(1)}, u32[]{:S(2)}, u32[]{:S(2)}) collective-permute-start(bf16[16,2432]{1,0:T(8,128)(2,1)S(1)} %get-tuple-element.23), channel_id=1, source_target_pairs={{0,10},{2,12},{4,14},{6,0},{8,2},{10,4},{12,6},{14,8},{1,11},{3,13... | collective-permute-start | bytes 233480 | tf_op jit(solution)/shard_map/ppermute | solution.py:135
  100.2 2.7 %collective-permute-done.25 = bf16[16,2432]{1,0:T(8,128)(2,1)S(1)} collective-permute-done((bf16[16,2432]{1,0:T(8,128)(2,1)S(1)}, bf16[16,2432]{1,0:T(8,128)(2,1)S(1)}, u32[]{:S(2)}, u32[]{:S(2)}) %collective-permute-start.25) | collective-permute-done | bytes 77856 | tf_op jit(solution)/shard_map/ppermute | solution.py:135
  102.9 3.5 %collective-permute-start.26 = (bf16[16,2432]{1,0:T(8,128)(2,1)S(1)}, bf16[16,2432]{1,0:T(8,128)(2,1)S(1)}, u32[]{:S(2)}, u32[]{:S(2)}) collective-permute-start(bf16[16,2432]{1,0:T(8,128)(2,1)S(1)} %get-tuple-element.20), channel_id=1, source_target_pairs={{0,8},{2,10},{4,12},{6,14},{8,0},{10,2},{12,4},{14,6},{1,9},{3,11}... | collective-permute-start | bytes 233480 | tf_op jit(solution)/shard_map/ppermute | solution.py:135
  106.3 2.4 %collective-permute-done.26 = bf16[16,2432]{1,0:T(8,128)(2,1)S(1)} collective-permute-done((bf16[16,2432]{1,0:T(8,128)(2,1)S(1)}, bf16[16,2432]{1,0:T(8,128)(2,1)S(1)}, u32[]{:S(2)}, u32[]{:S(2)}) %collective-permute-start.26) | collective-permute-done | bytes 77856 | tf_op jit(solution)/shard_map/ppermute | solution.py:135
  (164 shorter events, 28.8 us)
Async XLA Ops:
  4.5 18.6 %collective-permute-start.1 = (bf16[16,2432]{1,0:T(8,128)(2,1)}, bf16[16,2432]{1,0:T(8,128)(2,1)}, u32[]{:S(2)}, u32[]{:S(2)}) collective-permute-start(bf16[16,2432]{1,0:T(8,128)(2,1)} %get-tuple-element.11), channel_id=1, source_target_pairs={{0,2},{2,4},{4,6},{6,8},{8,10},{10,12},{12,14},{14,0},{1,3},{3,5},... | collective-permute-start | bytes 233480 | tf_op jit(solution)/shard_map/ppermute | solution.py:135
  7.5 18.8 %collective-permute-start.2 = (bf16[16,2432]{1,0:T(8,128)(2,1)}, bf16[16,2432]{1,0:T(8,128)(2,1)}, u32[]{:S(2)}, u32[]{:S(2)}) collective-permute-start(bf16[16,2432]{1,0:T(8,128)(2,1)} %get-tuple-element.12), channel_id=1, source_target_pairs={{0,4},{2,6},{4,8},{6,10},{8,12},{10,14},{12,0},{14,2},{1,5},{3,7},... | collective-permute-start | bytes 233480 | tf_op jit(solution)/shard_map/ppermute | solution.py:135
  9.1 20.3 %collective-permute-start.3 = (bf16[16,2432]{1,0:T(8,128)(2,1)}, bf16[16,2432]{1,0:T(8,128)(2,1)}, u32[]{:S(2)}, u32[]{:S(2)}) collective-permute-start(bf16[16,2432]{1,0:T(8,128)(2,1)} %get-tuple-element.13), channel_id=1, source_target_pairs={{0,6},{2,8},{4,10},{6,12},{8,14},{10,0},{12,2},{14,4},{1,7},{3,9},... | collective-permute-start | bytes 233480 | tf_op jit(solution)/shard_map/ppermute | solution.py:135
  11.6 20.0 %collective-permute-start.4 = (bf16[16,2432]{1,0:T(8,128)(2,1)S(1)}, bf16[16,2432]{1,0:T(8,128)(2,1)}, u32[]{:S(2)}, u32[]{:S(2)}) collective-permute-start(bf16[16,2432]{1,0:T(8,128)(2,1)S(1)} %get-tuple-element.14), channel_id=1, source_target_pairs={{0,8},{2,10},{4,12},{6,14},{8,0},{10,2},{12,4},{14,6},{1,9},{3,11}... | collective-permute-start | bytes 233480 | tf_op jit(solution)/shard_map/ppermute | solution.py:135
  16.7 6.4 %collective-permute-start.11 = (bf16[16,2432]{1,0:T(8,128)(2,1)S(1)}, bf16[16,2432]{1,0:T(8,128)(2,1)S(1)}, u32[]{:S(2)}, u32[]{:S(2)}) collective-permute-start(bf16[16,2432]{1,0:T(8,128)(2,1)S(1)} %copy-done.5), channel_id=1, source_target_pairs={{0,10},{2,12},{4,14},{6,0},{8,2},{10,4},{12,6},{14,8},{1,11},{3,13... | collective-permute-start | bytes 233480 | tf_op jit(solution)/shard_map/ppermute | solution.py:135
  23.1 9.4 %collective-permute-start.5 = (bf16[512,2304]{1,0:T(8,128)(2,1)}, bf16[512,2304]{1,0:T(8,128)(2,1)S(1)}, u32[]{:S(2)}, u32[]{:S(2)}) collective-permute-start(bf16[512,2304]{1,0:T(8,128)(2,1)} %pad_maximum_fusion), channel_id=1, source_target_pairs={{0,1},{1,0},{2,3},{3,2},{4,5},{5,4},{6,7},{7,6},{8,9},{9,8},{10,11... | collective-permute-start | bytes 7077896 | tf_op jit(solution)/shard_map/ppermute | solution.py:116
  23.2 7.1 %collective-permute-start.12 = (bf16[16,2432]{1,0:T(8,128)(2,1)S(1)}, bf16[16,2432]{1,0:T(8,128)(2,1)S(1)}, u32[]{:S(2)}, u32[]{:S(2)}) collective-permute-start(bf16[16,2432]{1,0:T(8,128)(2,1)S(1)} %copy-done.4), channel_id=1, source_target_pairs={{0,12},{2,14},{4,0},{6,2},{8,4},{10,6},{12,8},{14,10},{1,13},{3,15... | collective-permute-start | bytes 233480 | tf_op jit(solution)/shard_map/ppermute | solution.py:135
  26.3 5.2 %collective-permute-start.13 = (bf16[16,2432]{1,0:T(8,128)(2,1)S(1)}, bf16[16,2432]{1,0:T(8,128)(2,1)S(1)}, u32[]{:S(2)}, u32[]{:S(2)}) collective-permute-start(bf16[16,2432]{1,0:T(8,128)(2,1)S(1)} %get-tuple-element.9), channel_id=1, source_target_pairs={{0,14},{2,0},{4,2},{6,4},{8,6},{10,8},{12,10},{14,12},{1,15},{3,1}... | collective-permute-start | bytes 233480 | tf_op jit(solution)/shard_map/ppermute | solution.py:135
  34.7 4.8 %collective-permute-start.6 = (f32[80,384]{1,0:T(8,128)S(1)}, f32[80,384]{1,0:T(8,128)S(1)}, u32[]{:S(2)}, u32[]{:S(2)}) collective-permute-start(f32[80,384]{1,0:T(8,128)S(1)} %pad_maximum_fusion.1), channel_id=1, source_target_pairs={{0,1},{1,0},{2,3},{3,2},{4,5},{5,4},{6,7},{7,6},{8,9},{9,8},{10,11... | collective-permute-start | bytes 368648 | tf_op jit(solution)/shard_map/ppermute | solution.py:116
  36.6 21.9 %collective-permute-start.15 = (bf16[16,2432]{1,0:T(8,128)(2,1)S(1)}, bf16[16,2432]{1,0:T(8,128)(2,1)S(1)}, u32[]{:S(2)}, u32[]{:S(2)}) collective-permute-start(bf16[16,2432]{1,0:T(8,128)(2,1)S(1)} %get-tuple-element.36), channel_id=1, source_target_pairs={{0,6},{2,8},{4,10},{6,12},{8,14},{10,0},{12,2},{14,4},{1,7},{3,9},... | collective-permute-start | bytes 233480 | tf_op jit(solution)/shard_map/ppermute | solution.py:135
  38.6 20.0 %collective-permute-start.16 = (bf16[16,2432]{1,0:T(8,128)(2,1)S(1)}, bf16[16,2432]{1,0:T(8,128)(2,1)S(1)}, u32[]{:S(2)}, u32[]{:S(2)}) collective-permute-start(bf16[16,2432]{1,0:T(8,128)(2,1)S(1)} %get-tuple-element.37), channel_id=1, source_target_pairs={{0,4},{2,6},{4,8},{6,10},{8,12},{10,14},{12,0},{14,2},{1,5},{3,7},... | collective-permute-start | bytes 233480 | tf_op jit(solution)/shard_map/ppermute | solution.py:135
  38.6 20.1 %collective-permute-start.17 = (bf16[16,2432]{1,0:T(8,128)(2,1)S(1)}, bf16[16,2432]{1,0:T(8,128)(2,1)S(1)}, u32[]{:S(2)}, u32[]{:S(2)}) collective-permute-start(bf16[16,2432]{1,0:T(8,128)(2,1)S(1)} %get-tuple-element.35), channel_id=1, source_target_pairs={{0,2},{2,4},{4,6},{6,8},{8,10},{10,12},{12,14},{14,0},{1,3},{3,5},... | collective-permute-start | bytes 233480 | tf_op jit(solution)/shard_map/ppermute | solution.py:135
  40.3 8.5 %collective-permute-start.7 = (bf16[16,2432]{1,0:T(8,128)(2,1)S(1)}, bf16[16,2432]{1,0:T(8,128)(2,1)S(1)}, u32[]{:S(2)}, u32[]{:S(2)}) collective-permute-start(bf16[16,2432]{1,0:T(8,128)(2,1)S(1)} %get-tuple-element.25), channel_id=1, source_target_pairs={{0,14},{2,0},{4,2},{6,4},{8,6},{10,8},{12,10},{14,12},{1,15},{3,1}... | collective-permute-start | bytes 233480 | tf_op jit(solution)/shard_map/ppermute | solution.py:135
  44.1 6.8 %collective-permute-start.8 = (bf16[16,2432]{1,0:T(8,128)(2,1)S(1)}, bf16[16,2432]{1,0:T(8,128)(2,1)S(1)}, u32[]{:S(2)}, u32[]{:S(2)}) collective-permute-start(bf16[16,2432]{1,0:T(8,128)(2,1)S(1)} %get-tuple-element.26), channel_id=1, source_target_pairs={{0,12},{2,14},{4,0},{6,2},{8,4},{10,6},{12,8},{14,10},{1,13},{3,15... | collective-permute-start | bytes 233480 | tf_op jit(solution)/shard_map/ppermute | solution.py:135
  48.8 5.6 %collective-permute-start.9 = (bf16[16,2432]{1,0:T(8,128)(2,1)S(1)}, bf16[16,2432]{1,0:T(8,128)(2,1)S(1)}, u32[]{:S(2)}, u32[]{:S(2)}) collective-permute-start(bf16[16,2432]{1,0:T(8,128)(2,1)S(1)} %get-tuple-element.27), channel_id=1, source_target_pairs={{0,10},{2,12},{4,14},{6,0},{8,2},{10,4},{12,6},{14,8},{1,11},{3,13... | collective-permute-start | bytes 233480 | tf_op jit(solution)/shard_map/ppermute | solution.py:135
  51.0 7.6 %collective-permute-start.10 = (bf16[16,2432]{1,0:T(8,128)(2,1)S(1)}, bf16[16,2432]{1,0:T(8,128)(2,1)S(1)}, u32[]{:S(2)}, u32[]{:S(2)}) collective-permute-start(bf16[16,2432]{1,0:T(8,128)(2,1)S(1)} %get-tuple-element.24), channel_id=1, source_target_pairs={{0,8},{2,10},{4,12},{6,14},{8,0},{10,2},{12,4},{14,6},{1,9},{3,11}... | collective-permute-start | bytes 233480 | tf_op jit(solution)/shard_map/ppermute | solution.py:135
  58.9 8.1 %collective-permute-start.18 = (bf16[16,2432]{1,0:T(8,128)(2,1)S(1)}, bf16[16,2432]{1,0:T(8,128)(2,1)S(1)}, u32[]{:S(2)}, u32[]{:S(2)}) collective-permute-start(bf16[16,2432]{1,0:T(8,128)(2,1)S(1)} %get-tuple-element.6), channel_id=1, source_target_pairs={{0,2},{2,4},{4,6},{6,8},{8,10},{10,12},{12,14},{14,0},{1,3},{3,5},... | collective-permute-start | bytes 233480 | tf_op jit(solution)/shard_map/ppermute | solution.py:135
  59.6 50.5 %collective-permute-start.35 = (bf16[16,2304]{1,0:T(8,128)(2,1)S(1)}, bf16[16,2304]{1,0:T(8,128)(2,1)S(1)}, u32[]{:S(2)}, u32[]{:S(2)}) collective-permute-start(bf16[16,2304]{1,0:T(8,128)(2,1)S(1)} %add_convert_fusion.1), channel_id=1, source_target_pairs={{0,1},{1,0},{2,3},{3,2},{4,5},{5,4},{6,7},{7,6},{8,9},{9,8},{10,11... | collective-permute-start | bytes 221192 | tf_op jit(solution)/shard_map/ppermute | solution.py:116
  59.7 7.3 %collective-permute-start.19 = (bf16[16,2432]{1,0:T(8,128)(2,1)S(1)}, bf16[16,2432]{1,0:T(8,128)(2,1)S(1)}, u32[]{:S(2)}, u32[]{:S(2)}) collective-permute-start(bf16[16,2432]{1,0:T(8,128)(2,1)S(1)} %get-tuple-element.5), channel_id=1, source_target_pairs={{0,4},{2,6},{4,8},{6,10},{8,12},{10,14},{12,0},{14,2},{1,5},{3,7},... | collective-permute-start | bytes 233480 | tf_op jit(solution)/shard_map/ppermute | solution.py:135
  59.8 13.0 %collective-permute-start.20 = (bf16[16,2432]{1,0:T(8,128)(2,1)S(1)}, bf16[16,2432]{1,0:T(8,128)(2,1)S(1)}, u32[]{:S(2)}, u32[]{:S(2)}) collective-permute-start(bf16[16,2432]{1,0:T(8,128)(2,1)S(1)} %get-tuple-element.4), channel_id=1, source_target_pairs={{0,6},{2,8},{4,10},{6,12},{8,14},{10,0},{12,2},{14,4},{1,7},{3,9},... | collective-permute-start | bytes 233480 | tf_op jit(solution)/shard_map/ppermute | solution.py:135
  62.5 10.6 %collective-permute-start.21 = (bf16[16,2432]{1,0:T(8,128)(2,1)S(1)}, bf16[16,2432]{1,0:T(8,128)(2,1)S(1)}, u32[]{:S(2)}, u32[]{:S(2)}) collective-permute-start(bf16[16,2432]{1,0:T(8,128)(2,1)S(1)} %get-tuple-element.3), channel_id=1, source_target_pairs={{0,8},{2,10},{4,12},{6,14},{8,0},{10,2},{12,4},{14,6},{1,9},{3,11}... | collective-permute-start | bytes 233480 | tf_op jit(solution)/shard_map/ppermute | solution.py:135
  67.0 8.1 %collective-permute-start.27 = (bf16[16,2432]{1,0:T(8,128)(2,1)S(1)}, bf16[16,2432]{1,0:T(8,128)(2,1)S(1)}, u32[]{:S(2)}, u32[]{:S(2)}) collective-permute-start(bf16[16,2432]{1,0:T(8,128)(2,1)S(1)} %get-tuple-element.7), channel_id=1, source_target_pairs={{0,10},{2,12},{4,14},{6,0},{8,2},{10,4},{12,6},{14,8},{1,11},{3,13... | collective-permute-start | bytes 233480 | tf_op jit(solution)/shard_map/ppermute | solution.py:135
  67.0 8.6 %collective-permute-start.28 = (bf16[16,2432]{1,0:T(8,128)(2,1)S(1)}, bf16[16,2432]{1,0:T(8,128)(2,1)S(1)}, u32[]{:S(2)}, u32[]{:S(2)}) collective-permute-start(bf16[16,2432]{1,0:T(8,128)(2,1)S(1)} %get-tuple-element.8), channel_id=1, source_target_pairs={{0,12},{2,14},{4,0},{6,2},{8,4},{10,6},{12,8},{14,10},{1,13},{3,15... | collective-permute-start | bytes 233480 | tf_op jit(solution)/shard_map/ppermute | solution.py:135
  72.8 4.4 %collective-permute-start.29 = (bf16[16,2432]{1,0:T(8,128)(2,1)S(1)}, bf16[16,2432]{1,0:T(8,128)(2,1)S(1)}, u32[]{:S(2)}, u32[]{:S(2)}) collective-permute-start(bf16[16,2432]{1,0:T(8,128)(2,1)S(1)} %get-tuple-element.2), channel_id=1, source_target_pairs={{0,14},{2,0},{4,2},{6,4},{8,6},{10,8},{12,10},{14,12},{1,15},{3,1}... | collective-permute-start | bytes 233480 | tf_op jit(solution)/shard_map/ppermute | solution.py:135
  78.3 7.6 %collective-permute-start.22 = (f32[80,384]{1,0:T(8,128)S(1)}, f32[80,384]{1,0:T(8,128)S(1)}, u32[]{:S(2)}, u32[]{:S(2)}) collective-permute-start(f32[80,384]{1,0:T(8,128)S(1)} %pad_maximum_fusion.2), channel_id=1, source_target_pairs={{0,1},{1,0},{2,3},{3,2},{4,5},{5,4},{6,7},{7,6},{8,9},{9,8},{10,11... | collective-permute-start | bytes 368648 | tf_op jit(solution)/shard_map/ppermute | solution.py:116
  80.3 28.4 %collective-permute-start.31 = (bf16[16,2432]{1,0:T(8,128)(2,1)S(1)}, bf16[16,2432]{1,0:T(8,128)(2,1)S(1)}, u32[]{:S(2)}, u32[]{:S(2)}) collective-permute-start(bf16[16,2432]{1,0:T(8,128)(2,1)S(1)} %get-tuple-element.33), channel_id=1, source_target_pairs={{0,6},{2,8},{4,10},{6,12},{8,14},{10,0},{12,2},{14,4},{1,7},{3,9},... | collective-permute-start | bytes 233480 | tf_op jit(solution)/shard_map/ppermute | solution.py:135
  82.6 26.1 %collective-permute-start.32 = (bf16[16,2432]{1,0:T(8,128)(2,1)S(1)}, bf16[16,2432]{1,0:T(8,128)(2,1)S(1)}, u32[]{:S(2)}, u32[]{:S(2)}) collective-permute-start(bf16[16,2432]{1,0:T(8,128)(2,1)S(1)} %get-tuple-element.34), channel_id=1, source_target_pairs={{0,4},{2,6},{4,8},{6,10},{8,12},{10,14},{12,0},{14,2},{1,5},{3,7},... | collective-permute-start | bytes 233480 | tf_op jit(solution)/shard_map/ppermute | solution.py:135
  84.5 24.2 %collective-permute-start.33 = (bf16[16,2432]{1,0:T(8,128)(2,1)S(1)}, bf16[16,2432]{1,0:T(8,128)(2,1)S(1)}, u32[]{:S(2)}, u32[]{:S(2)}) collective-permute-start(bf16[16,2432]{1,0:T(8,128)(2,1)S(1)} %get-tuple-element.32), channel_id=1, source_target_pairs={{0,2},{2,4},{4,6},{6,8},{8,10},{10,12},{12,14},{14,0},{1,3},{3,5},... | collective-permute-start | bytes 233480 | tf_op jit(solution)/shard_map/ppermute | solution.py:135
  86.7 6.5 %collective-permute-start.23 = (bf16[16,2432]{1,0:T(8,128)(2,1)S(1)}, bf16[16,2432]{1,0:T(8,128)(2,1)S(1)}, u32[]{:S(2)}, u32[]{:S(2)}) collective-permute-start(bf16[16,2432]{1,0:T(8,128)(2,1)S(1)} %get-tuple-element.21), channel_id=1, source_target_pairs={{0,14},{2,0},{4,2},{6,4},{8,6},{10,8},{12,10},{14,12},{1,15},{3,1}... | collective-permute-start | bytes 233480 | tf_op jit(solution)/shard_map/ppermute | solution.py:135
  93.2 4.4 %collective-permute-start.24 = (bf16[16,2432]{1,0:T(8,128)(2,1)S(1)}, bf16[16,2432]{1,0:T(8,128)(2,1)S(1)}, u32[]{:S(2)}, u32[]{:S(2)}) collective-permute-start(bf16[16,2432]{1,0:T(8,128)(2,1)S(1)} %get-tuple-element.22), channel_id=1, source_target_pairs={{0,12},{2,14},{4,0},{6,2},{8,4},{10,6},{12,8},{14,10},{1,13},{3,15... | collective-permute-start | bytes 233480 | tf_op jit(solution)/shard_map/ppermute | solution.py:135
  97.6 5.3 %collective-permute-start.25 = (bf16[16,2432]{1,0:T(8,128)(2,1)S(1)}, bf16[16,2432]{1,0:T(8,128)(2,1)S(1)}, u32[]{:S(2)}, u32[]{:S(2)}) collective-permute-start(bf16[16,2432]{1,0:T(8,128)(2,1)S(1)} %get-tuple-element.23), channel_id=1, source_target_pairs={{0,10},{2,12},{4,14},{6,0},{8,2},{10,4},{12,6},{14,8},{1,11},{3,13... | collective-permute-start | bytes 233480 | tf_op jit(solution)/shard_map/ppermute | solution.py:135
  102.9 5.8 %collective-permute-start.26 = (bf16[16,2432]{1,0:T(8,128)(2,1)S(1)}, bf16[16,2432]{1,0:T(8,128)(2,1)S(1)}, u32[]{:S(2)}, u32[]{:S(2)}) collective-permute-start(bf16[16,2432]{1,0:T(8,128)(2,1)S(1)} %get-tuple-element.20), channel_id=1, source_target_pairs={{0,8},{2,10},{4,12},{6,14},{8,0},{10,2},{12,4},{14,6},{1,9},{3,11}... | collective-permute-start | bytes 233480 | tf_op jit(solution)/shard_map/ppermute | solution.py:135
  (13 other events, 81.9 us)

commit v10 on v5

--- a/solution.py
+++ b/solution.py
@@ -139,8 +139,9 @@
     at_rel = (rel[:, :, None] == shifts[None, None, :]).astype(jnp.bfloat16)
     act_grid = acts_l.reshape(rows, listed, block)
     live = (act_grid > 0).astype(jnp.bfloat16) * (1 + within).astype(jnp.bfloat16)[:, :, None]
-    placed = jnp.einsum(
-        "rks,rkj->srj", at_rel, live, preferred_element_type=jnp.float32
+    hit = rel[None, :, :, None] == shifts[:, None, None, None]
+    placed = jnp.sum(
+        jnp.where(hit, live[None], jnp.zeros_like(live[None])), axis=2
     ).astype(jnp.bfloat16)
     sent = jnp.concatenate(
         [jnp.broadcast_to(g_half[None], (peers, rows, half)), placed], axis=-1

time: 94.1 us -> 94.1 us (level)
  no operation moved by 1% of the time
where the time goes in v10:
time: 94.1 us; the launch traced here: 93.6 us
  starting transfers between devices  54.6 us (58%)
  waiting for transfers between devices  20 us (21%)
  local copies, waits for them, and re-layouts  8.28 us (9%)
  other arithmetic  5.68 us (6%)
  matrix products  3.93 us (4%)
  between operations  1.12 us (1%)
    ppermute x28, starting transfers between devices, exchange(): moved.append(lax.ppermute(parts[shift], 'dict', route))  53.1 us
    ppermute x28, waiting for transfers between devices, exchange(): moved.append(lax.ppermute(parts[shift], 'dict', route))  16.5 us
    unnamed x38, local copies, waits for them, and re-layouts  4.79 us
    ppermute x6, waiting for transfers between devices, swap_cores(): return lax.ppermute(block, 'section', [(0, 1), (1, 0)])  3.58 us
    dot_general x4, matrix products, with_dec(): lax.dot_general(g_all, dec, (((1,), (1,)), ((), ())), preferred_element_t...  2.18 us
  transfers between devices with their start and end apart: 34, of which 12 were waited for; matrix products, arithmetic and copies ran while one was open for 12% of the time, Pallas kernels for 0%

profile of v10, /device:TPU:0, one launch (start us, length us, event | category | flops | bytes accessed | tf_op | source)
XLA Modules:
  0.0 93.6 jit_solution(9834841532702571075)
XLA Ops:
  4.4 2.9 %collective-permute-start.1 = (bf16[16,2432]{1,0:T(8,128)(2,1)}, bf16[16,2432]{1,0:T(8,128)(2,1)}, u32[]{:S(2)}, u32[]{:S(2)}) collective-permute-start(bf16[16,2432]{1,0:T(8,128)(2,1)} %get-tuple-element.31), channel_id=1, source_target_pairs={{0,2},{2,4},{4,6},{6,8},{8,10},{10,12},{12,14},{14,0},{1,3},{3,5},... | collective-permute-start | bytes 233480 | tf_op jit(solution)/shard_map/ppermute | solution.py:124
  7.4 1.6 %collective-permute-start.2 = (bf16[16,2432]{1,0:T(8,128)(2,1)S(1)}, bf16[16,2432]{1,0:T(8,128)(2,1)}, u32[]{:S(2)}, u32[]{:S(2)}) collective-permute-start(bf16[16,2432]{1,0:T(8,128)(2,1)S(1)} %get-tuple-element.32), channel_id=1, source_target_pairs={{0,4},{2,6},{4,8},{6,10},{8,12},{10,14},{12,0},{14,2},{1,5},{3,7},... | collective-permute-start | bytes 233480 | tf_op jit(solution)/shard_map/ppermute | solution.py:124
  9.0 2.6 %collective-permute-start.3 = (bf16[16,2432]{1,0:T(8,128)(2,1)S(1)}, bf16[16,2432]{1,0:T(8,128)(2,1)}, u32[]{:S(2)}, u32[]{:S(2)}) collective-permute-start(bf16[16,2432]{1,0:T(8,128)(2,1)S(1)} %get-tuple-element.33), channel_id=1, source_target_pairs={{0,6},{2,8},{4,10},{6,12},{8,14},{10,0},{12,2},{14,4},{1,7},{3,9},... | collective-permute-start | bytes 233480 | tf_op jit(solution)/shard_map/ppermute | solution.py:124
  11.5 1.2 %collective-permute-start.4 = (bf16[16,2432]{1,0:T(8,128)(2,1)S(1)}, bf16[16,2432]{1,0:T(8,128)(2,1)}, u32[]{:S(2)}, u32[]{:S(2)}) collective-permute-start(bf16[16,2432]{1,0:T(8,128)(2,1)S(1)} %get-tuple-element.34), channel_id=1, source_target_pairs={{0,8},{2,10},{4,12},{6,14},{8,0},{10,2},{12,4},{14,6},{1,9},{3,11}... | collective-permute-start | bytes 233480 | tf_op jit(solution)/shard_map/ppermute | solution.py:124
  12.7 2.6 %collective-permute-start.5 = (bf16[16,2432]{1,0:T(8,128)(2,1)S(1)}, bf16[16,2432]{1,0:T(8,128)(2,1)}, u32[]{:S(2)}, u32[]{:S(2)}) collective-permute-start(bf16[16,2432]{1,0:T(8,128)(2,1)S(1)} %get-tuple-element.29), channel_id=1, source_target_pairs={{0,10},{2,12},{4,14},{6,0},{8,2},{10,4},{12,6},{14,8},{1,11},{3,13... | collective-permute-start | bytes 233480 | tf_op jit(solution)/shard_map/ppermute | solution.py:124
  15.4 1.5 %dynamic-slice_bitcast_fusion = (bf16[256,2304]{1,0:T(8,128)(2,1)S(1)}, bf16[256,2304]{1,0:T(8,128)(2,1)S(1)}) fusion(bf16[1,256,4608]{2,1,0:T(8,128)(2,1)} %param.11, s32[]{:T(128)S(6)} %select_n.207, bf16[1,256,4608]{2,1,0:T(8,128)(2,1)S(1)} %copy-done), kind=kLoop, calls=%fused_computation.48 | loop fusion | bytes 4718596 | tf_op jit(solution)/shard_map/dynamic_slice | solution.py:197
  16.9 1.6 %pad_maximum_fusion = bf16[512,2304]{1,0:T(8,128)(2,1)} fusion(bf16[256,2304]{1,0:T(8,128)(2,1)S(1)} %get-tuple-element.40, bf16[256,2304]{1,0:T(8,128)(2,1)S(1)} %get-tuple-element.41), kind=kLoop, calls=%fused_computation.4 | loop fusion | flops 4718592 | bytes 4718592 | tf_op jit(solution)/shard_map/concatenate | solution.py:194
  18.5 1.4 %collective-permute-start.6 = (bf16[16,2432]{1,0:T(8,128)(2,1)S(1)}, bf16[16,2432]{1,0:T(8,128)(2,1)S(1)}, u32[]{:S(2)}, u32[]{:S(2)}) collective-permute-start(bf16[16,2432]{1,0:T(8,128)(2,1)S(1)} %get-tuple-element.35), channel_id=1, source_target_pairs={{0,12},{2,14},{4,0},{6,2},{8,4},{10,6},{12,8},{14,10},{1,13},{3,15... | collective-permute-start | bytes 233480 | tf_op jit(solution)/shard_map/ppermute | solution.py:124
  20.8 1.5 %collective-permute-start.7 = (bf16[16,2432]{1,0:T(8,128)(2,1)S(1)}, bf16[16,2432]{1,0:T(8,128)(2,1)S(1)}, u32[]{:S(2)}, u32[]{:S(2)}) collective-permute-start(bf16[16,2432]{1,0:T(8,128)(2,1)S(1)} %get-tuple-element.28), channel_id=1, source_target_pairs={{0,14},{2,0},{4,2},{6,4},{8,6},{10,8},{12,10},{14,12},{1,15},{3,1}... | collective-permute-start | bytes 233480 | tf_op jit(solution)/shard_map/ppermute | solution.py:124
  23.3 0.9 bitcast_dynamic-update-slice_fusion.27
  26.6 1.4 %collective-permute-done.8 = bf16[512,2304]{1,0:T(8,128)(2,1)S(1)} collective-permute-done((bf16[512,2304]{1,0:T(8,128)(2,1)}, bf16[512,2304]{1,0:T(8,128)(2,1)S(1)}, u32[]{:S(2)}, u32[]{:S(2)}) %collective-permute-start.8) | collective-permute-done | bytes 2359328 | tf_op jit(solution)/shard_map/ppermute | solution.py:116
  29.4 1.2 %collective-permute-done.9 = f32[128,384]{1,0:T(8,128)S(1)} collective-permute-done((f32[128,384]{1,0:T(8,128)S(1)}, f32[128,384]{1,0:T(8,128)S(1)}, u32[]{:S(2)}, u32[]{:S(2)}) %collective-permute-start.9) | collective-permute-done | bytes 196640 | tf_op jit(solution)/shard_map/ppermute | solution.py:116
  31.5 1.5 %collective-permute-start.10 = (bf16[16,2432]{1,0:T(8,128)(2,1)S(1)}, bf16[16,2432]{1,0:T(8,128)(2,1)S(1)}, u32[]{:S(2)}, u32[]{:S(2)}) collective-permute-start(bf16[16,2432]{1,0:T(8,128)(2,1)S(1)} %get-tuple-element.22), channel_id=1, source_target_pairs={{0,14},{2,0},{4,2},{6,4},{8,6},{10,8},{12,10},{14,12},{1,15},{3,1}... | collective-permute-start | bytes 233480 | tf_op jit(solution)/shard_map/ppermute | solution.py:124
  33.3 1.8 %collective-permute-start.12 = (bf16[16,2432]{1,0:T(8,128)(2,1)S(1)}, bf16[16,2432]{1,0:T(8,128)(2,1)S(1)}, u32[]{:S(2)}, u32[]{:S(2)}) collective-permute-start(bf16[16,2432]{1,0:T(8,128)(2,1)S(1)} %get-tuple-element.24), channel_id=1, source_target_pairs={{0,10},{2,12},{4,14},{6,0},{8,2},{10,4},{12,6},{14,8},{1,11},{3,13... | collective-permute-start | bytes 233480 | tf_op jit(solution)/shard_map/ppermute | solution.py:124
  35.1 2.5 %collective-permute-start.13 = (bf16[16,2432]{1,0:T(8,128)(2,1)S(1)}, bf16[16,2432]{1,0:T(8,128)(2,1)S(1)}, u32[]{:S(2)}, u32[]{:S(2)}) collective-permute-start(bf16[16,2432]{1,0:T(8,128)(2,1)S(1)} %get-tuple-element.25), channel_id=1, source_target_pairs={{0,8},{2,10},{4,12},{6,14},{8,0},{10,2},{12,4},{14,6},{1,9},{3,11}... | collective-permute-start | bytes 233480 | tf_op jit(solution)/shard_map/ppermute | solution.py:124
  38.0 1.6 %collective-permute-start.15 = (bf16[16,2432]{1,0:T(8,128)(2,1)S(1)}, bf16[16,2432]{1,0:T(8,128)(2,1)S(1)}, u32[]{:S(2)}, u32[]{:S(2)}) collective-permute-start(bf16[16,2432]{1,0:T(8,128)(2,1)S(1)} %get-tuple-element.27), channel_id=1, source_target_pairs={{0,4},{2,6},{4,8},{6,10},{8,12},{10,14},{12,0},{14,2},{1,5},{3,7},... | collective-permute-start | bytes 233480 | tf_op jit(solution)/shard_map/ppermute | solution.py:124
  39.8 7.9 %collective-permute-done.13 = bf16[16,2432]{1,0:T(8,128)(2,1)S(1)} collective-permute-done((bf16[16,2432]{1,0:T(8,128)(2,1)S(1)}, bf16[16,2432]{1,0:T(8,128)(2,1)S(1)}, u32[]{:S(2)}, u32[]{:S(2)}) %collective-permute-start.13) | collective-permute-done | bytes 77856 | tf_op jit(solution)/shard_map/ppermute | solution.py:124
  47.7 1.8 %collective-permute-done.14 = bf16[16,2432]{1,0:T(8,128)(2,1)S(1)} collective-permute-done((bf16[16,2432]{1,0:T(8,128)(2,1)S(1)}, bf16[16,2432]{1,0:T(8,128)(2,1)S(1)}, u32[]{:S(2)}, u32[]{:S(2)}) %collective-permute-start.14) | collective-permute-done | bytes 77856 | tf_op jit(solution)/shard_map/ppermute | solution.py:124
  50.7 2.8 %collective-permute-start.19 = (bf16[16,2432]{1,0:T(8,128)(2,1)S(1)}, bf16[16,2432]{1,0:T(8,128)(2,1)S(1)}, u32[]{:S(2)}, u32[]{:S(2)}) collective-permute-start(bf16[16,2432]{1,0:T(8,128)(2,1)S(1)} %get-tuple-element.15), channel_id=1, source_target_pairs={{0,6},{2,8},{4,10},{6,12},{8,14},{10,0},{12,2},{14,4},{1,7},{3,9},... | collective-permute-start | bytes 233480 | tf_op jit(solution)/shard_map/ppermute | solution.py:124
  53.5 2.4 %collective-permute-start.20 = (bf16[16,2432]{1,0:T(8,128)(2,1)S(1)}, bf16[16,2432]{1,0:T(8,128)(2,1)S(1)}, u32[]{:S(2)}, u32[]{:S(2)}) collective-permute-start(bf16[16,2432]{1,0:T(8,128)(2,1)S(1)} %get-tuple-element.14), channel_id=1, source_target_pairs={{0,8},{2,10},{4,12},{6,14},{8,0},{10,2},{12,4},{14,6},{1,9},{3,11}... | collective-permute-start | bytes 233480 | tf_op jit(solution)/shard_map/ppermute | solution.py:124
  56.4 1.5 %collective-permute-done.17 = bf16[16,2432]{1,0:T(8,128)(2,1)S(1)} collective-permute-done((bf16[16,2432]{1,0:T(8,128)(2,1)S(1)}, bf16[16,2432]{1,0:T(8,128)(2,1)S(1)}, u32[]{:S(2)}, u32[]{:S(2)}) %collective-permute-start.17) | collective-permute-done | bytes 77856 | tf_op jit(solution)/shard_map/ppermute | solution.py:124
  57.9 0.9 collective-permute-start.22
  58.9 2.9 %collective-permute-start.23 = (bf16[16,2432]{1,0:T(8,128)(2,1)S(1)}, bf16[16,2432]{1,0:T(8,128)(2,1)S(1)}, u32[]{:S(2)}, u32[]{:S(2)}) collective-permute-start(bf16[16,2432]{1,0:T(8,128)(2,1)S(1)} %get-tuple-element.13), channel_id=1, source_target_pairs={{0,14},{2,0},{4,2},{6,4},{8,6},{10,8},{12,10},{14,12},{1,15},{3,1}... | collective-permute-start | bytes 233480 | tf_op jit(solution)/shard_map/ppermute | solution.py:124
  61.8 1.1 %collective-permute-done.19 = bf16[16,2432]{1,0:T(8,128)(2,1)S(1)} collective-permute-done((bf16[16,2432]{1,0:T(8,128)(2,1)S(1)}, bf16[16,2432]{1,0:T(8,128)(2,1)S(1)}, u32[]{:S(2)}, u32[]{:S(2)}) %collective-permute-start.19) | collective-permute-done | bytes 77856 | tf_op jit(solution)/shard_map/ppermute | solution.py:124
  62.9 1.3 %collective-permute-done.20 = bf16[16,2432]{1,0:T(8,128)(2,1)S(1)} collective-permute-done((bf16[16,2432]{1,0:T(8,128)(2,1)S(1)}, bf16[16,2432]{1,0:T(8,128)(2,1)S(1)}, u32[]{:S(2)}, u32[]{:S(2)}) %collective-permute-start.20) | collective-permute-done | bytes 77856 | tf_op jit(solution)/shard_map/ppermute | solution.py:124
  67.7 6.5 %collective-permute-start.25 = (bf16[16,2432]{1,0:T(8,128)(2,1)S(1)}, bf16[16,2432]{1,0:T(8,128)(2,1)S(1)}, u32[]{:S(2)}, u32[]{:S(2)}) collective-permute-start(bf16[16,2432]{1,0:T(8,128)(2,1)S(1)} %get-tuple-element.7), channel_id=1, source_target_pairs={{0,14},{2,0},{4,2},{6,4},{8,6},{10,8},{12,10},{14,12},{1,15},{3,1}... | collective-permute-start | bytes 233480 | tf_op jit(solution)/shard_map/ppermute | solution.py:124
  74.2 2.5 %collective-permute-start.26 = (bf16[16,2432]{1,0:T(8,128)(2,1)S(1)}, bf16[16,2432]{1,0:T(8,128)(2,1)S(1)}, u32[]{:S(2)}, u32[]{:S(2)}) collective-permute-start(bf16[16,2432]{1,0:T(8,128)(2,1)S(1)} %get-tuple-element.8), channel_id=1, source_target_pairs={{0,12},{2,14},{4,0},{6,2},{8,4},{10,6},{12,8},{14,10},{1,13},{3,15... | collective-permute-start | bytes 233480 | tf_op jit(solution)/shard_map/ppermute | solution.py:124
  76.8 1.1 %collective-permute-start.28 = (bf16[16,2432]{1,0:T(8,128)(2,1)S(1)}, bf16[16,2432]{1,0:T(8,128)(2,1)S(1)}, u32[]{:S(2)}, u32[]{:S(2)}) collective-permute-start(bf16[16,2432]{1,0:T(8,128)(2,1)S(1)} %get-tuple-element.10), channel_id=1, source_target_pairs={{0,8},{2,10},{4,12},{6,14},{8,0},{10,2},{12,4},{14,6},{1,9},{3,11}... | collective-permute-start | bytes 233480 | tf_op jit(solution)/shard_map/ppermute | solution.py:124
  77.9 1.8 %collective-permute-start.29 = (bf16[16,2432]{1,0:T(8,128)(2,1)S(1)}, bf16[16,2432]{1,0:T(8,128)(2,1)S(1)}, u32[]{:S(2)}, u32[]{:S(2)}) collective-permute-start(bf16[16,2432]{1,0:T(8,128)(2,1)S(1)} %get-tuple-element.11), channel_id=1, source_target_pairs={{0,6},{2,8},{4,10},{6,12},{8,14},{10,0},{12,2},{14,4},{1,7},{3,9},... | collective-permute-start | bytes 233480 | tf_op jit(solution)/shard_map/ppermute | solution.py:124
  79.7 2.3 %collective-permute-start.30 = (bf16[16,2432]{1,0:T(8,128)(2,1)S(1)}, bf16[16,2432]{1,0:T(8,128)(2,1)S(1)}, u32[]{:S(2)}, u32[]{:S(2)}) collective-permute-start(bf16[16,2432]{1,0:T(8,128)(2,1)S(1)} %get-tuple-element.12), channel_id=1, source_target_pairs={{0,4},{2,6},{4,8},{6,10},{8,12},{10,14},{12,0},{14,2},{1,5},{3,7},... | collective-permute-start | bytes 233480 | tf_op jit(solution)/shard_map/ppermute | solution.py:124
  82.9 6.5 %collective-permute-start.31 = (bf16[16,2432]{1,0:T(8,128)(2,1)S(1)}, bf16[16,2432]{1,0:T(8,128)(2,1)S(1)}, u32[]{:S(2)}, u32[]{:S(2)}) collective-permute-start(bf16[16,2432]{1,0:T(8,128)(2,1)S(1)} %get-tuple-element.6), channel_id=1, source_target_pairs={{0,2},{2,4},{4,6},{6,8},{8,10},{10,12},{12,14},{14,0},{1,3},{3,5},... | collective-permute-start | bytes 233480 | tf_op jit(solution)/shard_map/ppermute | solution.py:124
  90.2 1.2 %collective-permute-done.31 = bf16[16,2432]{1,0:T(8,128)(2,1)S(1)} collective-permute-done((bf16[16,2432]{1,0:T(8,128)(2,1)S(1)}, bf16[16,2432]{1,0:T(8,128)(2,1)S(1)}, u32[]{:S(2)}, u32[]{:S(2)}) %collective-permute-start.31) | collective-permute-done | bytes 77856 | tf_op jit(solution)/shard_map/ppermute | solution.py:124
  (132 shorter events, 20.3 us)
Async XLA Ops:
  4.4 14.1 %collective-permute-start.1 = (bf16[16,2432]{1,0:T(8,128)(2,1)}, bf16[16,2432]{1,0:T(8,128)(2,1)}, u32[]{:S(2)}, u32[]{:S(2)}) collective-permute-start(bf16[16,2432]{1,0:T(8,128)(2,1)} %get-tuple-element.31), channel_id=1, source_target_pairs={{0,2},{2,4},{4,6},{6,8},{8,10},{10,12},{12,14},{14,0},{1,3},{3,5},... | collective-permute-start | bytes 233480 | tf_op jit(solution)/shard_map/ppermute | solution.py:124
  7.4 13.4 %collective-permute-start.2 = (bf16[16,2432]{1,0:T(8,128)(2,1)S(1)}, bf16[16,2432]{1,0:T(8,128)(2,1)}, u32[]{:S(2)}, u32[]{:S(2)}) collective-permute-start(bf16[16,2432]{1,0:T(8,128)(2,1)S(1)} %get-tuple-element.32), channel_id=1, source_target_pairs={{0,4},{2,6},{4,8},{6,10},{8,12},{10,14},{12,0},{14,2},{1,5},{3,7},... | collective-permute-start | bytes 233480 | tf_op jit(solution)/shard_map/ppermute | solution.py:124
  9.0 14.2 %collective-permute-start.3 = (bf16[16,2432]{1,0:T(8,128)(2,1)S(1)}, bf16[16,2432]{1,0:T(8,128)(2,1)}, u32[]{:S(2)}, u32[]{:S(2)}) collective-permute-start(bf16[16,2432]{1,0:T(8,128)(2,1)S(1)} %get-tuple-element.33), channel_id=1, source_target_pairs={{0,6},{2,8},{4,10},{6,12},{8,14},{10,0},{12,2},{14,4},{1,7},{3,9},... | collective-permute-start | bytes 233480 | tf_op jit(solution)/shard_map/ppermute | solution.py:124
  11.5 12.7 %collective-permute-start.4 = (bf16[16,2432]{1,0:T(8,128)(2,1)S(1)}, bf16[16,2432]{1,0:T(8,128)(2,1)}, u32[]{:S(2)}, u32[]{:S(2)}) collective-permute-start(bf16[16,2432]{1,0:T(8,128)(2,1)S(1)} %get-tuple-element.34), channel_id=1, source_target_pairs={{0,8},{2,10},{4,12},{6,14},{8,0},{10,2},{12,4},{14,6},{1,9},{3,11}... | collective-permute-start | bytes 233480 | tf_op jit(solution)/shard_map/ppermute | solution.py:124
  12.7 12.9 %collective-permute-start.5 = (bf16[16,2432]{1,0:T(8,128)(2,1)S(1)}, bf16[16,2432]{1,0:T(8,128)(2,1)}, u32[]{:S(2)}, u32[]{:S(2)}) collective-permute-start(bf16[16,2432]{1,0:T(8,128)(2,1)S(1)} %get-tuple-element.29), channel_id=1, source_target_pairs={{0,10},{2,12},{4,14},{6,0},{8,2},{10,4},{12,6},{14,8},{1,11},{3,13... | collective-permute-start | bytes 233480 | tf_op jit(solution)/shard_map/ppermute | solution.py:124
  18.5 8.0 %collective-permute-start.6 = (bf16[16,2432]{1,0:T(8,128)(2,1)S(1)}, bf16[16,2432]{1,0:T(8,128)(2,1)S(1)}, u32[]{:S(2)}, u32[]{:S(2)}) collective-permute-start(bf16[16,2432]{1,0:T(8,128)(2,1)S(1)} %get-tuple-element.35), channel_id=1, source_target_pairs={{0,12},{2,14},{4,0},{6,2},{8,4},{10,6},{12,8},{14,10},{1,13},{3,15... | collective-permute-start | bytes 233480 | tf_op jit(solution)/shard_map/ppermute | solution.py:124
  20.8 5.7 %collective-permute-start.7 = (bf16[16,2432]{1,0:T(8,128)(2,1)S(1)}, bf16[16,2432]{1,0:T(8,128)(2,1)S(1)}, u32[]{:S(2)}, u32[]{:S(2)}) collective-permute-start(bf16[16,2432]{1,0:T(8,128)(2,1)S(1)} %get-tuple-element.28), channel_id=1, source_target_pairs={{0,14},{2,0},{4,2},{6,4},{8,6},{10,8},{12,10},{14,12},{1,15},{3,1}... | collective-permute-start | bytes 233480 | tf_op jit(solution)/shard_map/ppermute | solution.py:124
  23.2 4.8 %collective-permute-start.8 = (bf16[512,2304]{1,0:T(8,128)(2,1)}, bf16[512,2304]{1,0:T(8,128)(2,1)S(1)}, u32[]{:S(2)}, u32[]{:S(2)}) collective-permute-start(bf16[512,2304]{1,0:T(8,128)(2,1)} %pad_maximum_fusion), channel_id=1, source_target_pairs={{0,1},{1,0},{2,3},{3,2},{4,5},{5,4},{6,7},{7,6},{8,9},{9,8},{10,11... | collective-permute-start | bytes 7077896 | tf_op jit(solution)/shard_map/ppermute | solution.py:116
  24.2 5.2 %collective-permute-start = (f32[4624]{0:T(1024)S(1)}, f32[4624]{0:T(1024)S(1)}, u32[]{:S(2)}, u32[]{:S(2)}) collective-permute-start(f32[4624]{0:T(1024)S(1)} %pad_maximum_fusion.7), channel_id=1, source_target_pairs={{0,1},{1,0},{2,3},{3,2},{4,5},{5,4},{6,7},{7,6},{8,9},{9,8},{10,11... | collective-permute-start | bytes 55496 | tf_op jit(solution)/shard_map/ppermute | solution.py:116
  29.1 1.5 %collective-permute-start.9 = (f32[128,384]{1,0:T(8,128)S(1)}, f32[128,384]{1,0:T(8,128)S(1)}, u32[]{:S(2)}, u32[]{:S(2)}) collective-permute-start(f32[128,384]{1,0:T(8,128)S(1)} %pad_maximum_fusion.1), channel_id=1, source_target_pairs={{0,1},{1,0},{2,3},{3,2},{4,5},{5,4},{6,7},{7,6},{8,9},{9,8},{10,11... | collective-permute-start | bytes 589832 | tf_op jit(solution)/shard_map/ppermute | solution.py:116
  31.5 6.5 %collective-permute-start.10 = (bf16[16,2432]{1,0:T(8,128)(2,1)S(1)}, bf16[16,2432]{1,0:T(8,128)(2,1)S(1)}, u32[]{:S(2)}, u32[]{:S(2)}) collective-permute-start(bf16[16,2432]{1,0:T(8,128)(2,1)S(1)} %get-tuple-element.22), channel_id=1, source_target_pairs={{0,14},{2,0},{4,2},{6,4},{8,6},{10,8},{12,10},{14,12},{1,15},{3,1}... | collective-permute-start | bytes 233480 | tf_op jit(solution)/shard_map/ppermute | solution.py:124
  32.9 6.6 %collective-permute-start.11 = (bf16[16,2432]{1,0:T(8,128)(2,1)S(1)}, bf16[16,2432]{1,0:T(8,128)(2,1)S(1)}, u32[]{:S(2)}, u32[]{:S(2)}) collective-permute-start(bf16[16,2432]{1,0:T(8,128)(2,1)S(1)} %get-tuple-element.23), channel_id=1, source_target_pairs={{0,12},{2,14},{4,0},{6,2},{8,4},{10,6},{12,8},{14,10},{1,13},{3,15... | collective-permute-start | bytes 233480 | tf_op jit(solution)/shard_map/ppermute | solution.py:124
  33.3 6.4 %collective-permute-start.12 = (bf16[16,2432]{1,0:T(8,128)(2,1)S(1)}, bf16[16,2432]{1,0:T(8,128)(2,1)S(1)}, u32[]{:S(2)}, u32[]{:S(2)}) collective-permute-start(bf16[16,2432]{1,0:T(8,128)(2,1)S(1)} %get-tuple-element.24), channel_id=1, source_target_pairs={{0,10},{2,12},{4,14},{6,0},{8,2},{10,4},{12,6},{14,8},{1,11},{3,13... | collective-permute-start | bytes 233480 | tf_op jit(solution)/shard_map/ppermute | solution.py:124
  35.1 12.6 %collective-permute-start.13 = (bf16[16,2432]{1,0:T(8,128)(2,1)S(1)}, bf16[16,2432]{1,0:T(8,128)(2,1)S(1)}, u32[]{:S(2)}, u32[]{:S(2)}) collective-permute-start(bf16[16,2432]{1,0:T(8,128)(2,1)S(1)} %get-tuple-element.25), channel_id=1, source_target_pairs={{0,8},{2,10},{4,12},{6,14},{8,0},{10,2},{12,4},{14,6},{1,9},{3,11}... | collective-permute-start | bytes 233480 | tf_op jit(solution)/shard_map/ppermute | solution.py:124
  37.6 12.0 %collective-permute-start.14 = (bf16[16,2432]{1,0:T(8,128)(2,1)S(1)}, bf16[16,2432]{1,0:T(8,128)(2,1)S(1)}, u32[]{:S(2)}, u32[]{:S(2)}) collective-permute-start(bf16[16,2432]{1,0:T(8,128)(2,1)S(1)} %get-tuple-element.26), channel_id=1, source_target_pairs={{0,6},{2,8},{4,10},{6,12},{8,14},{10,0},{12,2},{14,4},{1,7},{3,9},... | collective-permute-start | bytes 233480 | tf_op jit(solution)/shard_map/ppermute | solution.py:124
  38.0 11.6 %collective-permute-start.15 = (bf16[16,2432]{1,0:T(8,128)(2,1)S(1)}, bf16[16,2432]{1,0:T(8,128)(2,1)S(1)}, u32[]{:S(2)}, u32[]{:S(2)}) collective-permute-start(bf16[16,2432]{1,0:T(8,128)(2,1)S(1)} %get-tuple-element.27), channel_id=1, source_target_pairs={{0,4},{2,6},{4,8},{6,10},{8,12},{10,14},{12,0},{14,2},{1,5},{3,7},... | collective-permute-start | bytes 233480 | tf_op jit(solution)/shard_map/ppermute | solution.py:124
  39.5 10.1 %collective-permute-start.16 = (bf16[16,2432]{1,0:T(8,128)(2,1)S(1)}, bf16[16,2432]{1,0:T(8,128)(2,1)S(1)}, u32[]{:S(2)}, u32[]{:S(2)}) collective-permute-start(bf16[16,2432]{1,0:T(8,128)(2,1)S(1)} %get-tuple-element.21), channel_id=1, source_target_pairs={{0,2},{2,4},{4,6},{6,8},{8,10},{10,12},{12,14},{14,0},{1,3},{3,5},... | collective-permute-start | bytes 233480 | tf_op jit(solution)/shard_map/ppermute | solution.py:124
  49.9 8.0 %collective-permute-start.17 = (bf16[16,2432]{1,0:T(8,128)(2,1)S(1)}, bf16[16,2432]{1,0:T(8,128)(2,1)S(1)}, u32[]{:S(2)}, u32[]{:S(2)}) collective-permute-start(bf16[16,2432]{1,0:T(8,128)(2,1)S(1)} %get-tuple-element.17), channel_id=1, source_target_pairs={{0,2},{2,4},{4,6},{6,8},{8,10},{10,12},{12,14},{14,0},{1,3},{3,5},... | collective-permute-start | bytes 233480 | tf_op jit(solution)/shard_map/ppermute | solution.py:124
  50.0 8.9 %collective-permute-start.18 = (bf16[16,2432]{1,0:T(8,128)(2,1)S(1)}, bf16[16,2432]{1,0:T(8,128)(2,1)S(1)}, u32[]{:S(2)}, u32[]{:S(2)}) collective-permute-start(bf16[16,2432]{1,0:T(8,128)(2,1)S(1)} %get-tuple-element.16), channel_id=1, source_target_pairs={{0,4},{2,6},{4,8},{6,10},{8,12},{10,14},{12,0},{14,2},{1,5},{3,7},... | collective-permute-start | bytes 233480 | tf_op jit(solution)/shard_map/ppermute | solution.py:124
  50.7 12.2 %collective-permute-start.19 = (bf16[16,2432]{1,0:T(8,128)(2,1)S(1)}, bf16[16,2432]{1,0:T(8,128)(2,1)S(1)}, u32[]{:S(2)}, u32[]{:S(2)}) collective-permute-start(bf16[16,2432]{1,0:T(8,128)(2,1)S(1)} %get-tuple-element.15), channel_id=1, source_target_pairs={{0,6},{2,8},{4,10},{6,12},{8,14},{10,0},{12,2},{14,4},{1,7},{3,9},... | collective-permute-start | bytes 233480 | tf_op jit(solution)/shard_map/ppermute | solution.py:124
  53.5 10.7 %collective-permute-start.20 = (bf16[16,2432]{1,0:T(8,128)(2,1)S(1)}, bf16[16,2432]{1,0:T(8,128)(2,1)S(1)}, u32[]{:S(2)}, u32[]{:S(2)}) collective-permute-start(bf16[16,2432]{1,0:T(8,128)(2,1)S(1)} %get-tuple-element.14), channel_id=1, source_target_pairs={{0,8},{2,10},{4,12},{6,14},{8,0},{10,2},{12,4},{14,6},{1,9},{3,11}... | collective-permute-start | bytes 233480 | tf_op jit(solution)/shard_map/ppermute | solution.py:124
  55.9 8.3 %collective-permute-start.21 = (bf16[16,2432]{1,0:T(8,128)(2,1)S(1)}, bf16[16,2432]{1,0:T(8,128)(2,1)S(1)}, u32[]{:S(2)}, u32[]{:S(2)}) collective-permute-start(bf16[16,2432]{1,0:T(8,128)(2,1)S(1)} %get-tuple-element.18), channel_id=1, source_target_pairs={{0,10},{2,12},{4,14},{6,0},{8,2},{10,4},{12,6},{14,8},{1,11},{3,13... | collective-permute-start | bytes 233480 | tf_op jit(solution)/shard_map/ppermute | solution.py:124
  57.9 6.3 %collective-permute-start.22 = (bf16[16,2432]{1,0:T(8,128)(2,1)S(1)}, bf16[16,2432]{1,0:T(8,128)(2,1)S(1)}, u32[]{:S(2)}, u32[]{:S(2)}) collective-permute-start(bf16[16,2432]{1,0:T(8,128)(2,1)S(1)} %get-tuple-element.19), channel_id=1, source_target_pairs={{0,12},{2,14},{4,0},{6,2},{8,4},{10,6},{12,8},{14,10},{1,13},{3,15... | collective-permute-start | bytes 233480 | tf_op jit(solution)/shard_map/ppermute | solution.py:124
  58.9 5.4 %collective-permute-start.23 = (bf16[16,2432]{1,0:T(8,128)(2,1)S(1)}, bf16[16,2432]{1,0:T(8,128)(2,1)S(1)}, u32[]{:S(2)}, u32[]{:S(2)}) collective-permute-start(bf16[16,2432]{1,0:T(8,128)(2,1)S(1)} %get-tuple-element.13), channel_id=1, source_target_pairs={{0,14},{2,0},{4,2},{6,4},{8,6},{10,8},{12,10},{14,12},{1,15},{3,1}... | collective-permute-start | bytes 233480 | tf_op jit(solution)/shard_map/ppermute | solution.py:124
  65.6 27.1 %collective-permute-start.33 = (bf16[16,2304]{1,0:T(8,128)(2,1)S(1)}, bf16[16,2304]{1,0:T(8,128)(2,1)S(1)}, u32[]{:S(2)}, u32[]{:S(2)}) collective-permute-start(bf16[16,2304]{1,0:T(8,128)(2,1)S(1)} %add_convert_fusion.1), channel_id=1, source_target_pairs={{0,1},{1,0},{2,3},{3,2},{4,5},{5,4},{6,7},{7,6},{8,9},{9,8},{10,11... | collective-permute-start | bytes 221192 | tf_op jit(solution)/shard_map/ppermute | solution.py:116
  67.7 10.2 %collective-permute-start.25 = (bf16[16,2432]{1,0:T(8,128)(2,1)S(1)}, bf16[16,2432]{1,0:T(8,128)(2,1)S(1)}, u32[]{:S(2)}, u32[]{:S(2)}) collective-permute-start(bf16[16,2432]{1,0:T(8,128)(2,1)S(1)} %get-tuple-element.7), channel_id=1, source_target_pairs={{0,14},{2,0},{4,2},{6,4},{8,6},{10,8},{12,10},{14,12},{1,15},{3,1}... | collective-permute-start | bytes 233480 | tf_op jit(solution)/shard_map/ppermute | solution.py:124
  74.2 5.5 %collective-permute-start.26 = (bf16[16,2432]{1,0:T(8,128)(2,1)S(1)}, bf16[16,2432]{1,0:T(8,128)(2,1)S(1)}, u32[]{:S(2)}, u32[]{:S(2)}) collective-permute-start(bf16[16,2432]{1,0:T(8,128)(2,1)S(1)} %get-tuple-element.8), channel_id=1, source_target_pairs={{0,12},{2,14},{4,0},{6,2},{8,4},{10,6},{12,8},{14,10},{1,13},{3,15... | collective-permute-start | bytes 233480 | tf_op jit(solution)/shard_map/ppermute | solution.py:124
  76.8 6.1 %collective-permute-start.27 = (bf16[16,2432]{1,0:T(8,128)(2,1)S(1)}, bf16[16,2432]{1,0:T(8,128)(2,1)S(1)}, u32[]{:S(2)}, u32[]{:S(2)}) collective-permute-start(bf16[16,2432]{1,0:T(8,128)(2,1)S(1)} %get-tuple-element.9), channel_id=1, source_target_pairs={{0,10},{2,12},{4,14},{6,0},{8,2},{10,4},{12,6},{14,8},{1,11},{3,13... | collective-permute-start | bytes 233480 | tf_op jit(solution)/shard_map/ppermute | solution.py:124
  76.8 12.6 %collective-permute-start.28 = (bf16[16,2432]{1,0:T(8,128)(2,1)S(1)}, bf16[16,2432]{1,0:T(8,128)(2,1)S(1)}, u32[]{:S(2)}, u32[]{:S(2)}) collective-permute-start(bf16[16,2432]{1,0:T(8,128)(2,1)S(1)} %get-tuple-element.10), channel_id=1, source_target_pairs={{0,8},{2,10},{4,12},{6,14},{8,0},{10,2},{12,4},{14,6},{1,9},{3,11}... | collective-permute-start | bytes 233480 | tf_op jit(solution)/shard_map/ppermute | solution.py:124
  77.9 12.3 %collective-permute-start.29 = (bf16[16,2432]{1,0:T(8,128)(2,1)S(1)}, bf16[16,2432]{1,0:T(8,128)(2,1)S(1)}, u32[]{:S(2)}, u32[]{:S(2)}) collective-permute-start(bf16[16,2432]{1,0:T(8,128)(2,1)S(1)} %get-tuple-element.11), channel_id=1, source_target_pairs={{0,6},{2,8},{4,10},{6,12},{8,14},{10,0},{12,2},{14,4},{1,7},{3,9},... | collective-permute-start | bytes 233480 | tf_op jit(solution)/shard_map/ppermute | solution.py:124
  79.7 10.5 %collective-permute-start.30 = (bf16[16,2432]{1,0:T(8,128)(2,1)S(1)}, bf16[16,2432]{1,0:T(8,128)(2,1)S(1)}, u32[]{:S(2)}, u32[]{:S(2)}) collective-permute-start(bf16[16,2432]{1,0:T(8,128)(2,1)S(1)} %get-tuple-element.12), channel_id=1, source_target_pairs={{0,4},{2,6},{4,8},{6,10},{8,12},{10,14},{12,0},{14,2},{1,5},{3,7},... | collective-permute-start | bytes 233480 | tf_op jit(solution)/shard_map/ppermute | solution.py:124
  82.9 8.5 %collective-permute-start.31 = (bf16[16,2432]{1,0:T(8,128)(2,1)S(1)}, bf16[16,2432]{1,0:T(8,128)(2,1)S(1)}, u32[]{:S(2)}, u32[]{:S(2)}) collective-permute-start(bf16[16,2432]{1,0:T(8,128)(2,1)S(1)} %get-tuple-element.6), channel_id=1, source_target_pairs={{0,2},{2,4},{4,6},{6,8},{8,10},{10,12},{12,14},{14,0},{1,3},{3,5},... | collective-permute-start | bytes 233480 | tf_op jit(solution)/shard_map/ppermute | solution.py:124
  (8 other events, 42.8 us)

commit v11 on v5

--- a/solution.py
+++ b/solution.py
@@ -116,16 +116,18 @@
     return lax.ppermute(block, "section", [(0, 1), (1, 0)])
 
 
-def exchange(parts, sign):
+def exchange(parts, sign, joined=False):
     peers = parts.shape[0]
     moved = [parts[0]]
     for shift in range(1, peers):
         route = [(d, (d + sign * shift) % peers) for d in range(peers)]
         moved.append(lax.ppermute(parts[shift], "dict", route))
+    if joined:
+        return jnp.concatenate(moved, axis=0).reshape(parts.shape)
     return jnp.stack(moved, axis=0)
 
 
-def split_layer(g_half, routes_l, acts_l, own, other, is_own, gain_half, scale_l):
+def split_layer(g_half, routes_l, acts_l, own, other, is_own, gain_half, scale_l, joined):
     peers = lax.axis_size("dict")
     me = lax.axis_index("dict")
     rows, listed = routes_l.shape
@@ -145,7 +147,7 @@
     sent = jnp.concatenate(
         [jnp.broadcast_to(g_half[None], (peers, rows, half)), placed], axis=-1
     )
-    got = exchange(sent, 1).reshape(peers * rows, half + block)
+    got = exchange(sent, 1, joined).reshape(peers * rows, half + block)
     g_all = got[:, :half]
     code_all = got[:, half:]
 
@@ -211,7 +213,9 @@
         s = jnp.where(is_own, small, other_small)
         gain_half = lax.dynamic_slice_in_dim(s[:width], mine, half, axis=0)
         scale_l = s[width:width + rows]
-        attr, g_half = split_layer(g_half, routes[0], acts[0], own, other, is_own, gain_half, scale_l)
+        attr, g_half = split_layer(
+            g_half, routes[0], acts[0], own, other, is_own, gain_half, scale_l, layer == depth - 1
+        )
         partner = swap_cores(g_half)
         full = jnp.where(
             here == 0,

time: 94.1 us -> 97.5 us (1.036)
  waiting for transfers between devices: 20 us -> 22.5 us
    ppermute x28, waiting for transfers between devices: 16.4 us -> 20.6 us  [exchange(): moved.append(lax.ppermute(parts[shift], 'dict', route))]
    ppermute x6, waiting for transfers between devices: 3.57 us -> 1.93 us  [swap_cores(): return lax.ppermute(block, 'section', [(0, 1), (1, 0)])]
  transfers between devices with their start and end apart: 34 -> 34, of which waited for: 12 -> 10; matrix products, arithmetic and copies ran while one was open for 12% -> 12% of each run, Pallas kernels for 0% -> 0%
where the time goes in v11:
time: 97.5 us; the launch traced here: 97 us
  starting transfers between devices  55.4 us (57%)
  waiting for transfers between devices  22.5 us (23%)
  local copies, waits for them, and re-layouts  8.29 us (9%)
  other arithmetic  5.45 us (6%)
  matrix products  4.19 us (4%)
  between operations  1.15 us (1%)
    ppermute x28, starting transfers between devices, exchange(): moved.append(lax.ppermute(parts[shift], 'dict', route))  54.1 us
    ppermute x28, waiting for transfers between devices, exchange(): moved.append(lax.ppermute(parts[shift], 'dict', route))  20.6 us
    unnamed x38, local copies, waits for them, and re-layouts  4.79 us
    dot_general x4, matrix products, with_dec(): lax.dot_general(g_all, dec, (((1,), (1,)), ((), ())), preferred_element_t...  2.17 us
  transfers between devices with their start and end apart: 34, of which 10 were waited for; matrix products, arithmetic and copies ran while one was open for 12% of the time, Pallas kernels for 0%

profile of v11, /device:TPU:0, one launch (start us, length us, event | category | flops | bytes accessed | tf_op | source)
XLA Modules:
  0.0 97.0 jit_solution(13414970770102714342)
XLA Ops:
  4.4 2.9 %collective-permute-start.1 = (bf16[16,2432]{1,0:T(8,128)(2,1)}, bf16[16,2432]{1,0:T(8,128)(2,1)}, u32[]{:S(2)}, u32[]{:S(2)}) collective-permute-start(bf16[16,2432]{1,0:T(8,128)(2,1)} %get-tuple-element.30), channel_id=1, source_target_pairs={{0,2},{2,4},{4,6},{6,8},{8,10},{10,12},{12,14},{14,0},{1,3},{3,5},... | collective-permute-start | bytes 233480 | tf_op jit(solution)/shard_map/ppermute | solution.py:124
  7.4 1.6 %collective-permute-start.2 = (bf16[16,2432]{1,0:T(8,128)(2,1)S(1)}, bf16[16,2432]{1,0:T(8,128)(2,1)}, u32[]{:S(2)}, u32[]{:S(2)}) collective-permute-start(bf16[16,2432]{1,0:T(8,128)(2,1)S(1)} %get-tuple-element.31), channel_id=1, source_target_pairs={{0,4},{2,6},{4,8},{6,10},{8,12},{10,14},{12,0},{14,2},{1,5},{3,7},... | collective-permute-start | bytes 233480 | tf_op jit(solution)/shard_map/ppermute | solution.py:124
  9.0 2.6 %collective-permute-start.3 = (bf16[16,2432]{1,0:T(8,128)(2,1)S(1)}, bf16[16,2432]{1,0:T(8,128)(2,1)}, u32[]{:S(2)}, u32[]{:S(2)}) collective-permute-start(bf16[16,2432]{1,0:T(8,128)(2,1)S(1)} %get-tuple-element.32), channel_id=1, source_target_pairs={{0,6},{2,8},{4,10},{6,12},{8,14},{10,0},{12,2},{14,4},{1,7},{3,9},... | collective-permute-start | bytes 233480 | tf_op jit(solution)/shard_map/ppermute | solution.py:124
  11.5 1.2 %collective-permute-start.4 = (bf16[16,2432]{1,0:T(8,128)(2,1)S(1)}, bf16[16,2432]{1,0:T(8,128)(2,1)}, u32[]{:S(2)}, u32[]{:S(2)}) collective-permute-start(bf16[16,2432]{1,0:T(8,128)(2,1)S(1)} %get-tuple-element.33), channel_id=1, source_target_pairs={{0,8},{2,10},{4,12},{6,14},{8,0},{10,2},{12,4},{14,6},{1,9},{3,11}... | collective-permute-start | bytes 233480 | tf_op jit(solution)/shard_map/ppermute | solution.py:124
  12.8 2.6 %collective-permute-start.5 = (bf16[16,2432]{1,0:T(8,128)(2,1)S(1)}, bf16[16,2432]{1,0:T(8,128)(2,1)}, u32[]{:S(2)}, u32[]{:S(2)}) collective-permute-start(bf16[16,2432]{1,0:T(8,128)(2,1)S(1)} %get-tuple-element.29), channel_id=1, source_target_pairs={{0,10},{2,12},{4,14},{6,0},{8,2},{10,4},{12,6},{14,8},{1,11},{3,13... | collective-permute-start | bytes 233480 | tf_op jit(solution)/shard_map/ppermute | solution.py:124
  15.4 1.5 %dynamic-slice_bitcast_fusion = (bf16[256,2304]{1,0:T(8,128)(2,1)S(1)}, bf16[256,2304]{1,0:T(8,128)(2,1)S(1)}) fusion(bf16[1,256,4608]{2,1,0:T(8,128)(2,1)} %param.11, s32[]{:T(128)S(6)} %select_n.193, bf16[1,256,4608]{2,1,0:T(8,128)(2,1)S(1)} %copy-done), kind=kLoop, calls=%fused_computation.48 | loop fusion | bytes 4718596 | tf_op jit(solution)/shard_map/dynamic_slice | solution.py:198
  16.9 1.6 %pad_maximum_fusion = bf16[512,2304]{1,0:T(8,128)(2,1)} fusion(bf16[256,2304]{1,0:T(8,128)(2,1)S(1)} %get-tuple-element.39, bf16[256,2304]{1,0:T(8,128)(2,1)S(1)} %get-tuple-element.40), kind=kLoop, calls=%fused_computation.4 | loop fusion | flops 4718592 | bytes 4718592 | tf_op jit(solution)/shard_map/concatenate | solution.py:195
  18.6 0.9 constant_dynamic-update-slice_fusion.6
  19.5 1.4 %collective-permute-start.6 = (bf16[16,2432]{1,0:T(8,128)(2,1)S(1)}, bf16[16,2432]{1,0:T(8,128)(2,1)S(1)}, u32[]{:S(2)}, u32[]{:S(2)}) collective-permute-start(bf16[16,2432]{1,0:T(8,128)(2,1)S(1)} %get-tuple-element.34), channel_id=1, source_target_pairs={{0,12},{2,14},{4,0},{6,2},{8,4},{10,6},{12,8},{14,10},{1,13},{3,15... | collective-permute-start | bytes 233480 | tf_op jit(solution)/shard_map/ppermute | solution.py:124
  21.8 2.2 %collective-permute-start.7 = (bf16[16,2432]{1,0:T(8,128)(2,1)S(1)}, bf16[16,2432]{1,0:T(8,128)(2,1)S(1)}, u32[]{:S(2)}, u32[]{:S(2)}) collective-permute-start(bf16[16,2432]{1,0:T(8,128)(2,1)S(1)} %get-tuple-element.28), channel_id=1, source_target_pairs={{0,14},{2,0},{4,2},{6,4},{8,6},{10,8},{12,10},{14,12},{1,15},{3,1}... | collective-permute-start | bytes 233480 | tf_op jit(solution)/shard_map/ppermute | solution.py:124
  24.0 0.9 constant_dynamic-update-slice_fusion.4
  25.0 0.9 constant_dynamic-update-slice_fusion.3
  25.9 0.9 constant_dynamic-update-slice_fusion.2
  28.7 1.0 collective-permute-done.9
  30.5 4.2 %collective-permute-start.10 = (bf16[16,2432]{1,0:T(8,128)(2,1)S(1)}, bf16[16,2432]{1,0:T(8,128)(2,1)S(1)}, u32[]{:S(2)}, u32[]{:S(2)}) collective-permute-start(bf16[16,2432]{1,0:T(8,128)(2,1)S(1)} %get-tuple-element.22), channel_id=1, source_target_pairs={{0,14},{2,0},{4,2},{6,4},{8,6},{10,8},{12,10},{14,12},{1,15},{3,1}... | collective-permute-start | bytes 233480 | tf_op jit(solution)/shard_map/ppermute | solution.py:124
  34.7 2.9 %collective-permute-start.13 = (bf16[16,2432]{1,0:T(8,128)(2,1)S(1)}, bf16[16,2432]{1,0:T(8,128)(2,1)S(1)}, u32[]{:S(2)}, u32[]{:S(2)}) collective-permute-start(bf16[16,2432]{1,0:T(8,128)(2,1)S(1)} %get-tuple-element.25), channel_id=1, source_target_pairs={{0,8},{2,10},{4,12},{6,14},{8,0},{10,2},{12,4},{14,6},{1,9},{3,11}... | collective-permute-start | bytes 233480 | tf_op jit(solution)/shard_map/ppermute | solution.py:124
  37.7 2.0 %collective-permute-start.15 = (bf16[16,2432]{1,0:T(8,128)(2,1)S(1)}, bf16[16,2432]{1,0:T(8,128)(2,1)S(1)}, u32[]{:S(2)}, u32[]{:S(2)}) collective-permute-start(bf16[16,2432]{1,0:T(8,128)(2,1)S(1)} %get-tuple-element.27), channel_id=1, source_target_pairs={{0,4},{2,6},{4,8},{6,10},{8,12},{10,14},{12,0},{14,2},{1,5},{3,7},... | collective-permute-start | bytes 233480 | tf_op jit(solution)/shard_map/ppermute | solution.py:124
  39.6 1.5 %collective-permute-start.16 = (bf16[16,2432]{1,0:T(8,128)(2,1)S(1)}, bf16[16,2432]{1,0:T(8,128)(2,1)S(1)}, u32[]{:S(2)}, u32[]{:S(2)}) collective-permute-start(bf16[16,2432]{1,0:T(8,128)(2,1)S(1)} %get-tuple-element.21), channel_id=1, source_target_pairs={{0,2},{2,4},{4,6},{6,8},{8,10},{10,12},{12,14},{14,0},{1,3},{3,5},... | collective-permute-start | bytes 233480 | tf_op jit(solution)/shard_map/ppermute | solution.py:124
  41.2 5.9 %collective-permute-done.13 = bf16[16,2432]{1,0:T(8,128)(2,1)S(1)} collective-permute-done((bf16[16,2432]{1,0:T(8,128)(2,1)S(1)}, bf16[16,2432]{1,0:T(8,128)(2,1)S(1)}, u32[]{:S(2)}, u32[]{:S(2)}) %collective-permute-start.13) | collective-permute-done | bytes 77856 | tf_op jit(solution)/shard_map/ppermute | solution.py:124
  47.1 3.8 %collective-permute-done.14 = bf16[16,2432]{1,0:T(8,128)(2,1)S(1)} collective-permute-done((bf16[16,2432]{1,0:T(8,128)(2,1)S(1)}, bf16[16,2432]{1,0:T(8,128)(2,1)S(1)}, u32[]{:S(2)}, u32[]{:S(2)}) %collective-permute-start.14) | collective-permute-done | bytes 77856 | tf_op jit(solution)/shard_map/ppermute | solution.py:124
  51.4 2.2 %collective-permute-start.19 = (bf16[16,2432]{1,0:T(8,128)(2,1)S(1)}, bf16[16,2432]{1,0:T(8,128)(2,1)S(1)}, u32[]{:S(2)}, u32[]{:S(2)}) collective-permute-start(bf16[16,2432]{1,0:T(8,128)(2,1)S(1)} %get-tuple-element.15), channel_id=1, source_target_pairs={{0,6},{2,8},{4,10},{6,12},{8,14},{10,0},{12,2},{14,4},{1,7},{3,9},... | collective-permute-start | bytes 233480 | tf_op jit(solution)/shard_map/ppermute | solution.py:124
  53.6 3.0 %collective-permute-start.20 = (bf16[16,2432]{1,0:T(8,128)(2,1)S(1)}, bf16[16,2432]{1,0:T(8,128)(2,1)S(1)}, u32[]{:S(2)}, u32[]{:S(2)}) collective-permute-start(bf16[16,2432]{1,0:T(8,128)(2,1)S(1)} %get-tuple-element.14), channel_id=1, source_target_pairs={{0,8},{2,10},{4,12},{6,14},{8,0},{10,2},{12,4},{14,6},{1,9},{3,11}... | collective-permute-start | bytes 233480 | tf_op jit(solution)/shard_map/ppermute | solution.py:124
  56.6 2.8 %collective-permute-done.17 = bf16[16,2432]{1,0:T(8,128)(2,1)S(1)} collective-permute-done((bf16[16,2432]{1,0:T(8,128)(2,1)S(1)}, bf16[16,2432]{1,0:T(8,128)(2,1)S(1)}, u32[]{:S(2)}, u32[]{:S(2)}) %collective-permute-start.17) | collective-permute-done | bytes 77856 | tf_op jit(solution)/shard_map/ppermute | solution.py:124
  59.5 2.3 %collective-permute-start.23 = (bf16[16,2432]{1,0:T(8,128)(2,1)S(1)}, bf16[16,2432]{1,0:T(8,128)(2,1)S(1)}, u32[]{:S(2)}, u32[]{:S(2)}) collective-permute-start(bf16[16,2432]{1,0:T(8,128)(2,1)S(1)} %get-tuple-element.13), channel_id=1, source_target_pairs={{0,14},{2,0},{4,2},{6,4},{8,6},{10,8},{12,10},{14,12},{1,15},{3,1}... | collective-permute-start | bytes 233480 | tf_op jit(solution)/shard_map/ppermute | solution.py:124
  61.9 1.8 %collective-permute-done.19 = bf16[16,2432]{1,0:T(8,128)(2,1)S(1)} collective-permute-done((bf16[16,2432]{1,0:T(8,128)(2,1)S(1)}, bf16[16,2432]{1,0:T(8,128)(2,1)S(1)}, u32[]{:S(2)}, u32[]{:S(2)}) %collective-permute-start.19) | collective-permute-done | bytes 77856 | tf_op jit(solution)/shard_map/ppermute | solution.py:124
  64.3 1.2 %collective-permute-done.22 = bf16[16,2432]{1,0:T(8,128)(2,1)S(1)} collective-permute-done((bf16[16,2432]{1,0:T(8,128)(2,1)S(1)}, bf16[16,2432]{1,0:T(8,128)(2,1)S(1)}, u32[]{:S(2)}, u32[]{:S(2)}) %collective-permute-start.22) | collective-permute-done | bytes 77856 | tf_op jit(solution)/shard_map/ppermute | solution.py:124
  69.0 5.9 %collective-permute-start.25 = (bf16[16,2432]{1,0:T(8,128)(2,1)S(1)}, bf16[16,2432]{1,0:T(8,128)(2,1)S(1)}, u32[]{:S(2)}, u32[]{:S(2)}) collective-permute-start(bf16[16,2432]{1,0:T(8,128)(2,1)S(1)} %get-tuple-element.7), channel_id=1, source_target_pairs={{0,14},{2,0},{4,2},{6,4},{8,6},{10,8},{12,10},{14,12},{1,15},{3,1}... | collective-permute-start | bytes 233480 | tf_op jit(solution)/shard_map/ppermute | solution.py:124
  75.6 2.3 %collective-permute-start.28 = (bf16[16,2432]{1,0:T(8,128)(2,1)S(1)}, bf16[16,2432]{1,0:T(8,128)(2,1)S(1)}, u32[]{:S(2)}, u32[]{:S(2)}) collective-permute-start(bf16[16,2432]{1,0:T(8,128)(2,1)S(1)} %get-tuple-element.10), channel_id=1, source_target_pairs={{0,8},{2,10},{4,12},{6,14},{8,0},{10,2},{12,4},{14,6},{1,9},{3,11}... | collective-permute-start | bytes 233480 | tf_op jit(solution)/shard_map/ppermute | solution.py:124
  77.9 2.6 %collective-permute-start.29 = (bf16[16,2432]{1,0:T(8,128)(2,1)S(1)}, bf16[16,2432]{1,0:T(8,128)(2,1)S(1)}, u32[]{:S(2)}, u32[]{:S(2)}) collective-permute-start(bf16[16,2432]{1,0:T(8,128)(2,1)S(1)} %get-tuple-element.11), channel_id=1, source_target_pairs={{0,6},{2,8},{4,10},{6,12},{8,14},{10,0},{12,2},{14,4},{1,7},{3,9},... | collective-permute-start | bytes 233480 | tf_op jit(solution)/shard_map/ppermute | solution.py:124
  80.5 7.1 %collective-permute-start.30 = (bf16[16,2432]{1,0:T(8,128)(2,1)S(1)}, bf16[16,2432]{1,0:T(8,128)(2,1)S(1)}, u32[]{:S(2)}, u32[]{:S(2)}) collective-permute-start(bf16[16,2432]{1,0:T(8,128)(2,1)S(1)} %get-tuple-element.12), channel_id=1, source_target_pairs={{0,4},{2,6},{4,8},{6,10},{8,12},{10,14},{12,0},{14,2},{1,5},{3,7},... | collective-permute-start | bytes 233480 | tf_op jit(solution)/shard_map/ppermute | solution.py:124
  87.6 2.5 %collective-permute-start.31 = (bf16[16,2432]{1,0:T(8,128)(2,1)S(1)}, bf16[16,2432]{1,0:T(8,128)(2,1)S(1)}, u32[]{:S(2)}, u32[]{:S(2)}) collective-permute-start(bf16[16,2432]{1,0:T(8,128)(2,1)S(1)} %get-tuple-element.6), channel_id=1, source_target_pairs={{0,2},{2,4},{4,6},{6,8},{8,10},{10,12},{12,14},{14,0},{1,3},{3,5},... | collective-permute-start | bytes 233480 | tf_op jit(solution)/shard_map/ppermute | solution.py:124
  90.2 4.5 %collective-permute-done.31 = bf16[16,2432]{1,0:T(8,128)(2,1)S(1)} collective-permute-done((bf16[16,2432]{1,0:T(8,128)(2,1)S(1)}, bf16[16,2432]{1,0:T(8,128)(2,1)S(1)}, u32[]{:S(2)}, u32[]{:S(2)}) %collective-permute-start.31) | collective-permute-done | bytes 77856 | tf_op jit(solution)/shard_map/ppermute | solution.py:124
  (133 shorter events, 15.3 us)
Async XLA Ops:
  4.4 14.1 %collective-permute-start.1 = (bf16[16,2432]{1,0:T(8,128)(2,1)}, bf16[16,2432]{1,0:T(8,128)(2,1)}, u32[]{:S(2)}, u32[]{:S(2)}) collective-permute-start(bf16[16,2432]{1,0:T(8,128)(2,1)} %get-tuple-element.30), channel_id=1, source_target_pairs={{0,2},{2,4},{4,6},{6,8},{8,10},{10,12},{12,14},{14,0},{1,3},{3,5},... | collective-permute-start | bytes 233480 | tf_op jit(solution)/shard_map/ppermute | solution.py:124
  7.4 12.1 %collective-permute-start.2 = (bf16[16,2432]{1,0:T(8,128)(2,1)S(1)}, bf16[16,2432]{1,0:T(8,128)(2,1)}, u32[]{:S(2)}, u32[]{:S(2)}) collective-permute-start(bf16[16,2432]{1,0:T(8,128)(2,1)S(1)} %get-tuple-element.31), channel_id=1, source_target_pairs={{0,4},{2,6},{4,8},{6,10},{8,12},{10,14},{12,0},{14,2},{1,5},{3,7},... | collective-permute-start | bytes 233480 | tf_op jit(solution)/shard_map/ppermute | solution.py:124
  9.0 12.9 %collective-permute-start.3 = (bf16[16,2432]{1,0:T(8,128)(2,1)S(1)}, bf16[16,2432]{1,0:T(8,128)(2,1)}, u32[]{:S(2)}, u32[]{:S(2)}) collective-permute-start(bf16[16,2432]{1,0:T(8,128)(2,1)S(1)} %get-tuple-element.32), channel_id=1, source_target_pairs={{0,6},{2,8},{4,10},{6,12},{8,14},{10,0},{12,2},{14,4},{1,7},{3,9},... | collective-permute-start | bytes 233480 | tf_op jit(solution)/shard_map/ppermute | solution.py:124
  11.5 13.4 %collective-permute-start.4 = (bf16[16,2432]{1,0:T(8,128)(2,1)S(1)}, bf16[16,2432]{1,0:T(8,128)(2,1)}, u32[]{:S(2)}, u32[]{:S(2)}) collective-permute-start(bf16[16,2432]{1,0:T(8,128)(2,1)S(1)} %get-tuple-element.33), channel_id=1, source_target_pairs={{0,8},{2,10},{4,12},{6,14},{8,0},{10,2},{12,4},{14,6},{1,9},{3,11}... | collective-permute-start | bytes 233480 | tf_op jit(solution)/shard_map/ppermute | solution.py:124
  12.8 13.1 %collective-permute-start.5 = (bf16[16,2432]{1,0:T(8,128)(2,1)S(1)}, bf16[16,2432]{1,0:T(8,128)(2,1)}, u32[]{:S(2)}, u32[]{:S(2)}) collective-permute-start(bf16[16,2432]{1,0:T(8,128)(2,1)S(1)} %get-tuple-element.29), channel_id=1, source_target_pairs={{0,10},{2,12},{4,14},{6,0},{8,2},{10,4},{12,6},{14,8},{1,11},{3,13... | collective-permute-start | bytes 233480 | tf_op jit(solution)/shard_map/ppermute | solution.py:124
  18.5 8.3 %collective-permute-start.8 = (bf16[512,2304]{1,0:T(8,128)(2,1)}, bf16[512,2304]{1,0:T(8,128)(2,1)S(1)}, u32[]{:S(2)}, u32[]{:S(2)}) collective-permute-start(bf16[512,2304]{1,0:T(8,128)(2,1)} %pad_maximum_fusion), channel_id=1, source_target_pairs={{0,1},{1,0},{2,3},{3,2},{4,5},{5,4},{6,7},{7,6},{8,9},{9,8},{10,11... | collective-permute-start | bytes 7077896 | tf_op jit(solution)/shard_map/ppermute | solution.py:116
  19.5 7.3 %collective-permute-start.6 = (bf16[16,2432]{1,0:T(8,128)(2,1)S(1)}, bf16[16,2432]{1,0:T(8,128)(2,1)S(1)}, u32[]{:S(2)}, u32[]{:S(2)}) collective-permute-start(bf16[16,2432]{1,0:T(8,128)(2,1)S(1)} %get-tuple-element.34), channel_id=1, source_target_pairs={{0,12},{2,14},{4,0},{6,2},{8,4},{10,6},{12,8},{14,10},{1,13},{3,15... | collective-permute-start | bytes 233480 | tf_op jit(solution)/shard_map/ppermute | solution.py:124
  21.8 5.0 %collective-permute-start.7 = (bf16[16,2432]{1,0:T(8,128)(2,1)S(1)}, bf16[16,2432]{1,0:T(8,128)(2,1)S(1)}, u32[]{:S(2)}, u32[]{:S(2)}) collective-permute-start(bf16[16,2432]{1,0:T(8,128)(2,1)S(1)} %get-tuple-element.28), channel_id=1, source_target_pairs={{0,14},{2,0},{4,2},{6,4},{8,6},{10,8},{12,10},{14,12},{1,15},{3,1}... | collective-permute-start | bytes 233480 | tf_op jit(solution)/shard_map/ppermute | solution.py:124
  24.9 3.6 %collective-permute-start = (f32[4624]{0:T(1024)S(1)}, f32[4624]{0:T(1024)S(1)}, u32[]{:S(2)}, u32[]{:S(2)}) collective-permute-start(f32[4624]{0:T(1024)S(1)} %pad_maximum_fusion.7), channel_id=1, source_target_pairs={{0,1},{1,0},{2,3},{3,2},{4,5},{5,4},{6,7},{7,6},{8,9},{9,8},{10,11... | collective-permute-start | bytes 55496 | tf_op jit(solution)/shard_map/ppermute | solution.py:116
  28.0 1.6 %collective-permute-start.9 = (f32[128,384]{1,0:T(8,128)S(1)}, f32[128,384]{1,0:T(8,128)S(1)}, u32[]{:S(2)}, u32[]{:S(2)}) collective-permute-start(f32[128,384]{1,0:T(8,128)S(1)} %pad_maximum_fusion.1), channel_id=1, source_target_pairs={{0,1},{1,0},{2,3},{3,2},{4,5},{5,4},{6,7},{7,6},{8,9},{9,8},{10,11... | collective-permute-start | bytes 589832 | tf_op jit(solution)/shard_map/ppermute | solution.py:116
  30.5 7.2 %collective-permute-start.10 = (bf16[16,2432]{1,0:T(8,128)(2,1)S(1)}, bf16[16,2432]{1,0:T(8,128)(2,1)S(1)}, u32[]{:S(2)}, u32[]{:S(2)}) collective-permute-start(bf16[16,2432]{1,0:T(8,128)(2,1)S(1)} %get-tuple-element.22), channel_id=1, source_target_pairs={{0,14},{2,0},{4,2},{6,4},{8,6},{10,8},{12,10},{14,12},{1,15},{3,1}... | collective-permute-start | bytes 233480 | tf_op jit(solution)/shard_map/ppermute | solution.py:124
  34.7 5.0 %collective-permute-start.11 = (bf16[16,2432]{1,0:T(8,128)(2,1)S(1)}, bf16[16,2432]{1,0:T(8,128)(2,1)S(1)}, u32[]{:S(2)}, u32[]{:S(2)}) collective-permute-start(bf16[16,2432]{1,0:T(8,128)(2,1)S(1)} %get-tuple-element.23), channel_id=1, source_target_pairs={{0,12},{2,14},{4,0},{6,2},{8,4},{10,6},{12,8},{14,10},{1,13},{3,15... | collective-permute-start | bytes 233480 | tf_op jit(solution)/shard_map/ppermute | solution.py:124
  34.7 6.5 %collective-permute-start.12 = (bf16[16,2432]{1,0:T(8,128)(2,1)S(1)}, bf16[16,2432]{1,0:T(8,128)(2,1)S(1)}, u32[]{:S(2)}, u32[]{:S(2)}) collective-permute-start(bf16[16,2432]{1,0:T(8,128)(2,1)S(1)} %get-tuple-element.24), channel_id=1, source_target_pairs={{0,10},{2,12},{4,14},{6,0},{8,2},{10,4},{12,6},{14,8},{1,11},{3,13... | collective-permute-start | bytes 233480 | tf_op jit(solution)/shard_map/ppermute | solution.py:124
  34.7 12.4 %collective-permute-start.13 = (bf16[16,2432]{1,0:T(8,128)(2,1)S(1)}, bf16[16,2432]{1,0:T(8,128)(2,1)S(1)}, u32[]{:S(2)}, u32[]{:S(2)}) collective-permute-start(bf16[16,2432]{1,0:T(8,128)(2,1)S(1)} %get-tuple-element.25), channel_id=1, source_target_pairs={{0,8},{2,10},{4,12},{6,14},{8,0},{10,2},{12,4},{14,6},{1,9},{3,11}... | collective-permute-start | bytes 233480 | tf_op jit(solution)/shard_map/ppermute | solution.py:124
  37.7 13.2 %collective-permute-start.14 = (bf16[16,2432]{1,0:T(8,128)(2,1)S(1)}, bf16[16,2432]{1,0:T(8,128)(2,1)S(1)}, u32[]{:S(2)}, u32[]{:S(2)}) collective-permute-start(bf16[16,2432]{1,0:T(8,128)(2,1)S(1)} %get-tuple-element.26), channel_id=1, source_target_pairs={{0,6},{2,8},{4,10},{6,12},{8,14},{10,0},{12,2},{14,4},{1,7},{3,9},... | collective-permute-start | bytes 233480 | tf_op jit(solution)/shard_map/ppermute | solution.py:124
  37.7 13.2 %collective-permute-start.15 = (bf16[16,2432]{1,0:T(8,128)(2,1)S(1)}, bf16[16,2432]{1,0:T(8,128)(2,1)S(1)}, u32[]{:S(2)}, u32[]{:S(2)}) collective-permute-start(bf16[16,2432]{1,0:T(8,128)(2,1)S(1)} %get-tuple-element.27), channel_id=1, source_target_pairs={{0,4},{2,6},{4,8},{6,10},{8,12},{10,14},{12,0},{14,2},{1,5},{3,7},... | collective-permute-start | bytes 233480 | tf_op jit(solution)/shard_map/ppermute | solution.py:124
  39.6 11.3 %collective-permute-start.16 = (bf16[16,2432]{1,0:T(8,128)(2,1)S(1)}, bf16[16,2432]{1,0:T(8,128)(2,1)S(1)}, u32[]{:S(2)}, u32[]{:S(2)}) collective-permute-start(bf16[16,2432]{1,0:T(8,128)(2,1)S(1)} %get-tuple-element.21), channel_id=1, source_target_pairs={{0,2},{2,4},{4,6},{6,8},{8,10},{10,12},{12,14},{14,0},{1,3},{3,5},... | collective-permute-start | bytes 233480 | tf_op jit(solution)/shard_map/ppermute | solution.py:124
  51.2 8.1 %collective-permute-start.17 = (bf16[16,2432]{1,0:T(8,128)(2,1)S(1)}, bf16[16,2432]{1,0:T(8,128)(2,1)S(1)}, u32[]{:S(2)}, u32[]{:S(2)}) collective-permute-start(bf16[16,2432]{1,0:T(8,128)(2,1)S(1)} %get-tuple-element.17), channel_id=1, source_target_pairs={{0,2},{2,4},{4,6},{6,8},{8,10},{10,12},{12,14},{14,0},{1,3},{3,5},... | collective-permute-start | bytes 233480 | tf_op jit(solution)/shard_map/ppermute | solution.py:124
  51.3 8.2 %collective-permute-start.18 = (bf16[16,2432]{1,0:T(8,128)(2,1)S(1)}, bf16[16,2432]{1,0:T(8,128)(2,1)S(1)}, u32[]{:S(2)}, u32[]{:S(2)}) collective-permute-start(bf16[16,2432]{1,0:T(8,128)(2,1)S(1)} %get-tuple-element.16), channel_id=1, source_target_pairs={{0,4},{2,6},{4,8},{6,10},{8,12},{10,14},{12,0},{14,2},{1,5},{3,7},... | collective-permute-start | bytes 233480 | tf_op jit(solution)/shard_map/ppermute | solution.py:124
  51.4 12.3 %collective-permute-start.19 = (bf16[16,2432]{1,0:T(8,128)(2,1)S(1)}, bf16[16,2432]{1,0:T(8,128)(2,1)S(1)}, u32[]{:S(2)}, u32[]{:S(2)}) collective-permute-start(bf16[16,2432]{1,0:T(8,128)(2,1)S(1)} %get-tuple-element.15), channel_id=1, source_target_pairs={{0,6},{2,8},{4,10},{6,12},{8,14},{10,0},{12,2},{14,4},{1,7},{3,9},... | collective-permute-start | bytes 233480 | tf_op jit(solution)/shard_map/ppermute | solution.py:124
  53.6 10.7 %collective-permute-start.20 = (bf16[16,2432]{1,0:T(8,128)(2,1)S(1)}, bf16[16,2432]{1,0:T(8,128)(2,1)S(1)}, u32[]{:S(2)}, u32[]{:S(2)}) collective-permute-start(bf16[16,2432]{1,0:T(8,128)(2,1)S(1)} %get-tuple-element.14), channel_id=1, source_target_pairs={{0,8},{2,10},{4,12},{6,14},{8,0},{10,2},{12,4},{14,6},{1,9},{3,11}... | collective-permute-start | bytes 233480 | tf_op jit(solution)/shard_map/ppermute | solution.py:124
  56.6 7.8 %collective-permute-start.21 = (bf16[16,2432]{1,0:T(8,128)(2,1)S(1)}, bf16[16,2432]{1,0:T(8,128)(2,1)S(1)}, u32[]{:S(2)}, u32[]{:S(2)}) collective-permute-start(bf16[16,2432]{1,0:T(8,128)(2,1)S(1)} %get-tuple-element.18), channel_id=1, source_target_pairs={{0,10},{2,12},{4,14},{6,0},{8,2},{10,4},{12,6},{14,8},{1,11},{3,13... | collective-permute-start | bytes 233480 | tf_op jit(solution)/shard_map/ppermute | solution.py:124
  59.3 6.2 %collective-permute-start.22 = (bf16[16,2432]{1,0:T(8,128)(2,1)S(1)}, bf16[16,2432]{1,0:T(8,128)(2,1)S(1)}, u32[]{:S(2)}, u32[]{:S(2)}) collective-permute-start(bf16[16,2432]{1,0:T(8,128)(2,1)S(1)} %get-tuple-element.19), channel_id=1, source_target_pairs={{0,12},{2,14},{4,0},{6,2},{8,4},{10,6},{12,8},{14,10},{1,13},{3,15... | collective-permute-start | bytes 233480 | tf_op jit(solution)/shard_map/ppermute | solution.py:124
  59.5 6.0 %collective-permute-start.23 = (bf16[16,2432]{1,0:T(8,128)(2,1)S(1)}, bf16[16,2432]{1,0:T(8,128)(2,1)S(1)}, u32[]{:S(2)}, u32[]{:S(2)}) collective-permute-start(bf16[16,2432]{1,0:T(8,128)(2,1)S(1)} %get-tuple-element.13), channel_id=1, source_target_pairs={{0,14},{2,0},{4,2},{6,4},{8,6},{10,8},{12,10},{14,12},{1,15},{3,1}... | collective-permute-start | bytes 233480 | tf_op jit(solution)/shard_map/ppermute | solution.py:124
  66.9 29.2 %collective-permute-start.33 = (bf16[16,2304]{1,0:T(8,128)(2,1)S(1)}, bf16[16,2304]{1,0:T(8,128)(2,1)S(1)}, u32[]{:S(2)}, u32[]{:S(2)}) collective-permute-start(bf16[16,2304]{1,0:T(8,128)(2,1)S(1)} %add_convert_fusion.1), channel_id=1, source_target_pairs={{0,1},{1,0},{2,3},{3,2},{4,5},{5,4},{6,7},{7,6},{8,9},{9,8},{10,11... | collective-permute-start | bytes 221192 | tf_op jit(solution)/shard_map/ppermute | solution.py:116
  69.0 8.9 %collective-permute-start.25 = (bf16[16,2432]{1,0:T(8,128)(2,1)S(1)}, bf16[16,2432]{1,0:T(8,128)(2,1)S(1)}, u32[]{:S(2)}, u32[]{:S(2)}) collective-permute-start(bf16[16,2432]{1,0:T(8,128)(2,1)S(1)} %get-tuple-element.7), channel_id=1, source_target_pairs={{0,14},{2,0},{4,2},{6,4},{8,6},{10,8},{12,10},{14,12},{1,15},{3,1}... | collective-permute-start | bytes 233480 | tf_op jit(solution)/shard_map/ppermute | solution.py:124
  74.9 5.6 %collective-permute-start.26 = (bf16[16,2432]{1,0:T(8,128)(2,1)S(1)}, bf16[16,2432]{1,0:T(8,128)(2,1)S(1)}, u32[]{:S(2)}, u32[]{:S(2)}) collective-permute-start(bf16[16,2432]{1,0:T(8,128)(2,1)S(1)} %get-tuple-element.8), channel_id=1, source_target_pairs={{0,12},{2,14},{4,0},{6,2},{8,4},{10,6},{12,8},{14,10},{1,13},{3,15... | collective-permute-start | bytes 233480 | tf_op jit(solution)/shard_map/ppermute | solution.py:124
  75.2 12.4 %collective-permute-start.27 = (bf16[16,2432]{1,0:T(8,128)(2,1)S(1)}, bf16[16,2432]{1,0:T(8,128)(2,1)S(1)}, u32[]{:S(2)}, u32[]{:S(2)}) collective-permute-start(bf16[16,2432]{1,0:T(8,128)(2,1)S(1)} %get-tuple-element.9), channel_id=1, source_target_pairs={{0,10},{2,12},{4,14},{6,0},{8,2},{10,4},{12,6},{14,8},{1,11},{3,13... | collective-permute-start | bytes 233480 | tf_op jit(solution)/shard_map/ppermute | solution.py:124
  75.6 14.6 %collective-permute-start.28 = (bf16[16,2432]{1,0:T(8,128)(2,1)S(1)}, bf16[16,2432]{1,0:T(8,128)(2,1)S(1)}, u32[]{:S(2)}, u32[]{:S(2)}) collective-permute-start(bf16[16,2432]{1,0:T(8,128)(2,1)S(1)} %get-tuple-element.10), channel_id=1, source_target_pairs={{0,8},{2,10},{4,12},{6,14},{8,0},{10,2},{12,4},{14,6},{1,9},{3,11}... | collective-permute-start | bytes 233480 | tf_op jit(solution)/shard_map/ppermute | solution.py:124
  77.9 12.2 %collective-permute-start.29 = (bf16[16,2432]{1,0:T(8,128)(2,1)S(1)}, bf16[16,2432]{1,0:T(8,128)(2,1)S(1)}, u32[]{:S(2)}, u32[]{:S(2)}) collective-permute-start(bf16[16,2432]{1,0:T(8,128)(2,1)S(1)} %get-tuple-element.11), channel_id=1, source_target_pairs={{0,6},{2,8},{4,10},{6,12},{8,14},{10,0},{12,2},{14,4},{1,7},{3,9},... | collective-permute-start | bytes 233480 | tf_op jit(solution)/shard_map/ppermute | solution.py:124
  80.5 9.7 %collective-permute-start.30 = (bf16[16,2432]{1,0:T(8,128)(2,1)S(1)}, bf16[16,2432]{1,0:T(8,128)(2,1)S(1)}, u32[]{:S(2)}, u32[]{:S(2)}) collective-permute-start(bf16[16,2432]{1,0:T(8,128)(2,1)S(1)} %get-tuple-element.12), channel_id=1, source_target_pairs={{0,4},{2,6},{4,8},{6,10},{8,12},{10,14},{12,0},{14,2},{1,5},{3,7},... | collective-permute-start | bytes 233480 | tf_op jit(solution)/shard_map/ppermute | solution.py:124
  87.6 7.1 %collective-permute-start.31 = (bf16[16,2432]{1,0:T(8,128)(2,1)S(1)}, bf16[16,2432]{1,0:T(8,128)(2,1)S(1)}, u32[]{:S(2)}, u32[]{:S(2)}) collective-permute-start(bf16[16,2432]{1,0:T(8,128)(2,1)S(1)} %get-tuple-element.6), channel_id=1, source_target_pairs={{0,2},{2,4},{4,6},{6,8},{8,10},{10,12},{12,14},{14,0},{1,3},{3,5},... | collective-permute-start | bytes 233480 | tf_op jit(solution)/shard_map/ppermute | solution.py:124
  (8 other events, 45.3 us)

commit v12 on v5

--- a/solution.py
+++ b/solution.py
@@ -180,6 +180,89 @@
     return attr, new_half
 
 
+def owner_layer(g_half, routes_l, acts_l, dec_full, enc_full, layer, gain_half, scale_l):
+    peers = lax.axis_size("dict")
+    me = lax.axis_index("dict")
+    here = lax.axis_index("section")
+    rows, listed = routes_l.shape
+    block = acts_l.shape[1] // listed
+    held = dec_full.shape[0] // block
+    half = g_half.shape[1]
+    owner = routes_l // held
+    within = routes_l - owner * held
+    rel = (owner - me) % peers
+    shifts = jnp.arange(peers, dtype=jnp.int32)
+    at_rel = (rel[:, :, None] == shifts[None, None, :]).astype(jnp.bfloat16)
+    act_grid = acts_l.reshape(rows, listed, block)
+    live = (act_grid > 0).astype(jnp.bfloat16) * (1 + within).astype(jnp.bfloat16)[:, :, None]
+    placed = jnp.einsum(
+        "rks,rkj->srj", at_rel, live, preferred_element_type=jnp.float32
+    ).astype(jnp.bfloat16)
+    sent = jnp.concatenate(
+        [jnp.broadcast_to(g_half[None], (peers, rows, half)), placed], axis=-1
+    )
+    got = exchange(sent, 1).reshape(peers * rows, half + block)
+    other = 1 - layer
+    lent = lax.ppermute(got[:, :half], "section", [(other, layer)])
+    halves = [None, None]
+    halves[layer] = got[:, :half]
+    halves[other] = lent
+    g_all = jnp.concatenate(halves, axis=1)
+    code = got[:, half:].astype(jnp.float32)
+    coef = lax.dot_general(
+        g_all, dec_full, (((1,), (1,)), ((), ())), preferred_element_type=jnp.float32
+    ).astype(jnp.bfloat16)
+    marks = jnp.concatenate([code == spot + 1 for spot in range(held)], axis=1)
+    dz = jnp.where(marks, coef, jnp.zeros_like(coef))
+    contrib = jnp.dot(dz, enc_full, preferred_element_type=jnp.float32).astype(jnp.bfloat16)
+    dz_pick = dz[:, :block]
+    for spot in range(1, held):
+        dz_pick = dz_pick + dz[:, spot * block:(spot + 1) * block]
+    kept = jnp.concatenate([contrib[:, layer * half:(layer + 1) * half], dz_pick], axis=-1)
+    given = jnp.concatenate([contrib[:, other * half:(other + 1) * half], dz_pick], axis=-1)
+    given = lax.ppermute(given, "section", [(layer, other)])
+    back = jnp.where(here == layer, kept, given).reshape(peers, rows, half + block)
+    returned = exchange(back, -1)
+    total = jnp.sum(returned[:, :, :half].astype(jnp.float32), axis=0)
+    dz_back = returned[:, :, half:]
+    dz_slot = jnp.einsum("rks,srj->rkj", at_rel, dz_back, preferred_element_type=jnp.float32)
+    attr = (act_grid.astype(jnp.float32) * dz_slot).reshape(rows, listed * block)
+    new_half = (g_half.astype(jnp.float32) + scale_l[:, None] * gain_half[None, :] * total).astype(
+        jnp.bfloat16
+    )
+    return attr, new_half
+
+
+def owner_device(cotangent, routes, acts, decoder, encoder, gain, inv_rms):
+    depth = lax.axis_size("section")
+    here = lax.axis_index("section")
+    rows, width = cotangent.shape
+    half = width // depth
+    mine = here * half
+    small = jnp.concatenate([gain[0], inv_rms[0]], axis=0)
+    other_small = swap_cores(small)
+    attr_keep = jnp.zeros((rows, acts.shape[2]), jnp.float32)
+    grad_keep = jnp.zeros(cotangent.shape, jnp.bfloat16)
+    g_half = lax.dynamic_slice_in_dim(cotangent, mine, half, axis=1)
+    for layer in reversed(range(depth)):
+        is_own = here == layer
+        s = jnp.where(is_own, small, other_small)
+        gain_half = lax.dynamic_slice_in_dim(s[:width], mine, half, axis=0)
+        scale_l = s[width:width + rows]
+        attr, g_half = owner_layer(
+            g_half, routes[0], acts[0], decoder[0], encoder[0], layer, gain_half, scale_l
+        )
+        partner = swap_cores(g_half)
+        full = jnp.where(
+            here == 0,
+            jnp.concatenate([g_half, partner], axis=1),
+            jnp.concatenate([partner, g_half], axis=1),
+        )
+        attr_keep = jnp.where(is_own, attr, attr_keep)
+        grad_keep = jnp.where(is_own, full, grad_keep)
+    return (attr_keep[None], grad_keep[None])
+
+
 def split_device(cotangent, routes, acts, decoder, encoder, gain, inv_rms):
     depth = lax.axis_size("section")
     here = lax.axis_index("section")
@@ -229,7 +312,7 @@
     listed = routes.shape[-1]
     width = cotangent.shape[1]
     if listed == peers and depth == 2 and width % (depth * 128) == 0:
-        return split_device(cotangent, routes, acts, decoder, encoder, gain, inv_rms)
+        return owner_device(cotangent, routes, acts, decoder, encoder, gain, inv_rms)
     return slot_device(cotangent, routes, acts, decoder, encoder, gain, inv_rms)
 
 

time: 94.1 us -> 115 us (1.22)
  waiting for transfers between devices: 20 us -> 39.8 us
  starting transfers between devices: 54.6 us -> 62.4 us
  local copies, waits for them, and re-layouts: 8.28 us -> 2.75 us
    ppermute x28, waiting for transfers between devices: 16.4 us -> 33.3 us  [exchange(): moved.append(lax.ppermute(parts[shift], 'dict', route))]
    ppermute x0 -> x4, starting transfers between devices: none -> 5.98 us  [the longest x2 3.36 us: owner_layer(): given = lax.ppermute(given, 'section', [(layer, other)])]
    ppermute x0 -> x4, waiting for transfers between devices: none -> 5.51 us  [the longest x2 4.11 us: owner_layer(): lent = lax.ppermute(got[:, :half], 'section', [(other, layer)])]
    unnamed x38 -> x42, local copies, waits for them, and re-layouts: 4.79 us -> 0.39 us
    ppermute x6 -> x3, waiting for transfers between devices: 3.57 us -> 1.02 us  [swap_cores(): return lax.ppermute(block, 'section', [(0, 1), (1, 0)])]
    dynamic_slice x4 -> x3, local copies, waits for them, and re-layouts: 2.52 us -> 1.06 us  [the longest x1 0.9 us: owner_device(): g_half = lax.dynamic_slice_in_dim(cotangent, mine, half, axis=1)]
    select_n x5, other arithmetic: 1.67 us -> 2.99 us  [the longest x2 1.37 us: owner_layer(): jnp.where(here == layer, kept, given).reshape(peers, rows, half + block)]
    dot_general x11 -> x7, matrix products: 4.18 us -> 3.4 us  [the longest x2 1.74 us: owner_layer(): lax.dot_general(g_all, dec_full, (((1,), (1,)), ((), ())), preferred_elem...]
  transfers between devices with their start and end apart: 34 -> 35, of which waited for: 12 -> 19; matrix products, arithmetic and copies ran while one was open for 12% -> 2% of each run, Pallas kernels for 0% -> 0%
where the time goes in v12:
time: 115 us
  starting transfers between devices  62.4 us (54%)
  waiting for transfers between devices  39.8 us (35%)
  other arithmetic  5.33 us (5%)
  matrix products  3.4 us (3%)
  local copies, waits for them, and re-layouts  2.75 us (2%)
  between operations  1.2 us (1%)
    ppermute x28, starting transfers between devices, exchange(): moved.append(lax.ppermute(parts[shift], 'dict', route))  54.2 us
    ppermute x28, waiting for transfers between devices, exchange(): moved.append(lax.ppermute(parts[shift], 'dict', route))  33.3 us
    ppermute x2, waiting for transfers between devices, owner_layer(): lent = lax.ppermute(got[:, :half], 'section', [(other, layer)])  4.11 us
    ppermute x2, starting transfers between devices, owner_layer(): given = lax.ppermute(given, 'section', [(layer, other)])  3.36 us
    ppermute x2, starting transfers between devices, owner_layer(): lent = lax.ppermute(got[:, :half], 'section', [(other, layer)])  2.62 us
  transfers between devices with their start and end apart: 35, of which 19 were waited for; matrix products, arithmetic and copies ran while one was open for 2% of the time, Pallas kernels for 0%

profile of v12, /device:TPU:0, one launch (start us, length us, event | category | flops | bytes accessed | tf_op | source)
XLA Modules:
  0.0 114.9 jit_solution(3347912919487221869)
XLA Ops:
  3.8 3.0 %collective-permute-start.1 = (bf16[16,2432]{1,0:T(8,128)(2,1)S(1)}, bf16[16,2432]{1,0:T(8,128)(2,1)S(1)}, u32[]{:S(2)}, u32[]{:S(2)}) collective-permute-start(bf16[16,2432]{1,0:T(8,128)(2,1)S(1)} %get-tuple-element.35), channel_id=1, source_target_pairs={{0,2},{2,4},{4,6},{6,8},{8,10},{10,12},{12,14},{14,0},{1,3},{3,5},... | collective-permute-start | bytes 233480 | tf_op jit(solution)/shard_map/ppermute | solution.py:124
  6.8 3.1 %collective-permute-start.7 = (bf16[16,2432]{1,0:T(8,128)(2,1)S(1)}, bf16[16,2432]{1,0:T(8,128)(2,1)S(1)}, u32[]{:S(2)}, u32[]{:S(2)}) collective-permute-start(bf16[16,2432]{1,0:T(8,128)(2,1)S(1)} %get-tuple-element.32), channel_id=1, source_target_pairs={{0,14},{2,0},{4,2},{6,4},{8,6},{10,8},{12,10},{14,12},{1,15},{3,1}... | collective-permute-start | bytes 233480 | tf_op jit(solution)/shard_map/ppermute | solution.py:124
  10.9 1.6 %collective-permute-start.2 = (bf16[16,2432]{1,0:T(8,128)(2,1)S(1)}, bf16[16,2432]{1,0:T(8,128)(2,1)S(1)}, u32[]{:S(2)}, u32[]{:S(2)}) collective-permute-start(bf16[16,2432]{1,0:T(8,128)(2,1)S(1)} %get-tuple-element.36), channel_id=1, source_target_pairs={{0,4},{2,6},{4,8},{6,10},{8,12},{10,14},{12,0},{14,2},{1,5},{3,7},... | collective-permute-start | bytes 233480 | tf_op jit(solution)/shard_map/ppermute | solution.py:124
  12.9 4.3 %collective-permute-start.4 = (bf16[16,2432]{1,0:T(8,128)(2,1)S(1)}, bf16[16,2432]{1,0:T(8,128)(2,1)S(1)}, u32[]{:S(2)}, u32[]{:S(2)}) collective-permute-start(bf16[16,2432]{1,0:T(8,128)(2,1)S(1)} %get-tuple-element.38), channel_id=1, source_target_pairs={{0,8},{2,10},{4,12},{6,14},{8,0},{10,2},{12,4},{14,6},{1,9},{3,11}... | collective-permute-start | bytes 233480 | tf_op jit(solution)/shard_map/ppermute | solution.py:124
  18.0 5.0 %collective-permute-done.3 = bf16[16,2432]{1,0:T(8,128)(2,1)S(1)} collective-permute-done((bf16[16,2432]{1,0:T(8,128)(2,1)S(1)}, bf16[16,2432]{1,0:T(8,128)(2,1)S(1)}, u32[]{:S(2)}, u32[]{:S(2)}) %collective-permute-start.3) | collective-permute-done | bytes 77856 | tf_op jit(solution)/shard_map/ppermute | solution.py:124
  23.6 1.3 %collective-permute-start.8 = (bf16[128,2304]{1,0:T(8,128)(2,1)S(1)}, bf16[128,2304]{1,0:T(8,128)(2,1)S(1)}, u32[]{:S(2)}, u32[]{:S(2)}) collective-permute-start(bf16[128,2304]{1,0:T(8,128)(2,1)S(1)} %slice.249), channel_id=1, source_target_pairs={{0,1},{2,3},{4,5},{6,7},{8,9},{10,11},{12,13},{14,15},{16,17},{18,... | collective-permute-start | bytes 1769480 | tf_op jit(solution)/shard_map/ppermute | solution.py:206
  24.9 1.5 %collective-permute-done.8 = bf16[128,2304]{1,0:T(8,128)(2,1)S(1)} collective-permute-done((bf16[128,2304]{1,0:T(8,128)(2,1)S(1)}, bf16[128,2304]{1,0:T(8,128)(2,1)S(1)}, u32[]{:S(2)}, u32[]{:S(2)}) %collective-permute-start.8) | collective-permute-done | bytes 589856 | tf_op jit(solution)/shard_map/ppermute | solution.py:206
  30.2 2.0 %collective-permute-start = (f32[4624]{0:T(1024)S(1)}, f32[4624]{0:T(1024)S(1)}, u32[]{:S(2)}, u32[]{:S(2)}) collective-permute-start(f32[4624]{0:T(1024)S(1)} %pad_maximum_fusion.6), channel_id=1, source_target_pairs={{0,1},{1,0},{2,3},{3,2},{4,5},{5,4},{6,7},{7,6},{8,9},{9,8},{10,11... | collective-permute-start | bytes 55496 | tf_op jit(solution)/shard_map/ppermute | solution.py:116
  34.5 4.3 %collective-permute-start.10 = (bf16[16,2432]{1,0:T(8,128)(2,1)S(1)}, bf16[16,2432]{1,0:T(8,128)(2,1)S(1)}, u32[]{:S(2)}, u32[]{:S(2)}) collective-permute-start(bf16[16,2432]{1,0:T(8,128)(2,1)S(1)} %get-tuple-element.29), channel_id=1, source_target_pairs={{0,14},{2,0},{4,2},{6,4},{8,6},{10,8},{12,10},{14,12},{1,15},{3,1}... | collective-permute-start | bytes 233480 | tf_op jit(solution)/shard_map/ppermute | solution.py:124
  38.9 2.4 %collective-permute-start.14 = (bf16[16,2432]{1,0:T(8,128)(2,1)S(1)}, bf16[16,2432]{1,0:T(8,128)(2,1)S(1)}, u32[]{:S(2)}, u32[]{:S(2)}) collective-permute-start(bf16[16,2432]{1,0:T(8,128)(2,1)S(1)} %get-tuple-element.25), channel_id=1, source_target_pairs={{0,6},{2,8},{4,10},{6,12},{8,14},{10,0},{12,2},{14,4},{1,7},{3,9},... | collective-permute-start | bytes 233480 | tf_op jit(solution)/shard_map/ppermute | solution.py:124
  41.4 2.8 %collective-permute-start.13 = (bf16[16,2432]{1,0:T(8,128)(2,1)S(1)}, bf16[16,2432]{1,0:T(8,128)(2,1)S(1)}, u32[]{:S(2)}, u32[]{:S(2)}) collective-permute-start(bf16[16,2432]{1,0:T(8,128)(2,1)S(1)} %get-tuple-element.26), channel_id=1, source_target_pairs={{0,8},{2,10},{4,12},{6,14},{8,0},{10,2},{12,4},{14,6},{1,9},{3,11}... | collective-permute-start | bytes 233480 | tf_op jit(solution)/shard_map/ppermute | solution.py:124
  44.2 2.9 %collective-permute-start.11 = (bf16[16,2432]{1,0:T(8,128)(2,1)S(1)}, bf16[16,2432]{1,0:T(8,128)(2,1)S(1)}, u32[]{:S(2)}, u32[]{:S(2)}) collective-permute-start(bf16[16,2432]{1,0:T(8,128)(2,1)S(1)} %get-tuple-element.28), channel_id=1, source_target_pairs={{0,12},{2,14},{4,0},{6,2},{8,4},{10,6},{12,8},{14,10},{1,13},{3,15... | collective-permute-start | bytes 233480 | tf_op jit(solution)/shard_map/ppermute | solution.py:124
  47.1 2.0 %collective-permute-done.11 = bf16[16,2432]{1,0:T(8,128)(2,1)S(1)} collective-permute-done((bf16[16,2432]{1,0:T(8,128)(2,1)S(1)}, bf16[16,2432]{1,0:T(8,128)(2,1)S(1)}, u32[]{:S(2)}, u32[]{:S(2)}) %collective-permute-start.11) | collective-permute-done | bytes 77856 | tf_op jit(solution)/shard_map/ppermute | solution.py:124
  49.1 5.3 %collective-permute-start.12 = (bf16[16,2432]{1,0:T(8,128)(2,1)S(1)}, bf16[16,2432]{1,0:T(8,128)(2,1)S(1)}, u32[]{:S(2)}, u32[]{:S(2)}) collective-permute-start(bf16[16,2432]{1,0:T(8,128)(2,1)S(1)} %get-tuple-element.27), channel_id=1, source_target_pairs={{0,10},{2,12},{4,14},{6,0},{8,2},{10,4},{12,6},{14,8},{1,11},{3,13... | collective-permute-start | bytes 233480 | tf_op jit(solution)/shard_map/ppermute | solution.py:124
  54.4 3.5 %collective-permute-done.12 = bf16[16,2432]{1,0:T(8,128)(2,1)S(1)} collective-permute-done((bf16[16,2432]{1,0:T(8,128)(2,1)S(1)}, bf16[16,2432]{1,0:T(8,128)(2,1)S(1)}, u32[]{:S(2)}, u32[]{:S(2)}) %collective-permute-start.12) | collective-permute-done | bytes 77856 | tf_op jit(solution)/shard_map/ppermute | solution.py:124
  58.4 4.7 %collective-permute-start.23 = (bf16[16,2432]{1,0:T(8,128)(2,1)S(1)}, bf16[16,2432]{1,0:T(8,128)(2,1)S(1)}, u32[]{:S(2)}, u32[]{:S(2)}) collective-permute-start(bf16[16,2432]{1,0:T(8,128)(2,1)S(1)} %get-tuple-element.15), channel_id=1, source_target_pairs={{0,14},{2,0},{4,2},{6,4},{8,6},{10,8},{12,10},{14,12},{1,15},{3,1}... | collective-permute-start | bytes 233480 | tf_op jit(solution)/shard_map/ppermute | solution.py:124
  64.4 1.5 %collective-permute-done.17 = bf16[16,2432]{1,0:T(8,128)(2,1)S(1)} collective-permute-done((bf16[16,2432]{1,0:T(8,128)(2,1)S(1)}, bf16[16,2432]{1,0:T(8,128)(2,1)S(1)}, u32[]{:S(2)}, u32[]{:S(2)}) %collective-permute-start.17) | collective-permute-done | bytes 77856 | tf_op jit(solution)/shard_map/ppermute | solution.py:124
  65.8 2.3 %collective-permute-start.21 = (bf16[16,2432]{1,0:T(8,128)(2,1)S(1)}, bf16[16,2432]{1,0:T(8,128)(2,1)S(1)}, u32[]{:S(2)}, u32[]{:S(2)}) collective-permute-start(bf16[16,2432]{1,0:T(8,128)(2,1)S(1)} %get-tuple-element.20), channel_id=1, source_target_pairs={{0,10},{2,12},{4,14},{6,0},{8,2},{10,4},{12,6},{14,8},{1,11},{3,13... | collective-permute-start | bytes 233480 | tf_op jit(solution)/shard_map/ppermute | solution.py:124
  68.2 3.1 %collective-permute-done.18 = bf16[16,2432]{1,0:T(8,128)(2,1)S(1)} collective-permute-done((bf16[16,2432]{1,0:T(8,128)(2,1)S(1)}, bf16[16,2432]{1,0:T(8,128)(2,1)S(1)}, u32[]{:S(2)}, u32[]{:S(2)}) %collective-permute-start.18) | collective-permute-done | bytes 77856 | tf_op jit(solution)/shard_map/ppermute | solution.py:124
  71.3 1.5 %collective-permute-start.22 = (bf16[16,2432]{1,0:T(8,128)(2,1)S(1)}, bf16[16,2432]{1,0:T(8,128)(2,1)S(1)}, u32[]{:S(2)}, u32[]{:S(2)}) collective-permute-start(bf16[16,2432]{1,0:T(8,128)(2,1)S(1)} %get-tuple-element.21), channel_id=1, source_target_pairs={{0,12},{2,14},{4,0},{6,2},{8,4},{10,6},{12,8},{14,10},{1,13},{3,15... | collective-permute-start | bytes 233480 | tf_op jit(solution)/shard_map/ppermute | solution.py:124
  74.0 2.5 %collective-permute-done.22 = bf16[16,2432]{1,0:T(8,128)(2,1)S(1)} collective-permute-done((bf16[16,2432]{1,0:T(8,128)(2,1)S(1)}, bf16[16,2432]{1,0:T(8,128)(2,1)S(1)}, u32[]{:S(2)}, u32[]{:S(2)}) %collective-permute-start.22) | collective-permute-done | bytes 77856 | tf_op jit(solution)/shard_map/ppermute | solution.py:124
  76.6 1.3 %collective-permute-start.24 = (bf16[128,2304]{1,0:T(8,128)(2,1)S(1)}, bf16[128,2304]{1,0:T(8,128)(2,1)S(1)}, u32[]{:S(2)}, u32[]{:S(2)}) collective-permute-start(bf16[128,2304]{1,0:T(8,128)(2,1)S(1)} %slice.278), channel_id=1, source_target_pairs={{1,0},{3,2},{5,4},{7,6},{9,8},{11,10},{13,12},{15,14},{17,16},{19,... | collective-permute-start | bytes 1769480 | tf_op jit(solution)/shard_map/ppermute | solution.py:206
  78.0 2.6 %collective-permute-done.24 = bf16[128,2304]{1,0:T(8,128)(2,1)S(1)} collective-permute-done((bf16[128,2304]{1,0:T(8,128)(2,1)S(1)}, bf16[128,2304]{1,0:T(8,128)(2,1)S(1)}, u32[]{:S(2)}, u32[]{:S(2)}) %collective-permute-start.24) | collective-permute-done | bytes 589856 | tf_op jit(solution)/shard_map/ppermute | solution.py:206
  82.1 2.1 %collective-permute-start.25 = (bf16[128,2432]{1,0:T(8,128)(2,1)S(1)}, bf16[128,2432]{1,0:T(8,128)(2,1)S(1)}, u32[]{:S(2)}, u32[]{:S(2)}) collective-permute-start(bf16[128,2432]{1,0:T(8,128)(2,1)S(1)} %pad_maximum_fusion.2), channel_id=1, source_target_pairs={{0,1},{2,3},{4,5},{6,7},{8,9},{10,11},{12,13},{14,15},{16,17},{18,... | collective-permute-start | bytes 1867784 | tf_op jit(solution)/shard_map/ppermute | solution.py:223
  84.4 1.4 %collective-permute-done.25 = bf16[128,2432]{1,0:T(8,128)(2,1)S(1)} collective-permute-done((bf16[128,2432]{1,0:T(8,128)(2,1)S(1)}, bf16[128,2432]{1,0:T(8,128)(2,1)S(1)}, u32[]{:S(2)}, u32[]{:S(2)}) %collective-permute-start.25) | collective-permute-done | bytes 622624 | tf_op jit(solution)/shard_map/ppermute | solution.py:223
  86.0 3.6 %collective-permute-start.26 = (bf16[16,2432]{1,0:T(8,128)(2,1)S(1)}, bf16[16,2432]{1,0:T(8,128)(2,1)S(1)}, u32[]{:S(2)}, u32[]{:S(2)}) collective-permute-start(bf16[16,2432]{1,0:T(8,128)(2,1)S(1)} %get-tuple-element.12), channel_id=1, source_target_pairs={{0,14},{2,0},{4,2},{6,4},{8,6},{10,8},{12,10},{14,12},{1,15},{3,1}... | collective-permute-start | bytes 233480 | tf_op jit(solution)/shard_map/ppermute | solution.py:124
  90.5 3.4 %collective-permute-start.30 = (bf16[16,2432]{1,0:T(8,128)(2,1)S(1)}, bf16[16,2432]{1,0:T(8,128)(2,1)S(1)}, u32[]{:S(2)}, u32[]{:S(2)}) collective-permute-start(bf16[16,2432]{1,0:T(8,128)(2,1)S(1)} %get-tuple-element.8), channel_id=1, source_target_pairs={{0,6},{2,8},{4,10},{6,12},{8,14},{10,0},{12,2},{14,4},{1,7},{3,9},... | collective-permute-start | bytes 233480 | tf_op jit(solution)/shard_map/ppermute | solution.py:124
  94.0 1.8 %collective-permute-start.27 = (bf16[16,2432]{1,0:T(8,128)(2,1)S(1)}, bf16[16,2432]{1,0:T(8,128)(2,1)S(1)}, u32[]{:S(2)}, u32[]{:S(2)}) collective-permute-start(bf16[16,2432]{1,0:T(8,128)(2,1)S(1)} %get-tuple-element.11), channel_id=1, source_target_pairs={{0,12},{2,14},{4,0},{6,2},{8,4},{10,6},{12,8},{14,10},{1,13},{3,15... | collective-permute-start | bytes 233480 | tf_op jit(solution)/shard_map/ppermute | solution.py:124
  95.8 3.8 %collective-permute-done.27 = bf16[16,2432]{1,0:T(8,128)(2,1)S(1)} collective-permute-done((bf16[16,2432]{1,0:T(8,128)(2,1)S(1)}, bf16[16,2432]{1,0:T(8,128)(2,1)S(1)}, u32[]{:S(2)}, u32[]{:S(2)}) %collective-permute-start.27) | collective-permute-done | bytes 77856 | tf_op jit(solution)/shard_map/ppermute | solution.py:124
  99.6 3.3 %collective-permute-start.28 = (bf16[16,2432]{1,0:T(8,128)(2,1)S(1)}, bf16[16,2432]{1,0:T(8,128)(2,1)S(1)}, u32[]{:S(2)}, u32[]{:S(2)}) collective-permute-start(bf16[16,2432]{1,0:T(8,128)(2,1)S(1)} %get-tuple-element.10), channel_id=1, source_target_pairs={{0,10},{2,12},{4,14},{6,0},{8,2},{10,4},{12,6},{14,8},{1,11},{3,13... | collective-permute-start | bytes 233480 | tf_op jit(solution)/shard_map/ppermute | solution.py:124
  102.9 3.5 %collective-permute-done.28 = bf16[16,2432]{1,0:T(8,128)(2,1)S(1)} collective-permute-done((bf16[16,2432]{1,0:T(8,128)(2,1)S(1)}, bf16[16,2432]{1,0:T(8,128)(2,1)S(1)}, u32[]{:S(2)}, u32[]{:S(2)}) %collective-permute-start.28) | collective-permute-done | bytes 77856 | tf_op jit(solution)/shard_map/ppermute | solution.py:124
  106.6 5.9 %collective-permute-done.29 = bf16[16,2432]{1,0:T(8,128)(2,1)S(1)} collective-permute-done((bf16[16,2432]{1,0:T(8,128)(2,1)S(1)}, bf16[16,2432]{1,0:T(8,128)(2,1)S(1)}, u32[]{:S(2)}, u32[]{:S(2)}) %collective-permute-start.29) | collective-permute-done | bytes 77856 | tf_op jit(solution)/shard_map/ppermute | solution.py:124
  (132 shorter events, 20.3 us)
Async XLA Ops:
  3.8 9.0 %collective-permute-start.1 = (bf16[16,2432]{1,0:T(8,128)(2,1)S(1)}, bf16[16,2432]{1,0:T(8,128)(2,1)S(1)}, u32[]{:S(2)}, u32[]{:S(2)}) collective-permute-start(bf16[16,2432]{1,0:T(8,128)(2,1)S(1)} %get-tuple-element.35), channel_id=1, source_target_pairs={{0,2},{2,4},{4,6},{6,8},{8,10},{10,12},{12,14},{14,0},{1,3},{3,5},... | collective-permute-start | bytes 233480 | tf_op jit(solution)/shard_map/ppermute | solution.py:124
  6.8 16.7 %collective-permute-start.7 = (bf16[16,2432]{1,0:T(8,128)(2,1)S(1)}, bf16[16,2432]{1,0:T(8,128)(2,1)S(1)}, u32[]{:S(2)}, u32[]{:S(2)}) collective-permute-start(bf16[16,2432]{1,0:T(8,128)(2,1)S(1)} %get-tuple-element.32), channel_id=1, source_target_pairs={{0,14},{2,0},{4,2},{6,4},{8,6},{10,8},{12,10},{14,12},{1,15},{3,1}... | collective-permute-start | bytes 233480 | tf_op jit(solution)/shard_map/ppermute | solution.py:124
  9.9 13.2 %collective-permute-start.5 = (bf16[16,2432]{1,0:T(8,128)(2,1)S(1)}, bf16[16,2432]{1,0:T(8,128)(2,1)S(1)}, u32[]{:S(2)}, u32[]{:S(2)}) collective-permute-start(bf16[16,2432]{1,0:T(8,128)(2,1)S(1)} %get-tuple-element.33), channel_id=1, source_target_pairs={{0,10},{2,12},{4,14},{6,0},{8,2},{10,4},{12,6},{14,8},{1,11},{3,13... | collective-permute-start | bytes 233480 | tf_op jit(solution)/shard_map/ppermute | solution.py:124
  10.9 7.0 %collective-permute-start.2 = (bf16[16,2432]{1,0:T(8,128)(2,1)S(1)}, bf16[16,2432]{1,0:T(8,128)(2,1)S(1)}, u32[]{:S(2)}, u32[]{:S(2)}) collective-permute-start(bf16[16,2432]{1,0:T(8,128)(2,1)S(1)} %get-tuple-element.36), channel_id=1, source_target_pairs={{0,4},{2,6},{4,8},{6,10},{8,12},{10,14},{12,0},{14,2},{1,5},{3,7},... | collective-permute-start | bytes 233480 | tf_op jit(solution)/shard_map/ppermute | solution.py:124
  12.5 10.5 %collective-permute-start.3 = (bf16[16,2432]{1,0:T(8,128)(2,1)S(1)}, bf16[16,2432]{1,0:T(8,128)(2,1)S(1)}, u32[]{:S(2)}, u32[]{:S(2)}) collective-permute-start(bf16[16,2432]{1,0:T(8,128)(2,1)S(1)} %get-tuple-element.37), channel_id=1, source_target_pairs={{0,6},{2,8},{4,10},{6,12},{8,14},{10,0},{12,2},{14,4},{1,7},{3,9},... | collective-permute-start | bytes 233480 | tf_op jit(solution)/shard_map/ppermute | solution.py:124
  12.9 10.3 %collective-permute-start.4 = (bf16[16,2432]{1,0:T(8,128)(2,1)S(1)}, bf16[16,2432]{1,0:T(8,128)(2,1)S(1)}, u32[]{:S(2)}, u32[]{:S(2)}) collective-permute-start(bf16[16,2432]{1,0:T(8,128)(2,1)S(1)} %get-tuple-element.38), channel_id=1, source_target_pairs={{0,8},{2,10},{4,12},{6,14},{8,0},{10,2},{12,4},{14,6},{1,9},{3,11}... | collective-permute-start | bytes 233480 | tf_op jit(solution)/shard_map/ppermute | solution.py:124
  17.9 5.6 %collective-permute-start.6 = (bf16[16,2432]{1,0:T(8,128)(2,1)S(1)}, bf16[16,2432]{1,0:T(8,128)(2,1)S(1)}, u32[]{:S(2)}, u32[]{:S(2)}) collective-permute-start(bf16[16,2432]{1,0:T(8,128)(2,1)S(1)} %get-tuple-element.39), channel_id=1, source_target_pairs={{0,12},{2,14},{4,0},{6,2},{8,4},{10,6},{12,8},{14,10},{1,13},{3,15... | collective-permute-start | bytes 233480 | tf_op jit(solution)/shard_map/ppermute | solution.py:124
  28.9 4.4 %collective-permute-start.9 = (bf16[128,2432]{1,0:T(8,128)(2,1)}, bf16[128,2432]{1,0:T(8,128)(2,1)}, u32[]{:S(2)}, u32[]{:S(2)}) collective-permute-start(bf16[128,2432]{1,0:T(8,128)(2,1)} %pad_maximum_fusion), channel_id=1, source_target_pairs={{1,0},{3,2},{5,4},{7,6},{9,8},{11,10},{13,12},{15,14},{17,16},{19,... | collective-permute-start | bytes 1867784 | tf_op jit(solution)/shard_map/ppermute | solution.py:223
  34.5 9.6 %collective-permute-start.10 = (bf16[16,2432]{1,0:T(8,128)(2,1)S(1)}, bf16[16,2432]{1,0:T(8,128)(2,1)S(1)}, u32[]{:S(2)}, u32[]{:S(2)}) collective-permute-start(bf16[16,2432]{1,0:T(8,128)(2,1)S(1)} %get-tuple-element.29), channel_id=1, source_target_pairs={{0,14},{2,0},{4,2},{6,4},{8,6},{10,8},{12,10},{14,12},{1,15},{3,1}... | collective-permute-start | bytes 233480 | tf_op jit(solution)/shard_map/ppermute | solution.py:124
  38.9 19.2 %collective-permute-start.16 = (bf16[16,2432]{1,0:T(8,128)(2,1)S(1)}, bf16[16,2432]{1,0:T(8,128)(2,1)S(1)}, u32[]{:S(2)}, u32[]{:S(2)}) collective-permute-start(bf16[16,2432]{1,0:T(8,128)(2,1)S(1)} %get-tuple-element.23), channel_id=1, source_target_pairs={{0,2},{2,4},{4,6},{6,8},{8,10},{10,12},{12,14},{14,0},{1,3},{3,5},... | collective-permute-start | bytes 233480 | tf_op jit(solution)/shard_map/ppermute | solution.py:124
  38.9 19.1 %collective-permute-start.15 = (bf16[16,2432]{1,0:T(8,128)(2,1)S(1)}, bf16[16,2432]{1,0:T(8,128)(2,1)S(1)}, u32[]{:S(2)}, u32[]{:S(2)}) collective-permute-start(bf16[16,2432]{1,0:T(8,128)(2,1)S(1)} %get-tuple-element.24), channel_id=1, source_target_pairs={{0,4},{2,6},{4,8},{6,10},{8,12},{10,14},{12,0},{14,2},{1,5},{3,7},... | collective-permute-start | bytes 233480 | tf_op jit(solution)/shard_map/ppermute | solution.py:124
  38.9 19.0 %collective-permute-start.14 = (bf16[16,2432]{1,0:T(8,128)(2,1)S(1)}, bf16[16,2432]{1,0:T(8,128)(2,1)S(1)}, u32[]{:S(2)}, u32[]{:S(2)}) collective-permute-start(bf16[16,2432]{1,0:T(8,128)(2,1)S(1)} %get-tuple-element.25), channel_id=1, source_target_pairs={{0,6},{2,8},{4,10},{6,12},{8,14},{10,0},{12,2},{14,4},{1,7},{3,9},... | collective-permute-start | bytes 233480 | tf_op jit(solution)/shard_map/ppermute | solution.py:124
  41.4 16.6 %collective-permute-start.13 = (bf16[16,2432]{1,0:T(8,128)(2,1)S(1)}, bf16[16,2432]{1,0:T(8,128)(2,1)S(1)}, u32[]{:S(2)}, u32[]{:S(2)}) collective-permute-start(bf16[16,2432]{1,0:T(8,128)(2,1)S(1)} %get-tuple-element.26), channel_id=1, source_target_pairs={{0,8},{2,10},{4,12},{6,14},{8,0},{10,2},{12,4},{14,6},{1,9},{3,11}... | collective-permute-start | bytes 233480 | tf_op jit(solution)/shard_map/ppermute | solution.py:124
  44.2 4.9 %collective-permute-start.11 = (bf16[16,2432]{1,0:T(8,128)(2,1)S(1)}, bf16[16,2432]{1,0:T(8,128)(2,1)S(1)}, u32[]{:S(2)}, u32[]{:S(2)}) collective-permute-start(bf16[16,2432]{1,0:T(8,128)(2,1)S(1)} %get-tuple-element.28), channel_id=1, source_target_pairs={{0,12},{2,14},{4,0},{6,2},{8,4},{10,6},{12,8},{14,10},{1,13},{3,15... | collective-permute-start | bytes 233480 | tf_op jit(solution)/shard_map/ppermute | solution.py:124
  49.1 8.8 %collective-permute-start.12 = (bf16[16,2432]{1,0:T(8,128)(2,1)S(1)}, bf16[16,2432]{1,0:T(8,128)(2,1)S(1)}, u32[]{:S(2)}, u32[]{:S(2)}) collective-permute-start(bf16[16,2432]{1,0:T(8,128)(2,1)S(1)} %get-tuple-element.27), channel_id=1, source_target_pairs={{0,10},{2,12},{4,14},{6,0},{8,2},{10,4},{12,6},{14,8},{1,11},{3,13... | collective-permute-start | bytes 233480 | tf_op jit(solution)/shard_map/ppermute | solution.py:124
  58.4 7.5 %collective-permute-start.17 = (bf16[16,2432]{1,0:T(8,128)(2,1)S(1)}, bf16[16,2432]{1,0:T(8,128)(2,1)S(1)}, u32[]{:S(2)}, u32[]{:S(2)}) collective-permute-start(bf16[16,2432]{1,0:T(8,128)(2,1)S(1)} %get-tuple-element.19), channel_id=1, source_target_pairs={{0,2},{2,4},{4,6},{6,8},{8,10},{10,12},{12,14},{14,0},{1,3},{3,5},... | collective-permute-start | bytes 233480 | tf_op jit(solution)/shard_map/ppermute | solution.py:124
  58.4 18.1 %collective-permute-start.23 = (bf16[16,2432]{1,0:T(8,128)(2,1)S(1)}, bf16[16,2432]{1,0:T(8,128)(2,1)S(1)}, u32[]{:S(2)}, u32[]{:S(2)}) collective-permute-start(bf16[16,2432]{1,0:T(8,128)(2,1)S(1)} %get-tuple-element.15), channel_id=1, source_target_pairs={{0,14},{2,0},{4,2},{6,4},{8,6},{10,8},{12,10},{14,12},{1,15},{3,1}... | collective-permute-start | bytes 233480 | tf_op jit(solution)/shard_map/ppermute | solution.py:124
  63.1 10.9 %collective-permute-start.20 = (bf16[16,2432]{1,0:T(8,128)(2,1)S(1)}, bf16[16,2432]{1,0:T(8,128)(2,1)S(1)}, u32[]{:S(2)}, u32[]{:S(2)}) collective-permute-start(bf16[16,2432]{1,0:T(8,128)(2,1)S(1)} %get-tuple-element.16), channel_id=1, source_target_pairs={{0,8},{2,10},{4,12},{6,14},{8,0},{10,2},{12,4},{14,6},{1,9},{3,11}... | collective-permute-start | bytes 233480 | tf_op jit(solution)/shard_map/ppermute | solution.py:124
  63.6 10.1 %collective-permute-start.19 = (bf16[16,2432]{1,0:T(8,128)(2,1)S(1)}, bf16[16,2432]{1,0:T(8,128)(2,1)S(1)}, u32[]{:S(2)}, u32[]{:S(2)}) collective-permute-start(bf16[16,2432]{1,0:T(8,128)(2,1)S(1)} %get-tuple-element.17), channel_id=1, source_target_pairs={{0,6},{2,8},{4,10},{6,12},{8,14},{10,0},{12,2},{14,4},{1,7},{3,9},... | collective-permute-start | bytes 233480 | tf_op jit(solution)/shard_map/ppermute | solution.py:124
  64.1 7.2 %collective-permute-start.18 = (bf16[16,2432]{1,0:T(8,128)(2,1)S(1)}, bf16[16,2432]{1,0:T(8,128)(2,1)S(1)}, u32[]{:S(2)}, u32[]{:S(2)}) collective-permute-start(bf16[16,2432]{1,0:T(8,128)(2,1)S(1)} %get-tuple-element.18), channel_id=1, source_target_pairs={{0,4},{2,6},{4,8},{6,10},{8,12},{10,14},{12,0},{14,2},{1,5},{3,7},... | collective-permute-start | bytes 233480 | tf_op jit(solution)/shard_map/ppermute | solution.py:124
  65.8 8.2 %collective-permute-start.21 = (bf16[16,2432]{1,0:T(8,128)(2,1)S(1)}, bf16[16,2432]{1,0:T(8,128)(2,1)S(1)}, u32[]{:S(2)}, u32[]{:S(2)}) collective-permute-start(bf16[16,2432]{1,0:T(8,128)(2,1)S(1)} %get-tuple-element.20), channel_id=1, source_target_pairs={{0,10},{2,12},{4,14},{6,0},{8,2},{10,4},{12,6},{14,8},{1,11},{3,13... | collective-permute-start | bytes 233480 | tf_op jit(solution)/shard_map/ppermute | solution.py:124
  71.3 5.3 %collective-permute-start.22 = (bf16[16,2432]{1,0:T(8,128)(2,1)S(1)}, bf16[16,2432]{1,0:T(8,128)(2,1)S(1)}, u32[]{:S(2)}, u32[]{:S(2)}) collective-permute-start(bf16[16,2432]{1,0:T(8,128)(2,1)S(1)} %get-tuple-element.21), channel_id=1, source_target_pairs={{0,12},{2,14},{4,0},{6,2},{8,4},{10,6},{12,8},{14,10},{1,13},{3,15... | collective-permute-start | bytes 233480 | tf_op jit(solution)/shard_map/ppermute | solution.py:124
  76.6 3.9 %collective-permute-start.24 = (bf16[128,2304]{1,0:T(8,128)(2,1)S(1)}, bf16[128,2304]{1,0:T(8,128)(2,1)S(1)}, u32[]{:S(2)}, u32[]{:S(2)}) collective-permute-start(bf16[128,2304]{1,0:T(8,128)(2,1)S(1)} %slice.278), channel_id=1, source_target_pairs={{1,0},{3,2},{5,4},{7,6},{9,8},{11,10},{13,12},{15,14},{17,16},{19,... | collective-permute-start | bytes 1769480 | tf_op jit(solution)/shard_map/ppermute | solution.py:206
  82.1 3.7 %collective-permute-start.25 = (bf16[128,2432]{1,0:T(8,128)(2,1)S(1)}, bf16[128,2432]{1,0:T(8,128)(2,1)S(1)}, u32[]{:S(2)}, u32[]{:S(2)}) collective-permute-start(bf16[128,2432]{1,0:T(8,128)(2,1)S(1)} %pad_maximum_fusion.2), channel_id=1, source_target_pairs={{0,1},{2,3},{4,5},{6,7},{8,9},{10,11},{12,13},{14,15},{16,17},{18,... | collective-permute-start | bytes 1867784 | tf_op jit(solution)/shard_map/ppermute | solution.py:223
  84.3 29.6 %collective-permute-start.34 = (bf16[16,2304]{1,0:T(8,128)(2,1)S(1)}, bf16[16,2304]{1,0:T(8,128)(2,1)S(1)}, u32[]{:S(2)}, u32[]{:S(2)}) collective-permute-start(bf16[16,2304]{1,0:T(8,128)(2,1)S(1)} %add_convert_fusion.1), channel_id=1, source_target_pairs={{0,1},{1,0},{2,3},{3,2},{4,5},{5,4},{6,7},{7,6},{8,9},{9,8},{10,11... | collective-permute-start | bytes 221192 | tf_op jit(solution)/shard_map/ppermute | solution.py:116
  86.0 8.0 %collective-permute-start.26 = (bf16[16,2432]{1,0:T(8,128)(2,1)S(1)}, bf16[16,2432]{1,0:T(8,128)(2,1)S(1)}, u32[]{:S(2)}, u32[]{:S(2)}) collective-permute-start(bf16[16,2432]{1,0:T(8,128)(2,1)S(1)} %get-tuple-element.12), channel_id=1, source_target_pairs={{0,14},{2,0},{4,2},{6,4},{8,6},{10,8},{12,10},{14,12},{1,15},{3,1}... | collective-permute-start | bytes 233480 | tf_op jit(solution)/shard_map/ppermute | solution.py:124
  89.5 23.0 %collective-permute-start.32 = (bf16[16,2432]{1,0:T(8,128)(2,1)S(1)}, bf16[16,2432]{1,0:T(8,128)(2,1)S(1)}, u32[]{:S(2)}, u32[]{:S(2)}) collective-permute-start(bf16[16,2432]{1,0:T(8,128)(2,1)S(1)} %get-tuple-element.6), channel_id=1, source_target_pairs={{0,2},{2,4},{4,6},{6,8},{8,10},{10,12},{12,14},{14,0},{1,3},{3,5},... | collective-permute-start | bytes 233480 | tf_op jit(solution)/shard_map/ppermute | solution.py:124
  89.6 23.0 %collective-permute-start.31 = (bf16[16,2432]{1,0:T(8,128)(2,1)S(1)}, bf16[16,2432]{1,0:T(8,128)(2,1)S(1)}, u32[]{:S(2)}, u32[]{:S(2)}) collective-permute-start(bf16[16,2432]{1,0:T(8,128)(2,1)S(1)} %get-tuple-element.7), channel_id=1, source_target_pairs={{0,4},{2,6},{4,8},{6,10},{8,12},{10,14},{12,0},{14,2},{1,5},{3,7},... | collective-permute-start | bytes 233480 | tf_op jit(solution)/shard_map/ppermute | solution.py:124
  90.5 22.0 %collective-permute-start.30 = (bf16[16,2432]{1,0:T(8,128)(2,1)S(1)}, bf16[16,2432]{1,0:T(8,128)(2,1)S(1)}, u32[]{:S(2)}, u32[]{:S(2)}) collective-permute-start(bf16[16,2432]{1,0:T(8,128)(2,1)S(1)} %get-tuple-element.8), channel_id=1, source_target_pairs={{0,6},{2,8},{4,10},{6,12},{8,14},{10,0},{12,2},{14,4},{1,7},{3,9},... | collective-permute-start | bytes 233480 | tf_op jit(solution)/shard_map/ppermute | solution.py:124
  94.0 5.6 %collective-permute-start.27 = (bf16[16,2432]{1,0:T(8,128)(2,1)S(1)}, bf16[16,2432]{1,0:T(8,128)(2,1)S(1)}, u32[]{:S(2)}, u32[]{:S(2)}) collective-permute-start(bf16[16,2432]{1,0:T(8,128)(2,1)S(1)} %get-tuple-element.11), channel_id=1, source_target_pairs={{0,12},{2,14},{4,0},{6,2},{8,4},{10,6},{12,8},{14,10},{1,13},{3,15... | collective-permute-start | bytes 233480 | tf_op jit(solution)/shard_map/ppermute | solution.py:124
  99.6 6.8 %collective-permute-start.28 = (bf16[16,2432]{1,0:T(8,128)(2,1)S(1)}, bf16[16,2432]{1,0:T(8,128)(2,1)S(1)}, u32[]{:S(2)}, u32[]{:S(2)}) collective-permute-start(bf16[16,2432]{1,0:T(8,128)(2,1)S(1)} %get-tuple-element.10), channel_id=1, source_target_pairs={{0,10},{2,12},{4,14},{6,0},{8,2},{10,4},{12,6},{14,8},{1,11},{3,13... | collective-permute-start | bytes 233480 | tf_op jit(solution)/shard_map/ppermute | solution.py:124
  106.4 6.1 %collective-permute-start.29 = (bf16[16,2432]{1,0:T(8,128)(2,1)S(1)}, bf16[16,2432]{1,0:T(8,128)(2,1)S(1)}, u32[]{:S(2)}, u32[]{:S(2)}) collective-permute-start(bf16[16,2432]{1,0:T(8,128)(2,1)S(1)} %get-tuple-element.9), channel_id=1, source_target_pairs={{0,8},{2,10},{4,12},{6,14},{8,0},{10,2},{12,4},{14,6},{1,9},{3,11}... | collective-permute-start | bytes 233480 | tf_op jit(solution)/shard_map/ppermute | solution.py:124
  (10 other events, 109.3 us)

commit v13 on v5

--- a/solution.py
+++ b/solution.py
@@ -120,7 +120,7 @@
     peers = parts.shape[0]
     moved = [parts[0]]
     for shift in range(1, peers):
-        route = [(d, (d + sign * shift) % peers) for d in range(peers)]
+        route = [(d, d ^ shift) for d in range(peers)]
         moved.append(lax.ppermute(parts[shift], "dict", route))
     return jnp.stack(moved, axis=0)
 
@@ -134,7 +134,7 @@
     half = g_half.shape[1]
     owner = routes_l // held
     within = routes_l - owner * held
-    rel = (owner - me) % peers
+    rel = lax.bitwise_xor(owner, me)
     shifts = jnp.arange(peers, dtype=jnp.int32)
     at_rel = (rel[:, :, None] == shifts[None, None, :]).astype(jnp.bfloat16)
     act_grid = acts_l.reshape(rows, listed, block)
@@ -228,7 +228,7 @@
     depth = lax.axis_size("section")
     listed = routes.shape[-1]
     width = cotangent.shape[1]
-    if listed == peers and depth == 2 and width % (depth * 128) == 0:
+    if listed == peers and peers & (peers - 1) == 0 and depth == 2 and width % (depth * 128) == 0:
         return split_device(cotangent, routes, acts, decoder, encoder, gain, inv_rms)
     return slot_device(cotangent, routes, acts, decoder, encoder, gain, inv_rms)
 

time: 94.1 us -> 95.2 us (1.012); the launches traced: 93.6 us -> 93.7 us
  starting transfers between devices: 54.6 us -> 50.6 us
  waiting for transfers between devices: 20 us -> 24 us
    ppermute x28, waiting for transfers between devices: 16.4 us -> 21.7 us  [exchange(): moved.append(lax.ppermute(parts[shift], 'dict', route))]
    ppermute x28, starting transfers between devices: 53.2 us -> 49.3 us  [exchange(): moved.append(lax.ppermute(parts[shift], 'dict', route))]
    ppermute x6, waiting for transfers between devices: 3.57 us -> 2.28 us  [swap_cores(): return lax.ppermute(block, 'section', [(0, 1), (1, 0)])]
  transfers between devices with their start and end apart: 34 -> 34, of which waited for: 12 -> 9; matrix products, arithmetic and copies ran while one was open for 12% -> 12% of each run, Pallas kernels for 0% -> 0%
where the time goes in v13:
time: 95.2 us; the launch traced here: 93.7 us
  starting transfers between devices  50.6 us (53%)
  waiting for transfers between devices  24 us (25%)
  local copies, waits for them, and re-layouts  8.28 us (9%)
  other arithmetic  5.45 us (6%)
  matrix products  4.18 us (4%)
  between operations  1.14 us (1%)
    ppermute x28, starting transfers between devices, exchange(): moved.append(lax.ppermute(parts[shift], 'dict', route))  49.3 us
    ppermute x28, waiting for transfers between devices, exchange(): moved.append(lax.ppermute(parts[shift], 'dict', route))  21.7 us
    unnamed x38, local copies, waits for them, and re-layouts  4.78 us
    ppermute x6, waiting for transfers between devices, swap_cores(): return lax.ppermute(block, 'section', [(0, 1), (1, 0)])  2.28 us
    dot_general x4, matrix products, with_dec(): lax.dot_general(g_all, dec, (((1,), (1,)), ((), ())), preferred_element_t...  2.17 us
  transfers between devices with their start and end apart: 34, of which 9 were waited for; matrix products, arithmetic and copies ran while one was open for 12% of the time, Pallas kernels for 0%

profile of v13, /device:TPU:0, one launch (start us, length us, event | category | flops | bytes accessed | tf_op | source)
XLA Modules:
  0.0 93.7 jit_solution(1837661758685607582)
XLA Ops:
  4.4 2.9 %collective-permute-start.1 = (bf16[16,2432]{1,0:T(8,128)(2,1)}, bf16[16,2432]{1,0:T(8,128)(2,1)}, u32[]{:S(2)}, u32[]{:S(2)}) collective-permute-start(bf16[16,2432]{1,0:T(8,128)(2,1)} %get-tuple-element.31), channel_id=1, source_target_pairs={{0,2},{2,0},{4,6},{6,4},{8,10},{10,8},{12,14},{14,12},{1,3},{3,1},... | collective-permute-start | bytes 233480 | tf_op jit(solution)/shard_map/ppermute | solution.py:124
  7.4 1.6 %collective-permute-start.2 = (bf16[16,2432]{1,0:T(8,128)(2,1)S(1)}, bf16[16,2432]{1,0:T(8,128)(2,1)}, u32[]{:S(2)}, u32[]{:S(2)}) collective-permute-start(bf16[16,2432]{1,0:T(8,128)(2,1)S(1)} %get-tuple-element.32), channel_id=1, source_target_pairs={{0,4},{2,6},{4,0},{6,2},{8,12},{10,14},{12,8},{14,10},{1,5},{3,7},... | collective-permute-start | bytes 233480 | tf_op jit(solution)/shard_map/ppermute | solution.py:124
  9.0 3.0 %collective-permute-start.4 = (bf16[16,2432]{1,0:T(8,128)(2,1)S(1)}, bf16[16,2432]{1,0:T(8,128)(2,1)}, u32[]{:S(2)}, u32[]{:S(2)}) collective-permute-start(bf16[16,2432]{1,0:T(8,128)(2,1)S(1)} %get-tuple-element.34), channel_id=1, source_target_pairs={{0,8},{2,10},{4,12},{6,14},{8,0},{10,2},{12,4},{14,6},{1,9},{3,11}... | collective-permute-start | bytes 233480 | tf_op jit(solution)/shard_map/ppermute | solution.py:124
  12.0 1.3 %collective-permute-start.5 = (bf16[16,2432]{1,0:T(8,128)(2,1)S(1)}, bf16[16,2432]{1,0:T(8,128)(2,1)}, u32[]{:S(2)}, u32[]{:S(2)}) collective-permute-start(bf16[16,2432]{1,0:T(8,128)(2,1)S(1)} %get-tuple-element.29), channel_id=1, source_target_pairs={{0,10},{2,8},{4,14},{6,12},{8,2},{10,0},{12,6},{14,4},{1,11},{3,9}... | collective-permute-start | bytes 233480 | tf_op jit(solution)/shard_map/ppermute | solution.py:124
  13.2 1.5 %dynamic-slice_bitcast_fusion = (bf16[256,2304]{1,0:T(8,128)(2,1)S(1)}, bf16[256,2304]{1,0:T(8,128)(2,1)S(1)}) fusion(bf16[1,256,4608]{2,1,0:T(8,128)(2,1)} %param.11, s32[]{:T(128)S(6)} %select_n.179, bf16[1,256,4608]{2,1,0:T(8,128)(2,1)S(1)} %copy-done), kind=kLoop, calls=%fused_computation.48 | loop fusion | bytes 4718596 | tf_op jit(solution)/shard_map/dynamic_slice | solution.py:196
  14.7 1.6 %pad_maximum_fusion = bf16[512,2304]{1,0:T(8,128)(2,1)} fusion(bf16[256,2304]{1,0:T(8,128)(2,1)S(1)} %get-tuple-element.40, bf16[256,2304]{1,0:T(8,128)(2,1)S(1)} %get-tuple-element.41), kind=kLoop, calls=%fused_computation.4 | loop fusion | flops 4718592 | bytes 4718592 | tf_op jit(solution)/shard_map/concatenate | solution.py:193
  16.4 3.7 %collective-permute-start.6 = (bf16[16,2432]{1,0:T(8,128)(2,1)S(1)}, bf16[16,2432]{1,0:T(8,128)(2,1)S(1)}, u32[]{:S(2)}, u32[]{:S(2)}) collective-permute-start(bf16[16,2432]{1,0:T(8,128)(2,1)S(1)} %get-tuple-element.35), channel_id=1, source_target_pairs={{0,12},{2,14},{4,8},{6,10},{8,4},{10,6},{12,0},{14,2},{1,13},{3,15... | collective-permute-start | bytes 233480 | tf_op jit(solution)/shard_map/ppermute | solution.py:124
  21.0 0.9 bitcast_dynamic-update-slice_fusion.28
  22.0 0.9 bitcast_dynamic-update-slice_fusion.27
  25.3 2.8 %collective-permute-done.7 = bf16[16,2432]{1,0:T(8,128)(2,1)S(1)} collective-permute-done((bf16[16,2432]{1,0:T(8,128)(2,1)S(1)}, bf16[16,2432]{1,0:T(8,128)(2,1)S(1)}, u32[]{:S(2)}, u32[]{:S(2)}) %collective-permute-start.7) | collective-permute-done | bytes 77856 | tf_op jit(solution)/shard_map/ppermute | solution.py:124
  29.5 1.3 %collective-permute-done.9 = f32[128,384]{1,0:T(8,128)S(1)} collective-permute-done((f32[128,384]{1,0:T(8,128)S(1)}, f32[128,384]{1,0:T(8,128)S(1)}, u32[]{:S(2)}, u32[]{:S(2)}) %collective-permute-start.9) | collective-permute-done | bytes 196640 | tf_op jit(solution)/shard_map/ppermute | solution.py:116
  32.2 2.9 %collective-permute-start.12 = (bf16[16,2432]{1,0:T(8,128)(2,1)S(1)}, bf16[16,2432]{1,0:T(8,128)(2,1)S(1)}, u32[]{:S(2)}, u32[]{:S(2)}) collective-permute-start(bf16[16,2432]{1,0:T(8,128)(2,1)S(1)} %get-tuple-element.24), channel_id=1, source_target_pairs={{0,6},{2,4},{4,2},{6,0},{8,14},{10,12},{12,10},{14,8},{1,7},{3,5},... | collective-permute-start | bytes 233480 | tf_op jit(solution)/shard_map/ppermute | solution.py:124
  35.2 1.0 %collective-permute-start.13 = (bf16[16,2432]{1,0:T(8,128)(2,1)S(1)}, bf16[16,2432]{1,0:T(8,128)(2,1)S(1)}, u32[]{:S(2)}, u32[]{:S(2)}) collective-permute-start(bf16[16,2432]{1,0:T(8,128)(2,1)S(1)} %get-tuple-element.25), channel_id=1, source_target_pairs={{0,8},{2,10},{4,12},{6,14},{8,0},{10,2},{12,4},{14,6},{1,9},{3,11}... | collective-permute-start | bytes 233480 | tf_op jit(solution)/shard_map/ppermute | solution.py:124
  36.2 1.9 %collective-permute-start.14 = (bf16[16,2432]{1,0:T(8,128)(2,1)S(1)}, bf16[16,2432]{1,0:T(8,128)(2,1)S(1)}, u32[]{:S(2)}, u32[]{:S(2)}) collective-permute-start(bf16[16,2432]{1,0:T(8,128)(2,1)S(1)} %get-tuple-element.26), channel_id=1, source_target_pairs={{0,10},{2,8},{4,14},{6,12},{8,2},{10,0},{12,6},{14,4},{1,11},{3,9}... | collective-permute-start | bytes 233480 | tf_op jit(solution)/shard_map/ppermute | solution.py:124
  38.1 3.3 %collective-permute-start.15 = (bf16[16,2432]{1,0:T(8,128)(2,1)S(1)}, bf16[16,2432]{1,0:T(8,128)(2,1)S(1)}, u32[]{:S(2)}, u32[]{:S(2)}) collective-permute-start(bf16[16,2432]{1,0:T(8,128)(2,1)S(1)} %get-tuple-element.27), channel_id=1, source_target_pairs={{0,12},{2,14},{4,8},{6,10},{8,4},{10,6},{12,0},{14,2},{1,13},{3,15... | collective-permute-start | bytes 233480 | tf_op jit(solution)/shard_map/ppermute | solution.py:124
  41.4 1.5 %collective-permute-start.16 = (bf16[16,2432]{1,0:T(8,128)(2,1)S(1)}, bf16[16,2432]{1,0:T(8,128)(2,1)S(1)}, u32[]{:S(2)}, u32[]{:S(2)}) collective-permute-start(bf16[16,2432]{1,0:T(8,128)(2,1)S(1)} %get-tuple-element.21), channel_id=1, source_target_pairs={{0,14},{2,12},{4,10},{6,8},{8,6},{10,4},{12,2},{14,0},{1,15},{3,13... | collective-permute-start | bytes 233480 | tf_op jit(solution)/shard_map/ppermute | solution.py:124
  42.9 3.5 %collective-permute-done.13 = bf16[16,2432]{1,0:T(8,128)(2,1)S(1)} collective-permute-done((bf16[16,2432]{1,0:T(8,128)(2,1)S(1)}, bf16[16,2432]{1,0:T(8,128)(2,1)S(1)}, u32[]{:S(2)}, u32[]{:S(2)}) %collective-permute-start.13) | collective-permute-done | bytes 77856 | tf_op jit(solution)/shard_map/ppermute | solution.py:124
  46.4 3.0 %collective-permute-done.14 = bf16[16,2432]{1,0:T(8,128)(2,1)S(1)} collective-permute-done((bf16[16,2432]{1,0:T(8,128)(2,1)S(1)}, bf16[16,2432]{1,0:T(8,128)(2,1)S(1)}, u32[]{:S(2)}, u32[]{:S(2)}) %collective-permute-start.14) | collective-permute-done | bytes 77856 | tf_op jit(solution)/shard_map/ppermute | solution.py:124
  49.8 1.0 %collective-permute-start.17 = (bf16[16,2432]{1,0:T(8,128)(2,1)S(1)}, bf16[16,2432]{1,0:T(8,128)(2,1)S(1)}, u32[]{:S(2)}, u32[]{:S(2)}) collective-permute-start(bf16[16,2432]{1,0:T(8,128)(2,1)S(1)} %get-tuple-element.17), channel_id=1, source_target_pairs={{0,2},{2,0},{4,6},{6,4},{8,10},{10,8},{12,14},{14,12},{1,3},{3,1},... | collective-permute-start | bytes 233480 | tf_op jit(solution)/shard_map/ppermute | solution.py:124
  50.8 3.1 %collective-permute-start.18 = (bf16[16,2432]{1,0:T(8,128)(2,1)S(1)}, bf16[16,2432]{1,0:T(8,128)(2,1)S(1)}, u32[]{:S(2)}, u32[]{:S(2)}) collective-permute-start(bf16[16,2432]{1,0:T(8,128)(2,1)S(1)} %get-tuple-element.16), channel_id=1, source_target_pairs={{0,4},{2,6},{4,0},{6,2},{8,12},{10,14},{12,8},{14,10},{1,5},{3,7},... | collective-permute-start | bytes 233480 | tf_op jit(solution)/shard_map/ppermute | solution.py:124
  54.4 3.1 %collective-permute-start.20 = (bf16[16,2432]{1,0:T(8,128)(2,1)S(1)}, bf16[16,2432]{1,0:T(8,128)(2,1)S(1)}, u32[]{:S(2)}, u32[]{:S(2)}) collective-permute-start(bf16[16,2432]{1,0:T(8,128)(2,1)S(1)} %get-tuple-element.14), channel_id=1, source_target_pairs={{0,8},{2,10},{4,12},{6,14},{8,0},{10,2},{12,4},{14,6},{1,9},{3,11}... | collective-permute-start | bytes 233480 | tf_op jit(solution)/shard_map/ppermute | solution.py:124
  57.7 2.1 %collective-permute-start.22 = (bf16[16,2432]{1,0:T(8,128)(2,1)S(1)}, bf16[16,2432]{1,0:T(8,128)(2,1)S(1)}, u32[]{:S(2)}, u32[]{:S(2)}) collective-permute-start(bf16[16,2432]{1,0:T(8,128)(2,1)S(1)} %get-tuple-element.19), channel_id=1, source_target_pairs={{0,12},{2,14},{4,8},{6,10},{8,4},{10,6},{12,0},{14,2},{1,13},{3,15... | collective-permute-start | bytes 233480 | tf_op jit(solution)/shard_map/ppermute | solution.py:124
  59.8 2.4 %collective-permute-start.23 = (bf16[16,2432]{1,0:T(8,128)(2,1)S(1)}, bf16[16,2432]{1,0:T(8,128)(2,1)S(1)}, u32[]{:S(2)}, u32[]{:S(2)}) collective-permute-start(bf16[16,2432]{1,0:T(8,128)(2,1)S(1)} %get-tuple-element.13), channel_id=1, source_target_pairs={{0,14},{2,12},{4,10},{6,8},{8,6},{10,4},{12,2},{14,0},{1,15},{3,13... | collective-permute-start | bytes 233480 | tf_op jit(solution)/shard_map/ppermute | solution.py:124
  62.3 3.5 %collective-permute-done.20 = bf16[16,2432]{1,0:T(8,128)(2,1)S(1)} collective-permute-done((bf16[16,2432]{1,0:T(8,128)(2,1)S(1)}, bf16[16,2432]{1,0:T(8,128)(2,1)S(1)}, u32[]{:S(2)}, u32[]{:S(2)}) %collective-permute-start.20) | collective-permute-done | bytes 77856 | tf_op jit(solution)/shard_map/ppermute | solution.py:124
  65.8 2.8 %collective-permute-done.21 = bf16[16,2432]{1,0:T(8,128)(2,1)S(1)} collective-permute-done((bf16[16,2432]{1,0:T(8,128)(2,1)S(1)}, bf16[16,2432]{1,0:T(8,128)(2,1)S(1)}, u32[]{:S(2)}, u32[]{:S(2)}) %collective-permute-start.21) | collective-permute-done | bytes 77856 | tf_op jit(solution)/shard_map/ppermute | solution.py:124
  72.1 1.2 %collective-permute-start.25 = (bf16[16,2432]{1,0:T(8,128)(2,1)S(1)}, bf16[16,2432]{1,0:T(8,128)(2,1)S(1)}, u32[]{:S(2)}, u32[]{:S(2)}) collective-permute-start(bf16[16,2432]{1,0:T(8,128)(2,1)S(1)} %get-tuple-element.7), channel_id=1, source_target_pairs={{0,2},{2,0},{4,6},{6,4},{8,10},{10,8},{12,14},{14,12},{1,3},{3,1},... | collective-permute-start | bytes 233480 | tf_op jit(solution)/shard_map/ppermute | solution.py:124
  73.3 3.1 %collective-permute-start.26 = (bf16[16,2432]{1,0:T(8,128)(2,1)S(1)}, bf16[16,2432]{1,0:T(8,128)(2,1)S(1)}, u32[]{:S(2)}, u32[]{:S(2)}) collective-permute-start(bf16[16,2432]{1,0:T(8,128)(2,1)S(1)} %get-tuple-element.8), channel_id=1, source_target_pairs={{0,4},{2,6},{4,0},{6,2},{8,12},{10,14},{12,8},{14,10},{1,5},{3,7},... | collective-permute-start | bytes 233480 | tf_op jit(solution)/shard_map/ppermute | solution.py:124
  77.0 2.5 %collective-permute-start.28 = (bf16[16,2432]{1,0:T(8,128)(2,1)S(1)}, bf16[16,2432]{1,0:T(8,128)(2,1)S(1)}, u32[]{:S(2)}, u32[]{:S(2)}) collective-permute-start(bf16[16,2432]{1,0:T(8,128)(2,1)S(1)} %get-tuple-element.10), channel_id=1, source_target_pairs={{0,8},{2,10},{4,12},{6,14},{8,0},{10,2},{12,4},{14,6},{1,9},{3,11}... | collective-permute-start | bytes 233480 | tf_op jit(solution)/shard_map/ppermute | solution.py:124
  79.5 1.8 %collective-permute-start.29 = (bf16[16,2432]{1,0:T(8,128)(2,1)S(1)}, bf16[16,2432]{1,0:T(8,128)(2,1)S(1)}, u32[]{:S(2)}, u32[]{:S(2)}) collective-permute-start(bf16[16,2432]{1,0:T(8,128)(2,1)S(1)} %get-tuple-element.11), channel_id=1, source_target_pairs={{0,10},{2,8},{4,14},{6,12},{8,2},{10,0},{12,6},{14,4},{1,11},{3,9}... | collective-permute-start | bytes 233480 | tf_op jit(solution)/shard_map/ppermute | solution.py:124
  81.2 1.6 %collective-permute-start.30 = (bf16[16,2432]{1,0:T(8,128)(2,1)S(1)}, bf16[16,2432]{1,0:T(8,128)(2,1)S(1)}, u32[]{:S(2)}, u32[]{:S(2)}) collective-permute-start(bf16[16,2432]{1,0:T(8,128)(2,1)S(1)} %get-tuple-element.12), channel_id=1, source_target_pairs={{0,12},{2,14},{4,8},{6,10},{8,4},{10,6},{12,0},{14,2},{1,13},{3,15... | collective-permute-start | bytes 233480 | tf_op jit(solution)/shard_map/ppermute | solution.py:124
  82.9 2.4 %collective-permute-start.31 = (bf16[16,2432]{1,0:T(8,128)(2,1)S(1)}, bf16[16,2432]{1,0:T(8,128)(2,1)S(1)}, u32[]{:S(2)}, u32[]{:S(2)}) collective-permute-start(bf16[16,2432]{1,0:T(8,128)(2,1)S(1)} %get-tuple-element.6), channel_id=1, source_target_pairs={{0,14},{2,12},{4,10},{6,8},{8,6},{10,4},{12,2},{14,0},{1,15},{3,13... | collective-permute-start | bytes 233480 | tf_op jit(solution)/shard_map/ppermute | solution.py:124
  85.3 6.1 %collective-permute-done.29 = bf16[16,2432]{1,0:T(8,128)(2,1)S(1)} collective-permute-done((bf16[16,2432]{1,0:T(8,128)(2,1)S(1)}, bf16[16,2432]{1,0:T(8,128)(2,1)S(1)}, u32[]{:S(2)}, u32[]{:S(2)}) %collective-permute-start.29) | collective-permute-done | bytes 77856 | tf_op jit(solution)/shard_map/ppermute | solution.py:124
  (132 shorter events, 17.4 us)
Async XLA Ops:
  4.4 11.9 %collective-permute-start.1 = (bf16[16,2432]{1,0:T(8,128)(2,1)}, bf16[16,2432]{1,0:T(8,128)(2,1)}, u32[]{:S(2)}, u32[]{:S(2)}) collective-permute-start(bf16[16,2432]{1,0:T(8,128)(2,1)} %get-tuple-element.31), channel_id=1, source_target_pairs={{0,2},{2,0},{4,6},{6,4},{8,10},{10,8},{12,14},{14,12},{1,3},{3,1},... | collective-permute-start | bytes 233480 | tf_op jit(solution)/shard_map/ppermute | solution.py:124
  7.4 13.6 %collective-permute-start.2 = (bf16[16,2432]{1,0:T(8,128)(2,1)S(1)}, bf16[16,2432]{1,0:T(8,128)(2,1)}, u32[]{:S(2)}, u32[]{:S(2)}) collective-permute-start(bf16[16,2432]{1,0:T(8,128)(2,1)S(1)} %get-tuple-element.32), channel_id=1, source_target_pairs={{0,4},{2,6},{4,0},{6,2},{8,12},{10,14},{12,8},{14,10},{1,5},{3,7},... | collective-permute-start | bytes 233480 | tf_op jit(solution)/shard_map/ppermute | solution.py:124
  9.0 13.0 %collective-permute-start.3 = (bf16[16,2432]{1,0:T(8,128)(2,1)S(1)}, bf16[16,2432]{1,0:T(8,128)(2,1)}, u32[]{:S(2)}, u32[]{:S(2)}) collective-permute-start(bf16[16,2432]{1,0:T(8,128)(2,1)S(1)} %get-tuple-element.33), channel_id=1, source_target_pairs={{0,6},{2,4},{4,2},{6,0},{8,14},{10,12},{12,10},{14,8},{1,7},{3,5},... | collective-permute-start | bytes 233480 | tf_op jit(solution)/shard_map/ppermute | solution.py:124
  9.0 14.0 %collective-permute-start.4 = (bf16[16,2432]{1,0:T(8,128)(2,1)S(1)}, bf16[16,2432]{1,0:T(8,128)(2,1)}, u32[]{:S(2)}, u32[]{:S(2)}) collective-permute-start(bf16[16,2432]{1,0:T(8,128)(2,1)S(1)} %get-tuple-element.34), channel_id=1, source_target_pairs={{0,8},{2,10},{4,12},{6,14},{8,0},{10,2},{12,4},{14,6},{1,9},{3,11}... | collective-permute-start | bytes 233480 | tf_op jit(solution)/shard_map/ppermute | solution.py:124
  12.0 12.4 %collective-permute-start.5 = (bf16[16,2432]{1,0:T(8,128)(2,1)S(1)}, bf16[16,2432]{1,0:T(8,128)(2,1)}, u32[]{:S(2)}, u32[]{:S(2)}) collective-permute-start(bf16[16,2432]{1,0:T(8,128)(2,1)S(1)} %get-tuple-element.29), channel_id=1, source_target_pairs={{0,10},{2,8},{4,14},{6,12},{8,2},{10,0},{12,6},{14,4},{1,11},{3,9}... | collective-permute-start | bytes 233480 | tf_op jit(solution)/shard_map/ppermute | solution.py:124
  16.4 8.9 %collective-permute-start.6 = (bf16[16,2432]{1,0:T(8,128)(2,1)S(1)}, bf16[16,2432]{1,0:T(8,128)(2,1)S(1)}, u32[]{:S(2)}, u32[]{:S(2)}) collective-permute-start(bf16[16,2432]{1,0:T(8,128)(2,1)S(1)} %get-tuple-element.35), channel_id=1, source_target_pairs={{0,12},{2,14},{4,8},{6,10},{8,4},{10,6},{12,0},{14,2},{1,13},{3,15... | collective-permute-start | bytes 233480 | tf_op jit(solution)/shard_map/ppermute | solution.py:124
  21.0 7.2 %collective-permute-start.7 = (bf16[16,2432]{1,0:T(8,128)(2,1)S(1)}, bf16[16,2432]{1,0:T(8,128)(2,1)S(1)}, u32[]{:S(2)}, u32[]{:S(2)}) collective-permute-start(bf16[16,2432]{1,0:T(8,128)(2,1)S(1)} %get-tuple-element.28), channel_id=1, source_target_pairs={{0,14},{2,12},{4,10},{6,8},{8,6},{10,4},{12,2},{14,0},{1,15},{3,13... | collective-permute-start | bytes 233480 | tf_op jit(solution)/shard_map/ppermute | solution.py:124
  21.9 6.2 %collective-permute-start.8 = (bf16[512,2304]{1,0:T(8,128)(2,1)}, bf16[512,2304]{1,0:T(8,128)(2,1)S(1)}, u32[]{:S(2)}, u32[]{:S(2)}) collective-permute-start(bf16[512,2304]{1,0:T(8,128)(2,1)} %pad_maximum_fusion), channel_id=1, source_target_pairs={{0,1},{1,0},{2,3},{3,2},{4,5},{5,4},{6,7},{7,6},{8,9},{9,8},{10,11... | collective-permute-start | bytes 7077896 | tf_op jit(solution)/shard_map/ppermute | solution.py:116
  22.9 6.4 %collective-permute-start = (f32[4624]{0:T(1024)S(1)}, f32[4624]{0:T(1024)S(1)}, u32[]{:S(2)}, u32[]{:S(2)}) collective-permute-start(f32[4624]{0:T(1024)S(1)} %pad_maximum_fusion.7), channel_id=1, source_target_pairs={{0,1},{1,0},{2,3},{3,2},{4,5},{5,4},{6,7},{7,6},{8,9},{9,8},{10,11... | collective-permute-start | bytes 55496 | tf_op jit(solution)/shard_map/ppermute | solution.py:116
  29.3 1.5 %collective-permute-start.9 = (f32[128,384]{1,0:T(8,128)S(1)}, f32[128,384]{1,0:T(8,128)S(1)}, u32[]{:S(2)}, u32[]{:S(2)}) collective-permute-start(f32[128,384]{1,0:T(8,128)S(1)} %pad_maximum_fusion.1), channel_id=1, source_target_pairs={{0,1},{1,0},{2,3},{3,2},{4,5},{5,4},{6,7},{7,6},{8,9},{9,8},{10,11... | collective-permute-start | bytes 589832 | tf_op jit(solution)/shard_map/ppermute | solution.py:116
  31.6 6.5 %collective-permute-start.10 = (bf16[16,2432]{1,0:T(8,128)(2,1)S(1)}, bf16[16,2432]{1,0:T(8,128)(2,1)S(1)}, u32[]{:S(2)}, u32[]{:S(2)}) collective-permute-start(bf16[16,2432]{1,0:T(8,128)(2,1)S(1)} %get-tuple-element.22), channel_id=1, source_target_pairs={{0,2},{2,0},{4,6},{6,4},{8,10},{10,8},{12,14},{14,12},{1,3},{3,1},... | collective-permute-start | bytes 233480 | tf_op jit(solution)/shard_map/ppermute | solution.py:124
  32.2 9.2 %collective-permute-start.11 = (bf16[16,2432]{1,0:T(8,128)(2,1)S(1)}, bf16[16,2432]{1,0:T(8,128)(2,1)S(1)}, u32[]{:S(2)}, u32[]{:S(2)}) collective-permute-start(bf16[16,2432]{1,0:T(8,128)(2,1)S(1)} %get-tuple-element.23), channel_id=1, source_target_pairs={{0,4},{2,6},{4,0},{6,2},{8,12},{10,14},{12,8},{14,10},{1,5},{3,7},... | collective-permute-start | bytes 233480 | tf_op jit(solution)/shard_map/ppermute | solution.py:124
  32.2 10.7 %collective-permute-start.12 = (bf16[16,2432]{1,0:T(8,128)(2,1)S(1)}, bf16[16,2432]{1,0:T(8,128)(2,1)S(1)}, u32[]{:S(2)}, u32[]{:S(2)}) collective-permute-start(bf16[16,2432]{1,0:T(8,128)(2,1)S(1)} %get-tuple-element.24), channel_id=1, source_target_pairs={{0,6},{2,4},{4,2},{6,0},{8,14},{10,12},{12,10},{14,8},{1,7},{3,5},... | collective-permute-start | bytes 233480 | tf_op jit(solution)/shard_map/ppermute | solution.py:124
  35.2 11.2 %collective-permute-start.13 = (bf16[16,2432]{1,0:T(8,128)(2,1)S(1)}, bf16[16,2432]{1,0:T(8,128)(2,1)S(1)}, u32[]{:S(2)}, u32[]{:S(2)}) collective-permute-start(bf16[16,2432]{1,0:T(8,128)(2,1)S(1)} %get-tuple-element.25), channel_id=1, source_target_pairs={{0,8},{2,10},{4,12},{6,14},{8,0},{10,2},{12,4},{14,6},{1,9},{3,11}... | collective-permute-start | bytes 233480 | tf_op jit(solution)/shard_map/ppermute | solution.py:124
  36.2 13.3 %collective-permute-start.14 = (bf16[16,2432]{1,0:T(8,128)(2,1)S(1)}, bf16[16,2432]{1,0:T(8,128)(2,1)S(1)}, u32[]{:S(2)}, u32[]{:S(2)}) collective-permute-start(bf16[16,2432]{1,0:T(8,128)(2,1)S(1)} %get-tuple-element.26), channel_id=1, source_target_pairs={{0,10},{2,8},{4,14},{6,12},{8,2},{10,0},{12,6},{14,4},{1,11},{3,9}... | collective-permute-start | bytes 233480 | tf_op jit(solution)/shard_map/ppermute | solution.py:124
  38.1 11.4 %collective-permute-start.15 = (bf16[16,2432]{1,0:T(8,128)(2,1)S(1)}, bf16[16,2432]{1,0:T(8,128)(2,1)S(1)}, u32[]{:S(2)}, u32[]{:S(2)}) collective-permute-start(bf16[16,2432]{1,0:T(8,128)(2,1)S(1)} %get-tuple-element.27), channel_id=1, source_target_pairs={{0,12},{2,14},{4,8},{6,10},{8,4},{10,6},{12,0},{14,2},{1,13},{3,15... | collective-permute-start | bytes 233480 | tf_op jit(solution)/shard_map/ppermute | solution.py:124
  41.4 8.1 %collective-permute-start.16 = (bf16[16,2432]{1,0:T(8,128)(2,1)S(1)}, bf16[16,2432]{1,0:T(8,128)(2,1)S(1)}, u32[]{:S(2)}, u32[]{:S(2)}) collective-permute-start(bf16[16,2432]{1,0:T(8,128)(2,1)S(1)} %get-tuple-element.21), channel_id=1, source_target_pairs={{0,14},{2,12},{4,10},{6,8},{8,6},{10,4},{12,2},{14,0},{1,15},{3,13... | collective-permute-start | bytes 233480 | tf_op jit(solution)/shard_map/ppermute | solution.py:124
  49.8 7.9 %collective-permute-start.17 = (bf16[16,2432]{1,0:T(8,128)(2,1)S(1)}, bf16[16,2432]{1,0:T(8,128)(2,1)S(1)}, u32[]{:S(2)}, u32[]{:S(2)}) collective-permute-start(bf16[16,2432]{1,0:T(8,128)(2,1)S(1)} %get-tuple-element.17), channel_id=1, source_target_pairs={{0,2},{2,0},{4,6},{6,4},{8,10},{10,8},{12,14},{14,12},{1,3},{3,1},... | collective-permute-start | bytes 233480 | tf_op jit(solution)/shard_map/ppermute | solution.py:124
  50.8 9.0 %collective-permute-start.18 = (bf16[16,2432]{1,0:T(8,128)(2,1)S(1)}, bf16[16,2432]{1,0:T(8,128)(2,1)S(1)}, u32[]{:S(2)}, u32[]{:S(2)}) collective-permute-start(bf16[16,2432]{1,0:T(8,128)(2,1)S(1)} %get-tuple-element.16), channel_id=1, source_target_pairs={{0,4},{2,6},{4,0},{6,2},{8,12},{10,14},{12,8},{14,10},{1,5},{3,7},... | collective-permute-start | bytes 233480 | tf_op jit(solution)/shard_map/ppermute | solution.py:124
  53.9 8.3 %collective-permute-start.19 = (bf16[16,2432]{1,0:T(8,128)(2,1)S(1)}, bf16[16,2432]{1,0:T(8,128)(2,1)S(1)}, u32[]{:S(2)}, u32[]{:S(2)}) collective-permute-start(bf16[16,2432]{1,0:T(8,128)(2,1)S(1)} %get-tuple-element.15), channel_id=1, source_target_pairs={{0,6},{2,4},{4,2},{6,0},{8,14},{10,12},{12,10},{14,8},{1,7},{3,5},... | collective-permute-start | bytes 233480 | tf_op jit(solution)/shard_map/ppermute | solution.py:124
  54.4 11.4 %collective-permute-start.20 = (bf16[16,2432]{1,0:T(8,128)(2,1)S(1)}, bf16[16,2432]{1,0:T(8,128)(2,1)S(1)}, u32[]{:S(2)}, u32[]{:S(2)}) collective-permute-start(bf16[16,2432]{1,0:T(8,128)(2,1)S(1)} %get-tuple-element.14), channel_id=1, source_target_pairs={{0,8},{2,10},{4,12},{6,14},{8,0},{10,2},{12,4},{14,6},{1,9},{3,11}... | collective-permute-start | bytes 233480 | tf_op jit(solution)/shard_map/ppermute | solution.py:124
  57.4 11.2 %collective-permute-start.21 = (bf16[16,2432]{1,0:T(8,128)(2,1)S(1)}, bf16[16,2432]{1,0:T(8,128)(2,1)S(1)}, u32[]{:S(2)}, u32[]{:S(2)}) collective-permute-start(bf16[16,2432]{1,0:T(8,128)(2,1)S(1)} %get-tuple-element.18), channel_id=1, source_target_pairs={{0,10},{2,8},{4,14},{6,12},{8,2},{10,0},{12,6},{14,4},{1,11},{3,9}... | collective-permute-start | bytes 233480 | tf_op jit(solution)/shard_map/ppermute | solution.py:124
  57.7 10.9 %collective-permute-start.22 = (bf16[16,2432]{1,0:T(8,128)(2,1)S(1)}, bf16[16,2432]{1,0:T(8,128)(2,1)S(1)}, u32[]{:S(2)}, u32[]{:S(2)}) collective-permute-start(bf16[16,2432]{1,0:T(8,128)(2,1)S(1)} %get-tuple-element.19), channel_id=1, source_target_pairs={{0,12},{2,14},{4,8},{6,10},{8,4},{10,6},{12,0},{14,2},{1,13},{3,15... | collective-permute-start | bytes 233480 | tf_op jit(solution)/shard_map/ppermute | solution.py:124
  59.8 8.8 %collective-permute-start.23 = (bf16[16,2432]{1,0:T(8,128)(2,1)S(1)}, bf16[16,2432]{1,0:T(8,128)(2,1)S(1)}, u32[]{:S(2)}, u32[]{:S(2)}) collective-permute-start(bf16[16,2432]{1,0:T(8,128)(2,1)S(1)} %get-tuple-element.13), channel_id=1, source_target_pairs={{0,14},{2,12},{4,10},{6,8},{8,6},{10,4},{12,2},{14,0},{1,15},{3,13... | collective-permute-start | bytes 233480 | tf_op jit(solution)/shard_map/ppermute | solution.py:124
  70.0 22.8 %collective-permute-start.33 = (bf16[16,2304]{1,0:T(8,128)(2,1)S(1)}, bf16[16,2304]{1,0:T(8,128)(2,1)S(1)}, u32[]{:S(2)}, u32[]{:S(2)}) collective-permute-start(bf16[16,2304]{1,0:T(8,128)(2,1)S(1)} %add_convert_fusion.1), channel_id=1, source_target_pairs={{0,1},{1,0},{2,3},{3,2},{4,5},{5,4},{6,7},{7,6},{8,9},{9,8},{10,11... | collective-permute-start | bytes 221192 | tf_op jit(solution)/shard_map/ppermute | solution.py:116
  72.1 7.4 %collective-permute-start.25 = (bf16[16,2432]{1,0:T(8,128)(2,1)S(1)}, bf16[16,2432]{1,0:T(8,128)(2,1)S(1)}, u32[]{:S(2)}, u32[]{:S(2)}) collective-permute-start(bf16[16,2432]{1,0:T(8,128)(2,1)S(1)} %get-tuple-element.7), channel_id=1, source_target_pairs={{0,2},{2,0},{4,6},{6,4},{8,10},{10,8},{12,14},{14,12},{1,3},{3,1},... | collective-permute-start | bytes 233480 | tf_op jit(solution)/shard_map/ppermute | solution.py:124
  73.3 7.9 %collective-permute-start.26 = (bf16[16,2432]{1,0:T(8,128)(2,1)S(1)}, bf16[16,2432]{1,0:T(8,128)(2,1)S(1)}, u32[]{:S(2)}, u32[]{:S(2)}) collective-permute-start(bf16[16,2432]{1,0:T(8,128)(2,1)S(1)} %get-tuple-element.8), channel_id=1, source_target_pairs={{0,4},{2,6},{4,0},{6,2},{8,12},{10,14},{12,8},{14,10},{1,5},{3,7},... | collective-permute-start | bytes 233480 | tf_op jit(solution)/shard_map/ppermute | solution.py:124
  76.5 6.4 %collective-permute-start.27 = (bf16[16,2432]{1,0:T(8,128)(2,1)S(1)}, bf16[16,2432]{1,0:T(8,128)(2,1)S(1)}, u32[]{:S(2)}, u32[]{:S(2)}) collective-permute-start(bf16[16,2432]{1,0:T(8,128)(2,1)S(1)} %get-tuple-element.9), channel_id=1, source_target_pairs={{0,6},{2,4},{4,2},{6,0},{8,14},{10,12},{12,10},{14,8},{1,7},{3,5},... | collective-permute-start | bytes 233480 | tf_op jit(solution)/shard_map/ppermute | solution.py:124
  77.0 8.3 %collective-permute-start.28 = (bf16[16,2432]{1,0:T(8,128)(2,1)S(1)}, bf16[16,2432]{1,0:T(8,128)(2,1)S(1)}, u32[]{:S(2)}, u32[]{:S(2)}) collective-permute-start(bf16[16,2432]{1,0:T(8,128)(2,1)S(1)} %get-tuple-element.10), channel_id=1, source_target_pairs={{0,8},{2,10},{4,12},{6,14},{8,0},{10,2},{12,4},{14,6},{1,9},{3,11}... | collective-permute-start | bytes 233480 | tf_op jit(solution)/shard_map/ppermute | solution.py:124
  79.5 11.9 %collective-permute-start.29 = (bf16[16,2432]{1,0:T(8,128)(2,1)S(1)}, bf16[16,2432]{1,0:T(8,128)(2,1)S(1)}, u32[]{:S(2)}, u32[]{:S(2)}) collective-permute-start(bf16[16,2432]{1,0:T(8,128)(2,1)S(1)} %get-tuple-element.11), channel_id=1, source_target_pairs={{0,10},{2,8},{4,14},{6,12},{8,2},{10,0},{12,6},{14,4},{1,11},{3,9}... | collective-permute-start | bytes 233480 | tf_op jit(solution)/shard_map/ppermute | solution.py:124
  81.2 10.1 %collective-permute-start.30 = (bf16[16,2432]{1,0:T(8,128)(2,1)S(1)}, bf16[16,2432]{1,0:T(8,128)(2,1)S(1)}, u32[]{:S(2)}, u32[]{:S(2)}) collective-permute-start(bf16[16,2432]{1,0:T(8,128)(2,1)S(1)} %get-tuple-element.12), channel_id=1, source_target_pairs={{0,12},{2,14},{4,8},{6,10},{8,4},{10,6},{12,0},{14,2},{1,13},{3,15... | collective-permute-start | bytes 233480 | tf_op jit(solution)/shard_map/ppermute | solution.py:124
  82.9 8.5 %collective-permute-start.31 = (bf16[16,2432]{1,0:T(8,128)(2,1)S(1)}, bf16[16,2432]{1,0:T(8,128)(2,1)S(1)}, u32[]{:S(2)}, u32[]{:S(2)}) collective-permute-start(bf16[16,2432]{1,0:T(8,128)(2,1)S(1)} %get-tuple-element.6), channel_id=1, source_target_pairs={{0,14},{2,12},{4,10},{6,8},{8,6},{10,4},{12,2},{14,0},{1,15},{3,13... | collective-permute-start | bytes 233480 | tf_op jit(solution)/shard_map/ppermute | solution.py:124
  (8 other events, 40.5 us)

commit v14 on v5

--- a/solution.py
+++ b/solution.py
@@ -154,7 +154,7 @@
             g_all, dec, (((1,), (1,)), ((), ())), preferred_element_type=jnp.float32
         )
 
-    part = jnp.where(is_own, with_dec(own[0]), with_dec(other[0]))
+    part = lax.cond(is_own, lambda: with_dec(own[0]), lambda: with_dec(other[0]))
     paired = swap_cores(jnp.concatenate([part, code_all.astype(jnp.float32)], axis=1))
     coef = (part + paired[:, :held * block]).astype(jnp.bfloat16)
     code = jnp.where(is_own, code_all.astype(jnp.float32), paired[:, held * block:])
@@ -164,7 +164,9 @@
     def with_enc(enc):
         return jnp.dot(dz, enc, preferred_element_type=jnp.float32)
 
-    contrib = jnp.where(is_own, with_enc(own[1]), with_enc(other[1])).astype(jnp.bfloat16)
+    contrib = lax.cond(is_own, lambda: with_enc(own[1]), lambda: with_enc(other[1])).astype(
+        jnp.bfloat16
+    )
     dz_pick = dz[:, :block]
     for spot in range(1, held):
         dz_pick = dz_pick + dz[:, spot * block:(spot + 1) * block]

time: 94.1 us -> 126 us (1.34); the launches traced: 93.6 us -> 124 us
  local copies, waits for them, and re-layouts: 8.28 us -> 34.1 us
  other arithmetic: 5.44 us -> 22.8 us
  starting transfers between devices: 54.6 us -> 43.2 us
  waiting for transfers between devices: 20 us -> 17.6 us
    another operation x4 -> x18, local copies, waits for them, and re-layouts: 0.05 us -> 16 us  [exchange(): return jnp.stack(moved, axis=0)]
    ppermute x28, starting transfers between devices: 53.2 us -> 42.8 us  [exchange(): moved.append(lax.ppermute(parts[shift], 'dict', route))]
    unnamed x38 -> x46, local copies, waits for them, and re-layouts: 4.79 us -> 11.9 us
    slice x2 -> x5, local copies, waits for them, and re-layouts: 0.01 us -> 3.08 us  [the longest x2 1.78 us: exchange(): moved = [parts[0]]]
    concatenate x2, other arithmetic: 0.03 us -> 2.6 us  [split_layer(): jnp.concatenate([part, code_all.astype(jnp.float32)], axis=1)]
    convert_element_type x2, other arithmetic: 0.01 us -> 2.11 us  [split_layer(): code_all.astype(jnp.float32)]
    concatenate x2, other arithmetic: 0.08 us -> 2.1 us  [split_layer(): jnp.concatenate([contrib, dz_pick], axis=-1)]
    select_n x2, other arithmetic: 0.05 us -> 1.93 us  [split_layer(): dz = jnp.where(marks, coef, jnp.zeros_like(coef))]
  transfers between devices with their start and end apart: 34 -> 34, of which waited for: 12 -> 9; matrix products, arithmetic and copies ran while one was open for 12% -> 24% of each run, Pallas kernels for 0% -> 0%
where the time goes in v14:
time: 126 us; the launch traced here: 124 us
  starting transfers between devices  43.2 us (34%)
  local copies, waits for them, and re-layouts  34.1 us (27%)
  other arithmetic  22.8 us (18%)
  waiting for transfers between devices  17.6 us (14%)
  matrix products  5.34 us (4%)
    ppermute x28, starting transfers between devices, exchange(): moved.append(lax.ppermute(parts[shift], 'dict', route))  42.8 us
    another operation x18, local copies, waits for them, and re-layouts, exchange(): return jnp.stack(moved, axis=0)  16 us
    ppermute x28, waiting for transfers between devices, exchange(): moved.append(lax.ppermute(parts[shift], 'dict', route))  14.8 us
    unnamed x46, local copies, waits for them, and re-layouts  11.9 us
    ppermute x6, waiting for transfers between devices, swap_cores(): return lax.ppermute(block, 'section', [(0, 1), (1, 0)])  2.84 us
    concatenate x2, other arithmetic, split_layer(): jnp.concatenate([part, code_all.astype(jnp.float32)], axis=1)  2.6 us
  transfers between devices with their start and end apart: 34, of which 9 were waited for; matrix products, arithmetic and copies ran while one was open for 24% of the time, Pallas kernels for 0%

profile of v14, /device:TPU:0, one launch (start us, length us, event | category | flops | bytes accessed | tf_op | source)
XLA Modules:
  0.0 124.1 jit_solution(9851234574539260578)
XLA Ops:
  4.7 2.9 %collective-permute-start.1 = (bf16[16,2432]{1,0:T(8,128)(2,1)}, bf16[16,2432]{1,0:T(8,128)(2,1)}, u32[]{:S(2)}, u32[]{:S(2)}) collective-permute-start(bf16[16,2432]{1,0:T(8,128)(2,1)} %get-tuple-element.99), channel_id=1, source_target_pairs={{0,2},{2,4},{4,6},{6,8},{8,10},{10,12},{12,14},{14,0},{1,3},{3,5},... | collective-permute-start | bytes 233480 | tf_op jit(solution)/shard_map/ppermute | solution.py:124
  7.6 1.6 %collective-permute-start.2 = (bf16[16,2432]{1,0:T(8,128)(2,1)}, bf16[16,2432]{1,0:T(8,128)(2,1)}, u32[]{:S(2)}, u32[]{:S(2)}) collective-permute-start(bf16[16,2432]{1,0:T(8,128)(2,1)} %get-tuple-element.100), channel_id=1, source_target_pairs={{0,4},{2,6},{4,8},{6,10},{8,12},{10,14},{12,0},{14,2},{1,5},{3,7},... | collective-permute-start | bytes 233480 | tf_op jit(solution)/shard_map/ppermute | solution.py:124
  9.2 2.6 %collective-permute-start.3 = (bf16[16,2432]{1,0:T(8,128)(2,1)}, bf16[16,2432]{1,0:T(8,128)(2,1)}, u32[]{:S(2)}, u32[]{:S(2)}) collective-permute-start(bf16[16,2432]{1,0:T(8,128)(2,1)} %get-tuple-element.101), channel_id=1, source_target_pairs={{0,6},{2,8},{4,10},{6,12},{8,14},{10,0},{12,2},{14,4},{1,7},{3,9},... | collective-permute-start | bytes 233480 | tf_op jit(solution)/shard_map/ppermute | solution.py:124
  13.0 2.6 %collective-permute-start.5 = (bf16[16,2432]{1,0:T(8,128)(2,1)}, bf16[16,2432]{1,0:T(8,128)(2,1)}, u32[]{:S(2)}, u32[]{:S(2)}) collective-permute-start(bf16[16,2432]{1,0:T(8,128)(2,1)} %get-tuple-element.97), channel_id=1, source_target_pairs={{0,10},{2,12},{4,14},{6,0},{8,2},{10,4},{12,6},{14,8},{1,11},{3,13... | collective-permute-start | bytes 233480 | tf_op jit(solution)/shard_map/ppermute | solution.py:124
  15.8 1.5 %copy-done.3 = bf16[1,256,4608]{2,1,0:T(8,128)(2,1)S(1)} copy-done((bf16[1,256,4608]{2,1,0:T(8,128)(2,1)S(1)}, bf16[1,256,4608]{2,1,0:T(8,128)(2,1)}, u32[]{:S(2)}) %copy-start.3) | copy-done | bytes 2359320
  17.4 1.6 %pad_maximum_fusion = bf16[512,2304]{1,0:T(8,128)(2,1)} fusion(bf16[256,2304]{1,0:T(8,128)(2,1)S(1)} %get-tuple-element.63, bf16[256,2304]{1,0:T(8,128)(2,1)S(1)} %get-tuple-element.67), kind=kLoop, calls=%fused_computation | loop fusion | flops 4718592 | bytes 4718592 | tf_op jit(solution)/shard_map/concatenate | solution.py:195
  21.3 1.5 %collective-permute-start.7 = (bf16[16,2432]{1,0:T(8,128)(2,1)S(1)}, bf16[16,2432]{1,0:T(8,128)(2,1)S(1)}, u32[]{:S(2)}, u32[]{:S(2)}) collective-permute-start(bf16[16,2432]{1,0:T(8,128)(2,1)S(1)} %copy-done.12), channel_id=1, source_target_pairs={{0,14},{2,0},{4,2},{6,4},{8,6},{10,8},{12,10},{14,12},{1,15},{3,1}... | collective-permute-start | bytes 233480 | tf_op jit(solution)/shard_map/ppermute | solution.py:124
  30.9 1.6 %pad_maximum_fusion.1 = f32[128,384]{1,0:T(8,128)} fusion(f32[128,128]{1,0:T(8,128)} %slice_convert_fusion.1, f32[128,256]{1,0:T(8,128)} %get-tuple-element.108), kind=kLoop, calls=%fused_computation.62 | loop fusion | flops 49152 | bytes 393216 | tf_op jit(solution)/shard_map/concatenate | solution.py:158
  38.0 2.1 %pad_maximum_fusion.6 = (bf16[16,2432]{1,0:T(8,128)(2,1)}, bf16[1,16,2432]{2,1,0:T(8,128)(2,1)}, bf16[16,2432]{1,0:T(8,128)(2,1)}, bf16[16,2432]{1,0:T(8,128)(2,...) fusion(bf16[128,128]{1,0:T(8,128)(2,1)} %slice_add_fusion.3, ...), kind=kLoop, calls=%fused_computation.123 | loop fusion | flops 1245184 | bytes 1245184 | tf_op jit(solution)/shard_map/concatenate | solution.py:173
  40.1 2.3 %collective-permute-start.10 = (bf16[16,2432]{1,0:T(8,128)(2,1)}, bf16[16,2432]{1,0:T(8,128)(2,1)}, u32[]{:S(2)}, u32[]{:S(2)}) collective-permute-start(bf16[16,2432]{1,0:T(8,128)(2,1)} %get-tuple-element.90), channel_id=1, source_target_pairs={{0,14},{2,0},{4,2},{6,4},{8,6},{10,8},{12,10},{14,12},{1,15},{3,1}... | collective-permute-start | bytes 233480 | tf_op jit(solution)/shard_map/ppermute | solution.py:124
  44.3 2.2 %collective-permute-start.13 = (bf16[16,2432]{1,0:T(8,128)(2,1)}, bf16[16,2432]{1,0:T(8,128)(2,1)S(1)}, u32[]{:S(2)}, u32[]{:S(2)}) collective-permute-start(bf16[16,2432]{1,0:T(8,128)(2,1)} %get-tuple-element.93), channel_id=1, source_target_pairs={{0,8},{2,10},{4,12},{6,14},{8,0},{10,2},{12,4},{14,6},{1,9},{3,11}... | collective-permute-start | bytes 233480 | tf_op jit(solution)/shard_map/ppermute | solution.py:124
  47.2 1.6 %collective-permute-start.15 = (bf16[16,2432]{1,0:T(8,128)(2,1)}, bf16[16,2432]{1,0:T(8,128)(2,1)S(1)}, u32[]{:S(2)}, u32[]{:S(2)}) collective-permute-start(bf16[16,2432]{1,0:T(8,128)(2,1)} %get-tuple-element.95), channel_id=1, source_target_pairs={{0,4},{2,6},{4,8},{6,10},{8,12},{10,14},{12,0},{14,2},{1,5},{3,7},... | collective-permute-start | bytes 233480 | tf_op jit(solution)/shard_map/ppermute | solution.py:124
  51.4 1.7 %copy.165 = bf16[1,16,2432]{2,0,1:T(2,128)(2,1)} copy(bf16[1,16,2432]{2,1,0:T(8,128)(2,1)} %get-tuple-element.89) | data formatting | bytes 155648 | tf_op jit(solution)/shard_map/slice | solution.py:121
  53.1 1.7 %copy.166 = bf16[1,16,2432]{2,0,1:T(2,128)(2,1)} copy(bf16[1,16,2432]{2,1,0:T(8,128)(2,1)} %bitcast.23) | data formatting | bytes 155648 | tf_op jit(solution)/shard_map/stack | solution.py:125
  54.8 1.7 %copy.167 = bf16[1,16,2432]{2,0,1:T(2,128)(2,1)} copy(bf16[1,16,2432]{2,1,0:T(8,128)(2,1)} %bitcast.24) | data formatting | bytes 155648 | tf_op jit(solution)/shard_map/stack | solution.py:125
  58.6 1.7 %collective-permute-done.14 = bf16[16,2432]{1,0:T(8,128)(2,1)S(1)} collective-permute-done((bf16[16,2432]{1,0:T(8,128)(2,1)}, bf16[16,2432]{1,0:T(8,128)(2,1)S(1)}, u32[]{:S(2)}, u32[]{:S(2)}) %collective-permute-start.14) | collective-permute-done | bytes 77856 | tf_op jit(solution)/shard_map/ppermute | solution.py:124
  62.7 4.5 %stack.111 = bf16[8,16,2432]{2,0,1:T(8,128)(2,1)} concatenate(bf16[1,16,2432]{2,0,1:T(2,128)(2,1)} %copy.165, bf16[1,16,2432]{2,0,1:T(2,128)(2,1)} %copy.166, bf16[1,16,2432]{2,0,1:T(2,128)(2,1)} %copy.167, bf16[1,16,2432]{2,0,1:T(2,128)(2,1)} %copy.168, bf16[1,16,2432]{2,0,1:T(2,128)(2,1)} %copy.169, bf16[1,16,2432]{2,0,1:T(2,128)(2,1)} %copy.170, bf16[1,16,2432]{2,0,1:T(2,128)(2,1)} %copy.171, ...), dimensions={0} | concatenate | bytes 1245184 | tf_op jit(solution)/shard_map/stack | solution.py:125
  67.2 1.5 %convert_reduce_fusion.1 = f32[16,2304]{1,0:T(8,128)S(1)} fusion(bf16[8,16,2432]{2,0,1:T(8,128)(2,1)} %stack.111), kind=kLoop, calls=%fused_computation.37 | loop fusion | flops 552960 | bytes 737280 | tf_op jit(solution)/shard_map/reduce_sum | solution.py:175
  70.6 2.0 %collective-permute-start.18 = (bf16[16,2432]{1,0:T(8,128)(2,1)}, bf16[16,2432]{1,0:T(8,128)(2,1)S(1)}, u32[]{:S(2)}, u32[]{:S(2)}) collective-permute-start(bf16[16,2432]{1,0:T(8,128)(2,1)} %get-tuple-element.83), channel_id=1, source_target_pairs={{0,4},{2,6},{4,8},{6,10},{8,12},{10,14},{12,0},{14,2},{1,5},{3,7},... | collective-permute-start | bytes 233480 | tf_op jit(solution)/shard_map/ppermute | solution.py:124
  73.4 2.4 %collective-permute-start.20 = (bf16[16,2432]{1,0:T(8,128)(2,1)}, bf16[16,2432]{1,0:T(8,128)(2,1)S(1)}, u32[]{:S(2)}, u32[]{:S(2)}) collective-permute-start(bf16[16,2432]{1,0:T(8,128)(2,1)} %get-tuple-element.81), channel_id=1, source_target_pairs={{0,8},{2,10},{4,12},{6,14},{8,0},{10,2},{12,4},{14,6},{1,9},{3,11}... | collective-permute-start | bytes 233480 | tf_op jit(solution)/shard_map/ppermute | solution.py:124
  75.8 1.4 %collective-permute-start.21 = (bf16[16,2432]{1,0:T(8,128)(2,1)}, bf16[16,2432]{1,0:T(8,128)(2,1)S(1)}, u32[]{:S(2)}, u32[]{:S(2)}) collective-permute-start(bf16[16,2432]{1,0:T(8,128)(2,1)} %get-tuple-element.85), channel_id=1, source_target_pairs={{0,10},{2,12},{4,14},{6,0},{8,2},{10,4},{12,6},{14,8},{1,11},{3,13... | collective-permute-start | bytes 233480 | tf_op jit(solution)/shard_map/ppermute | solution.py:124
  77.2 1.7 %collective-permute-done.17 = bf16[16,2432]{1,0:T(8,128)(2,1)} collective-permute-done((bf16[16,2432]{1,0:T(8,128)(2,1)}, bf16[16,2432]{1,0:T(8,128)(2,1)}, u32[]{:S(2)}, u32[]{:S(2)}) %collective-permute-start.17) | collective-permute-done | bytes 77856 | tf_op jit(solution)/shard_map/ppermute | solution.py:124
  79.1 1.5 %bitcast_dynamic-update-slice_fusion.6 = bf16[8,16,2432]{2,1,0:T(8,128)(2,1)} fusion(bf16[8,16,2432]{2,1,0:T(8,128)(2,1)} %get-tuple-element.87, bf16[16,2432]{1,0:T(8,128)(2,1)} %collective-permute-done.17), kind=kLoop, calls=%fused_computation.130 | loop fusion | bytes 155648
  82.5 1.8 %collective-permute-done.19 = bf16[16,2432]{1,0:T(8,128)(2,1)S(1)} collective-permute-done((bf16[16,2432]{1,0:T(8,128)(2,1)}, bf16[16,2432]{1,0:T(8,128)(2,1)S(1)}, u32[]{:S(2)}, u32[]{:S(2)}) %collective-permute-start.19) | collective-permute-done | bytes 77856 | tf_op jit(solution)/shard_map/ppermute | solution.py:124
  88.6 1.4 %slice_convert_fusion = f32[128,128]{1,0:T(8,128)} fusion(bf16[128,2432]{1,0:T(8,128)(2,1)} %bitcast.149), kind=kLoop, calls=%fused_computation.149 | loop fusion | flops 16384 | bytes 98304 | tf_op jit(solution)/shard_map/convert_element_type | solution.py:160
  92.3 1.4 %collective-permute-done.24 = f32[128,384]{1,0:T(8,128)S(1)} collective-permute-done((f32[128,384]{1,0:T(8,128)S(1)}, f32[128,384]{1,0:T(8,128)S(1)}, u32[]{:S(2)}, u32[]{:S(2)}) %collective-permute-start.24) | collective-permute-done | bytes 196640 | tf_op jit(solution)/shard_map/ppermute | solution.py:116
  95.9 5.7 %collective-permute-start.25 = (bf16[16,2432]{1,0:T(8,128)(2,1)S(1)}, bf16[16,2432]{1,0:T(8,128)(2,1)S(1)}, u32[]{:S(2)}, u32[]{:S(2)}) collective-permute-start(bf16[16,2432]{1,0:T(8,128)(2,1)S(1)} %get-tuple-element.74), channel_id=1, source_target_pairs={{0,14},{2,0},{4,2},{6,4},{8,6},{10,8},{12,10},{14,12},{1,15},{3,1}... | collective-permute-start | bytes 233480 | tf_op jit(solution)/shard_map/ppermute | solution.py:124
  101.6 3.3 %collective-permute-start.28 = (bf16[16,2432]{1,0:T(8,128)(2,1)S(1)}, bf16[16,2432]{1,0:T(8,128)(2,1)S(1)}, u32[]{:S(2)}, u32[]{:S(2)}) collective-permute-start(bf16[16,2432]{1,0:T(8,128)(2,1)S(1)} %get-tuple-element.77), channel_id=1, source_target_pairs={{0,8},{2,10},{4,12},{6,14},{8,0},{10,2},{12,4},{14,6},{1,9},{3,11}... | collective-permute-start | bytes 233480 | tf_op jit(solution)/shard_map/ppermute | solution.py:124
  104.9 1.9 %collective-permute-start.30 = (bf16[16,2432]{1,0:T(8,128)(2,1)S(1)}, bf16[16,2432]{1,0:T(8,128)(2,1)S(1)}, u32[]{:S(2)}, u32[]{:S(2)}) collective-permute-start(bf16[16,2432]{1,0:T(8,128)(2,1)S(1)} %get-tuple-element.79), channel_id=1, source_target_pairs={{0,4},{2,6},{4,8},{6,10},{8,12},{10,14},{12,0},{14,2},{1,5},{3,7},... | collective-permute-start | bytes 233480 | tf_op jit(solution)/shard_map/ppermute | solution.py:124
  108.8 6.3 %collective-permute-done.28 = bf16[16,2432]{1,0:T(8,128)(2,1)S(1)} collective-permute-done((bf16[16,2432]{1,0:T(8,128)(2,1)S(1)}, bf16[16,2432]{1,0:T(8,128)(2,1)S(1)}, u32[]{:S(2)}, u32[]{:S(2)}) %collective-permute-start.28) | collective-permute-done | bytes 77856 | tf_op jit(solution)/shard_map/ppermute | solution.py:124
  115.2 2.6 %collective-permute-done.29 = bf16[16,2432]{1,0:T(8,128)(2,1)S(1)} collective-permute-done((bf16[16,2432]{1,0:T(8,128)(2,1)S(1)}, bf16[16,2432]{1,0:T(8,128)(2,1)S(1)}, u32[]{:S(2)}, u32[]{:S(2)}) %collective-permute-start.29) | collective-permute-done | bytes 77856 | tf_op jit(solution)/shard_map/ppermute | solution.py:124
  118.2 2.7 %stack.127 = bf16[8,16,2432]{2,0,1:T(8,128)(2,1)S(1)} concatenate(bf16[1,16,2432]{2,0,1:T(2,128)(2,1)S(1)} %copy.174, bf16[1,16,2432]{2,0,1:T(2,128)(2,1)S(1)} %copy.175, bf16[1,16,2432]{2,0,1:T(2,128)(2,1)S(1)} %copy.176, bf16[1,16,2432]{2,0,1:T(2,128)(2,1)S(1)} %copy.177, bf16[1,16,2432]{2,0,1:T(2,128)(2,1)S(1)} %copy.178, bf16[1,16,2432]{2,0,1:T(2,128)(2,1)S(1)} %copy.179, ...), dimensions={0} | concatenate | bytes 1245184 | tf_op jit(solution)/shard_map/stack | solution.py:125
  (156 shorter events, 54.0 us)
Async XLA Ops:
  4.7 14.4 %collective-permute-start.1 = (bf16[16,2432]{1,0:T(8,128)(2,1)}, bf16[16,2432]{1,0:T(8,128)(2,1)}, u32[]{:S(2)}, u32[]{:S(2)}) collective-permute-start(bf16[16,2432]{1,0:T(8,128)(2,1)} %get-tuple-element.99), channel_id=1, source_target_pairs={{0,2},{2,4},{4,6},{6,8},{8,10},{10,12},{12,14},{14,0},{1,3},{3,5},... | collective-permute-start | bytes 233480 | tf_op jit(solution)/shard_map/ppermute | solution.py:124
  7.6 13.7 %collective-permute-start.2 = (bf16[16,2432]{1,0:T(8,128)(2,1)}, bf16[16,2432]{1,0:T(8,128)(2,1)}, u32[]{:S(2)}, u32[]{:S(2)}) collective-permute-start(bf16[16,2432]{1,0:T(8,128)(2,1)} %get-tuple-element.100), channel_id=1, source_target_pairs={{0,4},{2,6},{4,8},{6,10},{8,12},{10,14},{12,0},{14,2},{1,5},{3,7},... | collective-permute-start | bytes 233480 | tf_op jit(solution)/shard_map/ppermute | solution.py:124
  9.2 14.5 %collective-permute-start.3 = (bf16[16,2432]{1,0:T(8,128)(2,1)}, bf16[16,2432]{1,0:T(8,128)(2,1)}, u32[]{:S(2)}, u32[]{:S(2)}) collective-permute-start(bf16[16,2432]{1,0:T(8,128)(2,1)} %get-tuple-element.101), channel_id=1, source_target_pairs={{0,6},{2,8},{4,10},{6,12},{8,14},{10,0},{12,2},{14,4},{1,7},{3,9},... | collective-permute-start | bytes 233480 | tf_op jit(solution)/shard_map/ppermute | solution.py:124
  11.7 12.9 %collective-permute-start.4 = (bf16[16,2432]{1,0:T(8,128)(2,1)}, bf16[16,2432]{1,0:T(8,128)(2,1)}, u32[]{:S(2)}, u32[]{:S(2)}) collective-permute-start(bf16[16,2432]{1,0:T(8,128)(2,1)} %get-tuple-element.102), channel_id=1, source_target_pairs={{0,8},{2,10},{4,12},{6,14},{8,0},{10,2},{12,4},{14,6},{1,9},{3,11}... | collective-permute-start | bytes 233480 | tf_op jit(solution)/shard_map/ppermute | solution.py:124
  13.0 12.6 %collective-permute-start.5 = (bf16[16,2432]{1,0:T(8,128)(2,1)}, bf16[16,2432]{1,0:T(8,128)(2,1)}, u32[]{:S(2)}, u32[]{:S(2)}) collective-permute-start(bf16[16,2432]{1,0:T(8,128)(2,1)} %get-tuple-element.97), channel_id=1, source_target_pairs={{0,10},{2,12},{4,14},{6,0},{8,2},{10,4},{12,6},{14,8},{1,11},{3,13... | collective-permute-start | bytes 233480 | tf_op jit(solution)/shard_map/ppermute | solution.py:124
  19.0 7.4 %collective-permute-start.6 = (bf16[16,2432]{1,0:T(8,128)(2,1)S(1)}, bf16[16,2432]{1,0:T(8,128)(2,1)S(1)}, u32[]{:S(2)}, u32[]{:S(2)}) collective-permute-start(bf16[16,2432]{1,0:T(8,128)(2,1)S(1)} %copy-done.13), channel_id=1, source_target_pairs={{0,12},{2,14},{4,0},{6,2},{8,4},{10,6},{12,8},{14,10},{1,13},{3,15... | collective-permute-start | bytes 233480 | tf_op jit(solution)/shard_map/ppermute | solution.py:124
  21.3 5.2 %collective-permute-start.7 = (bf16[16,2432]{1,0:T(8,128)(2,1)S(1)}, bf16[16,2432]{1,0:T(8,128)(2,1)S(1)}, u32[]{:S(2)}, u32[]{:S(2)}) collective-permute-start(bf16[16,2432]{1,0:T(8,128)(2,1)S(1)} %copy-done.12), channel_id=1, source_target_pairs={{0,14},{2,0},{4,2},{6,4},{8,6},{10,8},{12,10},{14,12},{1,15},{3,1}... | collective-permute-start | bytes 233480 | tf_op jit(solution)/shard_map/ppermute | solution.py:124
  23.7 4.8 %collective-permute-start.8 = (bf16[512,2304]{1,0:T(8,128)(2,1)}, bf16[512,2304]{1,0:T(8,128)(2,1)S(1)}, u32[]{:S(2)}, u32[]{:S(2)}) collective-permute-start(bf16[512,2304]{1,0:T(8,128)(2,1)} %pad_maximum_fusion), channel_id=1, source_target_pairs={{0,1},{1,0},{2,3},{3,2},{4,5},{5,4},{6,7},{7,6},{8,9},{9,8},{10,11... | collective-permute-start | bytes 7077896 | tf_op jit(solution)/shard_map/ppermute | solution.py:116
  40.1 7.1 %collective-permute-start.10 = (bf16[16,2432]{1,0:T(8,128)(2,1)}, bf16[16,2432]{1,0:T(8,128)(2,1)}, u32[]{:S(2)}, u32[]{:S(2)}) collective-permute-start(bf16[16,2432]{1,0:T(8,128)(2,1)} %get-tuple-element.90), channel_id=1, source_target_pairs={{0,14},{2,0},{4,2},{6,4},{8,6},{10,8},{12,10},{14,12},{1,15},{3,1}... | collective-permute-start | bytes 233480 | tf_op jit(solution)/shard_map/ppermute | solution.py:124
  42.4 6.4 %collective-permute-start.11 = (bf16[16,2432]{1,0:T(8,128)(2,1)}, bf16[16,2432]{1,0:T(8,128)(2,1)}, u32[]{:S(2)}, u32[]{:S(2)}) collective-permute-start(bf16[16,2432]{1,0:T(8,128)(2,1)} %get-tuple-element.91), channel_id=1, source_target_pairs={{0,12},{2,14},{4,0},{6,2},{8,4},{10,6},{12,8},{14,10},{1,13},{3,15... | collective-permute-start | bytes 233480 | tf_op jit(solution)/shard_map/ppermute | solution.py:124
  43.0 3.6 %collective-permute-start = (f32[4624]{0:T(1024)}, f32[4624]{0:T(1024)}, u32[]{:S(2)}, u32[]{:S(2)}) collective-permute-start(f32[4624]{0:T(1024)} %pad_maximum_fusion.7), channel_id=1, source_target_pairs={{0,1},{1,0},{2,3},{3,2},{4,5},{5,4},{6,7},{7,6},{8,9},{9,8},{10,11... | collective-permute-start | bytes 55496 | tf_op jit(solution)/shard_map/ppermute | solution.py:116
  43.0 13.5 %collective-permute-start.12 = (bf16[16,2432]{1,0:T(8,128)(2,1)}, bf16[16,2432]{1,0:T(8,128)(2,1)S(1)}, u32[]{:S(2)}, u32[]{:S(2)}) collective-permute-start(bf16[16,2432]{1,0:T(8,128)(2,1)} %get-tuple-element.92), channel_id=1, source_target_pairs={{0,10},{2,12},{4,14},{6,0},{8,2},{10,4},{12,6},{14,8},{1,11},{3,13... | collective-permute-start | bytes 233480 | tf_op jit(solution)/shard_map/ppermute | solution.py:124
  44.3 13.5 %collective-permute-start.13 = (bf16[16,2432]{1,0:T(8,128)(2,1)}, bf16[16,2432]{1,0:T(8,128)(2,1)S(1)}, u32[]{:S(2)}, u32[]{:S(2)}) collective-permute-start(bf16[16,2432]{1,0:T(8,128)(2,1)} %get-tuple-element.93), channel_id=1, source_target_pairs={{0,8},{2,10},{4,12},{6,14},{8,0},{10,2},{12,4},{14,6},{1,9},{3,11}... | collective-permute-start | bytes 233480 | tf_op jit(solution)/shard_map/ppermute | solution.py:124
  46.5 13.8 %collective-permute-start.14 = (bf16[16,2432]{1,0:T(8,128)(2,1)}, bf16[16,2432]{1,0:T(8,128)(2,1)S(1)}, u32[]{:S(2)}, u32[]{:S(2)}) collective-permute-start(bf16[16,2432]{1,0:T(8,128)(2,1)} %get-tuple-element.94), channel_id=1, source_target_pairs={{0,6},{2,8},{4,10},{6,12},{8,14},{10,0},{12,2},{14,4},{1,7},{3,9},... | collective-permute-start | bytes 233480 | tf_op jit(solution)/shard_map/ppermute | solution.py:124
  47.2 14.0 %collective-permute-start.15 = (bf16[16,2432]{1,0:T(8,128)(2,1)}, bf16[16,2432]{1,0:T(8,128)(2,1)S(1)}, u32[]{:S(2)}, u32[]{:S(2)}) collective-permute-start(bf16[16,2432]{1,0:T(8,128)(2,1)} %get-tuple-element.95), channel_id=1, source_target_pairs={{0,4},{2,6},{4,8},{6,10},{8,12},{10,14},{12,0},{14,2},{1,5},{3,7},... | collective-permute-start | bytes 233480 | tf_op jit(solution)/shard_map/ppermute | solution.py:124
  48.7 13.2 %collective-permute-start.16 = (bf16[16,2432]{1,0:T(8,128)(2,1)}, bf16[16,2432]{1,0:T(8,128)(2,1)S(1)}, u32[]{:S(2)}, u32[]{:S(2)}) collective-permute-start(bf16[16,2432]{1,0:T(8,128)(2,1)} %get-tuple-element.88), channel_id=1, source_target_pairs={{0,2},{2,4},{4,6},{6,8},{8,10},{10,12},{12,14},{14,0},{1,3},{3,5},... | collective-permute-start | bytes 233480 | tf_op jit(solution)/shard_map/ppermute | solution.py:124
  70.6 8.4 %collective-permute-start.17 = (bf16[16,2432]{1,0:T(8,128)(2,1)}, bf16[16,2432]{1,0:T(8,128)(2,1)}, u32[]{:S(2)}, u32[]{:S(2)}) collective-permute-start(bf16[16,2432]{1,0:T(8,128)(2,1)} %get-tuple-element.84), channel_id=1, source_target_pairs={{0,2},{2,4},{4,6},{6,8},{8,10},{10,12},{12,14},{14,0},{1,3},{3,5},... | collective-permute-start | bytes 233480 | tf_op jit(solution)/shard_map/ppermute | solution.py:124
  70.6 10.0 %collective-permute-start.18 = (bf16[16,2432]{1,0:T(8,128)(2,1)}, bf16[16,2432]{1,0:T(8,128)(2,1)S(1)}, u32[]{:S(2)}, u32[]{:S(2)}) collective-permute-start(bf16[16,2432]{1,0:T(8,128)(2,1)} %get-tuple-element.83), channel_id=1, source_target_pairs={{0,4},{2,6},{4,8},{6,10},{8,12},{10,14},{12,0},{14,2},{1,5},{3,7},... | collective-permute-start | bytes 233480 | tf_op jit(solution)/shard_map/ppermute | solution.py:124
  72.6 11.7 %collective-permute-start.19 = (bf16[16,2432]{1,0:T(8,128)(2,1)}, bf16[16,2432]{1,0:T(8,128)(2,1)S(1)}, u32[]{:S(2)}, u32[]{:S(2)}) collective-permute-start(bf16[16,2432]{1,0:T(8,128)(2,1)} %get-tuple-element.82), channel_id=1, source_target_pairs={{0,6},{2,8},{4,10},{6,12},{8,14},{10,0},{12,2},{14,4},{1,7},{3,9},... | collective-permute-start | bytes 233480 | tf_op jit(solution)/shard_map/ppermute | solution.py:124
  73.4 11.6 %collective-permute-start.20 = (bf16[16,2432]{1,0:T(8,128)(2,1)}, bf16[16,2432]{1,0:T(8,128)(2,1)S(1)}, u32[]{:S(2)}, u32[]{:S(2)}) collective-permute-start(bf16[16,2432]{1,0:T(8,128)(2,1)} %get-tuple-element.81), channel_id=1, source_target_pairs={{0,8},{2,10},{4,12},{6,14},{8,0},{10,2},{12,4},{14,6},{1,9},{3,11}... | collective-permute-start | bytes 233480 | tf_op jit(solution)/shard_map/ppermute | solution.py:124
  75.8 9.7 %collective-permute-start.21 = (bf16[16,2432]{1,0:T(8,128)(2,1)}, bf16[16,2432]{1,0:T(8,128)(2,1)S(1)}, u32[]{:S(2)}, u32[]{:S(2)}) collective-permute-start(bf16[16,2432]{1,0:T(8,128)(2,1)} %get-tuple-element.85), channel_id=1, source_target_pairs={{0,10},{2,12},{4,14},{6,0},{8,2},{10,4},{12,6},{14,8},{1,11},{3,13... | collective-permute-start | bytes 233480 | tf_op jit(solution)/shard_map/ppermute | solution.py:124
  78.9 7.3 %collective-permute-start.22 = (bf16[16,2432]{1,0:T(8,128)(2,1)}, bf16[16,2432]{1,0:T(8,128)(2,1)S(1)}, u32[]{:S(2)}, u32[]{:S(2)}) collective-permute-start(bf16[16,2432]{1,0:T(8,128)(2,1)} %get-tuple-element.86), channel_id=1, source_target_pairs={{0,12},{2,14},{4,0},{6,2},{8,4},{10,6},{12,8},{14,10},{1,13},{3,15... | collective-permute-start | bytes 233480 | tf_op jit(solution)/shard_map/ppermute | solution.py:124
  80.6 6.3 %collective-permute-start.23 = (bf16[16,2432]{1,0:T(8,128)(2,1)}, bf16[16,2432]{1,0:T(8,128)(2,1)S(1)}, u32[]{:S(2)}, u32[]{:S(2)}) collective-permute-start(bf16[16,2432]{1,0:T(8,128)(2,1)} %get-tuple-element.80), channel_id=1, source_target_pairs={{0,14},{2,0},{4,2},{6,4},{8,6},{10,8},{12,10},{14,12},{1,15},{3,1}... | collective-permute-start | bytes 233480 | tf_op jit(solution)/shard_map/ppermute | solution.py:124
  95.9 9.0 %collective-permute-start.25 = (bf16[16,2432]{1,0:T(8,128)(2,1)S(1)}, bf16[16,2432]{1,0:T(8,128)(2,1)S(1)}, u32[]{:S(2)}, u32[]{:S(2)}) collective-permute-start(bf16[16,2432]{1,0:T(8,128)(2,1)S(1)} %get-tuple-element.74), channel_id=1, source_target_pairs={{0,14},{2,0},{4,2},{6,4},{8,6},{10,8},{12,10},{14,12},{1,15},{3,1}... | collective-permute-start | bytes 233480 | tf_op jit(solution)/shard_map/ppermute | solution.py:124
  101.6 5.2 %collective-permute-start.26 = (bf16[16,2432]{1,0:T(8,128)(2,1)S(1)}, bf16[16,2432]{1,0:T(8,128)(2,1)S(1)}, u32[]{:S(2)}, u32[]{:S(2)}) collective-permute-start(bf16[16,2432]{1,0:T(8,128)(2,1)S(1)} %get-tuple-element.75), channel_id=1, source_target_pairs={{0,12},{2,14},{4,0},{6,2},{8,4},{10,6},{12,8},{14,10},{1,13},{3,15... | collective-permute-start | bytes 233480 | tf_op jit(solution)/shard_map/ppermute | solution.py:124
  101.6 6.9 %collective-permute-start.27 = (bf16[16,2432]{1,0:T(8,128)(2,1)S(1)}, bf16[16,2432]{1,0:T(8,128)(2,1)S(1)}, u32[]{:S(2)}, u32[]{:S(2)}) collective-permute-start(bf16[16,2432]{1,0:T(8,128)(2,1)S(1)} %get-tuple-element.76), channel_id=1, source_target_pairs={{0,10},{2,12},{4,14},{6,0},{8,2},{10,4},{12,6},{14,8},{1,11},{3,13... | collective-permute-start | bytes 233480 | tf_op jit(solution)/shard_map/ppermute | solution.py:124
  101.6 13.4 %collective-permute-start.28 = (bf16[16,2432]{1,0:T(8,128)(2,1)S(1)}, bf16[16,2432]{1,0:T(8,128)(2,1)S(1)}, u32[]{:S(2)}, u32[]{:S(2)}) collective-permute-start(bf16[16,2432]{1,0:T(8,128)(2,1)S(1)} %get-tuple-element.77), channel_id=1, source_target_pairs={{0,8},{2,10},{4,12},{6,14},{8,0},{10,2},{12,4},{14,6},{1,9},{3,11}... | collective-permute-start | bytes 233480 | tf_op jit(solution)/shard_map/ppermute | solution.py:124
  104.9 12.9 %collective-permute-start.29 = (bf16[16,2432]{1,0:T(8,128)(2,1)S(1)}, bf16[16,2432]{1,0:T(8,128)(2,1)S(1)}, u32[]{:S(2)}, u32[]{:S(2)}) collective-permute-start(bf16[16,2432]{1,0:T(8,128)(2,1)S(1)} %get-tuple-element.78), channel_id=1, source_target_pairs={{0,6},{2,8},{4,10},{6,12},{8,14},{10,0},{12,2},{14,4},{1,7},{3,9},... | collective-permute-start | bytes 233480 | tf_op jit(solution)/shard_map/ppermute | solution.py:124
  104.9 13.0 %collective-permute-start.30 = (bf16[16,2432]{1,0:T(8,128)(2,1)S(1)}, bf16[16,2432]{1,0:T(8,128)(2,1)S(1)}, u32[]{:S(2)}, u32[]{:S(2)}) collective-permute-start(bf16[16,2432]{1,0:T(8,128)(2,1)S(1)} %get-tuple-element.79), channel_id=1, source_target_pairs={{0,4},{2,6},{4,8},{6,10},{8,12},{10,14},{12,0},{14,2},{1,5},{3,7},... | collective-permute-start | bytes 233480 | tf_op jit(solution)/shard_map/ppermute | solution.py:124
  106.8 11.3 %collective-permute-start.31 = (bf16[16,2432]{1,0:T(8,128)(2,1)S(1)}, bf16[16,2432]{1,0:T(8,128)(2,1)S(1)}, u32[]{:S(2)}, u32[]{:S(2)}) collective-permute-start(bf16[16,2432]{1,0:T(8,128)(2,1)S(1)} %get-tuple-element.72), channel_id=1, source_target_pairs={{0,2},{2,4},{4,6},{6,8},{8,10},{10,12},{12,14},{14,0},{1,3},{3,5},... | collective-permute-start | bytes 233480 | tf_op jit(solution)/shard_map/ppermute | solution.py:124
  108.6 14.8 %collective-permute-start.33 = (bf16[16,2304]{1,0:T(8,128)(2,1)S(1)}, bf16[16,2304]{1,0:T(8,128)(2,1)S(1)}, u32[]{:S(2)}, u32[]{:S(2)}) collective-permute-start(bf16[16,2304]{1,0:T(8,128)(2,1)S(1)} %copy-done.5), channel_id=1, source_target_pairs={{0,1},{1,0},{2,3},{3,2},{4,5},{5,4},{6,7},{7,6},{8,9},{9,8},{10,11... | collective-permute-start | bytes 221192 | tf_op jit(solution)/shard_map/ppermute | solution.py:116
  121.5 1.9 %collective-permute-start.32 = (bf16[16,2304]{1,0:T(8,128)(2,1)S(1)}, bf16[16,2304]{1,0:T(8,128)(2,1)S(1)}, u32[]{:S(2)}, u32[]{:S(2)}) collective-permute-start(bf16[16,2304]{1,0:T(8,128)(2,1)S(1)} %add_convert_fusion), channel_id=1, source_target_pairs={{0,1},{1,0},{2,3},{3,2},{4,5},{5,4},{6,7},{7,6},{8,9},{9,8},{10,11... | collective-permute-start | bytes 221192 | tf_op jit(solution)/shard_map/ppermute | solution.py:116
  (18 other events, 109.0 us)

commit v15 on v7

--- a/solution.py
+++ b/solution.py
@@ -200,7 +200,7 @@
     )
     attr_keep = jnp.zeros((rows, acts.shape[2]), jnp.float32)
     grad_keep = jnp.zeros(cotangent.shape, jnp.bfloat16)
-    g_half = jnp.where(here == 0, cotangent[:, :half], cotangent[:, half:])
+    g_half = lax.dynamic_slice_in_dim(cotangent, mine, half, axis=1)
     for layer in reversed(range(depth)):
         is_own = here == layer
         s = jnp.where(is_own, small, other_small)

time: 104 us -> 104 us (level)
  no operation moved by 1% of the time
where the time goes in v15:
time: 104 us; the launch traced here: 102 us
  starting transfers between devices  47.7 us (46%)
  waiting for transfers between devices  34 us (33%)
  local copies, waits for them, and re-layouts  9.67 us (9%)
  other arithmetic  5.25 us (5%)
  matrix products  4.19 us (4%)
  between operations  1.07 us (1%)
    ppermute x28, starting transfers between devices, exchange(): moved.append(lax.ppermute(parts[shift], 'dict', route))  45.8 us
    ppermute x28, waiting for transfers between devices, exchange(): moved.append(lax.ppermute(parts[shift], 'dict', route))  31.7 us
    unnamed x36, local copies, waits for them, and re-layouts  3.27 us
    dynamic_slice x1, local copies, waits for them, and re-layouts, split_device(): lax.dynamic_slice_in_dim(decoder[0], theirs, half, axis=1)  2.39 us
    ppermute x7, waiting for transfers between devices, swap_cores(): return lax.ppermute(block, 'section', [(0, 1), (1, 0)])  2.34 us
    dot_general x4, matrix products, with_dec(): lax.dot_general(g_all, dec, (((1,), (1,)), ((), ())), preferred_element_t...  2.16 us
  transfers between devices with their start and end apart: 35, of which 17 were waited for; matrix products, arithmetic and copies ran while one was open for 14% of the time, Pallas kernels for 0%

profile of v15, /device:TPU:0, one launch (start us, length us, event | category | flops | bytes accessed | tf_op | source)
XLA Modules:
  0.0 101.9 jit_solution(15544570868921893028)
XLA Ops:
  0.6 0.9 reduce
  6.3 5.5 %collective-permute-start.7 = (bf16[16,2432]{1,0:T(8,128)(2,1)S(1)}, bf16[16,2432]{1,0:T(8,128)(2,1)}, u32[]{:S(2)}, u32[]{:S(2)}) collective-permute-start(bf16[16,2432]{1,0:T(8,128)(2,1)S(1)} %get-tuple-element.28), channel_id=1, source_target_pairs={{0,14},{2,0},{4,2},{6,4},{8,6},{10,8},{12,10},{14,12},{1,15},{3,1}... | collective-permute-start | bytes 233480 | tf_op jit(solution)/shard_map/ppermute | solution.py:124
  11.9 1.9 %collective-permute-start.1 = (bf16[16,2432]{1,0:T(8,128)(2,1)}, bf16[16,2432]{1,0:T(8,128)(2,1)}, u32[]{:S(2)}, u32[]{:S(2)}) collective-permute-start(bf16[16,2432]{1,0:T(8,128)(2,1)} %get-tuple-element.31), channel_id=1, source_target_pairs={{0,2},{2,4},{4,6},{6,8},{8,10},{10,12},{12,14},{14,0},{1,3},{3,5},... | collective-permute-start | bytes 233480 | tf_op jit(solution)/shard_map/ppermute | solution.py:124
  13.8 1.6 %collective-permute-start.2 = (bf16[16,2432]{1,0:T(8,128)(2,1)S(1)}, bf16[16,2432]{1,0:T(8,128)(2,1)}, u32[]{:S(2)}, u32[]{:S(2)}) collective-permute-start(bf16[16,2432]{1,0:T(8,128)(2,1)S(1)} %get-tuple-element.32), channel_id=1, source_target_pairs={{0,4},{2,6},{4,8},{6,10},{8,12},{10,14},{12,0},{14,2},{1,5},{3,7},... | collective-permute-start | bytes 233480 | tf_op jit(solution)/shard_map/ppermute | solution.py:124
  15.4 2.4 %dynamic-slice_bitcast_fusion.1 = bf16[256,2304]{1,0:T(8,128)(2,1)} fusion(bf16[1,256,4608]{2,1,0:T(8,128)(2,1)} %param.10, s32[]{:T(128)S(6)} %select_n.193), kind=kLoop, calls=%fused_computation.48 | loop fusion | bytes 2359300 | tf_op jit(solution)/shard_map/dynamic_slice | solution.py:194
  17.8 1.1 %dynamic-slice_bitcast_fusion = bf16[256,2304]{1,0:T(8,128)(2,1)} fusion(bf16[1,256,4608]{2,1,0:T(8,128)(2,1)S(1)} %copy-done, s32[]{:T(128)S(6)} %select_n.193), kind=kLoop, calls=%fused_computation.47 | loop fusion | bytes 2359300 | tf_op jit(solution)/shard_map/dynamic_slice | solution.py:195
  18.8 1.2 %collective-permute-done.1 = bf16[16,2432]{1,0:T(8,128)(2,1)} collective-permute-done((bf16[16,2432]{1,0:T(8,128)(2,1)}, bf16[16,2432]{1,0:T(8,128)(2,1)}, u32[]{:S(2)}, u32[]{:S(2)}) %collective-permute-start.1) | collective-permute-done | bytes 77856 | tf_op jit(solution)/shard_map/ppermute | solution.py:124
  20.1 0.9 bitcast_dynamic-update-slice_fusion.29
  21.0 1.7 %collective-permute-start.4 = (bf16[16,2432]{1,0:T(8,128)(2,1)S(1)}, bf16[16,2432]{1,0:T(8,128)(2,1)S(1)}, u32[]{:S(2)}, u32[]{:S(2)}) collective-permute-start(bf16[16,2432]{1,0:T(8,128)(2,1)S(1)} %get-tuple-element.34), channel_id=1, source_target_pairs={{0,8},{2,10},{4,12},{6,14},{8,0},{10,2},{12,4},{14,6},{1,9},{3,11}... | collective-permute-start | bytes 233480 | tf_op jit(solution)/shard_map/ppermute | solution.py:124
  23.6 5.5 %collective-permute-done.3 = bf16[16,2432]{1,0:T(8,128)(2,1)S(1)} collective-permute-done((bf16[16,2432]{1,0:T(8,128)(2,1)S(1)}, bf16[16,2432]{1,0:T(8,128)(2,1)S(1)}, u32[]{:S(2)}, u32[]{:S(2)}) %collective-permute-start.3) | collective-permute-done | bytes 77856 | tf_op jit(solution)/shard_map/ppermute | solution.py:124
  30.6 1.0 %bitcast_dynamic-update-slice_fusion.25 = bf16[8,16,2432]{2,1,0:T(8,128)(2,1)S(1)} fusion(bf16[8,16,2432]{2,1,0:T(8,128)(2,1)S(1)} %bitcast_dynamic-update-slice_fusion.26, bf16[16,2432]{1,0:T(8,128)(2,1)} %collective-permute-done.5), kind=kLoop, calls=%fused_computation.168 | loop fusion | bytes 155648
  31.6 1.9 %collective-permute-done.6 = bf16[16,2432]{1,0:T(8,128)(2,1)S(1)} collective-permute-done((bf16[16,2432]{1,0:T(8,128)(2,1)S(1)}, bf16[16,2432]{1,0:T(8,128)(2,1)S(1)}, u32[]{:S(2)}, u32[]{:S(2)}) %collective-permute-start.6) | collective-permute-done | bytes 77856 | tf_op jit(solution)/shard_map/ppermute | solution.py:124
  33.6 0.9 bitcast_dynamic-update-slice_fusion.23
  36.2 1.2 %collective-permute-done.9 = f32[128,384]{1,0:T(8,128)S(1)} collective-permute-done((f32[128,384]{1,0:T(8,128)S(1)}, f32[128,384]{1,0:T(8,128)S(1)}, u32[]{:S(2)}, u32[]{:S(2)}) %collective-permute-start.9) | collective-permute-done | bytes 196640 | tf_op jit(solution)/shard_map/ppermute | solution.py:116
  38.2 3.3 %collective-permute-start.11 = (bf16[16,2432]{1,0:T(8,128)(2,1)S(1)}, bf16[16,2432]{1,0:T(8,128)(2,1)S(1)}, u32[]{:S(2)}, u32[]{:S(2)}) collective-permute-start(bf16[16,2432]{1,0:T(8,128)(2,1)S(1)} %get-tuple-element.22), channel_id=1, source_target_pairs={{0,14},{2,0},{4,2},{6,4},{8,6},{10,8},{12,10},{14,12},{1,15},{3,1}... | collective-permute-start | bytes 233480 | tf_op jit(solution)/shard_map/ppermute | solution.py:124
  41.5 1.1 %collective-permute-start.12 = (bf16[16,2432]{1,0:T(8,128)(2,1)S(1)}, bf16[16,2432]{1,0:T(8,128)(2,1)S(1)}, u32[]{:S(2)}, u32[]{:S(2)}) collective-permute-start(bf16[16,2432]{1,0:T(8,128)(2,1)S(1)} %get-tuple-element.23), channel_id=1, source_target_pairs={{0,12},{2,14},{4,0},{6,2},{8,4},{10,6},{12,8},{14,10},{1,13},{3,15... | collective-permute-start | bytes 233480 | tf_op jit(solution)/shard_map/ppermute | solution.py:124
  43.1 6.0 %collective-permute-start.14 = (bf16[16,2432]{1,0:T(8,128)(2,1)S(1)}, bf16[16,2432]{1,0:T(8,128)(2,1)S(1)}, u32[]{:S(2)}, u32[]{:S(2)}) collective-permute-start(bf16[16,2432]{1,0:T(8,128)(2,1)S(1)} %get-tuple-element.25), channel_id=1, source_target_pairs={{0,8},{2,10},{4,12},{6,14},{8,0},{10,2},{12,4},{14,6},{1,9},{3,11}... | collective-permute-start | bytes 233480 | tf_op jit(solution)/shard_map/ppermute | solution.py:124
  50.4 7.0 %collective-permute-done.14 = bf16[16,2432]{1,0:T(8,128)(2,1)S(1)} collective-permute-done((bf16[16,2432]{1,0:T(8,128)(2,1)S(1)}, bf16[16,2432]{1,0:T(8,128)(2,1)S(1)}, u32[]{:S(2)}, u32[]{:S(2)}) %collective-permute-start.14) | collective-permute-done | bytes 77856 | tf_op jit(solution)/shard_map/ppermute | solution.py:124
  58.5 4.7 %collective-permute-start.24 = (bf16[16,2432]{1,0:T(8,128)(2,1)S(1)}, bf16[16,2432]{1,0:T(8,128)(2,1)S(1)}, u32[]{:S(2)}, u32[]{:S(2)}) collective-permute-start(bf16[16,2432]{1,0:T(8,128)(2,1)S(1)} %get-tuple-element.13), channel_id=1, source_target_pairs={{0,14},{2,0},{4,2},{6,4},{8,6},{10,8},{12,10},{14,12},{1,15},{3,1}... | collective-permute-start | bytes 233480 | tf_op jit(solution)/shard_map/ppermute | solution.py:124
  64.0 2.5 %collective-permute-done.18 = bf16[16,2432]{1,0:T(8,128)(2,1)S(1)} collective-permute-done((bf16[16,2432]{1,0:T(8,128)(2,1)S(1)}, bf16[16,2432]{1,0:T(8,128)(2,1)S(1)}, u32[]{:S(2)}, u32[]{:S(2)}) %collective-permute-start.18) | collective-permute-done | bytes 77856 | tf_op jit(solution)/shard_map/ppermute | solution.py:124
  66.5 1.3 %collective-permute-start.22 = (bf16[16,2432]{1,0:T(8,128)(2,1)S(1)}, bf16[16,2432]{1,0:T(8,128)(2,1)S(1)}, u32[]{:S(2)}, u32[]{:S(2)}) collective-permute-start(bf16[16,2432]{1,0:T(8,128)(2,1)S(1)} %get-tuple-element.18), channel_id=1, source_target_pairs={{0,10},{2,12},{4,14},{6,0},{8,2},{10,4},{12,6},{14,8},{1,11},{3,13... | collective-permute-start | bytes 233480 | tf_op jit(solution)/shard_map/ppermute | solution.py:124
  67.8 2.9 %collective-permute-done.19 = bf16[16,2432]{1,0:T(8,128)(2,1)S(1)} collective-permute-done((bf16[16,2432]{1,0:T(8,128)(2,1)S(1)}, bf16[16,2432]{1,0:T(8,128)(2,1)S(1)}, u32[]{:S(2)}, u32[]{:S(2)}) %collective-permute-start.19) | collective-permute-done | bytes 77856 | tf_op jit(solution)/shard_map/ppermute | solution.py:124
  70.8 2.2 %collective-permute-start.23 = (bf16[16,2432]{1,0:T(8,128)(2,1)S(1)}, bf16[16,2432]{1,0:T(8,128)(2,1)S(1)}, u32[]{:S(2)}, u32[]{:S(2)}) collective-permute-start(bf16[16,2432]{1,0:T(8,128)(2,1)S(1)} %get-tuple-element.19), channel_id=1, source_target_pairs={{0,12},{2,14},{4,0},{6,2},{8,4},{10,6},{12,8},{14,10},{1,13},{3,15... | collective-permute-start | bytes 233480 | tf_op jit(solution)/shard_map/ppermute | solution.py:124
  74.1 1.8 %collective-permute-done.23 = bf16[16,2432]{1,0:T(8,128)(2,1)S(1)} collective-permute-done((bf16[16,2432]{1,0:T(8,128)(2,1)S(1)}, bf16[16,2432]{1,0:T(8,128)(2,1)S(1)}, u32[]{:S(2)}, u32[]{:S(2)}) %collective-permute-start.23) | collective-permute-done | bytes 77856 | tf_op jit(solution)/shard_map/ppermute | solution.py:124
  79.4 3.9 %collective-permute-start.26 = (bf16[16,2432]{1,0:T(8,128)(2,1)S(1)}, bf16[16,2432]{1,0:T(8,128)(2,1)S(1)}, u32[]{:S(2)}, u32[]{:S(2)}) collective-permute-start(bf16[16,2432]{1,0:T(8,128)(2,1)S(1)} %get-tuple-element.7), channel_id=1, source_target_pairs={{0,14},{2,0},{4,2},{6,4},{8,6},{10,8},{12,10},{14,12},{1,15},{3,1}... | collective-permute-start | bytes 233480 | tf_op jit(solution)/shard_map/ppermute | solution.py:124
  83.3 1.8 %collective-permute-start.27 = (bf16[16,2432]{1,0:T(8,128)(2,1)S(1)}, bf16[16,2432]{1,0:T(8,128)(2,1)S(1)}, u32[]{:S(2)}, u32[]{:S(2)}) collective-permute-start(bf16[16,2432]{1,0:T(8,128)(2,1)S(1)} %get-tuple-element.8), channel_id=1, source_target_pairs={{0,12},{2,14},{4,0},{6,2},{8,4},{10,6},{12,8},{14,10},{1,13},{3,15... | collective-permute-start | bytes 233480 | tf_op jit(solution)/shard_map/ppermute | solution.py:124
  85.2 1.4 %collective-permute-start.28 = (bf16[16,2432]{1,0:T(8,128)(2,1)S(1)}, bf16[16,2432]{1,0:T(8,128)(2,1)S(1)}, u32[]{:S(2)}, u32[]{:S(2)}) collective-permute-start(bf16[16,2432]{1,0:T(8,128)(2,1)S(1)} %get-tuple-element.9), channel_id=1, source_target_pairs={{0,10},{2,12},{4,14},{6,0},{8,2},{10,4},{12,6},{14,8},{1,11},{3,13... | collective-permute-start | bytes 233480 | tf_op jit(solution)/shard_map/ppermute | solution.py:124
  86.6 4.4 %collective-permute-start.29 = (bf16[16,2432]{1,0:T(8,128)(2,1)S(1)}, bf16[16,2432]{1,0:T(8,128)(2,1)S(1)}, u32[]{:S(2)}, u32[]{:S(2)}) collective-permute-start(bf16[16,2432]{1,0:T(8,128)(2,1)S(1)} %get-tuple-element.10), channel_id=1, source_target_pairs={{0,8},{2,10},{4,12},{6,14},{8,0},{10,2},{12,4},{14,6},{1,9},{3,11}... | collective-permute-start | bytes 233480 | tf_op jit(solution)/shard_map/ppermute | solution.py:124
  91.0 1.0 collective-permute-start.30
  92.0 1.0 collective-permute-done.28
  93.0 1.2 %collective-permute-start.31 = (bf16[16,2432]{1,0:T(8,128)(2,1)S(1)}, bf16[16,2432]{1,0:T(8,128)(2,1)S(1)}, u32[]{:S(2)}, u32[]{:S(2)}) collective-permute-start(bf16[16,2432]{1,0:T(8,128)(2,1)S(1)} %get-tuple-element.12), channel_id=1, source_target_pairs={{0,4},{2,6},{4,8},{6,10},{8,12},{10,14},{12,0},{14,2},{1,5},{3,7},... | collective-permute-start | bytes 233480 | tf_op jit(solution)/shard_map/ppermute | solution.py:124
  94.1 5.4 %collective-permute-done.29 = bf16[16,2432]{1,0:T(8,128)(2,1)S(1)} collective-permute-done((bf16[16,2432]{1,0:T(8,128)(2,1)S(1)}, bf16[16,2432]{1,0:T(8,128)(2,1)S(1)}, u32[]{:S(2)}, u32[]{:S(2)}) %collective-permute-start.29) | collective-permute-done | bytes 77856 | tf_op jit(solution)/shard_map/ppermute | solution.py:124
  (132 shorter events, 20.0 us)
Async XLA Ops:
  2.2 33.8 %collective-permute-start = (f32[4624]{0:T(1024)S(1)}, f32[4624]{0:T(1024)S(1)}, u32[]{:S(2)}, u32[]{:S(2)}) collective-permute-start(f32[4624]{0:T(1024)S(1)} %pad_maximum_fusion.6), channel_id=1, source_target_pairs={{0,1},{1,0},{2,3},{3,2},{4,5},{5,4},{6,7},{7,6},{8,9},{9,8},{10,11... | collective-permute-start | bytes 55496 | tf_op jit(solution)/shard_map/ppermute | solution.py:116
  6.3 27.2 %collective-permute-start.7 = (bf16[16,2432]{1,0:T(8,128)(2,1)S(1)}, bf16[16,2432]{1,0:T(8,128)(2,1)}, u32[]{:S(2)}, u32[]{:S(2)}) collective-permute-start(bf16[16,2432]{1,0:T(8,128)(2,1)S(1)} %get-tuple-element.28), channel_id=1, source_target_pairs={{0,14},{2,0},{4,2},{6,4},{8,6},{10,8},{12,10},{14,12},{1,15},{3,1}... | collective-permute-start | bytes 233480 | tf_op jit(solution)/shard_map/ppermute | solution.py:124
  11.9 18.1 %collective-permute-start.5 = (bf16[16,2432]{1,0:T(8,128)(2,1)S(1)}, bf16[16,2432]{1,0:T(8,128)(2,1)}, u32[]{:S(2)}, u32[]{:S(2)}) collective-permute-start(bf16[16,2432]{1,0:T(8,128)(2,1)S(1)} %get-tuple-element.29), channel_id=1, source_target_pairs={{0,10},{2,12},{4,14},{6,0},{8,2},{10,4},{12,6},{14,8},{1,11},{3,13... | collective-permute-start | bytes 233480 | tf_op jit(solution)/shard_map/ppermute | solution.py:124
  11.9 8.2 %collective-permute-start.1 = (bf16[16,2432]{1,0:T(8,128)(2,1)}, bf16[16,2432]{1,0:T(8,128)(2,1)}, u32[]{:S(2)}, u32[]{:S(2)}) collective-permute-start(bf16[16,2432]{1,0:T(8,128)(2,1)} %get-tuple-element.31), channel_id=1, source_target_pairs={{0,2},{2,4},{4,6},{6,8},{8,10},{10,12},{12,14},{14,0},{1,3},{3,5},... | collective-permute-start | bytes 233480 | tf_op jit(solution)/shard_map/ppermute | solution.py:124
  13.8 7.2 %collective-permute-start.2 = (bf16[16,2432]{1,0:T(8,128)(2,1)S(1)}, bf16[16,2432]{1,0:T(8,128)(2,1)}, u32[]{:S(2)}, u32[]{:S(2)}) collective-permute-start(bf16[16,2432]{1,0:T(8,128)(2,1)S(1)} %get-tuple-element.32), channel_id=1, source_target_pairs={{0,4},{2,6},{4,8},{6,10},{8,12},{10,14},{12,0},{14,2},{1,5},{3,7},... | collective-permute-start | bytes 233480 | tf_op jit(solution)/shard_map/ppermute | solution.py:124
  20.1 9.1 %collective-permute-start.3 = (bf16[16,2432]{1,0:T(8,128)(2,1)S(1)}, bf16[16,2432]{1,0:T(8,128)(2,1)S(1)}, u32[]{:S(2)}, u32[]{:S(2)}) collective-permute-start(bf16[16,2432]{1,0:T(8,128)(2,1)S(1)} %get-tuple-element.33), channel_id=1, source_target_pairs={{0,6},{2,8},{4,10},{6,12},{8,14},{10,0},{12,2},{14,4},{1,7},{3,9},... | collective-permute-start | bytes 233480 | tf_op jit(solution)/shard_map/ppermute | solution.py:124
  21.0 8.9 %collective-permute-start.4 = (bf16[16,2432]{1,0:T(8,128)(2,1)S(1)}, bf16[16,2432]{1,0:T(8,128)(2,1)S(1)}, u32[]{:S(2)}, u32[]{:S(2)}) collective-permute-start(bf16[16,2432]{1,0:T(8,128)(2,1)S(1)} %get-tuple-element.34), channel_id=1, source_target_pairs={{0,8},{2,10},{4,12},{6,14},{8,0},{10,2},{12,4},{14,6},{1,9},{3,11}... | collective-permute-start | bytes 233480 | tf_op jit(solution)/shard_map/ppermute | solution.py:124
  29.1 4.4 %collective-permute-start.6 = (bf16[16,2432]{1,0:T(8,128)(2,1)S(1)}, bf16[16,2432]{1,0:T(8,128)(2,1)S(1)}, u32[]{:S(2)}, u32[]{:S(2)}) collective-permute-start(bf16[16,2432]{1,0:T(8,128)(2,1)S(1)} %get-tuple-element.35), channel_id=1, source_target_pairs={{0,12},{2,14},{4,0},{6,2},{8,4},{10,6},{12,8},{14,10},{1,13},{3,15... | collective-permute-start | bytes 233480 | tf_op jit(solution)/shard_map/ppermute | solution.py:124
  29.9 7.5 %collective-permute-start.10 = (bf16[256,2304]{1,0:T(8,128)(2,1)}, bf16[256,2304]{1,0:T(8,128)(2,1)S(1)}, u32[]{:S(2)}, u32[]{:S(2)}) collective-permute-start(bf16[256,2304]{1,0:T(8,128)(2,1)} %dynamic-slice_bitcast_fusion), channel_id=1, source_target_pairs={{0,1},{1,0},{2,3},{3,2},{4,5},{5,4},{6,7},{7,6},{8,9},{9,8},{10,11... | collective-permute-start | bytes 3538952 | tf_op jit(solution)/shard_map/ppermute | solution.py:116
  30.0 4.7 %collective-permute-start.8 = (bf16[256,2304]{1,0:T(8,128)(2,1)}, bf16[256,2304]{1,0:T(8,128)(2,1)S(1)}, u32[]{:S(2)}, u32[]{:S(2)}) collective-permute-start(bf16[256,2304]{1,0:T(8,128)(2,1)} %dynamic-slice_bitcast_fusion.1), channel_id=1, source_target_pairs={{0,1},{1,0},{2,3},{3,2},{4,5},{5,4},{6,7},{7,6},{8,9},{9,8},{10,11... | collective-permute-start | bytes 3538952 | tf_op jit(solution)/shard_map/ppermute | solution.py:116
  38.2 11.0 %collective-permute-start.11 = (bf16[16,2432]{1,0:T(8,128)(2,1)S(1)}, bf16[16,2432]{1,0:T(8,128)(2,1)S(1)}, u32[]{:S(2)}, u32[]{:S(2)}) collective-permute-start(bf16[16,2432]{1,0:T(8,128)(2,1)S(1)} %get-tuple-element.22), channel_id=1, source_target_pairs={{0,14},{2,0},{4,2},{6,4},{8,6},{10,8},{12,10},{14,12},{1,15},{3,1}... | collective-permute-start | bytes 233480 | tf_op jit(solution)/shard_map/ppermute | solution.py:124
  41.5 16.7 %collective-permute-start.17 = (bf16[16,2432]{1,0:T(8,128)(2,1)S(1)}, bf16[16,2432]{1,0:T(8,128)(2,1)S(1)}, u32[]{:S(2)}, u32[]{:S(2)}) collective-permute-start(bf16[16,2432]{1,0:T(8,128)(2,1)S(1)} %get-tuple-element.21), channel_id=1, source_target_pairs={{0,2},{2,4},{4,6},{6,8},{8,10},{10,12},{12,14},{14,0},{1,3},{3,5},... | collective-permute-start | bytes 233480 | tf_op jit(solution)/shard_map/ppermute | solution.py:124
  41.5 7.7 %collective-permute-start.12 = (bf16[16,2432]{1,0:T(8,128)(2,1)S(1)}, bf16[16,2432]{1,0:T(8,128)(2,1)S(1)}, u32[]{:S(2)}, u32[]{:S(2)}) collective-permute-start(bf16[16,2432]{1,0:T(8,128)(2,1)S(1)} %get-tuple-element.23), channel_id=1, source_target_pairs={{0,12},{2,14},{4,0},{6,2},{8,4},{10,6},{12,8},{14,10},{1,13},{3,15... | collective-permute-start | bytes 233480 | tf_op jit(solution)/shard_map/ppermute | solution.py:124
  42.6 7.8 %collective-permute-start.13 = (bf16[16,2432]{1,0:T(8,128)(2,1)S(1)}, bf16[16,2432]{1,0:T(8,128)(2,1)S(1)}, u32[]{:S(2)}, u32[]{:S(2)}) collective-permute-start(bf16[16,2432]{1,0:T(8,128)(2,1)S(1)} %get-tuple-element.24), channel_id=1, source_target_pairs={{0,10},{2,12},{4,14},{6,0},{8,2},{10,4},{12,6},{14,8},{1,11},{3,13... | collective-permute-start | bytes 233480 | tf_op jit(solution)/shard_map/ppermute | solution.py:124
  43.1 14.3 %collective-permute-start.14 = (bf16[16,2432]{1,0:T(8,128)(2,1)S(1)}, bf16[16,2432]{1,0:T(8,128)(2,1)S(1)}, u32[]{:S(2)}, u32[]{:S(2)}) collective-permute-start(bf16[16,2432]{1,0:T(8,128)(2,1)S(1)} %get-tuple-element.25), channel_id=1, source_target_pairs={{0,8},{2,10},{4,12},{6,14},{8,0},{10,2},{12,4},{14,6},{1,9},{3,11}... | collective-permute-start | bytes 233480 | tf_op jit(solution)/shard_map/ppermute | solution.py:124
  49.1 9.0 %collective-permute-start.15 = (bf16[16,2432]{1,0:T(8,128)(2,1)S(1)}, bf16[16,2432]{1,0:T(8,128)(2,1)S(1)}, u32[]{:S(2)}, u32[]{:S(2)}) collective-permute-start(bf16[16,2432]{1,0:T(8,128)(2,1)S(1)} %get-tuple-element.26), channel_id=1, source_target_pairs={{0,6},{2,8},{4,10},{6,12},{8,14},{10,0},{12,2},{14,4},{1,7},{3,9},... | collective-permute-start | bytes 233480 | tf_op jit(solution)/shard_map/ppermute | solution.py:124
  49.2 9.0 %collective-permute-start.16 = (bf16[16,2432]{1,0:T(8,128)(2,1)S(1)}, bf16[16,2432]{1,0:T(8,128)(2,1)S(1)}, u32[]{:S(2)}, u32[]{:S(2)}) collective-permute-start(bf16[16,2432]{1,0:T(8,128)(2,1)S(1)} %get-tuple-element.27), channel_id=1, source_target_pairs={{0,4},{2,6},{4,8},{6,10},{8,12},{10,14},{12,0},{14,2},{1,5},{3,7},... | collective-permute-start | bytes 233480 | tf_op jit(solution)/shard_map/ppermute | solution.py:124
  58.5 8.1 %collective-permute-start.18 = (bf16[16,2432]{1,0:T(8,128)(2,1)S(1)}, bf16[16,2432]{1,0:T(8,128)(2,1)S(1)}, u32[]{:S(2)}, u32[]{:S(2)}) collective-permute-start(bf16[16,2432]{1,0:T(8,128)(2,1)S(1)} %get-tuple-element.17), channel_id=1, source_target_pairs={{0,2},{2,4},{4,6},{6,8},{8,10},{10,12},{12,14},{14,0},{1,3},{3,5},... | collective-permute-start | bytes 233480 | tf_op jit(solution)/shard_map/ppermute | solution.py:124
  58.5 17.4 %collective-permute-start.24 = (bf16[16,2432]{1,0:T(8,128)(2,1)S(1)}, bf16[16,2432]{1,0:T(8,128)(2,1)S(1)}, u32[]{:S(2)}, u32[]{:S(2)}) collective-permute-start(bf16[16,2432]{1,0:T(8,128)(2,1)S(1)} %get-tuple-element.13), channel_id=1, source_target_pairs={{0,14},{2,0},{4,2},{6,4},{8,6},{10,8},{12,10},{14,12},{1,15},{3,1}... | collective-permute-start | bytes 233480 | tf_op jit(solution)/shard_map/ppermute | solution.py:124
  63.2 10.6 %collective-permute-start.21 = (bf16[16,2432]{1,0:T(8,128)(2,1)S(1)}, bf16[16,2432]{1,0:T(8,128)(2,1)S(1)}, u32[]{:S(2)}, u32[]{:S(2)}) collective-permute-start(bf16[16,2432]{1,0:T(8,128)(2,1)S(1)} %get-tuple-element.14), channel_id=1, source_target_pairs={{0,8},{2,10},{4,12},{6,14},{8,0},{10,2},{12,4},{14,6},{1,9},{3,11}... | collective-permute-start | bytes 233480 | tf_op jit(solution)/shard_map/ppermute | solution.py:124
  63.3 10.5 %collective-permute-start.20 = (bf16[16,2432]{1,0:T(8,128)(2,1)S(1)}, bf16[16,2432]{1,0:T(8,128)(2,1)S(1)}, u32[]{:S(2)}, u32[]{:S(2)}) collective-permute-start(bf16[16,2432]{1,0:T(8,128)(2,1)S(1)} %get-tuple-element.15), channel_id=1, source_target_pairs={{0,6},{2,8},{4,10},{6,12},{8,14},{10,0},{12,2},{14,4},{1,7},{3,9},... | collective-permute-start | bytes 233480 | tf_op jit(solution)/shard_map/ppermute | solution.py:124
  63.8 7.0 %collective-permute-start.19 = (bf16[16,2432]{1,0:T(8,128)(2,1)S(1)}, bf16[16,2432]{1,0:T(8,128)(2,1)S(1)}, u32[]{:S(2)}, u32[]{:S(2)}) collective-permute-start(bf16[16,2432]{1,0:T(8,128)(2,1)S(1)} %get-tuple-element.16), channel_id=1, source_target_pairs={{0,4},{2,6},{4,8},{6,10},{8,12},{10,14},{12,0},{14,2},{1,5},{3,7},... | collective-permute-start | bytes 233480 | tf_op jit(solution)/shard_map/ppermute | solution.py:124
  66.5 7.6 %collective-permute-start.22 = (bf16[16,2432]{1,0:T(8,128)(2,1)S(1)}, bf16[16,2432]{1,0:T(8,128)(2,1)S(1)}, u32[]{:S(2)}, u32[]{:S(2)}) collective-permute-start(bf16[16,2432]{1,0:T(8,128)(2,1)S(1)} %get-tuple-element.18), channel_id=1, source_target_pairs={{0,10},{2,12},{4,14},{6,0},{8,2},{10,4},{12,6},{14,8},{1,11},{3,13... | collective-permute-start | bytes 233480 | tf_op jit(solution)/shard_map/ppermute | solution.py:124
  70.8 5.1 %collective-permute-start.23 = (bf16[16,2432]{1,0:T(8,128)(2,1)S(1)}, bf16[16,2432]{1,0:T(8,128)(2,1)S(1)}, u32[]{:S(2)}, u32[]{:S(2)}) collective-permute-start(bf16[16,2432]{1,0:T(8,128)(2,1)S(1)} %get-tuple-element.19), channel_id=1, source_target_pairs={{0,12},{2,14},{4,0},{6,2},{8,4},{10,6},{12,8},{14,10},{1,13},{3,15... | collective-permute-start | bytes 233480 | tf_op jit(solution)/shard_map/ppermute | solution.py:124
  77.4 23.6 %collective-permute-start.34 = (bf16[16,2304]{1,0:T(8,128)(2,1)S(1)}, bf16[16,2304]{1,0:T(8,128)(2,1)S(1)}, u32[]{:S(2)}, u32[]{:S(2)}) collective-permute-start(bf16[16,2304]{1,0:T(8,128)(2,1)S(1)} %add_convert_fusion.1), channel_id=1, source_target_pairs={{0,1},{1,0},{2,3},{3,2},{4,5},{5,4},{6,7},{7,6},{8,9},{9,8},{10,11... | collective-permute-start | bytes 221192 | tf_op jit(solution)/shard_map/ppermute | solution.py:116
  79.4 7.2 %collective-permute-start.26 = (bf16[16,2432]{1,0:T(8,128)(2,1)S(1)}, bf16[16,2432]{1,0:T(8,128)(2,1)S(1)}, u32[]{:S(2)}, u32[]{:S(2)}) collective-permute-start(bf16[16,2432]{1,0:T(8,128)(2,1)S(1)} %get-tuple-element.7), channel_id=1, source_target_pairs={{0,14},{2,0},{4,2},{6,4},{8,6},{10,8},{12,10},{14,12},{1,15},{3,1}... | collective-permute-start | bytes 233480 | tf_op jit(solution)/shard_map/ppermute | solution.py:124
  83.3 16.3 %collective-permute-start.32 = (bf16[16,2432]{1,0:T(8,128)(2,1)S(1)}, bf16[16,2432]{1,0:T(8,128)(2,1)S(1)}, u32[]{:S(2)}, u32[]{:S(2)}) collective-permute-start(bf16[16,2432]{1,0:T(8,128)(2,1)S(1)} %get-tuple-element.6), channel_id=1, source_target_pairs={{0,2},{2,4},{4,6},{6,8},{8,10},{10,12},{12,14},{14,0},{1,3},{3,5},... | collective-permute-start | bytes 233480 | tf_op jit(solution)/shard_map/ppermute | solution.py:124
  83.3 7.7 %collective-permute-start.27 = (bf16[16,2432]{1,0:T(8,128)(2,1)S(1)}, bf16[16,2432]{1,0:T(8,128)(2,1)S(1)}, u32[]{:S(2)}, u32[]{:S(2)}) collective-permute-start(bf16[16,2432]{1,0:T(8,128)(2,1)S(1)} %get-tuple-element.8), channel_id=1, source_target_pairs={{0,12},{2,14},{4,0},{6,2},{8,4},{10,6},{12,8},{14,10},{1,13},{3,15... | collective-permute-start | bytes 233480 | tf_op jit(solution)/shard_map/ppermute | solution.py:124
  85.2 7.8 %collective-permute-start.28 = (bf16[16,2432]{1,0:T(8,128)(2,1)S(1)}, bf16[16,2432]{1,0:T(8,128)(2,1)S(1)}, u32[]{:S(2)}, u32[]{:S(2)}) collective-permute-start(bf16[16,2432]{1,0:T(8,128)(2,1)S(1)} %get-tuple-element.9), channel_id=1, source_target_pairs={{0,10},{2,12},{4,14},{6,0},{8,2},{10,4},{12,6},{14,8},{1,11},{3,13... | collective-permute-start | bytes 233480 | tf_op jit(solution)/shard_map/ppermute | solution.py:124
  86.6 13.0 %collective-permute-start.29 = (bf16[16,2432]{1,0:T(8,128)(2,1)S(1)}, bf16[16,2432]{1,0:T(8,128)(2,1)S(1)}, u32[]{:S(2)}, u32[]{:S(2)}) collective-permute-start(bf16[16,2432]{1,0:T(8,128)(2,1)S(1)} %get-tuple-element.10), channel_id=1, source_target_pairs={{0,8},{2,10},{4,12},{6,14},{8,0},{10,2},{12,4},{14,6},{1,9},{3,11}... | collective-permute-start | bytes 233480 | tf_op jit(solution)/shard_map/ppermute | solution.py:124
  91.0 8.6 %collective-permute-start.30 = (bf16[16,2432]{1,0:T(8,128)(2,1)S(1)}, bf16[16,2432]{1,0:T(8,128)(2,1)S(1)}, u32[]{:S(2)}, u32[]{:S(2)}) collective-permute-start(bf16[16,2432]{1,0:T(8,128)(2,1)S(1)} %get-tuple-element.11), channel_id=1, source_target_pairs={{0,6},{2,8},{4,10},{6,12},{8,14},{10,0},{12,2},{14,4},{1,7},{3,9},... | collective-permute-start | bytes 233480 | tf_op jit(solution)/shard_map/ppermute | solution.py:124
  93.0 6.6 %collective-permute-start.31 = (bf16[16,2432]{1,0:T(8,128)(2,1)S(1)}, bf16[16,2432]{1,0:T(8,128)(2,1)S(1)}, u32[]{:S(2)}, u32[]{:S(2)}) collective-permute-start(bf16[16,2432]{1,0:T(8,128)(2,1)S(1)} %get-tuple-element.12), channel_id=1, source_target_pairs={{0,4},{2,6},{4,8},{6,10},{8,12},{10,14},{12,0},{14,2},{1,5},{3,7},... | collective-permute-start | bytes 233480 | tf_op jit(solution)/shard_map/ppermute | solution.py:124
  (8 other events, 47.8 us)

commit v16 on v5

--- a/solution.py
+++ b/solution.py
@@ -125,7 +125,7 @@
     return jnp.stack(moved, axis=0)
 
 
-def split_layer(g_half, routes_l, acts_l, own, other, is_own, gain_half, scale_l):
+def split_layer(g_half, routes_l, acts_l, own, other, is_own, small, other_small):
     peers = lax.axis_size("dict")
     me = lax.axis_index("dict")
     rows, listed = routes_l.shape
@@ -146,6 +146,9 @@
         [jnp.broadcast_to(g_half[None], (peers, rows, half)), placed], axis=-1
     )
     got = exchange(sent, 1).reshape(peers * rows, half + block)
+    if other_small is None:
+        small, got = lax.optimization_barrier((small, got))
+        other_small = swap_cores(small)
     g_all = got[:, :half]
     code_all = got[:, half:]
 
@@ -174,10 +177,14 @@
     dz_back = returned[:, :, half:]
     dz_slot = jnp.einsum("rks,srj->rkj", at_rel, dz_back, preferred_element_type=jnp.float32)
     attr = (act_grid.astype(jnp.float32) * dz_slot).reshape(rows, listed * block)
+    width = half * lax.axis_size("section")
+    s = jnp.where(is_own, small, other_small)
+    gain_half = lax.dynamic_slice_in_dim(s[:width], lax.axis_index("section") * half, half, axis=0)
+    scale_l = s[width:width + rows]
     new_half = (g_half.astype(jnp.float32) + scale_l[:, None] * gain_half[None, :] * total).astype(
         jnp.bfloat16
     )
-    return attr, new_half
+    return attr, new_half, other_small
 
 
 def split_device(cotangent, routes, acts, decoder, encoder, gain, inv_rms):
@@ -189,7 +196,7 @@
     mine = here * half
     theirs = (1 - here) * half
     small = jnp.concatenate([gain[0], inv_rms[0]], axis=0)
-    other_small = swap_cores(small)
+    other_small = None
     sent_w = jnp.concatenate(
         [
             lax.dynamic_slice_in_dim(decoder[0], theirs, half, axis=1),
@@ -208,10 +215,9 @@
     g_half = lax.dynamic_slice_in_dim(cotangent, mine, half, axis=1)
     for layer in reversed(range(depth)):
         is_own = here == layer
-        s = jnp.where(is_own, small, other_small)
-        gain_half = lax.dynamic_slice_in_dim(s[:width], mine, half, axis=0)
-        scale_l = s[width:width + rows]
-        attr, g_half = split_layer(g_half, routes[0], acts[0], own, other, is_own, gain_half, scale_l)
+        attr, g_half, other_small = split_layer(
+            g_half, routes[0], acts[0], own, other, is_own, small, other_small
+        )
         partner = swap_cores(g_half)
         full = jnp.where(
             here == 0,

time: 94.1 us -> 93.9 us (level)
  starting transfers between devices: 54.6 us -> 58.4 us
  waiting for transfers between devices: 20 us -> 17 us
  other arithmetic: 5.44 us -> 4.02 us
    ppermute x28, starting transfers between devices: 53.2 us -> 56.9 us  [exchange(): moved.append(lax.ppermute(parts[shift], 'dict', route))]
    ppermute x28, waiting for transfers between devices: 16.4 us -> 14.2 us  [exchange(): moved.append(lax.ppermute(parts[shift], 'dict', route))]
    concatenate x1, other arithmetic: 1.58 us -> 0.15 us  [split_device(): jnp.concatenate([lax.dynamic_slice_in_dim(decoder[0], theirs, half, axis=...]
  transfers between devices with their start and end apart: 34 -> 34, of which waited for: 12 -> 12; matrix products, arithmetic and copies ran while one was open for 12% -> 10% of each run, Pallas kernels for 0% -> 0%
where the time goes in v16:
time: 93.9 us; the launch traced here: 93.5 us
  starting transfers between devices  58.4 us (62%)
  waiting for transfers between devices  17 us (18%)
  local copies, waits for them, and re-layouts  8.77 us (9%)
  matrix products  4.18 us (4%)
  other arithmetic  4.02 us (4%)
  between operations  1.1 us (1%)
    ppermute x28, starting transfers between devices, exchange(): moved.append(lax.ppermute(parts[shift], 'dict', route))  56.9 us
    ppermute x28, waiting for transfers between devices, exchange(): moved.append(lax.ppermute(parts[shift], 'dict', route))  14.2 us
    unnamed x38, local copies, waits for them, and re-layouts  5.26 us
    ppermute x6, waiting for transfers between devices, swap_cores(): return lax.ppermute(block, 'section', [(0, 1), (1, 0)])  2.82 us
    dot_general x4, matrix products, with_dec(): lax.dot_general(g_all, dec, (((1,), (1,)), ((), ())), preferred_element_t...  2.16 us
  transfers between devices with their start and end apart: 34, of which 12 were waited for; matrix products, arithmetic and copies ran while one was open for 10% of the time, Pallas kernels for 0%

profile of v16, /device:TPU:0, one launch (start us, length us, event | category | flops | bytes accessed | tf_op | source)
XLA Modules:
  0.0 93.5 jit_solution(15475601688179924728)
XLA Ops:
  4.5 2.9 %collective-permute-start = (bf16[16,2432]{1,0:T(8,128)(2,1)}, bf16[16,2432]{1,0:T(8,128)(2,1)}, u32[]{:S(2)}, u32[]{:S(2)}) collective-permute-start(bf16[16,2432]{1,0:T(8,128)(2,1)} %get-tuple-element.35), channel_id=1, source_target_pairs={{0,2},{2,4},{4,6},{6,8},{8,10},{10,12},{12,14},{14,0},{1,3},{3,5},... | collective-permute-start | bytes 233480 | tf_op jit(solution)/shard_map/ppermute | solution.py:124
  7.4 1.6 %collective-permute-start.1 = (bf16[16,2432]{1,0:T(8,128)(2,1)S(1)}, bf16[16,2432]{1,0:T(8,128)(2,1)}, u32[]{:S(2)}, u32[]{:S(2)}) collective-permute-start(bf16[16,2432]{1,0:T(8,128)(2,1)S(1)} %get-tuple-element.36), channel_id=1, source_target_pairs={{0,4},{2,6},{4,8},{6,10},{8,12},{10,14},{12,0},{14,2},{1,5},{3,7},... | collective-permute-start | bytes 233480 | tf_op jit(solution)/shard_map/ppermute | solution.py:124
  9.0 2.6 %collective-permute-start.2 = (bf16[16,2432]{1,0:T(8,128)(2,1)S(1)}, bf16[16,2432]{1,0:T(8,128)(2,1)}, u32[]{:S(2)}, u32[]{:S(2)}) collective-permute-start(bf16[16,2432]{1,0:T(8,128)(2,1)S(1)} %get-tuple-element.37), channel_id=1, source_target_pairs={{0,6},{2,8},{4,10},{6,12},{8,14},{10,0},{12,2},{14,4},{1,7},{3,9},... | collective-permute-start | bytes 233480 | tf_op jit(solution)/shard_map/ppermute | solution.py:124
  11.5 1.2 %collective-permute-start.3 = (bf16[16,2432]{1,0:T(8,128)(2,1)S(1)}, bf16[16,2432]{1,0:T(8,128)(2,1)}, u32[]{:S(2)}, u32[]{:S(2)}) collective-permute-start(bf16[16,2432]{1,0:T(8,128)(2,1)S(1)} %get-tuple-element.38), channel_id=1, source_target_pairs={{0,8},{2,10},{4,12},{6,14},{8,0},{10,2},{12,4},{14,6},{1,9},{3,11}... | collective-permute-start | bytes 233480 | tf_op jit(solution)/shard_map/ppermute | solution.py:124
  12.8 2.6 %collective-permute-start.4 = (bf16[16,2432]{1,0:T(8,128)(2,1)S(1)}, bf16[16,2432]{1,0:T(8,128)(2,1)}, u32[]{:S(2)}, u32[]{:S(2)}) collective-permute-start(bf16[16,2432]{1,0:T(8,128)(2,1)S(1)} %get-tuple-element.33), channel_id=1, source_target_pairs={{0,10},{2,12},{4,14},{6,0},{8,2},{10,4},{12,6},{14,8},{1,11},{3,13... | collective-permute-start | bytes 233480 | tf_op jit(solution)/shard_map/ppermute | solution.py:124
  15.5 1.5 %dynamic-slice_bitcast_fusion = (bf16[256,2304]{1,0:T(8,128)(2,1)S(1)}, bf16[256,2304]{1,0:T(8,128)(2,1)S(1)}) fusion(bf16[1,256,4608]{2,1,0:T(8,128)(2,1)} %param.11, s32[]{:T(128)S(6)} %select_n.193, bf16[1,256,4608]{2,1,0:T(8,128)(2,1)S(1)} %copy-done), kind=kLoop, calls=%fused_computation.48 | loop fusion | bytes 4718596 | tf_op jit(solution)/shard_map/dynamic_slice | solution.py:203
  17.6 1.4 %collective-permute-start.5 = (bf16[16,2432]{1,0:T(8,128)(2,1)S(1)}, bf16[16,2432]{1,0:T(8,128)(2,1)S(1)}, u32[]{:S(2)}, u32[]{:S(2)}) collective-permute-start(bf16[16,2432]{1,0:T(8,128)(2,1)S(1)} %get-tuple-element.39), channel_id=1, source_target_pairs={{0,12},{2,14},{4,0},{6,2},{8,4},{10,6},{12,8},{14,10},{1,13},{3,15... | collective-permute-start | bytes 233480 | tf_op jit(solution)/shard_map/ppermute | solution.py:124
  19.9 1.5 %collective-permute-start.6 = (bf16[16,2432]{1,0:T(8,128)(2,1)S(1)}, bf16[16,2432]{1,0:T(8,128)(2,1)S(1)}, u32[]{:S(2)}, u32[]{:S(2)}) collective-permute-start(bf16[16,2432]{1,0:T(8,128)(2,1)S(1)} %get-tuple-element.32), channel_id=1, source_target_pairs={{0,14},{2,0},{4,2},{6,4},{8,6},{10,8},{12,10},{14,12},{1,15},{3,1}... | collective-permute-start | bytes 233480 | tf_op jit(solution)/shard_map/ppermute | solution.py:124
  22.4 0.9 bitcast_dynamic-update-slice_fusion.27
  23.3 0.9 bitcast_dynamic-update-slice_fusion.26
  24.2 0.9 bitcast_dynamic-update-slice_fusion.25
  27.8 1.2 %collective-permute-done.9 = f32[128,384]{1,0:T(8,128)S(1)} collective-permute-done((f32[128,384]{1,0:T(8,128)S(1)}, f32[128,384]{1,0:T(8,128)S(1)}, u32[]{:S(2)}, u32[]{:S(2)}) %collective-permute-start.9) | collective-permute-done | bytes 196640 | tf_op jit(solution)/shard_map/ppermute | solution.py:116
  29.8 2.4 %collective-permute-start.10 = (bf16[16,2432]{1,0:T(8,128)(2,1)S(1)}, bf16[16,2432]{1,0:T(8,128)(2,1)S(1)}, u32[]{:S(2)}, u32[]{:S(2)}) collective-permute-start(bf16[16,2432]{1,0:T(8,128)(2,1)S(1)} %get-tuple-element.26), channel_id=1, source_target_pairs={{0,14},{2,0},{4,2},{6,4},{8,6},{10,8},{12,10},{14,12},{1,15},{3,1}... | collective-permute-start | bytes 233480 | tf_op jit(solution)/shard_map/ppermute | solution.py:124
  32.2 1.1 %collective-permute-start.11 = (bf16[16,2432]{1,0:T(8,128)(2,1)S(1)}, bf16[16,2432]{1,0:T(8,128)(2,1)S(1)}, u32[]{:S(2)}, u32[]{:S(2)}) collective-permute-start(bf16[16,2432]{1,0:T(8,128)(2,1)S(1)} %get-tuple-element.27), channel_id=1, source_target_pairs={{0,12},{2,14},{4,0},{6,2},{8,4},{10,6},{12,8},{14,10},{1,13},{3,15... | collective-permute-start | bytes 233480 | tf_op jit(solution)/shard_map/ppermute | solution.py:124
  33.4 4.3 %collective-permute-start.13 = (bf16[16,2432]{1,0:T(8,128)(2,1)S(1)}, bf16[16,2432]{1,0:T(8,128)(2,1)S(1)}, u32[]{:S(2)}, u32[]{:S(2)}) collective-permute-start(bf16[16,2432]{1,0:T(8,128)(2,1)S(1)} %get-tuple-element.29), channel_id=1, source_target_pairs={{0,8},{2,10},{4,12},{6,14},{8,0},{10,2},{12,4},{14,6},{1,9},{3,11}... | collective-permute-start | bytes 233480 | tf_op jit(solution)/shard_map/ppermute | solution.py:124
  38.3 1.6 %collective-permute-start.16 = (bf16[16,2432]{1,0:T(8,128)(2,1)S(1)}, bf16[16,2432]{1,0:T(8,128)(2,1)S(1)}, u32[]{:S(2)}, u32[]{:S(2)}) collective-permute-start(bf16[16,2432]{1,0:T(8,128)(2,1)S(1)} %get-tuple-element.25), channel_id=1, source_target_pairs={{0,2},{2,4},{4,6},{6,8},{8,10},{10,12},{12,14},{14,0},{1,3},{3,5},... | collective-permute-start | bytes 233480 | tf_op jit(solution)/shard_map/ppermute | solution.py:124
  39.9 7.6 %collective-permute-done.13 = bf16[16,2432]{1,0:T(8,128)(2,1)S(1)} collective-permute-done((bf16[16,2432]{1,0:T(8,128)(2,1)S(1)}, bf16[16,2432]{1,0:T(8,128)(2,1)S(1)}, u32[]{:S(2)}, u32[]{:S(2)}) %collective-permute-start.13) | collective-permute-done | bytes 77856 | tf_op jit(solution)/shard_map/ppermute | solution.py:124
  47.5 1.2 %collective-permute-done.14 = bf16[16,2432]{1,0:T(8,128)(2,1)S(1)} collective-permute-done((bf16[16,2432]{1,0:T(8,128)(2,1)S(1)}, bf16[16,2432]{1,0:T(8,128)(2,1)S(1)}, u32[]{:S(2)}, u32[]{:S(2)}) %collective-permute-start.14) | collective-permute-done | bytes 77856 | tf_op jit(solution)/shard_map/ppermute | solution.py:124
  49.1 1.4 %collective-permute-start.18 = (bf16[16,2432]{1,0:T(8,128)(2,1)S(1)}, bf16[16,2432]{1,0:T(8,128)(2,1)S(1)}, u32[]{:S(2)}, u32[]{:S(2)}) collective-permute-start(bf16[16,2432]{1,0:T(8,128)(2,1)S(1)} %get-tuple-element.20), channel_id=1, source_target_pairs={{0,4},{2,6},{4,8},{6,10},{8,12},{10,14},{12,0},{14,2},{1,5},{3,7},... | collective-permute-start | bytes 233480 | tf_op jit(solution)/shard_map/ppermute | solution.py:124
  50.5 2.8 %collective-permute-start.19 = (bf16[16,2432]{1,0:T(8,128)(2,1)S(1)}, bf16[16,2432]{1,0:T(8,128)(2,1)S(1)}, u32[]{:S(2)}, u32[]{:S(2)}) collective-permute-start(bf16[16,2432]{1,0:T(8,128)(2,1)S(1)} %get-tuple-element.19), channel_id=1, source_target_pairs={{0,6},{2,8},{4,10},{6,12},{8,14},{10,0},{12,2},{14,4},{1,7},{3,9},... | collective-permute-start | bytes 233480 | tf_op jit(solution)/shard_map/ppermute | solution.py:124
  53.3 1.1 %collective-permute-start.20 = (bf16[16,2432]{1,0:T(8,128)(2,1)S(1)}, bf16[16,2432]{1,0:T(8,128)(2,1)S(1)}, u32[]{:S(2)}, u32[]{:S(2)}) collective-permute-start(bf16[16,2432]{1,0:T(8,128)(2,1)S(1)} %get-tuple-element.18), channel_id=1, source_target_pairs={{0,8},{2,10},{4,12},{6,14},{8,0},{10,2},{12,4},{14,6},{1,9},{3,11}... | collective-permute-start | bytes 233480 | tf_op jit(solution)/shard_map/ppermute | solution.py:124
  54.4 1.9 %collective-permute-start.21 = (bf16[16,2432]{1,0:T(8,128)(2,1)S(1)}, bf16[16,2432]{1,0:T(8,128)(2,1)S(1)}, u32[]{:S(2)}, u32[]{:S(2)}) collective-permute-start(bf16[16,2432]{1,0:T(8,128)(2,1)S(1)} %get-tuple-element.22), channel_id=1, source_target_pairs={{0,10},{2,12},{4,14},{6,0},{8,2},{10,4},{12,6},{14,8},{1,11},{3,13... | collective-permute-start | bytes 233480 | tf_op jit(solution)/shard_map/ppermute | solution.py:124
  56.5 2.2 %collective-permute-start.22 = (bf16[16,2432]{1,0:T(8,128)(2,1)S(1)}, bf16[16,2432]{1,0:T(8,128)(2,1)S(1)}, u32[]{:S(2)}, u32[]{:S(2)}) collective-permute-start(bf16[16,2432]{1,0:T(8,128)(2,1)S(1)} %get-tuple-element.23), channel_id=1, source_target_pairs={{0,12},{2,14},{4,0},{6,2},{8,4},{10,6},{12,8},{14,10},{1,13},{3,15... | collective-permute-start | bytes 233480 | tf_op jit(solution)/shard_map/ppermute | solution.py:124
  58.7 2.9 %collective-permute-start.23 = (bf16[16,2432]{1,0:T(8,128)(2,1)S(1)}, bf16[16,2432]{1,0:T(8,128)(2,1)S(1)}, u32[]{:S(2)}, u32[]{:S(2)}) collective-permute-start(bf16[16,2432]{1,0:T(8,128)(2,1)S(1)} %get-tuple-element.17), channel_id=1, source_target_pairs={{0,14},{2,0},{4,2},{6,4},{8,6},{10,8},{12,10},{14,12},{1,15},{3,1}... | collective-permute-start | bytes 233480 | tf_op jit(solution)/shard_map/ppermute | solution.py:124
  62.3 1.7 %collective-permute-done.20 = bf16[16,2432]{1,0:T(8,128)(2,1)S(1)} collective-permute-done((bf16[16,2432]{1,0:T(8,128)(2,1)S(1)}, bf16[16,2432]{1,0:T(8,128)(2,1)S(1)}, u32[]{:S(2)}, u32[]{:S(2)}) %collective-permute-start.20) | collective-permute-done | bytes 77856 | tf_op jit(solution)/shard_map/ppermute | solution.py:124
  67.6 6.1 %collective-permute-start.25 = (bf16[16,2432]{1,0:T(8,128)(2,1)S(1)}, bf16[16,2432]{1,0:T(8,128)(2,1)S(1)}, u32[]{:S(2)}, u32[]{:S(2)}) collective-permute-start(bf16[16,2432]{1,0:T(8,128)(2,1)S(1)} %get-tuple-element.11), channel_id=1, source_target_pairs={{0,14},{2,0},{4,2},{6,4},{8,6},{10,8},{12,10},{14,12},{1,15},{3,1}... | collective-permute-start | bytes 233480 | tf_op jit(solution)/shard_map/ppermute | solution.py:124
  73.7 2.9 %collective-permute-start.26 = (bf16[16,2432]{1,0:T(8,128)(2,1)S(1)}, bf16[16,2432]{1,0:T(8,128)(2,1)S(1)}, u32[]{:S(2)}, u32[]{:S(2)}) collective-permute-start(bf16[16,2432]{1,0:T(8,128)(2,1)S(1)} %get-tuple-element.12), channel_id=1, source_target_pairs={{0,12},{2,14},{4,0},{6,2},{8,4},{10,6},{12,8},{14,10},{1,13},{3,15... | collective-permute-start | bytes 233480 | tf_op jit(solution)/shard_map/ppermute | solution.py:124
  76.6 1.1 %collective-permute-start.28 = (bf16[16,2432]{1,0:T(8,128)(2,1)S(1)}, bf16[16,2432]{1,0:T(8,128)(2,1)S(1)}, u32[]{:S(2)}, u32[]{:S(2)}) collective-permute-start(bf16[16,2432]{1,0:T(8,128)(2,1)S(1)} %get-tuple-element.14), channel_id=1, source_target_pairs={{0,8},{2,10},{4,12},{6,14},{8,0},{10,2},{12,4},{14,6},{1,9},{3,11}... | collective-permute-start | bytes 233480 | tf_op jit(solution)/shard_map/ppermute | solution.py:124
  77.7 1.8 %collective-permute-start.29 = (bf16[16,2432]{1,0:T(8,128)(2,1)S(1)}, bf16[16,2432]{1,0:T(8,128)(2,1)S(1)}, u32[]{:S(2)}, u32[]{:S(2)}) collective-permute-start(bf16[16,2432]{1,0:T(8,128)(2,1)S(1)} %get-tuple-element.15), channel_id=1, source_target_pairs={{0,6},{2,8},{4,10},{6,12},{8,14},{10,0},{12,2},{14,4},{1,7},{3,9},... | collective-permute-start | bytes 233480 | tf_op jit(solution)/shard_map/ppermute | solution.py:124
  79.5 2.3 %collective-permute-start.30 = (bf16[16,2432]{1,0:T(8,128)(2,1)S(1)}, bf16[16,2432]{1,0:T(8,128)(2,1)S(1)}, u32[]{:S(2)}, u32[]{:S(2)}) collective-permute-start(bf16[16,2432]{1,0:T(8,128)(2,1)S(1)} %get-tuple-element.16), channel_id=1, source_target_pairs={{0,4},{2,6},{4,8},{6,10},{8,12},{10,14},{12,0},{14,2},{1,5},{3,7},... | collective-permute-start | bytes 233480 | tf_op jit(solution)/shard_map/ppermute | solution.py:124
  82.7 6.5 %collective-permute-start.31 = (bf16[16,2432]{1,0:T(8,128)(2,1)S(1)}, bf16[16,2432]{1,0:T(8,128)(2,1)S(1)}, u32[]{:S(2)}, u32[]{:S(2)}) collective-permute-start(bf16[16,2432]{1,0:T(8,128)(2,1)S(1)} %get-tuple-element.10), channel_id=1, source_target_pairs={{0,2},{2,4},{4,6},{6,8},{8,10},{10,12},{12,14},{14,0},{1,3},{3,5},... | collective-permute-start | bytes 233480 | tf_op jit(solution)/shard_map/ppermute | solution.py:124
  89.8 1.3 %collective-permute-done.31 = bf16[16,2432]{1,0:T(8,128)(2,1)S(1)} collective-permute-done((bf16[16,2432]{1,0:T(8,128)(2,1)S(1)}, bf16[16,2432]{1,0:T(8,128)(2,1)S(1)}, u32[]{:S(2)}, u32[]{:S(2)}) %collective-permute-start.31) | collective-permute-done | bytes 77856 | tf_op jit(solution)/shard_map/ppermute | solution.py:124
  (132 shorter events, 18.9 us)
Async XLA Ops:
  4.5 13.1 %collective-permute-start = (bf16[16,2432]{1,0:T(8,128)(2,1)}, bf16[16,2432]{1,0:T(8,128)(2,1)}, u32[]{:S(2)}, u32[]{:S(2)}) collective-permute-start(bf16[16,2432]{1,0:T(8,128)(2,1)} %get-tuple-element.35), channel_id=1, source_target_pairs={{0,2},{2,4},{4,6},{6,8},{8,10},{10,12},{12,14},{14,0},{1,3},{3,5},... | collective-permute-start | bytes 233480 | tf_op jit(solution)/shard_map/ppermute | solution.py:124
  7.4 12.5 %collective-permute-start.1 = (bf16[16,2432]{1,0:T(8,128)(2,1)S(1)}, bf16[16,2432]{1,0:T(8,128)(2,1)}, u32[]{:S(2)}, u32[]{:S(2)}) collective-permute-start(bf16[16,2432]{1,0:T(8,128)(2,1)S(1)} %get-tuple-element.36), channel_id=1, source_target_pairs={{0,4},{2,6},{4,8},{6,10},{8,12},{10,14},{12,0},{14,2},{1,5},{3,7},... | collective-permute-start | bytes 233480 | tf_op jit(solution)/shard_map/ppermute | solution.py:124
  9.0 13.3 %collective-permute-start.2 = (bf16[16,2432]{1,0:T(8,128)(2,1)S(1)}, bf16[16,2432]{1,0:T(8,128)(2,1)}, u32[]{:S(2)}, u32[]{:S(2)}) collective-permute-start(bf16[16,2432]{1,0:T(8,128)(2,1)S(1)} %get-tuple-element.37), channel_id=1, source_target_pairs={{0,6},{2,8},{4,10},{6,12},{8,14},{10,0},{12,2},{14,4},{1,7},{3,9},... | collective-permute-start | bytes 233480 | tf_op jit(solution)/shard_map/ppermute | solution.py:124
  11.5 11.7 %collective-permute-start.3 = (bf16[16,2432]{1,0:T(8,128)(2,1)S(1)}, bf16[16,2432]{1,0:T(8,128)(2,1)}, u32[]{:S(2)}, u32[]{:S(2)}) collective-permute-start(bf16[16,2432]{1,0:T(8,128)(2,1)S(1)} %get-tuple-element.38), channel_id=1, source_target_pairs={{0,8},{2,10},{4,12},{6,14},{8,0},{10,2},{12,4},{14,6},{1,9},{3,11}... | collective-permute-start | bytes 233480 | tf_op jit(solution)/shard_map/ppermute | solution.py:124
  12.8 11.4 %collective-permute-start.4 = (bf16[16,2432]{1,0:T(8,128)(2,1)S(1)}, bf16[16,2432]{1,0:T(8,128)(2,1)}, u32[]{:S(2)}, u32[]{:S(2)}) collective-permute-start(bf16[16,2432]{1,0:T(8,128)(2,1)S(1)} %get-tuple-element.33), channel_id=1, source_target_pairs={{0,10},{2,12},{4,14},{6,0},{8,2},{10,4},{12,6},{14,8},{1,11},{3,13... | collective-permute-start | bytes 233480 | tf_op jit(solution)/shard_map/ppermute | solution.py:124
  17.6 7.5 %collective-permute-start.5 = (bf16[16,2432]{1,0:T(8,128)(2,1)S(1)}, bf16[16,2432]{1,0:T(8,128)(2,1)S(1)}, u32[]{:S(2)}, u32[]{:S(2)}) collective-permute-start(bf16[16,2432]{1,0:T(8,128)(2,1)S(1)} %get-tuple-element.39), channel_id=1, source_target_pairs={{0,12},{2,14},{4,0},{6,2},{8,4},{10,6},{12,8},{14,10},{1,13},{3,15... | collective-permute-start | bytes 233480 | tf_op jit(solution)/shard_map/ppermute | solution.py:124
  19.9 5.2 %collective-permute-start.6 = (bf16[16,2432]{1,0:T(8,128)(2,1)S(1)}, bf16[16,2432]{1,0:T(8,128)(2,1)S(1)}, u32[]{:S(2)}, u32[]{:S(2)}) collective-permute-start(bf16[16,2432]{1,0:T(8,128)(2,1)S(1)} %get-tuple-element.32), channel_id=1, source_target_pairs={{0,14},{2,0},{4,2},{6,4},{8,6},{10,8},{12,10},{14,12},{1,15},{3,1}... | collective-permute-start | bytes 233480 | tf_op jit(solution)/shard_map/ppermute | solution.py:124
  22.3 4.6 %collective-permute-start.8 = (bf16[512,2304]{1,0:T(8,128)(2,1)S(1)}, bf16[512,2304]{1,0:T(8,128)(2,1)S(1)}, u32[]{:S(2)}, u32[]{:S(2)}) collective-permute-start(bf16[512,2304]{1,0:T(8,128)(2,1)S(1)} %pad_maximum_fusion), channel_id=1, source_target_pairs={{0,1},{1,0},{2,3},{3,2},{4,5},{5,4},{6,7},{7,6},{8,9},{9,8},{10,11... | collective-permute-start | bytes 7077896 | tf_op jit(solution)/shard_map/ppermute | solution.py:116
  25.1 2.5 %collective-permute-start.7 = (f32[4624]{0:T(1024)S(1)}, f32[4624]{0:T(1024)S(1)}, u32[]{:S(2)}, u32[]{:S(2)}) collective-permute-start(f32[4624]{0:T(1024)S(1)} %pad_maximum_fusion.7), channel_id=1, source_target_pairs={{0,1},{1,0},{2,3},{3,2},{4,5},{5,4},{6,7},{7,6},{8,9},{9,8},{10,11... | collective-permute-start | bytes 55496 | tf_op jit(solution)/shard_map/ppermute | solution.py:116
  27.4 1.5 %collective-permute-start.9 = (f32[128,384]{1,0:T(8,128)S(1)}, f32[128,384]{1,0:T(8,128)S(1)}, u32[]{:S(2)}, u32[]{:S(2)}) collective-permute-start(f32[128,384]{1,0:T(8,128)S(1)} %pad_maximum_fusion.1), channel_id=1, source_target_pairs={{0,1},{1,0},{2,3},{3,2},{4,5},{5,4},{6,7},{7,6},{8,9},{9,8},{10,11... | collective-permute-start | bytes 589832 | tf_op jit(solution)/shard_map/ppermute | solution.py:116
  29.8 7.9 %collective-permute-start.10 = (bf16[16,2432]{1,0:T(8,128)(2,1)S(1)}, bf16[16,2432]{1,0:T(8,128)(2,1)S(1)}, u32[]{:S(2)}, u32[]{:S(2)}) collective-permute-start(bf16[16,2432]{1,0:T(8,128)(2,1)S(1)} %get-tuple-element.26), channel_id=1, source_target_pairs={{0,14},{2,0},{4,2},{6,4},{8,6},{10,8},{12,10},{14,12},{1,15},{3,1}... | collective-permute-start | bytes 233480 | tf_op jit(solution)/shard_map/ppermute | solution.py:124
  32.2 6.0 %collective-permute-start.11 = (bf16[16,2432]{1,0:T(8,128)(2,1)S(1)}, bf16[16,2432]{1,0:T(8,128)(2,1)S(1)}, u32[]{:S(2)}, u32[]{:S(2)}) collective-permute-start(bf16[16,2432]{1,0:T(8,128)(2,1)S(1)} %get-tuple-element.27), channel_id=1, source_target_pairs={{0,12},{2,14},{4,0},{6,2},{8,4},{10,6},{12,8},{14,10},{1,13},{3,15... | collective-permute-start | bytes 233480 | tf_op jit(solution)/shard_map/ppermute | solution.py:124
  33.4 6.5 %collective-permute-start.12 = (bf16[16,2432]{1,0:T(8,128)(2,1)S(1)}, bf16[16,2432]{1,0:T(8,128)(2,1)S(1)}, u32[]{:S(2)}, u32[]{:S(2)}) collective-permute-start(bf16[16,2432]{1,0:T(8,128)(2,1)S(1)} %get-tuple-element.28), channel_id=1, source_target_pairs={{0,10},{2,12},{4,14},{6,0},{8,2},{10,4},{12,6},{14,8},{1,11},{3,13... | collective-permute-start | bytes 233480 | tf_op jit(solution)/shard_map/ppermute | solution.py:124
  33.4 14.1 %collective-permute-start.13 = (bf16[16,2432]{1,0:T(8,128)(2,1)S(1)}, bf16[16,2432]{1,0:T(8,128)(2,1)S(1)}, u32[]{:S(2)}, u32[]{:S(2)}) collective-permute-start(bf16[16,2432]{1,0:T(8,128)(2,1)S(1)} %get-tuple-element.29), channel_id=1, source_target_pairs={{0,8},{2,10},{4,12},{6,14},{8,0},{10,2},{12,4},{14,6},{1,9},{3,11}... | collective-permute-start | bytes 233480 | tf_op jit(solution)/shard_map/ppermute | solution.py:124
  37.7 11.0 %collective-permute-start.14 = (bf16[16,2432]{1,0:T(8,128)(2,1)S(1)}, bf16[16,2432]{1,0:T(8,128)(2,1)S(1)}, u32[]{:S(2)}, u32[]{:S(2)}) collective-permute-start(bf16[16,2432]{1,0:T(8,128)(2,1)S(1)} %get-tuple-element.30), channel_id=1, source_target_pairs={{0,6},{2,8},{4,10},{6,12},{8,14},{10,0},{12,2},{14,4},{1,7},{3,9},... | collective-permute-start | bytes 233480 | tf_op jit(solution)/shard_map/ppermute | solution.py:124
  37.7 11.0 %collective-permute-start.15 = (bf16[16,2432]{1,0:T(8,128)(2,1)S(1)}, bf16[16,2432]{1,0:T(8,128)(2,1)S(1)}, u32[]{:S(2)}, u32[]{:S(2)}) collective-permute-start(bf16[16,2432]{1,0:T(8,128)(2,1)S(1)} %get-tuple-element.31), channel_id=1, source_target_pairs={{0,4},{2,6},{4,8},{6,10},{8,12},{10,14},{12,0},{14,2},{1,5},{3,7},... | collective-permute-start | bytes 233480 | tf_op jit(solution)/shard_map/ppermute | solution.py:124
  38.3 10.4 %collective-permute-start.16 = (bf16[16,2432]{1,0:T(8,128)(2,1)S(1)}, bf16[16,2432]{1,0:T(8,128)(2,1)S(1)}, u32[]{:S(2)}, u32[]{:S(2)}) collective-permute-start(bf16[16,2432]{1,0:T(8,128)(2,1)S(1)} %get-tuple-element.25), channel_id=1, source_target_pairs={{0,2},{2,4},{4,6},{6,8},{8,10},{10,12},{12,14},{14,0},{1,3},{3,5},... | collective-permute-start | bytes 233480 | tf_op jit(solution)/shard_map/ppermute | solution.py:124
  49.0 7.4 %collective-permute-start.17 = (bf16[16,2432]{1,0:T(8,128)(2,1)S(1)}, bf16[16,2432]{1,0:T(8,128)(2,1)S(1)}, u32[]{:S(2)}, u32[]{:S(2)}) collective-permute-start(bf16[16,2432]{1,0:T(8,128)(2,1)S(1)} %get-tuple-element.21), channel_id=1, source_target_pairs={{0,2},{2,4},{4,6},{6,8},{8,10},{10,12},{12,14},{14,0},{1,3},{3,5},... | collective-permute-start | bytes 233480 | tf_op jit(solution)/shard_map/ppermute | solution.py:124
  49.1 9.6 %collective-permute-start.18 = (bf16[16,2432]{1,0:T(8,128)(2,1)S(1)}, bf16[16,2432]{1,0:T(8,128)(2,1)S(1)}, u32[]{:S(2)}, u32[]{:S(2)}) collective-permute-start(bf16[16,2432]{1,0:T(8,128)(2,1)S(1)} %get-tuple-element.20), channel_id=1, source_target_pairs={{0,4},{2,6},{4,8},{6,10},{8,12},{10,14},{12,0},{14,2},{1,5},{3,7},... | collective-permute-start | bytes 233480 | tf_op jit(solution)/shard_map/ppermute | solution.py:124
  50.5 11.8 %collective-permute-start.19 = (bf16[16,2432]{1,0:T(8,128)(2,1)S(1)}, bf16[16,2432]{1,0:T(8,128)(2,1)S(1)}, u32[]{:S(2)}, u32[]{:S(2)}) collective-permute-start(bf16[16,2432]{1,0:T(8,128)(2,1)S(1)} %get-tuple-element.19), channel_id=1, source_target_pairs={{0,6},{2,8},{4,10},{6,12},{8,14},{10,0},{12,2},{14,4},{1,7},{3,9},... | collective-permute-start | bytes 233480 | tf_op jit(solution)/shard_map/ppermute | solution.py:124
  53.3 10.7 %collective-permute-start.20 = (bf16[16,2432]{1,0:T(8,128)(2,1)S(1)}, bf16[16,2432]{1,0:T(8,128)(2,1)S(1)}, u32[]{:S(2)}, u32[]{:S(2)}) collective-permute-start(bf16[16,2432]{1,0:T(8,128)(2,1)S(1)} %get-tuple-element.18), channel_id=1, source_target_pairs={{0,8},{2,10},{4,12},{6,14},{8,0},{10,2},{12,4},{14,6},{1,9},{3,11}... | collective-permute-start | bytes 233480 | tf_op jit(solution)/shard_map/ppermute | solution.py:124
  54.4 9.6 %collective-permute-start.21 = (bf16[16,2432]{1,0:T(8,128)(2,1)S(1)}, bf16[16,2432]{1,0:T(8,128)(2,1)S(1)}, u32[]{:S(2)}, u32[]{:S(2)}) collective-permute-start(bf16[16,2432]{1,0:T(8,128)(2,1)S(1)} %get-tuple-element.22), channel_id=1, source_target_pairs={{0,10},{2,12},{4,14},{6,0},{8,2},{10,4},{12,6},{14,8},{1,11},{3,13... | collective-permute-start | bytes 233480 | tf_op jit(solution)/shard_map/ppermute | solution.py:124
  56.5 7.6 %collective-permute-start.22 = (bf16[16,2432]{1,0:T(8,128)(2,1)S(1)}, bf16[16,2432]{1,0:T(8,128)(2,1)S(1)}, u32[]{:S(2)}, u32[]{:S(2)}) collective-permute-start(bf16[16,2432]{1,0:T(8,128)(2,1)S(1)} %get-tuple-element.23), channel_id=1, source_target_pairs={{0,12},{2,14},{4,0},{6,2},{8,4},{10,6},{12,8},{14,10},{1,13},{3,15... | collective-permute-start | bytes 233480 | tf_op jit(solution)/shard_map/ppermute | solution.py:124
  58.7 5.4 %collective-permute-start.23 = (bf16[16,2432]{1,0:T(8,128)(2,1)S(1)}, bf16[16,2432]{1,0:T(8,128)(2,1)S(1)}, u32[]{:S(2)}, u32[]{:S(2)}) collective-permute-start(bf16[16,2432]{1,0:T(8,128)(2,1)S(1)} %get-tuple-element.17), channel_id=1, source_target_pairs={{0,14},{2,0},{4,2},{6,4},{8,6},{10,8},{12,10},{14,12},{1,15},{3,1}... | collective-permute-start | bytes 233480 | tf_op jit(solution)/shard_map/ppermute | solution.py:124
  65.5 27.1 %collective-permute-start.33 = (bf16[16,2304]{1,0:T(8,128)(2,1)S(1)}, bf16[16,2304]{1,0:T(8,128)(2,1)S(1)}, u32[]{:S(2)}, u32[]{:S(2)}) collective-permute-start(bf16[16,2304]{1,0:T(8,128)(2,1)S(1)} %add_convert_fusion.1), channel_id=1, source_target_pairs={{0,1},{1,0},{2,3},{3,2},{4,5},{5,4},{6,7},{7,6},{8,9},{9,8},{10,11... | collective-permute-start | bytes 221192 | tf_op jit(solution)/shard_map/ppermute | solution.py:116
  67.6 10.2 %collective-permute-start.25 = (bf16[16,2432]{1,0:T(8,128)(2,1)S(1)}, bf16[16,2432]{1,0:T(8,128)(2,1)S(1)}, u32[]{:S(2)}, u32[]{:S(2)}) collective-permute-start(bf16[16,2432]{1,0:T(8,128)(2,1)S(1)} %get-tuple-element.11), channel_id=1, source_target_pairs={{0,14},{2,0},{4,2},{6,4},{8,6},{10,8},{12,10},{14,12},{1,15},{3,1}... | collective-permute-start | bytes 233480 | tf_op jit(solution)/shard_map/ppermute | solution.py:124
  73.7 5.9 %collective-permute-start.26 = (bf16[16,2432]{1,0:T(8,128)(2,1)S(1)}, bf16[16,2432]{1,0:T(8,128)(2,1)S(1)}, u32[]{:S(2)}, u32[]{:S(2)}) collective-permute-start(bf16[16,2432]{1,0:T(8,128)(2,1)S(1)} %get-tuple-element.12), channel_id=1, source_target_pairs={{0,12},{2,14},{4,0},{6,2},{8,4},{10,6},{12,8},{14,10},{1,13},{3,15... | collective-permute-start | bytes 233480 | tf_op jit(solution)/shard_map/ppermute | solution.py:124
  76.6 6.1 %collective-permute-start.27 = (bf16[16,2432]{1,0:T(8,128)(2,1)S(1)}, bf16[16,2432]{1,0:T(8,128)(2,1)S(1)}, u32[]{:S(2)}, u32[]{:S(2)}) collective-permute-start(bf16[16,2432]{1,0:T(8,128)(2,1)S(1)} %get-tuple-element.13), channel_id=1, source_target_pairs={{0,10},{2,12},{4,14},{6,0},{8,2},{10,4},{12,6},{14,8},{1,11},{3,13... | collective-permute-start | bytes 233480 | tf_op jit(solution)/shard_map/ppermute | solution.py:124
  76.6 12.6 %collective-permute-start.28 = (bf16[16,2432]{1,0:T(8,128)(2,1)S(1)}, bf16[16,2432]{1,0:T(8,128)(2,1)S(1)}, u32[]{:S(2)}, u32[]{:S(2)}) collective-permute-start(bf16[16,2432]{1,0:T(8,128)(2,1)S(1)} %get-tuple-element.14), channel_id=1, source_target_pairs={{0,8},{2,10},{4,12},{6,14},{8,0},{10,2},{12,4},{14,6},{1,9},{3,11}... | collective-permute-start | bytes 233480 | tf_op jit(solution)/shard_map/ppermute | solution.py:124
  77.7 12.1 %collective-permute-start.29 = (bf16[16,2432]{1,0:T(8,128)(2,1)S(1)}, bf16[16,2432]{1,0:T(8,128)(2,1)S(1)}, u32[]{:S(2)}, u32[]{:S(2)}) collective-permute-start(bf16[16,2432]{1,0:T(8,128)(2,1)S(1)} %get-tuple-element.15), channel_id=1, source_target_pairs={{0,6},{2,8},{4,10},{6,12},{8,14},{10,0},{12,2},{14,4},{1,7},{3,9},... | collective-permute-start | bytes 233480 | tf_op jit(solution)/shard_map/ppermute | solution.py:124
  79.5 10.3 %collective-permute-start.30 = (bf16[16,2432]{1,0:T(8,128)(2,1)S(1)}, bf16[16,2432]{1,0:T(8,128)(2,1)S(1)}, u32[]{:S(2)}, u32[]{:S(2)}) collective-permute-start(bf16[16,2432]{1,0:T(8,128)(2,1)S(1)} %get-tuple-element.16), channel_id=1, source_target_pairs={{0,4},{2,6},{4,8},{6,10},{8,12},{10,14},{12,0},{14,2},{1,5},{3,7},... | collective-permute-start | bytes 233480 | tf_op jit(solution)/shard_map/ppermute | solution.py:124
  82.7 8.5 %collective-permute-start.31 = (bf16[16,2432]{1,0:T(8,128)(2,1)S(1)}, bf16[16,2432]{1,0:T(8,128)(2,1)S(1)}, u32[]{:S(2)}, u32[]{:S(2)}) collective-permute-start(bf16[16,2432]{1,0:T(8,128)(2,1)S(1)} %get-tuple-element.10), channel_id=1, source_target_pairs={{0,2},{2,4},{4,6},{6,8},{8,10},{10,12},{12,14},{14,0},{1,3},{3,5},... | collective-permute-start | bytes 233480 | tf_op jit(solution)/shard_map/ppermute | solution.py:124
  (8 other events, 56.5 us)

commit v17 on v13

--- a/solution.py
+++ b/solution.py
@@ -120,7 +120,7 @@
     peers = parts.shape[0]
     moved = [parts[0]]
     for shift in range(1, peers):
-        route = [(d, d ^ shift) for d in range(peers)]
+        route = [(d, d ^ (peers - shift)) for d in range(peers)]
         moved.append(lax.ppermute(parts[shift], "dict", route))
     return jnp.stack(moved, axis=0)
 
@@ -134,7 +134,7 @@
     half = g_half.shape[1]
     owner = routes_l // held
     within = routes_l - owner * held
-    rel = lax.bitwise_xor(owner, me)
+    rel = (peers - lax.bitwise_xor(owner, me)) % peers
     shifts = jnp.arange(peers, dtype=jnp.int32)
     at_rel = (rel[:, :, None] == shifts[None, None, :]).astype(jnp.bfloat16)
     act_grid = acts_l.reshape(rows, listed, block)

time: 95.2 us -> 93.7 us (0.984); the launches traced: 93.7 us -> 93.3 us
  waiting for transfers between devices: 24 us -> 17.2 us
  starting transfers between devices: 50.6 us -> 57 us
    ppermute x28, waiting for transfers between devices: 21.7 us -> 13.7 us  [exchange(): moved.append(lax.ppermute(parts[shift], 'dict', route))]
    ppermute x28, starting transfers between devices: 49.3 us -> 55.6 us  [exchange(): moved.append(lax.ppermute(parts[shift], 'dict', route))]
    ppermute x6, waiting for transfers between devices: 2.28 us -> 3.57 us  [swap_cores(): return lax.ppermute(block, 'section', [(0, 1), (1, 0)])]
  transfers between devices with their start and end apart: 34 -> 34, of which waited for: 9 -> 15; matrix products, arithmetic and copies ran while one was open for 12% -> 12% of each run, Pallas kernels for 0% -> 0%
where the time goes in v17:
time: 93.7 us; the launch traced here: 93.3 us
  starting transfers between devices  57 us (61%)
  waiting for transfers between devices  17.2 us (18%)
  local copies, waits for them, and re-layouts  8.28 us (9%)
  other arithmetic  5.45 us (6%)
  matrix products  4.18 us (4%)
  between operations  1.09 us (1%)
    ppermute x28, starting transfers between devices, exchange(): moved.append(lax.ppermute(parts[shift], 'dict', route))  55.6 us
    ppermute x28, waiting for transfers between devices, exchange(): moved.append(lax.ppermute(parts[shift], 'dict', route))  13.7 us
    unnamed x38, local copies, waits for them, and re-layouts  4.78 us
    ppermute x6, waiting for transfers between devices, swap_cores(): return lax.ppermute(block, 'section', [(0, 1), (1, 0)])  3.57 us
    dot_general x4, matrix products, with_dec(): lax.dot_general(g_all, dec, (((1,), (1,)), ((), ())), preferred_element_t...  2.16 us
  transfers between devices with their start and end apart: 34, of which 15 were waited for; matrix products, arithmetic and copies ran while one was open for 12% of the time, Pallas kernels for 0%

profile of v17, /device:TPU:0, one launch (start us, length us, event | category | flops | bytes accessed | tf_op | source)
XLA Modules:
  0.0 93.3 jit_solution(8668603309002273944)
XLA Ops:
  4.5 6.0 %collective-permute-start.1 = (bf16[16,2432]{1,0:T(8,128)(2,1)}, bf16[16,2432]{1,0:T(8,128)(2,1)}, u32[]{:S(2)}, u32[]{:S(2)}) collective-permute-start(bf16[16,2432]{1,0:T(8,128)(2,1)} %get-tuple-element.31), channel_id=1, source_target_pairs={{0,14},{2,12},{4,10},{6,8},{8,6},{10,4},{12,2},{14,0},{1,15},{3,13... | collective-permute-start | bytes 233480 | tf_op jit(solution)/shard_map/ppermute | solution.py:124
  11.4 1.9 %collective-permute-start.4 = (bf16[16,2432]{1,0:T(8,128)(2,1)S(1)}, bf16[16,2432]{1,0:T(8,128)(2,1)}, u32[]{:S(2)}, u32[]{:S(2)}) collective-permute-start(bf16[16,2432]{1,0:T(8,128)(2,1)S(1)} %get-tuple-element.34), channel_id=1, source_target_pairs={{0,8},{2,10},{4,12},{6,14},{8,0},{10,2},{12,4},{14,6},{1,9},{3,11}... | collective-permute-start | bytes 233480 | tf_op jit(solution)/shard_map/ppermute | solution.py:124
  13.4 2.4 %collective-permute-start.5 = (bf16[16,2432]{1,0:T(8,128)(2,1)S(1)}, bf16[16,2432]{1,0:T(8,128)(2,1)}, u32[]{:S(2)}, u32[]{:S(2)}) collective-permute-start(bf16[16,2432]{1,0:T(8,128)(2,1)S(1)} %get-tuple-element.29), channel_id=1, source_target_pairs={{0,6},{2,4},{4,2},{6,0},{8,14},{10,12},{12,10},{14,8},{1,7},{3,5},... | collective-permute-start | bytes 233480 | tf_op jit(solution)/shard_map/ppermute | solution.py:124
  15.7 1.5 %dynamic-slice_bitcast_fusion = (bf16[256,2304]{1,0:T(8,128)(2,1)S(1)}, bf16[256,2304]{1,0:T(8,128)(2,1)S(1)}) fusion(bf16[1,256,4608]{2,1,0:T(8,128)(2,1)} %param.11, s32[]{:T(128)S(6)} %select_n.193, bf16[1,256,4608]{2,1,0:T(8,128)(2,1)S(1)} %copy-done), kind=kLoop, calls=%fused_computation.48 | loop fusion | bytes 4718596 | tf_op jit(solution)/shard_map/dynamic_slice | solution.py:196
  17.2 1.6 %pad_maximum_fusion = bf16[512,2304]{1,0:T(8,128)(2,1)} fusion(bf16[256,2304]{1,0:T(8,128)(2,1)S(1)} %get-tuple-element.40, bf16[256,2304]{1,0:T(8,128)(2,1)S(1)} %get-tuple-element.41), kind=kLoop, calls=%fused_computation.4 | loop fusion | flops 4718592 | bytes 4718592 | tf_op jit(solution)/shard_map/concatenate | solution.py:193
  20.6 1.4 %collective-permute-start.7 = (bf16[16,2432]{1,0:T(8,128)(2,1)S(1)}, bf16[16,2432]{1,0:T(8,128)(2,1)S(1)}, u32[]{:S(2)}, u32[]{:S(2)}) collective-permute-start(bf16[16,2432]{1,0:T(8,128)(2,1)S(1)} %get-tuple-element.28), channel_id=1, source_target_pairs={{0,2},{2,0},{4,6},{6,4},{8,10},{10,8},{12,14},{14,12},{1,3},{3,1},... | collective-permute-start | bytes 233480 | tf_op jit(solution)/shard_map/ppermute | solution.py:124
  23.2 0.9 bitcast_dynamic-update-slice_fusion.27
  26.5 1.4 %collective-permute-done.8 = bf16[512,2304]{1,0:T(8,128)(2,1)S(1)} collective-permute-done((bf16[512,2304]{1,0:T(8,128)(2,1)}, bf16[512,2304]{1,0:T(8,128)(2,1)S(1)}, u32[]{:S(2)}, u32[]{:S(2)}) %collective-permute-start.8) | collective-permute-done | bytes 2359328 | tf_op jit(solution)/shard_map/ppermute | solution.py:116
  29.4 1.2 %collective-permute-done.9 = f32[128,384]{1,0:T(8,128)S(1)} collective-permute-done((f32[128,384]{1,0:T(8,128)S(1)}, f32[128,384]{1,0:T(8,128)S(1)}, u32[]{:S(2)}, u32[]{:S(2)}) %collective-permute-start.9) | collective-permute-done | bytes 196640 | tf_op jit(solution)/shard_map/ppermute | solution.py:116
  31.4 3.6 %collective-permute-start.10 = (bf16[16,2432]{1,0:T(8,128)(2,1)S(1)}, bf16[16,2432]{1,0:T(8,128)(2,1)S(1)}, u32[]{:S(2)}, u32[]{:S(2)}) collective-permute-start(bf16[16,2432]{1,0:T(8,128)(2,1)S(1)} %get-tuple-element.22), channel_id=1, source_target_pairs={{0,14},{2,12},{4,10},{6,8},{8,6},{10,4},{12,2},{14,0},{1,15},{3,13... | collective-permute-start | bytes 233480 | tf_op jit(solution)/shard_map/ppermute | solution.py:124
  35.0 1.2 %collective-permute-start.11 = (bf16[16,2432]{1,0:T(8,128)(2,1)S(1)}, bf16[16,2432]{1,0:T(8,128)(2,1)S(1)}, u32[]{:S(2)}, u32[]{:S(2)}) collective-permute-start(bf16[16,2432]{1,0:T(8,128)(2,1)S(1)} %get-tuple-element.23), channel_id=1, source_target_pairs={{0,12},{2,14},{4,8},{6,10},{8,4},{10,6},{12,0},{14,2},{1,13},{3,15... | collective-permute-start | bytes 233480 | tf_op jit(solution)/shard_map/ppermute | solution.py:124
  36.3 2.8 %collective-permute-start.13 = (bf16[16,2432]{1,0:T(8,128)(2,1)S(1)}, bf16[16,2432]{1,0:T(8,128)(2,1)S(1)}, u32[]{:S(2)}, u32[]{:S(2)}) collective-permute-start(bf16[16,2432]{1,0:T(8,128)(2,1)S(1)} %get-tuple-element.25), channel_id=1, source_target_pairs={{0,8},{2,10},{4,12},{6,14},{8,0},{10,2},{12,4},{14,6},{1,9},{3,11}... | collective-permute-start | bytes 233480 | tf_op jit(solution)/shard_map/ppermute | solution.py:124
  39.1 1.2 %collective-permute-start.14 = (bf16[16,2432]{1,0:T(8,128)(2,1)S(1)}, bf16[16,2432]{1,0:T(8,128)(2,1)S(1)}, u32[]{:S(2)}, u32[]{:S(2)}) collective-permute-start(bf16[16,2432]{1,0:T(8,128)(2,1)S(1)} %get-tuple-element.26), channel_id=1, source_target_pairs={{0,6},{2,4},{4,2},{6,0},{8,14},{10,12},{12,10},{14,8},{1,7},{3,5},... | collective-permute-start | bytes 233480 | tf_op jit(solution)/shard_map/ppermute | solution.py:124
  40.3 3.0 %collective-permute-start.15 = (bf16[16,2432]{1,0:T(8,128)(2,1)S(1)}, bf16[16,2432]{1,0:T(8,128)(2,1)S(1)}, u32[]{:S(2)}, u32[]{:S(2)}) collective-permute-start(bf16[16,2432]{1,0:T(8,128)(2,1)S(1)} %get-tuple-element.27), channel_id=1, source_target_pairs={{0,4},{2,6},{4,0},{6,2},{8,12},{10,14},{12,8},{14,10},{1,5},{3,7},... | collective-permute-start | bytes 233480 | tf_op jit(solution)/shard_map/ppermute | solution.py:124
  43.4 3.5 %collective-permute-done.12 = bf16[16,2432]{1,0:T(8,128)(2,1)S(1)} collective-permute-done((bf16[16,2432]{1,0:T(8,128)(2,1)S(1)}, bf16[16,2432]{1,0:T(8,128)(2,1)S(1)}, u32[]{:S(2)}, u32[]{:S(2)}) %collective-permute-start.12) | collective-permute-done | bytes 77856 | tf_op jit(solution)/shard_map/ppermute | solution.py:124
  46.9 1.4 %collective-permute-done.13 = bf16[16,2432]{1,0:T(8,128)(2,1)S(1)} collective-permute-done((bf16[16,2432]{1,0:T(8,128)(2,1)S(1)}, bf16[16,2432]{1,0:T(8,128)(2,1)S(1)}, u32[]{:S(2)}, u32[]{:S(2)}) %collective-permute-start.13) | collective-permute-done | bytes 77856 | tf_op jit(solution)/shard_map/ppermute | solution.py:124
  48.9 4.0 %collective-permute-start.17 = (bf16[16,2432]{1,0:T(8,128)(2,1)S(1)}, bf16[16,2432]{1,0:T(8,128)(2,1)S(1)}, u32[]{:S(2)}, u32[]{:S(2)}) collective-permute-start(bf16[16,2432]{1,0:T(8,128)(2,1)S(1)} %get-tuple-element.17), channel_id=1, source_target_pairs={{0,14},{2,12},{4,10},{6,8},{8,6},{10,4},{12,2},{14,0},{1,15},{3,13... | collective-permute-start | bytes 233480 | tf_op jit(solution)/shard_map/ppermute | solution.py:124
  53.2 2.1 %collective-permute-start.19 = (bf16[16,2432]{1,0:T(8,128)(2,1)S(1)}, bf16[16,2432]{1,0:T(8,128)(2,1)S(1)}, u32[]{:S(2)}, u32[]{:S(2)}) collective-permute-start(bf16[16,2432]{1,0:T(8,128)(2,1)S(1)} %get-tuple-element.15), channel_id=1, source_target_pairs={{0,10},{2,8},{4,14},{6,12},{8,2},{10,0},{12,6},{14,4},{1,11},{3,9}... | collective-permute-start | bytes 233480 | tf_op jit(solution)/shard_map/ppermute | solution.py:124
  55.2 1.4 %collective-permute-start.20 = (bf16[16,2432]{1,0:T(8,128)(2,1)S(1)}, bf16[16,2432]{1,0:T(8,128)(2,1)S(1)}, u32[]{:S(2)}, u32[]{:S(2)}) collective-permute-start(bf16[16,2432]{1,0:T(8,128)(2,1)S(1)} %get-tuple-element.14), channel_id=1, source_target_pairs={{0,8},{2,10},{4,12},{6,14},{8,0},{10,2},{12,4},{14,6},{1,9},{3,11}... | collective-permute-start | bytes 233480 | tf_op jit(solution)/shard_map/ppermute | solution.py:124
  56.6 1.6 %collective-permute-start.21 = (bf16[16,2432]{1,0:T(8,128)(2,1)S(1)}, bf16[16,2432]{1,0:T(8,128)(2,1)S(1)}, u32[]{:S(2)}, u32[]{:S(2)}) collective-permute-start(bf16[16,2432]{1,0:T(8,128)(2,1)S(1)} %get-tuple-element.18), channel_id=1, source_target_pairs={{0,6},{2,4},{4,2},{6,0},{8,14},{10,12},{12,10},{14,8},{1,7},{3,5},... | collective-permute-start | bytes 233480 | tf_op jit(solution)/shard_map/ppermute | solution.py:124
  58.2 2.8 %collective-permute-start.22 = (bf16[16,2432]{1,0:T(8,128)(2,1)S(1)}, bf16[16,2432]{1,0:T(8,128)(2,1)S(1)}, u32[]{:S(2)}, u32[]{:S(2)}) collective-permute-start(bf16[16,2432]{1,0:T(8,128)(2,1)S(1)} %get-tuple-element.19), channel_id=1, source_target_pairs={{0,4},{2,6},{4,0},{6,2},{8,12},{10,14},{12,8},{14,10},{1,5},{3,7},... | collective-permute-start | bytes 233480 | tf_op jit(solution)/shard_map/ppermute | solution.py:124
  61.0 1.3 %collective-permute-start.23 = (bf16[16,2432]{1,0:T(8,128)(2,1)S(1)}, bf16[16,2432]{1,0:T(8,128)(2,1)S(1)}, u32[]{:S(2)}, u32[]{:S(2)}) collective-permute-start(bf16[16,2432]{1,0:T(8,128)(2,1)S(1)} %get-tuple-element.13), channel_id=1, source_target_pairs={{0,2},{2,0},{4,6},{6,4},{8,10},{10,8},{12,14},{14,12},{1,3},{3,1},... | collective-permute-start | bytes 233480 | tf_op jit(solution)/shard_map/ppermute | solution.py:124
  62.3 2.3 %collective-permute-done.19 = bf16[16,2432]{1,0:T(8,128)(2,1)S(1)} collective-permute-done((bf16[16,2432]{1,0:T(8,128)(2,1)S(1)}, bf16[16,2432]{1,0:T(8,128)(2,1)S(1)}, u32[]{:S(2)}, u32[]{:S(2)}) %collective-permute-start.19) | collective-permute-done | bytes 77856 | tf_op jit(solution)/shard_map/ppermute | solution.py:124
  69.0 4.8 %collective-permute-start.25 = (bf16[16,2432]{1,0:T(8,128)(2,1)S(1)}, bf16[16,2432]{1,0:T(8,128)(2,1)S(1)}, u32[]{:S(2)}, u32[]{:S(2)}) collective-permute-start(bf16[16,2432]{1,0:T(8,128)(2,1)S(1)} %get-tuple-element.7), channel_id=1, source_target_pairs={{0,14},{2,12},{4,10},{6,8},{8,6},{10,4},{12,2},{14,0},{1,15},{3,13... | collective-permute-start | bytes 233480 | tf_op jit(solution)/shard_map/ppermute | solution.py:124
  73.8 2.2 %collective-permute-start.27 = (bf16[16,2432]{1,0:T(8,128)(2,1)S(1)}, bf16[16,2432]{1,0:T(8,128)(2,1)S(1)}, u32[]{:S(2)}, u32[]{:S(2)}) collective-permute-start(bf16[16,2432]{1,0:T(8,128)(2,1)S(1)} %get-tuple-element.9), channel_id=1, source_target_pairs={{0,10},{2,8},{4,14},{6,12},{8,2},{10,0},{12,6},{14,4},{1,11},{3,9}... | collective-permute-start | bytes 233480 | tf_op jit(solution)/shard_map/ppermute | solution.py:124
  76.0 1.2 %collective-permute-start.28 = (bf16[16,2432]{1,0:T(8,128)(2,1)S(1)}, bf16[16,2432]{1,0:T(8,128)(2,1)S(1)}, u32[]{:S(2)}, u32[]{:S(2)}) collective-permute-start(bf16[16,2432]{1,0:T(8,128)(2,1)S(1)} %get-tuple-element.10), channel_id=1, source_target_pairs={{0,8},{2,10},{4,12},{6,14},{8,0},{10,2},{12,4},{14,6},{1,9},{3,11}... | collective-permute-start | bytes 233480 | tf_op jit(solution)/shard_map/ppermute | solution.py:124
  77.1 6.6 %collective-permute-start.29 = (bf16[16,2432]{1,0:T(8,128)(2,1)S(1)}, bf16[16,2432]{1,0:T(8,128)(2,1)S(1)}, u32[]{:S(2)}, u32[]{:S(2)}) collective-permute-start(bf16[16,2432]{1,0:T(8,128)(2,1)S(1)} %get-tuple-element.11), channel_id=1, source_target_pairs={{0,6},{2,4},{4,2},{6,0},{8,14},{10,12},{12,10},{14,8},{1,7},{3,5},... | collective-permute-start | bytes 233480 | tf_op jit(solution)/shard_map/ppermute | solution.py:124
  83.8 1.1 %collective-permute-start.30 = (bf16[16,2432]{1,0:T(8,128)(2,1)S(1)}, bf16[16,2432]{1,0:T(8,128)(2,1)S(1)}, u32[]{:S(2)}, u32[]{:S(2)}) collective-permute-start(bf16[16,2432]{1,0:T(8,128)(2,1)S(1)} %get-tuple-element.12), channel_id=1, source_target_pairs={{0,4},{2,6},{4,0},{6,2},{8,12},{10,14},{12,8},{14,10},{1,5},{3,7},... | collective-permute-start | bytes 233480 | tf_op jit(solution)/shard_map/ppermute | solution.py:124
  84.9 1.7 %collective-permute-done.27 = bf16[16,2432]{1,0:T(8,128)(2,1)S(1)} collective-permute-done((bf16[16,2432]{1,0:T(8,128)(2,1)S(1)}, bf16[16,2432]{1,0:T(8,128)(2,1)S(1)}, u32[]{:S(2)}, u32[]{:S(2)}) %collective-permute-start.27) | collective-permute-done | bytes 77856 | tf_op jit(solution)/shard_map/ppermute | solution.py:124
  86.6 1.0 %collective-permute-start.31 = (bf16[16,2432]{1,0:T(8,128)(2,1)S(1)}, bf16[16,2432]{1,0:T(8,128)(2,1)S(1)}, u32[]{:S(2)}, u32[]{:S(2)}) collective-permute-start(bf16[16,2432]{1,0:T(8,128)(2,1)S(1)} %get-tuple-element.6), channel_id=1, source_target_pairs={{0,2},{2,0},{4,6},{6,4},{8,10},{10,8},{12,14},{14,12},{1,3},{3,1},... | collective-permute-start | bytes 233480 | tf_op jit(solution)/shard_map/ppermute | solution.py:124
  87.6 1.8 %collective-permute-done.29 = bf16[16,2432]{1,0:T(8,128)(2,1)S(1)} collective-permute-done((bf16[16,2432]{1,0:T(8,128)(2,1)S(1)}, bf16[16,2432]{1,0:T(8,128)(2,1)S(1)}, u32[]{:S(2)}, u32[]{:S(2)}) %collective-permute-start.29) | collective-permute-done | bytes 77856 | tf_op jit(solution)/shard_map/ppermute | solution.py:124
  89.9 1.1 %collective-permute-done.31 = bf16[16,2432]{1,0:T(8,128)(2,1)S(1)} collective-permute-done((bf16[16,2432]{1,0:T(8,128)(2,1)S(1)}, bf16[16,2432]{1,0:T(8,128)(2,1)S(1)}, u32[]{:S(2)}, u32[]{:S(2)}) %collective-permute-start.31) | collective-permute-done | bytes 77856 | tf_op jit(solution)/shard_map/ppermute | solution.py:124
  (132 shorter events, 20.6 us)
Async XLA Ops:
  4.5 14.4 %collective-permute-start.1 = (bf16[16,2432]{1,0:T(8,128)(2,1)}, bf16[16,2432]{1,0:T(8,128)(2,1)}, u32[]{:S(2)}, u32[]{:S(2)}) collective-permute-start(bf16[16,2432]{1,0:T(8,128)(2,1)} %get-tuple-element.31), channel_id=1, source_target_pairs={{0,14},{2,12},{4,10},{6,8},{8,6},{10,4},{12,2},{14,0},{1,15},{3,13... | collective-permute-start | bytes 233480 | tf_op jit(solution)/shard_map/ppermute | solution.py:124
  10.4 10.2 %collective-permute-start.2 = (bf16[16,2432]{1,0:T(8,128)(2,1)S(1)}, bf16[16,2432]{1,0:T(8,128)(2,1)}, u32[]{:S(2)}, u32[]{:S(2)}) collective-permute-start(bf16[16,2432]{1,0:T(8,128)(2,1)S(1)} %get-tuple-element.32), channel_id=1, source_target_pairs={{0,12},{2,14},{4,8},{6,10},{8,4},{10,6},{12,0},{14,2},{1,13},{3,15... | collective-permute-start | bytes 233480 | tf_op jit(solution)/shard_map/ppermute | solution.py:124
  10.7 12.6 %collective-permute-start.3 = (bf16[16,2432]{1,0:T(8,128)(2,1)S(1)}, bf16[16,2432]{1,0:T(8,128)(2,1)}, u32[]{:S(2)}, u32[]{:S(2)}) collective-permute-start(bf16[16,2432]{1,0:T(8,128)(2,1)S(1)} %get-tuple-element.33), channel_id=1, source_target_pairs={{0,10},{2,8},{4,14},{6,12},{8,2},{10,0},{12,6},{14,4},{1,11},{3,9}... | collective-permute-start | bytes 233480 | tf_op jit(solution)/shard_map/ppermute | solution.py:124
  11.4 12.7 %collective-permute-start.4 = (bf16[16,2432]{1,0:T(8,128)(2,1)S(1)}, bf16[16,2432]{1,0:T(8,128)(2,1)}, u32[]{:S(2)}, u32[]{:S(2)}) collective-permute-start(bf16[16,2432]{1,0:T(8,128)(2,1)S(1)} %get-tuple-element.34), channel_id=1, source_target_pairs={{0,8},{2,10},{4,12},{6,14},{8,0},{10,2},{12,4},{14,6},{1,9},{3,11}... | collective-permute-start | bytes 233480 | tf_op jit(solution)/shard_map/ppermute | solution.py:124
  13.4 12.2 %collective-permute-start.5 = (bf16[16,2432]{1,0:T(8,128)(2,1)S(1)}, bf16[16,2432]{1,0:T(8,128)(2,1)}, u32[]{:S(2)}, u32[]{:S(2)}) collective-permute-start(bf16[16,2432]{1,0:T(8,128)(2,1)S(1)} %get-tuple-element.29), channel_id=1, source_target_pairs={{0,6},{2,4},{4,2},{6,0},{8,14},{10,12},{12,10},{14,8},{1,7},{3,5},... | collective-permute-start | bytes 233480 | tf_op jit(solution)/shard_map/ppermute | solution.py:124
  18.9 7.6 %collective-permute-start.6 = (bf16[16,2432]{1,0:T(8,128)(2,1)S(1)}, bf16[16,2432]{1,0:T(8,128)(2,1)S(1)}, u32[]{:S(2)}, u32[]{:S(2)}) collective-permute-start(bf16[16,2432]{1,0:T(8,128)(2,1)S(1)} %get-tuple-element.35), channel_id=1, source_target_pairs={{0,4},{2,6},{4,0},{6,2},{8,12},{10,14},{12,8},{14,10},{1,5},{3,7},... | collective-permute-start | bytes 233480 | tf_op jit(solution)/shard_map/ppermute | solution.py:124
  20.6 5.9 %collective-permute-start.7 = (bf16[16,2432]{1,0:T(8,128)(2,1)S(1)}, bf16[16,2432]{1,0:T(8,128)(2,1)S(1)}, u32[]{:S(2)}, u32[]{:S(2)}) collective-permute-start(bf16[16,2432]{1,0:T(8,128)(2,1)S(1)} %get-tuple-element.28), channel_id=1, source_target_pairs={{0,2},{2,0},{4,6},{6,4},{8,10},{10,8},{12,14},{14,12},{1,3},{3,1},... | collective-permute-start | bytes 233480 | tf_op jit(solution)/shard_map/ppermute | solution.py:124
  23.2 4.7 %collective-permute-start.8 = (bf16[512,2304]{1,0:T(8,128)(2,1)}, bf16[512,2304]{1,0:T(8,128)(2,1)S(1)}, u32[]{:S(2)}, u32[]{:S(2)}) collective-permute-start(bf16[512,2304]{1,0:T(8,128)(2,1)} %pad_maximum_fusion), channel_id=1, source_target_pairs={{0,1},{1,0},{2,3},{3,2},{4,5},{5,4},{6,7},{7,6},{8,9},{9,8},{10,11... | collective-permute-start | bytes 7077896 | tf_op jit(solution)/shard_map/ppermute | solution.py:116
  24.1 5.2 %collective-permute-start = (f32[4624]{0:T(1024)S(1)}, f32[4624]{0:T(1024)S(1)}, u32[]{:S(2)}, u32[]{:S(2)}) collective-permute-start(f32[4624]{0:T(1024)S(1)} %pad_maximum_fusion.7), channel_id=1, source_target_pairs={{0,1},{1,0},{2,3},{3,2},{4,5},{5,4},{6,7},{7,6},{8,9},{9,8},{10,11... | collective-permute-start | bytes 55496 | tf_op jit(solution)/shard_map/ppermute | solution.py:116
  29.1 1.5 %collective-permute-start.9 = (f32[128,384]{1,0:T(8,128)S(1)}, f32[128,384]{1,0:T(8,128)S(1)}, u32[]{:S(2)}, u32[]{:S(2)}) collective-permute-start(f32[128,384]{1,0:T(8,128)S(1)} %pad_maximum_fusion.1), channel_id=1, source_target_pairs={{0,1},{1,0},{2,3},{3,2},{4,5},{5,4},{6,7},{7,6},{8,9},{9,8},{10,11... | collective-permute-start | bytes 589832 | tf_op jit(solution)/shard_map/ppermute | solution.py:116
  31.4 8.9 %collective-permute-start.10 = (bf16[16,2432]{1,0:T(8,128)(2,1)S(1)}, bf16[16,2432]{1,0:T(8,128)(2,1)S(1)}, u32[]{:S(2)}, u32[]{:S(2)}) collective-permute-start(bf16[16,2432]{1,0:T(8,128)(2,1)S(1)} %get-tuple-element.22), channel_id=1, source_target_pairs={{0,14},{2,12},{4,10},{6,8},{8,6},{10,4},{12,2},{14,0},{1,15},{3,13... | collective-permute-start | bytes 233480 | tf_op jit(solution)/shard_map/ppermute | solution.py:124
  35.0 8.3 %collective-permute-start.11 = (bf16[16,2432]{1,0:T(8,128)(2,1)S(1)}, bf16[16,2432]{1,0:T(8,128)(2,1)S(1)}, u32[]{:S(2)}, u32[]{:S(2)}) collective-permute-start(bf16[16,2432]{1,0:T(8,128)(2,1)S(1)} %get-tuple-element.23), channel_id=1, source_target_pairs={{0,12},{2,14},{4,8},{6,10},{8,4},{10,6},{12,0},{14,2},{1,13},{3,15... | collective-permute-start | bytes 233480 | tf_op jit(solution)/shard_map/ppermute | solution.py:124
  36.2 10.7 %collective-permute-start.12 = (bf16[16,2432]{1,0:T(8,128)(2,1)S(1)}, bf16[16,2432]{1,0:T(8,128)(2,1)S(1)}, u32[]{:S(2)}, u32[]{:S(2)}) collective-permute-start(bf16[16,2432]{1,0:T(8,128)(2,1)S(1)} %get-tuple-element.24), channel_id=1, source_target_pairs={{0,10},{2,8},{4,14},{6,12},{8,2},{10,0},{12,6},{14,4},{1,11},{3,9}... | collective-permute-start | bytes 233480 | tf_op jit(solution)/shard_map/ppermute | solution.py:124
  36.3 12.0 %collective-permute-start.13 = (bf16[16,2432]{1,0:T(8,128)(2,1)S(1)}, bf16[16,2432]{1,0:T(8,128)(2,1)S(1)}, u32[]{:S(2)}, u32[]{:S(2)}) collective-permute-start(bf16[16,2432]{1,0:T(8,128)(2,1)S(1)} %get-tuple-element.25), channel_id=1, source_target_pairs={{0,8},{2,10},{4,12},{6,14},{8,0},{10,2},{12,4},{14,6},{1,9},{3,11}... | collective-permute-start | bytes 233480 | tf_op jit(solution)/shard_map/ppermute | solution.py:124
  39.1 9.2 %collective-permute-start.14 = (bf16[16,2432]{1,0:T(8,128)(2,1)S(1)}, bf16[16,2432]{1,0:T(8,128)(2,1)S(1)}, u32[]{:S(2)}, u32[]{:S(2)}) collective-permute-start(bf16[16,2432]{1,0:T(8,128)(2,1)S(1)} %get-tuple-element.26), channel_id=1, source_target_pairs={{0,6},{2,4},{4,2},{6,0},{8,14},{10,12},{12,10},{14,8},{1,7},{3,5},... | collective-permute-start | bytes 233480 | tf_op jit(solution)/shard_map/ppermute | solution.py:124
  40.3 8.3 %collective-permute-start.15 = (bf16[16,2432]{1,0:T(8,128)(2,1)S(1)}, bf16[16,2432]{1,0:T(8,128)(2,1)S(1)}, u32[]{:S(2)}, u32[]{:S(2)}) collective-permute-start(bf16[16,2432]{1,0:T(8,128)(2,1)S(1)} %get-tuple-element.27), channel_id=1, source_target_pairs={{0,4},{2,6},{4,0},{6,2},{8,12},{10,14},{12,8},{14,10},{1,5},{3,7},... | collective-permute-start | bytes 233480 | tf_op jit(solution)/shard_map/ppermute | solution.py:124
  43.3 5.3 %collective-permute-start.16 = (bf16[16,2432]{1,0:T(8,128)(2,1)S(1)}, bf16[16,2432]{1,0:T(8,128)(2,1)S(1)}, u32[]{:S(2)}, u32[]{:S(2)}) collective-permute-start(bf16[16,2432]{1,0:T(8,128)(2,1)S(1)} %get-tuple-element.21), channel_id=1, source_target_pairs={{0,2},{2,0},{4,6},{6,4},{8,10},{10,8},{12,14},{14,12},{1,3},{3,1},... | collective-permute-start | bytes 233480 | tf_op jit(solution)/shard_map/ppermute | solution.py:124
  48.9 9.3 %collective-permute-start.17 = (bf16[16,2432]{1,0:T(8,128)(2,1)S(1)}, bf16[16,2432]{1,0:T(8,128)(2,1)S(1)}, u32[]{:S(2)}, u32[]{:S(2)}) collective-permute-start(bf16[16,2432]{1,0:T(8,128)(2,1)S(1)} %get-tuple-element.17), channel_id=1, source_target_pairs={{0,14},{2,12},{4,10},{6,8},{8,6},{10,4},{12,2},{14,0},{1,15},{3,13... | collective-permute-start | bytes 233480 | tf_op jit(solution)/shard_map/ppermute | solution.py:124
  52.9 8.1 %collective-permute-start.18 = (bf16[16,2432]{1,0:T(8,128)(2,1)S(1)}, bf16[16,2432]{1,0:T(8,128)(2,1)S(1)}, u32[]{:S(2)}, u32[]{:S(2)}) collective-permute-start(bf16[16,2432]{1,0:T(8,128)(2,1)S(1)} %get-tuple-element.16), channel_id=1, source_target_pairs={{0,12},{2,14},{4,8},{6,10},{8,4},{10,6},{12,0},{14,2},{1,13},{3,15... | collective-permute-start | bytes 233480 | tf_op jit(solution)/shard_map/ppermute | solution.py:124
  53.2 11.4 %collective-permute-start.19 = (bf16[16,2432]{1,0:T(8,128)(2,1)S(1)}, bf16[16,2432]{1,0:T(8,128)(2,1)S(1)}, u32[]{:S(2)}, u32[]{:S(2)}) collective-permute-start(bf16[16,2432]{1,0:T(8,128)(2,1)S(1)} %get-tuple-element.15), channel_id=1, source_target_pairs={{0,10},{2,8},{4,14},{6,12},{8,2},{10,0},{12,6},{14,4},{1,11},{3,9}... | collective-permute-start | bytes 233480 | tf_op jit(solution)/shard_map/ppermute | solution.py:124
  55.2 9.9 %collective-permute-start.20 = (bf16[16,2432]{1,0:T(8,128)(2,1)S(1)}, bf16[16,2432]{1,0:T(8,128)(2,1)S(1)}, u32[]{:S(2)}, u32[]{:S(2)}) collective-permute-start(bf16[16,2432]{1,0:T(8,128)(2,1)S(1)} %get-tuple-element.14), channel_id=1, source_target_pairs={{0,8},{2,10},{4,12},{6,14},{8,0},{10,2},{12,4},{14,6},{1,9},{3,11}... | collective-permute-start | bytes 233480 | tf_op jit(solution)/shard_map/ppermute | solution.py:124
  56.6 8.5 %collective-permute-start.21 = (bf16[16,2432]{1,0:T(8,128)(2,1)S(1)}, bf16[16,2432]{1,0:T(8,128)(2,1)S(1)}, u32[]{:S(2)}, u32[]{:S(2)}) collective-permute-start(bf16[16,2432]{1,0:T(8,128)(2,1)S(1)} %get-tuple-element.18), channel_id=1, source_target_pairs={{0,6},{2,4},{4,2},{6,0},{8,14},{10,12},{12,10},{14,8},{1,7},{3,5},... | collective-permute-start | bytes 233480 | tf_op jit(solution)/shard_map/ppermute | solution.py:124
  58.2 7.3 %collective-permute-start.22 = (bf16[16,2432]{1,0:T(8,128)(2,1)S(1)}, bf16[16,2432]{1,0:T(8,128)(2,1)S(1)}, u32[]{:S(2)}, u32[]{:S(2)}) collective-permute-start(bf16[16,2432]{1,0:T(8,128)(2,1)S(1)} %get-tuple-element.19), channel_id=1, source_target_pairs={{0,4},{2,6},{4,0},{6,2},{8,12},{10,14},{12,8},{14,10},{1,5},{3,7},... | collective-permute-start | bytes 233480 | tf_op jit(solution)/shard_map/ppermute | solution.py:124
  61.0 4.5 %collective-permute-start.23 = (bf16[16,2432]{1,0:T(8,128)(2,1)S(1)}, bf16[16,2432]{1,0:T(8,128)(2,1)S(1)}, u32[]{:S(2)}, u32[]{:S(2)}) collective-permute-start(bf16[16,2432]{1,0:T(8,128)(2,1)S(1)} %get-tuple-element.13), channel_id=1, source_target_pairs={{0,2},{2,0},{4,6},{6,4},{8,10},{10,8},{12,14},{14,12},{1,3},{3,1},... | collective-permute-start | bytes 233480 | tf_op jit(solution)/shard_map/ppermute | solution.py:124
  66.9 25.4 %collective-permute-start.33 = (bf16[16,2304]{1,0:T(8,128)(2,1)S(1)}, bf16[16,2304]{1,0:T(8,128)(2,1)S(1)}, u32[]{:S(2)}, u32[]{:S(2)}) collective-permute-start(bf16[16,2304]{1,0:T(8,128)(2,1)S(1)} %add_convert_fusion.1), channel_id=1, source_target_pairs={{0,1},{1,0},{2,3},{3,2},{4,5},{5,4},{6,7},{7,6},{8,9},{9,8},{10,11... | collective-permute-start | bytes 221192 | tf_op jit(solution)/shard_map/ppermute | solution.py:116
  69.0 8.2 %collective-permute-start.25 = (bf16[16,2432]{1,0:T(8,128)(2,1)S(1)}, bf16[16,2432]{1,0:T(8,128)(2,1)S(1)}, u32[]{:S(2)}, u32[]{:S(2)}) collective-permute-start(bf16[16,2432]{1,0:T(8,128)(2,1)S(1)} %get-tuple-element.7), channel_id=1, source_target_pairs={{0,14},{2,12},{4,10},{6,8},{8,6},{10,4},{12,2},{14,0},{1,15},{3,13... | collective-permute-start | bytes 233480 | tf_op jit(solution)/shard_map/ppermute | solution.py:124
  73.7 10.0 %collective-permute-start.26 = (bf16[16,2432]{1,0:T(8,128)(2,1)S(1)}, bf16[16,2432]{1,0:T(8,128)(2,1)S(1)}, u32[]{:S(2)}, u32[]{:S(2)}) collective-permute-start(bf16[16,2432]{1,0:T(8,128)(2,1)S(1)} %get-tuple-element.8), channel_id=1, source_target_pairs={{0,12},{2,14},{4,8},{6,10},{8,4},{10,6},{12,0},{14,2},{1,13},{3,15... | collective-permute-start | bytes 233480 | tf_op jit(solution)/shard_map/ppermute | solution.py:124
  73.8 12.8 %collective-permute-start.27 = (bf16[16,2432]{1,0:T(8,128)(2,1)S(1)}, bf16[16,2432]{1,0:T(8,128)(2,1)S(1)}, u32[]{:S(2)}, u32[]{:S(2)}) collective-permute-start(bf16[16,2432]{1,0:T(8,128)(2,1)S(1)} %get-tuple-element.9), channel_id=1, source_target_pairs={{0,10},{2,8},{4,14},{6,12},{8,2},{10,0},{12,6},{14,4},{1,11},{3,9}... | collective-permute-start | bytes 233480 | tf_op jit(solution)/shard_map/ppermute | solution.py:124
  76.0 11.6 %collective-permute-start.28 = (bf16[16,2432]{1,0:T(8,128)(2,1)S(1)}, bf16[16,2432]{1,0:T(8,128)(2,1)S(1)}, u32[]{:S(2)}, u32[]{:S(2)}) collective-permute-start(bf16[16,2432]{1,0:T(8,128)(2,1)S(1)} %get-tuple-element.10), channel_id=1, source_target_pairs={{0,8},{2,10},{4,12},{6,14},{8,0},{10,2},{12,4},{14,6},{1,9},{3,11}... | collective-permute-start | bytes 233480 | tf_op jit(solution)/shard_map/ppermute | solution.py:124
  77.1 12.2 %collective-permute-start.29 = (bf16[16,2432]{1,0:T(8,128)(2,1)S(1)}, bf16[16,2432]{1,0:T(8,128)(2,1)S(1)}, u32[]{:S(2)}, u32[]{:S(2)}) collective-permute-start(bf16[16,2432]{1,0:T(8,128)(2,1)S(1)} %get-tuple-element.11), channel_id=1, source_target_pairs={{0,6},{2,4},{4,2},{6,0},{8,14},{10,12},{12,10},{14,8},{1,7},{3,5},... | collective-permute-start | bytes 233480 | tf_op jit(solution)/shard_map/ppermute | solution.py:124
  83.8 6.1 %collective-permute-start.30 = (bf16[16,2432]{1,0:T(8,128)(2,1)S(1)}, bf16[16,2432]{1,0:T(8,128)(2,1)S(1)}, u32[]{:S(2)}, u32[]{:S(2)}) collective-permute-start(bf16[16,2432]{1,0:T(8,128)(2,1)S(1)} %get-tuple-element.12), channel_id=1, source_target_pairs={{0,4},{2,6},{4,0},{6,2},{8,12},{10,14},{12,8},{14,10},{1,5},{3,7},... | collective-permute-start | bytes 233480 | tf_op jit(solution)/shard_map/ppermute | solution.py:124
  86.6 4.4 %collective-permute-start.31 = (bf16[16,2432]{1,0:T(8,128)(2,1)S(1)}, bf16[16,2432]{1,0:T(8,128)(2,1)S(1)}, u32[]{:S(2)}, u32[]{:S(2)}) collective-permute-start(bf16[16,2432]{1,0:T(8,128)(2,1)S(1)} %get-tuple-element.6), channel_id=1, source_target_pairs={{0,2},{2,0},{4,6},{6,4},{8,10},{10,8},{12,14},{14,12},{1,3},{3,1},... | collective-permute-start | bytes 233480 | tf_op jit(solution)/shard_map/ppermute | solution.py:124
  (8 other events, 42.3 us)

commit v18 on v16

--- a/solution.py
+++ b/solution.py
@@ -120,7 +120,7 @@
     peers = parts.shape[0]
     moved = [parts[0]]
     for shift in range(1, peers):
-        route = [(d, (d + sign * shift) % peers) for d in range(peers)]
+        route = [(d, d ^ (peers - shift)) for d in range(peers)]
         moved.append(lax.ppermute(parts[shift], "dict", route))
     return jnp.stack(moved, axis=0)
 
@@ -134,7 +134,7 @@
     half = g_half.shape[1]
     owner = routes_l // held
     within = routes_l - owner * held
-    rel = (owner - me) % peers
+    rel = (peers - lax.bitwise_xor(owner, me)) % peers
     shifts = jnp.arange(peers, dtype=jnp.int32)
     at_rel = (rel[:, :, None] == shifts[None, None, :]).astype(jnp.bfloat16)
     act_grid = acts_l.reshape(rows, listed, block)
@@ -234,7 +234,7 @@
     depth = lax.axis_size("section")
     listed = routes.shape[-1]
     width = cotangent.shape[1]
-    if listed == peers and depth == 2 and width % (depth * 128) == 0:
+    if listed == peers and peers & (peers - 1) == 0 and depth == 2 and width % (depth * 128) == 0:
         return split_device(cotangent, routes, acts, decoder, encoder, gain, inv_rms)
     return slot_device(cotangent, routes, acts, decoder, encoder, gain, inv_rms)
 

time: 93.9 us -> 92.9 us (0.989)
  transfers between devices with their start and end apart: 34 -> 34, of which waited for: 12 -> 15; matrix products, arithmetic and copies ran while one was open for 10% -> 11% of each run, Pallas kernels for 0% -> 0%
where the time goes in v18:
time: 92.9 us; the launch traced here: 92.4 us
  starting transfers between devices  58.1 us (63%)
  waiting for transfers between devices  16.3 us (18%)
  local copies, waits for them, and re-layouts  8.77 us (9%)
  matrix products  4.19 us (5%)
  other arithmetic  4.02 us (4%)
  between operations  1.07 us (1%)
    ppermute x28, starting transfers between devices, exchange(): moved.append(lax.ppermute(parts[shift], 'dict', route))  56.7 us
    ppermute x28, waiting for transfers between devices, exchange(): moved.append(lax.ppermute(parts[shift], 'dict', route))  13.5 us
    unnamed x38, local copies, waits for them, and re-layouts  5.26 us
    ppermute x6, waiting for transfers between devices, swap_cores(): return lax.ppermute(block, 'section', [(0, 1), (1, 0)])  2.82 us
    dot_general x4, matrix products, with_dec(): lax.dot_general(g_all, dec, (((1,), (1,)), ((), ())), preferred_element_t...  2.17 us
  transfers between devices with their start and end apart: 34, of which 15 were waited for; matrix products, arithmetic and copies ran while one was open for 11% of the time, Pallas kernels for 0%

profile of v18, /device:TPU:0, one launch (start us, length us, event | category | flops | bytes accessed | tf_op | source)
XLA Modules:
  0.0 92.4 jit_solution(17334439576710761273)
XLA Ops:
  4.5 6.0 %collective-permute-start = (bf16[16,2432]{1,0:T(8,128)(2,1)}, bf16[16,2432]{1,0:T(8,128)(2,1)}, u32[]{:S(2)}, u32[]{:S(2)}) collective-permute-start(bf16[16,2432]{1,0:T(8,128)(2,1)} %get-tuple-element.35), channel_id=1, source_target_pairs={{0,14},{2,12},{4,10},{6,8},{8,6},{10,4},{12,2},{14,0},{1,15},{3,13... | collective-permute-start | bytes 233480 | tf_op jit(solution)/shard_map/ppermute | solution.py:124
  11.4 1.9 %collective-permute-start.3 = (bf16[16,2432]{1,0:T(8,128)(2,1)S(1)}, bf16[16,2432]{1,0:T(8,128)(2,1)}, u32[]{:S(2)}, u32[]{:S(2)}) collective-permute-start(bf16[16,2432]{1,0:T(8,128)(2,1)S(1)} %get-tuple-element.38), channel_id=1, source_target_pairs={{0,8},{2,10},{4,12},{6,14},{8,0},{10,2},{12,4},{14,6},{1,9},{3,11}... | collective-permute-start | bytes 233480 | tf_op jit(solution)/shard_map/ppermute | solution.py:124
  13.4 2.4 %collective-permute-start.4 = (bf16[16,2432]{1,0:T(8,128)(2,1)S(1)}, bf16[16,2432]{1,0:T(8,128)(2,1)}, u32[]{:S(2)}, u32[]{:S(2)}) collective-permute-start(bf16[16,2432]{1,0:T(8,128)(2,1)S(1)} %get-tuple-element.33), channel_id=1, source_target_pairs={{0,6},{2,4},{4,2},{6,0},{8,14},{10,12},{12,10},{14,8},{1,7},{3,5},... | collective-permute-start | bytes 233480 | tf_op jit(solution)/shard_map/ppermute | solution.py:124
  15.8 1.5 %dynamic-slice_bitcast_fusion = (bf16[256,2304]{1,0:T(8,128)(2,1)S(1)}, bf16[256,2304]{1,0:T(8,128)(2,1)S(1)}) fusion(bf16[1,256,4608]{2,1,0:T(8,128)(2,1)} %param.11, s32[]{:T(128)S(6)} %select_n.193, bf16[1,256,4608]{2,1,0:T(8,128)(2,1)S(1)} %copy-done), kind=kLoop, calls=%fused_computation.48 | loop fusion | bytes 4718596 | tf_op jit(solution)/shard_map/dynamic_slice | solution.py:203
  17.9 1.6 %collective-permute-start.5 = (bf16[16,2432]{1,0:T(8,128)(2,1)S(1)}, bf16[16,2432]{1,0:T(8,128)(2,1)S(1)}, u32[]{:S(2)}, u32[]{:S(2)}) collective-permute-start(bf16[16,2432]{1,0:T(8,128)(2,1)S(1)} %get-tuple-element.39), channel_id=1, source_target_pairs={{0,4},{2,6},{4,0},{6,2},{8,12},{10,14},{12,8},{14,10},{1,5},{3,7},... | collective-permute-start | bytes 233480 | tf_op jit(solution)/shard_map/ppermute | solution.py:124
  20.4 1.6 %collective-permute-start.6 = (bf16[16,2432]{1,0:T(8,128)(2,1)S(1)}, bf16[16,2432]{1,0:T(8,128)(2,1)S(1)}, u32[]{:S(2)}, u32[]{:S(2)}) collective-permute-start(bf16[16,2432]{1,0:T(8,128)(2,1)S(1)} %get-tuple-element.32), channel_id=1, source_target_pairs={{0,2},{2,0},{4,6},{6,4},{8,10},{10,8},{12,14},{14,12},{1,3},{3,1},... | collective-permute-start | bytes 233480 | tf_op jit(solution)/shard_map/ppermute | solution.py:124
  23.2 0.9 bitcast_dynamic-update-slice_fusion.27
  24.1 0.9 bitcast_dynamic-update-slice_fusion.26
  28.6 1.2 %collective-permute-done.9 = f32[128,384]{1,0:T(8,128)S(1)} collective-permute-done((f32[128,384]{1,0:T(8,128)S(1)}, f32[128,384]{1,0:T(8,128)S(1)}, u32[]{:S(2)}, u32[]{:S(2)}) %collective-permute-start.9) | collective-permute-done | bytes 196640 | tf_op jit(solution)/shard_map/ppermute | solution.py:116
  30.6 3.4 %collective-permute-start.10 = (bf16[16,2432]{1,0:T(8,128)(2,1)S(1)}, bf16[16,2432]{1,0:T(8,128)(2,1)S(1)}, u32[]{:S(2)}, u32[]{:S(2)}) collective-permute-start(bf16[16,2432]{1,0:T(8,128)(2,1)S(1)} %get-tuple-element.26), channel_id=1, source_target_pairs={{0,14},{2,12},{4,10},{6,8},{8,6},{10,4},{12,2},{14,0},{1,15},{3,13... | collective-permute-start | bytes 233480 | tf_op jit(solution)/shard_map/ppermute | solution.py:124
  34.1 1.3 %collective-permute-start.11 = (bf16[16,2432]{1,0:T(8,128)(2,1)S(1)}, bf16[16,2432]{1,0:T(8,128)(2,1)S(1)}, u32[]{:S(2)}, u32[]{:S(2)}) collective-permute-start(bf16[16,2432]{1,0:T(8,128)(2,1)S(1)} %get-tuple-element.27), channel_id=1, source_target_pairs={{0,12},{2,14},{4,8},{6,10},{8,4},{10,6},{12,0},{14,2},{1,13},{3,15... | collective-permute-start | bytes 233480 | tf_op jit(solution)/shard_map/ppermute | solution.py:124
  35.4 2.9 %collective-permute-start.13 = (bf16[16,2432]{1,0:T(8,128)(2,1)S(1)}, bf16[16,2432]{1,0:T(8,128)(2,1)S(1)}, u32[]{:S(2)}, u32[]{:S(2)}) collective-permute-start(bf16[16,2432]{1,0:T(8,128)(2,1)S(1)} %get-tuple-element.29), channel_id=1, source_target_pairs={{0,8},{2,10},{4,12},{6,14},{8,0},{10,2},{12,4},{14,6},{1,9},{3,11}... | collective-permute-start | bytes 233480 | tf_op jit(solution)/shard_map/ppermute | solution.py:124
  38.4 1.0 %collective-permute-start.14 = (bf16[16,2432]{1,0:T(8,128)(2,1)S(1)}, bf16[16,2432]{1,0:T(8,128)(2,1)S(1)}, u32[]{:S(2)}, u32[]{:S(2)}) collective-permute-start(bf16[16,2432]{1,0:T(8,128)(2,1)S(1)} %get-tuple-element.30), channel_id=1, source_target_pairs={{0,6},{2,4},{4,2},{6,0},{8,14},{10,12},{12,10},{14,8},{1,7},{3,5},... | collective-permute-start | bytes 233480 | tf_op jit(solution)/shard_map/ppermute | solution.py:124
  39.4 3.4 %collective-permute-start.15 = (bf16[16,2432]{1,0:T(8,128)(2,1)S(1)}, bf16[16,2432]{1,0:T(8,128)(2,1)S(1)}, u32[]{:S(2)}, u32[]{:S(2)}) collective-permute-start(bf16[16,2432]{1,0:T(8,128)(2,1)S(1)} %get-tuple-element.31), channel_id=1, source_target_pairs={{0,4},{2,6},{4,0},{6,2},{8,12},{10,14},{12,8},{14,10},{1,5},{3,7},... | collective-permute-start | bytes 233480 | tf_op jit(solution)/shard_map/ppermute | solution.py:124
  42.9 3.1 %collective-permute-done.12 = bf16[16,2432]{1,0:T(8,128)(2,1)S(1)} collective-permute-done((bf16[16,2432]{1,0:T(8,128)(2,1)S(1)}, bf16[16,2432]{1,0:T(8,128)(2,1)S(1)}, u32[]{:S(2)}, u32[]{:S(2)}) %collective-permute-start.12) | collective-permute-done | bytes 77856 | tf_op jit(solution)/shard_map/ppermute | solution.py:124
  46.1 1.5 %collective-permute-done.13 = bf16[16,2432]{1,0:T(8,128)(2,1)S(1)} collective-permute-done((bf16[16,2432]{1,0:T(8,128)(2,1)S(1)}, bf16[16,2432]{1,0:T(8,128)(2,1)S(1)}, u32[]{:S(2)}, u32[]{:S(2)}) %collective-permute-start.13) | collective-permute-done | bytes 77856 | tf_op jit(solution)/shard_map/ppermute | solution.py:124
  48.4 4.0 %collective-permute-start.17 = (bf16[16,2432]{1,0:T(8,128)(2,1)S(1)}, bf16[16,2432]{1,0:T(8,128)(2,1)S(1)}, u32[]{:S(2)}, u32[]{:S(2)}) collective-permute-start(bf16[16,2432]{1,0:T(8,128)(2,1)S(1)} %get-tuple-element.21), channel_id=1, source_target_pairs={{0,14},{2,12},{4,10},{6,8},{8,6},{10,4},{12,2},{14,0},{1,15},{3,13... | collective-permute-start | bytes 233480 | tf_op jit(solution)/shard_map/ppermute | solution.py:124
  52.4 2.1 %collective-permute-start.19 = (bf16[16,2432]{1,0:T(8,128)(2,1)S(1)}, bf16[16,2432]{1,0:T(8,128)(2,1)S(1)}, u32[]{:S(2)}, u32[]{:S(2)}) collective-permute-start(bf16[16,2432]{1,0:T(8,128)(2,1)S(1)} %get-tuple-element.19), channel_id=1, source_target_pairs={{0,10},{2,8},{4,14},{6,12},{8,2},{10,0},{12,6},{14,4},{1,11},{3,9}... | collective-permute-start | bytes 233480 | tf_op jit(solution)/shard_map/ppermute | solution.py:124
  54.5 1.6 %collective-permute-start.20 = (bf16[16,2432]{1,0:T(8,128)(2,1)S(1)}, bf16[16,2432]{1,0:T(8,128)(2,1)S(1)}, u32[]{:S(2)}, u32[]{:S(2)}) collective-permute-start(bf16[16,2432]{1,0:T(8,128)(2,1)S(1)} %get-tuple-element.18), channel_id=1, source_target_pairs={{0,8},{2,10},{4,12},{6,14},{8,0},{10,2},{12,4},{14,6},{1,9},{3,11}... | collective-permute-start | bytes 233480 | tf_op jit(solution)/shard_map/ppermute | solution.py:124
  56.1 1.6 %collective-permute-start.21 = (bf16[16,2432]{1,0:T(8,128)(2,1)S(1)}, bf16[16,2432]{1,0:T(8,128)(2,1)S(1)}, u32[]{:S(2)}, u32[]{:S(2)}) collective-permute-start(bf16[16,2432]{1,0:T(8,128)(2,1)S(1)} %get-tuple-element.22), channel_id=1, source_target_pairs={{0,6},{2,4},{4,2},{6,0},{8,14},{10,12},{12,10},{14,8},{1,7},{3,5},... | collective-permute-start | bytes 233480 | tf_op jit(solution)/shard_map/ppermute | solution.py:124
  57.6 2.6 %collective-permute-start.22 = (bf16[16,2432]{1,0:T(8,128)(2,1)S(1)}, bf16[16,2432]{1,0:T(8,128)(2,1)S(1)}, u32[]{:S(2)}, u32[]{:S(2)}) collective-permute-start(bf16[16,2432]{1,0:T(8,128)(2,1)S(1)} %get-tuple-element.23), channel_id=1, source_target_pairs={{0,4},{2,6},{4,0},{6,2},{8,12},{10,14},{12,8},{14,10},{1,5},{3,7},... | collective-permute-start | bytes 233480 | tf_op jit(solution)/shard_map/ppermute | solution.py:124
  60.2 1.2 %collective-permute-start.23 = (bf16[16,2432]{1,0:T(8,128)(2,1)S(1)}, bf16[16,2432]{1,0:T(8,128)(2,1)S(1)}, u32[]{:S(2)}, u32[]{:S(2)}) collective-permute-start(bf16[16,2432]{1,0:T(8,128)(2,1)S(1)} %get-tuple-element.17), channel_id=1, source_target_pairs={{0,2},{2,0},{4,6},{6,4},{8,10},{10,8},{12,14},{14,12},{1,3},{3,1},... | collective-permute-start | bytes 233480 | tf_op jit(solution)/shard_map/ppermute | solution.py:124
  61.5 2.8 %collective-permute-done.19 = bf16[16,2432]{1,0:T(8,128)(2,1)S(1)} collective-permute-done((bf16[16,2432]{1,0:T(8,128)(2,1)S(1)}, bf16[16,2432]{1,0:T(8,128)(2,1)S(1)}, u32[]{:S(2)}, u32[]{:S(2)}) %collective-permute-start.19) | collective-permute-done | bytes 77856 | tf_op jit(solution)/shard_map/ppermute | solution.py:124
  68.4 4.6 %collective-permute-start.25 = (bf16[16,2432]{1,0:T(8,128)(2,1)S(1)}, bf16[16,2432]{1,0:T(8,128)(2,1)S(1)}, u32[]{:S(2)}, u32[]{:S(2)}) collective-permute-start(bf16[16,2432]{1,0:T(8,128)(2,1)S(1)} %get-tuple-element.11), channel_id=1, source_target_pairs={{0,14},{2,12},{4,10},{6,8},{8,6},{10,4},{12,2},{14,0},{1,15},{3,13... | collective-permute-start | bytes 233480 | tf_op jit(solution)/shard_map/ppermute | solution.py:124
  73.0 2.1 %collective-permute-start.27 = (bf16[16,2432]{1,0:T(8,128)(2,1)S(1)}, bf16[16,2432]{1,0:T(8,128)(2,1)S(1)}, u32[]{:S(2)}, u32[]{:S(2)}) collective-permute-start(bf16[16,2432]{1,0:T(8,128)(2,1)S(1)} %get-tuple-element.13), channel_id=1, source_target_pairs={{0,10},{2,8},{4,14},{6,12},{8,2},{10,0},{12,6},{14,4},{1,11},{3,9}... | collective-permute-start | bytes 233480 | tf_op jit(solution)/shard_map/ppermute | solution.py:124
  75.1 1.2 %collective-permute-start.28 = (bf16[16,2432]{1,0:T(8,128)(2,1)S(1)}, bf16[16,2432]{1,0:T(8,128)(2,1)S(1)}, u32[]{:S(2)}, u32[]{:S(2)}) collective-permute-start(bf16[16,2432]{1,0:T(8,128)(2,1)S(1)} %get-tuple-element.14), channel_id=1, source_target_pairs={{0,8},{2,10},{4,12},{6,14},{8,0},{10,2},{12,4},{14,6},{1,9},{3,11}... | collective-permute-start | bytes 233480 | tf_op jit(solution)/shard_map/ppermute | solution.py:124
  76.3 6.5 %collective-permute-start.29 = (bf16[16,2432]{1,0:T(8,128)(2,1)S(1)}, bf16[16,2432]{1,0:T(8,128)(2,1)S(1)}, u32[]{:S(2)}, u32[]{:S(2)}) collective-permute-start(bf16[16,2432]{1,0:T(8,128)(2,1)S(1)} %get-tuple-element.15), channel_id=1, source_target_pairs={{0,6},{2,4},{4,2},{6,0},{8,14},{10,12},{12,10},{14,8},{1,7},{3,5},... | collective-permute-start | bytes 233480 | tf_op jit(solution)/shard_map/ppermute | solution.py:124
  82.9 1.3 %collective-permute-start.30 = (bf16[16,2432]{1,0:T(8,128)(2,1)S(1)}, bf16[16,2432]{1,0:T(8,128)(2,1)S(1)}, u32[]{:S(2)}, u32[]{:S(2)}) collective-permute-start(bf16[16,2432]{1,0:T(8,128)(2,1)S(1)} %get-tuple-element.16), channel_id=1, source_target_pairs={{0,4},{2,6},{4,0},{6,2},{8,12},{10,14},{12,8},{14,10},{1,5},{3,7},... | collective-permute-start | bytes 233480 | tf_op jit(solution)/shard_map/ppermute | solution.py:124
  84.2 1.5 %collective-permute-done.27 = bf16[16,2432]{1,0:T(8,128)(2,1)S(1)} collective-permute-done((bf16[16,2432]{1,0:T(8,128)(2,1)S(1)}, bf16[16,2432]{1,0:T(8,128)(2,1)S(1)}, u32[]{:S(2)}, u32[]{:S(2)}) %collective-permute-start.27) | collective-permute-done | bytes 77856 | tf_op jit(solution)/shard_map/ppermute | solution.py:124
  85.7 1.1 %collective-permute-start.31 = (bf16[16,2432]{1,0:T(8,128)(2,1)S(1)}, bf16[16,2432]{1,0:T(8,128)(2,1)S(1)}, u32[]{:S(2)}, u32[]{:S(2)}) collective-permute-start(bf16[16,2432]{1,0:T(8,128)(2,1)S(1)} %get-tuple-element.10), channel_id=1, source_target_pairs={{0,2},{2,0},{4,6},{6,4},{8,10},{10,8},{12,14},{14,12},{1,3},{3,1},... | collective-permute-start | bytes 233480 | tf_op jit(solution)/shard_map/ppermute | solution.py:124
  86.9 1.7 %collective-permute-done.29 = bf16[16,2432]{1,0:T(8,128)(2,1)S(1)} collective-permute-done((bf16[16,2432]{1,0:T(8,128)(2,1)S(1)}, bf16[16,2432]{1,0:T(8,128)(2,1)S(1)}, u32[]{:S(2)}, u32[]{:S(2)}) %collective-permute-start.29) | collective-permute-done | bytes 77856 | tf_op jit(solution)/shard_map/ppermute | solution.py:124
  88.9 1.2 %collective-permute-done.31 = bf16[16,2432]{1,0:T(8,128)(2,1)S(1)} collective-permute-done((bf16[16,2432]{1,0:T(8,128)(2,1)S(1)}, bf16[16,2432]{1,0:T(8,128)(2,1)S(1)}, u32[]{:S(2)}, u32[]{:S(2)}) %collective-permute-start.31) | collective-permute-done | bytes 77856 | tf_op jit(solution)/shard_map/ppermute | solution.py:124
  (132 shorter events, 19.4 us)
Async XLA Ops:
  4.5 13.5 %collective-permute-start = (bf16[16,2432]{1,0:T(8,128)(2,1)}, bf16[16,2432]{1,0:T(8,128)(2,1)}, u32[]{:S(2)}, u32[]{:S(2)}) collective-permute-start(bf16[16,2432]{1,0:T(8,128)(2,1)} %get-tuple-element.35), channel_id=1, source_target_pairs={{0,14},{2,12},{4,10},{6,8},{8,6},{10,4},{12,2},{14,0},{1,15},{3,13... | collective-permute-start | bytes 233480 | tf_op jit(solution)/shard_map/ppermute | solution.py:124
  10.4 10.0 %collective-permute-start.1 = (bf16[16,2432]{1,0:T(8,128)(2,1)S(1)}, bf16[16,2432]{1,0:T(8,128)(2,1)}, u32[]{:S(2)}, u32[]{:S(2)}) collective-permute-start(bf16[16,2432]{1,0:T(8,128)(2,1)S(1)} %get-tuple-element.36), channel_id=1, source_target_pairs={{0,12},{2,14},{4,8},{6,10},{8,4},{10,6},{12,0},{14,2},{1,13},{3,15... | collective-permute-start | bytes 233480 | tf_op jit(solution)/shard_map/ppermute | solution.py:124
  10.7 12.5 %collective-permute-start.2 = (bf16[16,2432]{1,0:T(8,128)(2,1)S(1)}, bf16[16,2432]{1,0:T(8,128)(2,1)}, u32[]{:S(2)}, u32[]{:S(2)}) collective-permute-start(bf16[16,2432]{1,0:T(8,128)(2,1)S(1)} %get-tuple-element.37), channel_id=1, source_target_pairs={{0,10},{2,8},{4,14},{6,12},{8,2},{10,0},{12,6},{14,4},{1,11},{3,9}... | collective-permute-start | bytes 233480 | tf_op jit(solution)/shard_map/ppermute | solution.py:124
  11.4 12.7 %collective-permute-start.3 = (bf16[16,2432]{1,0:T(8,128)(2,1)S(1)}, bf16[16,2432]{1,0:T(8,128)(2,1)}, u32[]{:S(2)}, u32[]{:S(2)}) collective-permute-start(bf16[16,2432]{1,0:T(8,128)(2,1)S(1)} %get-tuple-element.38), channel_id=1, source_target_pairs={{0,8},{2,10},{4,12},{6,14},{8,0},{10,2},{12,4},{14,6},{1,9},{3,11}... | collective-permute-start | bytes 233480 | tf_op jit(solution)/shard_map/ppermute | solution.py:124
  13.4 11.6 %collective-permute-start.4 = (bf16[16,2432]{1,0:T(8,128)(2,1)S(1)}, bf16[16,2432]{1,0:T(8,128)(2,1)}, u32[]{:S(2)}, u32[]{:S(2)}) collective-permute-start(bf16[16,2432]{1,0:T(8,128)(2,1)S(1)} %get-tuple-element.33), channel_id=1, source_target_pairs={{0,6},{2,4},{4,2},{6,0},{8,14},{10,12},{12,10},{14,8},{1,7},{3,5},... | collective-permute-start | bytes 233480 | tf_op jit(solution)/shard_map/ppermute | solution.py:124
  17.9 8.0 %collective-permute-start.5 = (bf16[16,2432]{1,0:T(8,128)(2,1)S(1)}, bf16[16,2432]{1,0:T(8,128)(2,1)S(1)}, u32[]{:S(2)}, u32[]{:S(2)}) collective-permute-start(bf16[16,2432]{1,0:T(8,128)(2,1)S(1)} %get-tuple-element.39), channel_id=1, source_target_pairs={{0,4},{2,6},{4,0},{6,2},{8,12},{10,14},{12,8},{14,10},{1,5},{3,7},... | collective-permute-start | bytes 233480 | tf_op jit(solution)/shard_map/ppermute | solution.py:124
  20.4 5.5 %collective-permute-start.6 = (bf16[16,2432]{1,0:T(8,128)(2,1)S(1)}, bf16[16,2432]{1,0:T(8,128)(2,1)S(1)}, u32[]{:S(2)}, u32[]{:S(2)}) collective-permute-start(bf16[16,2432]{1,0:T(8,128)(2,1)S(1)} %get-tuple-element.32), channel_id=1, source_target_pairs={{0,2},{2,0},{4,6},{6,4},{8,10},{10,8},{12,14},{14,12},{1,3},{3,1},... | collective-permute-start | bytes 233480 | tf_op jit(solution)/shard_map/ppermute | solution.py:124
  23.2 4.5 %collective-permute-start.8 = (bf16[512,2304]{1,0:T(8,128)(2,1)S(1)}, bf16[512,2304]{1,0:T(8,128)(2,1)S(1)}, u32[]{:S(2)}, u32[]{:S(2)}) collective-permute-start(bf16[512,2304]{1,0:T(8,128)(2,1)S(1)} %pad_maximum_fusion), channel_id=1, source_target_pairs={{0,1},{1,0},{2,3},{3,2},{4,5},{5,4},{6,7},{7,6},{8,9},{9,8},{10,11... | collective-permute-start | bytes 7077896 | tf_op jit(solution)/shard_map/ppermute | solution.py:116
  26.0 2.5 %collective-permute-start.7 = (f32[4624]{0:T(1024)S(1)}, f32[4624]{0:T(1024)S(1)}, u32[]{:S(2)}, u32[]{:S(2)}) collective-permute-start(f32[4624]{0:T(1024)S(1)} %pad_maximum_fusion.7), channel_id=1, source_target_pairs={{0,1},{1,0},{2,3},{3,2},{4,5},{5,4},{6,7},{7,6},{8,9},{9,8},{10,11... | collective-permute-start | bytes 55496 | tf_op jit(solution)/shard_map/ppermute | solution.py:116
  28.3 1.5 %collective-permute-start.9 = (f32[128,384]{1,0:T(8,128)S(1)}, f32[128,384]{1,0:T(8,128)S(1)}, u32[]{:S(2)}, u32[]{:S(2)}) collective-permute-start(f32[128,384]{1,0:T(8,128)S(1)} %pad_maximum_fusion.1), channel_id=1, source_target_pairs={{0,1},{1,0},{2,3},{3,2},{4,5},{5,4},{6,7},{7,6},{8,9},{9,8},{10,11... | collective-permute-start | bytes 589832 | tf_op jit(solution)/shard_map/ppermute | solution.py:116
  30.6 8.7 %collective-permute-start.10 = (bf16[16,2432]{1,0:T(8,128)(2,1)S(1)}, bf16[16,2432]{1,0:T(8,128)(2,1)S(1)}, u32[]{:S(2)}, u32[]{:S(2)}) collective-permute-start(bf16[16,2432]{1,0:T(8,128)(2,1)S(1)} %get-tuple-element.26), channel_id=1, source_target_pairs={{0,14},{2,12},{4,10},{6,8},{8,6},{10,4},{12,2},{14,0},{1,15},{3,13... | collective-permute-start | bytes 233480 | tf_op jit(solution)/shard_map/ppermute | solution.py:124
  34.1 8.7 %collective-permute-start.11 = (bf16[16,2432]{1,0:T(8,128)(2,1)S(1)}, bf16[16,2432]{1,0:T(8,128)(2,1)S(1)}, u32[]{:S(2)}, u32[]{:S(2)}) collective-permute-start(bf16[16,2432]{1,0:T(8,128)(2,1)S(1)} %get-tuple-element.27), channel_id=1, source_target_pairs={{0,12},{2,14},{4,8},{6,10},{8,4},{10,6},{12,0},{14,2},{1,13},{3,15... | collective-permute-start | bytes 233480 | tf_op jit(solution)/shard_map/ppermute | solution.py:124
  35.4 10.6 %collective-permute-start.12 = (bf16[16,2432]{1,0:T(8,128)(2,1)S(1)}, bf16[16,2432]{1,0:T(8,128)(2,1)S(1)}, u32[]{:S(2)}, u32[]{:S(2)}) collective-permute-start(bf16[16,2432]{1,0:T(8,128)(2,1)S(1)} %get-tuple-element.28), channel_id=1, source_target_pairs={{0,10},{2,8},{4,14},{6,12},{8,2},{10,0},{12,6},{14,4},{1,11},{3,9}... | collective-permute-start | bytes 233480 | tf_op jit(solution)/shard_map/ppermute | solution.py:124
  35.4 12.1 %collective-permute-start.13 = (bf16[16,2432]{1,0:T(8,128)(2,1)S(1)}, bf16[16,2432]{1,0:T(8,128)(2,1)S(1)}, u32[]{:S(2)}, u32[]{:S(2)}) collective-permute-start(bf16[16,2432]{1,0:T(8,128)(2,1)S(1)} %get-tuple-element.29), channel_id=1, source_target_pairs={{0,8},{2,10},{4,12},{6,14},{8,0},{10,2},{12,4},{14,6},{1,9},{3,11}... | collective-permute-start | bytes 233480 | tf_op jit(solution)/shard_map/ppermute | solution.py:124
  38.4 9.2 %collective-permute-start.14 = (bf16[16,2432]{1,0:T(8,128)(2,1)S(1)}, bf16[16,2432]{1,0:T(8,128)(2,1)S(1)}, u32[]{:S(2)}, u32[]{:S(2)}) collective-permute-start(bf16[16,2432]{1,0:T(8,128)(2,1)S(1)} %get-tuple-element.30), channel_id=1, source_target_pairs={{0,6},{2,4},{4,2},{6,0},{8,14},{10,12},{12,10},{14,8},{1,7},{3,5},... | collective-permute-start | bytes 233480 | tf_op jit(solution)/shard_map/ppermute | solution.py:124
  39.4 8.7 %collective-permute-start.15 = (bf16[16,2432]{1,0:T(8,128)(2,1)S(1)}, bf16[16,2432]{1,0:T(8,128)(2,1)S(1)}, u32[]{:S(2)}, u32[]{:S(2)}) collective-permute-start(bf16[16,2432]{1,0:T(8,128)(2,1)S(1)} %get-tuple-element.31), channel_id=1, source_target_pairs={{0,4},{2,6},{4,0},{6,2},{8,12},{10,14},{12,8},{14,10},{1,5},{3,7},... | collective-permute-start | bytes 233480 | tf_op jit(solution)/shard_map/ppermute | solution.py:124
  42.8 5.2 %collective-permute-start.16 = (bf16[16,2432]{1,0:T(8,128)(2,1)S(1)}, bf16[16,2432]{1,0:T(8,128)(2,1)S(1)}, u32[]{:S(2)}, u32[]{:S(2)}) collective-permute-start(bf16[16,2432]{1,0:T(8,128)(2,1)S(1)} %get-tuple-element.25), channel_id=1, source_target_pairs={{0,2},{2,0},{4,6},{6,4},{8,10},{10,8},{12,14},{14,12},{1,3},{3,1},... | collective-permute-start | bytes 233480 | tf_op jit(solution)/shard_map/ppermute | solution.py:124
  48.4 9.3 %collective-permute-start.17 = (bf16[16,2432]{1,0:T(8,128)(2,1)S(1)}, bf16[16,2432]{1,0:T(8,128)(2,1)S(1)}, u32[]{:S(2)}, u32[]{:S(2)}) collective-permute-start(bf16[16,2432]{1,0:T(8,128)(2,1)S(1)} %get-tuple-element.21), channel_id=1, source_target_pairs={{0,14},{2,12},{4,10},{6,8},{8,6},{10,4},{12,2},{14,0},{1,15},{3,13... | collective-permute-start | bytes 233480 | tf_op jit(solution)/shard_map/ppermute | solution.py:124
  52.3 7.9 %collective-permute-start.18 = (bf16[16,2432]{1,0:T(8,128)(2,1)S(1)}, bf16[16,2432]{1,0:T(8,128)(2,1)S(1)}, u32[]{:S(2)}, u32[]{:S(2)}) collective-permute-start(bf16[16,2432]{1,0:T(8,128)(2,1)S(1)} %get-tuple-element.20), channel_id=1, source_target_pairs={{0,12},{2,14},{4,8},{6,10},{8,4},{10,6},{12,0},{14,2},{1,13},{3,15... | collective-permute-start | bytes 233480 | tf_op jit(solution)/shard_map/ppermute | solution.py:124
  52.4 12.0 %collective-permute-start.19 = (bf16[16,2432]{1,0:T(8,128)(2,1)S(1)}, bf16[16,2432]{1,0:T(8,128)(2,1)S(1)}, u32[]{:S(2)}, u32[]{:S(2)}) collective-permute-start(bf16[16,2432]{1,0:T(8,128)(2,1)S(1)} %get-tuple-element.19), channel_id=1, source_target_pairs={{0,10},{2,8},{4,14},{6,12},{8,2},{10,0},{12,6},{14,4},{1,11},{3,9}... | collective-permute-start | bytes 233480 | tf_op jit(solution)/shard_map/ppermute | solution.py:124
  54.5 9.8 %collective-permute-start.20 = (bf16[16,2432]{1,0:T(8,128)(2,1)S(1)}, bf16[16,2432]{1,0:T(8,128)(2,1)S(1)}, u32[]{:S(2)}, u32[]{:S(2)}) collective-permute-start(bf16[16,2432]{1,0:T(8,128)(2,1)S(1)} %get-tuple-element.18), channel_id=1, source_target_pairs={{0,8},{2,10},{4,12},{6,14},{8,0},{10,2},{12,4},{14,6},{1,9},{3,11}... | collective-permute-start | bytes 233480 | tf_op jit(solution)/shard_map/ppermute | solution.py:124
  56.1 8.3 %collective-permute-start.21 = (bf16[16,2432]{1,0:T(8,128)(2,1)S(1)}, bf16[16,2432]{1,0:T(8,128)(2,1)S(1)}, u32[]{:S(2)}, u32[]{:S(2)}) collective-permute-start(bf16[16,2432]{1,0:T(8,128)(2,1)S(1)} %get-tuple-element.22), channel_id=1, source_target_pairs={{0,6},{2,4},{4,2},{6,0},{8,14},{10,12},{12,10},{14,8},{1,7},{3,5},... | collective-permute-start | bytes 233480 | tf_op jit(solution)/shard_map/ppermute | solution.py:124
  57.6 6.9 %collective-permute-start.22 = (bf16[16,2432]{1,0:T(8,128)(2,1)S(1)}, bf16[16,2432]{1,0:T(8,128)(2,1)S(1)}, u32[]{:S(2)}, u32[]{:S(2)}) collective-permute-start(bf16[16,2432]{1,0:T(8,128)(2,1)S(1)} %get-tuple-element.23), channel_id=1, source_target_pairs={{0,4},{2,6},{4,0},{6,2},{8,12},{10,14},{12,8},{14,10},{1,5},{3,7},... | collective-permute-start | bytes 233480 | tf_op jit(solution)/shard_map/ppermute | solution.py:124
  60.2 4.7 %collective-permute-start.23 = (bf16[16,2432]{1,0:T(8,128)(2,1)S(1)}, bf16[16,2432]{1,0:T(8,128)(2,1)S(1)}, u32[]{:S(2)}, u32[]{:S(2)}) collective-permute-start(bf16[16,2432]{1,0:T(8,128)(2,1)S(1)} %get-tuple-element.17), channel_id=1, source_target_pairs={{0,2},{2,0},{4,6},{6,4},{8,10},{10,8},{12,14},{14,12},{1,3},{3,1},... | collective-permute-start | bytes 233480 | tf_op jit(solution)/shard_map/ppermute | solution.py:124
  66.3 25.2 %collective-permute-start.33 = (bf16[16,2304]{1,0:T(8,128)(2,1)S(1)}, bf16[16,2304]{1,0:T(8,128)(2,1)S(1)}, u32[]{:S(2)}, u32[]{:S(2)}) collective-permute-start(bf16[16,2304]{1,0:T(8,128)(2,1)S(1)} %add_convert_fusion.1), channel_id=1, source_target_pairs={{0,1},{1,0},{2,3},{3,2},{4,5},{5,4},{6,7},{7,6},{8,9},{9,8},{10,11... | collective-permute-start | bytes 221192 | tf_op jit(solution)/shard_map/ppermute | solution.py:116
  68.4 8.0 %collective-permute-start.25 = (bf16[16,2432]{1,0:T(8,128)(2,1)S(1)}, bf16[16,2432]{1,0:T(8,128)(2,1)S(1)}, u32[]{:S(2)}, u32[]{:S(2)}) collective-permute-start(bf16[16,2432]{1,0:T(8,128)(2,1)S(1)} %get-tuple-element.11), channel_id=1, source_target_pairs={{0,14},{2,12},{4,10},{6,8},{8,6},{10,4},{12,2},{14,0},{1,15},{3,13... | collective-permute-start | bytes 233480 | tf_op jit(solution)/shard_map/ppermute | solution.py:124
  72.9 9.9 %collective-permute-start.26 = (bf16[16,2432]{1,0:T(8,128)(2,1)S(1)}, bf16[16,2432]{1,0:T(8,128)(2,1)S(1)}, u32[]{:S(2)}, u32[]{:S(2)}) collective-permute-start(bf16[16,2432]{1,0:T(8,128)(2,1)S(1)} %get-tuple-element.12), channel_id=1, source_target_pairs={{0,12},{2,14},{4,8},{6,10},{8,4},{10,6},{12,0},{14,2},{1,13},{3,15... | collective-permute-start | bytes 233480 | tf_op jit(solution)/shard_map/ppermute | solution.py:124
  73.0 12.7 %collective-permute-start.27 = (bf16[16,2432]{1,0:T(8,128)(2,1)S(1)}, bf16[16,2432]{1,0:T(8,128)(2,1)S(1)}, u32[]{:S(2)}, u32[]{:S(2)}) collective-permute-start(bf16[16,2432]{1,0:T(8,128)(2,1)S(1)} %get-tuple-element.13), channel_id=1, source_target_pairs={{0,10},{2,8},{4,14},{6,12},{8,2},{10,0},{12,6},{14,4},{1,11},{3,9}... | collective-permute-start | bytes 233480 | tf_op jit(solution)/shard_map/ppermute | solution.py:124
  75.1 11.8 %collective-permute-start.28 = (bf16[16,2432]{1,0:T(8,128)(2,1)S(1)}, bf16[16,2432]{1,0:T(8,128)(2,1)S(1)}, u32[]{:S(2)}, u32[]{:S(2)}) collective-permute-start(bf16[16,2432]{1,0:T(8,128)(2,1)S(1)} %get-tuple-element.14), channel_id=1, source_target_pairs={{0,8},{2,10},{4,12},{6,14},{8,0},{10,2},{12,4},{14,6},{1,9},{3,11}... | collective-permute-start | bytes 233480 | tf_op jit(solution)/shard_map/ppermute | solution.py:124
  76.3 12.3 %collective-permute-start.29 = (bf16[16,2432]{1,0:T(8,128)(2,1)S(1)}, bf16[16,2432]{1,0:T(8,128)(2,1)S(1)}, u32[]{:S(2)}, u32[]{:S(2)}) collective-permute-start(bf16[16,2432]{1,0:T(8,128)(2,1)S(1)} %get-tuple-element.15), channel_id=1, source_target_pairs={{0,6},{2,4},{4,2},{6,0},{8,14},{10,12},{12,10},{14,8},{1,7},{3,5},... | collective-permute-start | bytes 233480 | tf_op jit(solution)/shard_map/ppermute | solution.py:124
  82.9 6.0 %collective-permute-start.30 = (bf16[16,2432]{1,0:T(8,128)(2,1)S(1)}, bf16[16,2432]{1,0:T(8,128)(2,1)S(1)}, u32[]{:S(2)}, u32[]{:S(2)}) collective-permute-start(bf16[16,2432]{1,0:T(8,128)(2,1)S(1)} %get-tuple-element.16), channel_id=1, source_target_pairs={{0,4},{2,6},{4,0},{6,2},{8,12},{10,14},{12,8},{14,10},{1,5},{3,7},... | collective-permute-start | bytes 233480 | tf_op jit(solution)/shard_map/ppermute | solution.py:124
  85.7 4.4 %collective-permute-start.31 = (bf16[16,2432]{1,0:T(8,128)(2,1)S(1)}, bf16[16,2432]{1,0:T(8,128)(2,1)S(1)}, u32[]{:S(2)}, u32[]{:S(2)}) collective-permute-start(bf16[16,2432]{1,0:T(8,128)(2,1)S(1)} %get-tuple-element.10), channel_id=1, source_target_pairs={{0,2},{2,0},{4,6},{6,4},{8,10},{10,8},{12,14},{14,12},{1,3},{3,1},... | collective-permute-start | bytes 233480 | tf_op jit(solution)/shard_map/ppermute | solution.py:124
  (8 other events, 55.7 us)

commit v19 on v18

--- a/solution.py
+++ b/solution.py
@@ -197,6 +197,7 @@
     theirs = (1 - here) * half
     small = jnp.concatenate([gain[0], inv_rms[0]], axis=0)
     other_small = None
+    halves = []
     sent_w = jnp.concatenate(
         [
             lax.dynamic_slice_in_dim(decoder[0], theirs, half, axis=1),
@@ -218,14 +219,17 @@
         attr, g_half, other_small = split_layer(
             g_half, routes[0], acts[0], own, other, is_own, small, other_small
         )
-        partner = swap_cores(g_half)
+        halves.append(g_half)
+        attr_keep = jnp.where(is_own, attr, attr_keep)
+    mine_both = jnp.stack(halves, axis=0)
+    theirs_both = swap_cores(mine_both)
+    for step, layer in enumerate(reversed(range(depth))):
         full = jnp.where(
             here == 0,
-            jnp.concatenate([g_half, partner], axis=1),
-            jnp.concatenate([partner, g_half], axis=1),
-        )
-        attr_keep = jnp.where(is_own, attr, attr_keep)
-        grad_keep = jnp.where(is_own, full, grad_keep)
+            jnp.concatenate([mine_both[step], theirs_both[step]], axis=1),
+            jnp.concatenate([theirs_both[step], mine_both[step]], axis=1),
+        )
+        grad_keep = jnp.where(here == layer, full, grad_keep)
     return (attr_keep[None], grad_keep[None])
 
 

time: 92.9 us -> 90.2 us (0.971)
  starting transfers between devices: 58.1 us -> 55.8 us
    ppermute x28, starting transfers between devices: 56.7 us -> 54.8 us  [exchange(): moved.append(lax.ppermute(parts[shift], 'dict', route))]
    ppermute x28, waiting for transfers between devices: 13.5 us -> 12.5 us  [exchange(): moved.append(lax.ppermute(parts[shift], 'dict', route))]
    ppermute x6 -> x5, waiting for transfers between devices: 2.82 us -> 3.42 us  [swap_cores(): return lax.ppermute(block, 'section', [(0, 1), (1, 0)])]
  transfers between devices with their start and end apart: 34 -> 33, of which waited for: 15 -> 14; matrix products, arithmetic and copies ran while one was open for 11% -> 10% of each run, Pallas kernels for 0% -> 0%
where the time goes in v19:
time: 90.2 us; the launch traced here: 89.8 us
  starting transfers between devices  55.8 us (62%)
  waiting for transfers between devices  15.9 us (18%)
  local copies, waits for them, and re-layouts  8.78 us (10%)
  matrix products  4.19 us (5%)
  other arithmetic  4.04 us (4%)
  between operations  1.09 us (1%)
    ppermute x28, starting transfers between devices, exchange(): moved.append(lax.ppermute(parts[shift], 'dict', route))  54.8 us
    ppermute x28, waiting for transfers between devices, exchange(): moved.append(lax.ppermute(parts[shift], 'dict', route))  12.5 us
    unnamed x38, local copies, waits for them, and re-layouts  5.26 us
    ppermute x5, waiting for transfers between devices, swap_cores(): return lax.ppermute(block, 'section', [(0, 1), (1, 0)])  3.42 us
    dot_general x4, matrix products, with_dec(): lax.dot_general(g_all, dec, (((1,), (1,)), ((), ())), preferred_element_t...  2.17 us
  transfers between devices with their start and end apart: 33, of which 14 were waited for; matrix products, arithmetic and copies ran while one was open for 10% of the time, Pallas kernels for 0%

profile of v19, /device:TPU:0, one launch (start us, length us, event | category | flops | bytes accessed | tf_op | source)
XLA Modules:
  0.0 89.8 jit_solution(13863804577253466530)
XLA Ops:
  4.5 6.0 %collective-permute-start = (bf16[16,2432]{1,0:T(8,128)(2,1)}, bf16[16,2432]{1,0:T(8,128)(2,1)}, u32[]{:S(2)}, u32[]{:S(2)}) collective-permute-start(bf16[16,2432]{1,0:T(8,128)(2,1)} %get-tuple-element.35), channel_id=1, source_target_pairs={{0,14},{2,12},{4,10},{6,8},{8,6},{10,4},{12,2},{14,0},{1,15},{3,13... | collective-permute-start | bytes 233480 | tf_op jit(solution)/shard_map/ppermute | solution.py:124
  11.4 1.9 %collective-permute-start.3 = (bf16[16,2432]{1,0:T(8,128)(2,1)S(1)}, bf16[16,2432]{1,0:T(8,128)(2,1)}, u32[]{:S(2)}, u32[]{:S(2)}) collective-permute-start(bf16[16,2432]{1,0:T(8,128)(2,1)S(1)} %get-tuple-element.38), channel_id=1, source_target_pairs={{0,8},{2,10},{4,12},{6,14},{8,0},{10,2},{12,4},{14,6},{1,9},{3,11}... | collective-permute-start | bytes 233480 | tf_op jit(solution)/shard_map/ppermute | solution.py:124
  13.4 2.4 %collective-permute-start.4 = (bf16[16,2432]{1,0:T(8,128)(2,1)S(1)}, bf16[16,2432]{1,0:T(8,128)(2,1)}, u32[]{:S(2)}, u32[]{:S(2)}) collective-permute-start(bf16[16,2432]{1,0:T(8,128)(2,1)S(1)} %get-tuple-element.33), channel_id=1, source_target_pairs={{0,6},{2,4},{4,2},{6,0},{8,14},{10,12},{12,10},{14,8},{1,7},{3,5},... | collective-permute-start | bytes 233480 | tf_op jit(solution)/shard_map/ppermute | solution.py:124
  15.8 1.5 %dynamic-slice_bitcast_fusion = (bf16[256,2304]{1,0:T(8,128)(2,1)S(1)}, bf16[256,2304]{1,0:T(8,128)(2,1)S(1)}) fusion(bf16[1,256,4608]{2,1,0:T(8,128)(2,1)} %param.11, s32[]{:T(128)S(6)} %select_n.193, bf16[1,256,4608]{2,1,0:T(8,128)(2,1)S(1)} %copy-done), kind=kLoop, calls=%fused_computation.48 | loop fusion | bytes 4718596 | tf_op jit(solution)/shard_map/dynamic_slice | solution.py:204
  17.9 1.6 %collective-permute-start.5 = (bf16[16,2432]{1,0:T(8,128)(2,1)S(1)}, bf16[16,2432]{1,0:T(8,128)(2,1)S(1)}, u32[]{:S(2)}, u32[]{:S(2)}) collective-permute-start(bf16[16,2432]{1,0:T(8,128)(2,1)S(1)} %get-tuple-element.39), channel_id=1, source_target_pairs={{0,4},{2,6},{4,0},{6,2},{8,12},{10,14},{12,8},{14,10},{1,5},{3,7},... | collective-permute-start | bytes 233480 | tf_op jit(solution)/shard_map/ppermute | solution.py:124
  20.4 1.6 %collective-permute-start.6 = (bf16[16,2432]{1,0:T(8,128)(2,1)S(1)}, bf16[16,2432]{1,0:T(8,128)(2,1)S(1)}, u32[]{:S(2)}, u32[]{:S(2)}) collective-permute-start(bf16[16,2432]{1,0:T(8,128)(2,1)S(1)} %get-tuple-element.32), channel_id=1, source_target_pairs={{0,2},{2,0},{4,6},{6,4},{8,10},{10,8},{12,14},{14,12},{1,3},{3,1},... | collective-permute-start | bytes 233480 | tf_op jit(solution)/shard_map/ppermute | solution.py:124
  23.2 0.9 %bitcast_dynamic-update-slice_fusion.27 = bf16[8,16,2432]{2,1,0:T(8,128)(2,1)S(1)} fusion(bf16[8,16,2432]{2,1,0:T(8,128)(2,1)S(1)} %bitcast_dynamic-update-slice_fusion.28, bf16[16,2432]{1,0:T(8,128)(2,1)} %collective-permute-done.2), kind=kLoop, calls=%fused_computation.177 | loop fusion | bytes 155648
  24.1 0.9 %bitcast_dynamic-update-slice_fusion.26 = bf16[8,16,2432]{2,1,0:T(8,128)(2,1)S(1)} fusion(bf16[8,16,2432]{2,1,0:T(8,128)(2,1)S(1)} %bitcast_dynamic-update-slice_fusion.27, bf16[16,2432]{1,0:T(8,128)(2,1)} %collective-permute-done.3), kind=kLoop, calls=%fused_computation.176 | loop fusion | bytes 155648
  25.0 0.9 %bitcast_dynamic-update-slice_fusion.25 = bf16[8,16,2432]{2,1,0:T(8,128)(2,1)S(1)} fusion(bf16[8,16,2432]{2,1,0:T(8,128)(2,1)S(1)} %bitcast_dynamic-update-slice_fusion.26, bf16[16,2432]{1,0:T(8,128)(2,1)} %collective-permute-done.4), kind=kLoop, calls=%fused_computation.175 | loop fusion | bytes 155648
  28.6 1.2 %collective-permute-done.9 = f32[128,384]{1,0:T(8,128)S(1)} collective-permute-done((f32[128,384]{1,0:T(8,128)S(1)}, f32[128,384]{1,0:T(8,128)S(1)}, u32[]{:S(2)}, u32[]{:S(2)}) %collective-permute-start.9) | collective-permute-done | bytes 196640 | tf_op jit(solution)/shard_map/ppermute | solution.py:116
  30.6 3.4 %collective-permute-start.10 = (bf16[16,2432]{1,0:T(8,128)(2,1)S(1)}, bf16[16,2432]{1,0:T(8,128)(2,1)S(1)}, u32[]{:S(2)}, u32[]{:S(2)}) collective-permute-start(bf16[16,2432]{1,0:T(8,128)(2,1)S(1)} %get-tuple-element.26), channel_id=1, source_target_pairs={{0,14},{2,12},{4,10},{6,8},{8,6},{10,4},{12,2},{14,0},{1,15},{3,13... | collective-permute-start | bytes 233480 | tf_op jit(solution)/shard_map/ppermute | solution.py:124
  34.1 1.3 %collective-permute-start.11 = (bf16[16,2432]{1,0:T(8,128)(2,1)S(1)}, bf16[16,2432]{1,0:T(8,128)(2,1)S(1)}, u32[]{:S(2)}, u32[]{:S(2)}) collective-permute-start(bf16[16,2432]{1,0:T(8,128)(2,1)S(1)} %get-tuple-element.27), channel_id=1, source_target_pairs={{0,12},{2,14},{4,8},{6,10},{8,4},{10,6},{12,0},{14,2},{1,13},{3,15... | collective-permute-start | bytes 233480 | tf_op jit(solution)/shard_map/ppermute | solution.py:124
  35.4 2.9 %collective-permute-start.13 = (bf16[16,2432]{1,0:T(8,128)(2,1)S(1)}, bf16[16,2432]{1,0:T(8,128)(2,1)S(1)}, u32[]{:S(2)}, u32[]{:S(2)}) collective-permute-start(bf16[16,2432]{1,0:T(8,128)(2,1)S(1)} %get-tuple-element.29), channel_id=1, source_target_pairs={{0,8},{2,10},{4,12},{6,14},{8,0},{10,2},{12,4},{14,6},{1,9},{3,11}... | collective-permute-start | bytes 233480 | tf_op jit(solution)/shard_map/ppermute | solution.py:124
  38.4 1.0 %collective-permute-start.14 = (bf16[16,2432]{1,0:T(8,128)(2,1)S(1)}, bf16[16,2432]{1,0:T(8,128)(2,1)S(1)}, u32[]{:S(2)}, u32[]{:S(2)}) collective-permute-start(bf16[16,2432]{1,0:T(8,128)(2,1)S(1)} %get-tuple-element.30), channel_id=1, source_target_pairs={{0,6},{2,4},{4,2},{6,0},{8,14},{10,12},{12,10},{14,8},{1,7},{3,5},... | collective-permute-start | bytes 233480 | tf_op jit(solution)/shard_map/ppermute | solution.py:124
  39.4 3.4 %collective-permute-start.15 = (bf16[16,2432]{1,0:T(8,128)(2,1)S(1)}, bf16[16,2432]{1,0:T(8,128)(2,1)S(1)}, u32[]{:S(2)}, u32[]{:S(2)}) collective-permute-start(bf16[16,2432]{1,0:T(8,128)(2,1)S(1)} %get-tuple-element.31), channel_id=1, source_target_pairs={{0,4},{2,6},{4,0},{6,2},{8,12},{10,14},{12,8},{14,10},{1,5},{3,7},... | collective-permute-start | bytes 233480 | tf_op jit(solution)/shard_map/ppermute | solution.py:124
  42.9 3.1 %collective-permute-done.12 = bf16[16,2432]{1,0:T(8,128)(2,1)S(1)} collective-permute-done((bf16[16,2432]{1,0:T(8,128)(2,1)S(1)}, bf16[16,2432]{1,0:T(8,128)(2,1)S(1)}, u32[]{:S(2)}, u32[]{:S(2)}) %collective-permute-start.12) | collective-permute-done | bytes 77856 | tf_op jit(solution)/shard_map/ppermute | solution.py:124
  46.1 1.5 %collective-permute-done.13 = bf16[16,2432]{1,0:T(8,128)(2,1)S(1)} collective-permute-done((bf16[16,2432]{1,0:T(8,128)(2,1)S(1)}, bf16[16,2432]{1,0:T(8,128)(2,1)S(1)}, u32[]{:S(2)}, u32[]{:S(2)}) %collective-permute-start.13) | collective-permute-done | bytes 77856 | tf_op jit(solution)/shard_map/ppermute | solution.py:124
  48.4 4.0 %collective-permute-start.17 = (bf16[16,2432]{1,0:T(8,128)(2,1)S(1)}, bf16[16,2432]{1,0:T(8,128)(2,1)S(1)}, u32[]{:S(2)}, u32[]{:S(2)}) collective-permute-start(bf16[16,2432]{1,0:T(8,128)(2,1)S(1)} %get-tuple-element.21), channel_id=1, source_target_pairs={{0,14},{2,12},{4,10},{6,8},{8,6},{10,4},{12,2},{14,0},{1,15},{3,13... | collective-permute-start | bytes 233480 | tf_op jit(solution)/shard_map/ppermute | solution.py:124
  52.4 2.1 %collective-permute-start.19 = (bf16[16,2432]{1,0:T(8,128)(2,1)S(1)}, bf16[16,2432]{1,0:T(8,128)(2,1)S(1)}, u32[]{:S(2)}, u32[]{:S(2)}) collective-permute-start(bf16[16,2432]{1,0:T(8,128)(2,1)S(1)} %get-tuple-element.19), channel_id=1, source_target_pairs={{0,10},{2,8},{4,14},{6,12},{8,2},{10,0},{12,6},{14,4},{1,11},{3,9}... | collective-permute-start | bytes 233480 | tf_op jit(solution)/shard_map/ppermute | solution.py:124
  54.5 1.6 %collective-permute-start.20 = (bf16[16,2432]{1,0:T(8,128)(2,1)S(1)}, bf16[16,2432]{1,0:T(8,128)(2,1)S(1)}, u32[]{:S(2)}, u32[]{:S(2)}) collective-permute-start(bf16[16,2432]{1,0:T(8,128)(2,1)S(1)} %get-tuple-element.18), channel_id=1, source_target_pairs={{0,8},{2,10},{4,12},{6,14},{8,0},{10,2},{12,4},{14,6},{1,9},{3,11}... | collective-permute-start | bytes 233480 | tf_op jit(solution)/shard_map/ppermute | solution.py:124
  56.1 1.6 %collective-permute-start.21 = (bf16[16,2432]{1,0:T(8,128)(2,1)S(1)}, bf16[16,2432]{1,0:T(8,128)(2,1)S(1)}, u32[]{:S(2)}, u32[]{:S(2)}) collective-permute-start(bf16[16,2432]{1,0:T(8,128)(2,1)S(1)} %get-tuple-element.22), channel_id=1, source_target_pairs={{0,6},{2,4},{4,2},{6,0},{8,14},{10,12},{12,10},{14,8},{1,7},{3,5},... | collective-permute-start | bytes 233480 | tf_op jit(solution)/shard_map/ppermute | solution.py:124
  57.6 2.6 %collective-permute-start.22 = (bf16[16,2432]{1,0:T(8,128)(2,1)S(1)}, bf16[16,2432]{1,0:T(8,128)(2,1)S(1)}, u32[]{:S(2)}, u32[]{:S(2)}) collective-permute-start(bf16[16,2432]{1,0:T(8,128)(2,1)S(1)} %get-tuple-element.23), channel_id=1, source_target_pairs={{0,4},{2,6},{4,0},{6,2},{8,12},{10,14},{12,8},{14,10},{1,5},{3,7},... | collective-permute-start | bytes 233480 | tf_op jit(solution)/shard_map/ppermute | solution.py:124
  60.2 1.2 %collective-permute-start.23 = (bf16[16,2432]{1,0:T(8,128)(2,1)S(1)}, bf16[16,2432]{1,0:T(8,128)(2,1)S(1)}, u32[]{:S(2)}, u32[]{:S(2)}) collective-permute-start(bf16[16,2432]{1,0:T(8,128)(2,1)S(1)} %get-tuple-element.17), channel_id=1, source_target_pairs={{0,2},{2,0},{4,6},{6,4},{8,10},{10,8},{12,14},{14,12},{1,3},{3,1},... | collective-permute-start | bytes 233480 | tf_op jit(solution)/shard_map/ppermute | solution.py:124
  61.5 2.8 %collective-permute-done.19 = bf16[16,2432]{1,0:T(8,128)(2,1)S(1)} collective-permute-done((bf16[16,2432]{1,0:T(8,128)(2,1)S(1)}, bf16[16,2432]{1,0:T(8,128)(2,1)S(1)}, u32[]{:S(2)}, u32[]{:S(2)}) %collective-permute-start.19) | collective-permute-done | bytes 77856 | tf_op jit(solution)/shard_map/ppermute | solution.py:124
  66.3 1.3 %collective-permute-done.24 = f32[128,384]{1,0:T(8,128)S(1)} collective-permute-done((f32[128,384]{1,0:T(8,128)S(1)}, f32[128,384]{1,0:T(8,128)S(1)}, u32[]{:S(2)}, u32[]{:S(2)}) %collective-permute-start.24) | collective-permute-done | bytes 196640 | tf_op jit(solution)/shard_map/ppermute | solution.py:116
  68.4 4.6 %collective-permute-start.25 = (bf16[16,2432]{1,0:T(8,128)(2,1)S(1)}, bf16[16,2432]{1,0:T(8,128)(2,1)S(1)}, u32[]{:S(2)}, u32[]{:S(2)}) collective-permute-start(bf16[16,2432]{1,0:T(8,128)(2,1)S(1)} %get-tuple-element.11), channel_id=1, source_target_pairs={{0,14},{2,12},{4,10},{6,8},{8,6},{10,4},{12,2},{14,0},{1,15},{3,13... | collective-permute-start | bytes 233480 | tf_op jit(solution)/shard_map/ppermute | solution.py:124
  73.0 2.1 %collective-permute-start.27 = (bf16[16,2432]{1,0:T(8,128)(2,1)S(1)}, bf16[16,2432]{1,0:T(8,128)(2,1)S(1)}, u32[]{:S(2)}, u32[]{:S(2)}) collective-permute-start(bf16[16,2432]{1,0:T(8,128)(2,1)S(1)} %get-tuple-element.13), channel_id=1, source_target_pairs={{0,10},{2,8},{4,14},{6,12},{8,2},{10,0},{12,6},{14,4},{1,11},{3,9}... | collective-permute-start | bytes 233480 | tf_op jit(solution)/shard_map/ppermute | solution.py:124
  75.1 1.2 %collective-permute-start.28 = (bf16[16,2432]{1,0:T(8,128)(2,1)S(1)}, bf16[16,2432]{1,0:T(8,128)(2,1)S(1)}, u32[]{:S(2)}, u32[]{:S(2)}) collective-permute-start(bf16[16,2432]{1,0:T(8,128)(2,1)S(1)} %get-tuple-element.14), channel_id=1, source_target_pairs={{0,8},{2,10},{4,12},{6,14},{8,0},{10,2},{12,4},{14,6},{1,9},{3,11}... | collective-permute-start | bytes 233480 | tf_op jit(solution)/shard_map/ppermute | solution.py:124
  76.3 1.9 %collective-permute-start.29 = (bf16[16,2432]{1,0:T(8,128)(2,1)S(1)}, bf16[16,2432]{1,0:T(8,128)(2,1)S(1)}, u32[]{:S(2)}, u32[]{:S(2)}) collective-permute-start(bf16[16,2432]{1,0:T(8,128)(2,1)S(1)} %get-tuple-element.15), channel_id=1, source_target_pairs={{0,6},{2,4},{4,2},{6,0},{8,14},{10,12},{12,10},{14,8},{1,7},{3,5},... | collective-permute-start | bytes 233480 | tf_op jit(solution)/shard_map/ppermute | solution.py:124
  78.2 4.1 %collective-permute-start.30 = (bf16[16,2432]{1,0:T(8,128)(2,1)S(1)}, bf16[16,2432]{1,0:T(8,128)(2,1)S(1)}, u32[]{:S(2)}, u32[]{:S(2)}) collective-permute-start(bf16[16,2432]{1,0:T(8,128)(2,1)S(1)} %get-tuple-element.16), channel_id=1, source_target_pairs={{0,4},{2,6},{4,0},{6,2},{8,12},{10,14},{12,8},{14,10},{1,5},{3,7},... | collective-permute-start | bytes 233480 | tf_op jit(solution)/shard_map/ppermute | solution.py:124
  82.4 1.1 %collective-permute-start.31 = (bf16[16,2432]{1,0:T(8,128)(2,1)S(1)}, bf16[16,2432]{1,0:T(8,128)(2,1)S(1)}, u32[]{:S(2)}, u32[]{:S(2)}) collective-permute-start(bf16[16,2432]{1,0:T(8,128)(2,1)S(1)} %get-tuple-element.10), channel_id=1, source_target_pairs={{0,2},{2,0},{4,6},{6,4},{8,10},{10,8},{12,14},{14,12},{1,3},{3,1},... | collective-permute-start | bytes 233480 | tf_op jit(solution)/shard_map/ppermute | solution.py:124
  83.5 2.2 %collective-permute-done.27 = bf16[16,2432]{1,0:T(8,128)(2,1)S(1)} collective-permute-done((bf16[16,2432]{1,0:T(8,128)(2,1)S(1)}, bf16[16,2432]{1,0:T(8,128)(2,1)S(1)}, u32[]{:S(2)}, u32[]{:S(2)}) %collective-permute-start.27) | collective-permute-done | bytes 77856 | tf_op jit(solution)/shard_map/ppermute | solution.py:124
  (132 shorter events, 18.7 us)
Async XLA Ops:
  4.5 13.5 %collective-permute-start = (bf16[16,2432]{1,0:T(8,128)(2,1)}, bf16[16,2432]{1,0:T(8,128)(2,1)}, u32[]{:S(2)}, u32[]{:S(2)}) collective-permute-start(bf16[16,2432]{1,0:T(8,128)(2,1)} %get-tuple-element.35), channel_id=1, source_target_pairs={{0,14},{2,12},{4,10},{6,8},{8,6},{10,4},{12,2},{14,0},{1,15},{3,13... | collective-permute-start | bytes 233480 | tf_op jit(solution)/shard_map/ppermute | solution.py:124
  10.4 10.0 %collective-permute-start.1 = (bf16[16,2432]{1,0:T(8,128)(2,1)S(1)}, bf16[16,2432]{1,0:T(8,128)(2,1)}, u32[]{:S(2)}, u32[]{:S(2)}) collective-permute-start(bf16[16,2432]{1,0:T(8,128)(2,1)S(1)} %get-tuple-element.36), channel_id=1, source_target_pairs={{0,12},{2,14},{4,8},{6,10},{8,4},{10,6},{12,0},{14,2},{1,13},{3,15... | collective-permute-start | bytes 233480 | tf_op jit(solution)/shard_map/ppermute | solution.py:124
  10.7 12.5 %collective-permute-start.2 = (bf16[16,2432]{1,0:T(8,128)(2,1)S(1)}, bf16[16,2432]{1,0:T(8,128)(2,1)}, u32[]{:S(2)}, u32[]{:S(2)}) collective-permute-start(bf16[16,2432]{1,0:T(8,128)(2,1)S(1)} %get-tuple-element.37), channel_id=1, source_target_pairs={{0,10},{2,8},{4,14},{6,12},{8,2},{10,0},{12,6},{14,4},{1,11},{3,9}... | collective-permute-start | bytes 233480 | tf_op jit(solution)/shard_map/ppermute | solution.py:124
  11.4 12.7 %collective-permute-start.3 = (bf16[16,2432]{1,0:T(8,128)(2,1)S(1)}, bf16[16,2432]{1,0:T(8,128)(2,1)}, u32[]{:S(2)}, u32[]{:S(2)}) collective-permute-start(bf16[16,2432]{1,0:T(8,128)(2,1)S(1)} %get-tuple-element.38), channel_id=1, source_target_pairs={{0,8},{2,10},{4,12},{6,14},{8,0},{10,2},{12,4},{14,6},{1,9},{3,11}... | collective-permute-start | bytes 233480 | tf_op jit(solution)/shard_map/ppermute | solution.py:124
  13.4 11.6 %collective-permute-start.4 = (bf16[16,2432]{1,0:T(8,128)(2,1)S(1)}, bf16[16,2432]{1,0:T(8,128)(2,1)}, u32[]{:S(2)}, u32[]{:S(2)}) collective-permute-start(bf16[16,2432]{1,0:T(8,128)(2,1)S(1)} %get-tuple-element.33), channel_id=1, source_target_pairs={{0,6},{2,4},{4,2},{6,0},{8,14},{10,12},{12,10},{14,8},{1,7},{3,5},... | collective-permute-start | bytes 233480 | tf_op jit(solution)/shard_map/ppermute | solution.py:124
  17.9 8.0 %collective-permute-start.5 = (bf16[16,2432]{1,0:T(8,128)(2,1)S(1)}, bf16[16,2432]{1,0:T(8,128)(2,1)S(1)}, u32[]{:S(2)}, u32[]{:S(2)}) collective-permute-start(bf16[16,2432]{1,0:T(8,128)(2,1)S(1)} %get-tuple-element.39), channel_id=1, source_target_pairs={{0,4},{2,6},{4,0},{6,2},{8,12},{10,14},{12,8},{14,10},{1,5},{3,7},... | collective-permute-start | bytes 233480 | tf_op jit(solution)/shard_map/ppermute | solution.py:124
  20.4 5.5 %collective-permute-start.6 = (bf16[16,2432]{1,0:T(8,128)(2,1)S(1)}, bf16[16,2432]{1,0:T(8,128)(2,1)S(1)}, u32[]{:S(2)}, u32[]{:S(2)}) collective-permute-start(bf16[16,2432]{1,0:T(8,128)(2,1)S(1)} %get-tuple-element.32), channel_id=1, source_target_pairs={{0,2},{2,0},{4,6},{6,4},{8,10},{10,8},{12,14},{14,12},{1,3},{3,1},... | collective-permute-start | bytes 233480 | tf_op jit(solution)/shard_map/ppermute | solution.py:124
  23.2 4.5 %collective-permute-start.8 = (bf16[512,2304]{1,0:T(8,128)(2,1)S(1)}, bf16[512,2304]{1,0:T(8,128)(2,1)S(1)}, u32[]{:S(2)}, u32[]{:S(2)}) collective-permute-start(bf16[512,2304]{1,0:T(8,128)(2,1)S(1)} %pad_maximum_fusion), channel_id=1, source_target_pairs={{0,1},{1,0},{2,3},{3,2},{4,5},{5,4},{6,7},{7,6},{8,9},{9,8},{10,11... | collective-permute-start | bytes 7077896 | tf_op jit(solution)/shard_map/ppermute | solution.py:116
  26.0 2.5 %collective-permute-start.7 = (f32[4624]{0:T(1024)S(1)}, f32[4624]{0:T(1024)S(1)}, u32[]{:S(2)}, u32[]{:S(2)}) collective-permute-start(f32[4624]{0:T(1024)S(1)} %pad_maximum_fusion.8), channel_id=1, source_target_pairs={{0,1},{1,0},{2,3},{3,2},{4,5},{5,4},{6,7},{7,6},{8,9},{9,8},{10,11... | collective-permute-start | bytes 55496 | tf_op jit(solution)/shard_map/ppermute | solution.py:116
  28.3 1.5 %collective-permute-start.9 = (f32[128,384]{1,0:T(8,128)S(1)}, f32[128,384]{1,0:T(8,128)S(1)}, u32[]{:S(2)}, u32[]{:S(2)}) collective-permute-start(f32[128,384]{1,0:T(8,128)S(1)} %pad_maximum_fusion.1), channel_id=1, source_target_pairs={{0,1},{1,0},{2,3},{3,2},{4,5},{5,4},{6,7},{7,6},{8,9},{9,8},{10,11... | collective-permute-start | bytes 589832 | tf_op jit(solution)/shard_map/ppermute | solution.py:116
  30.6 8.7 %collective-permute-start.10 = (bf16[16,2432]{1,0:T(8,128)(2,1)S(1)}, bf16[16,2432]{1,0:T(8,128)(2,1)S(1)}, u32[]{:S(2)}, u32[]{:S(2)}) collective-permute-start(bf16[16,2432]{1,0:T(8,128)(2,1)S(1)} %get-tuple-element.26), channel_id=1, source_target_pairs={{0,14},{2,12},{4,10},{6,8},{8,6},{10,4},{12,2},{14,0},{1,15},{3,13... | collective-permute-start | bytes 233480 | tf_op jit(solution)/shard_map/ppermute | solution.py:124
  34.1 8.7 %collective-permute-start.11 = (bf16[16,2432]{1,0:T(8,128)(2,1)S(1)}, bf16[16,2432]{1,0:T(8,128)(2,1)S(1)}, u32[]{:S(2)}, u32[]{:S(2)}) collective-permute-start(bf16[16,2432]{1,0:T(8,128)(2,1)S(1)} %get-tuple-element.27), channel_id=1, source_target_pairs={{0,12},{2,14},{4,8},{6,10},{8,4},{10,6},{12,0},{14,2},{1,13},{3,15... | collective-permute-start | bytes 233480 | tf_op jit(solution)/shard_map/ppermute | solution.py:124
  35.4 10.6 %collective-permute-start.12 = (bf16[16,2432]{1,0:T(8,128)(2,1)S(1)}, bf16[16,2432]{1,0:T(8,128)(2,1)S(1)}, u32[]{:S(2)}, u32[]{:S(2)}) collective-permute-start(bf16[16,2432]{1,0:T(8,128)(2,1)S(1)} %get-tuple-element.28), channel_id=1, source_target_pairs={{0,10},{2,8},{4,14},{6,12},{8,2},{10,0},{12,6},{14,4},{1,11},{3,9}... | collective-permute-start | bytes 233480 | tf_op jit(solution)/shard_map/ppermute | solution.py:124
  35.4 12.1 %collective-permute-start.13 = (bf16[16,2432]{1,0:T(8,128)(2,1)S(1)}, bf16[16,2432]{1,0:T(8,128)(2,1)S(1)}, u32[]{:S(2)}, u32[]{:S(2)}) collective-permute-start(bf16[16,2432]{1,0:T(8,128)(2,1)S(1)} %get-tuple-element.29), channel_id=1, source_target_pairs={{0,8},{2,10},{4,12},{6,14},{8,0},{10,2},{12,4},{14,6},{1,9},{3,11}... | collective-permute-start | bytes 233480 | tf_op jit(solution)/shard_map/ppermute | solution.py:124
  38.4 9.2 %collective-permute-start.14 = (bf16[16,2432]{1,0:T(8,128)(2,1)S(1)}, bf16[16,2432]{1,0:T(8,128)(2,1)S(1)}, u32[]{:S(2)}, u32[]{:S(2)}) collective-permute-start(bf16[16,2432]{1,0:T(8,128)(2,1)S(1)} %get-tuple-element.30), channel_id=1, source_target_pairs={{0,6},{2,4},{4,2},{6,0},{8,14},{10,12},{12,10},{14,8},{1,7},{3,5},... | collective-permute-start | bytes 233480 | tf_op jit(solution)/shard_map/ppermute | solution.py:124
  39.4 8.7 %collective-permute-start.15 = (bf16[16,2432]{1,0:T(8,128)(2,1)S(1)}, bf16[16,2432]{1,0:T(8,128)(2,1)S(1)}, u32[]{:S(2)}, u32[]{:S(2)}) collective-permute-start(bf16[16,2432]{1,0:T(8,128)(2,1)S(1)} %get-tuple-element.31), channel_id=1, source_target_pairs={{0,4},{2,6},{4,0},{6,2},{8,12},{10,14},{12,8},{14,10},{1,5},{3,7},... | collective-permute-start | bytes 233480 | tf_op jit(solution)/shard_map/ppermute | solution.py:124
  42.8 5.2 %collective-permute-start.16 = (bf16[16,2432]{1,0:T(8,128)(2,1)S(1)}, bf16[16,2432]{1,0:T(8,128)(2,1)S(1)}, u32[]{:S(2)}, u32[]{:S(2)}) collective-permute-start(bf16[16,2432]{1,0:T(8,128)(2,1)S(1)} %get-tuple-element.25), channel_id=1, source_target_pairs={{0,2},{2,0},{4,6},{6,4},{8,10},{10,8},{12,14},{14,12},{1,3},{3,1},... | collective-permute-start | bytes 233480 | tf_op jit(solution)/shard_map/ppermute | solution.py:124
  48.4 9.3 %collective-permute-start.17 = (bf16[16,2432]{1,0:T(8,128)(2,1)S(1)}, bf16[16,2432]{1,0:T(8,128)(2,1)S(1)}, u32[]{:S(2)}, u32[]{:S(2)}) collective-permute-start(bf16[16,2432]{1,0:T(8,128)(2,1)S(1)} %get-tuple-element.21), channel_id=1, source_target_pairs={{0,14},{2,12},{4,10},{6,8},{8,6},{10,4},{12,2},{14,0},{1,15},{3,13... | collective-permute-start | bytes 233480 | tf_op jit(solution)/shard_map/ppermute | solution.py:124
  52.3 7.9 %collective-permute-start.18 = (bf16[16,2432]{1,0:T(8,128)(2,1)S(1)}, bf16[16,2432]{1,0:T(8,128)(2,1)S(1)}, u32[]{:S(2)}, u32[]{:S(2)}) collective-permute-start(bf16[16,2432]{1,0:T(8,128)(2,1)S(1)} %get-tuple-element.20), channel_id=1, source_target_pairs={{0,12},{2,14},{4,8},{6,10},{8,4},{10,6},{12,0},{14,2},{1,13},{3,15... | collective-permute-start | bytes 233480 | tf_op jit(solution)/shard_map/ppermute | solution.py:124
  52.4 12.0 %collective-permute-start.19 = (bf16[16,2432]{1,0:T(8,128)(2,1)S(1)}, bf16[16,2432]{1,0:T(8,128)(2,1)S(1)}, u32[]{:S(2)}, u32[]{:S(2)}) collective-permute-start(bf16[16,2432]{1,0:T(8,128)(2,1)S(1)} %get-tuple-element.19), channel_id=1, source_target_pairs={{0,10},{2,8},{4,14},{6,12},{8,2},{10,0},{12,6},{14,4},{1,11},{3,9}... | collective-permute-start | bytes 233480 | tf_op jit(solution)/shard_map/ppermute | solution.py:124
  54.5 9.8 %collective-permute-start.20 = (bf16[16,2432]{1,0:T(8,128)(2,1)S(1)}, bf16[16,2432]{1,0:T(8,128)(2,1)S(1)}, u32[]{:S(2)}, u32[]{:S(2)}) collective-permute-start(bf16[16,2432]{1,0:T(8,128)(2,1)S(1)} %get-tuple-element.18), channel_id=1, source_target_pairs={{0,8},{2,10},{4,12},{6,14},{8,0},{10,2},{12,4},{14,6},{1,9},{3,11}... | collective-permute-start | bytes 233480 | tf_op jit(solution)/shard_map/ppermute | solution.py:124
  56.1 8.3 %collective-permute-start.21 = (bf16[16,2432]{1,0:T(8,128)(2,1)S(1)}, bf16[16,2432]{1,0:T(8,128)(2,1)S(1)}, u32[]{:S(2)}, u32[]{:S(2)}) collective-permute-start(bf16[16,2432]{1,0:T(8,128)(2,1)S(1)} %get-tuple-element.22), channel_id=1, source_target_pairs={{0,6},{2,4},{4,2},{6,0},{8,14},{10,12},{12,10},{14,8},{1,7},{3,5},... | collective-permute-start | bytes 233480 | tf_op jit(solution)/shard_map/ppermute | solution.py:124
  57.6 6.9 %collective-permute-start.22 = (bf16[16,2432]{1,0:T(8,128)(2,1)S(1)}, bf16[16,2432]{1,0:T(8,128)(2,1)S(1)}, u32[]{:S(2)}, u32[]{:S(2)}) collective-permute-start(bf16[16,2432]{1,0:T(8,128)(2,1)S(1)} %get-tuple-element.23), channel_id=1, source_target_pairs={{0,4},{2,6},{4,0},{6,2},{8,12},{10,14},{12,8},{14,10},{1,5},{3,7},... | collective-permute-start | bytes 233480 | tf_op jit(solution)/shard_map/ppermute | solution.py:124
  60.2 4.7 %collective-permute-start.23 = (bf16[16,2432]{1,0:T(8,128)(2,1)S(1)}, bf16[16,2432]{1,0:T(8,128)(2,1)S(1)}, u32[]{:S(2)}, u32[]{:S(2)}) collective-permute-start(bf16[16,2432]{1,0:T(8,128)(2,1)S(1)} %get-tuple-element.17), channel_id=1, source_target_pairs={{0,2},{2,0},{4,6},{6,4},{8,10},{10,8},{12,14},{14,12},{1,3},{3,1},... | collective-permute-start | bytes 233480 | tf_op jit(solution)/shard_map/ppermute | solution.py:124
  66.1 1.5 %collective-permute-start.24 = (f32[128,384]{1,0:T(8,128)S(1)}, f32[128,384]{1,0:T(8,128)S(1)}, u32[]{:S(2)}, u32[]{:S(2)}) collective-permute-start(f32[128,384]{1,0:T(8,128)S(1)} %pad_maximum_fusion.2), channel_id=1, source_target_pairs={{0,1},{1,0},{2,3},{3,2},{4,5},{5,4},{6,7},{7,6},{8,9},{9,8},{10,11... | collective-permute-start | bytes 589832 | tf_op jit(solution)/shard_map/ppermute | solution.py:116
  68.4 9.9 %collective-permute-start.25 = (bf16[16,2432]{1,0:T(8,128)(2,1)S(1)}, bf16[16,2432]{1,0:T(8,128)(2,1)S(1)}, u32[]{:S(2)}, u32[]{:S(2)}) collective-permute-start(bf16[16,2432]{1,0:T(8,128)(2,1)S(1)} %get-tuple-element.11), channel_id=1, source_target_pairs={{0,14},{2,12},{4,10},{6,8},{8,6},{10,4},{12,2},{14,0},{1,15},{3,13... | collective-permute-start | bytes 233480 | tf_op jit(solution)/shard_map/ppermute | solution.py:124
  72.9 9.4 %collective-permute-start.26 = (bf16[16,2432]{1,0:T(8,128)(2,1)S(1)}, bf16[16,2432]{1,0:T(8,128)(2,1)S(1)}, u32[]{:S(2)}, u32[]{:S(2)}) collective-permute-start(bf16[16,2432]{1,0:T(8,128)(2,1)S(1)} %get-tuple-element.12), channel_id=1, source_target_pairs={{0,12},{2,14},{4,8},{6,10},{8,4},{10,6},{12,0},{14,2},{1,13},{3,15... | collective-permute-start | bytes 233480 | tf_op jit(solution)/shard_map/ppermute | solution.py:124
  73.0 12.7 %collective-permute-start.27 = (bf16[16,2432]{1,0:T(8,128)(2,1)S(1)}, bf16[16,2432]{1,0:T(8,128)(2,1)S(1)}, u32[]{:S(2)}, u32[]{:S(2)}) collective-permute-start(bf16[16,2432]{1,0:T(8,128)(2,1)S(1)} %get-tuple-element.13), channel_id=1, source_target_pairs={{0,10},{2,8},{4,14},{6,12},{8,2},{10,0},{12,6},{14,4},{1,11},{3,9}... | collective-permute-start | bytes 233480 | tf_op jit(solution)/shard_map/ppermute | solution.py:124
  75.1 11.5 %collective-permute-start.28 = (bf16[16,2432]{1,0:T(8,128)(2,1)S(1)}, bf16[16,2432]{1,0:T(8,128)(2,1)S(1)}, u32[]{:S(2)}, u32[]{:S(2)}) collective-permute-start(bf16[16,2432]{1,0:T(8,128)(2,1)S(1)} %get-tuple-element.14), channel_id=1, source_target_pairs={{0,8},{2,10},{4,12},{6,14},{8,0},{10,2},{12,4},{14,6},{1,9},{3,11}... | collective-permute-start | bytes 233480 | tf_op jit(solution)/shard_map/ppermute | solution.py:124
  76.3 10.3 %collective-permute-start.29 = (bf16[16,2432]{1,0:T(8,128)(2,1)S(1)}, bf16[16,2432]{1,0:T(8,128)(2,1)S(1)}, u32[]{:S(2)}, u32[]{:S(2)}) collective-permute-start(bf16[16,2432]{1,0:T(8,128)(2,1)S(1)} %get-tuple-element.15), channel_id=1, source_target_pairs={{0,6},{2,4},{4,2},{6,0},{8,14},{10,12},{12,10},{14,8},{1,7},{3,5},... | collective-permute-start | bytes 233480 | tf_op jit(solution)/shard_map/ppermute | solution.py:124
  78.2 9.1 %collective-permute-start.30 = (bf16[16,2432]{1,0:T(8,128)(2,1)S(1)}, bf16[16,2432]{1,0:T(8,128)(2,1)S(1)}, u32[]{:S(2)}, u32[]{:S(2)}) collective-permute-start(bf16[16,2432]{1,0:T(8,128)(2,1)S(1)} %get-tuple-element.16), channel_id=1, source_target_pairs={{0,4},{2,6},{4,0},{6,2},{8,12},{10,14},{12,8},{14,10},{1,5},{3,7},... | collective-permute-start | bytes 233480 | tf_op jit(solution)/shard_map/ppermute | solution.py:124
  82.4 5.0 %collective-permute-start.31 = (bf16[16,2432]{1,0:T(8,128)(2,1)S(1)}, bf16[16,2432]{1,0:T(8,128)(2,1)S(1)}, u32[]{:S(2)}, u32[]{:S(2)}) collective-permute-start(bf16[16,2432]{1,0:T(8,128)(2,1)S(1)} %get-tuple-element.10), channel_id=1, source_target_pairs={{0,2},{2,0},{4,6},{6,4},{8,10},{10,8},{12,14},{14,12},{1,3},{3,1},... | collective-permute-start | bytes 233480 | tf_op jit(solution)/shard_map/ppermute | solution.py:124
  (7 other events, 54.3 us)

commit v20 on v19

--- a/solution.py
+++ b/solution.py
@@ -146,9 +146,6 @@
         [jnp.broadcast_to(g_half[None], (peers, rows, half)), placed], axis=-1
     )
     got = exchange(sent, 1).reshape(peers * rows, half + block)
-    if other_small is None:
-        small, got = lax.optimization_barrier((small, got))
-        other_small = swap_cores(small)
     g_all = got[:, :half]
     code_all = got[:, half:]
 
@@ -158,7 +155,16 @@
         )
 
     part = jnp.where(is_own, with_dec(own[0]), with_dec(other[0]))
-    paired = swap_cores(jnp.concatenate([part, code_all.astype(jnp.float32)], axis=1))
+    joined = jnp.concatenate([part, code_all.astype(jnp.float32)], axis=1)
+    if other_small is None:
+        lanes = joined.shape[1]
+        extra = -(-small.shape[0] // lanes)
+        padded = jnp.pad(small, (0, extra * lanes - small.shape[0])).reshape(extra, lanes)
+        paired = swap_cores(jnp.concatenate([joined, padded], axis=0))
+        other_small = paired[joined.shape[0]:].reshape(-1)[:small.shape[0]]
+        paired = paired[:joined.shape[0]]
+    else:
+        paired = swap_cores(joined)
     coef = (part + paired[:, :held * block]).astype(jnp.bfloat16)
     code = jnp.where(is_own, code_all.astype(jnp.float32), paired[:, held * block:])
     marks = jnp.concatenate([code == spot + 1 for spot in range(held)], axis=1)

time: 90.2 us -> 96.8 us (1.073)
  local copies, waits for them, and re-layouts: 8.78 us -> 13.9 us
  starting transfers between devices: 55.8 us -> 51.3 us
  other arithmetic: 4.04 us -> 7.92 us
  matrix products: 4.19 us -> 5.46 us
    unnamed x38 -> x44, local copies, waits for them, and re-layouts: 5.26 us -> 9.67 us
    ppermute x28, starting transfers between devices: 54.8 us -> 51 us  [exchange(): moved.append(lax.ppermute(parts[shift], 'dict', route))]
    ppermute x5 -> x4, waiting for transfers between devices: 3.42 us -> 5.01 us  [swap_cores(): return lax.ppermute(block, 'section', [(0, 1), (1, 0)])]
    concatenate x1, other arithmetic: 0.15 us -> 1.57 us  [split_device(): jnp.concatenate([lax.dynamic_slice_in_dim(decoder[0], theirs, half, axis=...]
    dot_general x4, matrix products: 1.33 us -> 2.6 us  [with_enc(): return jnp.dot(dz, enc, preferred_element_type=jnp.float32)]
    ppermute x28, waiting for transfers between devices: 12.5 us -> 11.3 us  [exchange(): moved.append(lax.ppermute(parts[shift], 'dict', route))]
  transfers between devices with their start and end apart: 33 -> 32, of which waited for: 14 -> 14; matrix products, arithmetic and copies ran while one was open for 10% -> 15% of each run, Pallas kernels for 0% -> 0%
where the time goes in v20:
time: 96.8 us; the launch traced here: 96 us
  starting transfers between devices  51.3 us (53%)
  waiting for transfers between devices  16.3 us (17%)
  local copies, waits for them, and re-layouts  13.9 us (14%)
  other arithmetic  7.92 us (8%)
  matrix products  5.46 us (6%)
  between operations  1.13 us (1%)
    ppermute x28, starting transfers between devices, exchange(): moved.append(lax.ppermute(parts[shift], 'dict', route))  51 us
    ppermute x28, waiting for transfers between devices, exchange(): moved.append(lax.ppermute(parts[shift], 'dict', route))  11.3 us
    unnamed x44, local copies, waits for them, and re-layouts  9.67 us
    ppermute x4, waiting for transfers between devices, swap_cores(): return lax.ppermute(block, 'section', [(0, 1), (1, 0)])  5.01 us
    dot_general x4, matrix products, with_enc(): return jnp.dot(dz, enc, preferred_element_type=jnp.float32)  2.6 us
    dot_general x4, matrix products, with_dec(): lax.dot_general(g_all, dec, (((1,), (1,)), ((), ())), preferred_element_t...  2.17 us
  transfers between devices with their start and end apart: 32, of which 14 were waited for; matrix products, arithmetic and copies ran while one was open for 15% of the time, Pallas kernels for 0%

profile of v20, /device:TPU:0, one launch (start us, length us, event | category | flops | bytes accessed | tf_op | source)
XLA Modules:
  0.0 96.0 jit_solution(13011793186735093822)
XLA Ops:
  4.5 6.0 %collective-permute-start = (bf16[16,2432]{1,0:T(8,128)(2,1)}, bf16[16,2432]{1,0:T(8,128)(2,1)}, u32[]{:S(2)}, u32[]{:S(2)}) collective-permute-start(bf16[16,2432]{1,0:T(8,128)(2,1)} %get-tuple-element.31), channel_id=1, source_target_pairs={{0,14},{2,12},{4,10},{6,8},{8,6},{10,4},{12,2},{14,0},{1,15},{3,13... | collective-permute-start | bytes 233480 | tf_op jit(solution)/shard_map/ppermute | solution.py:124
  11.4 1.9 %collective-permute-start.3 = (bf16[16,2432]{1,0:T(8,128)(2,1)S(1)}, bf16[16,2432]{1,0:T(8,128)(2,1)}, u32[]{:S(2)}, u32[]{:S(2)}) collective-permute-start(bf16[16,2432]{1,0:T(8,128)(2,1)S(1)} %get-tuple-element.34), channel_id=1, source_target_pairs={{0,8},{2,10},{4,12},{6,14},{8,0},{10,2},{12,4},{14,6},{1,9},{3,11}... | collective-permute-start | bytes 233480 | tf_op jit(solution)/shard_map/ppermute | solution.py:124
  13.4 2.4 %collective-permute-start.4 = (bf16[16,2432]{1,0:T(8,128)(2,1)S(1)}, bf16[16,2432]{1,0:T(8,128)(2,1)}, u32[]{:S(2)}, u32[]{:S(2)}) collective-permute-start(bf16[16,2432]{1,0:T(8,128)(2,1)S(1)} %get-tuple-element.29), channel_id=1, source_target_pairs={{0,6},{2,4},{4,2},{6,0},{8,14},{10,12},{12,10},{14,8},{1,7},{3,5},... | collective-permute-start | bytes 233480 | tf_op jit(solution)/shard_map/ppermute | solution.py:124
  15.7 1.5 %dynamic-slice_bitcast_fusion = (bf16[256,2304]{1,0:T(8,128)(2,1)S(1)}, bf16[256,2304]{1,0:T(8,128)(2,1)S(1)}) fusion(bf16[1,256,4608]{2,1,0:T(8,128)(2,1)} %param.11, s32[]{:T(128)S(6)} %select_n.190, bf16[1,256,4608]{2,1,0:T(8,128)(2,1)S(1)} %copy-done), kind=kLoop, calls=%fused_computation.48 | loop fusion | bytes 4718596 | tf_op jit(solution)/shard_map/dynamic_slice | solution.py:210
  17.2 1.6 %pad_maximum_fusion = bf16[512,2304]{1,0:T(8,128)(2,1)} fusion(bf16[256,2304]{1,0:T(8,128)(2,1)S(1)} %get-tuple-element.42, bf16[256,2304]{1,0:T(8,128)(2,1)S(1)} %get-tuple-element.43), kind=kLoop, calls=%fused_computation.4 | loop fusion | flops 4718592 | bytes 4718592 | tf_op jit(solution)/shard_map/concatenate | solution.py:207
  22.0 1.2 %collective-permute-done.2 = bf16[16,2432]{1,0:T(8,128)(2,1)} collective-permute-done((bf16[16,2432]{1,0:T(8,128)(2,1)}, bf16[16,2432]{1,0:T(8,128)(2,1)}, u32[]{:S(2)}, u32[]{:S(2)}) %collective-permute-start.2) | collective-permute-done | bytes 77856 | tf_op jit(solution)/shard_map/ppermute | solution.py:124
  26.0 2.0 %collective-permute-done.7 = bf16[512,2304]{1,0:T(8,128)(2,1)S(1)} collective-permute-done((bf16[512,2304]{1,0:T(8,128)(2,1)}, bf16[512,2304]{1,0:T(8,128)(2,1)S(1)}, u32[]{:S(2)}, u32[]{:S(2)}) %collective-permute-start.7) | collective-permute-done | bytes 2359328 | tf_op jit(solution)/shard_map/ppermute | solution.py:116
  29.5 1.5 %collective-permute-done.8 = f32[141,384]{1,0:T(8,128)} collective-permute-done((f32[141,384]{1,0:T(8,128)S(1)}, f32[141,384]{1,0:T(8,128)}, u32[]{:S(2)}, u32[]{:S(2)}) %collective-permute-start.8) | collective-permute-done | bytes 216608 | tf_op jit(solution)/shard_map/ppermute | solution.py:116
  31.9 0.9 add_select_fusion
  32.8 1.6 %fusion.19 = bf16[128,2304]{1,0:T(8,128)(2,1)S(1)} fusion(bf16[128,256]{1,0:T(8,128)(2,1)S(1)} %add_select_fusion, bf16[512,2304]{1,0:T(8,128)(2,1)} %copy-done.3), kind=kOutput, calls=%fused_computation.60 | convolution fusion | flops 150994944 | bytes 1835008 | tf_op jit(solution)/shard_map/dot_general | solution.py:174
  35.5 3.6 %collective-permute-start.9 = (bf16[16,2432]{1,0:T(8,128)(2,1)}, bf16[16,2432]{1,0:T(8,128)(2,1)}, u32[]{:S(2)}, u32[]{:S(2)}) collective-permute-start(bf16[16,2432]{1,0:T(8,128)(2,1)} %get-tuple-element.22), channel_id=1, source_target_pairs={{0,14},{2,12},{4,10},{6,8},{8,6},{10,4},{12,2},{14,0},{1,15},{3,13... | collective-permute-start | bytes 233480 | tf_op jit(solution)/shard_map/ppermute | solution.py:124
  39.1 1.2 %collective-permute-start.10 = (bf16[16,2432]{1,0:T(8,128)(2,1)}, bf16[16,2432]{1,0:T(8,128)(2,1)}, u32[]{:S(2)}, u32[]{:S(2)}) collective-permute-start(bf16[16,2432]{1,0:T(8,128)(2,1)} %get-tuple-element.23), channel_id=1, source_target_pairs={{0,12},{2,14},{4,8},{6,10},{8,4},{10,6},{12,0},{14,2},{1,13},{3,15... | collective-permute-start | bytes 233480 | tf_op jit(solution)/shard_map/ppermute | solution.py:124
  40.4 2.8 %collective-permute-start.12 = (bf16[16,2432]{1,0:T(8,128)(2,1)}, bf16[16,2432]{1,0:T(8,128)(2,1)}, u32[]{:S(2)}, u32[]{:S(2)}) collective-permute-start(bf16[16,2432]{1,0:T(8,128)(2,1)} %get-tuple-element.25), channel_id=1, source_target_pairs={{0,8},{2,10},{4,12},{6,14},{8,0},{10,2},{12,4},{14,6},{1,9},{3,11}... | collective-permute-start | bytes 233480 | tf_op jit(solution)/shard_map/ppermute | solution.py:124
  43.2 1.2 %collective-permute-start.13 = (bf16[16,2432]{1,0:T(8,128)(2,1)}, bf16[16,2432]{1,0:T(8,128)(2,1)}, u32[]{:S(2)}, u32[]{:S(2)}) collective-permute-start(bf16[16,2432]{1,0:T(8,128)(2,1)} %get-tuple-element.26), channel_id=1, source_target_pairs={{0,6},{2,4},{4,2},{6,0},{8,14},{10,12},{12,10},{14,8},{1,7},{3,5},... | collective-permute-start | bytes 233480 | tf_op jit(solution)/shard_map/ppermute | solution.py:124
  45.3 2.4 %collective-permute-start.14 = (bf16[16,2432]{1,0:T(8,128)(2,1)S(1)}, bf16[16,2432]{1,0:T(8,128)(2,1)S(1)}, u32[]{:S(2)}, u32[]{:S(2)}) collective-permute-start(bf16[16,2432]{1,0:T(8,128)(2,1)S(1)} %get-tuple-element.27), channel_id=1, source_target_pairs={{0,4},{2,6},{4,0},{6,2},{8,12},{10,14},{12,8},{14,10},{1,5},{3,7},... | collective-permute-start | bytes 233480 | tf_op jit(solution)/shard_map/ppermute | solution.py:124
  48.7 0.9 bitcast_dynamic-update-slice_fusion.20
  49.6 1.7 %collective-permute-done.11 = bf16[16,2432]{1,0:T(8,128)(2,1)} collective-permute-done((bf16[16,2432]{1,0:T(8,128)(2,1)}, bf16[16,2432]{1,0:T(8,128)(2,1)}, u32[]{:S(2)}, u32[]{:S(2)}) %collective-permute-start.11) | collective-permute-done | bytes 77856 | tf_op jit(solution)/shard_map/ppermute | solution.py:124
  52.7 1.0 %bitcast_dynamic-update-slice_fusion.18 = bf16[8,16,2432]{2,1,0:T(8,128)(2,1)S(1)} fusion(bf16[8,16,2432]{2,1,0:T(8,128)(2,1)S(1)} %bitcast_dynamic-update-slice_fusion.19, bf16[16,2432]{1,0:T(8,128)(2,1)} %collective-permute-done.12), kind=kLoop, calls=%fused_computation.169 | loop fusion | bytes 155648
  55.0 3.8 %collective-permute-start.16 = (bf16[16,2432]{1,0:T(8,128)(2,1)S(1)}, bf16[16,2432]{1,0:T(8,128)(2,1)S(1)}, u32[]{:S(2)}, u32[]{:S(2)}) collective-permute-start(bf16[16,2432]{1,0:T(8,128)(2,1)S(1)} %get-tuple-element.17), channel_id=1, source_target_pairs={{0,14},{2,12},{4,10},{6,8},{8,6},{10,4},{12,2},{14,0},{1,15},{3,13... | collective-permute-start | bytes 233480 | tf_op jit(solution)/shard_map/ppermute | solution.py:124
  59.9 2.8 %collective-permute-start.19 = (bf16[16,2432]{1,0:T(8,128)(2,1)S(1)}, bf16[16,2432]{1,0:T(8,128)(2,1)S(1)}, u32[]{:S(2)}, u32[]{:S(2)}) collective-permute-start(bf16[16,2432]{1,0:T(8,128)(2,1)S(1)} %get-tuple-element.14), channel_id=1, source_target_pairs={{0,8},{2,10},{4,12},{6,14},{8,0},{10,2},{12,4},{14,6},{1,9},{3,11}... | collective-permute-start | bytes 233480 | tf_op jit(solution)/shard_map/ppermute | solution.py:124
  62.7 1.4 %collective-permute-start.20 = (bf16[16,2432]{1,0:T(8,128)(2,1)S(1)}, bf16[16,2432]{1,0:T(8,128)(2,1)S(1)}, u32[]{:S(2)}, u32[]{:S(2)}) collective-permute-start(bf16[16,2432]{1,0:T(8,128)(2,1)S(1)} %get-tuple-element.18), channel_id=1, source_target_pairs={{0,6},{2,4},{4,2},{6,0},{8,14},{10,12},{12,10},{14,8},{1,7},{3,5},... | collective-permute-start | bytes 233480 | tf_op jit(solution)/shard_map/ppermute | solution.py:124
  64.1 1.3 %collective-permute-start.21 = (bf16[16,2432]{1,0:T(8,128)(2,1)S(1)}, bf16[16,2432]{1,0:T(8,128)(2,1)S(1)}, u32[]{:S(2)}, u32[]{:S(2)}) collective-permute-start(bf16[16,2432]{1,0:T(8,128)(2,1)S(1)} %get-tuple-element.19), channel_id=1, source_target_pairs={{0,4},{2,6},{4,0},{6,2},{8,12},{10,14},{12,8},{14,10},{1,5},{3,7},... | collective-permute-start | bytes 233480 | tf_op jit(solution)/shard_map/ppermute | solution.py:124
  65.7 2.1 %collective-permute-start.22 = (bf16[16,2432]{1,0:T(8,128)(2,1)S(1)}, bf16[16,2432]{1,0:T(8,128)(2,1)S(1)}, u32[]{:S(2)}, u32[]{:S(2)}) collective-permute-start(bf16[16,2432]{1,0:T(8,128)(2,1)S(1)} %get-tuple-element.13), channel_id=1, source_target_pairs={{0,2},{2,0},{4,6},{6,4},{8,10},{10,8},{12,14},{14,12},{1,3},{3,1},... | collective-permute-start | bytes 233480 | tf_op jit(solution)/shard_map/ppermute | solution.py:124
  67.8 2.7 %collective-permute-done.18 = bf16[16,2432]{1,0:T(8,128)(2,1)S(1)} collective-permute-done((bf16[16,2432]{1,0:T(8,128)(2,1)S(1)}, bf16[16,2432]{1,0:T(8,128)(2,1)S(1)}, u32[]{:S(2)}, u32[]{:S(2)}) %collective-permute-start.18) | collective-permute-done | bytes 77856 | tf_op jit(solution)/shard_map/ppermute | solution.py:124
  72.9 1.3 %collective-permute-done.23 = f32[128,384]{1,0:T(8,128)S(1)} collective-permute-done((f32[128,384]{1,0:T(8,128)S(1)}, f32[128,384]{1,0:T(8,128)S(1)}, u32[]{:S(2)}, u32[]{:S(2)}) %collective-permute-start.23) | collective-permute-done | bytes 196640 | tf_op jit(solution)/shard_map/ppermute | solution.py:116
  75.0 3.6 %collective-permute-start.24 = (bf16[16,2432]{1,0:T(8,128)(2,1)S(1)}, bf16[16,2432]{1,0:T(8,128)(2,1)S(1)}, u32[]{:S(2)}, u32[]{:S(2)}) collective-permute-start(bf16[16,2432]{1,0:T(8,128)(2,1)S(1)} %get-tuple-element.7), channel_id=1, source_target_pairs={{0,14},{2,12},{4,10},{6,8},{8,6},{10,4},{12,2},{14,0},{1,15},{3,13... | collective-permute-start | bytes 233480 | tf_op jit(solution)/shard_map/ppermute | solution.py:124
  79.2 1.7 %collective-permute-start.26 = (bf16[16,2432]{1,0:T(8,128)(2,1)S(1)}, bf16[16,2432]{1,0:T(8,128)(2,1)S(1)}, u32[]{:S(2)}, u32[]{:S(2)}) collective-permute-start(bf16[16,2432]{1,0:T(8,128)(2,1)S(1)} %get-tuple-element.9), channel_id=1, source_target_pairs={{0,10},{2,8},{4,14},{6,12},{8,2},{10,0},{12,6},{14,4},{1,11},{3,9}... | collective-permute-start | bytes 233480 | tf_op jit(solution)/shard_map/ppermute | solution.py:124
  80.9 2.0 %collective-permute-start.27 = (bf16[16,2432]{1,0:T(8,128)(2,1)S(1)}, bf16[16,2432]{1,0:T(8,128)(2,1)S(1)}, u32[]{:S(2)}, u32[]{:S(2)}) collective-permute-start(bf16[16,2432]{1,0:T(8,128)(2,1)S(1)} %get-tuple-element.10), channel_id=1, source_target_pairs={{0,8},{2,10},{4,12},{6,14},{8,0},{10,2},{12,4},{14,6},{1,9},{3,11}... | collective-permute-start | bytes 233480 | tf_op jit(solution)/shard_map/ppermute | solution.py:124
  82.9 1.4 %collective-permute-start.28 = (bf16[16,2432]{1,0:T(8,128)(2,1)S(1)}, bf16[16,2432]{1,0:T(8,128)(2,1)S(1)}, u32[]{:S(2)}, u32[]{:S(2)}) collective-permute-start(bf16[16,2432]{1,0:T(8,128)(2,1)S(1)} %get-tuple-element.11), channel_id=1, source_target_pairs={{0,6},{2,4},{4,2},{6,0},{8,14},{10,12},{12,10},{14,8},{1,7},{3,5},... | collective-permute-start | bytes 233480 | tf_op jit(solution)/shard_map/ppermute | solution.py:124
  84.3 4.4 %collective-permute-start.29 = (bf16[16,2432]{1,0:T(8,128)(2,1)S(1)}, bf16[16,2432]{1,0:T(8,128)(2,1)S(1)}, u32[]{:S(2)}, u32[]{:S(2)}) collective-permute-start(bf16[16,2432]{1,0:T(8,128)(2,1)S(1)} %get-tuple-element.12), channel_id=1, source_target_pairs={{0,4},{2,6},{4,0},{6,2},{8,12},{10,14},{12,8},{14,10},{1,5},{3,7},... | collective-permute-start | bytes 233480 | tf_op jit(solution)/shard_map/ppermute | solution.py:124
  88.8 0.9 collective-permute-start.30
  89.7 2.6 %collective-permute-done.26 = bf16[16,2432]{1,0:T(8,128)(2,1)S(1)} collective-permute-done((bf16[16,2432]{1,0:T(8,128)(2,1)S(1)}, bf16[16,2432]{1,0:T(8,128)(2,1)S(1)}, u32[]{:S(2)}, u32[]{:S(2)}) %collective-permute-start.26) | collective-permute-done | bytes 77856 | tf_op jit(solution)/shard_map/ppermute | solution.py:124
  (140 shorter events, 27.5 us)
Async XLA Ops:
  4.5 14.4 %collective-permute-start = (bf16[16,2432]{1,0:T(8,128)(2,1)}, bf16[16,2432]{1,0:T(8,128)(2,1)}, u32[]{:S(2)}, u32[]{:S(2)}) collective-permute-start(bf16[16,2432]{1,0:T(8,128)(2,1)} %get-tuple-element.31), channel_id=1, source_target_pairs={{0,14},{2,12},{4,10},{6,8},{8,6},{10,4},{12,2},{14,0},{1,15},{3,13... | collective-permute-start | bytes 233480 | tf_op jit(solution)/shard_map/ppermute | solution.py:124
  10.5 10.2 %collective-permute-start.1 = (bf16[16,2432]{1,0:T(8,128)(2,1)}, bf16[16,2432]{1,0:T(8,128)(2,1)}, u32[]{:S(2)}, u32[]{:S(2)}) collective-permute-start(bf16[16,2432]{1,0:T(8,128)(2,1)} %get-tuple-element.32), channel_id=1, source_target_pairs={{0,12},{2,14},{4,8},{6,10},{8,4},{10,6},{12,0},{14,2},{1,13},{3,15... | collective-permute-start | bytes 233480 | tf_op jit(solution)/shard_map/ppermute | solution.py:124
  10.7 12.5 %collective-permute-start.2 = (bf16[16,2432]{1,0:T(8,128)(2,1)}, bf16[16,2432]{1,0:T(8,128)(2,1)}, u32[]{:S(2)}, u32[]{:S(2)}) collective-permute-start(bf16[16,2432]{1,0:T(8,128)(2,1)} %get-tuple-element.33), channel_id=1, source_target_pairs={{0,10},{2,8},{4,14},{6,12},{8,2},{10,0},{12,6},{14,4},{1,11},{3,9}... | collective-permute-start | bytes 233480 | tf_op jit(solution)/shard_map/ppermute | solution.py:124
  11.4 12.7 %collective-permute-start.3 = (bf16[16,2432]{1,0:T(8,128)(2,1)S(1)}, bf16[16,2432]{1,0:T(8,128)(2,1)}, u32[]{:S(2)}, u32[]{:S(2)}) collective-permute-start(bf16[16,2432]{1,0:T(8,128)(2,1)S(1)} %get-tuple-element.34), channel_id=1, source_target_pairs={{0,8},{2,10},{4,12},{6,14},{8,0},{10,2},{12,4},{14,6},{1,9},{3,11}... | collective-permute-start | bytes 233480 | tf_op jit(solution)/shard_map/ppermute | solution.py:124
  13.4 11.6 %collective-permute-start.4 = (bf16[16,2432]{1,0:T(8,128)(2,1)S(1)}, bf16[16,2432]{1,0:T(8,128)(2,1)}, u32[]{:S(2)}, u32[]{:S(2)}) collective-permute-start(bf16[16,2432]{1,0:T(8,128)(2,1)S(1)} %get-tuple-element.29), channel_id=1, source_target_pairs={{0,6},{2,4},{4,2},{6,0},{8,14},{10,12},{12,10},{14,8},{1,7},{3,5},... | collective-permute-start | bytes 233480 | tf_op jit(solution)/shard_map/ppermute | solution.py:124
  18.9 7.0 %collective-permute-start.5 = (bf16[16,2432]{1,0:T(8,128)(2,1)S(1)}, bf16[16,2432]{1,0:T(8,128)(2,1)S(1)}, u32[]{:S(2)}, u32[]{:S(2)}) collective-permute-start(bf16[16,2432]{1,0:T(8,128)(2,1)S(1)} %get-tuple-element.35), channel_id=1, source_target_pairs={{0,4},{2,6},{4,0},{6,2},{8,12},{10,14},{12,8},{14,10},{1,5},{3,7},... | collective-permute-start | bytes 233480 | tf_op jit(solution)/shard_map/ppermute | solution.py:124
  20.7 5.3 %collective-permute-start.6 = (bf16[16,2432]{1,0:T(8,128)(2,1)S(1)}, bf16[16,2432]{1,0:T(8,128)(2,1)S(1)}, u32[]{:S(2)}, u32[]{:S(2)}) collective-permute-start(bf16[16,2432]{1,0:T(8,128)(2,1)S(1)} %get-tuple-element.28), channel_id=1, source_target_pairs={{0,2},{2,0},{4,6},{6,4},{8,10},{10,8},{12,14},{14,12},{1,3},{3,1},... | collective-permute-start | bytes 233480 | tf_op jit(solution)/shard_map/ppermute | solution.py:124
  23.2 4.7 %collective-permute-start.7 = (bf16[512,2304]{1,0:T(8,128)(2,1)}, bf16[512,2304]{1,0:T(8,128)(2,1)S(1)}, u32[]{:S(2)}, u32[]{:S(2)}) collective-permute-start(bf16[512,2304]{1,0:T(8,128)(2,1)} %pad_maximum_fusion), channel_id=1, source_target_pairs={{0,1},{1,0},{2,3},{3,2},{4,5},{5,4},{6,7},{7,6},{8,9},{9,8},{10,11... | collective-permute-start | bytes 7077896 | tf_op jit(solution)/shard_map/ppermute | solution.py:116
  29.4 1.6 %collective-permute-start.8 = (f32[141,384]{1,0:T(8,128)S(1)}, f32[141,384]{1,0:T(8,128)}, u32[]{:S(2)}, u32[]{:S(2)}) collective-permute-start(f32[141,384]{1,0:T(8,128)S(1)} %pad_maximum_fusion.1), channel_id=1, source_target_pairs={{0,1},{1,0},{2,3},{3,2},{4,5},{5,4},{6,7},{7,6},{8,9},{9,8},{10,11... | collective-permute-start | bytes 649736 | tf_op jit(solution)/shard_map/ppermute | solution.py:116
  35.5 9.8 %collective-permute-start.9 = (bf16[16,2432]{1,0:T(8,128)(2,1)}, bf16[16,2432]{1,0:T(8,128)(2,1)}, u32[]{:S(2)}, u32[]{:S(2)}) collective-permute-start(bf16[16,2432]{1,0:T(8,128)(2,1)} %get-tuple-element.22), channel_id=1, source_target_pairs={{0,14},{2,12},{4,10},{6,8},{8,6},{10,4},{12,2},{14,0},{1,15},{3,13... | collective-permute-start | bytes 233480 | tf_op jit(solution)/shard_map/ppermute | solution.py:124
  39.1 9.5 %collective-permute-start.10 = (bf16[16,2432]{1,0:T(8,128)(2,1)}, bf16[16,2432]{1,0:T(8,128)(2,1)}, u32[]{:S(2)}, u32[]{:S(2)}) collective-permute-start(bf16[16,2432]{1,0:T(8,128)(2,1)} %get-tuple-element.23), channel_id=1, source_target_pairs={{0,12},{2,14},{4,8},{6,10},{8,4},{10,6},{12,0},{14,2},{1,13},{3,15... | collective-permute-start | bytes 233480 | tf_op jit(solution)/shard_map/ppermute | solution.py:124
  40.3 11.0 %collective-permute-start.11 = (bf16[16,2432]{1,0:T(8,128)(2,1)}, bf16[16,2432]{1,0:T(8,128)(2,1)}, u32[]{:S(2)}, u32[]{:S(2)}) collective-permute-start(bf16[16,2432]{1,0:T(8,128)(2,1)} %get-tuple-element.24), channel_id=1, source_target_pairs={{0,10},{2,8},{4,14},{6,12},{8,2},{10,0},{12,6},{14,4},{1,11},{3,9}... | collective-permute-start | bytes 233480 | tf_op jit(solution)/shard_map/ppermute | solution.py:124
  40.4 12.3 %collective-permute-start.12 = (bf16[16,2432]{1,0:T(8,128)(2,1)}, bf16[16,2432]{1,0:T(8,128)(2,1)}, u32[]{:S(2)}, u32[]{:S(2)}) collective-permute-start(bf16[16,2432]{1,0:T(8,128)(2,1)} %get-tuple-element.25), channel_id=1, source_target_pairs={{0,8},{2,10},{4,12},{6,14},{8,0},{10,2},{12,4},{14,6},{1,9},{3,11}... | collective-permute-start | bytes 233480 | tf_op jit(solution)/shard_map/ppermute | solution.py:124
  43.2 10.5 %collective-permute-start.13 = (bf16[16,2432]{1,0:T(8,128)(2,1)}, bf16[16,2432]{1,0:T(8,128)(2,1)}, u32[]{:S(2)}, u32[]{:S(2)}) collective-permute-start(bf16[16,2432]{1,0:T(8,128)(2,1)} %get-tuple-element.26), channel_id=1, source_target_pairs={{0,6},{2,4},{4,2},{6,0},{8,14},{10,12},{12,10},{14,8},{1,7},{3,5},... | collective-permute-start | bytes 233480 | tf_op jit(solution)/shard_map/ppermute | solution.py:124
  45.3 9.4 %collective-permute-start.14 = (bf16[16,2432]{1,0:T(8,128)(2,1)S(1)}, bf16[16,2432]{1,0:T(8,128)(2,1)S(1)}, u32[]{:S(2)}, u32[]{:S(2)}) collective-permute-start(bf16[16,2432]{1,0:T(8,128)(2,1)S(1)} %get-tuple-element.27), channel_id=1, source_target_pairs={{0,4},{2,6},{4,0},{6,2},{8,12},{10,14},{12,8},{14,10},{1,5},{3,7},... | collective-permute-start | bytes 233480 | tf_op jit(solution)/shard_map/ppermute | solution.py:124
  48.6 6.1 %collective-permute-start.15 = (bf16[16,2432]{1,0:T(8,128)(2,1)S(1)}, bf16[16,2432]{1,0:T(8,128)(2,1)S(1)}, u32[]{:S(2)}, u32[]{:S(2)}) collective-permute-start(bf16[16,2432]{1,0:T(8,128)(2,1)S(1)} %get-tuple-element.21), channel_id=1, source_target_pairs={{0,2},{2,0},{4,6},{6,4},{8,10},{10,8},{12,14},{14,12},{1,3},{3,1},... | collective-permute-start | bytes 233480 | tf_op jit(solution)/shard_map/ppermute | solution.py:124
  55.0 9.1 %collective-permute-start.16 = (bf16[16,2432]{1,0:T(8,128)(2,1)S(1)}, bf16[16,2432]{1,0:T(8,128)(2,1)S(1)}, u32[]{:S(2)}, u32[]{:S(2)}) collective-permute-start(bf16[16,2432]{1,0:T(8,128)(2,1)S(1)} %get-tuple-element.17), channel_id=1, source_target_pairs={{0,14},{2,12},{4,10},{6,8},{8,6},{10,4},{12,2},{14,0},{1,15},{3,13... | collective-permute-start | bytes 233480 | tf_op jit(solution)/shard_map/ppermute | solution.py:124
  58.8 6.8 %collective-permute-start.17 = (bf16[16,2432]{1,0:T(8,128)(2,1)S(1)}, bf16[16,2432]{1,0:T(8,128)(2,1)S(1)}, u32[]{:S(2)}, u32[]{:S(2)}) collective-permute-start(bf16[16,2432]{1,0:T(8,128)(2,1)S(1)} %get-tuple-element.16), channel_id=1, source_target_pairs={{0,12},{2,14},{4,8},{6,10},{8,4},{10,6},{12,0},{14,2},{1,13},{3,15... | collective-permute-start | bytes 233480 | tf_op jit(solution)/shard_map/ppermute | solution.py:124
  59.5 10.9 %collective-permute-start.18 = (bf16[16,2432]{1,0:T(8,128)(2,1)S(1)}, bf16[16,2432]{1,0:T(8,128)(2,1)S(1)}, u32[]{:S(2)}, u32[]{:S(2)}) collective-permute-start(bf16[16,2432]{1,0:T(8,128)(2,1)S(1)} %get-tuple-element.15), channel_id=1, source_target_pairs={{0,10},{2,8},{4,14},{6,12},{8,2},{10,0},{12,6},{14,4},{1,11},{3,9}... | collective-permute-start | bytes 233480 | tf_op jit(solution)/shard_map/ppermute | solution.py:124
  59.9 11.3 %collective-permute-start.19 = (bf16[16,2432]{1,0:T(8,128)(2,1)S(1)}, bf16[16,2432]{1,0:T(8,128)(2,1)S(1)}, u32[]{:S(2)}, u32[]{:S(2)}) collective-permute-start(bf16[16,2432]{1,0:T(8,128)(2,1)S(1)} %get-tuple-element.14), channel_id=1, source_target_pairs={{0,8},{2,10},{4,12},{6,14},{8,0},{10,2},{12,4},{14,6},{1,9},{3,11}... | collective-permute-start | bytes 233480 | tf_op jit(solution)/shard_map/ppermute | solution.py:124
  62.7 8.5 %collective-permute-start.20 = (bf16[16,2432]{1,0:T(8,128)(2,1)S(1)}, bf16[16,2432]{1,0:T(8,128)(2,1)S(1)}, u32[]{:S(2)}, u32[]{:S(2)}) collective-permute-start(bf16[16,2432]{1,0:T(8,128)(2,1)S(1)} %get-tuple-element.18), channel_id=1, source_target_pairs={{0,6},{2,4},{4,2},{6,0},{8,14},{10,12},{12,10},{14,8},{1,7},{3,5},... | collective-permute-start | bytes 233480 | tf_op jit(solution)/shard_map/ppermute | solution.py:124
  64.1 7.4 %collective-permute-start.21 = (bf16[16,2432]{1,0:T(8,128)(2,1)S(1)}, bf16[16,2432]{1,0:T(8,128)(2,1)S(1)}, u32[]{:S(2)}, u32[]{:S(2)}) collective-permute-start(bf16[16,2432]{1,0:T(8,128)(2,1)S(1)} %get-tuple-element.19), channel_id=1, source_target_pairs={{0,4},{2,6},{4,0},{6,2},{8,12},{10,14},{12,8},{14,10},{1,5},{3,7},... | collective-permute-start | bytes 233480 | tf_op jit(solution)/shard_map/ppermute | solution.py:124
  65.7 5.8 %collective-permute-start.22 = (bf16[16,2432]{1,0:T(8,128)(2,1)S(1)}, bf16[16,2432]{1,0:T(8,128)(2,1)S(1)}, u32[]{:S(2)}, u32[]{:S(2)}) collective-permute-start(bf16[16,2432]{1,0:T(8,128)(2,1)S(1)} %get-tuple-element.13), channel_id=1, source_target_pairs={{0,2},{2,0},{4,6},{6,4},{8,10},{10,8},{12,14},{14,12},{1,3},{3,1},... | collective-permute-start | bytes 233480 | tf_op jit(solution)/shard_map/ppermute | solution.py:124
  72.7 1.5 %collective-permute-start.23 = (f32[128,384]{1,0:T(8,128)S(1)}, f32[128,384]{1,0:T(8,128)S(1)}, u32[]{:S(2)}, u32[]{:S(2)}) collective-permute-start(f32[128,384]{1,0:T(8,128)S(1)} %pad_maximum_fusion.2), channel_id=1, source_target_pairs={{0,1},{1,0},{2,3},{3,2},{4,5},{5,4},{6,7},{7,6},{8,9},{9,8},{10,11... | collective-permute-start | bytes 589832 | tf_op jit(solution)/shard_map/ppermute | solution.py:116
  75.0 9.3 %collective-permute-start.24 = (bf16[16,2432]{1,0:T(8,128)(2,1)S(1)}, bf16[16,2432]{1,0:T(8,128)(2,1)S(1)}, u32[]{:S(2)}, u32[]{:S(2)}) collective-permute-start(bf16[16,2432]{1,0:T(8,128)(2,1)S(1)} %get-tuple-element.7), channel_id=1, source_target_pairs={{0,14},{2,12},{4,10},{6,8},{8,6},{10,4},{12,2},{14,0},{1,15},{3,13... | collective-permute-start | bytes 233480 | tf_op jit(solution)/shard_map/ppermute | solution.py:124
  78.6 10.1 %collective-permute-start.25 = (bf16[16,2432]{1,0:T(8,128)(2,1)S(1)}, bf16[16,2432]{1,0:T(8,128)(2,1)S(1)}, u32[]{:S(2)}, u32[]{:S(2)}) collective-permute-start(bf16[16,2432]{1,0:T(8,128)(2,1)S(1)} %get-tuple-element.8), channel_id=1, source_target_pairs={{0,12},{2,14},{4,8},{6,10},{8,4},{10,6},{12,0},{14,2},{1,13},{3,15... | collective-permute-start | bytes 233480 | tf_op jit(solution)/shard_map/ppermute | solution.py:124
  79.2 13.2 %collective-permute-start.26 = (bf16[16,2432]{1,0:T(8,128)(2,1)S(1)}, bf16[16,2432]{1,0:T(8,128)(2,1)S(1)}, u32[]{:S(2)}, u32[]{:S(2)}) collective-permute-start(bf16[16,2432]{1,0:T(8,128)(2,1)S(1)} %get-tuple-element.9), channel_id=1, source_target_pairs={{0,10},{2,8},{4,14},{6,12},{8,2},{10,0},{12,6},{14,4},{1,11},{3,9}... | collective-permute-start | bytes 233480 | tf_op jit(solution)/shard_map/ppermute | solution.py:124
  80.9 12.0 %collective-permute-start.27 = (bf16[16,2432]{1,0:T(8,128)(2,1)S(1)}, bf16[16,2432]{1,0:T(8,128)(2,1)S(1)}, u32[]{:S(2)}, u32[]{:S(2)}) collective-permute-start(bf16[16,2432]{1,0:T(8,128)(2,1)S(1)} %get-tuple-element.10), channel_id=1, source_target_pairs={{0,8},{2,10},{4,12},{6,14},{8,0},{10,2},{12,4},{14,6},{1,9},{3,11}... | collective-permute-start | bytes 233480 | tf_op jit(solution)/shard_map/ppermute | solution.py:124
  82.9 9.9 %collective-permute-start.28 = (bf16[16,2432]{1,0:T(8,128)(2,1)S(1)}, bf16[16,2432]{1,0:T(8,128)(2,1)S(1)}, u32[]{:S(2)}, u32[]{:S(2)}) collective-permute-start(bf16[16,2432]{1,0:T(8,128)(2,1)S(1)} %get-tuple-element.11), channel_id=1, source_target_pairs={{0,6},{2,4},{4,2},{6,0},{8,14},{10,12},{12,10},{14,8},{1,7},{3,5},... | collective-permute-start | bytes 233480 | tf_op jit(solution)/shard_map/ppermute | solution.py:124
  84.3 9.3 %collective-permute-start.29 = (bf16[16,2432]{1,0:T(8,128)(2,1)S(1)}, bf16[16,2432]{1,0:T(8,128)(2,1)S(1)}, u32[]{:S(2)}, u32[]{:S(2)}) collective-permute-start(bf16[16,2432]{1,0:T(8,128)(2,1)S(1)} %get-tuple-element.12), channel_id=1, source_target_pairs={{0,4},{2,6},{4,0},{6,2},{8,12},{10,14},{12,8},{14,10},{1,5},{3,7},... | collective-permute-start | bytes 233480 | tf_op jit(solution)/shard_map/ppermute | solution.py:124
  88.8 4.8 %collective-permute-start.30 = (bf16[16,2432]{1,0:T(8,128)(2,1)S(1)}, bf16[16,2432]{1,0:T(8,128)(2,1)S(1)}, u32[]{:S(2)}, u32[]{:S(2)}) collective-permute-start(bf16[16,2432]{1,0:T(8,128)(2,1)S(1)} %get-tuple-element.6), channel_id=1, source_target_pairs={{0,2},{2,0},{4,6},{6,4},{8,10},{10,8},{12,14},{14,12},{1,3},{3,1},... | collective-permute-start | bytes 233480 | tf_op jit(solution)/shard_map/ppermute | solution.py:124
  93.8 1.4 %collective-permute-start.31 = (bf16[2,16,2304]{2,1,0:T(8,128)(2,1)S(1)}, bf16[2,16,2304]{2,1,0:T(8,128)(2,1)S(1)}, u32[]{:S(2)}, u32[]{:S(2)}) collective-permute-start(bf16[2,16,2304]{2,1,0:T(8,128)(2,1)S(1)} %pad_maximum_fusion.3), channel_id=1, source_target_pairs={{0,1},{1,0},{2,3},{3,2},{4,5},{5,4},{6,7},{7,6},{8,9},{9,8},{10,11... | collective-permute-start | bytes 442376 | tf_op jit(solution)/shard_map/ppermute | solution.py:116
  (9 other events, 67.8 us)

commit v21 on v19

--- a/solution.py
+++ b/solution.py
@@ -145,10 +145,10 @@
     sent = jnp.concatenate(
         [jnp.broadcast_to(g_half[None], (peers, rows, half)), placed], axis=-1
     )
+    if other_small is None:
+        other_small = swap_cores(small)
+        sent, other_small = lax.optimization_barrier((sent, other_small))
     got = exchange(sent, 1).reshape(peers * rows, half + block)
-    if other_small is None:
-        small, got = lax.optimization_barrier((small, got))
-        other_small = swap_cores(small)
     g_all = got[:, :half]
     code_all = got[:, half:]
 

time: 90.2 us -> 92 us (1.020)
  waiting for transfers between devices: 15.9 us -> 24.8 us
  starting transfers between devices: 55.8 us -> 48.5 us
  other arithmetic: 4.04 us -> 6.05 us
  local copies, waits for them, and re-layouts: 8.78 us -> 6.94 us
    ppermute x28, waiting for transfers between devices: 12.5 us -> 22 us  [exchange(): moved.append(lax.ppermute(parts[shift], 'dict', route))]
    ppermute x28, starting transfers between devices: 54.8 us -> 47.6 us  [exchange(): moved.append(lax.ppermute(parts[shift], 'dict', route))]
    unnamed x38 -> x36, local copies, waits for them, and re-layouts: 5.26 us -> 2.44 us
    concatenate x1, other arithmetic: 0.15 us -> 1.57 us  [split_device(): jnp.concatenate([lax.dynamic_slice_in_dim(decoder[0], theirs, half, axis=...]
  transfers between devices with their start and end apart: 33 -> 33, of which waited for: 14 -> 18; matrix products, arithmetic and copies ran while one was open for 10% -> 10% of each run, Pallas kernels for 0% -> 0%
where the time goes in v21:
time: 92 us; the launch traced here: 91.5 us
  starting transfers between devices  48.5 us (53%)
  waiting for transfers between devices  24.8 us (27%)
  local copies, waits for them, and re-layouts  6.94 us (8%)
  other arithmetic  6.05 us (7%)
  matrix products  4.18 us (5%)
  between operations  1.07 us (1%)
    ppermute x28, starting transfers between devices, exchange(): moved.append(lax.ppermute(parts[shift], 'dict', route))  47.6 us
    ppermute x28, waiting for transfers between devices, exchange(): moved.append(lax.ppermute(parts[shift], 'dict', route))  22 us
    ppermute x5, waiting for transfers between devices, swap_cores(): return lax.ppermute(block, 'section', [(0, 1), (1, 0)])  2.78 us
    unnamed x36, local copies, waits for them, and re-layouts  2.44 us
    dot_general x4, matrix products, with_dec(): lax.dot_general(g_all, dec, (((1,), (1,)), ((), ())), preferred_element_t...  2.16 us
  transfers between devices with their start and end apart: 33, of which 18 were waited for; matrix products, arithmetic and copies ran while one was open for 10% of the time, Pallas kernels for 0%

profile of v21, /device:TPU:0, one launch (start us, length us, event | category | flops | bytes accessed | tf_op | source)
XLA Modules:
  0.0 91.5 jit_solution(15251735506826490698)
XLA Ops:
  4.6 0.9 constant_dynamic-slice_fusion
  5.5 1.8 %dynamic-slice_bitcast_fusion = (bf16[256,2304]{1,0:T(8,128)(2,1)S(1)}, bf16[256,2304]{1,0:T(8,128)(2,1)S(1)}) fusion(bf16[1,256,4608]{2,1,0:T(8,128)(2,1)} %param.11, s32[]{:T(128)S(6)} %select_n.193, bf16[1,256,4608]{2,1,0:T(8,128)(2,1)} %param.10), kind=kLoop, calls=%fused_computation.42 | loop fusion | bytes 4718596 | tf_op jit(solution)/shard_map/dynamic_slice | solution.py:204
  8.0 5.5 %collective-permute-start.1 = (bf16[16,2432]{1,0:T(8,128)(2,1)}, bf16[16,2432]{1,0:T(8,128)(2,1)}, u32[]{:S(2)}, u32[]{:S(2)}) collective-permute-start(bf16[16,2432]{1,0:T(8,128)(2,1)} %get-tuple-element.38), channel_id=1, source_target_pairs={{0,14},{2,12},{4,10},{6,8},{8,6},{10,4},{12,2},{14,0},{1,15},{3,13... | collective-permute-start | bytes 233480 | tf_op jit(solution)/shard_map/ppermute | solution.py:124
  13.6 1.6 %pad_maximum_fusion = bf16[512,2304]{1,0:T(8,128)(2,1)} fusion(bf16[256,2304]{1,0:T(8,128)(2,1)S(1)} %get-tuple-element.46, bf16[256,2304]{1,0:T(8,128)(2,1)S(1)} %get-tuple-element.47), kind=kLoop, calls=%fused_computation.4 | loop fusion | flops 4718592 | bytes 4718592 | tf_op jit(solution)/shard_map/concatenate | solution.py:201
  16.3 2.2 %collective-permute-start.4 = (bf16[16,2432]{1,0:T(8,128)(2,1)S(1)}, bf16[16,2432]{1,0:T(8,128)(2,1)S(1)}, u32[]{:S(2)}, u32[]{:S(2)}) collective-permute-start(bf16[16,2432]{1,0:T(8,128)(2,1)S(1)} %get-tuple-element.35), channel_id=1, source_target_pairs={{0,8},{2,10},{4,12},{6,14},{8,0},{10,2},{12,4},{14,6},{1,9},{3,11}... | collective-permute-start | bytes 233480 | tf_op jit(solution)/shard_map/ppermute | solution.py:124
  18.6 2.1 %collective-permute-start.5 = (bf16[16,2432]{1,0:T(8,128)(2,1)S(1)}, bf16[16,2432]{1,0:T(8,128)(2,1)S(1)}, u32[]{:S(2)}, u32[]{:S(2)}) collective-permute-start(bf16[16,2432]{1,0:T(8,128)(2,1)S(1)} %get-tuple-element.34), channel_id=1, source_target_pairs={{0,6},{2,4},{4,2},{6,0},{8,14},{10,12},{12,10},{14,8},{1,7},{3,5},... | collective-permute-start | bytes 233480 | tf_op jit(solution)/shard_map/ppermute | solution.py:124
  21.5 0.9 collective-permute-done.2
  22.4 1.8 %collective-permute-start.6 = (bf16[16,2432]{1,0:T(8,128)(2,1)S(1)}, bf16[16,2432]{1,0:T(8,128)(2,1)S(1)}, u32[]{:S(2)}, u32[]{:S(2)}) collective-permute-start(bf16[16,2432]{1,0:T(8,128)(2,1)S(1)} %get-tuple-element.33), channel_id=1, source_target_pairs={{0,4},{2,6},{4,0},{6,2},{8,12},{10,14},{12,8},{14,10},{1,5},{3,7},... | collective-permute-start | bytes 233480 | tf_op jit(solution)/shard_map/ppermute | solution.py:124
  24.3 2.5 %collective-permute-done.3 = bf16[16,2432]{1,0:T(8,128)(2,1)S(1)} collective-permute-done((bf16[16,2432]{1,0:T(8,128)(2,1)S(1)}, bf16[16,2432]{1,0:T(8,128)(2,1)S(1)}, u32[]{:S(2)}, u32[]{:S(2)}) %collective-permute-start.3) | collective-permute-done | bytes 77856 | tf_op jit(solution)/shard_map/ppermute | solution.py:124
  26.8 1.5 %collective-permute-start.7 = (bf16[16,2432]{1,0:T(8,128)(2,1)S(1)}, bf16[16,2432]{1,0:T(8,128)(2,1)S(1)}, u32[]{:S(2)}, u32[]{:S(2)}) collective-permute-start(bf16[16,2432]{1,0:T(8,128)(2,1)S(1)} %get-tuple-element.32), channel_id=1, source_target_pairs={{0,2},{2,0},{4,6},{6,4},{8,10},{10,8},{12,14},{14,12},{1,3},{3,1},... | collective-permute-start | bytes 233480 | tf_op jit(solution)/shard_map/ppermute | solution.py:124
  28.9 2.4 %collective-permute-done.7 = bf16[16,2432]{1,0:T(8,128)(2,1)S(1)} collective-permute-done((bf16[16,2432]{1,0:T(8,128)(2,1)S(1)}, bf16[16,2432]{1,0:T(8,128)(2,1)S(1)}, u32[]{:S(2)}, u32[]{:S(2)}) %collective-permute-start.7) | collective-permute-done | bytes 77856 | tf_op jit(solution)/shard_map/ppermute | solution.py:124
  31.8 1.1 %copy-done = bf16[1,256,4608]{2,1,0:T(8,128)(2,1)S(1)} copy-done((bf16[1,256,4608]{2,1,0:T(8,128)(2,1)S(1)}, bf16[1,256,4608]{2,1,0:T(8,128)(2,1)}, u32[]{:S(2)}) %copy-start) | copy-done | bytes 2359320
  33.7 1.3 %collective-permute-done.9 = f32[128,384]{1,0:T(8,128)S(1)} collective-permute-done((f32[128,384]{1,0:T(8,128)S(1)}, f32[128,384]{1,0:T(8,128)S(1)}, u32[]{:S(2)}, u32[]{:S(2)}) %collective-permute-start.9) | collective-permute-done | bytes 196640 | tf_op jit(solution)/shard_map/ppermute | solution.py:116
  35.8 3.0 %collective-permute-start.10 = (bf16[16,2432]{1,0:T(8,128)(2,1)S(1)}, bf16[16,2432]{1,0:T(8,128)(2,1)S(1)}, u32[]{:S(2)}, u32[]{:S(2)}) collective-permute-start(bf16[16,2432]{1,0:T(8,128)(2,1)S(1)} %get-tuple-element.26), channel_id=1, source_target_pairs={{0,14},{2,12},{4,10},{6,8},{8,6},{10,4},{12,2},{14,0},{1,15},{3,13... | collective-permute-start | bytes 233480 | tf_op jit(solution)/shard_map/ppermute | solution.py:124
  38.8 1.8 %collective-permute-start.11 = (bf16[16,2432]{1,0:T(8,128)(2,1)S(1)}, bf16[16,2432]{1,0:T(8,128)(2,1)S(1)}, u32[]{:S(2)}, u32[]{:S(2)}) collective-permute-start(bf16[16,2432]{1,0:T(8,128)(2,1)S(1)} %get-tuple-element.27), channel_id=1, source_target_pairs={{0,12},{2,14},{4,8},{6,10},{8,4},{10,6},{12,0},{14,2},{1,13},{3,15... | collective-permute-start | bytes 233480 | tf_op jit(solution)/shard_map/ppermute | solution.py:124
  40.6 2.9 %collective-permute-start.13 = (bf16[16,2432]{1,0:T(8,128)(2,1)S(1)}, bf16[16,2432]{1,0:T(8,128)(2,1)S(1)}, u32[]{:S(2)}, u32[]{:S(2)}) collective-permute-start(bf16[16,2432]{1,0:T(8,128)(2,1)S(1)} %get-tuple-element.29), channel_id=1, source_target_pairs={{0,8},{2,10},{4,12},{6,14},{8,0},{10,2},{12,4},{14,6},{1,9},{3,11}... | collective-permute-start | bytes 233480 | tf_op jit(solution)/shard_map/ppermute | solution.py:124
  44.1 2.4 %collective-permute-start.15 = (bf16[16,2432]{1,0:T(8,128)(2,1)S(1)}, bf16[16,2432]{1,0:T(8,128)(2,1)S(1)}, u32[]{:S(2)}, u32[]{:S(2)}) collective-permute-start(bf16[16,2432]{1,0:T(8,128)(2,1)S(1)} %get-tuple-element.31), channel_id=1, source_target_pairs={{0,4},{2,6},{4,0},{6,2},{8,12},{10,14},{12,8},{14,10},{1,5},{3,7},... | collective-permute-start | bytes 233480 | tf_op jit(solution)/shard_map/ppermute | solution.py:124
  47.1 2.9 %collective-permute-done.12 = bf16[16,2432]{1,0:T(8,128)(2,1)S(1)} collective-permute-done((bf16[16,2432]{1,0:T(8,128)(2,1)S(1)}, bf16[16,2432]{1,0:T(8,128)(2,1)S(1)}, u32[]{:S(2)}, u32[]{:S(2)}) %collective-permute-start.12) | collective-permute-done | bytes 77856 | tf_op jit(solution)/shard_map/ppermute | solution.py:124
  50.0 1.7 %collective-permute-done.13 = bf16[16,2432]{1,0:T(8,128)(2,1)S(1)} collective-permute-done((bf16[16,2432]{1,0:T(8,128)(2,1)S(1)}, bf16[16,2432]{1,0:T(8,128)(2,1)S(1)}, u32[]{:S(2)}, u32[]{:S(2)}) %collective-permute-start.13) | collective-permute-done | bytes 77856 | tf_op jit(solution)/shard_map/ppermute | solution.py:124
  53.2 2.2 %collective-permute-start.17 = (bf16[16,2432]{1,0:T(8,128)(2,1)S(1)}, bf16[16,2432]{1,0:T(8,128)(2,1)S(1)}, u32[]{:S(2)}, u32[]{:S(2)}) collective-permute-start(bf16[16,2432]{1,0:T(8,128)(2,1)S(1)} %get-tuple-element.20), channel_id=1, source_target_pairs={{0,14},{2,12},{4,10},{6,8},{8,6},{10,4},{12,2},{14,0},{1,15},{3,13... | collective-permute-start | bytes 233480 | tf_op jit(solution)/shard_map/ppermute | solution.py:124
  55.3 1.8 %collective-permute-start.18 = (bf16[16,2432]{1,0:T(8,128)(2,1)S(1)}, bf16[16,2432]{1,0:T(8,128)(2,1)S(1)}, u32[]{:S(2)}, u32[]{:S(2)}) collective-permute-start(bf16[16,2432]{1,0:T(8,128)(2,1)S(1)} %get-tuple-element.21), channel_id=1, source_target_pairs={{0,12},{2,14},{4,8},{6,10},{8,4},{10,6},{12,0},{14,2},{1,13},{3,15... | collective-permute-start | bytes 233480 | tf_op jit(solution)/shard_map/ppermute | solution.py:124
  57.1 3.7 %collective-permute-start.20 = (bf16[16,2432]{1,0:T(8,128)(2,1)S(1)}, bf16[16,2432]{1,0:T(8,128)(2,1)S(1)}, u32[]{:S(2)}, u32[]{:S(2)}) collective-permute-start(bf16[16,2432]{1,0:T(8,128)(2,1)S(1)} %get-tuple-element.23), channel_id=1, source_target_pairs={{0,8},{2,10},{4,12},{6,14},{8,0},{10,2},{12,4},{14,6},{1,9},{3,11}... | collective-permute-start | bytes 233480 | tf_op jit(solution)/shard_map/ppermute | solution.py:124
  61.2 1.8 %collective-permute-start.22 = (bf16[16,2432]{1,0:T(8,128)(2,1)S(1)}, bf16[16,2432]{1,0:T(8,128)(2,1)S(1)}, u32[]{:S(2)}, u32[]{:S(2)}) collective-permute-start(bf16[16,2432]{1,0:T(8,128)(2,1)S(1)} %get-tuple-element.18), channel_id=1, source_target_pairs={{0,4},{2,6},{4,0},{6,2},{8,12},{10,14},{12,8},{14,10},{1,5},{3,7},... | collective-permute-start | bytes 233480 | tf_op jit(solution)/shard_map/ppermute | solution.py:124
  63.0 1.4 %collective-permute-start.23 = (bf16[16,2432]{1,0:T(8,128)(2,1)S(1)}, bf16[16,2432]{1,0:T(8,128)(2,1)S(1)}, u32[]{:S(2)}, u32[]{:S(2)}) collective-permute-start(bf16[16,2432]{1,0:T(8,128)(2,1)S(1)} %get-tuple-element.17), channel_id=1, source_target_pairs={{0,2},{2,0},{4,6},{6,4},{8,10},{10,8},{12,14},{14,12},{1,3},{3,1},... | collective-permute-start | bytes 233480 | tf_op jit(solution)/shard_map/ppermute | solution.py:124
  64.5 2.3 %collective-permute-done.19 = bf16[16,2432]{1,0:T(8,128)(2,1)S(1)} collective-permute-done((bf16[16,2432]{1,0:T(8,128)(2,1)S(1)}, bf16[16,2432]{1,0:T(8,128)(2,1)S(1)}, u32[]{:S(2)}, u32[]{:S(2)}) %collective-permute-start.19) | collective-permute-done | bytes 77856 | tf_op jit(solution)/shard_map/ppermute | solution.py:124
  70.1 1.2 %collective-permute-done.24 = f32[128,384]{1,0:T(8,128)S(1)} collective-permute-done((f32[128,384]{1,0:T(8,128)S(1)}, f32[128,384]{1,0:T(8,128)S(1)}, u32[]{:S(2)}, u32[]{:S(2)}) %collective-permute-start.24) | collective-permute-done | bytes 196640 | tf_op jit(solution)/shard_map/ppermute | solution.py:116
  72.1 3.0 %collective-permute-start.25 = (bf16[16,2432]{1,0:T(8,128)(2,1)S(1)}, bf16[16,2432]{1,0:T(8,128)(2,1)S(1)}, u32[]{:S(2)}, u32[]{:S(2)}) collective-permute-start(bf16[16,2432]{1,0:T(8,128)(2,1)S(1)} %get-tuple-element.11), channel_id=1, source_target_pairs={{0,14},{2,12},{4,10},{6,8},{8,6},{10,4},{12,2},{14,0},{1,15},{3,13... | collective-permute-start | bytes 233480 | tf_op jit(solution)/shard_map/ppermute | solution.py:124
  75.1 1.7 %collective-permute-start.26 = (bf16[16,2432]{1,0:T(8,128)(2,1)S(1)}, bf16[16,2432]{1,0:T(8,128)(2,1)S(1)}, u32[]{:S(2)}, u32[]{:S(2)}) collective-permute-start(bf16[16,2432]{1,0:T(8,128)(2,1)S(1)} %get-tuple-element.12), channel_id=1, source_target_pairs={{0,12},{2,14},{4,8},{6,10},{8,4},{10,6},{12,0},{14,2},{1,13},{3,15... | collective-permute-start | bytes 233480 | tf_op jit(solution)/shard_map/ppermute | solution.py:124
  76.8 3.0 %collective-permute-start.28 = (bf16[16,2432]{1,0:T(8,128)(2,1)S(1)}, bf16[16,2432]{1,0:T(8,128)(2,1)S(1)}, u32[]{:S(2)}, u32[]{:S(2)}) collective-permute-start(bf16[16,2432]{1,0:T(8,128)(2,1)S(1)} %get-tuple-element.14), channel_id=1, source_target_pairs={{0,8},{2,10},{4,12},{6,14},{8,0},{10,2},{12,4},{14,6},{1,9},{3,11}... | collective-permute-start | bytes 233480 | tf_op jit(solution)/shard_map/ppermute | solution.py:124
  80.4 2.3 %collective-permute-start.30 = (bf16[16,2432]{1,0:T(8,128)(2,1)S(1)}, bf16[16,2432]{1,0:T(8,128)(2,1)S(1)}, u32[]{:S(2)}, u32[]{:S(2)}) collective-permute-start(bf16[16,2432]{1,0:T(8,128)(2,1)S(1)} %get-tuple-element.16), channel_id=1, source_target_pairs={{0,4},{2,6},{4,0},{6,2},{8,12},{10,14},{12,8},{14,10},{1,5},{3,7},... | collective-permute-start | bytes 233480 | tf_op jit(solution)/shard_map/ppermute | solution.py:124
  83.4 4.1 %collective-permute-done.27 = bf16[16,2432]{1,0:T(8,128)(2,1)S(1)} collective-permute-done((bf16[16,2432]{1,0:T(8,128)(2,1)S(1)}, bf16[16,2432]{1,0:T(8,128)(2,1)S(1)}, u32[]{:S(2)}, u32[]{:S(2)}) %collective-permute-start.27) | collective-permute-done | bytes 77856 | tf_op jit(solution)/shard_map/ppermute | solution.py:124
  88.1 0.9 %collective-permute-done.30 = bf16[16,2432]{1,0:T(8,128)(2,1)S(1)} collective-permute-done((bf16[16,2432]{1,0:T(8,128)(2,1)S(1)}, bf16[16,2432]{1,0:T(8,128)(2,1)S(1)}, u32[]{:S(2)}, u32[]{:S(2)}) %collective-permute-start.30) | collective-permute-done | bytes 77856 | tf_op jit(solution)/shard_map/ppermute | solution.py:124
  (131 shorter events, 20.7 us)
Async XLA Ops:
  2.1 5.3 %collective-permute-start = (f32[4624]{0:T(1024)S(1)}, f32[4624]{0:T(1024)S(1)}, u32[]{:S(2)}, u32[]{:S(2)}) collective-permute-start(f32[4624]{0:T(1024)S(1)} %pad_maximum_fusion.8), channel_id=1, source_target_pairs={{0,1},{1,0},{2,3},{3,2},{4,5},{5,4},{6,7},{7,6},{8,9},{9,8},{10,11... | collective-permute-start | bytes 55496 | tf_op jit(solution)/shard_map/ppermute | solution.py:116
  8.0 10.5 %collective-permute-start.1 = (bf16[16,2432]{1,0:T(8,128)(2,1)}, bf16[16,2432]{1,0:T(8,128)(2,1)}, u32[]{:S(2)}, u32[]{:S(2)}) collective-permute-start(bf16[16,2432]{1,0:T(8,128)(2,1)} %get-tuple-element.38), channel_id=1, source_target_pairs={{0,14},{2,12},{4,10},{6,8},{8,6},{10,4},{12,2},{14,0},{1,15},{3,13... | collective-permute-start | bytes 233480 | tf_op jit(solution)/shard_map/ppermute | solution.py:124
  15.1 16.2 %collective-permute-start.8 = (bf16[512,2304]{1,0:T(8,128)(2,1)}, bf16[512,2304]{1,0:T(8,128)(2,1)S(1)}, u32[]{:S(2)}, u32[]{:S(2)}) collective-permute-start(bf16[512,2304]{1,0:T(8,128)(2,1)} %pad_maximum_fusion), channel_id=1, source_target_pairs={{0,1},{1,0},{2,3},{3,2},{4,5},{5,4},{6,7},{7,6},{8,9},{9,8},{10,11... | collective-permute-start | bytes 7077896 | tf_op jit(solution)/shard_map/ppermute | solution.py:116
  15.4 7.1 %collective-permute-start.2 = (bf16[16,2432]{1,0:T(8,128)(2,1)S(1)}, bf16[16,2432]{1,0:T(8,128)(2,1)S(1)}, u32[]{:S(2)}, u32[]{:S(2)}) collective-permute-start(bf16[16,2432]{1,0:T(8,128)(2,1)S(1)} %get-tuple-element.37), channel_id=1, source_target_pairs={{0,12},{2,14},{4,8},{6,10},{8,4},{10,6},{12,0},{14,2},{1,13},{3,15... | collective-permute-start | bytes 233480 | tf_op jit(solution)/shard_map/ppermute | solution.py:124
  15.6 11.3 %collective-permute-start.3 = (bf16[16,2432]{1,0:T(8,128)(2,1)S(1)}, bf16[16,2432]{1,0:T(8,128)(2,1)S(1)}, u32[]{:S(2)}, u32[]{:S(2)}) collective-permute-start(bf16[16,2432]{1,0:T(8,128)(2,1)S(1)} %get-tuple-element.36), channel_id=1, source_target_pairs={{0,10},{2,8},{4,14},{6,12},{8,2},{10,0},{12,6},{14,4},{1,11},{3,9}... | collective-permute-start | bytes 233480 | tf_op jit(solution)/shard_map/ppermute | solution.py:124
  16.3 12.0 %collective-permute-start.4 = (bf16[16,2432]{1,0:T(8,128)(2,1)S(1)}, bf16[16,2432]{1,0:T(8,128)(2,1)S(1)}, u32[]{:S(2)}, u32[]{:S(2)}) collective-permute-start(bf16[16,2432]{1,0:T(8,128)(2,1)S(1)} %get-tuple-element.35), channel_id=1, source_target_pairs={{0,8},{2,10},{4,12},{6,14},{8,0},{10,2},{12,4},{14,6},{1,9},{3,11}... | collective-permute-start | bytes 233480 | tf_op jit(solution)/shard_map/ppermute | solution.py:124
  18.6 9.8 %collective-permute-start.5 = (bf16[16,2432]{1,0:T(8,128)(2,1)S(1)}, bf16[16,2432]{1,0:T(8,128)(2,1)S(1)}, u32[]{:S(2)}, u32[]{:S(2)}) collective-permute-start(bf16[16,2432]{1,0:T(8,128)(2,1)S(1)} %get-tuple-element.34), channel_id=1, source_target_pairs={{0,6},{2,4},{4,2},{6,0},{8,14},{10,12},{12,10},{14,8},{1,7},{3,5},... | collective-permute-start | bytes 233480 | tf_op jit(solution)/shard_map/ppermute | solution.py:124
  22.4 6.4 %collective-permute-start.6 = (bf16[16,2432]{1,0:T(8,128)(2,1)S(1)}, bf16[16,2432]{1,0:T(8,128)(2,1)S(1)}, u32[]{:S(2)}, u32[]{:S(2)}) collective-permute-start(bf16[16,2432]{1,0:T(8,128)(2,1)S(1)} %get-tuple-element.33), channel_id=1, source_target_pairs={{0,4},{2,6},{4,0},{6,2},{8,12},{10,14},{12,8},{14,10},{1,5},{3,7},... | collective-permute-start | bytes 233480 | tf_op jit(solution)/shard_map/ppermute | solution.py:124
  26.8 4.4 %collective-permute-start.7 = (bf16[16,2432]{1,0:T(8,128)(2,1)S(1)}, bf16[16,2432]{1,0:T(8,128)(2,1)S(1)}, u32[]{:S(2)}, u32[]{:S(2)}) collective-permute-start(bf16[16,2432]{1,0:T(8,128)(2,1)S(1)} %get-tuple-element.32), channel_id=1, source_target_pairs={{0,2},{2,0},{4,6},{6,4},{8,10},{10,8},{12,14},{14,12},{1,3},{3,1},... | collective-permute-start | bytes 233480 | tf_op jit(solution)/shard_map/ppermute | solution.py:124
  33.5 1.5 %collective-permute-start.9 = (f32[128,384]{1,0:T(8,128)S(1)}, f32[128,384]{1,0:T(8,128)S(1)}, u32[]{:S(2)}, u32[]{:S(2)}) collective-permute-start(f32[128,384]{1,0:T(8,128)S(1)} %pad_maximum_fusion.2), channel_id=1, source_target_pairs={{0,1},{1,0},{2,3},{3,2},{4,5},{5,4},{6,7},{7,6},{8,9},{9,8},{10,11... | collective-permute-start | bytes 589832 | tf_op jit(solution)/shard_map/ppermute | solution.py:116
  35.8 8.3 %collective-permute-start.10 = (bf16[16,2432]{1,0:T(8,128)(2,1)S(1)}, bf16[16,2432]{1,0:T(8,128)(2,1)S(1)}, u32[]{:S(2)}, u32[]{:S(2)}) collective-permute-start(bf16[16,2432]{1,0:T(8,128)(2,1)S(1)} %get-tuple-element.26), channel_id=1, source_target_pairs={{0,14},{2,12},{4,10},{6,8},{8,6},{10,4},{12,2},{14,0},{1,15},{3,13... | collective-permute-start | bytes 233480 | tf_op jit(solution)/shard_map/ppermute | solution.py:124
  38.8 7.7 %collective-permute-start.11 = (bf16[16,2432]{1,0:T(8,128)(2,1)S(1)}, bf16[16,2432]{1,0:T(8,128)(2,1)S(1)}, u32[]{:S(2)}, u32[]{:S(2)}) collective-permute-start(bf16[16,2432]{1,0:T(8,128)(2,1)S(1)} %get-tuple-element.27), channel_id=1, source_target_pairs={{0,12},{2,14},{4,8},{6,10},{8,4},{10,6},{12,0},{14,2},{1,13},{3,15... | collective-permute-start | bytes 233480 | tf_op jit(solution)/shard_map/ppermute | solution.py:124
  40.6 9.4 %collective-permute-start.12 = (bf16[16,2432]{1,0:T(8,128)(2,1)S(1)}, bf16[16,2432]{1,0:T(8,128)(2,1)S(1)}, u32[]{:S(2)}, u32[]{:S(2)}) collective-permute-start(bf16[16,2432]{1,0:T(8,128)(2,1)S(1)} %get-tuple-element.28), channel_id=1, source_target_pairs={{0,10},{2,8},{4,14},{6,12},{8,2},{10,0},{12,6},{14,4},{1,11},{3,9}... | collective-permute-start | bytes 233480 | tf_op jit(solution)/shard_map/ppermute | solution.py:124
  40.6 11.0 %collective-permute-start.13 = (bf16[16,2432]{1,0:T(8,128)(2,1)S(1)}, bf16[16,2432]{1,0:T(8,128)(2,1)S(1)}, u32[]{:S(2)}, u32[]{:S(2)}) collective-permute-start(bf16[16,2432]{1,0:T(8,128)(2,1)S(1)} %get-tuple-element.29), channel_id=1, source_target_pairs={{0,8},{2,10},{4,12},{6,14},{8,0},{10,2},{12,4},{14,6},{1,9},{3,11}... | collective-permute-start | bytes 233480 | tf_op jit(solution)/shard_map/ppermute | solution.py:124
  43.5 8.5 %collective-permute-start.14 = (bf16[16,2432]{1,0:T(8,128)(2,1)S(1)}, bf16[16,2432]{1,0:T(8,128)(2,1)S(1)}, u32[]{:S(2)}, u32[]{:S(2)}) collective-permute-start(bf16[16,2432]{1,0:T(8,128)(2,1)S(1)} %get-tuple-element.30), channel_id=1, source_target_pairs={{0,6},{2,4},{4,2},{6,0},{8,14},{10,12},{12,10},{14,8},{1,7},{3,5},... | collective-permute-start | bytes 233480 | tf_op jit(solution)/shard_map/ppermute | solution.py:124
  44.1 8.7 %collective-permute-start.15 = (bf16[16,2432]{1,0:T(8,128)(2,1)S(1)}, bf16[16,2432]{1,0:T(8,128)(2,1)S(1)}, u32[]{:S(2)}, u32[]{:S(2)}) collective-permute-start(bf16[16,2432]{1,0:T(8,128)(2,1)S(1)} %get-tuple-element.31), channel_id=1, source_target_pairs={{0,4},{2,6},{4,0},{6,2},{8,12},{10,14},{12,8},{14,10},{1,5},{3,7},... | collective-permute-start | bytes 233480 | tf_op jit(solution)/shard_map/ppermute | solution.py:124
  46.5 6.3 %collective-permute-start.16 = (bf16[16,2432]{1,0:T(8,128)(2,1)S(1)}, bf16[16,2432]{1,0:T(8,128)(2,1)S(1)}, u32[]{:S(2)}, u32[]{:S(2)}) collective-permute-start(bf16[16,2432]{1,0:T(8,128)(2,1)S(1)} %get-tuple-element.25), channel_id=1, source_target_pairs={{0,2},{2,0},{4,6},{6,4},{8,10},{10,8},{12,14},{14,12},{1,3},{3,1},... | collective-permute-start | bytes 233480 | tf_op jit(solution)/shard_map/ppermute | solution.py:124
  53.2 8.0 %collective-permute-start.17 = (bf16[16,2432]{1,0:T(8,128)(2,1)S(1)}, bf16[16,2432]{1,0:T(8,128)(2,1)S(1)}, u32[]{:S(2)}, u32[]{:S(2)}) collective-permute-start(bf16[16,2432]{1,0:T(8,128)(2,1)S(1)} %get-tuple-element.20), channel_id=1, source_target_pairs={{0,14},{2,12},{4,10},{6,8},{8,6},{10,4},{12,2},{14,0},{1,15},{3,13... | collective-permute-start | bytes 233480 | tf_op jit(solution)/shard_map/ppermute | solution.py:124
  55.3 7.7 %collective-permute-start.18 = (bf16[16,2432]{1,0:T(8,128)(2,1)S(1)}, bf16[16,2432]{1,0:T(8,128)(2,1)S(1)}, u32[]{:S(2)}, u32[]{:S(2)}) collective-permute-start(bf16[16,2432]{1,0:T(8,128)(2,1)S(1)} %get-tuple-element.21), channel_id=1, source_target_pairs={{0,12},{2,14},{4,8},{6,10},{8,4},{10,6},{12,0},{14,2},{1,13},{3,15... | collective-permute-start | bytes 233480 | tf_op jit(solution)/shard_map/ppermute | solution.py:124
  57.1 9.6 %collective-permute-start.19 = (bf16[16,2432]{1,0:T(8,128)(2,1)S(1)}, bf16[16,2432]{1,0:T(8,128)(2,1)S(1)}, u32[]{:S(2)}, u32[]{:S(2)}) collective-permute-start(bf16[16,2432]{1,0:T(8,128)(2,1)S(1)} %get-tuple-element.22), channel_id=1, source_target_pairs={{0,10},{2,8},{4,14},{6,12},{8,2},{10,0},{12,6},{14,4},{1,11},{3,9}... | collective-permute-start | bytes 233480 | tf_op jit(solution)/shard_map/ppermute | solution.py:124
  57.1 10.5 %collective-permute-start.20 = (bf16[16,2432]{1,0:T(8,128)(2,1)S(1)}, bf16[16,2432]{1,0:T(8,128)(2,1)S(1)}, u32[]{:S(2)}, u32[]{:S(2)}) collective-permute-start(bf16[16,2432]{1,0:T(8,128)(2,1)S(1)} %get-tuple-element.23), channel_id=1, source_target_pairs={{0,8},{2,10},{4,12},{6,14},{8,0},{10,2},{12,4},{14,6},{1,9},{3,11}... | collective-permute-start | bytes 233480 | tf_op jit(solution)/shard_map/ppermute | solution.py:124
  60.9 7.7 %collective-permute-start.21 = (bf16[16,2432]{1,0:T(8,128)(2,1)S(1)}, bf16[16,2432]{1,0:T(8,128)(2,1)S(1)}, u32[]{:S(2)}, u32[]{:S(2)}) collective-permute-start(bf16[16,2432]{1,0:T(8,128)(2,1)S(1)} %get-tuple-element.24), channel_id=1, source_target_pairs={{0,6},{2,4},{4,2},{6,0},{8,14},{10,12},{12,10},{14,8},{1,7},{3,5},... | collective-permute-start | bytes 233480 | tf_op jit(solution)/shard_map/ppermute | solution.py:124
  61.2 7.4 %collective-permute-start.22 = (bf16[16,2432]{1,0:T(8,128)(2,1)S(1)}, bf16[16,2432]{1,0:T(8,128)(2,1)S(1)}, u32[]{:S(2)}, u32[]{:S(2)}) collective-permute-start(bf16[16,2432]{1,0:T(8,128)(2,1)S(1)} %get-tuple-element.18), channel_id=1, source_target_pairs={{0,4},{2,6},{4,0},{6,2},{8,12},{10,14},{12,8},{14,10},{1,5},{3,7},... | collective-permute-start | bytes 233480 | tf_op jit(solution)/shard_map/ppermute | solution.py:124
  63.0 5.6 %collective-permute-start.23 = (bf16[16,2432]{1,0:T(8,128)(2,1)S(1)}, bf16[16,2432]{1,0:T(8,128)(2,1)S(1)}, u32[]{:S(2)}, u32[]{:S(2)}) collective-permute-start(bf16[16,2432]{1,0:T(8,128)(2,1)S(1)} %get-tuple-element.17), channel_id=1, source_target_pairs={{0,2},{2,0},{4,6},{6,4},{8,10},{10,8},{12,14},{14,12},{1,3},{3,1},... | collective-permute-start | bytes 233480 | tf_op jit(solution)/shard_map/ppermute | solution.py:124
  69.8 1.5 %collective-permute-start.24 = (f32[128,384]{1,0:T(8,128)S(1)}, f32[128,384]{1,0:T(8,128)S(1)}, u32[]{:S(2)}, u32[]{:S(2)}) collective-permute-start(f32[128,384]{1,0:T(8,128)S(1)} %pad_maximum_fusion.3), channel_id=1, source_target_pairs={{0,1},{1,0},{2,3},{3,2},{4,5},{5,4},{6,7},{7,6},{8,9},{9,8},{10,11... | collective-permute-start | bytes 589832 | tf_op jit(solution)/shard_map/ppermute | solution.py:116
  72.1 8.3 %collective-permute-start.25 = (bf16[16,2432]{1,0:T(8,128)(2,1)S(1)}, bf16[16,2432]{1,0:T(8,128)(2,1)S(1)}, u32[]{:S(2)}, u32[]{:S(2)}) collective-permute-start(bf16[16,2432]{1,0:T(8,128)(2,1)S(1)} %get-tuple-element.11), channel_id=1, source_target_pairs={{0,14},{2,12},{4,10},{6,8},{8,6},{10,4},{12,2},{14,0},{1,15},{3,13... | collective-permute-start | bytes 233480 | tf_op jit(solution)/shard_map/ppermute | solution.py:124
  75.1 7.6 %collective-permute-start.26 = (bf16[16,2432]{1,0:T(8,128)(2,1)S(1)}, bf16[16,2432]{1,0:T(8,128)(2,1)S(1)}, u32[]{:S(2)}, u32[]{:S(2)}) collective-permute-start(bf16[16,2432]{1,0:T(8,128)(2,1)S(1)} %get-tuple-element.12), channel_id=1, source_target_pairs={{0,12},{2,14},{4,8},{6,10},{8,4},{10,6},{12,0},{14,2},{1,13},{3,15... | collective-permute-start | bytes 233480 | tf_op jit(solution)/shard_map/ppermute | solution.py:124
  76.8 10.7 %collective-permute-start.27 = (bf16[16,2432]{1,0:T(8,128)(2,1)S(1)}, bf16[16,2432]{1,0:T(8,128)(2,1)S(1)}, u32[]{:S(2)}, u32[]{:S(2)}) collective-permute-start(bf16[16,2432]{1,0:T(8,128)(2,1)S(1)} %get-tuple-element.13), channel_id=1, source_target_pairs={{0,10},{2,8},{4,14},{6,12},{8,2},{10,0},{12,6},{14,4},{1,11},{3,9}... | collective-permute-start | bytes 233480 | tf_op jit(solution)/shard_map/ppermute | solution.py:124
  76.8 11.3 %collective-permute-start.28 = (bf16[16,2432]{1,0:T(8,128)(2,1)S(1)}, bf16[16,2432]{1,0:T(8,128)(2,1)S(1)}, u32[]{:S(2)}, u32[]{:S(2)}) collective-permute-start(bf16[16,2432]{1,0:T(8,128)(2,1)S(1)} %get-tuple-element.14), channel_id=1, source_target_pairs={{0,8},{2,10},{4,12},{6,14},{8,0},{10,2},{12,4},{14,6},{1,9},{3,11}... | collective-permute-start | bytes 233480 | tf_op jit(solution)/shard_map/ppermute | solution.py:124
  79.8 8.3 %collective-permute-start.29 = (bf16[16,2432]{1,0:T(8,128)(2,1)S(1)}, bf16[16,2432]{1,0:T(8,128)(2,1)S(1)}, u32[]{:S(2)}, u32[]{:S(2)}) collective-permute-start(bf16[16,2432]{1,0:T(8,128)(2,1)S(1)} %get-tuple-element.15), channel_id=1, source_target_pairs={{0,6},{2,4},{4,2},{6,0},{8,14},{10,12},{12,10},{14,8},{1,7},{3,5},... | collective-permute-start | bytes 233480 | tf_op jit(solution)/shard_map/ppermute | solution.py:124
  80.4 8.7 %collective-permute-start.30 = (bf16[16,2432]{1,0:T(8,128)(2,1)S(1)}, bf16[16,2432]{1,0:T(8,128)(2,1)S(1)}, u32[]{:S(2)}, u32[]{:S(2)}) collective-permute-start(bf16[16,2432]{1,0:T(8,128)(2,1)S(1)} %get-tuple-element.16), channel_id=1, source_target_pairs={{0,4},{2,6},{4,0},{6,2},{8,12},{10,14},{12,8},{14,10},{1,5},{3,7},... | collective-permute-start | bytes 233480 | tf_op jit(solution)/shard_map/ppermute | solution.py:124
  82.6 6.4 %collective-permute-start.31 = (bf16[16,2432]{1,0:T(8,128)(2,1)S(1)}, bf16[16,2432]{1,0:T(8,128)(2,1)S(1)}, u32[]{:S(2)}, u32[]{:S(2)}) collective-permute-start(bf16[16,2432]{1,0:T(8,128)(2,1)S(1)} %get-tuple-element.10), channel_id=1, source_target_pairs={{0,2},{2,0},{4,6},{6,4},{8,10},{10,8},{12,14},{14,12},{1,3},{3,1},... | collective-permute-start | bytes 233480 | tf_op jit(solution)/shard_map/ppermute | solution.py:124
  (6 other events, 23.5 us)

commit v22 on v19

--- a/solution.py
+++ b/solution.py
@@ -125,7 +125,7 @@
     return jnp.stack(moved, axis=0)
 
 
-def split_layer(g_half, routes_l, acts_l, own, other, is_own, small, other_small):
+def split_layer(g_half, routes_l, acts_l, own, other, is_own, small, other_small, early=None):
     peers = lax.axis_size("dict")
     me = lax.axis_index("dict")
     rows, listed = routes_l.shape
@@ -146,6 +146,9 @@
         [jnp.broadcast_to(g_half[None], (peers, rows, half)), placed], axis=-1
     )
     got = exchange(sent, 1).reshape(peers * rows, half + block)
+    if early is not None:
+        early, got = lax.optimization_barrier((early, got))
+        early = swap_cores(early)
     if other_small is None:
         small, got = lax.optimization_barrier((small, got))
         other_small = swap_cores(small)
@@ -184,7 +187,7 @@
     new_half = (g_half.astype(jnp.float32) + scale_l[:, None] * gain_half[None, :] * total).astype(
         jnp.bfloat16
     )
-    return attr, new_half, other_small
+    return attr, new_half, other_small, early
 
 
 def split_device(cotangent, routes, acts, decoder, encoder, gain, inv_rms):
@@ -214,20 +217,24 @@
     attr_keep = jnp.zeros((rows, acts.shape[2]), jnp.float32)
     grad_keep = jnp.zeros(cotangent.shape, jnp.bfloat16)
     g_half = lax.dynamic_slice_in_dim(cotangent, mine, half, axis=1)
+    lent = None
+    fulls = []
     for layer in reversed(range(depth)):
         is_own = here == layer
-        attr, g_half, other_small = split_layer(
-            g_half, routes[0], acts[0], own, other, is_own, small, other_small
-        )
+        attr, g_half, other_small, lent = split_layer(
+            g_half, routes[0], acts[0], own, other, is_own, small, other_small,
+            halves[-1] if halves else None,
+        )
+        if lent is not None:
+            fulls.append((halves[-1], lent))
         halves.append(g_half)
         attr_keep = jnp.where(is_own, attr, attr_keep)
-    mine_both = jnp.stack(halves, axis=0)
-    theirs_both = swap_cores(mine_both)
-    for step, layer in enumerate(reversed(range(depth))):
+    fulls.append((halves[-1], swap_cores(halves[-1])))
+    for (mine_h, theirs_h), layer in zip(fulls, reversed(range(depth))):
         full = jnp.where(
             here == 0,
-            jnp.concatenate([mine_both[step], theirs_both[step]], axis=1),
-            jnp.concatenate([theirs_both[step], mine_both[step]], axis=1),
+            jnp.concatenate([mine_h, theirs_h], axis=1),
+            jnp.concatenate([theirs_h, mine_h], axis=1),
         )
         grad_keep = jnp.where(here == layer, full, grad_keep)
     return (attr_keep[None], grad_keep[None])

time: 90.2 us -> 92.9 us (1.030)
  starting transfers between devices: 55.8 us -> 58.1 us
    ppermute x28, starting transfers between devices: 54.8 us -> 56.7 us  [exchange(): moved.append(lax.ppermute(parts[shift], 'dict', route))]
    ppermute x28, waiting for transfers between devices: 12.5 us -> 13.5 us  [exchange(): moved.append(lax.ppermute(parts[shift], 'dict', route))]
    ppermute x5 -> x6, waiting for transfers between devices: 3.42 us -> 2.77 us  [swap_cores(): return lax.ppermute(block, 'section', [(0, 1), (1, 0)])]
  transfers between devices with their start and end apart: 33 -> 34, of which waited for: 14 -> 15; matrix products, arithmetic and copies ran while one was open for 10% -> 11% of each run, Pallas kernels for 0% -> 0%
where the time goes in v22:
time: 92.9 us; the launch traced here: 92.4 us
  starting transfers between devices  58.1 us (63%)
  waiting for transfers between devices  16.2 us (17%)
  local copies, waits for them, and re-layouts  8.76 us (9%)
  matrix products  4.19 us (5%)
  other arithmetic  4.01 us (4%)
  between operations  1.07 us (1%)
    ppermute x28, starting transfers between devices, exchange(): moved.append(lax.ppermute(parts[shift], 'dict', route))  56.7 us
    ppermute x28, waiting for transfers between devices, exchange(): moved.append(lax.ppermute(parts[shift], 'dict', route))  13.5 us
    unnamed x38, local copies, waits for them, and re-layouts  5.26 us
    ppermute x6, waiting for transfers between devices, swap_cores(): return lax.ppermute(block, 'section', [(0, 1), (1, 0)])  2.77 us
    dot_general x4, matrix products, with_dec(): lax.dot_general(g_all, dec, (((1,), (1,)), ((), ())), preferred_element_t...  2.17 us
  transfers between devices with their start and end apart: 34, of which 15 were waited for; matrix products, arithmetic and copies ran while one was open for 11% of the time, Pallas kernels for 0%

profile of v22, /device:TPU:0, one launch (start us, length us, event | category | flops | bytes accessed | tf_op | source)
XLA Modules:
  0.0 92.4 jit_solution(2239675169860698809)
XLA Ops:
  4.5 6.0 %collective-permute-start = (bf16[16,2432]{1,0:T(8,128)(2,1)}, bf16[16,2432]{1,0:T(8,128)(2,1)}, u32[]{:S(2)}, u32[]{:S(2)}) collective-permute-start(bf16[16,2432]{1,0:T(8,128)(2,1)} %get-tuple-element.39), channel_id=1, source_target_pairs={{0,14},{2,12},{4,10},{6,8},{8,6},{10,4},{12,2},{14,0},{1,15},{3,13... | collective-permute-start | bytes 233480 | tf_op jit(solution)/shard_map/ppermute | solution.py:124
  11.4 1.9 %collective-permute-start.3 = (bf16[16,2432]{1,0:T(8,128)(2,1)S(1)}, bf16[16,2432]{1,0:T(8,128)(2,1)}, u32[]{:S(2)}, u32[]{:S(2)}) collective-permute-start(bf16[16,2432]{1,0:T(8,128)(2,1)S(1)} %get-tuple-element.42), channel_id=1, source_target_pairs={{0,8},{2,10},{4,12},{6,14},{8,0},{10,2},{12,4},{14,6},{1,9},{3,11}... | collective-permute-start | bytes 233480 | tf_op jit(solution)/shard_map/ppermute | solution.py:124
  13.4 2.4 %collective-permute-start.4 = (bf16[16,2432]{1,0:T(8,128)(2,1)S(1)}, bf16[16,2432]{1,0:T(8,128)(2,1)}, u32[]{:S(2)}, u32[]{:S(2)}) collective-permute-start(bf16[16,2432]{1,0:T(8,128)(2,1)S(1)} %get-tuple-element.37), channel_id=1, source_target_pairs={{0,6},{2,4},{4,2},{6,0},{8,14},{10,12},{12,10},{14,8},{1,7},{3,5},... | collective-permute-start | bytes 233480 | tf_op jit(solution)/shard_map/ppermute | solution.py:124
  15.8 1.5 %dynamic-slice_bitcast_fusion = (bf16[256,2304]{1,0:T(8,128)(2,1)S(1)}, bf16[256,2304]{1,0:T(8,128)(2,1)S(1)}) fusion(bf16[1,256,4608]{2,1,0:T(8,128)(2,1)} %param.11, s32[]{:T(128)S(6)} %select_n.193, bf16[1,256,4608]{2,1,0:T(8,128)(2,1)S(1)} %copy-done), kind=kLoop, calls=%fused_computation.48 | loop fusion | bytes 4718596 | tf_op jit(solution)/shard_map/dynamic_slice | solution.py:207
  17.9 1.6 %collective-permute-start.5 = (bf16[16,2432]{1,0:T(8,128)(2,1)S(1)}, bf16[16,2432]{1,0:T(8,128)(2,1)S(1)}, u32[]{:S(2)}, u32[]{:S(2)}) collective-permute-start(bf16[16,2432]{1,0:T(8,128)(2,1)S(1)} %get-tuple-element.43), channel_id=1, source_target_pairs={{0,4},{2,6},{4,0},{6,2},{8,12},{10,14},{12,8},{14,10},{1,5},{3,7},... | collective-permute-start | bytes 233480 | tf_op jit(solution)/shard_map/ppermute | solution.py:124
  20.4 1.6 %collective-permute-start.6 = (bf16[16,2432]{1,0:T(8,128)(2,1)S(1)}, bf16[16,2432]{1,0:T(8,128)(2,1)S(1)}, u32[]{:S(2)}, u32[]{:S(2)}) collective-permute-start(bf16[16,2432]{1,0:T(8,128)(2,1)S(1)} %get-tuple-element.36), channel_id=1, source_target_pairs={{0,2},{2,0},{4,6},{6,4},{8,10},{10,8},{12,14},{14,12},{1,3},{3,1},... | collective-permute-start | bytes 233480 | tf_op jit(solution)/shard_map/ppermute | solution.py:124
  23.2 0.9 bitcast_dynamic-update-slice_fusion.27
  24.1 0.9 bitcast_dynamic-update-slice_fusion.26
  28.6 1.2 %collective-permute-done.9 = f32[128,384]{1,0:T(8,128)S(1)} collective-permute-done((f32[128,384]{1,0:T(8,128)S(1)}, f32[128,384]{1,0:T(8,128)S(1)}, u32[]{:S(2)}, u32[]{:S(2)}) %collective-permute-start.9) | collective-permute-done | bytes 196640 | tf_op jit(solution)/shard_map/ppermute | solution.py:116
  30.6 3.4 %collective-permute-start.10 = (bf16[16,2432]{1,0:T(8,128)(2,1)S(1)}, bf16[16,2432]{1,0:T(8,128)(2,1)S(1)}, u32[]{:S(2)}, u32[]{:S(2)}) collective-permute-start(bf16[16,2432]{1,0:T(8,128)(2,1)S(1)} %get-tuple-element.30), channel_id=1, source_target_pairs={{0,14},{2,12},{4,10},{6,8},{8,6},{10,4},{12,2},{14,0},{1,15},{3,13... | collective-permute-start | bytes 233480 | tf_op jit(solution)/shard_map/ppermute | solution.py:124
  34.1 1.3 %collective-permute-start.11 = (bf16[16,2432]{1,0:T(8,128)(2,1)S(1)}, bf16[16,2432]{1,0:T(8,128)(2,1)S(1)}, u32[]{:S(2)}, u32[]{:S(2)}) collective-permute-start(bf16[16,2432]{1,0:T(8,128)(2,1)S(1)} %get-tuple-element.31), channel_id=1, source_target_pairs={{0,12},{2,14},{4,8},{6,10},{8,4},{10,6},{12,0},{14,2},{1,13},{3,15... | collective-permute-start | bytes 233480 | tf_op jit(solution)/shard_map/ppermute | solution.py:124
  35.4 2.9 %collective-permute-start.13 = (bf16[16,2432]{1,0:T(8,128)(2,1)S(1)}, bf16[16,2432]{1,0:T(8,128)(2,1)S(1)}, u32[]{:S(2)}, u32[]{:S(2)}) collective-permute-start(bf16[16,2432]{1,0:T(8,128)(2,1)S(1)} %get-tuple-element.33), channel_id=1, source_target_pairs={{0,8},{2,10},{4,12},{6,14},{8,0},{10,2},{12,4},{14,6},{1,9},{3,11}... | collective-permute-start | bytes 233480 | tf_op jit(solution)/shard_map/ppermute | solution.py:124
  38.4 1.0 %collective-permute-start.14 = (bf16[16,2432]{1,0:T(8,128)(2,1)S(1)}, bf16[16,2432]{1,0:T(8,128)(2,1)S(1)}, u32[]{:S(2)}, u32[]{:S(2)}) collective-permute-start(bf16[16,2432]{1,0:T(8,128)(2,1)S(1)} %get-tuple-element.34), channel_id=1, source_target_pairs={{0,6},{2,4},{4,2},{6,0},{8,14},{10,12},{12,10},{14,8},{1,7},{3,5},... | collective-permute-start | bytes 233480 | tf_op jit(solution)/shard_map/ppermute | solution.py:124
  39.4 3.4 %collective-permute-start.15 = (bf16[16,2432]{1,0:T(8,128)(2,1)S(1)}, bf16[16,2432]{1,0:T(8,128)(2,1)S(1)}, u32[]{:S(2)}, u32[]{:S(2)}) collective-permute-start(bf16[16,2432]{1,0:T(8,128)(2,1)S(1)} %get-tuple-element.35), channel_id=1, source_target_pairs={{0,4},{2,6},{4,0},{6,2},{8,12},{10,14},{12,8},{14,10},{1,5},{3,7},... | collective-permute-start | bytes 233480 | tf_op jit(solution)/shard_map/ppermute | solution.py:124
  42.9 3.1 %collective-permute-done.12 = bf16[16,2432]{1,0:T(8,128)(2,1)S(1)} collective-permute-done((bf16[16,2432]{1,0:T(8,128)(2,1)S(1)}, bf16[16,2432]{1,0:T(8,128)(2,1)S(1)}, u32[]{:S(2)}, u32[]{:S(2)}) %collective-permute-start.12) | collective-permute-done | bytes 77856 | tf_op jit(solution)/shard_map/ppermute | solution.py:124
  46.1 1.5 %collective-permute-done.13 = bf16[16,2432]{1,0:T(8,128)(2,1)S(1)} collective-permute-done((bf16[16,2432]{1,0:T(8,128)(2,1)S(1)}, bf16[16,2432]{1,0:T(8,128)(2,1)S(1)}, u32[]{:S(2)}, u32[]{:S(2)}) %collective-permute-start.13) | collective-permute-done | bytes 77856 | tf_op jit(solution)/shard_map/ppermute | solution.py:124
  48.4 4.0 %collective-permute-start.17 = (bf16[16,2432]{1,0:T(8,128)(2,1)S(1)}, bf16[16,2432]{1,0:T(8,128)(2,1)S(1)}, u32[]{:S(2)}, u32[]{:S(2)}) collective-permute-start(bf16[16,2432]{1,0:T(8,128)(2,1)S(1)} %get-tuple-element.25), channel_id=1, source_target_pairs={{0,14},{2,12},{4,10},{6,8},{8,6},{10,4},{12,2},{14,0},{1,15},{3,13... | collective-permute-start | bytes 233480 | tf_op jit(solution)/shard_map/ppermute | solution.py:124
  52.4 2.1 %collective-permute-start.19 = (bf16[16,2432]{1,0:T(8,128)(2,1)S(1)}, bf16[16,2432]{1,0:T(8,128)(2,1)S(1)}, u32[]{:S(2)}, u32[]{:S(2)}) collective-permute-start(bf16[16,2432]{1,0:T(8,128)(2,1)S(1)} %get-tuple-element.23), channel_id=1, source_target_pairs={{0,10},{2,8},{4,14},{6,12},{8,2},{10,0},{12,6},{14,4},{1,11},{3,9}... | collective-permute-start | bytes 233480 | tf_op jit(solution)/shard_map/ppermute | solution.py:124
  54.5 1.6 %collective-permute-start.20 = (bf16[16,2432]{1,0:T(8,128)(2,1)S(1)}, bf16[16,2432]{1,0:T(8,128)(2,1)S(1)}, u32[]{:S(2)}, u32[]{:S(2)}) collective-permute-start(bf16[16,2432]{1,0:T(8,128)(2,1)S(1)} %get-tuple-element.22), channel_id=1, source_target_pairs={{0,8},{2,10},{4,12},{6,14},{8,0},{10,2},{12,4},{14,6},{1,9},{3,11}... | collective-permute-start | bytes 233480 | tf_op jit(solution)/shard_map/ppermute | solution.py:124
  56.1 1.6 %collective-permute-start.21 = (bf16[16,2432]{1,0:T(8,128)(2,1)S(1)}, bf16[16,2432]{1,0:T(8,128)(2,1)S(1)}, u32[]{:S(2)}, u32[]{:S(2)}) collective-permute-start(bf16[16,2432]{1,0:T(8,128)(2,1)S(1)} %get-tuple-element.26), channel_id=1, source_target_pairs={{0,6},{2,4},{4,2},{6,0},{8,14},{10,12},{12,10},{14,8},{1,7},{3,5},... | collective-permute-start | bytes 233480 | tf_op jit(solution)/shard_map/ppermute | solution.py:124
  57.6 2.6 %collective-permute-start.22 = (bf16[16,2432]{1,0:T(8,128)(2,1)S(1)}, bf16[16,2432]{1,0:T(8,128)(2,1)S(1)}, u32[]{:S(2)}, u32[]{:S(2)}) collective-permute-start(bf16[16,2432]{1,0:T(8,128)(2,1)S(1)} %get-tuple-element.27), channel_id=1, source_target_pairs={{0,4},{2,6},{4,0},{6,2},{8,12},{10,14},{12,8},{14,10},{1,5},{3,7},... | collective-permute-start | bytes 233480 | tf_op jit(solution)/shard_map/ppermute | solution.py:124
  60.2 1.2 %collective-permute-start.23 = (bf16[16,2432]{1,0:T(8,128)(2,1)S(1)}, bf16[16,2432]{1,0:T(8,128)(2,1)S(1)}, u32[]{:S(2)}, u32[]{:S(2)}) collective-permute-start(bf16[16,2432]{1,0:T(8,128)(2,1)S(1)} %get-tuple-element.21), channel_id=1, source_target_pairs={{0,2},{2,0},{4,6},{6,4},{8,10},{10,8},{12,14},{14,12},{1,3},{3,1},... | collective-permute-start | bytes 233480 | tf_op jit(solution)/shard_map/ppermute | solution.py:124
  61.5 2.8 %collective-permute-done.19 = bf16[16,2432]{1,0:T(8,128)(2,1)S(1)} collective-permute-done((bf16[16,2432]{1,0:T(8,128)(2,1)S(1)}, bf16[16,2432]{1,0:T(8,128)(2,1)S(1)}, u32[]{:S(2)}, u32[]{:S(2)}) %collective-permute-start.19) | collective-permute-done | bytes 77856 | tf_op jit(solution)/shard_map/ppermute | solution.py:124
  68.4 4.5 %collective-permute-start.25 = (bf16[16,2432]{1,0:T(8,128)(2,1)S(1)}, bf16[16,2432]{1,0:T(8,128)(2,1)S(1)}, u32[]{:S(2)}, u32[]{:S(2)}) collective-permute-start(bf16[16,2432]{1,0:T(8,128)(2,1)S(1)} %get-tuple-element.15), channel_id=1, source_target_pairs={{0,14},{2,12},{4,10},{6,8},{8,6},{10,4},{12,2},{14,0},{1,15},{3,13... | collective-permute-start | bytes 233480 | tf_op jit(solution)/shard_map/ppermute | solution.py:124
  73.0 2.1 %collective-permute-start.27 = (bf16[16,2432]{1,0:T(8,128)(2,1)S(1)}, bf16[16,2432]{1,0:T(8,128)(2,1)S(1)}, u32[]{:S(2)}, u32[]{:S(2)}) collective-permute-start(bf16[16,2432]{1,0:T(8,128)(2,1)S(1)} %get-tuple-element.17), channel_id=1, source_target_pairs={{0,10},{2,8},{4,14},{6,12},{8,2},{10,0},{12,6},{14,4},{1,11},{3,9}... | collective-permute-start | bytes 233480 | tf_op jit(solution)/shard_map/ppermute | solution.py:124
  75.1 1.2 %collective-permute-start.28 = (bf16[16,2432]{1,0:T(8,128)(2,1)S(1)}, bf16[16,2432]{1,0:T(8,128)(2,1)S(1)}, u32[]{:S(2)}, u32[]{:S(2)}) collective-permute-start(bf16[16,2432]{1,0:T(8,128)(2,1)S(1)} %get-tuple-element.18), channel_id=1, source_target_pairs={{0,8},{2,10},{4,12},{6,14},{8,0},{10,2},{12,4},{14,6},{1,9},{3,11}... | collective-permute-start | bytes 233480 | tf_op jit(solution)/shard_map/ppermute | solution.py:124
  76.3 6.5 %collective-permute-start.29 = (bf16[16,2432]{1,0:T(8,128)(2,1)S(1)}, bf16[16,2432]{1,0:T(8,128)(2,1)S(1)}, u32[]{:S(2)}, u32[]{:S(2)}) collective-permute-start(bf16[16,2432]{1,0:T(8,128)(2,1)S(1)} %get-tuple-element.19), channel_id=1, source_target_pairs={{0,6},{2,4},{4,2},{6,0},{8,14},{10,12},{12,10},{14,8},{1,7},{3,5},... | collective-permute-start | bytes 233480 | tf_op jit(solution)/shard_map/ppermute | solution.py:124
  82.9 1.3 %collective-permute-start.30 = (bf16[16,2432]{1,0:T(8,128)(2,1)S(1)}, bf16[16,2432]{1,0:T(8,128)(2,1)S(1)}, u32[]{:S(2)}, u32[]{:S(2)}) collective-permute-start(bf16[16,2432]{1,0:T(8,128)(2,1)S(1)} %get-tuple-element.20), channel_id=1, source_target_pairs={{0,4},{2,6},{4,0},{6,2},{8,12},{10,14},{12,8},{14,10},{1,5},{3,7},... | collective-permute-start | bytes 233480 | tf_op jit(solution)/shard_map/ppermute | solution.py:124
  84.2 1.5 %collective-permute-done.27 = bf16[16,2432]{1,0:T(8,128)(2,1)S(1)} collective-permute-done((bf16[16,2432]{1,0:T(8,128)(2,1)S(1)}, bf16[16,2432]{1,0:T(8,128)(2,1)S(1)}, u32[]{:S(2)}, u32[]{:S(2)}) %collective-permute-start.27) | collective-permute-done | bytes 77856 | tf_op jit(solution)/shard_map/ppermute | solution.py:124
  85.7 1.1 %collective-permute-start.31 = (bf16[16,2432]{1,0:T(8,128)(2,1)S(1)}, bf16[16,2432]{1,0:T(8,128)(2,1)S(1)}, u32[]{:S(2)}, u32[]{:S(2)}) collective-permute-start(bf16[16,2432]{1,0:T(8,128)(2,1)S(1)} %get-tuple-element.14), channel_id=1, source_target_pairs={{0,2},{2,0},{4,6},{6,4},{8,10},{10,8},{12,14},{14,12},{1,3},{3,1},... | collective-permute-start | bytes 233480 | tf_op jit(solution)/shard_map/ppermute | solution.py:124
  86.9 1.7 %collective-permute-done.29 = bf16[16,2432]{1,0:T(8,128)(2,1)S(1)} collective-permute-done((bf16[16,2432]{1,0:T(8,128)(2,1)S(1)}, bf16[16,2432]{1,0:T(8,128)(2,1)S(1)}, u32[]{:S(2)}, u32[]{:S(2)}) %collective-permute-start.29) | collective-permute-done | bytes 77856 | tf_op jit(solution)/shard_map/ppermute | solution.py:124
  88.9 1.2 %collective-permute-done.31 = bf16[16,2432]{1,0:T(8,128)(2,1)S(1)} collective-permute-done((bf16[16,2432]{1,0:T(8,128)(2,1)S(1)}, bf16[16,2432]{1,0:T(8,128)(2,1)S(1)}, u32[]{:S(2)}, u32[]{:S(2)}) %collective-permute-start.31) | collective-permute-done | bytes 77856 | tf_op jit(solution)/shard_map/ppermute | solution.py:124
  (132 shorter events, 19.4 us)
Async XLA Ops:
  4.5 13.5 %collective-permute-start = (bf16[16,2432]{1,0:T(8,128)(2,1)}, bf16[16,2432]{1,0:T(8,128)(2,1)}, u32[]{:S(2)}, u32[]{:S(2)}) collective-permute-start(bf16[16,2432]{1,0:T(8,128)(2,1)} %get-tuple-element.39), channel_id=1, source_target_pairs={{0,14},{2,12},{4,10},{6,8},{8,6},{10,4},{12,2},{14,0},{1,15},{3,13... | collective-permute-start | bytes 233480 | tf_op jit(solution)/shard_map/ppermute | solution.py:124
  10.4 10.0 %collective-permute-start.1 = (bf16[16,2432]{1,0:T(8,128)(2,1)S(1)}, bf16[16,2432]{1,0:T(8,128)(2,1)}, u32[]{:S(2)}, u32[]{:S(2)}) collective-permute-start(bf16[16,2432]{1,0:T(8,128)(2,1)S(1)} %get-tuple-element.40), channel_id=1, source_target_pairs={{0,12},{2,14},{4,8},{6,10},{8,4},{10,6},{12,0},{14,2},{1,13},{3,15... | collective-permute-start | bytes 233480 | tf_op jit(solution)/shard_map/ppermute | solution.py:124
  10.7 12.5 %collective-permute-start.2 = (bf16[16,2432]{1,0:T(8,128)(2,1)S(1)}, bf16[16,2432]{1,0:T(8,128)(2,1)}, u32[]{:S(2)}, u32[]{:S(2)}) collective-permute-start(bf16[16,2432]{1,0:T(8,128)(2,1)S(1)} %get-tuple-element.41), channel_id=1, source_target_pairs={{0,10},{2,8},{4,14},{6,12},{8,2},{10,0},{12,6},{14,4},{1,11},{3,9}... | collective-permute-start | bytes 233480 | tf_op jit(solution)/shard_map/ppermute | solution.py:124
  11.4 12.7 %collective-permute-start.3 = (bf16[16,2432]{1,0:T(8,128)(2,1)S(1)}, bf16[16,2432]{1,0:T(8,128)(2,1)}, u32[]{:S(2)}, u32[]{:S(2)}) collective-permute-start(bf16[16,2432]{1,0:T(8,128)(2,1)S(1)} %get-tuple-element.42), channel_id=1, source_target_pairs={{0,8},{2,10},{4,12},{6,14},{8,0},{10,2},{12,4},{14,6},{1,9},{3,11}... | collective-permute-start | bytes 233480 | tf_op jit(solution)/shard_map/ppermute | solution.py:124
  13.4 11.6 %collective-permute-start.4 = (bf16[16,2432]{1,0:T(8,128)(2,1)S(1)}, bf16[16,2432]{1,0:T(8,128)(2,1)}, u32[]{:S(2)}, u32[]{:S(2)}) collective-permute-start(bf16[16,2432]{1,0:T(8,128)(2,1)S(1)} %get-tuple-element.37), channel_id=1, source_target_pairs={{0,6},{2,4},{4,2},{6,0},{8,14},{10,12},{12,10},{14,8},{1,7},{3,5},... | collective-permute-start | bytes 233480 | tf_op jit(solution)/shard_map/ppermute | solution.py:124
  17.9 8.0 %collective-permute-start.5 = (bf16[16,2432]{1,0:T(8,128)(2,1)S(1)}, bf16[16,2432]{1,0:T(8,128)(2,1)S(1)}, u32[]{:S(2)}, u32[]{:S(2)}) collective-permute-start(bf16[16,2432]{1,0:T(8,128)(2,1)S(1)} %get-tuple-element.43), channel_id=1, source_target_pairs={{0,4},{2,6},{4,0},{6,2},{8,12},{10,14},{12,8},{14,10},{1,5},{3,7},... | collective-permute-start | bytes 233480 | tf_op jit(solution)/shard_map/ppermute | solution.py:124
  20.4 5.5 %collective-permute-start.6 = (bf16[16,2432]{1,0:T(8,128)(2,1)S(1)}, bf16[16,2432]{1,0:T(8,128)(2,1)S(1)}, u32[]{:S(2)}, u32[]{:S(2)}) collective-permute-start(bf16[16,2432]{1,0:T(8,128)(2,1)S(1)} %get-tuple-element.36), channel_id=1, source_target_pairs={{0,2},{2,0},{4,6},{6,4},{8,10},{10,8},{12,14},{14,12},{1,3},{3,1},... | collective-permute-start | bytes 233480 | tf_op jit(solution)/shard_map/ppermute | solution.py:124
  23.2 4.5 %collective-permute-start.8 = (bf16[512,2304]{1,0:T(8,128)(2,1)S(1)}, bf16[512,2304]{1,0:T(8,128)(2,1)S(1)}, u32[]{:S(2)}, u32[]{:S(2)}) collective-permute-start(bf16[512,2304]{1,0:T(8,128)(2,1)S(1)} %pad_maximum_fusion), channel_id=1, source_target_pairs={{0,1},{1,0},{2,3},{3,2},{4,5},{5,4},{6,7},{7,6},{8,9},{9,8},{10,11... | collective-permute-start | bytes 7077896 | tf_op jit(solution)/shard_map/ppermute | solution.py:116
  26.0 2.5 %collective-permute-start.7 = (f32[4624]{0:T(1024)S(1)}, f32[4624]{0:T(1024)S(1)}, u32[]{:S(2)}, u32[]{:S(2)}) collective-permute-start(f32[4624]{0:T(1024)S(1)} %pad_maximum_fusion.7), channel_id=1, source_target_pairs={{0,1},{1,0},{2,3},{3,2},{4,5},{5,4},{6,7},{7,6},{8,9},{9,8},{10,11... | collective-permute-start | bytes 55496 | tf_op jit(solution)/shard_map/ppermute | solution.py:116
  28.3 1.5 %collective-permute-start.9 = (f32[128,384]{1,0:T(8,128)S(1)}, f32[128,384]{1,0:T(8,128)S(1)}, u32[]{:S(2)}, u32[]{:S(2)}) collective-permute-start(f32[128,384]{1,0:T(8,128)S(1)} %pad_maximum_fusion.1), channel_id=1, source_target_pairs={{0,1},{1,0},{2,3},{3,2},{4,5},{5,4},{6,7},{7,6},{8,9},{9,8},{10,11... | collective-permute-start | bytes 589832 | tf_op jit(solution)/shard_map/ppermute | solution.py:116
  30.6 8.7 %collective-permute-start.10 = (bf16[16,2432]{1,0:T(8,128)(2,1)S(1)}, bf16[16,2432]{1,0:T(8,128)(2,1)S(1)}, u32[]{:S(2)}, u32[]{:S(2)}) collective-permute-start(bf16[16,2432]{1,0:T(8,128)(2,1)S(1)} %get-tuple-element.30), channel_id=1, source_target_pairs={{0,14},{2,12},{4,10},{6,8},{8,6},{10,4},{12,2},{14,0},{1,15},{3,13... | collective-permute-start | bytes 233480 | tf_op jit(solution)/shard_map/ppermute | solution.py:124
  34.1 8.7 %collective-permute-start.11 = (bf16[16,2432]{1,0:T(8,128)(2,1)S(1)}, bf16[16,2432]{1,0:T(8,128)(2,1)S(1)}, u32[]{:S(2)}, u32[]{:S(2)}) collective-permute-start(bf16[16,2432]{1,0:T(8,128)(2,1)S(1)} %get-tuple-element.31), channel_id=1, source_target_pairs={{0,12},{2,14},{4,8},{6,10},{8,4},{10,6},{12,0},{14,2},{1,13},{3,15... | collective-permute-start | bytes 233480 | tf_op jit(solution)/shard_map/ppermute | solution.py:124
  35.4 10.6 %collective-permute-start.12 = (bf16[16,2432]{1,0:T(8,128)(2,1)S(1)}, bf16[16,2432]{1,0:T(8,128)(2,1)S(1)}, u32[]{:S(2)}, u32[]{:S(2)}) collective-permute-start(bf16[16,2432]{1,0:T(8,128)(2,1)S(1)} %get-tuple-element.32), channel_id=1, source_target_pairs={{0,10},{2,8},{4,14},{6,12},{8,2},{10,0},{12,6},{14,4},{1,11},{3,9}... | collective-permute-start | bytes 233480 | tf_op jit(solution)/shard_map/ppermute | solution.py:124
  35.4 12.1 %collective-permute-start.13 = (bf16[16,2432]{1,0:T(8,128)(2,1)S(1)}, bf16[16,2432]{1,0:T(8,128)(2,1)S(1)}, u32[]{:S(2)}, u32[]{:S(2)}) collective-permute-start(bf16[16,2432]{1,0:T(8,128)(2,1)S(1)} %get-tuple-element.33), channel_id=1, source_target_pairs={{0,8},{2,10},{4,12},{6,14},{8,0},{10,2},{12,4},{14,6},{1,9},{3,11}... | collective-permute-start | bytes 233480 | tf_op jit(solution)/shard_map/ppermute | solution.py:124
  38.4 9.2 %collective-permute-start.14 = (bf16[16,2432]{1,0:T(8,128)(2,1)S(1)}, bf16[16,2432]{1,0:T(8,128)(2,1)S(1)}, u32[]{:S(2)}, u32[]{:S(2)}) collective-permute-start(bf16[16,2432]{1,0:T(8,128)(2,1)S(1)} %get-tuple-element.34), channel_id=1, source_target_pairs={{0,6},{2,4},{4,2},{6,0},{8,14},{10,12},{12,10},{14,8},{1,7},{3,5},... | collective-permute-start | bytes 233480 | tf_op jit(solution)/shard_map/ppermute | solution.py:124
  39.4 8.7 %collective-permute-start.15 = (bf16[16,2432]{1,0:T(8,128)(2,1)S(1)}, bf16[16,2432]{1,0:T(8,128)(2,1)S(1)}, u32[]{:S(2)}, u32[]{:S(2)}) collective-permute-start(bf16[16,2432]{1,0:T(8,128)(2,1)S(1)} %get-tuple-element.35), channel_id=1, source_target_pairs={{0,4},{2,6},{4,0},{6,2},{8,12},{10,14},{12,8},{14,10},{1,5},{3,7},... | collective-permute-start | bytes 233480 | tf_op jit(solution)/shard_map/ppermute | solution.py:124
  42.8 5.2 %collective-permute-start.16 = (bf16[16,2432]{1,0:T(8,128)(2,1)S(1)}, bf16[16,2432]{1,0:T(8,128)(2,1)S(1)}, u32[]{:S(2)}, u32[]{:S(2)}) collective-permute-start(bf16[16,2432]{1,0:T(8,128)(2,1)S(1)} %get-tuple-element.29), channel_id=1, source_target_pairs={{0,2},{2,0},{4,6},{6,4},{8,10},{10,8},{12,14},{14,12},{1,3},{3,1},... | collective-permute-start | bytes 233480 | tf_op jit(solution)/shard_map/ppermute | solution.py:124
  48.4 9.3 %collective-permute-start.17 = (bf16[16,2432]{1,0:T(8,128)(2,1)S(1)}, bf16[16,2432]{1,0:T(8,128)(2,1)S(1)}, u32[]{:S(2)}, u32[]{:S(2)}) collective-permute-start(bf16[16,2432]{1,0:T(8,128)(2,1)S(1)} %get-tuple-element.25), channel_id=1, source_target_pairs={{0,14},{2,12},{4,10},{6,8},{8,6},{10,4},{12,2},{14,0},{1,15},{3,13... | collective-permute-start | bytes 233480 | tf_op jit(solution)/shard_map/ppermute | solution.py:124
  52.3 7.9 %collective-permute-start.18 = (bf16[16,2432]{1,0:T(8,128)(2,1)S(1)}, bf16[16,2432]{1,0:T(8,128)(2,1)S(1)}, u32[]{:S(2)}, u32[]{:S(2)}) collective-permute-start(bf16[16,2432]{1,0:T(8,128)(2,1)S(1)} %get-tuple-element.24), channel_id=1, source_target_pairs={{0,12},{2,14},{4,8},{6,10},{8,4},{10,6},{12,0},{14,2},{1,13},{3,15... | collective-permute-start | bytes 233480 | tf_op jit(solution)/shard_map/ppermute | solution.py:124
  52.4 12.0 %collective-permute-start.19 = (bf16[16,2432]{1,0:T(8,128)(2,1)S(1)}, bf16[16,2432]{1,0:T(8,128)(2,1)S(1)}, u32[]{:S(2)}, u32[]{:S(2)}) collective-permute-start(bf16[16,2432]{1,0:T(8,128)(2,1)S(1)} %get-tuple-element.23), channel_id=1, source_target_pairs={{0,10},{2,8},{4,14},{6,12},{8,2},{10,0},{12,6},{14,4},{1,11},{3,9}... | collective-permute-start | bytes 233480 | tf_op jit(solution)/shard_map/ppermute | solution.py:124
  54.5 9.8 %collective-permute-start.20 = (bf16[16,2432]{1,0:T(8,128)(2,1)S(1)}, bf16[16,2432]{1,0:T(8,128)(2,1)S(1)}, u32[]{:S(2)}, u32[]{:S(2)}) collective-permute-start(bf16[16,2432]{1,0:T(8,128)(2,1)S(1)} %get-tuple-element.22), channel_id=1, source_target_pairs={{0,8},{2,10},{4,12},{6,14},{8,0},{10,2},{12,4},{14,6},{1,9},{3,11}... | collective-permute-start | bytes 233480 | tf_op jit(solution)/shard_map/ppermute | solution.py:124
  56.1 8.3 %collective-permute-start.21 = (bf16[16,2432]{1,0:T(8,128)(2,1)S(1)}, bf16[16,2432]{1,0:T(8,128)(2,1)S(1)}, u32[]{:S(2)}, u32[]{:S(2)}) collective-permute-start(bf16[16,2432]{1,0:T(8,128)(2,1)S(1)} %get-tuple-element.26), channel_id=1, source_target_pairs={{0,6},{2,4},{4,2},{6,0},{8,14},{10,12},{12,10},{14,8},{1,7},{3,5},... | collective-permute-start | bytes 233480 | tf_op jit(solution)/shard_map/ppermute | solution.py:124
  57.6 6.9 %collective-permute-start.22 = (bf16[16,2432]{1,0:T(8,128)(2,1)S(1)}, bf16[16,2432]{1,0:T(8,128)(2,1)S(1)}, u32[]{:S(2)}, u32[]{:S(2)}) collective-permute-start(bf16[16,2432]{1,0:T(8,128)(2,1)S(1)} %get-tuple-element.27), channel_id=1, source_target_pairs={{0,4},{2,6},{4,0},{6,2},{8,12},{10,14},{12,8},{14,10},{1,5},{3,7},... | collective-permute-start | bytes 233480 | tf_op jit(solution)/shard_map/ppermute | solution.py:124
  60.2 4.7 %collective-permute-start.23 = (bf16[16,2432]{1,0:T(8,128)(2,1)S(1)}, bf16[16,2432]{1,0:T(8,128)(2,1)S(1)}, u32[]{:S(2)}, u32[]{:S(2)}) collective-permute-start(bf16[16,2432]{1,0:T(8,128)(2,1)S(1)} %get-tuple-element.21), channel_id=1, source_target_pairs={{0,2},{2,0},{4,6},{6,4},{8,10},{10,8},{12,14},{14,12},{1,3},{3,1},... | collective-permute-start | bytes 233480 | tf_op jit(solution)/shard_map/ppermute | solution.py:124
  66.3 25.2 %collective-permute-start.33 = (bf16[16,2304]{1,0:T(8,128)(2,1)S(1)}, bf16[16,2304]{1,0:T(8,128)(2,1)S(1)}, u32[]{:S(2)}, u32[]{:S(2)}) collective-permute-start(bf16[16,2304]{1,0:T(8,128)(2,1)S(1)} %add_convert_fusion.1), channel_id=1, source_target_pairs={{0,1},{1,0},{2,3},{3,2},{4,5},{5,4},{6,7},{7,6},{8,9},{9,8},{10,11... | collective-permute-start | bytes 221192 | tf_op jit(solution)/shard_map/ppermute | solution.py:116
  68.4 7.9 %collective-permute-start.25 = (bf16[16,2432]{1,0:T(8,128)(2,1)S(1)}, bf16[16,2432]{1,0:T(8,128)(2,1)S(1)}, u32[]{:S(2)}, u32[]{:S(2)}) collective-permute-start(bf16[16,2432]{1,0:T(8,128)(2,1)S(1)} %get-tuple-element.15), channel_id=1, source_target_pairs={{0,14},{2,12},{4,10},{6,8},{8,6},{10,4},{12,2},{14,0},{1,15},{3,13... | collective-permute-start | bytes 233480 | tf_op jit(solution)/shard_map/ppermute | solution.py:124
  72.9 10.0 %collective-permute-start.26 = (bf16[16,2432]{1,0:T(8,128)(2,1)S(1)}, bf16[16,2432]{1,0:T(8,128)(2,1)S(1)}, u32[]{:S(2)}, u32[]{:S(2)}) collective-permute-start(bf16[16,2432]{1,0:T(8,128)(2,1)S(1)} %get-tuple-element.16), channel_id=1, source_target_pairs={{0,12},{2,14},{4,8},{6,10},{8,4},{10,6},{12,0},{14,2},{1,13},{3,15... | collective-permute-start | bytes 233480 | tf_op jit(solution)/shard_map/ppermute | solution.py:124
  73.0 12.7 %collective-permute-start.27 = (bf16[16,2432]{1,0:T(8,128)(2,1)S(1)}, bf16[16,2432]{1,0:T(8,128)(2,1)S(1)}, u32[]{:S(2)}, u32[]{:S(2)}) collective-permute-start(bf16[16,2432]{1,0:T(8,128)(2,1)S(1)} %get-tuple-element.17), channel_id=1, source_target_pairs={{0,10},{2,8},{4,14},{6,12},{8,2},{10,0},{12,6},{14,4},{1,11},{3,9}... | collective-permute-start | bytes 233480 | tf_op jit(solution)/shard_map/ppermute | solution.py:124
  75.1 11.8 %collective-permute-start.28 = (bf16[16,2432]{1,0:T(8,128)(2,1)S(1)}, bf16[16,2432]{1,0:T(8,128)(2,1)S(1)}, u32[]{:S(2)}, u32[]{:S(2)}) collective-permute-start(bf16[16,2432]{1,0:T(8,128)(2,1)S(1)} %get-tuple-element.18), channel_id=1, source_target_pairs={{0,8},{2,10},{4,12},{6,14},{8,0},{10,2},{12,4},{14,6},{1,9},{3,11}... | collective-permute-start | bytes 233480 | tf_op jit(solution)/shard_map/ppermute | solution.py:124
  76.3 12.3 %collective-permute-start.29 = (bf16[16,2432]{1,0:T(8,128)(2,1)S(1)}, bf16[16,2432]{1,0:T(8,128)(2,1)S(1)}, u32[]{:S(2)}, u32[]{:S(2)}) collective-permute-start(bf16[16,2432]{1,0:T(8,128)(2,1)S(1)} %get-tuple-element.19), channel_id=1, source_target_pairs={{0,6},{2,4},{4,2},{6,0},{8,14},{10,12},{12,10},{14,8},{1,7},{3,5},... | collective-permute-start | bytes 233480 | tf_op jit(solution)/shard_map/ppermute | solution.py:124
  82.9 6.0 %collective-permute-start.30 = (bf16[16,2432]{1,0:T(8,128)(2,1)S(1)}, bf16[16,2432]{1,0:T(8,128)(2,1)S(1)}, u32[]{:S(2)}, u32[]{:S(2)}) collective-permute-start(bf16[16,2432]{1,0:T(8,128)(2,1)S(1)} %get-tuple-element.20), channel_id=1, source_target_pairs={{0,4},{2,6},{4,0},{6,2},{8,12},{10,14},{12,8},{14,10},{1,5},{3,7},... | collective-permute-start | bytes 233480 | tf_op jit(solution)/shard_map/ppermute | solution.py:124
  85.7 4.4 %collective-permute-start.31 = (bf16[16,2432]{1,0:T(8,128)(2,1)S(1)}, bf16[16,2432]{1,0:T(8,128)(2,1)S(1)}, u32[]{:S(2)}, u32[]{:S(2)}) collective-permute-start(bf16[16,2432]{1,0:T(8,128)(2,1)S(1)} %get-tuple-element.14), channel_id=1, source_target_pairs={{0,2},{2,0},{4,6},{6,4},{8,10},{10,8},{12,14},{14,12},{1,3},{3,1},... | collective-permute-start | bytes 233480 | tf_op jit(solution)/shard_map/ppermute | solution.py:124
  (8 other events, 55.7 us)
